TPU v7x, 32 devices: a whole 2x2x4 slice. The times are simulated.
32 devices in a mesh: len: 16 (over z, y, x), band: 2 (over core).
Axes of the slice: x: 2, y: 2, z: 4, core: 2. Of those that a mesh axis runs over, the one named last changes fastest.
Arguments:
- populations: float32 [19, 128, 32, 128], P(None, 'len', 'band'), as said below
- solid_mask: int32 [128, 32, 128], P('len', 'band'), may hold values from 0 to 1, as said below
- smoke_field: float32 [128, 32, 128], P('len', 'band'), may hold values from 0 to 1
- fan_hubs: int32 [8, 3], replicated, may hold values from 0 to 127, as said below
- fan_gain: float32 [8], replicated, may hold values from 0.15 to 0.5
- jet_speed: float32 [8], replicated, may hold values from 0.05 to 0.12
- sources: int32 [16, 3], replicated, may hold values from 0 to 127, as said below
- source_rate: float32 [16], replicated, may hold values from 0.2 to 1
Outputs:
- populations_out: float32 [19, 128, 32, 128], P(None, 'len', 'band')
- smoke_out: float32 [128, 32, 128], P('len', 'band')
Inputs may be any that keep to these rules, and one draw needn't show every extreme that they name: `solid_mask`: 1 on every node with y = 0, y = 31, y = 16, z = 0 or z = 128 - 1 (walls of the two bores). `fan_hubs`: hub_y lies in 4 .. 27 and hub_z in 4 .. 123. `sources`: source nodes have 1 <= y <= 30 and 1 <= z <= 126. `populations`: every population is positive.
All inputs are finite; a program needn't handle non-finite values.
Results may differ from a plain program's by a relative error of at most 0.0001.
Values sent between devices are 32-bit elements; how exact they have to be, the bound alone decides.
No kernel may reach another device: no remote copies, remote signals or barrier semaphores. Data moves between devices by JAX's collectives and lax.ppermute only.
A program may use at most 64 MiB of HBM per device.

v0:
```python
import jax
import jax.numpy as jnp
from jax import lax
from jax.sharding import PartitionSpec as P

RAD = 3
FAN_LEN = 16
ITERS = 3


VELOCITIES = (
    (0, 0, 0),
    (1, 0, 0),
    (-1, 0, 0),
    (0, 1, 0),
    (0, -1, 0),
    (0, 0, 1),
    (0, 0, -1),
    (1, 1, 0),
    (-1, -1, 0),
    (1, -1, 0),
    (-1, 1, 0),
    (1, 0, 1),
    (-1, 0, -1),
    (1, 0, -1),
    (-1, 0, 1),
    (0, 1, 1),
    (0, -1, -1),
    (0, 1, -1),
    (0, -1, 1),
)
WEIGHTS = (1.0 / 3.0,) + (1.0 / 18.0,) * 6 + (1.0 / 36.0,) * 12
OPPOSITE = (0, 2, 1, 4, 3, 6, 5, 8, 7, 10, 9, 12, 11, 14, 13, 16, 15, 18, 17)
RELAX_RATE = 1.0 / 0.6
DIFFUSIVITY = 0.12


def extended_2(cells, sides, width):
    for axis, dim in sides:
        count = lax.axis_size(axis)
        head = lax.slice_in_dim(cells, 0, width, axis=dim)
        tail = lax.slice_in_dim(cells, cells.shape[dim] - width, cells.shape[dim], axis=dim)
        cells = jnp.concatenate(
            [
                lax.ppermute(tail, axis, [(i, (i + 1) % count) for i in range(count)]),
                cells,
                lax.ppermute(head, axis, [((i + 1) % count, i) for i in range(count)]),
            ],
            axis=dim,
        )
    return cells


def moments(populations):
    density = jnp.sum(populations, axis=0)
    velocity = []
    for dimension in range(3):
        forward = [populations[which] for which in range(19) if VELOCITIES[which][dimension] == 1]
        backward = [populations[which] for which in range(19) if VELOCITIES[which][dimension] == -1]
        velocity.append((sum(forward) - sum(backward)) / density)
    return (density, velocity)


def collide(populations, density, velocity, force_field, solid_flag):
    speed_sq = velocity[0] * velocity[0] + velocity[1] * velocity[1] + velocity[2] * velocity[2]
    posts = []
    for which in range(19):
        shift_x, shift_y, shift_z = VELOCITIES[which]
        along = shift_x * velocity[0] + shift_y * velocity[1] + shift_z * velocity[2]
        balance = (
            WEIGHTS[which] * density * (1.0 + 3.0 * along + 4.5 * along * along - 1.5 * speed_sq)
        )
        relaxed = (
            populations[which]
            - RELAX_RATE * (populations[which] - balance)
            + 3.0 * WEIGHTS[which] * shift_x * force_field
        )
        posts.append(jnp.where(solid_flag, populations[OPPOSITE[which]], relaxed))
    return jnp.stack(posts)


def disc_count():
    inside = 0
    for offset_a in range(-RAD, RAD + 1):
        for offset_b in range(-RAD, RAD + 1):
            if offset_a * offset_a + offset_b * offset_b <= RAD * RAD:
                inside = inside + 1
    return FAN_LEN * inside


def fan_discs(fan_hubs, coord_x, coord_y, coord_z, length_total):
    discs = []
    for fan_number in range(fan_hubs.shape[0]):
        offset_x = jnp.mod(coord_x - fan_hubs[fan_number, 0], length_total)
        offset_y = coord_y - fan_hubs[fan_number, 1]
        offset_z = coord_z - fan_hubs[fan_number, 2]
        discs.append(
            (offset_x < FAN_LEN) & (offset_y * offset_y + offset_z * offset_z <= RAD * RAD)
        )
    return discs


def partial_flow(discs, velocity, solid_flag):
    return jnp.stack(
        [
            jnp.sum(jnp.where(disc_nodes & jnp.logical_not(solid_flag), velocity[0], 0.0))
            for disc_nodes in discs
        ]
    )


def force_from(discs, totals, fan_gain, jet_speed):
    strength = fan_gain * (jet_speed - totals / float(disc_count()))
    force_field = jnp.zeros(discs[0].shape, jnp.float32)
    for fan_number in range(len(discs)):
        force_field = force_field + jnp.where(discs[fan_number], strength[fan_number], 0.0)
    return force_field


def advance(center, ahead_x, behind_x, ahead_y, behind_y, ahead_z, behind_z, velocity, solid_flag):
    laplace = ahead_x + behind_x + ahead_y + behind_y + ahead_z + behind_z - 6.0 * center
    advect = 0.5 * (
        velocity[0] * (ahead_x - behind_x)
        + velocity[1] * (ahead_y - behind_y)
        + velocity[2] * (ahead_z - behind_z)
    )
    return jnp.where(solid_flag, 0.0, center + DIFFUSIVITY * laplace - advect)


def shift_height(field, shift_z):
    if shift_z == 0:
        return field
    zero_layer = jnp.zeros(field.shape[:-1] + (1,), field.dtype)
    if shift_z == 1:
        return jnp.concatenate([zero_layer, field[..., :-1]], axis=-1)
    return jnp.concatenate([field[..., 1:], zero_layer], axis=-1)


def stream_rimmed(extended, slab_len, band_width):
    moved = []
    for which in range(19):
        shift_x, shift_y, shift_z = VELOCITIES[which]
        piece = extended[
            which, 1 - shift_x : 1 - shift_x + slab_len, 1 - shift_y : 1 - shift_y + band_width, :
        ]
        moved.append(shift_height(piece, shift_z))
    return jnp.stack(moved)


def source_release(sources, source_rate, offset_len, offset_band, slab_len, band_width, height):
    local_x = sources[:, 0] - offset_len
    local_y = sources[:, 1] - offset_band
    pick_x = (local_x[:, None] == jnp.arange(slab_len, dtype=jnp.int32)[None, :]).astype(
        jnp.float32
    )
    pick_y = (local_y[:, None] == jnp.arange(band_width, dtype=jnp.int32)[None, :]).astype(
        jnp.float32
    )
    pick_z = (sources[:, 2][:, None] == jnp.arange(height, dtype=jnp.int32)[None, :]).astype(
        jnp.float32
    )
    weighted = source_rate[:, None] * pick_x
    cross_table = (pick_y[:, :, None] * pick_z[:, None, :]).reshape(
        sources.shape[0], band_width * height
    )
    released = jnp.dot(
        weighted.T, cross_table, precision=lax.Precision.HIGHEST, preferred_element_type=jnp.float32
    )
    return released.reshape(slab_len, band_width, height)


def body(populations, solid_mask, smoke_field, fan_hubs, fan_gain, jet_speed, sources, source_rate):
    slab_len = populations.shape[1]
    band_width = populations.shape[2]
    height = populations.shape[3]
    offset_len = lax.axis_index("len") * slab_len
    offset_band = lax.axis_index("band") * band_width
    length_total = slab_len * lax.axis_size("len")
    solid_flag = solid_mask == 1
    coord_x = offset_len + jnp.arange(slab_len, dtype=jnp.int32)[:, None, None]
    coord_y = offset_band + jnp.arange(band_width, dtype=jnp.int32)[None, :, None]
    coord_z = jnp.arange(height, dtype=jnp.int32)[None, None, :]
    discs = fan_discs(fan_hubs, coord_x, coord_y, coord_z, length_total)
    released = source_release(
        sources, source_rate, offset_len, offset_band, slab_len, band_width, height
    )
    for repeat in range(ITERS):
        density, velocity = moments(populations)
        partials = partial_flow(discs, velocity, solid_flag)
        totals = lax.psum(partials, ("len", "band"))
        force_field = force_from(discs, totals, fan_gain, jet_speed)
        posts = collide(populations, density, velocity, force_field, solid_flag)
        rimmed = extended_2(smoke_field, (("len", 0), ("band", 1)), 1)
        extended = extended_2(posts, (("len", 1), ("band", 2)), 1)
        read = stream_rimmed(extended, slab_len, band_width)
        ahead_x = rimmed[2:, 1:-1]
        behind_x = rimmed[:-2, 1:-1]
        ahead_y = rimmed[1:-1, 2:]
        behind_y = rimmed[1:-1, :-2]
        smoke_field = advance(
            smoke_field,
            ahead_x,
            behind_x,
            ahead_y,
            behind_y,
            shift_height(smoke_field, -1),
            shift_height(smoke_field, 1),
            velocity,
            solid_flag,
        )
        smoke_field = smoke_field + released
        populations = read
    return (populations, smoke_field)


def solution(mesh):
    placed = (
        P(None, "len", "band", None),
        P("len", "band", None),
        P("len", "band", None),
        P(),
        P(),
        P(),
        P(),
        P(),
    )
    return jax.shard_map(
        body,
        mesh=mesh,
        in_specs=placed,
        out_specs=(P(None, "len", "band", None), P("len", "band", None)),
        check_vma=False,
    )
```

profile of v0, /device:TPU:0, one launch (start us, length us, event | category | flops | bytes accessed | tf_op | source)
XLA Modules:
  0.0 521.5 jit_solution(3188985013215620775)
XLA Ops:
  1.3 6.9 %collective-permute-start.12 = (f32[1,16,128]{2,0,1:T(1,128)S(1)}, f32[1,16,128]{2,0,1:T(1,128)S(1)}, u32[]{:S(2)}, u32[]{:S(2)}) collective-permute-start(f32[1,16,128]{2,0,1:T(1,128)S(1)} %bitcast.685), channel_id=1, source_target_pairs={{2,0},{4,2},{6,4},{8,6},{10,8},{12,10},{14,12},{16,14},{18,16},{20... | collective-permute-start | bytes 24584 | tf_op jit(solution)/shard_map/ppermute | solution.py:47
  38.7 40.0 %psum.21 = f32[8]{0:T(128)S(1)} all-reduce(f32[8]{0:T(128)S(1)} %stack.324), channel_id=1, replica_groups=mesh['len'=16,'band'=2] {'len','band'}, use_global_device_ids=true, to_apply=%region_9.10 | all-reduce | flops 8 | bytes 64 | tf_op jit(solution)/shard_map/psum | solution.py:190
  85.1 5.2 %constant_dynamic-update-slice_fusion.18 = (f32[19,8,16,128]{3,1,2,0:T(8,128)S(1)}, f32[8,16,128]{2,0,1:T(8,128)S(1)}, f32[8,16,128]{2,0,1:T(8,128)S(1)}) fusion(pred[8,16,128]{2,0,1:T(8,128)(4,1)S(1)} %get-tuple-element.62, f32[]{:T(128)} %bitcast.58, pred[16,128]{1,0:T(8,128)(4,1)S(1)} %add_compare_fusion, pred[8]{0:T(512)(128)(4,1)S(1)} %get-tuple-element.218, ...), kind=kLoop, calls=%fused_computation.18 | loop fusion | flops 786431 | bytes 557152
  90.4 5.2 %constant_dynamic-update-slice_fusion.17 = f32[19,8,16,128]{3,1,2,0:T(8,128)S(1)} fusion(f32[19,8,16,128]{3,1,2,0:T(8,128)S(1)} %get-tuple-element.77, pred[8,16,128]{2,0,1:T(8,128)(4,1)S(1)} %get-tuple-element.62, f32[8,16,128]{2,0,1:T(8,128)S(1)} %get-tuple-element.79, f32[1,8,16,128]{3,2,1,0:T(8,128)S(1)} %get-tuple-element.139, ...), kind=kLoop, calls=%fused_computation.17 | loop fusion | flops 671744 | bytes 561184
  95.6 5.2 %constant_dynamic-update-slice_fusion.16 = f32[19,8,16,128]{3,1,2,0:T(8,128)S(1)} fusion(f32[19,8,16,128]{3,1,2,0:T(8,128)S(1)} %constant_dynamic-update-slice_fusion.17, pred[8,16,128]{2,0,1:T(8,128)(4,1)S(1)} %get-tuple-element.62, f32[8,16,128]{2,0,1:T(8,128)S(1)} %get-tuple-element.79, f32[1,8,16,128]{3,2,1,0:T(8,128)S(1)} %get-tuple-element.139, ...), kind=kLoop, calls=%fused_computation.16 | loop fusion | flops 688128 | bytes 561184
  100.8 5.2 %constant_dynamic-update-slice_fusion.15 = f32[19,8,16,128]{3,1,2,0:T(8,128)S(1)} fusion(f32[19,8,16,128]{3,1,2,0:T(8,128)S(1)} %constant_dynamic-update-slice_fusion.16, pred[8,16,128]{2,0,1:T(8,128)(4,1)S(1)} %get-tuple-element.62, f32[8,16,128]{2,0,1:T(8,128)S(1)} %get-tuple-element.79, f32[1,8,16,128]{3,2,1,0:T(8,128)S(1)} %get-tuple-element.129, ...), kind=kLoop, calls=%fused_computation.15 | loop fusion | flops 671744 | bytes 561184
  106.1 5.2 %constant_dynamic-update-slice_fusion.14 = f32[19,8,16,128]{3,1,2,0:T(8,128)S(1)} fusion(f32[19,8,16,128]{3,1,2,0:T(8,128)S(1)} %constant_dynamic-update-slice_fusion.15, pred[8,16,128]{2,0,1:T(8,128)(4,1)S(1)} %get-tuple-element.62, f32[8,16,128]{2,0,1:T(8,128)S(1)} %get-tuple-element.79, f32[1,8,16,128]{3,2,1,0:T(8,128)S(1)} %get-tuple-element.129, ...), kind=kLoop, calls=%fused_computation.14 | loop fusion | flops 688128 | bytes 561184
  111.3 5.2 %constant_dynamic-update-slice_fusion.13 = (f32[19,8,16,128]{3,1,2,0:T(8,128)S(1)}, f32[8,16,128]{2,0,1:T(8,128)S(1)}) fusion(f32[19,8,16,128]{3,1,2,0:T(8,128)S(1)} %constant_dynamic-update-slice_fusion.14, pred[8,16,128]{2,0,1:T(8,128)(4,1)S(1)} %get-tuple-element.62, f32[]{:T(128)} %bitcast.58, pred[16,128]{1,0:T(8,128)(4,1)S(1)} %add_compare_fusion, ...), kind=kLoop, calls=%fused_computation.13 | loop fusion | flops 671744 | bytes 626720
  116.6 5.2 %constant_dynamic-update-slice_fusion.12 = (f32[19,8,16,128]{3,1,2,0:T(8,128)S(1)}, f32[8,16,128]{2,0,1:T(8,128)S(1)}) fusion(f32[19,8,16,128]{3,1,2,0:T(8,128)S(1)} %get-tuple-element.75, pred[8,16,128]{2,0,1:T(8,128)(4,1)S(1)} %get-tuple-element.62, f32[]{:T(128)} %bitcast.58, pred[16,128]{1,0:T(8,128)(4,1)S(1)} %add_compare_fusion, ...), kind=kLoop, calls=%fused_computation.12 | loop fusion | flops 688128 | bytes 626720
  121.8 5.2 %constant_dynamic-update-slice_fusion.11 = f32[19,8,16,128]{3,1,2,0:T(8,128)S(1)} fusion(f32[19,8,16,128]{3,1,2,0:T(8,128)S(1)} %get-tuple-element.73, pred[8,16,128]{2,0,1:T(8,128)(4,1)S(1)} %get-tuple-element.62, f32[8,16,128]{2,0,1:T(8,128)S(1)} %get-tuple-element.79, f32[8,16,128]{2,0,1:T(8,128)S(1)} %get-tuple-element.59, ...), kind=kLoop, calls=%fused_computation.11 | loop fusion | flops 655360 | bytes 561184
  127.0 5.2 %constant_dynamic-update-slice_fusion.10 = f32[19,8,16,128]{3,1,2,0:T(8,128)S(1)} fusion(f32[19,8,16,128]{3,1,2,0:T(8,128)S(1)} %constant_dynamic-update-slice_fusion.11, pred[8,16,128]{2,0,1:T(8,128)(4,1)S(1)} %get-tuple-element.62, f32[8,16,128]{2,0,1:T(8,128)S(1)} %get-tuple-element.79, f32[8,16,128]{2,0,1:T(8,128)S(1)} %get-tuple-element.60, ...), kind=kLoop, calls=%fused_computation.10 | loop fusion | flops 688128 | bytes 561184
  132.3 5.2 %constant_dynamic-update-slice_fusion.9 = f32[19,8,16,128]{3,1,2,0:T(8,128)S(1)} fusion(f32[19,8,16,128]{3,1,2,0:T(8,128)S(1)} %constant_dynamic-update-slice_fusion.10, pred[8,16,128]{2,0,1:T(8,128)(4,1)S(1)} %get-tuple-element.62, f32[8,16,128]{2,0,1:T(8,128)S(1)} %get-tuple-element.79, f32[8,16,128]{2,0,1:T(8,128)S(1)} %get-tuple-element.59, ...), kind=kLoop, calls=%fused_computation.9 | loop fusion | flops 671744 | bytes 561184
  137.5 5.2 %constant_dynamic-update-slice_fusion.8 = f32[19,8,16,128]{3,1,2,0:T(8,128)S(1)} fusion(f32[19,8,16,128]{3,1,2,0:T(8,128)S(1)} %constant_dynamic-update-slice_fusion.9, pred[8,16,128]{2,0,1:T(8,128)(4,1)S(1)} %get-tuple-element.62, f32[8,16,128]{2,0,1:T(8,128)S(1)} %get-tuple-element.79, f32[8,16,128]{2,0,1:T(8,128)S(1)} %get-tuple-element.60, ...), kind=kLoop, calls=%fused_computation.8 | loop fusion | flops 671744 | bytes 561184
  142.8 5.2 %constant_dynamic-update-slice_fusion.7 = f32[19,8,16,128]{3,1,2,0:T(8,128)S(1)} fusion(f32[19,8,16,128]{3,1,2,0:T(8,128)S(1)} %constant_dynamic-update-slice_fusion.8, pred[8,16,128]{2,0,1:T(8,128)(4,1)S(1)} %get-tuple-element.62, f32[8,16,128]{2,0,1:T(8,128)S(1)} %get-tuple-element.79, f32[8,16,128]{2,0,1:T(8,128)S(1)} %get-tuple-element.61, ...), kind=kLoop, calls=%fused_computation.7 | loop fusion | flops 655360 | bytes 561184
  148.0 5.2 %constant_dynamic-update-slice_fusion.6 = f32[19,8,16,128]{3,1,2,0:T(8,128)S(1)} fusion(f32[19,8,16,128]{3,1,2,0:T(8,128)S(1)} %constant_dynamic-update-slice_fusion.7, pred[8,16,128]{2,0,1:T(8,128)(4,1)S(1)} %get-tuple-element.62, f32[8,16,128]{2,0,1:T(8,128)S(1)} %get-tuple-element.79, f32[1,8,16,128]{3,2,1,0:T(8,128)S(1)} %get-tuple-element.136, ...), kind=kLoop, calls=%fused_computation.6 | loop fusion | flops 688128 | bytes 561184
  153.2 5.2 %constant_dynamic-update-slice_fusion.5 = f32[19,8,16,128]{3,1,2,0:T(8,128)S(1)} fusion(f32[19,8,16,128]{3,1,2,0:T(8,128)S(1)} %constant_dynamic-update-slice_fusion.6, pred[8,16,128]{2,0,1:T(8,128)(4,1)S(1)} %get-tuple-element.62, f32[8,16,128]{2,0,1:T(8,128)S(1)} %get-tuple-element.79, f32[1,8,16,128]{3,2,1,0:T(8,128)S(1)} %get-tuple-element.135, ...), kind=kLoop, calls=%fused_computation.5 | loop fusion | flops 671744 | bytes 561184
  158.5 5.2 %constant_dynamic-update-slice_fusion.4 = f32[19,8,16,128]{3,1,2,0:T(8,128)S(1)} fusion(f32[19,8,16,128]{3,1,2,0:T(8,128)S(1)} %constant_dynamic-update-slice_fusion.5, pred[8,16,128]{2,0,1:T(8,128)(4,1)S(1)} %get-tuple-element.62, f32[8,16,128]{2,0,1:T(8,128)S(1)} %get-tuple-element.79, f32[8,16,128]{2,0,1:T(8,128)S(1)} %get-tuple-element.61, ...), kind=kLoop, calls=%fused_computation.4 | loop fusion | flops 671744 | bytes 561184
  163.7 5.2 %constant_dynamic-update-slice_fusion.3 = f32[19,8,16,128]{3,1,2,0:T(8,128)S(1)} fusion(f32[19,8,16,128]{3,1,2,0:T(8,128)S(1)} %constant_dynamic-update-slice_fusion.4, pred[8,16,128]{2,0,1:T(8,128)(4,1)S(1)} %get-tuple-element.62, f32[8,16,128]{2,0,1:T(8,128)S(1)} %get-tuple-element.79, f32[8,16,128]{2,0,1:T(8,128)S(1)} %get-tuple-element.61, ...), kind=kLoop, calls=%fused_computation.3 | loop fusion | flops 655360 | bytes 561184
  169.0 5.2 %constant_dynamic-update-slice_fusion.2 = f32[19,8,16,128]{3,1,2,0:T(8,128)S(1)} fusion(f32[19,8,16,128]{3,1,2,0:T(8,128)S(1)} %constant_dynamic-update-slice_fusion.3, pred[8,16,128]{2,0,1:T(8,128)(4,1)S(1)} %get-tuple-element.62, f32[8,16,128]{2,0,1:T(8,128)S(1)} %get-tuple-element.79, f32[1,8,16,128]{3,2,1,0:T(8,128)S(1)} %get-tuple-element.128, ...), kind=kLoop, calls=%fused_computation.2 | loop fusion | flops 688128 | bytes 561184
  174.2 5.2 %constant_dynamic-update-slice_fusion.1 = f32[19,8,16,128]{3,1,2,0:T(8,128)S(1)} fusion(f32[19,8,16,128]{3,1,2,0:T(8,128)S(1)} %constant_dynamic-update-slice_fusion.2, pred[8,16,128]{2,0,1:T(8,128)(4,1)S(1)} %get-tuple-element.62, f32[8,16,128]{2,0,1:T(8,128)S(1)} %get-tuple-element.79, f32[1,8,16,128]{3,2,1,0:T(8,128)S(1)} %get-tuple-element.127, ...), kind=kLoop, calls=%fused_computation.1 | loop fusion | flops 671744 | bytes 561184
  179.4 5.2 %constant_dynamic-update-slice_fusion = f32[19,8,16,128]{3,1,2,0:T(8,128)S(1)} fusion(f32[19,8,16,128]{3,1,2,0:T(8,128)S(1)} %constant_dynamic-update-slice_fusion.1, pred[8,16,128]{2,0,1:T(8,128)(4,1)S(1)} %get-tuple-element.62, f32[8,16,128]{2,0,1:T(8,128)S(1)} %get-tuple-element.79, f32[8,16,128]{2,0,1:T(8,128)S(1)} %get-tuple-element.61, ...), kind=kLoop, calls=%fused_computation | loop fusion | flops 671744 | bytes 561184 | tf_op jit(solution)/shard_map/stack | solution.py:79
  185.0 5.6 %collective-permute-start.1 = (f32[19,1,16,128]{3,1,2,0:T(1,128)S(1)}, f32[19,1,16,128]{3,1,2,0:T(1,128)S(1)}, u32[]{:S(2)}, u32[]{:S(2)}) collective-permute-start(f32[19,1,16,128]{3,1,2,0:T(1,128)S(1)} %get-tuple-element.121), channel_id=1, source_target_pairs={{2,0},{4,2},{6,4},{8,6},{10,8},{12,10},{14,12},{16,14},{18,16},{20... | collective-permute-start | bytes 466952 | tf_op jit(solution)/shard_map/ppermute | solution.py:47
  202.2 39.9 %psum.22 = f32[8]{0:T(128)S(1)} all-reduce(f32[8]{0:T(128)S(1)} %stack.353), channel_id=1, replica_groups=mesh['len'=16,'band'=2] {'len','band'}, use_global_device_ids=true, to_apply=%region_18.19 | all-reduce | flops 8 | bytes 64 | tf_op jit(solution)/shard_map/psum | solution.py:190
  258.9 5.2 %constant_dynamic-update-slice_fusion.35 = f32[19,8,16,128]{3,1,2,0:T(8,128)S(1)} fusion(f32[19,8,16,128]{3,1,2,0:T(8,128)S(1)} %constant_dynamic-update-slice_fusion.36, pred[8,16,128]{2,0,1:T(8,128)(4,1)S(1)} %get-tuple-element.62, f32[8,16,128]{2,0,1:T(8,128)S(1)} %get-tuple-element.50, f32[8,16,128]{2,0,1:T(8,128)S(1)} %get-tuple-element.51, ...), kind=kLoop, calls=%fused_computation.35 | loop fusion | flops 786432 | bytes 495648
  269.3 5.2 %constant_dynamic-update-slice_fusion.33 = f32[19,8,16,128]{3,1,2,0:T(8,128)S(1)} fusion(f32[19,8,16,128]{3,1,2,0:T(8,128)S(1)} %constant_dynamic-update-slice_fusion.34, pred[8,16,128]{2,0,1:T(8,128)(4,1)S(1)} %get-tuple-element.62, f32[8,16,128]{2,0,1:T(8,128)S(1)} %get-tuple-element.52, f32[8,16,128]{2,0,1:T(8,128)S(1)} %get-tuple-element.53, ...), kind=kLoop, calls=%fused_computation.33 | loop fusion | flops 786432 | bytes 495648
  274.6 5.2 %constant_dynamic-update-slice_fusion.32 = (f32[19,8,16,128]{3,1,2,0:T(8,128)S(1)}, f32[8,16,128]{2,0,1:T(8,128)S(1)}) fusion(f32[19,8,16,128]{3,1,2,0:T(8,128)S(1)} %constant_dynamic-update-slice_fusion.33, pred[8,16,128]{2,0,1:T(8,128)(4,1)S(1)} %get-tuple-element.62, f32[]{:T(128)} %bitcast.109, pred[16,128]{1,0:T(8,128)(4,1)S(1)} %add_compare_fusion, ...), kind=kLoop, calls=%fused_computation.32 | loop fusion | flops 770048 | bytes 561184
  279.8 5.2 %constant_dynamic-update-slice_fusion.31 = (f32[19,8,16,128]{3,1,2,0:T(8,128)S(1)}, f32[8,16,128]{2,0,1:T(8,128)S(1)}) fusion(f32[19,8,16,128]{3,1,2,0:T(8,128)S(1)} %get-tuple-element.69, pred[8,16,128]{2,0,1:T(8,128)(4,1)S(1)} %get-tuple-element.62, f32[]{:T(128)} %bitcast.109, pred[16,128]{1,0:T(8,128)(4,1)S(1)} %add_compare_fusion, ...), kind=kLoop, calls=%fused_computation.31 | loop fusion | flops 786432 | bytes 561184
  290.2 5.2 %constant_dynamic-update-slice_fusion.29 = f32[19,8,16,128]{3,1,2,0:T(8,128)S(1)} fusion(f32[19,8,16,128]{3,1,2,0:T(8,128)S(1)} %constant_dynamic-update-slice_fusion.30, pred[8,16,128]{2,0,1:T(8,128)(4,1)S(1)} %get-tuple-element.62, f32[8,16,128]{2,0,1:T(8,128)S(1)} %get-tuple-element.54, f32[8,16,128]{2,0,1:T(8,128)S(1)} %get-tuple-element.55, ...), kind=kLoop, calls=%fused_computation.29 | loop fusion | flops 786432 | bytes 495648
  305.9 5.2 %constant_dynamic-update-slice_fusion.26 = f32[19,8,16,128]{3,1,2,0:T(8,128)S(1)} fusion(f32[19,8,16,128]{3,1,2,0:T(8,128)S(1)} %constant_dynamic-update-slice_fusion.27, pred[8,16,128]{2,0,1:T(8,128)(4,1)S(1)} %get-tuple-element.62, f32[8,16,128]{2,0,1:T(8,128)S(1)} %get-tuple-element.48, f32[8,16,127]{2,0,1:T(8,128)S(1)} %slice.893, ...), kind=kLoop, calls=%fused_computation.26 | loop fusion | flops 753664 | bytes 495648
  311.1 5.2 %constant_dynamic-update-slice_fusion.25 = f32[19,8,16,128]{3,1,2,0:T(8,128)S(1)} fusion(f32[19,8,16,128]{3,1,2,0:T(8,128)S(1)} %constant_dynamic-update-slice_fusion.26, pred[8,16,128]{2,0,1:T(8,128)(4,1)S(1)} %get-tuple-element.62, f32[8,16,128]{2,0,1:T(8,128)S(1)} %get-tuple-element.48, f32[8,16,127]{2,0,1:T(8,128)S(1)} %slice.893, ...), kind=kLoop, calls=%fused_computation.25 | loop fusion | flops 786432 | bytes 495648
  316.3 5.2 %constant_dynamic-update-slice_fusion.24 = f32[19,8,16,128]{3,1,2,0:T(8,128)S(1)} fusion(f32[19,8,16,128]{3,1,2,0:T(8,128)S(1)} %constant_dynamic-update-slice_fusion.25, pred[8,16,128]{2,0,1:T(8,128)(4,1)S(1)} %get-tuple-element.62, f32[8,16,128]{2,0,1:T(8,128)S(1)} %get-tuple-element.48, f32[8,16,127]{2,0,1:T(8,128)S(1)} %bitcast.673, ...), kind=kLoop, calls=%fused_computation.24 | loop fusion | flops 770048 | bytes 495648
  321.5 5.2 %constant_dynamic-update-slice_fusion.23 = f32[19,8,16,128]{3,1,2,0:T(8,128)S(1)} fusion(f32[19,8,16,128]{3,1,2,0:T(8,128)S(1)} %constant_dynamic-update-slice_fusion.24, pred[8,16,128]{2,0,1:T(8,128)(4,1)S(1)} %get-tuple-element.62, f32[8,16,128]{2,0,1:T(8,128)S(1)} %get-tuple-element.48, f32[8,16,127]{2,0,1:T(8,128)S(1)} %bitcast.674, ...), kind=kLoop, calls=%fused_computation.23 | loop fusion | flops 770048 | bytes 495648
  326.8 5.2 %constant_dynamic-update-slice_fusion.22 = f32[19,8,16,128]{3,1,2,0:T(8,128)S(1)} fusion(f32[19,8,16,128]{3,1,2,0:T(8,128)S(1)} %constant_dynamic-update-slice_fusion.23, pred[8,16,128]{2,0,1:T(8,128)(4,1)S(1)} %get-tuple-element.62, f32[8,16,128]{2,0,1:T(8,128)S(1)} %get-tuple-element.48, f32[8,16,127]{2,0,1:T(8,128)S(1)} %slice.897, ...), kind=kLoop, calls=%fused_computation.22 | loop fusion | flops 753664 | bytes 495648
  332.0 5.2 %constant_dynamic-update-slice_fusion.21 = f32[19,8,16,128]{3,1,2,0:T(8,128)S(1)} fusion(f32[19,8,16,128]{3,1,2,0:T(8,128)S(1)} %constant_dynamic-update-slice_fusion.22, pred[8,16,128]{2,0,1:T(8,128)(4,1)S(1)} %get-tuple-element.62, f32[8,16,128]{2,0,1:T(8,128)S(1)} %get-tuple-element.48, f32[8,16,127]{2,0,1:T(8,128)S(1)} %slice.897, ...), kind=kLoop, calls=%fused_computation.21 | loop fusion | flops 786432 | bytes 495648
  337.2 5.2 %constant_dynamic-update-slice_fusion.20 = f32[19,8,16,128]{3,1,2,0:T(8,128)S(1)} fusion(f32[19,8,16,128]{3,1,2,0:T(8,128)S(1)} %constant_dynamic-update-slice_fusion.21, pred[8,16,128]{2,0,1:T(8,128)(4,1)S(1)} %get-tuple-element.62, f32[8,16,128]{2,0,1:T(8,128)S(1)} %get-tuple-element.48, f32[8,16,127]{2,0,1:T(8,128)S(1)} %bitcast.658, ...), kind=kLoop, calls=%fused_computation.20 | loop fusion | flops 770048 | bytes 495648
  342.4 5.2 %constant_dynamic-update-slice_fusion.19 = f32[19,8,16,128]{3,1,2,0:T(8,128)S(1)} fusion(f32[19,8,16,128]{3,1,2,0:T(8,128)S(1)} %constant_dynamic-update-slice_fusion.20, pred[8,16,128]{2,0,1:T(8,128)(4,1)S(1)} %get-tuple-element.62, f32[8,16,128]{2,0,1:T(8,128)S(1)} %get-tuple-element.48, f32[8,16,127]{2,0,1:T(8,128)S(1)} %bitcast.659, ...), kind=kLoop, calls=%fused_computation.19 | loop fusion | flops 770048 | bytes 495648 | tf_op jit(solution)/shard_map/stack | solution.py:79
  347.9 5.6 %collective-permute-start.5 = (f32[19,1,16,128]{3,1,2,0:T(1,128)S(1)}, f32[19,1,16,128]{3,1,2,0:T(1,128)S(1)}, u32[]{:S(2)}, u32[]{:S(2)}) collective-permute-start(f32[19,1,16,128]{3,1,2,0:T(1,128)S(1)} %get-tuple-element.118), channel_id=1, source_target_pairs={{2,0},{4,2},{6,4},{8,6},{10,8},{12,10},{14,12},{16,14},{18,16},{20... | collective-permute-start | bytes 466952 | tf_op jit(solution)/shard_map/ppermute | solution.py:47
  365.2 40.1 %psum.23 = f32[8]{0:T(128)S(1)} all-reduce(f32[8]{0:T(128)S(1)} %stack.382), channel_id=1, replica_groups=mesh['len'=16,'band'=2] {'len','band'}, use_global_device_ids=true, to_apply=%region_27.28 | all-reduce | flops 8 | bytes 64 | tf_op jit(solution)/shard_map/psum | solution.py:190
  432.2 5.2 %constant_dynamic-update-slice_fusion.51 = (f32[19,8,16,128]{3,1,2,0:T(8,128)S(1)}, f32[8,16,128]{2,0,1:T(8,128)S(1)}) fusion(f32[19,8,16,128]{3,1,2,0:T(8,128)S(1)} %constant_dynamic-update-slice_fusion.52, pred[8,16,128]{2,0,1:T(8,128)(4,1)S(1)} %get-tuple-element.62, f32[]{:T(128)} %bitcast.160, pred[16,128]{1,0:T(8,128)(4,1)S(1)} %add_compare_fusion, ...), kind=kLoop, calls=%fused_computation.51 | loop fusion | flops 770048 | bytes 561184
  437.4 5.2 %constant_dynamic-update-slice_fusion.50 = (f32[19,8,16,128]{3,1,2,0:T(8,128)S(1)}, f32[8,16,128]{2,0,1:T(8,128)S(1)}) fusion(f32[19,8,16,128]{3,1,2,0:T(8,128)S(1)} %get-tuple-element.65, pred[8,16,128]{2,0,1:T(8,128)(4,1)S(1)} %get-tuple-element.62, f32[]{:T(128)} %bitcast.160, pred[16,128]{1,0:T(8,128)(4,1)S(1)} %add_compare_fusion, ...), kind=kLoop, calls=%fused_computation.50 | loop fusion | flops 786432 | bytes 561184
  463.5 5.2 %constant_dynamic-update-slice_fusion.45 = f32[19,8,16,128]{3,1,2,0:T(8,128)S(1)} fusion(f32[19,8,16,128]{3,1,2,0:T(8,128)S(1)} %constant_dynamic-update-slice_fusion.46, pred[8,16,128]{2,0,1:T(8,128)(4,1)S(1)} %get-tuple-element.62, f32[8,16,128]{2,0,1:T(8,128)S(1)} %get-tuple-element.35, f32[8,16,127]{2,0,1:T(8,128)S(1)} %slice.905, ...), kind=kLoop, calls=%fused_computation.45 | loop fusion | flops 753664 | bytes 495648
  468.7 5.2 %constant_dynamic-update-slice_fusion.44 = f32[19,8,16,128]{3,1,2,0:T(8,128)S(1)} fusion(f32[19,8,16,128]{3,1,2,0:T(8,128)S(1)} %constant_dynamic-update-slice_fusion.45, pred[8,16,128]{2,0,1:T(8,128)(4,1)S(1)} %get-tuple-element.62, f32[8,16,128]{2,0,1:T(8,128)S(1)} %get-tuple-element.35, f32[8,16,127]{2,0,1:T(8,128)S(1)} %slice.905, ...), kind=kLoop, calls=%fused_computation.44 | loop fusion | flops 786432 | bytes 495648
  473.9 5.2 %constant_dynamic-update-slice_fusion.43 = f32[19,8,16,128]{3,1,2,0:T(8,128)S(1)} fusion(f32[19,8,16,128]{3,1,2,0:T(8,128)S(1)} %constant_dynamic-update-slice_fusion.44, pred[8,16,128]{2,0,1:T(8,128)(4,1)S(1)} %get-tuple-element.62, f32[8,16,128]{2,0,1:T(8,128)S(1)} %get-tuple-element.35, f32[8,16,127]{2,0,1:T(8,128)S(1)} %bitcast.676, ...), kind=kLoop, calls=%fused_computation.43 | loop fusion | flops 770048 | bytes 495648
  479.1 5.2 %constant_dynamic-update-slice_fusion.42 = f32[19,8,16,128]{3,1,2,0:T(8,128)S(1)} fusion(f32[19,8,16,128]{3,1,2,0:T(8,128)S(1)} %constant_dynamic-update-slice_fusion.43, pred[8,16,128]{2,0,1:T(8,128)(4,1)S(1)} %get-tuple-element.62, f32[8,16,128]{2,0,1:T(8,128)S(1)} %get-tuple-element.35, f32[8,16,127]{2,0,1:T(8,128)S(1)} %bitcast.677, ...), kind=kLoop, calls=%fused_computation.42 | loop fusion | flops 770048 | bytes 495648
  484.4 5.2 %constant_dynamic-update-slice_fusion.41 = f32[19,8,16,128]{3,1,2,0:T(8,128)S(1)} fusion(f32[19,8,16,128]{3,1,2,0:T(8,128)S(1)} %constant_dynamic-update-slice_fusion.42, pred[8,16,128]{2,0,1:T(8,128)(4,1)S(1)} %get-tuple-element.62, f32[8,16,128]{2,0,1:T(8,128)S(1)} %get-tuple-element.35, f32[8,16,127]{2,0,1:T(8,128)S(1)} %slice.909, ...), kind=kLoop, calls=%fused_computation.41 | loop fusion | flops 753664 | bytes 495648
  489.6 5.2 %constant_dynamic-update-slice_fusion.40 = f32[19,8,16,128]{3,1,2,0:T(8,128)S(1)} fusion(f32[19,8,16,128]{3,1,2,0:T(8,128)S(1)} %constant_dynamic-update-slice_fusion.41, pred[8,16,128]{2,0,1:T(8,128)(4,1)S(1)} %get-tuple-element.62, f32[8,16,128]{2,0,1:T(8,128)S(1)} %get-tuple-element.35, f32[8,16,127]{2,0,1:T(8,128)S(1)} %slice.909, ...), kind=kLoop, calls=%fused_computation.40 | loop fusion | flops 786432 | bytes 495648
  494.8 5.2 %constant_dynamic-update-slice_fusion.39 = f32[19,8,16,128]{3,1,2,0:T(8,128)S(1)} fusion(f32[19,8,16,128]{3,1,2,0:T(8,128)S(1)} %constant_dynamic-update-slice_fusion.40, pred[8,16,128]{2,0,1:T(8,128)(4,1)S(1)} %get-tuple-element.62, f32[8,16,128]{2,0,1:T(8,128)S(1)} %get-tuple-element.35, f32[8,16,127]{2,0,1:T(8,128)S(1)} %bitcast.655, ...), kind=kLoop, calls=%fused_computation.39 | loop fusion | flops 770048 | bytes 495648
  500.0 5.2 %constant_dynamic-update-slice_fusion.38 = f32[19,8,16,128]{3,1,2,0:T(8,128)S(1)} fusion(f32[19,8,16,128]{3,1,2,0:T(8,128)S(1)} %constant_dynamic-update-slice_fusion.39, pred[8,16,128]{2,0,1:T(8,128)(4,1)S(1)} %get-tuple-element.62, f32[8,16,128]{2,0,1:T(8,128)S(1)} %get-tuple-element.35, f32[8,16,127]{2,0,1:T(8,128)S(1)} %bitcast.656, ...), kind=kLoop, calls=%fused_computation.38 | loop fusion | flops 770048 | bytes 495648 | tf_op jit(solution)/shard_map/stack | solution.py:79
  (173 shorter events, 162.4 us)
Async XLA Ops:
  1.3 28.6 %collective-permute-start.12 = (f32[1,16,128]{2,0,1:T(1,128)S(1)}, f32[1,16,128]{2,0,1:T(1,128)S(1)}, u32[]{:S(2)}, u32[]{:S(2)}) collective-permute-start(f32[1,16,128]{2,0,1:T(1,128)S(1)} %bitcast.685), channel_id=1, source_target_pairs={{2,0},{4,2},{6,4},{8,6},{10,8},{12,10},{14,12},{16,14},{18,16},{20... | collective-permute-start | bytes 24584 | tf_op jit(solution)/shard_map/ppermute | solution.py:47
  8.3 21.7 %collective-permute-start.13 = (f32[1,16,128]{2,0,1:T(1,128)S(1)}, f32[1,16,128]{2,0,1:T(1,128)S(1)}, u32[]{:S(2)}, u32[]{:S(2)}) collective-permute-start(f32[1,16,128]{2,0,1:T(1,128)S(1)} %bitcast.684), channel_id=1, source_target_pairs={{0,2},{2,4},{4,6},{6,8},{8,10},{10,12},{12,14},{14,16},{16,18},{18... | collective-permute-start | bytes 24584 | tf_op jit(solution)/shard_map/ppermute | solution.py:45
  18.8 13.0 %copy-start = (f32[19,8,16,128]{3,2,1,0:T(8,128)S(1)}, f32[19,8,16,128]{3,2,1,0:T(8,128)}, u32[]{:S(2)}) copy-start(f32[19,8,16,128]{3,2,1,0:T(8,128)} %param.8) | copy-start | bytes 3735556
  20.4 11.6 %copy-start.3 = (s32[8,16,128]{2,1,0:T(8,128)S(1)}, s32[8,16,128]{2,1,0:T(8,128)}, u32[]{:S(2)}) copy-start(s32[8,16,128]{2,1,0:T(8,128)} %param.9) | copy-start | bytes 196612
  20.4 11.6 %copy-start.4 = (f32[16]{0:T(128)S(1)}, f32[16]{0:T(128)}, u32[]{:S(2)}) copy-start(f32[16]{0:T(128)} %param.15) | copy-start | bytes 196
  30.0 2.0 collective-permute-start.14
  30.1 1.9 collective-permute-start.15
  31.9 46.8 %copy-start.1 = (f32[8]{0:T(128)S(1)}, f32[8]{0:T(128)}, u32[]{:S(2)}) copy-start(f32[8]{0:T(128)} %param.12) | copy-start | bytes 100
  32.0 46.8 %copy-start.2 = (f32[8]{0:T(128)S(1)}, f32[8]{0:T(128)}, u32[]{:S(2)}) copy-start(f32[8]{0:T(128)} %param.13) | copy-start | bytes 100
  79.5 111.3 %collective-permute-start.17 = (f32[1,16,128]{2,0,1:T(1,128)S(1)}, f32[1,16,128]{2,0,1:T(1,128)S(1)}, u32[]{:S(2)}, u32[]{:S(2)}) collective-permute-start(f32[1,16,128]{2,0,1:T(1,128)S(1)} %get-tuple-element.151), channel_id=1, source_target_pairs={{0,2},{2,4},{4,6},{6,8},{8,10},{10,12},{12,14},{14,16},{16,18},{18... | collective-permute-start | bytes 24584 | tf_op jit(solution)/shard_map/ppermute | solution.py:45
  81.8 108.9 %collective-permute-start.16 = (f32[1,16,128]{2,0,1:T(1,128)S(1)}, f32[1,16,128]{2,0,1:T(1,128)S(1)}, u32[]{:S(2)}, u32[]{:S(2)}) collective-permute-start(f32[1,16,128]{2,0,1:T(1,128)S(1)} %get-tuple-element.152), channel_id=1, source_target_pairs={{2,0},{4,2},{6,4},{8,6},{10,8},{12,10},{14,12},{16,14},{18,16},{20... | collective-permute-start | bytes 24584 | tf_op jit(solution)/shard_map/ppermute | solution.py:47
  184.9 9.0 %collective-permute-start = (f32[19,1,16,128]{3,1,2,0:T(1,128)S(1)}, f32[19,1,16,128]{3,1,2,0:T(1,128)S(1)}, u32[]{:S(2)}, u32[]{:S(2)}) collective-permute-start(f32[19,1,16,128]{3,1,2,0:T(1,128)S(1)} %get-tuple-element.120), channel_id=1, source_target_pairs={{0,2},{2,4},{4,6},{6,8},{8,10},{10,12},{12,14},{14,16},{16,18},{18... | collective-permute-start | bytes 466952 | tf_op jit(solution)/shard_map/ppermute | solution.py:45
  185.0 8.9 %collective-permute-start.1 = (f32[19,1,16,128]{3,1,2,0:T(1,128)S(1)}, f32[19,1,16,128]{3,1,2,0:T(1,128)S(1)}, u32[]{:S(2)}, u32[]{:S(2)}) collective-permute-start(f32[19,1,16,128]{3,1,2,0:T(1,128)S(1)} %get-tuple-element.121), channel_id=1, source_target_pairs={{2,0},{4,2},{6,4},{8,6},{10,8},{12,10},{14,12},{16,14},{18,16},{20... | collective-permute-start | bytes 466952 | tf_op jit(solution)/shard_map/ppermute | solution.py:47
  190.8 5.1 collective-permute-start.18
  190.8 5.0 collective-permute-start.19
  193.9 1.4 collective-permute-start.2
  194.0 1.6 collective-permute-start.3
  242.8 110.9 %collective-permute-start.21 = (f32[1,16,128]{2,0,1:T(1,128)S(1)}, f32[1,16,128]{2,0,1:T(1,128)S(1)}, u32[]{:S(2)}, u32[]{:S(2)}) collective-permute-start(f32[1,16,128]{2,0,1:T(1,128)S(1)} %get-tuple-element.147), channel_id=1, source_target_pairs={{0,2},{2,4},{4,6},{6,8},{8,10},{10,12},{12,14},{14,16},{16,18},{18... | collective-permute-start | bytes 24584 | tf_op jit(solution)/shard_map/ppermute | solution.py:45
  245.1 108.6 %collective-permute-start.20 = (f32[1,16,128]{2,0,1:T(1,128)S(1)}, f32[1,16,128]{2,0,1:T(1,128)S(1)}, u32[]{:S(2)}, u32[]{:S(2)}) collective-permute-start(f32[1,16,128]{2,0,1:T(1,128)S(1)} %get-tuple-element.148), channel_id=1, source_target_pairs={{2,0},{4,2},{6,4},{8,6},{10,8},{12,10},{14,12},{16,14},{18,16},{20... | collective-permute-start | bytes 24584 | tf_op jit(solution)/shard_map/ppermute | solution.py:47
  347.9 9.0 %collective-permute-start.4 = (f32[19,1,16,128]{3,1,2,0:T(1,128)S(1)}, f32[19,1,16,128]{3,1,2,0:T(1,128)S(1)}, u32[]{:S(2)}, u32[]{:S(2)}) collective-permute-start(f32[19,1,16,128]{3,1,2,0:T(1,128)S(1)} %get-tuple-element.117), channel_id=1, source_target_pairs={{0,2},{2,4},{4,6},{6,8},{8,10},{10,12},{12,14},{14,16},{16,18},{18... | collective-permute-start | bytes 466952 | tf_op jit(solution)/shard_map/ppermute | solution.py:45
  347.9 8.9 %collective-permute-start.5 = (f32[19,1,16,128]{3,1,2,0:T(1,128)S(1)}, f32[19,1,16,128]{3,1,2,0:T(1,128)S(1)}, u32[]{:S(2)}, u32[]{:S(2)}) collective-permute-start(f32[19,1,16,128]{3,1,2,0:T(1,128)S(1)} %get-tuple-element.118), channel_id=1, source_target_pairs={{2,0},{4,2},{6,4},{8,6},{10,8},{12,10},{14,12},{16,14},{18,16},{20... | collective-permute-start | bytes 466952 | tf_op jit(solution)/shard_map/ppermute | solution.py:47
  353.7 5.1 collective-permute-start.22
  353.8 5.0 collective-permute-start.23
  356.9 1.4 collective-permute-start.6
  357.0 1.6 collective-permute-start.7
  505.5 6.8 %collective-permute-start.9 = (f32[19,1,16,128]{3,1,2,0:T(1,128)S(1)}, f32[19,1,16,128]{3,1,2,0:T(1,128)S(1)}, u32[]{:S(2)}, u32[]{:S(2)}) collective-permute-start(f32[19,1,16,128]{3,1,2,0:T(1,128)S(1)} %get-tuple-element.114), channel_id=1, source_target_pairs={{2,0},{4,2},{6,4},{8,6},{10,8},{12,10},{14,12},{16,14},{18,16},{20... | collective-permute-start | bytes 466952 | tf_op jit(solution)/shard_map/ppermute | solution.py:47
  508.6 8.8 %collective-permute-start.8 = (f32[19,1,16,128]{3,1,2,0:T(1,128)S(1)}, f32[19,1,16,128]{3,1,2,0:T(1,128)S(1)}, u32[]{:S(2)}, u32[]{:S(2)}) collective-permute-start(f32[19,1,16,128]{3,1,2,0:T(1,128)S(1)} %get-tuple-element.115), channel_id=1, source_target_pairs={{0,2},{2,4},{4,6},{6,8},{8,10},{10,12},{12,14},{14,16},{16,18},{18... | collective-permute-start | bytes 466952 | tf_op jit(solution)/shard_map/ppermute | solution.py:45
  517.4 1.7 collective-permute-start.11
  517.5 1.6 collective-permute-start.10
where the time goes:
time: 526 us; the launch traced here: 521 us
  other arithmetic  318 us (60%)
  blocking collectives  120 us (23%)
  starting transfers between devices  36.1 us (7%)
  local copies, waits for them, and re-layouts  28.6 us (5%)
  waiting for transfers between devices  16.1 us (3%)
    unnamed x60, other arithmetic  282 us
    psum x3, blocking collectives, body(): totals = lax.psum(partials, ('len', 'band'))  120 us
    ppermute x12, starting transfers between devices, extended_2(): lax.ppermute(head, axis, [((i + 1) % count, i) for i in range(count)])  29.2 us
    another operation x3, other arithmetic, collide(): return jnp.stack(posts)  15.7 us
    another operation x3, local copies, waits for them, and re-layouts, partial_flow(): jnp.stack([jnp.sum(jnp.where(disc_nodes & jnp.logical_not(solid_flag), ve...  15.3 us
    ppermute x12, waiting for transfers between devices, extended_2(): lax.ppermute(tail, axis, [(i, (i + 1) % count) for i in range(count)])  12.6 us
  transfers between devices with their start and end apart: 24, of which 9 were waited for; matrix products, arithmetic and copies ran while one was open for 43% of the time, Pallas kernels for 0%

commit v1 on v0

--- a/solution.py
+++ b/solution.py
@@ -1,6 +1,8 @@
 import jax
 import jax.numpy as jnp
 from jax import lax
+from jax.experimental import pallas as pl
+from jax.experimental.pallas import tpu as pltpu
 from jax.sharding import PartitionSpec as P
 
 RAD = 3
@@ -136,15 +138,42 @@
     return jnp.concatenate([field[..., 1:], zero_layer], axis=-1)
 
 
-def stream_rimmed(extended, slab_len, band_width):
-    moved = []
+def stream_kernel(extended_ref, out_ref):
+    slab_len, band_width, height = out_ref.shape[1:]
+    lane = lax.broadcasted_iota(jnp.int32, (slab_len, band_width, height), 2)
     for which in range(19):
         shift_x, shift_y, shift_z = VELOCITIES[which]
-        piece = extended[
+        piece = extended_ref[
             which, 1 - shift_x : 1 - shift_x + slab_len, 1 - shift_y : 1 - shift_y + band_width, :
         ]
-        moved.append(shift_height(piece, shift_z))
-    return jnp.stack(moved)
+        if shift_z == 1:
+            piece = jnp.where(lane == 0, 0.0, pltpu.roll(piece, 1, 2))
+        elif shift_z == -1:
+            piece = jnp.where(lane == height - 1, 0.0, pltpu.roll(piece, height - 1, 2))
+        out_ref[which] = piece
+
+
+def stream_rimmed(extended, slab_len, band_width):
+    shape = (19, slab_len, band_width, extended.shape[3])
+    return pl.pallas_call(
+        stream_kernel,
+        out_shape=jax.ShapeDtypeStruct(shape, jnp.float32),
+        in_specs=[pl.BlockSpec(memory_space=pltpu.VMEM)],
+        out_specs=pl.BlockSpec(memory_space=pltpu.VMEM),
+        cost_estimate=pl.CostEstimate(
+            flops=0, transcendentals=0, bytes_accessed=8 * extended.size
+        ),
+    )(extended)
+
+
+def window_sum(values, axis, width):
+    count = lax.axis_size(axis)
+    total = values
+    for offset in sorted(set(step % count for step in range(-width, width + 1)) - {0}):
+        total = total + lax.ppermute(
+            values, axis, [(i, (i + offset) % count) for i in range(count)]
+        )
+    return total
 
 
 def source_release(sources, source_rate, offset_len, offset_band, slab_len, band_width, height):
@@ -184,10 +213,12 @@
     released = source_release(
         sources, source_rate, offset_len, offset_band, slab_len, band_width, height
     )
+    len_reach = -(-(FAN_LEN - 1) // slab_len)
+    band_reach = -(-(2 * RAD) // band_width)
     for repeat in range(ITERS):
         density, velocity = moments(populations)
         partials = partial_flow(discs, velocity, solid_flag)
-        totals = lax.psum(partials, ("len", "band"))
+        totals = window_sum(window_sum(partials, "band", band_reach), "len", len_reach)
         force_field = force_from(discs, totals, fan_gain, jet_speed)
         posts = collide(populations, density, velocity, force_field, solid_flag)
         rimmed = extended_2(smoke_field, (("len", 0), ("band", 1)), 1)

time: 526 us -> 450 us (0.86)
  blocking collectives: 120 us -> 0 us
  waiting for transfers between devices: 16.1 us -> 45.7 us
  Pallas kernels: 0 us -> 8.78 us
  other arithmetic: 318 us -> 326 us
    psum x3 -> x0, blocking collectives: 120 us -> none  [body(): totals = lax.psum(partials, ('len', 'band'))]
    ppermute x0 -> x15, waiting for transfers between devices: none -> 20.2 us  [window_sum(): lax.ppermute(values, axis, [(i, (i + offset) % count) for i in range(coun...]
    ppermute x0 -> x15, starting transfers between devices: none -> 18.1 us  [window_sum(): lax.ppermute(values, axis, [(i, (i + offset) % count) for i in range(coun...]
    ppermute x12, starting transfers between devices: 29.2 us -> 11.3 us  [extended_2(): lax.ppermute(head, axis, [((i + 1) % count, i) for i in range(count)])]
    pallas_call x0 -> x3, Pallas kernels: none -> 8.78 us  [stream_rimmed(): pl.pallas_call(stream_kernel, out_shape=jax.ShapeDtypeStruct(shape, jnp.f...]
    ppermute x12, waiting for transfers between devices: 3.44 us -> 12.1 us  [extended_2(): lax.ppermute(head, axis, [((i + 1) % count, i) for i in range(count)])]
    unnamed x60 -> x54, other arithmetic: 282 us -> 280 us
  transfers between devices with their start and end apart: 24 -> 39, of which waited for: 9 -> 21; matrix products, arithmetic and copies ran while one was open for 43% -> 52% of each run, Pallas kernels for 0% -> 1%
where the time goes in v1:
time: 450 us; the launch traced here: 445 us
  other arithmetic  326 us (72%)
  waiting for transfers between devices  45.7 us (10%)
  starting transfers between devices  38.8 us (9%)
  local copies, waits for them, and re-layouts  24.1 us (5%)
  Pallas kernels  8.78 us (2%)
    unnamed x54, other arithmetic  280 us
    ppermute x15, waiting for transfers between devices, window_sum(): lax.ppermute(values, axis, [(i, (i + offset) % count) for i in range(coun...  20.2 us
    ppermute x15, starting transfers between devices, window_sum(): lax.ppermute(values, axis, [(i, (i + offset) % count) for i in range(coun...  18.1 us
    another operation x3, other arithmetic, collide(): return jnp.stack(posts)  15.5 us
    another operation x3, local copies, waits for them, and re-layouts, partial_flow(): jnp.stack([jnp.sum(jnp.where(disc_nodes & jnp.logical_not(solid_flag), ve...  15.2 us
    ppermute x12, waiting for transfers between devices, extended_2(): lax.ppermute(tail, axis, [(i, (i + 1) % count) for i in range(count)])  13.4 us
    ppermute x12, waiting for transfers between devices, extended_2(): lax.ppermute(head, axis, [((i + 1) % count, i) for i in range(count)])  12.1 us
    ppermute x12, starting transfers between devices, extended_2(): lax.ppermute(head, axis, [((i + 1) % count, i) for i in range(count)])  11.3 us
  transfers between devices with their start and end apart: 39, of which 21 were waited for; matrix products, arithmetic and copies ran while one was open for 52% of the time, Pallas kernels for 1%

profile of v1, /device:TPU:0, one launch (start us, length us, event | category | flops | bytes accessed | tf_op | source)
XLA Modules:
  0.0 445.3 jit_solution(3532274423076564965)
XLA Ops:
  41.9 5.6 %collective-permute-start.4 = (f32[8]{0:T(128)S(1)}, f32[8]{0:T(128)S(1)}, u32[]{:S(2)}, u32[]{:S(2)}) collective-permute-start(f32[8]{0:T(128)S(1)} %add.1578), channel_id=1, source_target_pairs={{0,30},{2,0},{4,2},{6,4},{8,6},{10,8},{12,10},{14,12},{16,14},{18,... | collective-permute-start | bytes 104 | tf_op jit(solution)/shard_map/ppermute | solution.py:173
  57.3 5.2 %constant_dynamic-update-slice_fusion.18 = (f32[19,8,16,128]{3,2,1,0:T(8,128)S(1)}, f32[8,16,128]{2,1,0:T(8,128)S(1)}) fusion(pred[8,16,128]{2,1,0:T(8,128)(4,1)S(1)} %get-tuple-element.38, f32[8,16,128]{2,1,0:T(8,128)S(1)} %reduce_sum.243, f32[19,8,16,128]{3,2,1,0:T(8,128)S(1)} %copy-done.2, f32[8,16,128]{2,1,0:T(8,128)S(1)} %get-tuple-element.37, ...), kind=kLoop, calls=%fused_computation.25 | loop fusion | flops 786431 | bytes 491616
  62.5 5.2 %constant_dynamic-update-slice_fusion.17 = f32[19,8,16,128]{3,2,1,0:T(8,128)S(1)} fusion(f32[19,8,16,128]{3,2,1,0:T(8,128)S(1)} %get-tuple-element.43, pred[8,16,128]{2,1,0:T(8,128)(4,1)S(1)} %get-tuple-element.38, f32[8,16,128]{2,1,0:T(8,128)S(1)} %get-tuple-element.44, f32[19,8,16,128]{3,2,1,0:T(8,128)S(1)} %copy-done.2, ...), kind=kLoop, calls=%fused_computation.24 | loop fusion | flops 671744 | bytes 561184
  67.7 5.2 %constant_dynamic-update-slice_fusion.16 = f32[19,8,16,128]{3,2,1,0:T(8,128)S(1)} fusion(f32[19,8,16,128]{3,2,1,0:T(8,128)S(1)} %constant_dynamic-update-slice_fusion.17, pred[8,16,128]{2,1,0:T(8,128)(4,1)S(1)} %get-tuple-element.38, f32[8,16,128]{2,1,0:T(8,128)S(1)} %get-tuple-element.44, f32[19,8,16,128]{3,2,1,0:T(8,128)S(1)} %copy-done.2, ...), kind=kLoop, calls=%fused_computation.23 | loop fusion | flops 688128 | bytes 561184
  72.9 5.2 %constant_dynamic-update-slice_fusion.15 = f32[19,8,16,128]{3,2,1,0:T(8,128)S(1)} fusion(f32[19,8,16,128]{3,2,1,0:T(8,128)S(1)} %constant_dynamic-update-slice_fusion.16, pred[8,16,128]{2,1,0:T(8,128)(4,1)S(1)} %get-tuple-element.38, f32[8,16,128]{2,1,0:T(8,128)S(1)} %get-tuple-element.44, f32[19,8,16,128]{3,2,1,0:T(8,128)S(1)} %copy-done.2, ...), kind=kLoop, calls=%fused_computation.22 | loop fusion | flops 671744 | bytes 561184
  78.1 5.2 %constant_dynamic-update-slice_fusion.14 = f32[19,8,16,128]{3,2,1,0:T(8,128)S(1)} fusion(f32[19,8,16,128]{3,2,1,0:T(8,128)S(1)} %constant_dynamic-update-slice_fusion.15, pred[8,16,128]{2,1,0:T(8,128)(4,1)S(1)} %get-tuple-element.38, f32[8,16,128]{2,1,0:T(8,128)S(1)} %get-tuple-element.44, f32[19,8,16,128]{3,2,1,0:T(8,128)S(1)} %copy-done.2, ...), kind=kLoop, calls=%fused_computation.21 | loop fusion | flops 688128 | bytes 561184
  83.3 5.2 %constant_dynamic-update-slice_fusion.13 = f32[19,8,16,128]{3,2,1,0:T(8,128)S(1)} fusion(f32[19,8,16,128]{3,2,1,0:T(8,128)S(1)} %constant_dynamic-update-slice_fusion.14, pred[8,16,128]{2,1,0:T(8,128)(4,1)S(1)} %get-tuple-element.38, f32[8,16,128]{2,1,0:T(8,128)S(1)} %get-tuple-element.44, f32[8,16,128]{2,1,0:T(8,128)S(1)} %get-tuple-element.37, ...), kind=kLoop, calls=%fused_computation.20 | loop fusion | flops 671744 | bytes 561184
  88.5 5.2 %constant_dynamic-update-slice_fusion.12 = f32[19,8,16,128]{3,2,1,0:T(8,128)S(1)} fusion(f32[19,8,16,128]{3,2,1,0:T(8,128)S(1)} %constant_dynamic-update-slice_fusion.13, pred[8,16,128]{2,1,0:T(8,128)(4,1)S(1)} %get-tuple-element.38, f32[8,16,128]{2,1,0:T(8,128)S(1)} %get-tuple-element.44, f32[19,8,16,128]{3,2,1,0:T(8,128)S(1)} %copy-done.2, ...), kind=kLoop, calls=%fused_computation.19 | loop fusion | flops 688128 | bytes 561184
  93.7 5.2 %constant_dynamic-update-slice_fusion.11 = f32[19,8,16,128]{3,2,1,0:T(8,128)S(1)} fusion(f32[19,8,16,128]{3,2,1,0:T(8,128)S(1)} %constant_dynamic-update-slice_fusion.12, pred[8,16,128]{2,1,0:T(8,128)(4,1)S(1)} %get-tuple-element.38, f32[8,16,128]{2,1,0:T(8,128)S(1)} %get-tuple-element.44, f32[8,16,128]{2,1,0:T(8,128)S(1)} %get-tuple-element.35, ...), kind=kLoop, calls=%fused_computation.18 | loop fusion | flops 655360 | bytes 561184
  98.9 5.2 %constant_dynamic-update-slice_fusion.10 = f32[19,8,16,128]{3,2,1,0:T(8,128)S(1)} fusion(f32[19,8,16,128]{3,2,1,0:T(8,128)S(1)} %constant_dynamic-update-slice_fusion.11, pred[8,16,128]{2,1,0:T(8,128)(4,1)S(1)} %get-tuple-element.38, f32[8,16,128]{2,1,0:T(8,128)S(1)} %get-tuple-element.44, f32[8,16,128]{2,1,0:T(8,128)S(1)} %get-tuple-element.36, ...), kind=kLoop, calls=%fused_computation.17 | loop fusion | flops 688128 | bytes 561184
  104.1 5.2 %constant_dynamic-update-slice_fusion.9 = f32[19,8,16,128]{3,2,1,0:T(8,128)S(1)} fusion(f32[19,8,16,128]{3,2,1,0:T(8,128)S(1)} %constant_dynamic-update-slice_fusion.10, pred[8,16,128]{2,1,0:T(8,128)(4,1)S(1)} %get-tuple-element.38, f32[8,16,128]{2,1,0:T(8,128)S(1)} %get-tuple-element.44, f32[8,16,128]{2,1,0:T(8,128)S(1)} %get-tuple-element.35, ...), kind=kLoop, calls=%fused_computation.16 | loop fusion | flops 671744 | bytes 561184
  109.3 5.2 %constant_dynamic-update-slice_fusion.8 = f32[19,8,16,128]{3,2,1,0:T(8,128)S(1)} fusion(f32[19,8,16,128]{3,2,1,0:T(8,128)S(1)} %constant_dynamic-update-slice_fusion.9, pred[8,16,128]{2,1,0:T(8,128)(4,1)S(1)} %get-tuple-element.38, f32[8,16,128]{2,1,0:T(8,128)S(1)} %get-tuple-element.44, f32[8,16,128]{2,1,0:T(8,128)S(1)} %get-tuple-element.36, ...), kind=kLoop, calls=%fused_computation.15 | loop fusion | flops 671744 | bytes 561184
  114.5 5.2 %constant_dynamic-update-slice_fusion.7 = f32[19,8,16,128]{3,2,1,0:T(8,128)S(1)} fusion(f32[19,8,16,128]{3,2,1,0:T(8,128)S(1)} %constant_dynamic-update-slice_fusion.8, pred[8,16,128]{2,1,0:T(8,128)(4,1)S(1)} %get-tuple-element.38, f32[8,16,128]{2,1,0:T(8,128)S(1)} %get-tuple-element.44, f32[8,16,128]{2,1,0:T(8,128)S(1)} %get-tuple-element.37, ...), kind=kLoop, calls=%fused_computation.14 | loop fusion | flops 655360 | bytes 561184
  119.6 5.2 %constant_dynamic-update-slice_fusion.6 = f32[19,8,16,128]{3,2,1,0:T(8,128)S(1)} fusion(f32[19,8,16,128]{3,2,1,0:T(8,128)S(1)} %constant_dynamic-update-slice_fusion.7, pred[8,16,128]{2,1,0:T(8,128)(4,1)S(1)} %get-tuple-element.38, f32[8,16,128]{2,1,0:T(8,128)S(1)} %get-tuple-element.44, f32[19,8,16,128]{3,2,1,0:T(8,128)S(1)} %copy-done.2, ...), kind=kLoop, calls=%fused_computation.13 | loop fusion | flops 688128 | bytes 561184
  124.8 5.2 %constant_dynamic-update-slice_fusion.5 = f32[19,8,16,128]{3,2,1,0:T(8,128)S(1)} fusion(f32[19,8,16,128]{3,2,1,0:T(8,128)S(1)} %constant_dynamic-update-slice_fusion.6, pred[8,16,128]{2,1,0:T(8,128)(4,1)S(1)} %get-tuple-element.38, f32[8,16,128]{2,1,0:T(8,128)S(1)} %get-tuple-element.44, f32[19,8,16,128]{3,2,1,0:T(8,128)S(1)} %copy-done.2, ...), kind=kLoop, calls=%fused_computation.12 | loop fusion | flops 671744 | bytes 561184
  130.0 5.2 %constant_dynamic-update-slice_fusion.4 = f32[19,8,16,128]{3,2,1,0:T(8,128)S(1)} fusion(f32[19,8,16,128]{3,2,1,0:T(8,128)S(1)} %constant_dynamic-update-slice_fusion.5, pred[8,16,128]{2,1,0:T(8,128)(4,1)S(1)} %get-tuple-element.38, f32[8,16,128]{2,1,0:T(8,128)S(1)} %get-tuple-element.44, f32[8,16,128]{2,1,0:T(8,128)S(1)} %get-tuple-element.37, ...), kind=kLoop, calls=%fused_computation.11 | loop fusion | flops 671744 | bytes 561184
  135.2 5.2 %constant_dynamic-update-slice_fusion.3 = f32[19,8,16,128]{3,2,1,0:T(8,128)S(1)} fusion(f32[19,8,16,128]{3,2,1,0:T(8,128)S(1)} %constant_dynamic-update-slice_fusion.4, pred[8,16,128]{2,1,0:T(8,128)(4,1)S(1)} %get-tuple-element.38, f32[8,16,128]{2,1,0:T(8,128)S(1)} %get-tuple-element.44, f32[8,16,128]{2,1,0:T(8,128)S(1)} %get-tuple-element.37, ...), kind=kLoop, calls=%fused_computation.10 | loop fusion | flops 655360 | bytes 561184
  140.4 5.2 %constant_dynamic-update-slice_fusion.2 = f32[19,8,16,128]{3,2,1,0:T(8,128)S(1)} fusion(f32[19,8,16,128]{3,2,1,0:T(8,128)S(1)} %constant_dynamic-update-slice_fusion.3, pred[8,16,128]{2,1,0:T(8,128)(4,1)S(1)} %get-tuple-element.38, f32[8,16,128]{2,1,0:T(8,128)S(1)} %get-tuple-element.44, f32[19,8,16,128]{3,2,1,0:T(8,128)S(1)} %copy-done.2, ...), kind=kLoop, calls=%fused_computation.9 | loop fusion | flops 688128 | bytes 561184
  145.6 5.2 %constant_dynamic-update-slice_fusion.1 = f32[19,8,16,128]{3,2,1,0:T(8,128)S(1)} fusion(f32[19,8,16,128]{3,2,1,0:T(8,128)S(1)} %constant_dynamic-update-slice_fusion.2, pred[8,16,128]{2,1,0:T(8,128)(4,1)S(1)} %get-tuple-element.38, f32[8,16,128]{2,1,0:T(8,128)S(1)} %get-tuple-element.44, f32[19,8,16,128]{3,2,1,0:T(8,128)S(1)} %copy-done.2, ...), kind=kLoop, calls=%fused_computation.8 | loop fusion | flops 671744 | bytes 561184
  150.8 5.2 %constant_dynamic-update-slice_fusion = f32[19,8,16,128]{3,2,1,0:T(8,128)S(1)} fusion(f32[19,8,16,128]{3,2,1,0:T(8,128)S(1)} %constant_dynamic-update-slice_fusion.1, pred[8,16,128]{2,1,0:T(8,128)(4,1)S(1)} %get-tuple-element.38, f32[8,16,128]{2,1,0:T(8,128)S(1)} %get-tuple-element.44, f32[8,16,128]{2,1,0:T(8,128)S(1)} %get-tuple-element.37, ...), kind=kLoop, calls=%fused_computation.7 | loop fusion | flops 671744 | bytes 561184 | tf_op jit(solution)/shard_map/stack | solution.py:81
  196.4 5.2 %constant_dynamic-update-slice_fusion.37 = (f32[19,8,16,128]{3,2,1,0:T(8,128)S(1)}, f32[8,16,128]{2,1,0:T(8,128)S(1)}) fusion(pred[8,16,128]{2,1,0:T(8,128)(4,1)S(1)} %get-tuple-element.38, f32[19,8,16,128]{3,2,1,0:T(8,128)S(1)} %copy-done.1, f32[8,16,128]{2,1,0:T(8,128)S(1)} %reduce_sum.252, f32[8,16,128]{2,1,0:T(8,128)S(1)} %get-tuple-element.33, ...), kind=kLoop, calls=%fused_computation.44 | loop fusion | flops 786431 | bytes 491616
  201.6 5.2 %constant_dynamic-update-slice_fusion.36 = f32[19,8,16,128]{3,2,1,0:T(8,128)S(1)} fusion(f32[19,8,16,128]{3,2,1,0:T(8,128)S(1)} %get-tuple-element.41, pred[8,16,128]{2,1,0:T(8,128)(4,1)S(1)} %get-tuple-element.38, f32[8,16,128]{2,1,0:T(8,128)S(1)} %get-tuple-element.42, f32[19,8,16,128]{3,2,1,0:T(8,128)S(1)} %copy-done.1, ...), kind=kLoop, calls=%fused_computation.43 | loop fusion | flops 671744 | bytes 561184
  206.8 5.2 %constant_dynamic-update-slice_fusion.35 = f32[19,8,16,128]{3,2,1,0:T(8,128)S(1)} fusion(f32[19,8,16,128]{3,2,1,0:T(8,128)S(1)} %constant_dynamic-update-slice_fusion.36, pred[8,16,128]{2,1,0:T(8,128)(4,1)S(1)} %get-tuple-element.38, f32[8,16,128]{2,1,0:T(8,128)S(1)} %get-tuple-element.42, f32[19,8,16,128]{3,2,1,0:T(8,128)S(1)} %copy-done.1, ...), kind=kLoop, calls=%fused_computation.42 | loop fusion | flops 688128 | bytes 561184
  212.0 5.2 %constant_dynamic-update-slice_fusion.34 = f32[19,8,16,128]{3,2,1,0:T(8,128)S(1)} fusion(f32[19,8,16,128]{3,2,1,0:T(8,128)S(1)} %constant_dynamic-update-slice_fusion.35, pred[8,16,128]{2,1,0:T(8,128)(4,1)S(1)} %get-tuple-element.38, f32[8,16,128]{2,1,0:T(8,128)S(1)} %get-tuple-element.42, f32[19,8,16,128]{3,2,1,0:T(8,128)S(1)} %copy-done.1, ...), kind=kLoop, calls=%fused_computation.41 | loop fusion | flops 671744 | bytes 561184
  217.2 5.2 %constant_dynamic-update-slice_fusion.33 = f32[19,8,16,128]{3,2,1,0:T(8,128)S(1)} fusion(f32[19,8,16,128]{3,2,1,0:T(8,128)S(1)} %constant_dynamic-update-slice_fusion.34, pred[8,16,128]{2,1,0:T(8,128)(4,1)S(1)} %get-tuple-element.38, f32[8,16,128]{2,1,0:T(8,128)S(1)} %get-tuple-element.42, f32[19,8,16,128]{3,2,1,0:T(8,128)S(1)} %copy-done.1, ...), kind=kLoop, calls=%fused_computation.40 | loop fusion | flops 688128 | bytes 561184
  222.4 5.2 %constant_dynamic-update-slice_fusion.32 = f32[19,8,16,128]{3,2,1,0:T(8,128)S(1)} fusion(f32[19,8,16,128]{3,2,1,0:T(8,128)S(1)} %constant_dynamic-update-slice_fusion.33, pred[8,16,128]{2,1,0:T(8,128)(4,1)S(1)} %get-tuple-element.38, f32[8,16,128]{2,1,0:T(8,128)S(1)} %get-tuple-element.42, f32[8,16,128]{2,1,0:T(8,128)S(1)} %get-tuple-element.33, ...), kind=kLoop, calls=%fused_computation.39 | loop fusion | flops 671744 | bytes 561184
  227.5 5.2 %constant_dynamic-update-slice_fusion.31 = f32[19,8,16,128]{3,2,1,0:T(8,128)S(1)} fusion(f32[19,8,16,128]{3,2,1,0:T(8,128)S(1)} %constant_dynamic-update-slice_fusion.32, pred[8,16,128]{2,1,0:T(8,128)(4,1)S(1)} %get-tuple-element.38, f32[8,16,128]{2,1,0:T(8,128)S(1)} %get-tuple-element.42, f32[19,8,16,128]{3,2,1,0:T(8,128)S(1)} %copy-done.1, ...), kind=kLoop, calls=%fused_computation.38 | loop fusion | flops 688128 | bytes 561184
  232.7 5.2 %constant_dynamic-update-slice_fusion.30 = f32[19,8,16,128]{3,2,1,0:T(8,128)S(1)} fusion(f32[19,8,16,128]{3,2,1,0:T(8,128)S(1)} %constant_dynamic-update-slice_fusion.31, pred[8,16,128]{2,1,0:T(8,128)(4,1)S(1)} %get-tuple-element.38, f32[8,16,128]{2,1,0:T(8,128)S(1)} %get-tuple-element.42, f32[8,16,128]{2,1,0:T(8,128)S(1)} %get-tuple-element.31, ...), kind=kLoop, calls=%fused_computation.37 | loop fusion | flops 655360 | bytes 561184
  237.9 5.2 %constant_dynamic-update-slice_fusion.29 = f32[19,8,16,128]{3,2,1,0:T(8,128)S(1)} fusion(f32[19,8,16,128]{3,2,1,0:T(8,128)S(1)} %constant_dynamic-update-slice_fusion.30, pred[8,16,128]{2,1,0:T(8,128)(4,1)S(1)} %get-tuple-element.38, f32[8,16,128]{2,1,0:T(8,128)S(1)} %get-tuple-element.42, f32[8,16,128]{2,1,0:T(8,128)S(1)} %get-tuple-element.32, ...), kind=kLoop, calls=%fused_computation.36 | loop fusion | flops 688128 | bytes 561184
  243.1 5.2 %constant_dynamic-update-slice_fusion.28 = f32[19,8,16,128]{3,2,1,0:T(8,128)S(1)} fusion(f32[19,8,16,128]{3,2,1,0:T(8,128)S(1)} %constant_dynamic-update-slice_fusion.29, pred[8,16,128]{2,1,0:T(8,128)(4,1)S(1)} %get-tuple-element.38, f32[8,16,128]{2,1,0:T(8,128)S(1)} %get-tuple-element.42, f32[8,16,128]{2,1,0:T(8,128)S(1)} %get-tuple-element.31, ...), kind=kLoop, calls=%fused_computation.35 | loop fusion | flops 671744 | bytes 561184
  248.3 5.2 %constant_dynamic-update-slice_fusion.27 = f32[19,8,16,128]{3,2,1,0:T(8,128)S(1)} fusion(f32[19,8,16,128]{3,2,1,0:T(8,128)S(1)} %constant_dynamic-update-slice_fusion.28, pred[8,16,128]{2,1,0:T(8,128)(4,1)S(1)} %get-tuple-element.38, f32[8,16,128]{2,1,0:T(8,128)S(1)} %get-tuple-element.42, f32[8,16,128]{2,1,0:T(8,128)S(1)} %get-tuple-element.32, ...), kind=kLoop, calls=%fused_computation.34 | loop fusion | flops 671744 | bytes 561184
  253.5 5.2 %constant_dynamic-update-slice_fusion.26 = f32[19,8,16,128]{3,2,1,0:T(8,128)S(1)} fusion(f32[19,8,16,128]{3,2,1,0:T(8,128)S(1)} %constant_dynamic-update-slice_fusion.27, pred[8,16,128]{2,1,0:T(8,128)(4,1)S(1)} %get-tuple-element.38, f32[8,16,128]{2,1,0:T(8,128)S(1)} %get-tuple-element.42, f32[8,16,128]{2,1,0:T(8,128)S(1)} %get-tuple-element.33, ...), kind=kLoop, calls=%fused_computation.33 | loop fusion | flops 655360 | bytes 561184
  258.7 5.2 %constant_dynamic-update-slice_fusion.25 = f32[19,8,16,128]{3,2,1,0:T(8,128)S(1)} fusion(f32[19,8,16,128]{3,2,1,0:T(8,128)S(1)} %constant_dynamic-update-slice_fusion.26, pred[8,16,128]{2,1,0:T(8,128)(4,1)S(1)} %get-tuple-element.38, f32[8,16,128]{2,1,0:T(8,128)S(1)} %get-tuple-element.42, f32[19,8,16,128]{3,2,1,0:T(8,128)S(1)} %copy-done.1, ...), kind=kLoop, calls=%fused_computation.32 | loop fusion | flops 688128 | bytes 561184
  263.9 5.2 %constant_dynamic-update-slice_fusion.24 = f32[19,8,16,128]{3,2,1,0:T(8,128)S(1)} fusion(f32[19,8,16,128]{3,2,1,0:T(8,128)S(1)} %constant_dynamic-update-slice_fusion.25, pred[8,16,128]{2,1,0:T(8,128)(4,1)S(1)} %get-tuple-element.38, f32[8,16,128]{2,1,0:T(8,128)S(1)} %get-tuple-element.42, f32[19,8,16,128]{3,2,1,0:T(8,128)S(1)} %copy-done.1, ...), kind=kLoop, calls=%fused_computation.31 | loop fusion | flops 671744 | bytes 561184
  269.1 5.2 %constant_dynamic-update-slice_fusion.23 = f32[19,8,16,128]{3,2,1,0:T(8,128)S(1)} fusion(f32[19,8,16,128]{3,2,1,0:T(8,128)S(1)} %constant_dynamic-update-slice_fusion.24, pred[8,16,128]{2,1,0:T(8,128)(4,1)S(1)} %get-tuple-element.38, f32[8,16,128]{2,1,0:T(8,128)S(1)} %get-tuple-element.42, f32[8,16,128]{2,1,0:T(8,128)S(1)} %get-tuple-element.33, ...), kind=kLoop, calls=%fused_computation.30 | loop fusion | flops 671744 | bytes 561184
  274.3 5.2 %constant_dynamic-update-slice_fusion.22 = f32[19,8,16,128]{3,2,1,0:T(8,128)S(1)} fusion(f32[19,8,16,128]{3,2,1,0:T(8,128)S(1)} %constant_dynamic-update-slice_fusion.23, pred[8,16,128]{2,1,0:T(8,128)(4,1)S(1)} %get-tuple-element.38, f32[8,16,128]{2,1,0:T(8,128)S(1)} %get-tuple-element.42, f32[8,16,128]{2,1,0:T(8,128)S(1)} %get-tuple-element.33, ...), kind=kLoop, calls=%fused_computation.29 | loop fusion | flops 655360 | bytes 561184
  279.5 5.2 %constant_dynamic-update-slice_fusion.21 = f32[19,8,16,128]{3,2,1,0:T(8,128)S(1)} fusion(f32[19,8,16,128]{3,2,1,0:T(8,128)S(1)} %constant_dynamic-update-slice_fusion.22, pred[8,16,128]{2,1,0:T(8,128)(4,1)S(1)} %get-tuple-element.38, f32[8,16,128]{2,1,0:T(8,128)S(1)} %get-tuple-element.42, f32[19,8,16,128]{3,2,1,0:T(8,128)S(1)} %copy-done.1, ...), kind=kLoop, calls=%fused_computation.28 | loop fusion | flops 688128 | bytes 561184
  284.7 5.2 %constant_dynamic-update-slice_fusion.20 = f32[19,8,16,128]{3,2,1,0:T(8,128)S(1)} fusion(f32[19,8,16,128]{3,2,1,0:T(8,128)S(1)} %constant_dynamic-update-slice_fusion.21, pred[8,16,128]{2,1,0:T(8,128)(4,1)S(1)} %get-tuple-element.38, f32[8,16,128]{2,1,0:T(8,128)S(1)} %get-tuple-element.42, f32[19,8,16,128]{3,2,1,0:T(8,128)S(1)} %copy-done.1, ...), kind=kLoop, calls=%fused_computation.27 | loop fusion | flops 671744 | bytes 561184
  289.9 5.2 %constant_dynamic-update-slice_fusion.19 = f32[19,8,16,128]{3,2,1,0:T(8,128)S(1)} fusion(f32[19,8,16,128]{3,2,1,0:T(8,128)S(1)} %constant_dynamic-update-slice_fusion.20, pred[8,16,128]{2,1,0:T(8,128)(4,1)S(1)} %get-tuple-element.38, f32[8,16,128]{2,1,0:T(8,128)S(1)} %get-tuple-element.42, f32[8,16,128]{2,1,0:T(8,128)S(1)} %get-tuple-element.33, ...), kind=kLoop, calls=%fused_computation.26 | loop fusion | flops 671744 | bytes 561184 | tf_op jit(solution)/shard_map/stack | solution.py:81
  341.6 5.2 %constant_dynamic-update-slice_fusion.54 = f32[19,8,16,128]{3,2,1,0:T(8,128)S(1)} fusion(f32[19,8,16,128]{3,2,1,0:T(8,128)S(1)} %constant_dynamic-update-slice_fusion.55, pred[8,16,128]{2,1,0:T(8,128)(4,1)S(1)} %get-tuple-element.38, f32[8,16,128]{2,1,0:T(8,128)S(1)} %get-tuple-element.40, f32[19,8,16,128]{3,2,1,0:T(8,128)S(1)} %copy-done, ...), kind=kLoop, calls=%fused_computation.61 | loop fusion | flops 688128 | bytes 561184
  351.9 5.2 %constant_dynamic-update-slice_fusion.52 = f32[19,8,16,128]{3,2,1,0:T(8,128)S(1)} fusion(f32[19,8,16,128]{3,2,1,0:T(8,128)S(1)} %constant_dynamic-update-slice_fusion.53, pred[8,16,128]{2,1,0:T(8,128)(4,1)S(1)} %get-tuple-element.38, f32[8,16,128]{2,1,0:T(8,128)S(1)} %get-tuple-element.40, f32[19,8,16,128]{3,2,1,0:T(8,128)S(1)} %copy-done, ...), kind=kLoop, calls=%fused_computation.59 | loop fusion | flops 688128 | bytes 561184
  362.3 5.2 %constant_dynamic-update-slice_fusion.50 = f32[19,8,16,128]{3,2,1,0:T(8,128)S(1)} fusion(f32[19,8,16,128]{3,2,1,0:T(8,128)S(1)} %constant_dynamic-update-slice_fusion.51, pred[8,16,128]{2,1,0:T(8,128)(4,1)S(1)} %get-tuple-element.38, f32[8,16,128]{2,1,0:T(8,128)S(1)} %get-tuple-element.40, f32[19,8,16,128]{3,2,1,0:T(8,128)S(1)} %copy-done, ...), kind=kLoop, calls=%fused_computation.57 | loop fusion | flops 688128 | bytes 561184
  367.4 5.2 %constant_dynamic-update-slice_fusion.49 = f32[19,8,16,128]{3,2,1,0:T(8,128)S(1)} fusion(f32[19,8,16,128]{3,2,1,0:T(8,128)S(1)} %constant_dynamic-update-slice_fusion.50, pred[8,16,128]{2,1,0:T(8,128)(4,1)S(1)} %get-tuple-element.38, f32[8,16,128]{2,1,0:T(8,128)S(1)} %get-tuple-element.40, f32[8,16,128]{2,1,0:T(8,128)S(1)} %get-tuple-element.27, ...), kind=kLoop, calls=%fused_computation.56 | loop fusion | flops 655360 | bytes 561184
  372.6 5.2 %constant_dynamic-update-slice_fusion.48 = f32[19,8,16,128]{3,2,1,0:T(8,128)S(1)} fusion(f32[19,8,16,128]{3,2,1,0:T(8,128)S(1)} %constant_dynamic-update-slice_fusion.49, pred[8,16,128]{2,1,0:T(8,128)(4,1)S(1)} %get-tuple-element.38, f32[8,16,128]{2,1,0:T(8,128)S(1)} %get-tuple-element.40, f32[8,16,128]{2,1,0:T(8,128)S(1)} %get-tuple-element.28, ...), kind=kLoop, calls=%fused_computation.55 | loop fusion | flops 688128 | bytes 561184
  388.1 5.2 %constant_dynamic-update-slice_fusion.45 = f32[19,8,16,128]{3,2,1,0:T(8,128)S(1)} fusion(f32[19,8,16,128]{3,2,1,0:T(8,128)S(1)} %constant_dynamic-update-slice_fusion.46, pred[8,16,128]{2,1,0:T(8,128)(4,1)S(1)} %get-tuple-element.38, f32[8,16,128]{2,1,0:T(8,128)S(1)} %get-tuple-element.40, f32[8,16,128]{2,1,0:T(8,128)S(1)} %get-tuple-element.29, ...), kind=kLoop, calls=%fused_computation.52 | loop fusion | flops 655360 | bytes 561184
  393.3 5.2 %constant_dynamic-update-slice_fusion.44 = f32[19,8,16,128]{3,2,1,0:T(8,128)S(1)} fusion(f32[19,8,16,128]{3,2,1,0:T(8,128)S(1)} %constant_dynamic-update-slice_fusion.45, pred[8,16,128]{2,1,0:T(8,128)(4,1)S(1)} %get-tuple-element.38, f32[8,16,128]{2,1,0:T(8,128)S(1)} %get-tuple-element.40, f32[19,8,16,128]{3,2,1,0:T(8,128)S(1)} %copy-done, ...), kind=kLoop, calls=%fused_computation.51 | loop fusion | flops 688128 | bytes 561184
  408.8 5.2 %constant_dynamic-update-slice_fusion.41 = f32[19,8,16,128]{3,2,1,0:T(8,128)S(1)} fusion(f32[19,8,16,128]{3,2,1,0:T(8,128)S(1)} %constant_dynamic-update-slice_fusion.42, pred[8,16,128]{2,1,0:T(8,128)(4,1)S(1)} %get-tuple-element.38, f32[8,16,128]{2,1,0:T(8,128)S(1)} %get-tuple-element.40, f32[8,16,128]{2,1,0:T(8,128)S(1)} %get-tuple-element.29, ...), kind=kLoop, calls=%fused_computation.48 | loop fusion | flops 655360 | bytes 561184
  413.9 5.2 %constant_dynamic-update-slice_fusion.40 = f32[19,8,16,128]{3,2,1,0:T(8,128)S(1)} fusion(f32[19,8,16,128]{3,2,1,0:T(8,128)S(1)} %constant_dynamic-update-slice_fusion.41, pred[8,16,128]{2,1,0:T(8,128)(4,1)S(1)} %get-tuple-element.38, f32[8,16,128]{2,1,0:T(8,128)S(1)} %get-tuple-element.40, f32[19,8,16,128]{3,2,1,0:T(8,128)S(1)} %copy-done, ...), kind=kLoop, calls=%fused_computation.47 | loop fusion | flops 688128 | bytes 561184
  (177 shorter events, 194.8 us)
Async XLA Ops:
  0.6 33.0 %copy-start.3 = (f32[8,16,128]{2,1,0:T(8,128)S(1)}, f32[8,16,128]{2,1,0:T(8,128)}, u32[]{:S(2)}) copy-start(f32[8,16,128]{2,1,0:T(8,128)} %param.10) | copy-start | bytes 196612
  0.6 33.0 %copy-start.2 = (f32[19,8,16,128]{3,2,1,0:T(8,128)S(1)}, f32[19,8,16,128]{3,2,1,0:T(8,128)}, u32[]{:S(2)}) copy-start(f32[19,8,16,128]{3,2,1,0:T(8,128)} %param.8) | copy-start | bytes 3735556
  0.7 33.0 %copy-start.4 = (s32[8,16,128]{2,1,0:T(8,128)S(1)}, s32[8,16,128]{2,1,0:T(8,128)}, u32[]{:S(2)}) copy-start(s32[8,16,128]{2,1,0:T(8,128)} %param.9) | copy-start | bytes 196612
  1.5 27.9 %collective-permute-start.28 = (f32[1,16,128]{2,1,0:T(8,128)S(1)}, f32[1,16,128]{2,1,0:T(8,128)S(1)}, u32[]{:S(2)}, u32[]{:S(2)}) collective-permute-start(f32[1,16,128]{2,1,0:T(8,128)S(1)} %get-tuple-element.72), channel_id=1, source_target_pairs={{0,2},{2,4},{4,6},{6,8},{8,10},{10,12},{12,14},{14,16},{16,18},{18... | collective-permute-start | bytes 24584 | tf_op jit(solution)/shard_map/ppermute | solution.py:47
  4.4 25.8 %collective-permute-start.27 = (f32[1,16,128]{2,1,0:T(8,128)S(1)}, f32[1,16,128]{2,1,0:T(8,128)S(1)}, u32[]{:S(2)}, u32[]{:S(2)}) collective-permute-start(f32[1,16,128]{2,1,0:T(8,128)S(1)} %get-tuple-element.71), channel_id=1, source_target_pairs={{2,0},{4,2},{6,4},{8,6},{10,8},{12,10},{14,12},{16,14},{18,16},{20... | collective-permute-start | bytes 24584 | tf_op jit(solution)/shard_map/ppermute | solution.py:49
  30.2 3.3 collective-permute-start.30
  30.3 3.3 collective-permute-start.29
  33.5 23.1 %copy-start.5 = (f32[8]{0:T(128)S(1)}, f32[8]{0:T(128)}, u32[]{:S(2)}) copy-start(f32[8]{0:T(128)} %param.12) | copy-start | bytes 100
  33.6 23.1 %copy-start.6 = (f32[8]{0:T(128)S(1)}, f32[8]{0:T(128)}, u32[]{:S(2)}) copy-start(f32[8]{0:T(128)} %param.13) | copy-start | bytes 100
  39.7 2.1 collective-permute-start
  39.8 127.3 %collective-permute-start.31 = (f32[1,16,128]{2,1,0:T(8,128)S(1)}, f32[1,16,128]{2,1,0:T(8,128)S(1)}, u32[]{:S(2)}, u32[]{:S(2)}) collective-permute-start(f32[1,16,128]{2,1,0:T(8,128)S(1)} %get-tuple-element.68), channel_id=1, source_target_pairs={{2,0},{4,2},{6,4},{8,6},{10,8},{12,10},{14,12},{16,14},{18,16},{20... | collective-permute-start | bytes 24584 | tf_op jit(solution)/shard_map/ppermute | solution.py:49
  41.9 125.3 %collective-permute-start.32 = (f32[1,16,128]{2,1,0:T(8,128)S(1)}, f32[1,16,128]{2,1,0:T(8,128)S(1)}, u32[]{:S(2)}, u32[]{:S(2)}) collective-permute-start(f32[1,16,128]{2,1,0:T(8,128)S(1)} %get-tuple-element.67), channel_id=1, source_target_pairs={{0,2},{2,4},{4,6},{6,8},{8,10},{10,12},{12,14},{14,16},{16,18},{18... | collective-permute-start | bytes 24584 | tf_op jit(solution)/shard_map/ppermute | solution.py:47
  41.9 7.6 %collective-permute-start.4 = (f32[8]{0:T(128)S(1)}, f32[8]{0:T(128)S(1)}, u32[]{:S(2)}, u32[]{:S(2)}) collective-permute-start(f32[8]{0:T(128)S(1)} %add.1578), channel_id=1, source_target_pairs={{0,30},{2,0},{4,2},{6,4},{8,6},{10,8},{12,10},{14,12},{16,14},{18,... | collective-permute-start | bytes 104 | tf_op jit(solution)/shard_map/ppermute | solution.py:173
  47.5 3.5 collective-permute-start.3
  47.5 6.2 %collective-permute-start.2 = (f32[8]{0:T(128)S(1)}, f32[8]{0:T(128)S(1)}, u32[]{:S(2)}, u32[]{:S(2)}) collective-permute-start(f32[8]{0:T(128)S(1)} %add.1578), channel_id=1, source_target_pairs={{0,4},{2,6},{4,8},{6,10},{8,12},{10,14},{12,16},{14,18},{16,20},{1... | collective-permute-start | bytes 104 | tf_op jit(solution)/shard_map/ppermute | solution.py:173
  49.5 7.1 %collective-permute-start.1 = (f32[8]{0:T(128)S(1)}, f32[8]{0:T(128)S(1)}, u32[]{:S(2)}, u32[]{:S(2)}) collective-permute-start(f32[8]{0:T(128)S(1)} %add.1578), channel_id=1, source_target_pairs={{0,2},{2,4},{4,6},{6,8},{8,10},{10,12},{12,14},{14,16},{16,18},{18... | collective-permute-start | bytes 104 | tf_op jit(solution)/shard_map/ppermute | solution.py:173
  156.0 5.5 %collective-permute-start.6 = (f32[19,1,16,128]{3,2,1,0:T(8,128)S(1)}, f32[19,1,16,128]{3,2,1,0:T(8,128)S(1)}, u32[]{:S(2)}, u32[]{:S(2)}) collective-permute-start(f32[19,1,16,128]{3,2,1,0:T(8,128)S(1)} %get-tuple-element.56), channel_id=1, source_target_pairs={{2,0},{4,2},{6,4},{8,6},{10,8},{12,10},{14,12},{16,14},{18,16},{20... | collective-permute-start | bytes 466952 | tf_op jit(solution)/shard_map/ppermute | solution.py:49
  157.6 8.8 %collective-permute-start.5 = (f32[19,1,16,128]{3,2,1,0:T(8,128)S(1)}, f32[19,1,16,128]{3,2,1,0:T(8,128)S(1)}, u32[]{:S(2)}, u32[]{:S(2)}) collective-permute-start(f32[19,1,16,128]{3,2,1,0:T(8,128)S(1)} %get-tuple-element.55), channel_id=1, source_target_pairs={{0,2},{2,4},{4,6},{6,8},{8,10},{10,12},{12,14},{14,16},{16,18},{18... | collective-permute-start | bytes 466952 | tf_op jit(solution)/shard_map/ppermute | solution.py:47
  166.6 1.4 collective-permute-start.8
  166.6 1.4 collective-permute-start.7
  167.1 7.1 %collective-permute-start.34 = (f32[10,1,128]{2,1,0:T(1,128)S(1)}, f32[10,1,128]{2,1,0:T(1,128)S(1)}, u32[]{:S(2)}, u32[]{:S(2)}) collective-permute-start(f32[10,1,128]{2,1,0:T(1,128)S(1)} %get-tuple-element.60), channel_id=1, source_target_pairs={{0,1},{1,0},{2,3},{3,2},{4,5},{5,4},{6,7},{7,6},{8,9},{9,8},{10,11... | collective-permute-start | bytes 15368 | tf_op jit(solution)/shard_map/ppermute | solution.py:47
  167.3 7.0 %collective-permute-start.33 = (f32[10,1,128]{2,1,0:T(1,128)S(1)}, f32[10,1,128]{2,1,0:T(1,128)S(1)}, u32[]{:S(2)}, u32[]{:S(2)}) collective-permute-start(f32[10,1,128]{2,1,0:T(1,128)S(1)} %get-tuple-element.59), channel_id=1, source_target_pairs={{1,0},{0,1},{3,2},{2,3},{5,4},{4,5},{7,6},{6,7},{9,8},{8,9},{11,10... | collective-permute-start | bytes 15368 | tf_op jit(solution)/shard_map/ppermute | solution.py:49
  172.8 1.7 copy-start.1
  180.5 2.4 collective-permute-start.9
  180.9 125.3 %collective-permute-start.35 = (f32[1,16,128]{2,1,0:T(8,128)S(1)}, f32[1,16,128]{2,1,0:T(8,128)S(1)}, u32[]{:S(2)}, u32[]{:S(2)}) collective-permute-start(f32[1,16,128]{2,1,0:T(8,128)S(1)} %get-tuple-element.64), channel_id=1, source_target_pairs={{2,0},{4,2},{6,4},{8,6},{10,8},{12,10},{14,12},{16,14},{18,16},{20... | collective-permute-start | bytes 24584 | tf_op jit(solution)/shard_map/ppermute | solution.py:49
  180.9 125.3 %collective-permute-start.36 = (f32[1,16,128]{2,1,0:T(8,128)S(1)}, f32[1,16,128]{2,1,0:T(8,128)S(1)}, u32[]{:S(2)}, u32[]{:S(2)}) collective-permute-start(f32[1,16,128]{2,1,0:T(8,128)S(1)} %get-tuple-element.63), channel_id=1, source_target_pairs={{0,2},{2,4},{4,6},{6,8},{8,10},{10,12},{12,14},{14,16},{16,18},{18... | collective-permute-start | bytes 24584 | tf_op jit(solution)/shard_map/ppermute | solution.py:47
  182.9 5.6 %collective-permute-start.13 = (f32[8]{0:T(128)S(1)}, f32[8]{0:T(128)S(1)}, u32[]{:S(2)}, u32[]{:S(2)}) collective-permute-start(f32[8]{0:T(128)S(1)} %add.1701), channel_id=1, source_target_pairs={{0,30},{2,0},{4,2},{6,4},{8,6},{10,8},{12,10},{14,12},{16,14},{18,... | collective-permute-start | bytes 104 | tf_op jit(solution)/shard_map/ppermute | solution.py:173
  186.5 3.5 collective-permute-start.12
  186.5 6.2 %collective-permute-start.11 = (f32[8]{0:T(128)S(1)}, f32[8]{0:T(128)S(1)}, u32[]{:S(2)}, u32[]{:S(2)}) collective-permute-start(f32[8]{0:T(128)S(1)} %add.1701), channel_id=1, source_target_pairs={{0,4},{2,6},{4,8},{6,10},{8,12},{10,14},{12,16},{14,18},{16,20},{1... | collective-permute-start | bytes 104 | tf_op jit(solution)/shard_map/ppermute | solution.py:173
  188.6 7.1 %collective-permute-start.10 = (f32[8]{0:T(128)S(1)}, f32[8]{0:T(128)S(1)}, u32[]{:S(2)}, u32[]{:S(2)}) collective-permute-start(f32[8]{0:T(128)S(1)} %add.1701), channel_id=1, source_target_pairs={{0,2},{2,4},{4,6},{6,8},{8,10},{10,12},{12,14},{14,16},{16,18},{18... | collective-permute-start | bytes 104 | tf_op jit(solution)/shard_map/ppermute | solution.py:173
  295.1 5.5 %collective-permute-start.15 = (f32[19,1,16,128]{3,2,1,0:T(8,128)S(1)}, f32[19,1,16,128]{3,2,1,0:T(8,128)S(1)}, u32[]{:S(2)}, u32[]{:S(2)}) collective-permute-start(f32[19,1,16,128]{3,2,1,0:T(8,128)S(1)} %get-tuple-element.54), channel_id=1, source_target_pairs={{2,0},{4,2},{6,4},{8,6},{10,8},{12,10},{14,12},{16,14},{18,16},{20... | collective-permute-start | bytes 466952 | tf_op jit(solution)/shard_map/ppermute | solution.py:49
  296.6 8.8 %collective-permute-start.14 = (f32[19,1,16,128]{3,2,1,0:T(8,128)S(1)}, f32[19,1,16,128]{3,2,1,0:T(8,128)S(1)}, u32[]{:S(2)}, u32[]{:S(2)}) collective-permute-start(f32[19,1,16,128]{3,2,1,0:T(8,128)S(1)} %get-tuple-element.53), channel_id=1, source_target_pairs={{0,2},{2,4},{4,6},{6,8},{8,10},{10,12},{12,14},{14,16},{16,18},{18... | collective-permute-start | bytes 466952 | tf_op jit(solution)/shard_map/ppermute | solution.py:47
  305.6 1.4 collective-permute-start.17
  305.7 1.4 collective-permute-start.16
  306.2 7.1 %collective-permute-start.38 = (f32[10,1,128]{2,1,0:T(1,128)S(1)}, f32[10,1,128]{2,1,0:T(1,128)S(1)}, u32[]{:S(2)}, u32[]{:S(2)}) collective-permute-start(f32[10,1,128]{2,1,0:T(1,128)S(1)} %get-tuple-element.58), channel_id=1, source_target_pairs={{0,1},{1,0},{2,3},{3,2},{4,5},{5,4},{6,7},{7,6},{8,9},{9,8},{10,11... | collective-permute-start | bytes 15368 | tf_op jit(solution)/shard_map/ppermute | solution.py:47
  306.3 7.0 %collective-permute-start.37 = (f32[10,1,128]{2,1,0:T(1,128)S(1)}, f32[10,1,128]{2,1,0:T(1,128)S(1)}, u32[]{:S(2)}, u32[]{:S(2)}) collective-permute-start(f32[10,1,128]{2,1,0:T(1,128)S(1)} %get-tuple-element.57), channel_id=1, source_target_pairs={{1,0},{0,1},{3,2},{2,3},{5,4},{4,5},{7,6},{6,7},{9,8},{8,9},{11,10... | collective-permute-start | bytes 15368 | tf_op jit(solution)/shard_map/ppermute | solution.py:49
  311.8 1.7 copy-start
  320.2 1.2 collective-permute-start.18
  321.4 4.1 collective-permute-start.22
  321.4 4.1 collective-permute-start.21
  321.4 6.3 %collective-permute-start.20 = (f32[8]{0:T(128)S(1)}, f32[8]{0:T(128)S(1)}, u32[]{:S(2)}, u32[]{:S(2)}) collective-permute-start(f32[8]{0:T(128)S(1)} %add.1824), channel_id=1, source_target_pairs={{0,4},{2,6},{4,8},{6,10},{8,12},{10,14},{12,16},{14,18},{16,20},{1... | collective-permute-start | bytes 104 | tf_op jit(solution)/shard_map/ppermute | solution.py:173
  323.4 7.1 %collective-permute-start.19 = (f32[8]{0:T(128)S(1)}, f32[8]{0:T(128)S(1)}, u32[]{:S(2)}, u32[]{:S(2)}) collective-permute-start(f32[8]{0:T(128)S(1)} %add.1824), channel_id=1, source_target_pairs={{0,2},{2,4},{4,6},{6,8},{8,10},{10,12},{12,14},{14,16},{16,18},{18... | collective-permute-start | bytes 104 | tf_op jit(solution)/shard_map/ppermute | solution.py:173
  429.5 6.2 %collective-permute-start.24 = (f32[19,1,16,128]{3,2,1,0:T(8,128)S(1)}, f32[19,1,16,128]{3,2,1,0:T(8,128)S(1)}, u32[]{:S(2)}, u32[]{:S(2)}) collective-permute-start(f32[19,1,16,128]{3,2,1,0:T(8,128)S(1)} %get-tuple-element.52), channel_id=1, source_target_pairs={{2,0},{4,2},{6,4},{8,6},{10,8},{12,10},{14,12},{16,14},{18,16},{20... | collective-permute-start | bytes 466952 | tf_op jit(solution)/shard_map/ppermute | solution.py:49
  430.1 8.8 %collective-permute-start.23 = (f32[19,1,16,128]{3,2,1,0:T(8,128)S(1)}, f32[19,1,16,128]{3,2,1,0:T(8,128)S(1)}, u32[]{:S(2)}, u32[]{:S(2)}) collective-permute-start(f32[19,1,16,128]{3,2,1,0:T(8,128)S(1)} %get-tuple-element.51), channel_id=1, source_target_pairs={{0,2},{2,4},{4,6},{6,8},{8,10},{10,12},{12,14},{14,16},{16,18},{18... | collective-permute-start | bytes 466952 | tf_op jit(solution)/shard_map/ppermute | solution.py:47
  439.1 1.4 collective-permute-start.26
  439.1 1.4 collective-permute-start.25

commit v2 on v1

--- a/solution.py
+++ b/solution.py
@@ -63,22 +63,45 @@
     return (density, velocity)
 
 
-def collide(populations, density, velocity, force_field, solid_flag):
-    speed_sq = velocity[0] * velocity[0] + velocity[1] * velocity[1] + velocity[2] * velocity[2]
-    posts = []
-    for which in range(19):
-        shift_x, shift_y, shift_z = VELOCITIES[which]
-        along = shift_x * velocity[0] + shift_y * velocity[1] + shift_z * velocity[2]
-        balance = (
-            WEIGHTS[which] * density * (1.0 + 3.0 * along + 4.5 * along * along - 1.5 * speed_sq)
-        )
-        relaxed = (
-            populations[which]
-            - RELAX_RATE * (populations[which] - balance)
-            + 3.0 * WEIGHTS[which] * shift_x * force_field
-        )
-        posts.append(jnp.where(solid_flag, populations[OPPOSITE[which]], relaxed))
-    return jnp.stack(posts)
+def collide_kernel(populations_ref, force_ref, solid_ref, posts_ref):
+    def plane(index, carry):
+        populations = [populations_ref[which, index] for which in range(19)]
+        density = sum(populations[1:], populations[0])
+        velocity = []
+        for dimension in range(3):
+            forward = [populations[which] for which in range(19) if VELOCITIES[which][dimension] == 1]
+            backward = [
+                populations[which] for which in range(19) if VELOCITIES[which][dimension] == -1
+            ]
+            velocity.append((sum(forward) - sum(backward)) / density)
+        force_field = force_ref[index]
+        solid_flag = solid_ref[index] != 0
+        speed_sq = velocity[0] * velocity[0] + velocity[1] * velocity[1] + velocity[2] * velocity[2]
+        for which in range(19):
+            shift_x, shift_y, shift_z = VELOCITIES[which]
+            along = shift_x * velocity[0] + shift_y * velocity[1] + shift_z * velocity[2]
+            balance = (
+                WEIGHTS[which] * density * (1.0 + 3.0 * along + 4.5 * along * along - 1.5 * speed_sq)
+            )
+            relaxed = populations[which] - RELAX_RATE * (populations[which] - balance)
+            if shift_x != 0:
+                relaxed = relaxed + 3.0 * WEIGHTS[which] * shift_x * force_field
+            posts_ref[which, index] = jnp.where(solid_flag, populations[OPPOSITE[which]], relaxed)
+        return carry
+
+    lax.fori_loop(0, populations_ref.shape[1], plane, 0)
+
+
+def collide(populations, force_field, solid_mask):
+    return pl.pallas_call(
+        collide_kernel,
+        out_shape=jax.ShapeDtypeStruct(populations.shape, jnp.float32),
+        in_specs=[pl.BlockSpec(memory_space=pltpu.VMEM)] * 3,
+        out_specs=pl.BlockSpec(memory_space=pltpu.VMEM),
+        cost_estimate=pl.CostEstimate(
+            flops=200 * force_field.size, transcendentals=0, bytes_accessed=8 * populations.size
+        ),
+    )(populations, force_field, solid_mask)
 
 
 def disc_count():
@@ -220,7 +243,7 @@
         partials = partial_flow(discs, velocity, solid_flag)
         totals = window_sum(window_sum(partials, "band", band_reach), "len", len_reach)
         force_field = force_from(discs, totals, fan_gain, jet_speed)
-        posts = collide(populations, density, velocity, force_field, solid_flag)
+        posts = collide(populations, force_field, solid_mask)
         rimmed = extended_2(smoke_field, (("len", 0), ("band", 1)), 1)
         extended = extended_2(posts, (("len", 1), ("band", 2)), 1)
         read = stream_rimmed(extended, slab_len, band_width)

time: 450 us -> 188 us (0.42)
  other arithmetic: 326 us -> 54 us
  Pallas kernels: 8.78 us -> 18.6 us
    unnamed x54 -> x0, other arithmetic: 280 us -> none
    add x0 -> x3, other arithmetic: none -> 17.2 us  [force_from(): force_field + jnp.where(discs[fan_number], strength[fan_number], 0.0)]
    another operation x3 -> x0, other arithmetic: 15.5 us -> none  [collide(): return jnp.stack(posts)]
    pallas_call x0 -> x3, Pallas kernels: none -> 9.84 us  [collide(): pl.pallas_call(collide_kernel, out_shape=jax.ShapeDtypeStruct(populations...]
  transfers between devices with their start and end apart: 39 -> 39, of which waited for: 21 -> 21; matrix products, arithmetic and copies ran while one was open for 52% -> 26% of each run, Pallas kernels for 1% -> 7%
where the time goes in v2:
time: 188 us; the launch traced here: 186 us
  other arithmetic  54 us (29%)
  waiting for transfers between devices  45.7 us (24%)
  starting transfers between devices  38.8 us (21%)
  local copies, waits for them, and re-layouts  27 us (14%)
  Pallas kernels  18.6 us (10%)
    ppermute x15, waiting for transfers between devices, window_sum(): lax.ppermute(values, axis, [(i, (i + offset) % count) for i in range(coun...  20.2 us
    ppermute x15, starting transfers between devices, window_sum(): lax.ppermute(values, axis, [(i, (i + offset) % count) for i in range(coun...  18.1 us
    add x3, other arithmetic, force_from(): force_field + jnp.where(discs[fan_number], strength[fan_number], 0.0)  17.2 us
    another operation x3, local copies, waits for them, and re-layouts, partial_flow(): jnp.stack([jnp.sum(jnp.where(disc_nodes & jnp.logical_not(solid_flag), ve...  15.2 us
    ppermute x12, waiting for transfers between devices, extended_2(): lax.ppermute(tail, axis, [(i, (i + 1) % count) for i in range(count)])  13.4 us
    ppermute x12, waiting for transfers between devices, extended_2(): lax.ppermute(head, axis, [((i + 1) % count, i) for i in range(count)])  12.1 us
    ppermute x12, starting transfers between devices, extended_2(): lax.ppermute(head, axis, [((i + 1) % count, i) for i in range(count)])  10.8 us
    ppermute x12, starting transfers between devices, extended_2(): lax.ppermute(tail, axis, [(i, (i + 1) % count) for i in range(count)])  9.88 us
  transfers between devices with their start and end apart: 39, of which 21 were waited for; matrix products, arithmetic and copies ran while one was open for 26% of the time, Pallas kernels for 7%

profile of v2, /device:TPU:0, one launch (start us, length us, event | category | flops | bytes accessed | tf_op | source)
XLA Modules:
  0.0 186.0 jit_solution(14567028219064625318)
XLA Ops:
  1.5 2.9 %collective-permute-start.28 = (f32[1,16,128]{2,1,0:T(8,128)S(1)}, f32[1,16,128]{2,1,0:T(8,128)S(1)}, u32[]{:S(2)}, u32[]{:S(2)}) collective-permute-start(f32[1,16,128]{2,1,0:T(8,128)S(1)} %get-tuple-element.60), channel_id=1, source_target_pairs={{0,2},{2,4},{4,6},{6,8},{8,10},{10,12},{12,14},{14,16},{16,18},{18... | collective-permute-start | bytes 24584 | tf_op jit(solution)/shard_map/ppermute | solution.py:47
  4.4 4.0 %collective-permute-start.27 = (f32[1,16,128]{2,1,0:T(8,128)S(1)}, f32[1,16,128]{2,1,0:T(8,128)S(1)}, u32[]{:S(2)}, u32[]{:S(2)}) collective-permute-start(f32[1,16,128]{2,1,0:T(8,128)S(1)} %get-tuple-element.59), channel_id=1, source_target_pairs={{2,0},{4,2},{6,4},{8,6},{10,8},{12,10},{14,12},{16,14},{18,16},{20... | collective-permute-start | bytes 24584 | tf_op jit(solution)/shard_map/ppermute | solution.py:49
  9.4 1.5 fusion.131
  11.0 2.1 %fusion.130 = (s32[1,1]{0,1:T(1,128)}, s32[1,1]{0,1:T(1,128)}, s32[1,1]{0,1:T(1,128)}, s32[1,1]{0,1:T(1,128)}, s32[1,1]{0,1:T(1,128)}, /*index=5*/s32[1,1]{0,1:T...) fusion(s32[8,3]{0,1:T(4,128)} %param.11), kind=kLoop, calls=%fused_computation.304 | loop fusion | bytes 152 | tf_op jit(solution)/shard_map/slice | solution.py:119
  34.7 5.1 %stack.89 = f32[8]{0:T(128)S(1)} concatenate(f32[1]{0:T(128)} %bitcast.4, f32[1]{0:T(128)} %bitcast.8, f32[1]{0:T(128)} %bitcast.12, f32[1]{0:T(128)} %bitcast.16, f32[1]{0:T(128)} %bitcast.20, f32[1]{0:T(128)} %bitcast.24, f32[1]{0:T(128)} %bitcast.28, f32[1]{0:T(128)} %bitcast.32), dimensions={0} | concatenate | bytes 64 | tf_op jit(solution)/shard_map/stack | solution.py:129
  39.9 2.0 %collective-permute-start.31 = (f32[1,16,128]{2,1,0:T(8,128)S(1)}, f32[1,16,128]{2,1,0:T(8,128)S(1)}, u32[]{:S(2)}, u32[]{:S(2)}) collective-permute-start(f32[1,16,128]{2,1,0:T(8,128)S(1)} %get-tuple-element.58), channel_id=1, source_target_pairs={{2,0},{4,2},{6,4},{8,6},{10,8},{12,10},{14,12},{16,14},{18,16},{20... | collective-permute-start | bytes 24584 | tf_op jit(solution)/shard_map/ppermute | solution.py:49
  41.9 5.6 %collective-permute-start.4 = (f32[8]{0:T(128)S(1)}, f32[8]{0:T(128)S(1)}, u32[]{:S(2)}, u32[]{:S(2)}) collective-permute-start(f32[8]{0:T(128)S(1)} %add.829), channel_id=1, source_target_pairs={{0,30},{2,0},{4,2},{6,4},{8,6},{10,8},{12,10},{14,12},{16,14},{18,... | collective-permute-start | bytes 104 | tf_op jit(solution)/shard_map/ppermute | solution.py:196
  47.6 2.0 %collective-permute-start.2 = (f32[8]{0:T(128)S(1)}, f32[8]{0:T(128)S(1)}, u32[]{:S(2)}, u32[]{:S(2)}) collective-permute-start(f32[8]{0:T(128)S(1)} %add.829), channel_id=1, source_target_pairs={{0,4},{2,6},{4,8},{6,10},{8,12},{10,14},{12,16},{14,18},{16,20},{1... | collective-permute-start | bytes 104 | tf_op jit(solution)/shard_map/ppermute | solution.py:196
  49.6 1.5 collective-permute-done.3
  51.1 2.7 %collective-permute-done.2 = f32[8]{0:T(128)S(1)} collective-permute-done((f32[8]{0:T(128)S(1)}, f32[8]{0:T(128)S(1)}, u32[]{:S(2)}, u32[]{:S(2)}) %collective-permute-start.2) | collective-permute-done | bytes 64 | tf_op jit(solution)/shard_map/ppermute | solution.py:196
  53.8 2.9 %collective-permute-done.1 = f32[8]{0:T(128)S(1)} collective-permute-done((f32[8]{0:T(128)S(1)}, f32[8]{0:T(128)S(1)}, u32[]{:S(2)}, u32[]{:S(2)}) %collective-permute-start.1) | collective-permute-done | bytes 64 | tf_op jit(solution)/shard_map/ppermute | solution.py:196
  57.4 5.7 %fusion.9.force_ref = f32[8,16,128]{2,1,0:T(8,128)} fusion(f32[]{:T(128)} %bitcast.40, f32[]{:T(128)} %bitcast.39, f32[]{:T(128)} %bitcast.38, f32[]{:T(128)} %bitcast.37, f32[]{:T(128)} %bitcast.36, f32[]{:T(128)} %bitcast.35, f32[]{:T(128)} %bitcast.34, f32[]{:T(128)} %bitcast.33, pred[16,128]{1,0:T(8,128)(4,1)S(1)} %add_compare_fusion, ...), kind=kLoop, calls=%fused_computation.54 | loop fusion | flops 376832 | bytes 82016 | tf_op jit(solution)/shard_map/add | solution.py:141
  63.1 3.3 %shard_map.95 = f32[19,8,16,128]{3,2,1,0:T(8,128)} custom-call(f32[19,8,16,128]{3,2,1,0:T(8,128)} %populations_ref.1, f32[8,16,128]{2,1,0:T(8,128)} %fusion.9.force_ref, s32[8,16,128]{2,1,0:T(8,128)} %solid_ref.5), custom_call_target="tpu_custom_call" | custom-call | flops 3276800 | bytes 2490368 | tf_op jit(solution)/shard_map/pallas_call | solution.py:96
  67.5 1.6 collective-permute-start.6
  69.7 3.4 %collective-permute-done.6 = f32[19,1,16,128]{3,2,1,0:T(8,128)S(1)} collective-permute-done((f32[19,1,16,128]{3,2,1,0:T(8,128)S(1)}, f32[19,1,16,128]{3,2,1,0:T(8,128)S(1)}, u32[]{:S(2)}, u32[]{:S(2)}) %collective-permute-start.6) | collective-permute-done | bytes 155680 | tf_op jit(solution)/shard_map/ppermute | solution.py:49
  73.1 4.8 %collective-permute-done.5 = f32[19,1,16,128]{3,2,1,0:T(8,128)S(1)} collective-permute-done((f32[19,1,16,128]{3,2,1,0:T(8,128)S(1)}, f32[19,1,16,128]{3,2,1,0:T(8,128)S(1)}, u32[]{:S(2)}, u32[]{:S(2)}) %collective-permute-start.5) | collective-permute-done | bytes 155680 | tf_op jit(solution)/shard_map/ppermute | solution.py:47
  77.9 1.4 pad_maximum_fusion.11
  80.9 1.8 pad_maximum_fusion.extended_ref
  82.7 2.9 %shard_map.96.populations_ref = f32[19,8,16,128]{3,2,1,0:T(8,128)} custom-call(f32[19,10,18,128]{3,2,1,0:T(8,128)} %pad_maximum_fusion.extended_ref), custom_call_target="tpu_custom_call" | custom-call | bytes 3502080 | tf_op jit(solution)/shard_map/pallas_call | solution.py:181
  87.0 1.5 select_add_fusion.1
  89.3 5.0 %stack.98 = f32[8]{0:T(128)S(1)} concatenate(f32[1]{0:T(128)} %bitcast.42, f32[1]{0:T(128)} %bitcast.43, f32[1]{0:T(128)} %bitcast.44, f32[1]{0:T(128)} %bitcast.45, f32[1]{0:T(128)} %bitcast.46, f32[1]{0:T(128)} %bitcast.47, f32[1]{0:T(128)} %bitcast.48, f32[1]{0:T(128)} %bitcast.49), dimensions={0} | concatenate | bytes 64 | tf_op jit(solution)/shard_map/stack | solution.py:129
  94.7 2.0 %collective-permute-start.36 = (f32[1,16,128]{2,1,0:T(8,128)S(1)}, f32[1,16,128]{2,1,0:T(8,128)S(1)}, u32[]{:S(2)}, u32[]{:S(2)}) collective-permute-start(f32[1,16,128]{2,1,0:T(8,128)S(1)} %get-tuple-element.53), channel_id=1, source_target_pairs={{0,2},{2,4},{4,6},{6,8},{8,10},{10,12},{12,14},{14,16},{16,18},{18... | collective-permute-start | bytes 24584 | tf_op jit(solution)/shard_map/ppermute | solution.py:47
  96.7 3.6 %collective-permute-start.13 = (f32[8]{0:T(128)S(1)}, f32[8]{0:T(128)S(1)}, u32[]{:S(2)}, u32[]{:S(2)}) collective-permute-start(f32[8]{0:T(128)S(1)} %add.851), channel_id=1, source_target_pairs={{0,30},{2,0},{4,2},{6,4},{8,6},{10,8},{12,10},{14,12},{16,14},{18,... | collective-permute-start | bytes 104 | tf_op jit(solution)/shard_map/ppermute | solution.py:196
  100.3 2.0 %collective-permute-start.11 = (f32[8]{0:T(128)S(1)}, f32[8]{0:T(128)S(1)}, u32[]{:S(2)}, u32[]{:S(2)}) collective-permute-start(f32[8]{0:T(128)S(1)} %add.851), channel_id=1, source_target_pairs={{0,4},{2,6},{4,8},{6,10},{8,12},{10,14},{12,16},{14,18},{16,20},{1... | collective-permute-start | bytes 104 | tf_op jit(solution)/shard_map/ppermute | solution.py:196
  102.4 1.5 collective-permute-done.12
  103.9 2.7 %collective-permute-done.11 = f32[8]{0:T(128)S(1)} collective-permute-done((f32[8]{0:T(128)S(1)}, f32[8]{0:T(128)S(1)}, u32[]{:S(2)}, u32[]{:S(2)}) %collective-permute-start.11) | collective-permute-done | bytes 64 | tf_op jit(solution)/shard_map/ppermute | solution.py:196
  106.6 2.9 %collective-permute-done.10 = f32[8]{0:T(128)S(1)} collective-permute-done((f32[8]{0:T(128)S(1)}, f32[8]{0:T(128)S(1)}, u32[]{:S(2)}, u32[]{:S(2)}) %collective-permute-start.10) | collective-permute-done | bytes 64 | tf_op jit(solution)/shard_map/ppermute | solution.py:196
  110.2 5.7 %fusion.16.force_ref = f32[8,16,128]{2,1,0:T(8,128)} fusion(f32[]{:T(128)} %bitcast.57, f32[]{:T(128)} %bitcast.56, f32[]{:T(128)} %bitcast.55, f32[]{:T(128)} %bitcast.54, f32[]{:T(128)} %bitcast.53, f32[]{:T(128)} %bitcast.52, f32[]{:T(128)} %bitcast.51, f32[]{:T(128)} %bitcast.50, pred[16,128]{1,0:T(8,128)(4,1)S(1)} %add_compare_fusion, ...), kind=kLoop, calls=%fused_computation.61 | loop fusion | flops 376832 | bytes 82016 | tf_op jit(solution)/shard_map/add | solution.py:141
  115.9 3.3 %shard_map.97 = f32[19,8,16,128]{3,2,1,0:T(8,128)} custom-call(f32[19,8,16,128]{3,2,1,0:T(8,128)} %shard_map.96.populations_ref, f32[8,16,128]{2,1,0:T(8,128)} %fusion.16.force_ref, s32[8,16,128]{2,1,0:T(8,128)} %solid_ref.5), custom_call_target="tpu_custom_call" | custom-call | flops 3276800 | bytes 2490368 | tf_op jit(solution)/shard_map/pallas_call | solution.py:96
  120.3 1.6 collective-permute-start.15
  122.5 3.4 %collective-permute-done.15 = f32[19,1,16,128]{3,2,1,0:T(8,128)S(1)} collective-permute-done((f32[19,1,16,128]{3,2,1,0:T(8,128)S(1)}, f32[19,1,16,128]{3,2,1,0:T(8,128)S(1)}, u32[]{:S(2)}, u32[]{:S(2)}) %collective-permute-start.15) | collective-permute-done | bytes 155680 | tf_op jit(solution)/shard_map/ppermute | solution.py:49
  125.9 4.9 %collective-permute-done.14 = f32[19,1,16,128]{3,2,1,0:T(8,128)S(1)} collective-permute-done((f32[19,1,16,128]{3,2,1,0:T(8,128)S(1)}, f32[19,1,16,128]{3,2,1,0:T(8,128)S(1)}, u32[]{:S(2)}, u32[]{:S(2)}) %collective-permute-start.14) | collective-permute-done | bytes 155680 | tf_op jit(solution)/shard_map/ppermute | solution.py:47
  130.7 1.4 pad_maximum_fusion.8
  133.7 1.8 pad_maximum_fusion.1.extended_ref
  135.5 2.9 %shard_map.98.populations_ref = f32[19,8,16,128]{3,2,1,0:T(8,128)} custom-call(f32[19,10,18,128]{3,2,1,0:T(8,128)} %pad_maximum_fusion.1.extended_ref), custom_call_target="tpu_custom_call" | custom-call | bytes 3502080 | tf_op jit(solution)/shard_map/pallas_call | solution.py:181
  139.8 2.1 %select_add_fusion = (f32[8,16,128]{2,1,0:T(8,128)}, f32[8,16,128]{2,1,0:T(8,128)S(1)}) fusion(pred[8,16,128]{2,1,0:T(8,128)(4,1)S(1)} %get-tuple-element.31, f32[8,16,128]{2,1,0:T(8,128)S(1)} %get-tuple-element.28, f32[8,16,128]{2,1,0:T(8,128)S(1)} %reduce_sum.261, f32[19,8,16,128]{3,2,1,0:T(8,128)} %shard_map.98.populations_ref, ...), kind=kLoop, calls=%fused_computation.174 | loop fusion | flops 966656 | bytes 1680384 | tf_op jit(solution)/shard_map/add | solution.py:265
  142.7 5.1 %stack.107 = f32[8]{0:T(128)S(1)} concatenate(f32[1]{0:T(128)} %bitcast.59, f32[1]{0:T(128)} %bitcast.60, f32[1]{0:T(128)} %bitcast.61, f32[1]{0:T(128)} %bitcast.62, f32[1]{0:T(128)} %bitcast.63, f32[1]{0:T(128)} %bitcast.64, f32[1]{0:T(128)} %bitcast.65, f32[1]{0:T(128)} %bitcast.66), dimensions={0} | concatenate | bytes 64 | tf_op jit(solution)/shard_map/stack | solution.py:129
  149.0 2.0 %collective-permute-start.20 = (f32[8]{0:T(128)S(1)}, f32[8]{0:T(128)S(1)}, u32[]{:S(2)}, u32[]{:S(2)}) collective-permute-start(f32[8]{0:T(128)S(1)} %add.873), channel_id=1, source_target_pairs={{0,4},{2,6},{4,8},{6,10},{8,12},{10,14},{12,16},{14,18},{16,20},{1... | collective-permute-start | bytes 104 | tf_op jit(solution)/shard_map/ppermute | solution.py:196
  151.0 2.0 %collective-permute-start.19 = (f32[8]{0:T(128)S(1)}, f32[8]{0:T(128)S(1)}, u32[]{:S(2)}, u32[]{:S(2)}) collective-permute-start(f32[8]{0:T(128)S(1)} %add.873), channel_id=1, source_target_pairs={{0,2},{2,4},{4,6},{6,8},{8,10},{10,12},{12,14},{14,16},{16,18},{18... | collective-permute-start | bytes 104 | tf_op jit(solution)/shard_map/ppermute | solution.py:196
  153.0 2.2 %collective-permute-done.20 = f32[8]{0:T(128)S(1)} collective-permute-done((f32[8]{0:T(128)S(1)}, f32[8]{0:T(128)S(1)}, u32[]{:S(2)}, u32[]{:S(2)}) %collective-permute-start.20) | collective-permute-done | bytes 64 | tf_op jit(solution)/shard_map/ppermute | solution.py:196
  155.3 2.9 %collective-permute-done.19 = f32[8]{0:T(128)S(1)} collective-permute-done((f32[8]{0:T(128)S(1)}, f32[8]{0:T(128)S(1)}, u32[]{:S(2)}, u32[]{:S(2)}) %collective-permute-start.19) | collective-permute-done | bytes 64 | tf_op jit(solution)/shard_map/ppermute | solution.py:196
  158.8 5.7 %fusion.23.force_ref = f32[8,16,128]{2,1,0:T(8,128)} fusion(f32[]{:T(128)} %bitcast.74, f32[]{:T(128)} %bitcast.73, f32[]{:T(128)} %bitcast.72, f32[]{:T(128)} %bitcast.71, f32[]{:T(128)} %bitcast.70, f32[]{:T(128)} %bitcast.69, f32[]{:T(128)} %bitcast.68, f32[]{:T(128)} %bitcast.67, pred[16,128]{1,0:T(8,128)(4,1)S(1)} %add_compare_fusion, ...), kind=kLoop, calls=%fused_computation.68 | loop fusion | flops 376832 | bytes 82016 | tf_op jit(solution)/shard_map/add | solution.py:141
  164.6 3.3 %shard_map.99 = f32[19,8,16,128]{3,2,1,0:T(8,128)} custom-call(f32[19,8,16,128]{3,2,1,0:T(8,128)} %shard_map.98.populations_ref, f32[8,16,128]{2,1,0:T(8,128)} %fusion.23.force_ref, s32[8,16,128]{2,1,0:T(8,128)} %solid_ref.5), custom_call_target="tpu_custom_call" | custom-call | flops 3276800 | bytes 2490368 | tf_op jit(solution)/shard_map/pallas_call | solution.py:96
  169.6 1.5 collective-permute-start.23
  171.0 4.2 %collective-permute-done.24 = f32[19,1,16,128]{3,2,1,0:T(8,128)S(1)} collective-permute-done((f32[19,1,16,128]{3,2,1,0:T(8,128)S(1)}, f32[19,1,16,128]{3,2,1,0:T(8,128)S(1)}, u32[]{:S(2)}, u32[]{:S(2)}) %collective-permute-start.24) | collective-permute-done | bytes 155680 | tf_op jit(solution)/shard_map/ppermute | solution.py:49
  175.2 3.2 %collective-permute-done.23 = f32[19,1,16,128]{3,2,1,0:T(8,128)S(1)} collective-permute-done((f32[19,1,16,128]{3,2,1,0:T(8,128)S(1)}, f32[19,1,16,128]{3,2,1,0:T(8,128)S(1)}, u32[]{:S(2)}, u32[]{:S(2)}) %collective-permute-start.23) | collective-permute-done | bytes 155680 | tf_op jit(solution)/shard_map/ppermute | solution.py:47
  181.4 1.8 pad_maximum_fusion.2.extended_ref
  183.1 2.9 %shard_map.100 = f32[19,8,16,128]{3,2,1,0:T(8,128)} custom-call(f32[19,10,18,128]{3,2,1,0:T(8,128)} %pad_maximum_fusion.2.extended_ref), custom_call_target="tpu_custom_call" | custom-call | bytes 3502080 | tf_op jit(solution)/shard_map/pallas_call | solution.py:181
  (128 shorter events, 42.6 us)
Async XLA Ops:
  0.6 33.0 %copy-start.4 = (f32[8,16,128]{2,1,0:T(8,128)S(1)}, f32[8,16,128]{2,1,0:T(8,128)}, u32[]{:S(2)}) copy-start(f32[8,16,128]{2,1,0:T(8,128)} %param.10) | copy-start | bytes 196612
  0.6 33.0 %copy-start.3 = (f32[19,8,16,128]{3,2,1,0:T(8,128)S(1)}, f32[19,8,16,128]{3,2,1,0:T(8,128)}, u32[]{:S(2)}) copy-start(f32[19,8,16,128]{3,2,1,0:T(8,128)} %populations_ref.1) | copy-start | bytes 3735556
  0.7 33.0 %copy-start.5 = (s32[8,16,128]{2,1,0:T(8,128)S(1)}, s32[8,16,128]{2,1,0:T(8,128)}, u32[]{:S(2)}) copy-start(s32[8,16,128]{2,1,0:T(8,128)} %solid_ref.5) | copy-start | bytes 196612
  0.7 56.1 %copy-start.6 = (f32[8]{0:T(128)S(1)}, f32[8]{0:T(128)}, u32[]{:S(2)}) copy-start(f32[8]{0:T(128)} %param.12) | copy-start | bytes 100
  0.7 56.1 %copy-start.7 = (f32[8]{0:T(128)S(1)}, f32[8]{0:T(128)}, u32[]{:S(2)}) copy-start(f32[8]{0:T(128)} %param.13) | copy-start | bytes 100
  1.5 28.0 %collective-permute-start.28 = (f32[1,16,128]{2,1,0:T(8,128)S(1)}, f32[1,16,128]{2,1,0:T(8,128)S(1)}, u32[]{:S(2)}, u32[]{:S(2)}) collective-permute-start(f32[1,16,128]{2,1,0:T(8,128)S(1)} %get-tuple-element.60), channel_id=1, source_target_pairs={{0,2},{2,4},{4,6},{6,8},{8,10},{10,12},{12,14},{14,16},{16,18},{18... | collective-permute-start | bytes 24584 | tf_op jit(solution)/shard_map/ppermute | solution.py:47
  4.4 25.9 %collective-permute-start.27 = (f32[1,16,128]{2,1,0:T(8,128)S(1)}, f32[1,16,128]{2,1,0:T(8,128)S(1)}, u32[]{:S(2)}, u32[]{:S(2)}) collective-permute-start(f32[1,16,128]{2,1,0:T(8,128)S(1)} %get-tuple-element.59), channel_id=1, source_target_pairs={{2,0},{4,2},{6,4},{8,6},{10,8},{12,10},{14,12},{16,14},{18,16},{20... | collective-permute-start | bytes 24584 | tf_op jit(solution)/shard_map/ppermute | solution.py:49
  30.4 3.2 %collective-permute-start.30 = (f32[10,1,128]{2,1,0:T(1,128)S(1)}, f32[10,1,128]{2,1,0:T(1,128)S(1)}, u32[]{:S(2)}, u32[]{:S(2)}) collective-permute-start(f32[10,1,128]{2,1,0:T(1,128)S(1)} %get-tuple-element.50), channel_id=1, source_target_pairs={{0,1},{1,0},{2,3},{3,2},{4,5},{5,4},{6,7},{7,6},{8,9},{9,8},{10,11... | collective-permute-start | bytes 15368 | tf_op jit(solution)/shard_map/ppermute | solution.py:47
  30.5 3.2 %collective-permute-start.29 = (f32[10,1,128]{2,1,0:T(1,128)S(1)}, f32[10,1,128]{2,1,0:T(1,128)S(1)}, u32[]{:S(2)}, u32[]{:S(2)}) collective-permute-start(f32[10,1,128]{2,1,0:T(1,128)S(1)} %get-tuple-element.49), channel_id=1, source_target_pairs={{1,0},{0,1},{3,2},{2,3},{5,4},{4,5},{7,6},{6,7},{9,8},{8,9},{11,10... | collective-permute-start | bytes 15368 | tf_op jit(solution)/shard_map/ppermute | solution.py:49
  39.8 2.1 %collective-permute-start = (f32[8]{0:T(128)S(1)}, f32[8]{0:T(128)S(1)}, u32[]{:S(2)}, u32[]{:S(2)}) collective-permute-start(f32[8]{0:T(128)S(1)} %stack.89), channel_id=1, source_target_pairs={{0,1},{1,0},{2,3},{3,2},{4,5},{5,4},{6,7},{7,6},{8,9},{9,8},{10,11... | collective-permute-start | bytes 104 | tf_op jit(solution)/shard_map/ppermute | solution.py:196
  39.9 40.0 %collective-permute-start.31 = (f32[1,16,128]{2,1,0:T(8,128)S(1)}, f32[1,16,128]{2,1,0:T(8,128)S(1)}, u32[]{:S(2)}, u32[]{:S(2)}) collective-permute-start(f32[1,16,128]{2,1,0:T(8,128)S(1)} %get-tuple-element.58), channel_id=1, source_target_pairs={{2,0},{4,2},{6,4},{8,6},{10,8},{12,10},{14,12},{16,14},{18,16},{20... | collective-permute-start | bytes 24584 | tf_op jit(solution)/shard_map/ppermute | solution.py:49
  41.9 38.0 %collective-permute-start.32 = (f32[1,16,128]{2,1,0:T(8,128)S(1)}, f32[1,16,128]{2,1,0:T(8,128)S(1)}, u32[]{:S(2)}, u32[]{:S(2)}) collective-permute-start(f32[1,16,128]{2,1,0:T(8,128)S(1)} %get-tuple-element.57), channel_id=1, source_target_pairs={{0,2},{2,4},{4,6},{6,8},{8,10},{10,12},{12,14},{14,16},{16,18},{18... | collective-permute-start | bytes 24584 | tf_op jit(solution)/shard_map/ppermute | solution.py:47
  41.9 7.6 %collective-permute-start.4 = (f32[8]{0:T(128)S(1)}, f32[8]{0:T(128)S(1)}, u32[]{:S(2)}, u32[]{:S(2)}) collective-permute-start(f32[8]{0:T(128)S(1)} %add.829), channel_id=1, source_target_pairs={{0,30},{2,0},{4,2},{6,4},{8,6},{10,8},{12,10},{14,12},{16,14},{18,... | collective-permute-start | bytes 104 | tf_op jit(solution)/shard_map/ppermute | solution.py:196
  47.6 3.5 %collective-permute-start.3 = (f32[8]{0:T(128)S(1)}, f32[8]{0:T(128)S(1)}, u32[]{:S(2)}, u32[]{:S(2)}) collective-permute-start(f32[8]{0:T(128)S(1)} %add.829), channel_id=1, source_target_pairs={{0,28},{2,30},{4,0},{6,2},{8,4},{10,6},{12,8},{14,10},{16,12},{18,... | collective-permute-start | bytes 104 | tf_op jit(solution)/shard_map/ppermute | solution.py:196
  47.6 6.2 %collective-permute-start.2 = (f32[8]{0:T(128)S(1)}, f32[8]{0:T(128)S(1)}, u32[]{:S(2)}, u32[]{:S(2)}) collective-permute-start(f32[8]{0:T(128)S(1)} %add.829), channel_id=1, source_target_pairs={{0,4},{2,6},{4,8},{6,10},{8,12},{10,14},{12,16},{14,18},{16,20},{1... | collective-permute-start | bytes 104 | tf_op jit(solution)/shard_map/ppermute | solution.py:196
  49.6 7.1 %collective-permute-start.1 = (f32[8]{0:T(128)S(1)}, f32[8]{0:T(128)S(1)}, u32[]{:S(2)}, u32[]{:S(2)}) collective-permute-start(f32[8]{0:T(128)S(1)} %add.829), channel_id=1, source_target_pairs={{0,2},{2,4},{4,6},{6,8},{8,10},{10,12},{12,14},{14,16},{16,18},{18... | collective-permute-start | bytes 104 | tf_op jit(solution)/shard_map/ppermute | solution.py:196
  66.4 14.5 %copy-start.1 = (f32[19,8,16,128]{3,2,1,0:T(8,128)S(1)}, f32[19,8,16,128]{3,2,1,0:T(8,128)}, u32[]{:S(2)}) copy-start(f32[19,8,16,128]{3,2,1,0:T(8,128)} %shard_map.95) | copy-start | bytes 3735556
  67.5 5.5 %collective-permute-start.6 = (f32[19,1,16,128]{3,2,1,0:T(8,128)S(1)}, f32[19,1,16,128]{3,2,1,0:T(8,128)S(1)}, u32[]{:S(2)}, u32[]{:S(2)}) collective-permute-start(f32[19,1,16,128]{3,2,1,0:T(8,128)S(1)} %get-tuple-element.44), channel_id=1, source_target_pairs={{2,0},{4,2},{6,4},{8,6},{10,8},{12,10},{14,12},{16,14},{18,16},{20... | collective-permute-start | bytes 466952 | tf_op jit(solution)/shard_map/ppermute | solution.py:49
  69.1 8.8 %collective-permute-start.5 = (f32[19,1,16,128]{3,2,1,0:T(8,128)S(1)}, f32[19,1,16,128]{3,2,1,0:T(8,128)S(1)}, u32[]{:S(2)}, u32[]{:S(2)}) collective-permute-start(f32[19,1,16,128]{3,2,1,0:T(8,128)S(1)} %get-tuple-element.43), channel_id=1, source_target_pairs={{0,2},{2,4},{4,6},{6,8},{8,10},{10,12},{12,14},{14,16},{16,18},{18... | collective-permute-start | bytes 466952 | tf_op jit(solution)/shard_map/ppermute | solution.py:47
  79.4 1.4 collective-permute-start.8
  79.4 1.4 collective-permute-start.7
  80.0 7.0 %collective-permute-start.33 = (f32[10,1,128]{2,1,0:T(1,128)S(1)}, f32[10,1,128]{2,1,0:T(1,128)S(1)}, u32[]{:S(2)}, u32[]{:S(2)}) collective-permute-start(f32[10,1,128]{2,1,0:T(1,128)S(1)} %get-tuple-element.48), channel_id=1, source_target_pairs={{1,0},{0,1},{3,2},{2,3},{5,4},{4,5},{7,6},{6,7},{9,8},{8,9},{11,10... | collective-permute-start | bytes 15368 | tf_op jit(solution)/shard_map/ppermute | solution.py:49
  80.1 6.9 %collective-permute-start.34 = (f32[10,1,128]{2,1,0:T(1,128)S(1)}, f32[10,1,128]{2,1,0:T(1,128)S(1)}, u32[]{:S(2)}, u32[]{:S(2)}) collective-permute-start(f32[10,1,128]{2,1,0:T(1,128)S(1)} %get-tuple-element.47), channel_id=1, source_target_pairs={{0,1},{1,0},{2,3},{3,2},{4,5},{5,4},{6,7},{7,6},{8,9},{9,8},{10,11... | collective-permute-start | bytes 15368 | tf_op jit(solution)/shard_map/ppermute | solution.py:47
  94.3 2.4 %collective-permute-start.9 = (f32[8]{0:T(128)S(1)}, f32[8]{0:T(128)S(1)}, u32[]{:S(2)}, u32[]{:S(2)}) collective-permute-start(f32[8]{0:T(128)S(1)} %stack.98), channel_id=1, source_target_pairs={{0,1},{1,0},{2,3},{3,2},{4,5},{5,4},{6,7},{7,6},{8,9},{9,8},{10,11... | collective-permute-start | bytes 104 | tf_op jit(solution)/shard_map/ppermute | solution.py:196
  94.7 38.0 %collective-permute-start.35 = (f32[1,16,128]{2,1,0:T(8,128)S(1)}, f32[1,16,128]{2,1,0:T(8,128)S(1)}, u32[]{:S(2)}, u32[]{:S(2)}) collective-permute-start(f32[1,16,128]{2,1,0:T(8,128)S(1)} %get-tuple-element.54), channel_id=1, source_target_pairs={{2,0},{4,2},{6,4},{8,6},{10,8},{12,10},{14,12},{16,14},{18,16},{20... | collective-permute-start | bytes 24584 | tf_op jit(solution)/shard_map/ppermute | solution.py:49
  94.7 38.0 %collective-permute-start.36 = (f32[1,16,128]{2,1,0:T(8,128)S(1)}, f32[1,16,128]{2,1,0:T(8,128)S(1)}, u32[]{:S(2)}, u32[]{:S(2)}) collective-permute-start(f32[1,16,128]{2,1,0:T(8,128)S(1)} %get-tuple-element.53), channel_id=1, source_target_pairs={{0,2},{2,4},{4,6},{6,8},{8,10},{10,12},{12,14},{14,16},{16,18},{18... | collective-permute-start | bytes 24584 | tf_op jit(solution)/shard_map/ppermute | solution.py:47
  96.7 5.6 %collective-permute-start.13 = (f32[8]{0:T(128)S(1)}, f32[8]{0:T(128)S(1)}, u32[]{:S(2)}, u32[]{:S(2)}) collective-permute-start(f32[8]{0:T(128)S(1)} %add.851), channel_id=1, source_target_pairs={{0,30},{2,0},{4,2},{6,4},{8,6},{10,8},{12,10},{14,12},{16,14},{18,... | collective-permute-start | bytes 104 | tf_op jit(solution)/shard_map/ppermute | solution.py:196
  100.3 3.5 %collective-permute-start.12 = (f32[8]{0:T(128)S(1)}, f32[8]{0:T(128)S(1)}, u32[]{:S(2)}, u32[]{:S(2)}) collective-permute-start(f32[8]{0:T(128)S(1)} %add.851), channel_id=1, source_target_pairs={{0,28},{2,30},{4,0},{6,2},{8,4},{10,6},{12,8},{14,10},{16,12},{18,... | collective-permute-start | bytes 104 | tf_op jit(solution)/shard_map/ppermute | solution.py:196
  100.3 6.2 %collective-permute-start.11 = (f32[8]{0:T(128)S(1)}, f32[8]{0:T(128)S(1)}, u32[]{:S(2)}, u32[]{:S(2)}) collective-permute-start(f32[8]{0:T(128)S(1)} %add.851), channel_id=1, source_target_pairs={{0,4},{2,6},{4,8},{6,10},{8,12},{10,14},{12,16},{14,18},{16,20},{1... | collective-permute-start | bytes 104 | tf_op jit(solution)/shard_map/ppermute | solution.py:196
  102.4 7.1 %collective-permute-start.10 = (f32[8]{0:T(128)S(1)}, f32[8]{0:T(128)S(1)}, u32[]{:S(2)}, u32[]{:S(2)}) collective-permute-start(f32[8]{0:T(128)S(1)} %add.851), channel_id=1, source_target_pairs={{0,2},{2,4},{4,6},{6,8},{8,10},{10,12},{12,14},{14,16},{16,18},{18... | collective-permute-start | bytes 104 | tf_op jit(solution)/shard_map/ppermute | solution.py:196
  119.2 14.5 %copy-start = (f32[19,8,16,128]{3,2,1,0:T(8,128)S(1)}, f32[19,8,16,128]{3,2,1,0:T(8,128)}, u32[]{:S(2)}) copy-start(f32[19,8,16,128]{3,2,1,0:T(8,128)} %shard_map.97) | copy-start | bytes 3735556
  120.3 5.5 %collective-permute-start.15 = (f32[19,1,16,128]{3,2,1,0:T(8,128)S(1)}, f32[19,1,16,128]{3,2,1,0:T(8,128)S(1)}, u32[]{:S(2)}, u32[]{:S(2)}) collective-permute-start(f32[19,1,16,128]{3,2,1,0:T(8,128)S(1)} %get-tuple-element.42), channel_id=1, source_target_pairs={{2,0},{4,2},{6,4},{8,6},{10,8},{12,10},{14,12},{16,14},{18,16},{20... | collective-permute-start | bytes 466952 | tf_op jit(solution)/shard_map/ppermute | solution.py:49
  121.9 8.8 %collective-permute-start.14 = (f32[19,1,16,128]{3,2,1,0:T(8,128)S(1)}, f32[19,1,16,128]{3,2,1,0:T(8,128)S(1)}, u32[]{:S(2)}, u32[]{:S(2)}) collective-permute-start(f32[19,1,16,128]{3,2,1,0:T(8,128)S(1)} %get-tuple-element.41), channel_id=1, source_target_pairs={{0,2},{2,4},{4,6},{6,8},{8,10},{10,12},{12,14},{14,16},{16,18},{18... | collective-permute-start | bytes 466952 | tf_op jit(solution)/shard_map/ppermute | solution.py:47
  132.2 1.4 collective-permute-start.17
  132.2 1.4 collective-permute-start.16
  132.8 7.0 %collective-permute-start.37 = (f32[10,1,128]{2,1,0:T(1,128)S(1)}, f32[10,1,128]{2,1,0:T(1,128)S(1)}, u32[]{:S(2)}, u32[]{:S(2)}) collective-permute-start(f32[10,1,128]{2,1,0:T(1,128)S(1)} %get-tuple-element.46), channel_id=1, source_target_pairs={{1,0},{0,1},{3,2},{2,3},{5,4},{4,5},{7,6},{6,7},{9,8},{8,9},{11,10... | collective-permute-start | bytes 15368 | tf_op jit(solution)/shard_map/ppermute | solution.py:49
  132.9 6.9 %collective-permute-start.38 = (f32[10,1,128]{2,1,0:T(1,128)S(1)}, f32[10,1,128]{2,1,0:T(1,128)S(1)}, u32[]{:S(2)}, u32[]{:S(2)}) collective-permute-start(f32[10,1,128]{2,1,0:T(1,128)S(1)} %get-tuple-element.45), channel_id=1, source_target_pairs={{0,1},{1,0},{2,3},{3,2},{4,5},{5,4},{6,7},{7,6},{8,9},{9,8},{10,11... | collective-permute-start | bytes 15368 | tf_op jit(solution)/shard_map/ppermute | solution.py:47
  147.8 1.2 collective-permute-start.18
  149.0 4.1 %collective-permute-start.22 = (f32[8]{0:T(128)S(1)}, f32[8]{0:T(128)S(1)}, u32[]{:S(2)}, u32[]{:S(2)}) collective-permute-start(f32[8]{0:T(128)S(1)} %add.873), channel_id=1, source_target_pairs={{0,30},{2,0},{4,2},{6,4},{8,6},{10,8},{12,10},{14,12},{16,14},{18,... | collective-permute-start | bytes 104 | tf_op jit(solution)/shard_map/ppermute | solution.py:196
  149.0 4.1 %collective-permute-start.21 = (f32[8]{0:T(128)S(1)}, f32[8]{0:T(128)S(1)}, u32[]{:S(2)}, u32[]{:S(2)}) collective-permute-start(f32[8]{0:T(128)S(1)} %add.873), channel_id=1, source_target_pairs={{0,28},{2,30},{4,0},{6,2},{8,4},{10,6},{12,8},{14,10},{16,12},{18,... | collective-permute-start | bytes 104 | tf_op jit(solution)/shard_map/ppermute | solution.py:196
  149.0 6.3 %collective-permute-start.20 = (f32[8]{0:T(128)S(1)}, f32[8]{0:T(128)S(1)}, u32[]{:S(2)}, u32[]{:S(2)}) collective-permute-start(f32[8]{0:T(128)S(1)} %add.873), channel_id=1, source_target_pairs={{0,4},{2,6},{4,8},{6,10},{8,12},{10,14},{12,16},{14,18},{16,20},{1... | collective-permute-start | bytes 104 | tf_op jit(solution)/shard_map/ppermute | solution.py:196
  151.0 7.1 %collective-permute-start.19 = (f32[8]{0:T(128)S(1)}, f32[8]{0:T(128)S(1)}, u32[]{:S(2)}, u32[]{:S(2)}) collective-permute-start(f32[8]{0:T(128)S(1)} %add.873), channel_id=1, source_target_pairs={{0,2},{2,4},{4,6},{6,8},{8,10},{10,12},{12,14},{14,16},{16,18},{18... | collective-permute-start | bytes 104 | tf_op jit(solution)/shard_map/ppermute | solution.py:196
  167.8 13.5 %copy-start.2 = (f32[19,8,16,128]{3,2,1,0:T(8,128)S(1)}, f32[19,8,16,128]{3,2,1,0:T(8,128)}, u32[]{:S(2)}) copy-start(f32[19,8,16,128]{3,2,1,0:T(8,128)} %shard_map.99) | copy-start | bytes 3735556
  169.0 6.2 %collective-permute-start.24 = (f32[19,1,16,128]{3,2,1,0:T(8,128)S(1)}, f32[19,1,16,128]{3,2,1,0:T(8,128)S(1)}, u32[]{:S(2)}, u32[]{:S(2)}) collective-permute-start(f32[19,1,16,128]{3,2,1,0:T(8,128)S(1)} %get-tuple-element.40), channel_id=1, source_target_pairs={{2,0},{4,2},{6,4},{8,6},{10,8},{12,10},{14,12},{16,14},{18,16},{20... | collective-permute-start | bytes 466952 | tf_op jit(solution)/shard_map/ppermute | solution.py:49
  169.6 8.8 %collective-permute-start.23 = (f32[19,1,16,128]{3,2,1,0:T(8,128)S(1)}, f32[19,1,16,128]{3,2,1,0:T(8,128)S(1)}, u32[]{:S(2)}, u32[]{:S(2)}) collective-permute-start(f32[19,1,16,128]{3,2,1,0:T(8,128)S(1)} %get-tuple-element.39), channel_id=1, source_target_pairs={{0,2},{2,4},{4,6},{6,8},{8,10},{10,12},{12,14},{14,16},{16,18},{18... | collective-permute-start | bytes 466952 | tf_op jit(solution)/shard_map/ppermute | solution.py:47
  179.8 1.4 collective-permute-start.26
  179.9 1.4 collective-permute-start.25

commit v3 on v2

--- a/solution.py
+++ b/solution.py
@@ -1,3 +1,5 @@
+import functools
+
 import jax
 import jax.numpy as jnp
 from jax import lax
@@ -63,19 +65,31 @@
     return (density, velocity)
 
 
-def collide_kernel(populations_ref, force_ref, solid_ref, posts_ref):
-    def plane(index, carry):
+def plane_moments(populations):
+    density = sum(populations[1:], populations[0])
+    velocity = []
+    for dimension in range(3):
+        forward = [populations[which] for which in range(19) if VELOCITIES[which][dimension] == 1]
+        backward = [populations[which] for which in range(19) if VELOCITIES[which][dimension] == -1]
+        velocity.append((sum(forward) - sum(backward)) / density)
+    return (density, velocity)
+
+
+def step_kernel(with_moments, strength_ref, populations_ref, discs_ref, solid_ref, *rest):
+    if with_moments:
+        out_ref, velocity_ref, flow_ref, posts_ref = rest
+    else:
+        out_ref, posts_ref = rest
+    fans = discs_ref.shape[0]
+    slab_len, band_width, height = out_ref.shape[1:]
+
+    def collide_plane(index, carry):
         populations = [populations_ref[which, index] for which in range(19)]
-        density = sum(populations[1:], populations[0])
-        velocity = []
-        for dimension in range(3):
-            forward = [populations[which] for which in range(19) if VELOCITIES[which][dimension] == 1]
-            backward = [
-                populations[which] for which in range(19) if VELOCITIES[which][dimension] == -1
-            ]
-            velocity.append((sum(forward) - sum(backward)) / density)
-        force_field = force_ref[index]
-        solid_flag = solid_ref[index] != 0
+        density, velocity = plane_moments(populations)
+        force_field = strength_ref[0] * discs_ref[0, index]
+        for fan_number in range(1, fans):
+            force_field = force_field + strength_ref[fan_number] * discs_ref[fan_number, index]
+        solid_flag = solid_ref[index] != 0.0
         speed_sq = velocity[0] * velocity[0] + velocity[1] * velocity[1] + velocity[2] * velocity[2]
         for which in range(19):
             shift_x, shift_y, shift_z = VELOCITIES[which]
@@ -89,19 +103,55 @@
             posts_ref[which, index] = jnp.where(solid_flag, populations[OPPOSITE[which]], relaxed)
         return carry
 
-    lax.fori_loop(0, populations_ref.shape[1], plane, 0)
-
-
-def collide(populations, force_field, solid_mask):
+    lax.fori_loop(0, populations_ref.shape[1], collide_plane, 0)
+    lane = lax.broadcasted_iota(jnp.int32, (slab_len, band_width, height), 2)
+    for which in range(19):
+        shift_x, shift_y, shift_z = VELOCITIES[which]
+        piece = posts_ref[
+            which, 1 - shift_x : 1 - shift_x + slab_len, 1 - shift_y : 1 - shift_y + band_width, :
+        ]
+        if shift_z == 1:
+            piece = jnp.where(lane == 0, 0.0, pltpu.roll(piece, 1, 2))
+        elif shift_z == -1:
+            piece = jnp.where(lane == height - 1, 0.0, pltpu.roll(piece, height - 1, 2))
+        out_ref[which] = piece
+    if not with_moments:
+        return
+    flow_ref[...] = jnp.zeros(flow_ref.shape, jnp.float32)
+
+    def moment_plane(index, carry):
+        density, velocity = plane_moments([out_ref[which, index] for which in range(19)])
+        for dimension in range(3):
+            velocity_ref[dimension, index] = velocity[dimension]
+        for fan_number in range(fans):
+            flow_ref[fan_number] += (
+                discs_ref[fan_number, index + 1, 1 : 1 + band_width, :] * velocity[0]
+            )
+        return carry
+
+    lax.fori_loop(0, slab_len, moment_plane, 0)
+
+
+def lattice_step(strength, extended, discs, solid_rim, with_moments):
+    slab_len = extended.shape[1] - 2
+    band_width = extended.shape[2] - 2
+    height = extended.shape[3]
+    fans = discs.shape[0]
+    out_shape = [jax.ShapeDtypeStruct((19, slab_len, band_width, height), jnp.float32)]
+    if with_moments:
+        out_shape.append(jax.ShapeDtypeStruct((3, slab_len, band_width, height), jnp.float32))
+        out_shape.append(jax.ShapeDtypeStruct((fans, band_width, height), jnp.float32))
+    vmem = pl.BlockSpec(memory_space=pltpu.VMEM)
     return pl.pallas_call(
-        collide_kernel,
-        out_shape=jax.ShapeDtypeStruct(populations.shape, jnp.float32),
-        in_specs=[pl.BlockSpec(memory_space=pltpu.VMEM)] * 3,
-        out_specs=pl.BlockSpec(memory_space=pltpu.VMEM),
+        functools.partial(step_kernel, with_moments),
+        out_shape=tuple(out_shape),
+        in_specs=[pl.BlockSpec(memory_space=pltpu.SMEM), vmem, vmem, vmem],
+        out_specs=tuple([vmem] * len(out_shape)),
+        scratch_shapes=[pltpu.VMEM(extended.shape, jnp.float32)],
         cost_estimate=pl.CostEstimate(
-            flops=200 * force_field.size, transcendentals=0, bytes_accessed=8 * populations.size
+            flops=300 * solid_rim.size, transcendentals=0, bytes_accessed=12 * extended.size
         ),
-    )(populations, force_field, solid_mask)
+    )(strength, extended, discs, solid_rim)
 
 
 def disc_count():
@@ -161,34 +211,6 @@
     return jnp.concatenate([field[..., 1:], zero_layer], axis=-1)
 
 
-def stream_kernel(extended_ref, out_ref):
-    slab_len, band_width, height = out_ref.shape[1:]
-    lane = lax.broadcasted_iota(jnp.int32, (slab_len, band_width, height), 2)
-    for which in range(19):
-        shift_x, shift_y, shift_z = VELOCITIES[which]
-        piece = extended_ref[
-            which, 1 - shift_x : 1 - shift_x + slab_len, 1 - shift_y : 1 - shift_y + band_width, :
-        ]
-        if shift_z == 1:
-            piece = jnp.where(lane == 0, 0.0, pltpu.roll(piece, 1, 2))
-        elif shift_z == -1:
-            piece = jnp.where(lane == height - 1, 0.0, pltpu.roll(piece, height - 1, 2))
-        out_ref[which] = piece
-
-
-def stream_rimmed(extended, slab_len, band_width):
-    shape = (19, slab_len, band_width, extended.shape[3])
-    return pl.pallas_call(
-        stream_kernel,
-        out_shape=jax.ShapeDtypeStruct(shape, jnp.float32),
-        in_specs=[pl.BlockSpec(memory_space=pltpu.VMEM)],
-        out_specs=pl.BlockSpec(memory_space=pltpu.VMEM),
-        cost_estimate=pl.CostEstimate(
-            flops=0, transcendentals=0, bytes_accessed=8 * extended.size
-        ),
-    )(extended)
-
-
 def window_sum(values, axis, width):
     count = lax.axis_size(axis)
     total = values
@@ -228,25 +250,36 @@
     offset_len = lax.axis_index("len") * slab_len
     offset_band = lax.axis_index("band") * band_width
     length_total = slab_len * lax.axis_size("len")
+    breadth_total = band_width * lax.axis_size("band")
     solid_flag = solid_mask == 1
-    coord_x = offset_len + jnp.arange(slab_len, dtype=jnp.int32)[:, None, None]
-    coord_y = offset_band + jnp.arange(band_width, dtype=jnp.int32)[None, :, None]
+    solid_rim = extended_2(solid_flag.astype(jnp.float32), (("len", 0), ("band", 1)), 1)
+    coord_x = offset_len - 1 + jnp.arange(slab_len + 2, dtype=jnp.int32)[:, None, None]
+    coord_y = jnp.mod(
+        offset_band - 1 + jnp.arange(band_width + 2, dtype=jnp.int32)[None, :, None], breadth_total
+    )
     coord_z = jnp.arange(height, dtype=jnp.int32)[None, None, :]
-    discs = fan_discs(fan_hubs, coord_x, coord_y, coord_z, length_total)
+    air_rim = solid_rim == 0.0
+    discs = jnp.stack(
+        [
+            (disc_nodes & air_rim).astype(jnp.float32)
+            for disc_nodes in fan_discs(fan_hubs, coord_x, coord_y, coord_z, length_total)
+        ]
+    )
     released = source_release(
         sources, source_rate, offset_len, offset_band, slab_len, band_width, height
     )
-    len_reach = -(-(FAN_LEN - 1) // slab_len)
-    band_reach = -(-(2 * RAD) // band_width)
+    len_reach = max(-(-FAN_LEN // slab_len), (slab_len + FAN_LEN - 1) // slab_len)
+    band_reach = max(-(-(2 * RAD + 1) // band_width), (band_width + 2 * RAD) // band_width)
+    density, velocity = moments(populations)
+    velocity = jnp.stack(velocity)
+    partials = jnp.sum(discs[:, 1:-1, 1:-1, :] * velocity[0][None], axis=(1, 2, 3))
     for repeat in range(ITERS):
-        density, velocity = moments(populations)
-        partials = partial_flow(discs, velocity, solid_flag)
         totals = window_sum(window_sum(partials, "band", band_reach), "len", len_reach)
-        force_field = force_from(discs, totals, fan_gain, jet_speed)
-        posts = collide(populations, force_field, solid_mask)
+        strength = fan_gain * (jet_speed - totals / float(disc_count()))
+        extended = extended_2(populations, (("len", 1), ("band", 2)), 1)
+        last = repeat == ITERS - 1
+        stepped = lattice_step(strength, extended, discs, solid_rim, not last)
         rimmed = extended_2(smoke_field, (("len", 0), ("band", 1)), 1)
-        extended = extended_2(posts, (("len", 1), ("band", 2)), 1)
-        read = stream_rimmed(extended, slab_len, band_width)
         ahead_x = rimmed[2:, 1:-1]
         behind_x = rimmed[:-2, 1:-1]
         ahead_y = rimmed[1:-1, 2:]
@@ -263,7 +296,10 @@
             solid_flag,
         )
         smoke_field = smoke_field + released
-        populations = read
+        populations = stepped[0]
+        if not last:
+            velocity = stepped[1]
+            partials = jnp.sum(stepped[2], axis=(1, 2))
     return (populations, smoke_field)
 
 

time: 188 us -> 159 us (0.85)
  other arithmetic: 54 us -> 30.7 us
  starting transfers between devices: 38.8 us -> 60.4 us
  local copies, waits for them, and re-layouts: 27 us -> 9.37 us
  waiting for transfers between devices: 45.7 us -> 40.8 us
  Pallas kernels: 18.6 us -> 15.2 us
    ppermute x12 -> x14, starting transfers between devices: 10.8 us -> 30.9 us  [extended_2(): lax.ppermute(head, axis, [((i + 1) % count, i) for i in range(count)])]
    ppermute x15, waiting for transfers between devices: 20.2 us -> 37.9 us  [window_sum(): lax.ppermute(values, axis, [(i, (i + offset) % count) for i in range(coun...]
    add x3 -> x0, other arithmetic: 17.2 us -> none  [force_from(): force_field + jnp.where(discs[fan_number], strength[fan_number], 0.0)]
    another operation x3 -> x0, local copies, waits for them, and re-layouts: 15.2 us -> none  [partial_flow(): jnp.stack([jnp.sum(jnp.where(disc_nodes & jnp.logical_not(solid_flag), ve...]
    ppermute x12 -> x14, waiting for transfers between devices: 12.1 us -> 0.68 us  [extended_2(): lax.ppermute(head, axis, [((i + 1) % count, i) for i in range(count)])]
    ppermute x12 -> x14, waiting for transfers between devices: 13.4 us -> 2.28 us  [extended_2(): lax.ppermute(tail, axis, [(i, (i + 1) % count) for i in range(count)])]
    ppermute x15, starting transfers between devices: 18.1 us -> 22.8 us  [window_sum(): lax.ppermute(values, axis, [(i, (i + offset) % count) for i in range(coun...]
    reduce_sum x6 -> x3, other arithmetic: 6.68 us -> 2.24 us  [the longest x2 2.07 us: body(): partials = jnp.sum(stepped[2], axis=(1, 2))]
  transfers between devices with their start and end apart: 39 -> 43, of which waited for: 21 -> 19; matrix products, arithmetic and copies ran while one was open for 26% -> 23% of each run, Pallas kernels for 7% -> 7%
where the time goes in v3:
time: 159 us
  starting transfers between devices  60.4 us (38%)
  waiting for transfers between devices  40.8 us (26%)
  other arithmetic  30.7 us (19%)
  Pallas kernels  15.2 us (10%)
  local copies, waits for them, and re-layouts  9.37 us (6%)
    ppermute x15, waiting for transfers between devices, window_sum(): lax.ppermute(values, axis, [(i, (i + offset) % count) for i in range(coun...  37.9 us
    ppermute x14, starting transfers between devices, extended_2(): lax.ppermute(head, axis, [((i + 1) % count, i) for i in range(count)])  30.9 us
    ppermute x15, starting transfers between devices, window_sum(): lax.ppermute(values, axis, [(i, (i + offset) % count) for i in range(coun...  22.8 us
    pallas_call x3, Pallas kernels, lattice_step(): pl.pallas_call(functools.partial(step_kernel, with_moments), out_shape=tu...  15.2 us
    ppermute x14, starting transfers between devices, extended_2(): lax.ppermute(tail, axis, [(i, (i + 1) % count) for i in range(count)])  6.7 us
    concatenate x5, other arithmetic, extended_2(): jnp.concatenate([lax.ppermute(tail, axis, [(i, (i + 1) % count) for i in...  5.94 us
    lt x5, other arithmetic, fan_discs(): offset_x < FAN_LEN  5.1 us
    mul x5, other arithmetic, fan_discs(): offset_y * offset_y + offset_z * offset_z <= RAD * RAD  5.06 us
  transfers between devices with their start and end apart: 43, of which 19 were waited for; matrix products, arithmetic and copies ran while one was open for 23% of the time, Pallas kernels for 7%

profile of v3, /device:TPU:0, one launch (start us, length us, event | category | flops | bytes accessed | tf_op | source)
XLA Modules:
  0.0 158.6 jit_solution(14855033673361039831)
XLA Ops:
  0.7 0.8 fusion.65
  1.5 6.9 %collective-permute-start.31 = (f32[1,16,128]{2,1,0:T(8,128)S(1)}, f32[1,16,128]{2,1,0:T(8,128)S(1)}, u32[]{:S(2)}, u32[]{:S(2)}) collective-permute-start(f32[1,16,128]{2,1,0:T(8,128)S(1)} %get-tuple-element.53), channel_id=1, source_target_pairs={{2,0},{4,2},{6,4},{8,6},{10,8},{12,10},{14,12},{16,14},{18,16},{20... | collective-permute-start | bytes 24584 | tf_op jit(solution)/shard_map/ppermute | solution.py:51
  8.4 1.0 fusion.57
  9.4 5.7 %collective-permute-start.10 = (f32[19,1,16,128]{3,2,1,0:T(8,128)S(1)}, f32[19,1,16,128]{3,2,1,0:T(8,128)S(1)}, u32[]{:S(2)}, u32[]{:S(2)}) collective-permute-start(f32[19,1,16,128]{3,2,1,0:T(8,128)S(1)} %get-tuple-element.29), channel_id=1, source_target_pairs={{2,0},{4,2},{6,4},{8,6},{10,8},{12,10},{14,12},{16,14},{18,16},{20... | collective-permute-start | bytes 466952 | tf_op jit(solution)/shard_map/ppermute | solution.py:51
  15.1 1.5 fusion.68
  16.6 2.1 %fusion.67 = (s32[1,1]{0,1:T(1,128)}, s32[1,1]{0,1:T(1,128)}, s32[1,1]{0,1:T(1,128)}, s32[1,1]{0,1:T(1,128)}, s32[1,1]{0,1:T(1,128)}, /*index=5*/s32[1,1]{0,1:T(...) fusion(s32[8,3]{0,1:T(4,128)} %param.11), kind=kLoop, calls=%fused_computation.195 | loop fusion | bytes 152 | tf_op jit(solution)/shard_map/slice | solution.py:169
  18.7 1.0 fusion.66
  27.7 1.2 subtract_multiply_fusion.4
  29.0 1.4 fusion.38
  30.4 1.2 subtract_multiply_fusion.8
  31.6 1.3 subtract_multiply_fusion.12
  32.9 1.2 fusion.36
  34.1 1.2 fusion.34
  35.9 0.9 fusion.1
  39.3 5.7 %collective-permute-start.35 = (f32[1,16,128]{2,1,0:T(8,128)S(1)}, f32[1,16,128]{2,1,0:T(8,128)S(1)}, u32[]{:S(2)}, u32[]{:S(2)}) collective-permute-start(f32[1,16,128]{2,1,0:T(8,128)S(1)} %get-tuple-element.48), channel_id=1, source_target_pairs={{2,0},{4,2},{6,4},{8,6},{10,8},{12,10},{14,12},{16,14},{18,16},{20... | collective-permute-start | bytes 24584 | tf_op jit(solution)/shard_map/ppermute | solution.py:51
  45.1 5.6 %collective-permute-start.1 = (f32[1,16,128]{2,1,0:T(8,128)S(1)}, f32[1,16,128]{2,1,0:T(8,128)S(1)}, u32[]{:S(2)}, u32[]{:S(2)}) collective-permute-start(f32[1,16,128]{2,1,0:T(8,128)S(1)} %get-tuple-element.52), channel_id=1, source_target_pairs={{2,0},{4,2},{6,4},{8,6},{10,8},{12,10},{14,12},{16,14},{18,16},{20... | collective-permute-start | bytes 24584 | tf_op jit(solution)/shard_map/ppermute | solution.py:51
  51.0 1.3 collective-permute-done
  56.3 5.3 %collective-permute-start.8 = (f32[8]{0:T(128)S(1)}, f32[8]{0:T(128)S(1)}, u32[]{:S(2)}, u32[]{:S(2)}) collective-permute-start(f32[8]{0:T(128)S(1)} %add.607), channel_id=1, source_target_pairs={{0,30},{2,0},{4,2},{6,4},{8,6},{10,8},{12,10},{14,12},{16,14},{18,... | collective-permute-start | bytes 104 | tf_op jit(solution)/shard_map/ppermute | solution.py:218
  61.7 1.3 collective-permute-done.8
  63.7 2.8 %collective-permute-done.7 = f32[8]{0:T(128)S(1)} collective-permute-done((f32[8]{0:T(128)S(1)}, f32[8]{0:T(128)S(1)}, u32[]{:S(2)}, u32[]{:S(2)}) %collective-permute-start.7) | collective-permute-done | bytes 64 | tf_op jit(solution)/shard_map/ppermute | solution.py:218
  66.5 6.2 %collective-permute-done.6 = f32[8]{0:T(128)S(1)} collective-permute-done((f32[8]{0:T(128)S(1)}, f32[8]{0:T(128)S(1)}, u32[]{:S(2)}, u32[]{:S(2)}) %collective-permute-start.6) | collective-permute-done | bytes 64 | tf_op jit(solution)/shard_map/ppermute | solution.py:218
  72.7 4.4 %collective-permute-start.5 = (f32[8]{0:T(128)S(1)}, f32[8]{0:T(128)S(1)}, u32[]{:S(2)}, u32[]{:S(2)}) collective-permute-start(f32[8]{0:T(128)S(1)} %add.607), channel_id=1, source_target_pairs={{0,2},{2,4},{4,6},{6,8},{8,10},{10,12},{12,14},{14,16},{16,18},{18... | collective-permute-start | bytes 104 | tf_op jit(solution)/shard_map/ppermute | solution.py:218
  77.1 3.0 %collective-permute-done.5 = f32[8]{0:T(128)S(1)} collective-permute-done((f32[8]{0:T(128)S(1)}, f32[8]{0:T(128)S(1)}, u32[]{:S(2)}, u32[]{:S(2)}) %collective-permute-start.5) | collective-permute-done | bytes 64 | tf_op jit(solution)/shard_map/ppermute | solution.py:218
  80.7 1.8 %pad_maximum_fusion.populations_ref = f32[19,10,18,128]{3,2,1,0:T(8,128)} fusion(f32[19,10,1,128]{3,2,1,0:T(1,128)S(1)} %collective-permute-done.12, f32[19,10,16,128]{3,2,1,0:T(8,128)S(1)} %constant_dynamic-update-slice_fusion, f32[19,10,1,128]{3,2,1,0:T(1,128)S(1)} %collective-permute-done.11), kind=kLoop, calls=%fused_computation | loop fusion | flops 875520 | bytes 3502080 | tf_op jit(solution)/shard_map/concatenate | solution.py:47
  82.5 5.2 %shard_map.95 = (f32[19,8,16,128]{3,2,1,0:T(8,128)}, f32[3,8,16,128]{3,2,1,0:T(8,128)}, f32[8,16,128]{2,1,0:T(8,128)}) custom-call(f32[8]{0:T(128)} %subtract_multiply_fusion.2.strength_ref, f32[19,10,18,128]{3,2,1,0:T(8,128)} %pad_maximum_fusion.populations_ref, f32[8,10,18,128]{3,2,1,0:T(8,128)} %copy-done, f32[10,18,128]{2,1,0:T(8,128)} %pad_maximum_fusion.3.solid_ref), custom_call_target="tpu_custom_call" | custom-call | flops 6912000 | bytes 5253120 | tf_op jit(solution)/shard_map/pallas_call | solution.py:145
  87.6 1.1 fusion.14
  88.8 1.0 reduce_sum.41
  90.5 5.1 %collective-permute-start.39 = (f32[1,16,128]{2,1,0:T(8,128)S(1)}, f32[1,16,128]{2,1,0:T(8,128)S(1)}, u32[]{:S(2)}, u32[]{:S(2)}) collective-permute-start(f32[1,16,128]{2,1,0:T(8,128)S(1)} %get-tuple-element.44), channel_id=1, source_target_pairs={{2,0},{4,2},{6,4},{8,6},{10,8},{12,10},{14,12},{16,14},{18,16},{20... | collective-permute-start | bytes 24584 | tf_op jit(solution)/shard_map/ppermute | solution.py:51
  95.6 1.0 fusion.56
  96.6 2.0 %collective-permute-start.18 = (f32[19,1,16,128]{3,2,1,0:T(8,128)S(1)}, f32[19,1,16,128]{3,2,1,0:T(8,128)S(1)}, u32[]{:S(2)}, u32[]{:S(2)}) collective-permute-start(f32[19,1,16,128]{3,2,1,0:T(8,128)S(1)} %get-tuple-element.28), channel_id=1, source_target_pairs={{0,2},{2,4},{4,6},{6,8},{8,10},{10,12},{12,14},{14,16},{16,18},{18... | collective-permute-start | bytes 466952 | tf_op jit(solution)/shard_map/ppermute | solution.py:49
  98.7 3.7 %collective-permute-start.17 = (f32[8]{0:T(128)S(1)}, f32[8]{0:T(128)S(1)}, u32[]{:S(2)}, u32[]{:S(2)}) collective-permute-start(f32[8]{0:T(128)S(1)} %add.612), channel_id=1, source_target_pairs={{0,30},{2,0},{4,2},{6,4},{8,6},{10,8},{12,10},{14,12},{16,14},{18,... | collective-permute-start | bytes 104 | tf_op jit(solution)/shard_map/ppermute | solution.py:218
  102.3 3.4 %collective-permute-done.17 = f32[8]{0:T(128)S(1)} collective-permute-done((f32[8]{0:T(128)S(1)}, f32[8]{0:T(128)S(1)}, u32[]{:S(2)}, u32[]{:S(2)}) %collective-permute-start.17) | collective-permute-done | bytes 64 | tf_op jit(solution)/shard_map/ppermute | solution.py:218
  105.8 3.5 %collective-permute-done.16 = f32[8]{0:T(128)S(1)} collective-permute-done((f32[8]{0:T(128)S(1)}, f32[8]{0:T(128)S(1)}, u32[]{:S(2)}, u32[]{:S(2)}) %collective-permute-start.16) | collective-permute-done | bytes 64 | tf_op jit(solution)/shard_map/ppermute | solution.py:218
  109.3 6.2 %collective-permute-done.15 = f32[8]{0:T(128)S(1)} collective-permute-done((f32[8]{0:T(128)S(1)}, f32[8]{0:T(128)S(1)}, u32[]{:S(2)}, u32[]{:S(2)}) %collective-permute-start.15) | collective-permute-done | bytes 64 | tf_op jit(solution)/shard_map/ppermute | solution.py:218
  115.5 2.2 %collective-permute-start.14 = (f32[8]{0:T(128)S(1)}, f32[8]{0:T(128)S(1)}, u32[]{:S(2)}, u32[]{:S(2)}) collective-permute-start(f32[8]{0:T(128)S(1)} %add.612), channel_id=1, source_target_pairs={{0,2},{2,4},{4,6},{6,8},{8,10},{10,12},{12,14},{14,16},{16,18},{18... | collective-permute-start | bytes 104 | tf_op jit(solution)/shard_map/ppermute | solution.py:218
  117.8 4.9 %collective-permute-done.14 = f32[8]{0:T(128)S(1)} collective-permute-done((f32[8]{0:T(128)S(1)}, f32[8]{0:T(128)S(1)}, u32[]{:S(2)}, u32[]{:S(2)}) %collective-permute-start.14) | collective-permute-done | bytes 64 | tf_op jit(solution)/shard_map/ppermute | solution.py:218
  125.1 1.8 %pad_maximum_fusion.1.populations_ref = f32[19,10,18,128]{3,2,1,0:T(8,128)} fusion(f32[19,10,1,128]{3,2,1,0:T(1,128)S(1)} %collective-permute-done.21, f32[19,10,16,128]{3,2,1,0:T(8,128)S(1)} %constant_dynamic-update-slice_fusion.3, f32[19,10,1,128]{3,2,1,0:T(1,128)S(1)} %collective-permute-done.20), kind=kLoop, calls=%fused_computation.1 | loop fusion | flops 875520 | bytes 3502080 | tf_op jit(solution)/shard_map/concatenate | solution.py:47
  126.9 5.2 %shard_map.96 = (f32[19,8,16,128]{3,2,1,0:T(8,128)}, f32[3,8,16,128]{3,2,1,0:T(8,128)}, f32[8,16,128]{2,1,0:T(8,128)}) custom-call(f32[8]{0:T(128)} %subtract_multiply_fusion.1.strength_ref, f32[19,10,18,128]{3,2,1,0:T(8,128)} %pad_maximum_fusion.1.populations_ref, f32[8,10,18,128]{3,2,1,0:T(8,128)} %copy-done, f32[10,18,128]{2,1,0:T(8,128)} %pad_maximum_fusion.3.solid_ref), custom_call_target="tpu_custom_call" | custom-call | flops 6912000 | bytes 5253120 | tf_op jit(solution)/shard_map/pallas_call | solution.py:145
  132.0 1.1 reduce_sum.42
  133.5 1.0 fusion.55
  134.7 1.9 %collective-permute-start.27 = (f32[19,1,16,128]{3,2,1,0:T(8,128)S(1)}, f32[19,1,16,128]{3,2,1,0:T(8,128)S(1)}, u32[]{:S(2)}, u32[]{:S(2)}) collective-permute-start(f32[19,1,16,128]{3,2,1,0:T(8,128)S(1)} %get-tuple-element.26), channel_id=1, source_target_pairs={{0,2},{2,4},{4,6},{6,8},{8,10},{10,12},{12,14},{14,16},{16,18},{18... | collective-permute-start | bytes 466952 | tf_op jit(solution)/shard_map/ppermute | solution.py:49
  136.6 1.6 %fusion.8 = f32[8,16,128]{2,1,0:T(8,128)} fusion(pred[8,16,128]{2,1,0:T(8,128)(4,1)S(1)} %get-tuple-element.16, f32[3,8,16,128]{3,2,1,0:T(8,128)} %get-tuple-element.13, f32[8,16,128]{2,1,0:T(8,128)S(1)} %fusion.14, f32[8,16,127]{2,1,0:T(8,128)S(1)} %get-tuple-element.46, f32[8,16,127]{2,1,0:T(8,128)S(1)} %get-tuple-element.45, ...), kind=kLoop, calls=%fused_computation.45 | loop fusion | flops 475136 | bytes 566272 | tf_op jit(solution)/shard_map/add | solution.py:298
  138.3 3.7 %collective-permute-start.26 = (f32[8]{0:T(128)S(1)}, f32[8]{0:T(128)S(1)}, u32[]{:S(2)}, u32[]{:S(2)}) collective-permute-start(f32[8]{0:T(128)S(1)} %add.617), channel_id=1, source_target_pairs={{0,30},{2,0},{4,2},{6,4},{8,6},{10,8},{12,10},{14,12},{16,14},{18,... | collective-permute-start | bytes 104 | tf_op jit(solution)/shard_map/ppermute | solution.py:218
  142.0 2.0 %collective-permute-start.24 = (f32[8]{0:T(128)S(1)}, f32[8]{0:T(128)S(1)}, u32[]{:S(2)}, u32[]{:S(2)}) collective-permute-start(f32[8]{0:T(128)S(1)} %add.617), channel_id=1, source_target_pairs={{0,4},{2,6},{4,8},{6,10},{8,12},{10,14},{12,16},{14,18},{16,20},{1... | collective-permute-start | bytes 104 | tf_op jit(solution)/shard_map/ppermute | solution.py:218
  145.5 2.7 %collective-permute-done.24 = f32[8]{0:T(128)S(1)} collective-permute-done((f32[8]{0:T(128)S(1)}, f32[8]{0:T(128)S(1)}, u32[]{:S(2)}, u32[]{:S(2)}) %collective-permute-start.24) | collective-permute-done | bytes 64 | tf_op jit(solution)/shard_map/ppermute | solution.py:218
  148.2 3.3 %collective-permute-done.23 = f32[8]{0:T(128)S(1)} collective-permute-done((f32[8]{0:T(128)S(1)}, f32[8]{0:T(128)S(1)}, u32[]{:S(2)}, u32[]{:S(2)}) %collective-permute-start.23) | collective-permute-done | bytes 64 | tf_op jit(solution)/shard_map/ppermute | solution.py:218
  152.0 1.8 %pad_maximum_fusion.2.populations_ref = f32[19,10,18,128]{3,2,1,0:T(8,128)} fusion(f32[19,10,1,128]{3,2,1,0:T(1,128)S(1)} %collective-permute-done.30, f32[19,10,16,128]{3,2,1,0:T(8,128)S(1)} %constant_dynamic-update-slice_fusion.6, f32[19,10,1,128]{3,2,1,0:T(1,128)S(1)} %collective-permute-done.29), kind=kLoop, calls=%fused_computation.2 | loop fusion | flops 875520 | bytes 3502080 | tf_op jit(solution)/shard_map/concatenate | solution.py:47
  153.8 4.8 %shard_map.97 = f32[19,8,16,128]{3,2,1,0:T(8,128)} custom-call(f32[8]{0:T(128)} %subtract_multiply_fusion.strength_ref, f32[19,10,18,128]{3,2,1,0:T(8,128)} %pad_maximum_fusion.2.populations_ref, f32[8,10,18,128]{3,2,1,0:T(8,128)} %copy-done, f32[10,18,128]{2,1,0:T(8,128)} %pad_maximum_fusion.3.solid_ref), custom_call_target="tpu_custom_call" | custom-call | flops 6912000 | bytes 5253120 | tf_op jit(solution)/shard_map/pallas_call | solution.py:145
  (147 shorter events, 22.5 us)
Async XLA Ops:
  0.6 36.9 %copy-start.4 = (f32[8,16,128]{2,1,0:T(8,128)S(1)}, f32[8,16,128]{2,1,0:T(8,128)}, u32[]{:S(2)}) copy-start(f32[8,16,128]{2,1,0:T(8,128)} %param.10) | copy-start | bytes 196612
  0.6 37.6 %copy-start.1 = (f32[19,8,16,128]{3,2,1,0:T(8,128)S(1)}, f32[19,8,16,128]{3,2,1,0:T(8,128)}, u32[]{:S(2)}) copy-start(f32[19,8,16,128]{3,2,1,0:T(8,128)} %param.8) | copy-start | bytes 3735556
  1.5 36.1 %collective-permute-start.31 = (f32[1,16,128]{2,1,0:T(8,128)S(1)}, f32[1,16,128]{2,1,0:T(8,128)S(1)}, u32[]{:S(2)}, u32[]{:S(2)}) collective-permute-start(f32[1,16,128]{2,1,0:T(8,128)S(1)} %get-tuple-element.53), channel_id=1, source_target_pairs={{2,0},{4,2},{6,4},{8,6},{10,8},{12,10},{14,12},{16,14},{18,16},{20... | collective-permute-start | bytes 24584 | tf_op jit(solution)/shard_map/ppermute | solution.py:51
  8.4 29.1 %collective-permute-start.32 = (f32[1,16,128]{2,1,0:T(8,128)S(1)}, f32[1,16,128]{2,1,0:T(8,128)S(1)}, u32[]{:S(2)}, u32[]{:S(2)}) collective-permute-start(f32[1,16,128]{2,1,0:T(8,128)S(1)} %get-tuple-element.54), channel_id=1, source_target_pairs={{0,2},{2,4},{4,6},{6,8},{8,10},{10,12},{12,14},{14,16},{16,18},{18... | collective-permute-start | bytes 24584 | tf_op jit(solution)/shard_map/ppermute | solution.py:49
  9.4 41.3 %collective-permute-start.10 = (f32[19,1,16,128]{3,2,1,0:T(8,128)S(1)}, f32[19,1,16,128]{3,2,1,0:T(8,128)S(1)}, u32[]{:S(2)}, u32[]{:S(2)}) collective-permute-start(f32[19,1,16,128]{3,2,1,0:T(8,128)S(1)} %get-tuple-element.29), channel_id=1, source_target_pairs={{2,0},{4,2},{6,4},{8,6},{10,8},{12,10},{14,12},{16,14},{18,16},{20... | collective-permute-start | bytes 466952 | tf_op jit(solution)/shard_map/ppermute | solution.py:51
  15.1 23.1 %collective-permute-start.9 = (f32[19,1,16,128]{3,2,1,0:T(8,128)S(1)}, f32[19,1,16,128]{3,2,1,0:T(8,128)S(1)}, u32[]{:S(2)}, u32[]{:S(2)}) collective-permute-start(f32[19,1,16,128]{3,2,1,0:T(8,128)S(1)} %get-tuple-element.30), channel_id=1, source_target_pairs={{0,2},{2,4},{4,6},{6,8},{8,10},{10,12},{12,14},{14,16},{16,18},{18... | collective-permute-start | bytes 466952 | tf_op jit(solution)/shard_map/ppermute | solution.py:49
  37.6 1.2 collective-permute-start.33
  37.7 1.3 collective-permute-start.34
  39.3 13.6 %collective-permute-start.36 = (f32[1,16,128]{2,1,0:T(8,128)S(1)}, f32[1,16,128]{2,1,0:T(8,128)S(1)}, u32[]{:S(2)}, u32[]{:S(2)}) collective-permute-start(f32[1,16,128]{2,1,0:T(8,128)S(1)} %get-tuple-element.47), channel_id=1, source_target_pairs={{0,2},{2,4},{4,6},{6,8},{8,10},{10,12},{12,14},{14,16},{16,18},{18... | collective-permute-start | bytes 24584 | tf_op jit(solution)/shard_map/ppermute | solution.py:49
  39.3 13.7 %collective-permute-start.35 = (f32[1,16,128]{2,1,0:T(8,128)S(1)}, f32[1,16,128]{2,1,0:T(8,128)S(1)}, u32[]{:S(2)}, u32[]{:S(2)}) collective-permute-start(f32[1,16,128]{2,1,0:T(8,128)S(1)} %get-tuple-element.48), channel_id=1, source_target_pairs={{2,0},{4,2},{6,4},{8,6},{10,8},{12,10},{14,12},{16,14},{18,16},{20... | collective-permute-start | bytes 24584 | tf_op jit(solution)/shard_map/ppermute | solution.py:51
  45.0 7.3 %collective-permute-start = (f32[1,16,128]{2,1,0:T(8,128)S(1)}, f32[1,16,128]{2,1,0:T(8,128)S(1)}, u32[]{:S(2)}, u32[]{:S(2)}) collective-permute-start(f32[1,16,128]{2,1,0:T(8,128)S(1)} %get-tuple-element.51), channel_id=1, source_target_pairs={{0,2},{2,4},{4,6},{6,8},{8,10},{10,12},{12,14},{14,16},{16,18},{18... | collective-permute-start | bytes 24584 | tf_op jit(solution)/shard_map/ppermute | solution.py:49
  45.1 7.2 %collective-permute-start.1 = (f32[1,16,128]{2,1,0:T(8,128)S(1)}, f32[1,16,128]{2,1,0:T(8,128)S(1)}, u32[]{:S(2)}, u32[]{:S(2)}) collective-permute-start(f32[1,16,128]{2,1,0:T(8,128)S(1)} %get-tuple-element.52), channel_id=1, source_target_pairs={{2,0},{4,2},{6,4},{8,6},{10,8},{12,10},{14,12},{16,14},{18,16},{20... | collective-permute-start | bytes 24584 | tf_op jit(solution)/shard_map/ppermute | solution.py:51
  50.9 29.2 %copy-start.6 = (f32[8]{0:T(128)S(1)}, f32[8]{0:T(128)}, u32[]{:S(2)}) copy-start(f32[8]{0:T(128)} %param.12) | copy-start | bytes 100
  50.9 29.2 %copy-start.7 = (f32[8]{0:T(128)S(1)}, f32[8]{0:T(128)}, u32[]{:S(2)}) copy-start(f32[8]{0:T(128)} %param.13) | copy-start | bytes 100
  50.9 29.8 %collective-permute-start.11 = (f32[19,10,1,128]{3,2,1,0:T(1,128)S(1)}, f32[19,10,1,128]{3,2,1,0:T(1,128)S(1)}, u32[]{:S(2)}, u32[]{:S(2)}) collective-permute-start(f32[19,10,1,128]{3,2,1,0:T(1,128)S(1)} %get-tuple-element.23), channel_id=1, source_target_pairs={{0,1},{1,0},{2,3},{3,2},{4,5},{5,4},{6,7},{7,6},{8,9},{9,8},{10,11... | collective-permute-start | bytes 291848 | tf_op jit(solution)/shard_map/ppermute | solution.py:49
  52.3 28.4 %collective-permute-start.12 = (f32[19,10,1,128]{3,2,1,0:T(1,128)S(1)}, f32[19,10,1,128]{3,2,1,0:T(1,128)S(1)}, u32[]{:S(2)}, u32[]{:S(2)}) collective-permute-start(f32[19,10,1,128]{3,2,1,0:T(1,128)S(1)} %get-tuple-element.24), channel_id=1, source_target_pairs={{1,0},{0,1},{3,2},{2,3},{5,4},{4,5},{7,6},{6,7},{9,8},{8,9},{11,10... | collective-permute-start | bytes 291848 | tf_op jit(solution)/shard_map/ppermute | solution.py:51
  52.4 1.4 collective-permute-start.2
  52.9 1.2 collective-permute-start.3
  53.0 34.6 %collective-permute-start.37 = (f32[10,1,128]{2,1,0:T(1,128)S(1)}, f32[10,1,128]{2,1,0:T(1,128)S(1)}, u32[]{:S(2)}, u32[]{:S(2)}) collective-permute-start(f32[10,1,128]{2,1,0:T(1,128)S(1)} %get-tuple-element.35), channel_id=1, source_target_pairs={{1,0},{0,1},{3,2},{2,3},{5,4},{4,5},{7,6},{6,7},{9,8},{8,9},{11,10... | collective-permute-start | bytes 15368 | tf_op jit(solution)/shard_map/ppermute | solution.py:51
  53.8 33.9 %collective-permute-start.38 = (f32[10,1,128]{2,1,0:T(1,128)S(1)}, f32[10,1,128]{2,1,0:T(1,128)S(1)}, u32[]{:S(2)}, u32[]{:S(2)}) collective-permute-start(f32[10,1,128]{2,1,0:T(1,128)S(1)} %get-tuple-element.36), channel_id=1, source_target_pairs={{0,1},{1,0},{2,3},{3,2},{4,5},{5,4},{6,7},{7,6},{8,9},{9,8},{10,11... | collective-permute-start | bytes 15368 | tf_op jit(solution)/shard_map/ppermute | solution.py:49
  55.2 1.2 collective-permute-start.4
  56.3 6.6 %collective-permute-start.8 = (f32[8]{0:T(128)S(1)}, f32[8]{0:T(128)S(1)}, u32[]{:S(2)}, u32[]{:S(2)}) collective-permute-start(f32[8]{0:T(128)S(1)} %add.607), channel_id=1, source_target_pairs={{0,30},{2,0},{4,2},{6,4},{8,6},{10,8},{12,10},{14,12},{16,14},{18,... | collective-permute-start | bytes 104 | tf_op jit(solution)/shard_map/ppermute | solution.py:218
  63.0 3.5 %collective-permute-start.7 = (f32[8]{0:T(128)S(1)}, f32[8]{0:T(128)S(1)}, u32[]{:S(2)}, u32[]{:S(2)}) collective-permute-start(f32[8]{0:T(128)S(1)} %add.607), channel_id=1, source_target_pairs={{0,28},{2,30},{4,0},{6,2},{8,4},{10,6},{12,8},{14,10},{16,12},{18,... | collective-permute-start | bytes 104 | tf_op jit(solution)/shard_map/ppermute | solution.py:218
  66.5 6.2 %collective-permute-start.6 = (f32[8]{0:T(128)S(1)}, f32[8]{0:T(128)S(1)}, u32[]{:S(2)}, u32[]{:S(2)}) collective-permute-start(f32[8]{0:T(128)S(1)} %add.607), channel_id=1, source_target_pairs={{0,4},{2,6},{4,8},{6,10},{8,12},{10,14},{12,16},{14,18},{16,20},{1... | collective-permute-start | bytes 104 | tf_op jit(solution)/shard_map/ppermute | solution.py:218
  72.7 7.4 %collective-permute-start.5 = (f32[8]{0:T(128)S(1)}, f32[8]{0:T(128)S(1)}, u32[]{:S(2)}, u32[]{:S(2)}) collective-permute-start(f32[8]{0:T(128)S(1)} %add.607), channel_id=1, source_target_pairs={{0,2},{2,4},{4,6},{6,8},{8,10},{10,12},{12,14},{14,16},{16,18},{18... | collective-permute-start | bytes 104 | tf_op jit(solution)/shard_map/ppermute | solution.py:218
  87.6 35.7 %copy-start.2 = (f32[19,8,16,128]{3,2,1,0:T(8,128)S(1)}, f32[19,8,16,128]{3,2,1,0:T(8,128)}, u32[]{:S(2)}) copy-start(f32[19,8,16,128]{3,2,1,0:T(8,128)} %get-tuple-element.9) | copy-start | bytes 3735556
  89.8 8.8 %collective-permute-start.13 = (f32[8]{0:T(128)S(1)}, f32[8]{0:T(128)S(1)}, u32[]{:S(2)}, u32[]{:S(2)}) collective-permute-start(f32[8]{0:T(128)S(1)} %reduce_sum.41), channel_id=1, source_target_pairs={{0,1},{1,0},{2,3},{3,2},{4,5},{5,4},{6,7},{7,6},{8,9},{9,8},{10,11... | collective-permute-start | bytes 104 | tf_op jit(solution)/shard_map/ppermute | solution.py:218
  89.9 34.3 %collective-permute-start.40 = (f32[1,16,128]{2,1,0:T(8,128)S(1)}, f32[1,16,128]{2,1,0:T(8,128)S(1)}, u32[]{:S(2)}, u32[]{:S(2)}) collective-permute-start(f32[1,16,128]{2,1,0:T(8,128)S(1)} %get-tuple-element.43), channel_id=1, source_target_pairs={{0,2},{2,4},{4,6},{6,8},{8,10},{10,12},{12,14},{14,16},{16,18},{18... | collective-permute-start | bytes 24584 | tf_op jit(solution)/shard_map/ppermute | solution.py:49
  90.5 33.7 %collective-permute-start.39 = (f32[1,16,128]{2,1,0:T(8,128)S(1)}, f32[1,16,128]{2,1,0:T(8,128)S(1)}, u32[]{:S(2)}, u32[]{:S(2)}) collective-permute-start(f32[1,16,128]{2,1,0:T(8,128)S(1)} %get-tuple-element.44), channel_id=1, source_target_pairs={{2,0},{4,2},{6,4},{8,6},{10,8},{12,10},{14,12},{16,14},{18,16},{20... | collective-permute-start | bytes 24584 | tf_op jit(solution)/shard_map/ppermute | solution.py:51
  96.6 26.8 %collective-permute-start.19 = (f32[19,1,16,128]{3,2,1,0:T(8,128)S(1)}, f32[19,1,16,128]{3,2,1,0:T(8,128)S(1)}, u32[]{:S(2)}, u32[]{:S(2)}) collective-permute-start(f32[19,1,16,128]{3,2,1,0:T(8,128)S(1)} %get-tuple-element.27), channel_id=1, source_target_pairs={{2,0},{4,2},{6,4},{8,6},{10,8},{12,10},{14,12},{16,14},{18,16},{20... | collective-permute-start | bytes 466952 | tf_op jit(solution)/shard_map/ppermute | solution.py:51
  96.6 26.6 %collective-permute-start.18 = (f32[19,1,16,128]{3,2,1,0:T(8,128)S(1)}, f32[19,1,16,128]{3,2,1,0:T(8,128)S(1)}, u32[]{:S(2)}, u32[]{:S(2)}) collective-permute-start(f32[19,1,16,128]{3,2,1,0:T(8,128)S(1)} %get-tuple-element.28), channel_id=1, source_target_pairs={{0,2},{2,4},{4,6},{6,8},{8,10},{10,12},{12,14},{14,16},{16,18},{18... | collective-permute-start | bytes 466952 | tf_op jit(solution)/shard_map/ppermute | solution.py:49
  98.7 7.1 %collective-permute-start.17 = (f32[8]{0:T(128)S(1)}, f32[8]{0:T(128)S(1)}, u32[]{:S(2)}, u32[]{:S(2)}) collective-permute-start(f32[8]{0:T(128)S(1)} %add.612), channel_id=1, source_target_pairs={{0,30},{2,0},{4,2},{6,4},{8,6},{10,8},{12,10},{14,12},{16,14},{18,... | collective-permute-start | bytes 104 | tf_op jit(solution)/shard_map/ppermute | solution.py:218
  105.8 3.5 %collective-permute-start.16 = (f32[8]{0:T(128)S(1)}, f32[8]{0:T(128)S(1)}, u32[]{:S(2)}, u32[]{:S(2)}) collective-permute-start(f32[8]{0:T(128)S(1)} %add.612), channel_id=1, source_target_pairs={{0,28},{2,30},{4,0},{6,2},{8,4},{10,6},{12,8},{14,10},{16,12},{18,... | collective-permute-start | bytes 104 | tf_op jit(solution)/shard_map/ppermute | solution.py:218
  109.3 6.2 %collective-permute-start.15 = (f32[8]{0:T(128)S(1)}, f32[8]{0:T(128)S(1)}, u32[]{:S(2)}, u32[]{:S(2)}) collective-permute-start(f32[8]{0:T(128)S(1)} %add.612), channel_id=1, source_target_pairs={{0,4},{2,6},{4,8},{6,10},{8,12},{10,14},{12,16},{14,18},{16,20},{1... | collective-permute-start | bytes 104 | tf_op jit(solution)/shard_map/ppermute | solution.py:218
  115.5 7.1 %collective-permute-start.14 = (f32[8]{0:T(128)S(1)}, f32[8]{0:T(128)S(1)}, u32[]{:S(2)}, u32[]{:S(2)}) collective-permute-start(f32[8]{0:T(128)S(1)} %add.612), channel_id=1, source_target_pairs={{0,2},{2,4},{4,6},{6,8},{8,10},{10,12},{12,14},{14,16},{16,18},{18... | collective-permute-start | bytes 104 | tf_op jit(solution)/shard_map/ppermute | solution.py:218
  123.6 1.4 collective-permute-start.20
  123.7 1.4 collective-permute-start.21
  124.2 12.4 %collective-permute-start.41 = (f32[10,1,128]{2,1,0:T(1,128)S(1)}, f32[10,1,128]{2,1,0:T(1,128)S(1)}, u32[]{:S(2)}, u32[]{:S(2)}) collective-permute-start(f32[10,1,128]{2,1,0:T(1,128)S(1)} %get-tuple-element.33), channel_id=1, source_target_pairs={{1,0},{0,1},{3,2},{2,3},{5,4},{4,5},{7,6},{6,7},{9,8},{8,9},{11,10... | collective-permute-start | bytes 15368 | tf_op jit(solution)/shard_map/ppermute | solution.py:51
  124.3 12.3 %collective-permute-start.42 = (f32[10,1,128]{2,1,0:T(1,128)S(1)}, f32[10,1,128]{2,1,0:T(1,128)S(1)}, u32[]{:S(2)}, u32[]{:S(2)}) collective-permute-start(f32[10,1,128]{2,1,0:T(1,128)S(1)} %get-tuple-element.34), channel_id=1, source_target_pairs={{0,1},{1,0},{2,3},{3,2},{4,5},{5,4},{6,7},{7,6},{8,9},{9,8},{10,11... | collective-permute-start | bytes 15368 | tf_op jit(solution)/shard_map/ppermute | solution.py:49
  133.1 5.2 %collective-permute-start.22 = (f32[8]{0:T(128)S(1)}, f32[8]{0:T(128)S(1)}, u32[]{:S(2)}, u32[]{:S(2)}) collective-permute-start(f32[8]{0:T(128)S(1)} %reduce_sum.42), channel_id=1, source_target_pairs={{0,1},{1,0},{2,3},{3,2},{4,5},{5,4},{6,7},{7,6},{8,9},{9,8},{10,11... | collective-permute-start | bytes 104 | tf_op jit(solution)/shard_map/ppermute | solution.py:218
  134.5 10.0 %collective-permute-start.28 = (f32[19,1,16,128]{3,2,1,0:T(8,128)S(1)}, f32[19,1,16,128]{3,2,1,0:T(8,128)S(1)}, u32[]{:S(2)}, u32[]{:S(2)}) collective-permute-start(f32[19,1,16,128]{3,2,1,0:T(8,128)S(1)} %get-tuple-element.25), channel_id=1, source_target_pairs={{2,0},{4,2},{6,4},{8,6},{10,8},{12,10},{14,12},{16,14},{18,16},{20... | collective-permute-start | bytes 466952 | tf_op jit(solution)/shard_map/ppermute | solution.py:51
  134.7 9.6 %collective-permute-start.27 = (f32[19,1,16,128]{3,2,1,0:T(8,128)S(1)}, f32[19,1,16,128]{3,2,1,0:T(8,128)S(1)}, u32[]{:S(2)}, u32[]{:S(2)}) collective-permute-start(f32[19,1,16,128]{3,2,1,0:T(8,128)S(1)} %get-tuple-element.26), channel_id=1, source_target_pairs={{0,2},{2,4},{4,6},{6,8},{8,10},{10,12},{12,14},{14,16},{16,18},{18... | collective-permute-start | bytes 466952 | tf_op jit(solution)/shard_map/ppermute | solution.py:49
  138.3 6.5 %collective-permute-start.26 = (f32[8]{0:T(128)S(1)}, f32[8]{0:T(128)S(1)}, u32[]{:S(2)}, u32[]{:S(2)}) collective-permute-start(f32[8]{0:T(128)S(1)} %add.617), channel_id=1, source_target_pairs={{0,30},{2,0},{4,2},{6,4},{8,6},{10,8},{12,10},{14,12},{16,14},{18,... | collective-permute-start | bytes 104 | tf_op jit(solution)/shard_map/ppermute | solution.py:218
  142.0 3.5 %collective-permute-start.25 = (f32[8]{0:T(128)S(1)}, f32[8]{0:T(128)S(1)}, u32[]{:S(2)}, u32[]{:S(2)}) collective-permute-start(f32[8]{0:T(128)S(1)} %add.617), channel_id=1, source_target_pairs={{0,28},{2,30},{4,0},{6,2},{8,4},{10,6},{12,8},{14,10},{16,12},{18,... | collective-permute-start | bytes 104 | tf_op jit(solution)/shard_map/ppermute | solution.py:218
  142.0 6.2 %collective-permute-start.24 = (f32[8]{0:T(128)S(1)}, f32[8]{0:T(128)S(1)}, u32[]{:S(2)}, u32[]{:S(2)}) collective-permute-start(f32[8]{0:T(128)S(1)} %add.617), channel_id=1, source_target_pairs={{0,4},{2,6},{4,8},{6,10},{8,12},{10,14},{12,16},{14,18},{16,20},{1... | collective-permute-start | bytes 104 | tf_op jit(solution)/shard_map/ppermute | solution.py:218
  144.3 7.1 %collective-permute-start.23 = (f32[8]{0:T(128)S(1)}, f32[8]{0:T(128)S(1)}, u32[]{:S(2)}, u32[]{:S(2)}) collective-permute-start(f32[8]{0:T(128)S(1)} %add.617), channel_id=1, source_target_pairs={{0,2},{2,4},{4,6},{6,8},{8,10},{10,12},{12,14},{14,16},{16,18},{18... | collective-permute-start | bytes 104 | tf_op jit(solution)/shard_map/ppermute | solution.py:218
  144.7 7.4 %collective-permute-start.29 = (f32[19,10,1,128]{3,2,1,0:T(1,128)S(1)}, f32[19,10,1,128]{3,2,1,0:T(1,128)S(1)}, u32[]{:S(2)}, u32[]{:S(2)}) collective-permute-start(f32[19,10,1,128]{3,2,1,0:T(1,128)S(1)} %get-tuple-element.19), channel_id=1, source_target_pairs={{0,1},{1,0},{2,3},{3,2},{4,5},{5,4},{6,7},{7,6},{8,9},{9,8},{10,11... | collective-permute-start | bytes 291848 | tf_op jit(solution)/shard_map/ppermute | solution.py:49
  144.7 7.3 %collective-permute-start.30 = (f32[19,10,1,128]{3,2,1,0:T(1,128)S(1)}, f32[19,10,1,128]{3,2,1,0:T(1,128)S(1)}, u32[]{:S(2)}, u32[]{:S(2)}) collective-permute-start(f32[19,10,1,128]{3,2,1,0:T(1,128)S(1)} %get-tuple-element.20), channel_id=1, source_target_pairs={{1,0},{0,1},{3,2},{2,3},{5,4},{4,5},{7,6},{6,7},{9,8},{8,9},{11,10... | collective-permute-start | bytes 291848 | tf_op jit(solution)/shard_map/ppermute | solution.py:51
  (3 other events, 42.0 us)

commit v4 on v3

--- a/solution.py
+++ b/solution.py
@@ -211,6 +211,36 @@
     return jnp.concatenate([field[..., 1:], zero_layer], axis=-1)
 
 
+def rim_round(populations, smoke, flow, axis, dim, reach):
+    count = lax.axis_size(axis)
+    fans = flow.shape[0]
+
+    def piece(start):
+        cells = lax.slice_in_dim(populations, start, start + 1, axis=dim)
+        fumes = lax.slice_in_dim(smoke, start, start + 1, axis=dim - 1)[None]
+        carrier = jnp.zeros(cells.shape[1:], jnp.float32).at[0, 0, :fans].set(flow)[None]
+        return jnp.concatenate([cells, fumes, carrier], axis=0)
+
+    head = piece(0)
+    tail = piece(populations.shape[dim] - 1)
+    forward = [(i, (i + 1) % count) for i in range(count)]
+    backward = [((i + 1) % count, i) for i in range(count)]
+    if count == 2:
+        both = lax.ppermute(jnp.concatenate([tail, head], axis=0), axis, forward)
+        from_left = both[: tail.shape[0]]
+        from_right = both[tail.shape[0] :]
+        total = flow + from_left[-1, 0, 0, :fans]
+    else:
+        from_left = lax.ppermute(tail, axis, forward)
+        from_right = lax.ppermute(head, axis, backward)
+        total = flow + from_left[-1, 0, 0, :fans] + from_right[-1, 0, 0, :fans]
+    for offset in sorted(set(step % count for step in range(-reach, reach + 1)) - {0, 1, count - 1}):
+        total = total + lax.ppermute(flow, axis, [(i, (i + offset) % count) for i in range(count)])
+    populations = jnp.concatenate([from_left[:19], populations, from_right[:19]], axis=dim)
+    smoke = jnp.concatenate([from_left[19], smoke, from_right[19]], axis=dim - 1)
+    return (populations, smoke, total)
+
+
 def window_sum(values, axis, width):
     count = lax.axis_size(axis)
     total = values
@@ -274,12 +304,11 @@
     velocity = jnp.stack(velocity)
     partials = jnp.sum(discs[:, 1:-1, 1:-1, :] * velocity[0][None], axis=(1, 2, 3))
     for repeat in range(ITERS):
-        totals = window_sum(window_sum(partials, "band", band_reach), "len", len_reach)
+        extended, rimmed, totals = rim_round(populations, smoke_field, partials, "len", 1, len_reach)
+        extended, rimmed, totals = rim_round(extended, rimmed, totals, "band", 2, band_reach)
         strength = fan_gain * (jet_speed - totals / float(disc_count()))
-        extended = extended_2(populations, (("len", 1), ("band", 2)), 1)
         last = repeat == ITERS - 1
         stepped = lattice_step(strength, extended, discs, solid_rim, not last)
-        rimmed = extended_2(smoke_field, (("len", 0), ("band", 1)), 1)
         ahead_x = rimmed[2:, 1:-1]
         behind_x = rimmed[:-2, 1:-1]
         ahead_y = rimmed[1:-1, 2:]

time: 159 us -> 104 us (0.65)
  starting transfers between devices: 60.4 us -> 31 us
  waiting for transfers between devices: 40.8 us -> 15.8 us
    ppermute x14 -> x2, starting transfers between devices: 30.9 us -> 4.56 us  [extended_2(): lax.ppermute(head, axis, [((i + 1) % count, i) for i in range(count)])]
    ppermute x15, waiting for transfers between devices: 37.9 us -> 15.6 us  [the longest x3 7.15 us: rim_round(): from_left = lax.ppermute(tail, axis, forward)]
    concatenate x0 -> x6, other arithmetic: none -> 5.41 us  [the longest x3 5.29 us: rim_round(): jnp.concatenate([from_left[:19], populations, from_right[:19]], axis=dim)]
    concatenate x5 -> x2, other arithmetic: 5.94 us -> 0.7 us  [extended_2(): jnp.concatenate([lax.ppermute(tail, axis, [(i, (i + 1) % count) for i in...]
    ppermute x14 -> x2, starting transfers between devices: 6.7 us -> 3.06 us  [extended_2(): lax.ppermute(tail, axis, [(i, (i + 1) % count) for i in range(count)])]
    ppermute x14 -> x2, waiting for transfers between devices: 2.28 us -> 0.04 us  [extended_2(): lax.ppermute(tail, axis, [(i, (i + 1) % count) for i in range(count)])]
    add x3, other arithmetic: 2.94 us -> 1 us  [body(): smoke_field = smoke_field + released]
    slice x5 -> x12, local copies, waits for them, and re-layouts: 3.86 us -> 3.19 us  [the longest x3 3.04 us: piece(): cells = lax.slice_in_dim(populations, start, start + 1, axis=dim)]
  transfers between devices with their start and end apart: 43 -> 19, of which waited for: 19 -> 10; matrix products, arithmetic and copies ran while one was open for 23% -> 24% of each run, Pallas kernels for 7% -> 0%
where the time goes in v4:
time: 104 us; the launch traced here: 103 us
  other arithmetic  31.6 us (30%)
  starting transfers between devices  31 us (30%)
  waiting for transfers between devices  15.8 us (15%)
  Pallas kernels  15.2 us (15%)
  local copies, waits for them, and re-layouts  7.94 us (8%)
  between operations  1.25 us (1%)
    ppermute x3, starting transfers between devices, rim_round(): from_right = lax.ppermute(head, axis, backward)  15.8 us
    pallas_call x3, Pallas kernels, lattice_step(): pl.pallas_call(functools.partial(step_kernel, with_moments), out_shape=tu...  15.2 us
    ppermute x3, waiting for transfers between devices, rim_round(): from_left = lax.ppermute(tail, axis, forward)  7.15 us
    ppermute x6, starting transfers between devices, rim_round(): lax.ppermute(flow, axis, [(i, (i + offset) % count) for i in range(count)])  6.12 us
    concatenate x3, other arithmetic, rim_round(): jnp.concatenate([from_left[:19], populations, from_right[:19]], axis=dim)  5.29 us
    mul x8, other arithmetic, fan_discs(): offset_z * offset_z  5.12 us
    lt x5, other arithmetic, fan_discs(): offset_x < FAN_LEN  5.03 us
    mul x5, other arithmetic, fan_discs(): offset_y * offset_y + offset_z * offset_z <= RAD * RAD  4.99 us
  transfers between devices with their start and end apart: 19, of which 10 were waited for; matrix products, arithmetic and copies ran while one was open for 24% of the time, Pallas kernels for 0%

profile of v4, /device:TPU:0, one launch (start us, length us, event | category | flops | bytes accessed | tf_op | source)
XLA Modules:
  0.0 103.0 jit_solution(15109991726303037403)
XLA Ops:
  0.6 1.0 fusion.84
  1.6 3.0 %collective-permute-start = (f32[1,16,128]{2,1,0:T(8,128)S(1)}, f32[1,16,128]{2,1,0:T(8,128)S(1)}, u32[]{:S(2)}, u32[]{:S(2)}) collective-permute-start(f32[1,16,128]{2,1,0:T(8,128)S(1)} %get-tuple-element.174), channel_id=1, source_target_pairs={{0,2},{2,4},{4,6},{6,8},{8,10},{10,12},{12,14},{14,16},{16,18},{18... | collective-permute-start | bytes 24584 | tf_op jit(solution)/shard_map/ppermute | solution.py:49
  4.6 4.1 %collective-permute-start.1 = (f32[1,16,128]{2,1,0:T(8,128)S(1)}, f32[1,16,128]{2,1,0:T(8,128)S(1)}, u32[]{:S(2)}, u32[]{:S(2)}) collective-permute-start(f32[1,16,128]{2,1,0:T(8,128)S(1)} %get-tuple-element.175), channel_id=1, source_target_pairs={{2,0},{4,2},{6,4},{8,6},{10,8},{12,10},{14,12},{16,14},{18,16},{20... | collective-permute-start | bytes 24584 | tf_op jit(solution)/shard_map/ppermute | solution.py:51
  8.7 1.5 %fusion.97 = (s32[1,1]{0,1:T(1,128)}, s32[1,1]{0,1:T(1,128)}, s32[1,1]{0,1:T(1,128)}, s32[1,1]{0,1:T(1,128)}, s32[1,1]{0,1:T(1,128)}) fusion(s32[8,3]{0,1:T(4,128)} %param.35), kind=kLoop, calls=%fused_computation.273 | loop fusion | bytes 40 | tf_op jit(solution)/shard_map/slice | solution.py:170
  10.2 2.1 %fusion.96 = (s32[1,1]{0,1:T(1,128)}, s32[1,1]{0,1:T(1,128)}, s32[1,1]{0,1:T(1,128)}, s32[1,1]{0,1:T(1,128)}, s32[1,1]{0,1:T(1,128)}, /*index=5*/s32[1,1]{0,1:T(...) fusion(s32[8,3]{0,1:T(4,128)} %param.35), kind=kLoop, calls=%fused_computation.272 | loop fusion | bytes 152 | tf_op jit(solution)/shard_map/slice | solution.py:169
  12.3 0.8 subtract_bitcast_fusion.1
  13.1 0.6 subtract_multiply_fusion.14
  13.7 0.7 subtract_multiply_fusion
  14.6 0.7 subtract_multiply_fusion.2
  15.9 0.6 subtract_multiply_fusion.6
  19.0 0.6 subtract_multiply_fusion.13
  19.6 0.7 slice_bitcast_fusion.11
  20.3 1.0 fusion.87
  21.4 1.4 %reduce_sum.38 = f32[8,16,128]{2,1,0:T(8,128)S(1)} reduce(f32[19,8,16,128]{3,2,1,0:T(8,128)} %param.32, f32[]{:T(128)} %constant.305.clone.1), dimensions={0}, to_apply=%region_0.1 | reduce | flops 294912 | bytes 1310724 | tf_op jit(solution)/shard_map/reduce_sum | solution.py:59
  22.9 1.3 %subtract_multiply_fusion.1 = (s32[18]{0:T(128)S(1)}, s32[18]{0:T(128)S(1)}) fusion(s32[]{:T(128)} %bitcast.25, s32[]{:T(128)S(6)} %sub.355, s32[]{:T(128)} %bitcast.22), kind=kLoop, calls=%fused_computation.239 | loop fusion | flops 288 | bytes 156 | tf_op jit(solution)/shard_map/mul | solution.py:173
  24.2 1.2 %subtract_multiply_fusion.5 = (s32[18]{0:T(128)S(1)}, s32[18]{0:T(128)S(1)}) fusion(s32[]{:T(128)} %bitcast.19, s32[]{:T(128)S(6)} %sub.355, s32[]{:T(128)} %bitcast.16), kind=kLoop, calls=%fused_computation.243 | loop fusion | flops 288 | bytes 156 | tf_op jit(solution)/shard_map/mul | solution.py:173
  25.4 1.3 %subtract_multiply_fusion.9 = (s32[18]{0:T(128)S(1)}, s32[18]{0:T(128)S(1)}) fusion(s32[]{:T(128)} %bitcast.13, s32[]{:T(128)S(6)} %sub.355, s32[]{:T(128)} %bitcast.10), kind=kLoop, calls=%fused_computation.247 | loop fusion | flops 288 | bytes 156 | tf_op jit(solution)/shard_map/mul | solution.py:173
  26.7 1.3 %fusion.46 = (pred[10]{0:T(512)(128)(4,1)S(1)}, pred[10]{0:T(512)(128)(4,1)S(1)}) fusion(s32[]{:T(128)} %bitcast.18, s32[]{:T(128)S(6)} %sub.352, s32[]{:T(128)} %bitcast.21), kind=kLoop, calls=%fused_computation.193 | loop fusion | flops 270 | bytes 32 | tf_op jit(solution)/shard_map/lt | solution.py:173
  28.0 1.3 %fusion.44 = (pred[10]{0:T(512)(128)(4,1)S(1)}, pred[10]{0:T(512)(128)(4,1)S(1)}) fusion(s32[]{:T(128)} %bitcast.12, s32[]{:T(128)S(6)} %sub.352, s32[]{:T(128)} %bitcast.15), kind=kLoop, calls=%fused_computation.191 | loop fusion | flops 270 | bytes 32 | tf_op jit(solution)/shard_map/lt | solution.py:173
  29.3 1.2 %fusion.42 = (pred[10]{0:T(512)(128)(4,1)S(1)}, pred[10]{0:T(512)(128)(4,1)S(1)}) fusion(s32[]{:T(128)} %bitcast.6, s32[]{:T(128)S(6)} %sub.352, s32[]{:T(128)} %bitcast.9), kind=kLoop, calls=%fused_computation.189 | loop fusion | flops 270 | bytes 32 | tf_op jit(solution)/shard_map/lt | solution.py:173
  31.1 0.6 fusion.41
  34.4 5.6 %collective-permute-start.5 = (f32[21,1,16,128]{3,2,1,0:T(8,128)S(1)}, f32[21,1,16,128]{3,2,1,0:T(8,128)S(1)}, u32[]{:S(2)}, u32[]{:S(2)}) collective-permute-start(f32[21,1,16,128]{3,2,1,0:T(8,128)S(1)} %get-tuple-element.208), channel_id=1, source_target_pairs={{2,0},{4,2},{6,4},{8,6},{10,8},{12,10},{14,12},{16,14},{18,16},{20... | collective-permute-start | bytes 516104 | tf_op jit(solution)/shard_map/ppermute | solution.py:235
  40.3 2.0 %collective-permute-start.6 = (f32[8]{0:T(128)S(1)}, f32[8]{0:T(128)S(1)}, u32[]{:S(2)}, u32[]{:S(2)}) collective-permute-start(f32[8]{0:T(128)S(1)} %fusion), channel_id=1, source_target_pairs={{0,4},{2,6},{4,8},{6,10},{8,12},{10,14},{12,16},{14,18},{16,20},{1... | collective-permute-start | bytes 104 | tf_op jit(solution)/shard_map/ppermute | solution.py:238
  42.3 2.4 %collective-permute-done.4 = f32[21,1,16,128]{3,2,1,0:T(8,128)S(1)} collective-permute-done((f32[21,1,16,128]{3,2,1,0:T(8,128)S(1)}, f32[21,1,16,128]{3,2,1,0:T(8,128)S(1)}, u32[]{:S(2)}, u32[]{:S(2)}) %collective-permute-start.4) | collective-permute-done | bytes 172064 | tf_op jit(solution)/shard_map/ppermute | solution.py:234
  44.9 1.7 %collective-permute-done.6 = f32[8]{0:T(128)S(1)} collective-permute-done((f32[8]{0:T(128)S(1)}, f32[8]{0:T(128)S(1)}, u32[]{:S(2)}, u32[]{:S(2)}) %collective-permute-start.6) | collective-permute-done | bytes 64 | tf_op jit(solution)/shard_map/ppermute | solution.py:238
  46.9 0.7 pad_maximum_fusion.7.solid_ref
  47.6 0.7 collective-permute-done.8
  48.5 1.8 %pad_maximum_fusion.populations_ref = f32[19,10,18,128]{3,2,1,0:T(8,128)} fusion(f32[19,10,1,128]{3,2,1,0:T(1,128)S(1)} %get-tuple-element.157, f32[19,1,16,128]{3,2,1,0:T(8,128)S(1)} %slice.781, f32[19,8,16,128]{3,2,1,0:T(8,128)S(1)} %copy-done, f32[19,1,16,128]{3,2,1,0:T(8,128)S(1)} %slice.780, f32[19,10,1,128]{3,2,1,0:T(1,128)S(1)} %get-tuple-element.156), kind=kLoop, calls=%fused_computation | loop fusion | flops 1751040 | bytes 3502080 | tf_op jit(solution)/shard_map/concatenate | solution.py:239
  50.8 5.2 %shard_map.95 = (f32[19,8,16,128]{3,2,1,0:T(8,128)}, f32[3,8,16,128]{3,2,1,0:T(8,128)}, f32[8,16,128]{2,1,0:T(8,128)}) custom-call(f32[8]{0:T(128)} %fusion.79.strength_ref, f32[19,10,18,128]{3,2,1,0:T(8,128)} %pad_maximum_fusion.populations_ref, f32[8,10,18,128]{3,2,1,0:T(8,128)} %copy-done.1, f32[10,18,128]{2,1,0:T(8,128)} %pad_maximum_fusion.7.solid_ref), custom_call_target="tpu_custom_call" | custom-call | flops 6912000 | bytes 5253120 | tf_op jit(solution)/shard_map/pallas_call | solution.py:145
  56.0 1.1 %reduce_sum.41 = f32[8]{0:T(128)S(1)} reduce(f32[8,16,128]{2,1,0:T(8,128)} %get-tuple-element.128, f32[]{:T(128)} %constant.305.clone.1), dimensions={1,2}, to_apply=%region_2.3 | reduce | flops 16376 | bytes 65572 | tf_op jit(solution)/shard_map/reduce_sum | solution.py:331
  57.1 1.0 fusion.86
  58.7 5.1 %collective-permute-start.10 = (f32[21,1,16,128]{3,2,1,0:T(8,128)S(1)}, f32[21,1,16,128]{3,2,1,0:T(8,128)S(1)}, u32[]{:S(2)}, u32[]{:S(2)}) collective-permute-start(f32[21,1,16,128]{3,2,1,0:T(8,128)S(1)} %get-tuple-element.179), channel_id=1, source_target_pairs={{2,0},{4,2},{6,4},{8,6},{10,8},{12,10},{14,12},{16,14},{18,16},{20... | collective-permute-start | bytes 516104 | tf_op jit(solution)/shard_map/ppermute | solution.py:235
  63.8 2.0 %collective-permute-start.11 = (f32[8]{0:T(128)S(1)}, f32[8]{0:T(128)S(1)}, u32[]{:S(2)}, u32[]{:S(2)}) collective-permute-start(f32[8]{0:T(128)S(1)} %reduce_sum.41), channel_id=1, source_target_pairs={{0,4},{2,6},{4,8},{6,10},{8,12},{10,14},{12,16},{14,18},{16,20},{1... | collective-permute-start | bytes 104 | tf_op jit(solution)/shard_map/ppermute | solution.py:238
  65.8 2.4 %collective-permute-done.9 = f32[21,1,16,128]{3,2,1,0:T(8,128)S(1)} collective-permute-done((f32[21,1,16,128]{3,2,1,0:T(8,128)S(1)}, f32[21,1,16,128]{3,2,1,0:T(8,128)S(1)}, u32[]{:S(2)}, u32[]{:S(2)}) %collective-permute-start.9) | collective-permute-done | bytes 172064 | tf_op jit(solution)/shard_map/ppermute | solution.py:234
  68.4 1.6 %collective-permute-done.11 = f32[8]{0:T(128)S(1)} collective-permute-done((f32[8]{0:T(128)S(1)}, f32[8]{0:T(128)S(1)}, u32[]{:S(2)}, u32[]{:S(2)}) %collective-permute-start.11) | collective-permute-done | bytes 64 | tf_op jit(solution)/shard_map/ppermute | solution.py:238
  70.3 1.4 %collective-permute-done.13 = f32[42,10,1,128]{3,2,1,0:T(1,128)S(1)} collective-permute-done((f32[42,10,1,128]{3,2,1,0:T(1,128)S(1)}, f32[42,10,1,128]{3,2,1,0:T(1,128)S(1)}, u32[]{:S(2)}, u32[]{:S(2)}) %collective-permute-start.13) | collective-permute-done | bytes 215072 | tf_op jit(solution)/shard_map/ppermute | solution.py:229
  71.9 1.8 %pad_maximum_fusion.1.populations_ref = f32[19,10,18,128]{3,2,1,0:T(8,128)} fusion(f32[19,10,1,128]{3,2,1,0:T(1,128)S(1)} %get-tuple-element.153, f32[19,1,16,128]{3,2,1,0:T(8,128)S(1)} %slice.794, f32[19,8,16,128]{3,2,1,0:T(8,128)S(1)} %copy-done.2, f32[19,1,16,128]{3,2,1,0:T(8,128)S(1)} %slice.793, f32[19,10,1,128]{3,2,1,0:T(1,128)S(1)} %get-tuple-element.152), kind=kLoop, calls=%fused_computation.1 | loop fusion | flops 1751040 | bytes 3502080 | tf_op jit(solution)/shard_map/concatenate | solution.py:239
  74.2 5.2 %shard_map.96 = (f32[19,8,16,128]{3,2,1,0:T(8,128)}, f32[3,8,16,128]{3,2,1,0:T(8,128)}, f32[8,16,128]{2,1,0:T(8,128)}) custom-call(f32[8]{0:T(128)} %fusion.80.strength_ref, f32[19,10,18,128]{3,2,1,0:T(8,128)} %pad_maximum_fusion.1.populations_ref, f32[8,10,18,128]{3,2,1,0:T(8,128)} %copy-done.1, f32[10,18,128]{2,1,0:T(8,128)} %pad_maximum_fusion.7.solid_ref), custom_call_target="tpu_custom_call" | custom-call | flops 6912000 | bytes 5253120 | tf_op jit(solution)/shard_map/pallas_call | solution.py:145
  79.3 1.1 %reduce_sum.42 = f32[8]{0:T(128)S(1)} reduce(f32[8,16,128]{2,1,0:T(8,128)} %get-tuple-element.130, f32[]{:T(128)} %constant.305.clone.1), dimensions={1,2}, to_apply=%region_3.4 | reduce | flops 16376 | bytes 65572 | tf_op jit(solution)/shard_map/reduce_sum | solution.py:331
  80.4 1.0 fusion.85
  82.1 5.1 %collective-permute-start.15 = (f32[21,1,16,128]{3,2,1,0:T(8,128)S(1)}, f32[21,1,16,128]{3,2,1,0:T(8,128)S(1)}, u32[]{:S(2)}, u32[]{:S(2)}) collective-permute-start(f32[21,1,16,128]{3,2,1,0:T(8,128)S(1)} %get-tuple-element.177), channel_id=1, source_target_pairs={{2,0},{4,2},{6,4},{8,6},{10,8},{12,10},{14,12},{16,14},{18,16},{20... | collective-permute-start | bytes 516104 | tf_op jit(solution)/shard_map/ppermute | solution.py:235
  87.2 2.0 %collective-permute-start.16 = (f32[8]{0:T(128)S(1)}, f32[8]{0:T(128)S(1)}, u32[]{:S(2)}, u32[]{:S(2)}) collective-permute-start(f32[8]{0:T(128)S(1)} %reduce_sum.42), channel_id=1, source_target_pairs={{0,4},{2,6},{4,8},{6,10},{8,12},{10,14},{12,16},{14,18},{16,20},{1... | collective-permute-start | bytes 104 | tf_op jit(solution)/shard_map/ppermute | solution.py:238
  89.2 2.4 %collective-permute-done.14 = f32[21,1,16,128]{3,2,1,0:T(8,128)S(1)} collective-permute-done((f32[21,1,16,128]{3,2,1,0:T(8,128)S(1)}, f32[21,1,16,128]{3,2,1,0:T(8,128)S(1)}, u32[]{:S(2)}, u32[]{:S(2)}) %collective-permute-start.14) | collective-permute-done | bytes 172064 | tf_op jit(solution)/shard_map/ppermute | solution.py:234
  91.7 1.6 %collective-permute-done.16 = f32[8]{0:T(128)S(1)} collective-permute-done((f32[8]{0:T(128)S(1)}, f32[8]{0:T(128)S(1)}, u32[]{:S(2)}, u32[]{:S(2)}) %collective-permute-start.16) | collective-permute-done | bytes 64 | tf_op jit(solution)/shard_map/ppermute | solution.py:238
  93.7 1.4 %collective-permute-done.18 = f32[42,10,1,128]{3,2,1,0:T(1,128)S(1)} collective-permute-done((f32[42,10,1,128]{3,2,1,0:T(1,128)S(1)}, f32[42,10,1,128]{3,2,1,0:T(1,128)S(1)}, u32[]{:S(2)}, u32[]{:S(2)}) %collective-permute-start.18) | collective-permute-done | bytes 215072 | tf_op jit(solution)/shard_map/ppermute | solution.py:229
  95.1 1.8 %pad_maximum_fusion.2.populations_ref = f32[19,10,18,128]{3,2,1,0:T(8,128)} fusion(f32[19,10,1,128]{3,2,1,0:T(1,128)S(1)} %get-tuple-element.149, f32[19,1,16,128]{3,2,1,0:T(8,128)S(1)} %slice.809, f32[19,8,16,128]{3,2,1,0:T(8,128)S(1)} %copy-done.3, f32[19,1,16,128]{3,2,1,0:T(8,128)S(1)} %slice.808, f32[19,10,1,128]{3,2,1,0:T(1,128)S(1)} %get-tuple-element.148), kind=kLoop, calls=%fused_computation.2 | loop fusion | flops 1751040 | bytes 3502080 | tf_op jit(solution)/shard_map/concatenate | solution.py:239
  97.3 4.9 %shard_map.97 = f32[19,8,16,128]{3,2,1,0:T(8,128)} custom-call(f32[8]{0:T(128)} %fusion.81.strength_ref, f32[19,10,18,128]{3,2,1,0:T(8,128)} %pad_maximum_fusion.2.populations_ref, f32[8,10,18,128]{3,2,1,0:T(8,128)} %copy-done.1, f32[10,18,128]{2,1,0:T(8,128)} %pad_maximum_fusion.7.solid_ref), custom_call_target="tpu_custom_call" | custom-call | flops 6912000 | bytes 5253120 | tf_op jit(solution)/shard_map/pallas_call | solution.py:145
  102.2 0.7 fusion.13
  (127 shorter events, 11.2 us)
Async XLA Ops:
  0.6 22.1 %copy-start = (f32[19,8,16,128]{3,2,1,0:T(8,128)S(1)}, f32[19,8,16,128]{3,2,1,0:T(8,128)}, u32[]{:S(2)}) copy-start(f32[19,8,16,128]{3,2,1,0:T(8,128)} %param.32) | copy-start | bytes 3735556
  1.6 30.1 %collective-permute-start = (f32[1,16,128]{2,1,0:T(8,128)S(1)}, f32[1,16,128]{2,1,0:T(8,128)S(1)}, u32[]{:S(2)}, u32[]{:S(2)}) collective-permute-start(f32[1,16,128]{2,1,0:T(8,128)S(1)} %get-tuple-element.174), channel_id=1, source_target_pairs={{0,2},{2,4},{4,6},{6,8},{8,10},{10,12},{12,14},{14,16},{16,18},{18... | collective-permute-start | bytes 24584 | tf_op jit(solution)/shard_map/ppermute | solution.py:49
  4.6 27.2 %collective-permute-start.1 = (f32[1,16,128]{2,1,0:T(8,128)S(1)}, f32[1,16,128]{2,1,0:T(8,128)S(1)}, u32[]{:S(2)}, u32[]{:S(2)}) collective-permute-start(f32[1,16,128]{2,1,0:T(8,128)S(1)} %get-tuple-element.175), channel_id=1, source_target_pairs={{2,0},{4,2},{6,4},{8,6},{10,8},{12,10},{14,12},{16,14},{18,16},{20... | collective-permute-start | bytes 24584 | tf_op jit(solution)/shard_map/ppermute | solution.py:51
  22.7 17.3 %copy-start.9 = (f32[16]{0:T(128)S(1)}, f32[16]{0:T(128)}, u32[]{:S(2)}) copy-start(f32[16]{0:T(128)} %param.39) | copy-start | bytes 196
  31.8 1.2 %collective-permute-start.2 = (f32[10,1,128]{2,1,0:T(1,128)S(1)}, f32[10,1,128]{2,1,0:T(1,128)S(1)}, u32[]{:S(2)}, u32[]{:S(2)}) collective-permute-start(f32[10,1,128]{2,1,0:T(1,128)S(1)} %get-tuple-element.158), channel_id=1, source_target_pairs={{0,1},{1,0},{2,3},{3,2},{4,5},{5,4},{6,7},{7,6},{8,9},{9,8},{10,11... | collective-permute-start | bytes 15368 | tf_op jit(solution)/shard_map/ppermute | solution.py:49
  31.9 1.3 %collective-permute-start.3 = (f32[10,1,128]{2,1,0:T(1,128)S(1)}, f32[10,1,128]{2,1,0:T(1,128)S(1)}, u32[]{:S(2)}, u32[]{:S(2)}) collective-permute-start(f32[10,1,128]{2,1,0:T(1,128)S(1)} %get-tuple-element.159), channel_id=1, source_target_pairs={{1,0},{0,1},{3,2},{2,3},{5,4},{4,5},{7,6},{6,7},{9,8},{8,9},{11,10... | collective-permute-start | bytes 15368 | tf_op jit(solution)/shard_map/ppermute | solution.py:51
  34.0 10.9 %copy-start.4 = (f32[8,16,128]{2,1,0:T(8,128)S(1)}, f32[8,16,128]{2,1,0:T(8,128)}, u32[]{:S(2)}) copy-start(f32[8,16,128]{2,1,0:T(8,128)} %param.34) | copy-start | bytes 196612
  34.1 12.6 %copy-start.1 = (f32[8,10,18,128]{3,2,1,0:T(8,128)}, f32[8,10,18,128]{3,2,1,0:T(8,128)S(1)}, u32[]{:S(2)}) copy-start(f32[8,10,18,128]{3,2,1,0:T(8,128)S(1)} %stack.5.discs_ref) | copy-start | bytes 2211844
  34.3 10.4 %collective-permute-start.4 = (f32[21,1,16,128]{3,2,1,0:T(8,128)S(1)}, f32[21,1,16,128]{3,2,1,0:T(8,128)S(1)}, u32[]{:S(2)}, u32[]{:S(2)}) collective-permute-start(f32[21,1,16,128]{3,2,1,0:T(8,128)S(1)} %get-tuple-element.207), channel_id=1, source_target_pairs={{0,2},{2,4},{4,6},{6,8},{8,10},{10,12},{12,14},{14,16},{16,18},{18... | collective-permute-start | bytes 516104 | tf_op jit(solution)/shard_map/ppermute | solution.py:234
  34.4 10.3 %collective-permute-start.5 = (f32[21,1,16,128]{3,2,1,0:T(8,128)S(1)}, f32[21,1,16,128]{3,2,1,0:T(8,128)S(1)}, u32[]{:S(2)}, u32[]{:S(2)}) collective-permute-start(f32[21,1,16,128]{3,2,1,0:T(8,128)S(1)} %get-tuple-element.208), channel_id=1, source_target_pairs={{2,0},{4,2},{6,4},{8,6},{10,8},{12,10},{14,12},{16,14},{18,16},{20... | collective-permute-start | bytes 516104 | tf_op jit(solution)/shard_map/ppermute | solution.py:235
  40.2 4.7 %collective-permute-start.7 = (f32[8]{0:T(128)S(1)}, f32[8]{0:T(128)S(1)}, u32[]{:S(2)}, u32[]{:S(2)}) collective-permute-start(f32[8]{0:T(128)S(1)} %fusion), channel_id=1, source_target_pairs={{0,28},{2,30},{4,0},{6,2},{8,4},{10,6},{12,8},{14,10},{16,12},{18,... | collective-permute-start | bytes 104 | tf_op jit(solution)/shard_map/ppermute | solution.py:238
  40.3 6.3 %collective-permute-start.6 = (f32[8]{0:T(128)S(1)}, f32[8]{0:T(128)S(1)}, u32[]{:S(2)}, u32[]{:S(2)}) collective-permute-start(f32[8]{0:T(128)S(1)} %fusion), channel_id=1, source_target_pairs={{0,4},{2,6},{4,8},{6,10},{8,12},{10,14},{12,16},{14,18},{16,20},{1... | collective-permute-start | bytes 104 | tf_op jit(solution)/shard_map/ppermute | solution.py:238
  46.7 1.5 %collective-permute-start.8 = (f32[42,10,1,128]{3,2,1,0:T(1,128)S(1)}, f32[42,10,1,128]{3,2,1,0:T(1,128)S(1)}, u32[]{:S(2)}, u32[]{:S(2)}) collective-permute-start(f32[42,10,1,128]{3,2,1,0:T(1,128)S(1)} %constant_dynamic-update-slice_fusion), channel_id=1, source_target_pairs={{0,1},{1,0},{2,3},{3,2},{4,5},{5,4},{6,7},{7,6},{8,9},{9,8},{10,11... | collective-permute-start | bytes 645128 | tf_op jit(solution)/shard_map/ppermute | solution.py:229
  48.4 1.8 %copy-start.7 = (f32[8]{0:T(128)S(1)}, f32[8]{0:T(128)}, u32[]{:S(2)}) copy-start(f32[8]{0:T(128)} %param.36) | copy-start | bytes 100
  48.4 1.8 %copy-start.8 = (f32[8]{0:T(128)S(1)}, f32[8]{0:T(128)}, u32[]{:S(2)}) copy-start(f32[8]{0:T(128)} %param.37) | copy-start | bytes 100
  56.0 12.3 %copy-start.2 = (f32[19,8,16,128]{3,2,1,0:T(8,128)S(1)}, f32[19,8,16,128]{3,2,1,0:T(8,128)}, u32[]{:S(2)}) copy-start(f32[19,8,16,128]{3,2,1,0:T(8,128)} %get-tuple-element.129) | copy-start | bytes 3735556
  58.1 13.6 %copy-start.6 = (f32[3,8,16,128]{3,2,1,0:T(8,128)S(1)}, f32[3,8,16,128]{3,2,1,0:T(8,128)}, u32[]{:S(2)}) copy-start(f32[3,8,16,128]{3,2,1,0:T(8,128)} %get-tuple-element.132) | copy-start | bytes 589828
  58.1 10.1 %collective-permute-start.9 = (f32[21,1,16,128]{3,2,1,0:T(8,128)S(1)}, f32[21,1,16,128]{3,2,1,0:T(8,128)S(1)}, u32[]{:S(2)}, u32[]{:S(2)}) collective-permute-start(f32[21,1,16,128]{3,2,1,0:T(8,128)S(1)} %get-tuple-element.178), channel_id=1, source_target_pairs={{0,2},{2,4},{4,6},{6,8},{8,10},{10,12},{12,14},{14,16},{16,18},{18... | collective-permute-start | bytes 516104 | tf_op jit(solution)/shard_map/ppermute | solution.py:234
  58.7 9.5 %collective-permute-start.10 = (f32[21,1,16,128]{3,2,1,0:T(8,128)S(1)}, f32[21,1,16,128]{3,2,1,0:T(8,128)S(1)}, u32[]{:S(2)}, u32[]{:S(2)}) collective-permute-start(f32[21,1,16,128]{3,2,1,0:T(8,128)S(1)} %get-tuple-element.179), channel_id=1, source_target_pairs={{2,0},{4,2},{6,4},{8,6},{10,8},{12,10},{14,12},{16,14},{18,16},{20... | collective-permute-start | bytes 516104 | tf_op jit(solution)/shard_map/ppermute | solution.py:235
  63.8 4.6 %collective-permute-start.12 = (f32[8]{0:T(128)S(1)}, f32[8]{0:T(128)S(1)}, u32[]{:S(2)}, u32[]{:S(2)}) collective-permute-start(f32[8]{0:T(128)S(1)} %reduce_sum.41), channel_id=1, source_target_pairs={{0,28},{2,30},{4,0},{6,2},{8,4},{10,6},{12,8},{14,10},{16,12},{18,... | collective-permute-start | bytes 104 | tf_op jit(solution)/shard_map/ppermute | solution.py:238
  63.8 6.2 %collective-permute-start.11 = (f32[8]{0:T(128)S(1)}, f32[8]{0:T(128)S(1)}, u32[]{:S(2)}, u32[]{:S(2)}) collective-permute-start(f32[8]{0:T(128)S(1)} %reduce_sum.41), channel_id=1, source_target_pairs={{0,4},{2,6},{4,8},{6,10},{8,12},{10,14},{12,16},{14,18},{16,20},{1... | collective-permute-start | bytes 104 | tf_op jit(solution)/shard_map/ppermute | solution.py:238
  70.2 1.5 %collective-permute-start.13 = (f32[42,10,1,128]{3,2,1,0:T(1,128)S(1)}, f32[42,10,1,128]{3,2,1,0:T(1,128)S(1)}, u32[]{:S(2)}, u32[]{:S(2)}) collective-permute-start(f32[42,10,1,128]{3,2,1,0:T(1,128)S(1)} %constant_dynamic-update-slice_fusion.4), channel_id=1, source_target_pairs={{0,1},{1,0},{2,3},{3,2},{4,5},{5,4},{6,7},{7,6},{8,9},{9,8},{10,11... | collective-permute-start | bytes 645128 | tf_op jit(solution)/shard_map/ppermute | solution.py:229
  79.3 12.3 %copy-start.3 = (f32[19,8,16,128]{3,2,1,0:T(8,128)S(1)}, f32[19,8,16,128]{3,2,1,0:T(8,128)}, u32[]{:S(2)}) copy-start(f32[19,8,16,128]{3,2,1,0:T(8,128)} %get-tuple-element.131) | copy-start | bytes 3735556
  81.5 10.1 %collective-permute-start.14 = (f32[21,1,16,128]{3,2,1,0:T(8,128)S(1)}, f32[21,1,16,128]{3,2,1,0:T(8,128)S(1)}, u32[]{:S(2)}, u32[]{:S(2)}) collective-permute-start(f32[21,1,16,128]{3,2,1,0:T(8,128)S(1)} %get-tuple-element.176), channel_id=1, source_target_pairs={{0,2},{2,4},{4,6},{6,8},{8,10},{10,12},{12,14},{14,16},{16,18},{18... | collective-permute-start | bytes 516104 | tf_op jit(solution)/shard_map/ppermute | solution.py:234
  82.1 9.5 %collective-permute-start.15 = (f32[21,1,16,128]{3,2,1,0:T(8,128)S(1)}, f32[21,1,16,128]{3,2,1,0:T(8,128)S(1)}, u32[]{:S(2)}, u32[]{:S(2)}) collective-permute-start(f32[21,1,16,128]{3,2,1,0:T(8,128)S(1)} %get-tuple-element.177), channel_id=1, source_target_pairs={{2,0},{4,2},{6,4},{8,6},{10,8},{12,10},{14,12},{16,14},{18,16},{20... | collective-permute-start | bytes 516104 | tf_op jit(solution)/shard_map/ppermute | solution.py:235
  87.1 4.6 %collective-permute-start.17 = (f32[8]{0:T(128)S(1)}, f32[8]{0:T(128)S(1)}, u32[]{:S(2)}, u32[]{:S(2)}) collective-permute-start(f32[8]{0:T(128)S(1)} %reduce_sum.42), channel_id=1, source_target_pairs={{0,28},{2,30},{4,0},{6,2},{8,4},{10,6},{12,8},{14,10},{16,12},{18,... | collective-permute-start | bytes 104 | tf_op jit(solution)/shard_map/ppermute | solution.py:238
  87.2 6.2 %collective-permute-start.16 = (f32[8]{0:T(128)S(1)}, f32[8]{0:T(128)S(1)}, u32[]{:S(2)}, u32[]{:S(2)}) collective-permute-start(f32[8]{0:T(128)S(1)} %reduce_sum.42), channel_id=1, source_target_pairs={{0,4},{2,6},{4,8},{6,10},{8,12},{10,14},{12,16},{14,18},{16,20},{1... | collective-permute-start | bytes 104 | tf_op jit(solution)/shard_map/ppermute | solution.py:238
  93.5 1.5 %collective-permute-start.18 = (f32[42,10,1,128]{3,2,1,0:T(1,128)S(1)}, f32[42,10,1,128]{3,2,1,0:T(1,128)S(1)}, u32[]{:S(2)}, u32[]{:S(2)}) collective-permute-start(f32[42,10,1,128]{3,2,1,0:T(1,128)S(1)} %constant_dynamic-update-slice_fusion.8), channel_id=1, source_target_pairs={{0,1},{1,0},{2,3},{3,2},{4,5},{5,4},{6,7},{7,6},{8,9},{9,8},{10,11... | collective-permute-start | bytes 645128 | tf_op jit(solution)/shard_map/ppermute | solution.py:229
  97.3 4.9 %copy-start.5 = (f32[3,8,16,128]{3,2,1,0:T(8,128)S(1)}, f32[3,8,16,128]{3,2,1,0:T(8,128)}, u32[]{:S(2)}) copy-start(f32[3,8,16,128]{3,2,1,0:T(8,128)} %get-tuple-element.133) | copy-start | bytes 589828

commit v5 on v4

--- a/solution.py
+++ b/solution.py
@@ -117,19 +117,44 @@
         out_ref[which] = piece
     if not with_moments:
         return
+    moments_into(out_ref, discs_ref, 1, velocity_ref, flow_ref)
+
+
+def moments_into(populations_ref, discs_ref, rim, velocity_ref, flow_ref):
+    fans = discs_ref.shape[0]
+    band_width = populations_ref.shape[2]
     flow_ref[...] = jnp.zeros(flow_ref.shape, jnp.float32)
 
     def moment_plane(index, carry):
-        density, velocity = plane_moments([out_ref[which, index] for which in range(19)])
+        density, velocity = plane_moments([populations_ref[which, index] for which in range(19)])
         for dimension in range(3):
             velocity_ref[dimension, index] = velocity[dimension]
         for fan_number in range(fans):
             flow_ref[fan_number] += (
-                discs_ref[fan_number, index + 1, 1 : 1 + band_width, :] * velocity[0]
+                discs_ref[fan_number, index + rim, rim : rim + band_width, :] * velocity[0]
             )
         return carry
 
-    lax.fori_loop(0, slab_len, moment_plane, 0)
+    lax.fori_loop(0, populations_ref.shape[1], moment_plane, 0)
+
+
+def first_moments(populations, discs):
+    fans, slab_len, band_width, height = discs.shape
+    vmem = pl.BlockSpec(memory_space=pltpu.VMEM)
+    return pl.pallas_call(
+        lambda populations_ref, discs_ref, velocity_ref, flow_ref: moments_into(
+            populations_ref, discs_ref, 0, velocity_ref, flow_ref
+        ),
+        out_shape=(
+            jax.ShapeDtypeStruct((3, slab_len, band_width, height), jnp.float32),
+            jax.ShapeDtypeStruct((fans, band_width, height), jnp.float32),
+        ),
+        in_specs=[vmem, vmem],
+        out_specs=(vmem, vmem),
+        cost_estimate=pl.CostEstimate(
+            flops=60 * discs[0].size, transcendentals=0, bytes_accessed=4 * populations.size
+        ),
+    )(populations, discs)
 
 
 def lattice_step(strength, extended, discs, solid_rim, with_moments):
@@ -300,9 +325,17 @@
     )
     len_reach = max(-(-FAN_LEN // slab_len), (slab_len + FAN_LEN - 1) // slab_len)
     band_reach = max(-(-(2 * RAD + 1) // band_width), (band_width + 2 * RAD) // band_width)
-    density, velocity = moments(populations)
-    velocity = jnp.stack(velocity)
-    partials = jnp.sum(discs[:, 1:-1, 1:-1, :] * velocity[0][None], axis=(1, 2, 3))
+    inner_x = offset_len + jnp.arange(slab_len, dtype=jnp.int32)[:, None, None]
+    inner_y = offset_band + jnp.arange(band_width, dtype=jnp.int32)[None, :, None]
+    air = jnp.logical_not(solid_flag)
+    inner_discs = jnp.stack(
+        [
+            (disc_nodes & air).astype(jnp.float32)
+            for disc_nodes in fan_discs(fan_hubs, inner_x, inner_y, coord_z, length_total)
+        ]
+    )
+    velocity, flow = first_moments(populations, inner_discs)
+    partials = jnp.sum(flow, axis=(1, 2))
     for repeat in range(ITERS):
         extended, rimmed, totals = rim_round(populations, smoke_field, partials, "len", 1, len_reach)
         extended, rimmed, totals = rim_round(extended, rimmed, totals, "band", 2, band_reach)

time: 104 us -> 118 us (1.13)
  other arithmetic: 31.6 us -> 43.3 us
  starting transfers between devices: 31 us -> 34.1 us
  Pallas kernels: 15.2 us -> 17.6 us
  local copies, waits for them, and re-layouts: 7.94 us -> 6.19 us
  waiting for transfers between devices: 15.8 us -> 14.5 us
    lt x5 -> x9, other arithmetic: 5.03 us -> 10.2 us  [fan_discs(): offset_x < FAN_LEN]
    mul x5 -> x9, other arithmetic: 4.99 us -> 10.1 us  [fan_discs(): offset_y * offset_y + offset_z * offset_z <= RAD * RAD]
    ppermute x6, starting transfers between devices: 6.12 us -> 10.1 us  [rim_round(): lax.ppermute(flow, axis, [(i, (i + offset) % count) for i in range(count)])]
    ppermute x3, waiting for transfers between devices: 0.01 us -> 3.52 us  [rim_round(): from_right = lax.ppermute(head, axis, backward)]
    pallas_call x0 -> x1, Pallas kernels: none -> 2.39 us  [first_moments(): pl.pallas_call(lambda populations_ref, discs_ref, velocity_ref, flow_ref:...]
    ppermute x6, waiting for transfers between devices: 4.96 us -> 2.91 us  [rim_round(): lax.ppermute(flow, axis, [(i, (i + offset) % count) for i in range(count)])]
    ppermute x3, waiting for transfers between devices: 7.15 us -> 5.33 us  [rim_round(): from_left = lax.ppermute(tail, axis, forward)]
    ppermute x2, starting transfers between devices: 3.06 us -> 1.56 us  [extended_2(): lax.ppermute(tail, axis, [(i, (i + 1) % count) for i in range(count)])]
  transfers between devices with their start and end apart: 19 -> 19, of which waited for: 10 -> 8; matrix products, arithmetic and copies ran while one was open for 24% -> 12% of each run, Pallas kernels for 0% -> 0%
where the time goes in v5:
time: 118 us; the launch traced here: 117 us
  other arithmetic  43.3 us (37%)
  starting transfers between devices  34.1 us (29%)
  Pallas kernels  17.6 us (15%)
  waiting for transfers between devices  14.5 us (12%)
  local copies, waits for them, and re-layouts  6.19 us (5%)
  between operations  1.33 us (1%)
    ppermute x3, starting transfers between devices, rim_round(): from_right = lax.ppermute(head, axis, backward)  15.4 us
    pallas_call x3, Pallas kernels, lattice_step(): pl.pallas_call(functools.partial(step_kernel, with_moments), out_shape=tu...  15.2 us
    lt x9, other arithmetic, fan_discs(): offset_x < FAN_LEN  10.2 us
    mul x9, other arithmetic, fan_discs(): offset_y * offset_y + offset_z * offset_z <= RAD * RAD  10.1 us
    ppermute x6, starting transfers between devices, rim_round(): lax.ppermute(flow, axis, [(i, (i + offset) % count) for i in range(count)])  10.1 us
    ppermute x3, waiting for transfers between devices, rim_round(): from_left = lax.ppermute(tail, axis, forward)  5.33 us
    concatenate x3, other arithmetic, rim_round(): jnp.concatenate([from_left[:19], populations, from_right[:19]], axis=dim)  5.31 us
    mul x8, other arithmetic, fan_discs(): offset_z * offset_z  5.01 us
  transfers between devices with their start and end apart: 19, of which 8 were waited for; matrix products, arithmetic and copies ran while one was open for 12% of the time, Pallas kernels for 0%

profile of v5, /device:TPU:0, one launch (start us, length us, event | category | flops | bytes accessed | tf_op | source)
XLA Modules:
  0.0 117.2 jit_solution(11485682894568474410)
XLA Ops:
  0.7 1.5 %fusion.108 = (s32[1,1]{0,1:T(1,128)}, s32[1,1]{0,1:T(1,128)}, s32[1,1]{0,1:T(1,128)}, s32[1,1]{0,1:T(1,128)}, s32[1,1]{0,1:T(1,128)}) fusion(s32[8,3]{0,1:T(4,128)} %param.35), kind=kLoop, calls=%fused_computation.331 | loop fusion | bytes 40 | tf_op jit(solution)/shard_map/slice | solution.py:195
  2.1 2.1 %fusion.107 = (s32[1,1]{0,1:T(1,128)}, s32[1,1]{0,1:T(1,128)}, s32[1,1]{0,1:T(1,128)}, s32[1,1]{0,1:T(1,128)}, s32[1,1]{0,1:T(1,128)}, /*index=5*/s32[1,1]{0,1:T...) fusion(s32[8,3]{0,1:T(4,128)} %param.35), kind=kLoop, calls=%fused_computation.330 | loop fusion | bytes 152 | tf_op jit(solution)/shard_map/slice | solution.py:194
  9.3 0.9 fusion.95
  10.2 1.2 %fusion.42 = (pred[8]{0:T(512)(128)(4,1)S(1)}, pred[8]{0:T(512)(128)(4,1)S(1)}) fusion(s32[]{:T(128)} %bitcast.24, s32[]{:T(128)S(6)} %mul.294, s32[]{:T(128)} %bitcast.28), kind=kLoop, calls=%fused_computation.226 | loop fusion | flops 216 | bytes 28 | tf_op jit(solution)/shard_map/lt | solution.py:198
  11.4 1.3 %fusion.40 = (pred[8]{0:T(512)(128)(4,1)S(1)}, pred[8]{0:T(512)(128)(4,1)S(1)}) fusion(s32[]{:T(128)} %bitcast.16, s32[]{:T(128)S(6)} %mul.294, s32[]{:T(128)} %bitcast.20), kind=kLoop, calls=%fused_computation.224 | loop fusion | flops 216 | bytes 28 | tf_op jit(solution)/shard_map/lt | solution.py:198
  12.7 1.3 %fusion.38 = (pred[8]{0:T(512)(128)(4,1)S(1)}, pred[8]{0:T(512)(128)(4,1)S(1)}) fusion(s32[]{:T(128)} %bitcast.8, s32[]{:T(128)S(6)} %mul.294, s32[]{:T(128)} %bitcast.12), kind=kLoop, calls=%fused_computation.222 | loop fusion | flops 216 | bytes 28 | tf_op jit(solution)/shard_map/lt | solution.py:198
  14.0 1.3 %fusion.36 = (pred[8]{0:T(512)(128)(4,1)S(1)}, pred[8]{0:T(512)(128)(4,1)S(1)}) fusion(s32[]{:T(128)} %bitcast, s32[]{:T(128)S(6)} %mul.294, s32[]{:T(128)} %bitcast.4), kind=kLoop, calls=%fused_computation.220 | loop fusion | flops 216 | bytes 28 | tf_op jit(solution)/shard_map/lt | solution.py:198
  15.3 1.3 %subtract_multiply_fusion.21 = (s32[16]{0:T(128)S(1)}, s32[16]{0:T(128)S(1)}) fusion(s32[]{:T(128)} %bitcast.5, s32[]{:T(128)S(6)} %mul.295, s32[]{:T(128)} %bitcast.1), kind=kLoop, calls=%fused_computation.308 | loop fusion | flops 80 | bytes 140 | tf_op jit(solution)/shard_map/mul | solution.py:198
  16.6 1.2 %subtract_multiply_fusion.9 = (s32[16]{0:T(128)S(1)}, s32[16]{0:T(128)S(1)}) fusion(s32[]{:T(128)} %bitcast.29, s32[]{:T(128)S(6)} %mul.295, s32[]{:T(128)} %bitcast.25), kind=kLoop, calls=%fused_computation.296 | loop fusion | flops 80 | bytes 140 | tf_op jit(solution)/shard_map/mul | solution.py:198
  17.8 1.3 %subtract_multiply_fusion.13 = (s32[16]{0:T(128)S(1)}, s32[16]{0:T(128)S(1)}) fusion(s32[]{:T(128)} %bitcast.21, s32[]{:T(128)S(6)} %mul.295, s32[]{:T(128)} %bitcast.17), kind=kLoop, calls=%fused_computation.300 | loop fusion | flops 80 | bytes 140 | tf_op jit(solution)/shard_map/mul | solution.py:198
  19.1 1.3 %subtract_multiply_fusion.17 = (s32[16]{0:T(128)S(1)}, s32[16]{0:T(128)S(1)}) fusion(s32[]{:T(128)} %bitcast.13, s32[]{:T(128)S(6)} %mul.295, s32[]{:T(128)} %bitcast.9), kind=kLoop, calls=%fused_computation.304 | loop fusion | flops 80 | bytes 140 | tf_op jit(solution)/shard_map/mul | solution.py:198
  21.7 0.8 stack.59.discs_ref
  22.5 2.4 %shard_map.95 = (f32[3,8,16,128]{3,2,1,0:T(8,128)}, f32[8,16,128]{2,1,0:T(8,128)}) custom-call(f32[19,8,16,128]{3,2,1,0:T(8,128)} %populations_ref.1, f32[8,8,16,128]{3,2,1,0:T(8,128)} %stack.59.discs_ref), custom_call_target="tpu_custom_call" | custom-call | flops 983040 | bytes 1245184 | tf_op jit(solution)/shard_map/pallas_call | solution.py:144
  24.9 1.0 reduce_sum.27
  25.9 6.0 %collective-permute-start.3 = (f32[8]{0:T(128)S(1)}, f32[8]{0:T(128)S(1)}, u32[]{:S(2)}, u32[]{:S(2)}) collective-permute-start(f32[8]{0:T(128)S(1)} %reduce_sum.27), channel_id=1, source_target_pairs={{0,28},{2,30},{4,0},{6,2},{8,4},{10,6},{12,8},{14,10},{16,12},{18,... | collective-permute-start | bytes 104 | tf_op jit(solution)/shard_map/ppermute | solution.py:263
  32.0 1.5 %collective-permute-start.5 = (f32[1,16,128]{2,1,0:T(8,128)S(1)}, f32[1,16,128]{2,1,0:T(8,128)S(1)}, u32[]{:S(2)}, u32[]{:S(2)}) collective-permute-start(f32[1,16,128]{2,1,0:T(8,128)S(1)} %get-tuple-element.174), channel_id=1, source_target_pairs={{0,2},{2,4},{4,6},{6,8},{8,10},{10,12},{12,14},{14,16},{16,18},{18... | collective-permute-start | bytes 24584 | tf_op jit(solution)/shard_map/ppermute | solution.py:49
  33.4 4.2 %collective-permute-start.6 = (f32[1,16,128]{2,1,0:T(8,128)S(1)}, f32[1,16,128]{2,1,0:T(8,128)S(1)}, u32[]{:S(2)}, u32[]{:S(2)}) collective-permute-start(f32[1,16,128]{2,1,0:T(8,128)S(1)} %get-tuple-element.175), channel_id=1, source_target_pairs={{2,0},{4,2},{6,4},{8,6},{10,8},{12,10},{14,12},{16,14},{18,16},{20... | collective-permute-start | bytes 24584 | tf_op jit(solution)/shard_map/ppermute | solution.py:51
  39.1 1.2 %fusion.49 = (pred[10]{0:T(512)(128)(4,1)S(1)}, pred[10]{0:T(512)(128)(4,1)S(1)}) fusion(s32[]{:T(128)} %bitcast.20, s32[]{:T(128)S(6)} %sub.581, s32[]{:T(128)} %bitcast.24), kind=kLoop, calls=%fused_computation.233 | loop fusion | flops 270 | bytes 32 | tf_op jit(solution)/shard_map/lt | solution.py:198
  40.3 1.3 %fusion.47 = (pred[10]{0:T(512)(128)(4,1)S(1)}, pred[10]{0:T(512)(128)(4,1)S(1)}) fusion(s32[]{:T(128)} %bitcast.12, s32[]{:T(128)S(6)} %sub.581, s32[]{:T(128)} %bitcast.16), kind=kLoop, calls=%fused_computation.231 | loop fusion | flops 270 | bytes 32 | tf_op jit(solution)/shard_map/lt | solution.py:198
  41.6 1.3 %fusion.45 = (pred[10]{0:T(512)(128)(4,1)S(1)}, pred[10]{0:T(512)(128)(4,1)S(1)}) fusion(s32[]{:T(128)} %bitcast.4, s32[]{:T(128)S(6)} %sub.581, s32[]{:T(128)} %bitcast.8), kind=kLoop, calls=%fused_computation.229 | loop fusion | flops 270 | bytes 32 | tf_op jit(solution)/shard_map/lt | solution.py:198
  42.9 1.2 %subtract_multiply_fusion = (s32[18]{0:T(128)S(1)}, s32[18]{0:T(128)S(1)}) fusion(s32[]{:T(128)} %bitcast.29, s32[]{:T(128)S(6)} %sub.584, s32[]{:T(128)} %bitcast.25), kind=kLoop, calls=%fused_computation.286 | loop fusion | flops 288 | bytes 156 | tf_op jit(solution)/shard_map/mul | solution.py:198
  44.1 1.3 %subtract_multiply_fusion.2 = (s32[18]{0:T(128)S(1)}, s32[18]{0:T(128)S(1)}) fusion(s32[]{:T(128)} %bitcast.21, s32[]{:T(128)S(6)} %sub.584, s32[]{:T(128)} %bitcast.17), kind=kLoop, calls=%fused_computation.288 | loop fusion | flops 288 | bytes 156 | tf_op jit(solution)/shard_map/mul | solution.py:198
  45.3 1.3 %subtract_multiply_fusion.4 = (s32[18]{0:T(128)S(1)}, s32[18]{0:T(128)S(1)}) fusion(s32[]{:T(128)} %bitcast.13, s32[]{:T(128)S(6)} %sub.584, s32[]{:T(128)} %bitcast.9), kind=kLoop, calls=%fused_computation.290 | loop fusion | flops 288 | bytes 156 | tf_op jit(solution)/shard_map/mul | solution.py:198
  49.8 5.6 %collective-permute-start.1 = (f32[21,1,16,128]{3,2,1,0:T(8,128)S(1)}, f32[21,1,16,128]{3,2,1,0:T(8,128)S(1)}, u32[]{:S(2)}, u32[]{:S(2)}) collective-permute-start(f32[21,1,16,128]{3,2,1,0:T(8,128)S(1)} %get-tuple-element.210), channel_id=1, source_target_pairs={{2,0},{4,2},{6,4},{8,6},{10,8},{12,10},{14,12},{16,14},{18,16},{20... | collective-permute-start | bytes 516104 | tf_op jit(solution)/shard_map/ppermute | solution.py:260
  56.2 3.2 %collective-permute-done.1 = f32[21,1,16,128]{3,2,1,0:T(8,128)S(1)} collective-permute-done((f32[21,1,16,128]{3,2,1,0:T(8,128)S(1)}, f32[21,1,16,128]{3,2,1,0:T(8,128)S(1)}, u32[]{:S(2)}, u32[]{:S(2)}) %collective-permute-start.1) | collective-permute-done | bytes 172064 | tf_op jit(solution)/shard_map/ppermute | solution.py:260
  59.9 1.0 stack.61.discs_ref
  61.8 1.8 %pad_maximum_fusion.populations_ref = f32[19,10,18,128]{3,2,1,0:T(8,128)} fusion(f32[19,10,1,128]{3,2,1,0:T(1,128)S(1)} %get-tuple-element.159, f32[19,1,16,128]{3,2,1,0:T(8,128)S(1)} %slice.724, f32[19,8,16,128]{3,2,1,0:T(8,128)S(1)} %copy-done, f32[19,1,16,128]{3,2,1,0:T(8,128)S(1)} %slice.723, f32[19,10,1,128]{3,2,1,0:T(1,128)S(1)} %get-tuple-element.158), kind=kLoop, calls=%fused_computation | loop fusion | flops 1751040 | bytes 3502080 | tf_op jit(solution)/shard_map/concatenate | solution.py:264
  64.1 5.2 %shard_map.96 = (f32[19,8,16,128]{3,2,1,0:T(8,128)}, f32[3,8,16,128]{3,2,1,0:T(8,128)}, f32[8,16,128]{2,1,0:T(8,128)}) custom-call(f32[8]{0:T(128)} %fusion.90.strength_ref, f32[19,10,18,128]{3,2,1,0:T(8,128)} %pad_maximum_fusion.populations_ref, f32[8,10,18,128]{3,2,1,0:T(8,128)} %stack.61.discs_ref, f32[10,18,128]{2,1,0:T(8,128)} %pad_maximum_fusion.7.solid_ref), custom_call_target="tpu_custom_call" | custom-call | flops 6912000 | bytes 5253120 | tf_op jit(solution)/shard_map/pallas_call | solution.py:170
  69.2 1.1 reduce_sum.28
  70.3 1.0 fusion.97
  71.5 6.1 %collective-permute-start.10 = (f32[21,1,16,128]{3,2,1,0:T(8,128)S(1)}, f32[21,1,16,128]{3,2,1,0:T(8,128)S(1)}, u32[]{:S(2)}, u32[]{:S(2)}) collective-permute-start(f32[21,1,16,128]{3,2,1,0:T(8,128)S(1)} %get-tuple-element.181), channel_id=1, source_target_pairs={{2,0},{4,2},{6,4},{8,6},{10,8},{12,10},{14,12},{16,14},{18,16},{20... | collective-permute-start | bytes 516104 | tf_op jit(solution)/shard_map/ppermute | solution.py:260
  78.1 1.5 %collective-permute-start.11 = (f32[8]{0:T(128)S(1)}, f32[8]{0:T(128)S(1)}, u32[]{:S(2)}, u32[]{:S(2)}) collective-permute-start(f32[8]{0:T(128)S(1)} %reduce_sum.28), channel_id=1, source_target_pairs={{0,4},{2,6},{4,8},{6,10},{8,12},{10,14},{12,16},{14,18},{16,20},{1... | collective-permute-start | bytes 104 | tf_op jit(solution)/shard_map/ppermute | solution.py:263
  79.6 3.0 %collective-permute-done.9 = f32[21,1,16,128]{3,2,1,0:T(8,128)S(1)} collective-permute-done((f32[21,1,16,128]{3,2,1,0:T(8,128)S(1)}, f32[21,1,16,128]{3,2,1,0:T(8,128)S(1)}, u32[]{:S(2)}, u32[]{:S(2)}) %collective-permute-start.9) | collective-permute-done | bytes 172064 | tf_op jit(solution)/shard_map/ppermute | solution.py:259
  82.8 1.6 %collective-permute-done.11 = f32[8]{0:T(128)S(1)} collective-permute-done((f32[8]{0:T(128)S(1)}, f32[8]{0:T(128)S(1)}, u32[]{:S(2)}, u32[]{:S(2)}) %collective-permute-start.11) | collective-permute-done | bytes 64 | tf_op jit(solution)/shard_map/ppermute | solution.py:263
  84.6 1.4 %collective-permute-done.13 = f32[42,10,1,128]{3,2,1,0:T(1,128)S(1)} collective-permute-done((f32[42,10,1,128]{3,2,1,0:T(1,128)S(1)}, f32[42,10,1,128]{3,2,1,0:T(1,128)S(1)}, u32[]{:S(2)}, u32[]{:S(2)}) %collective-permute-start.13) | collective-permute-done | bytes 215072 | tf_op jit(solution)/shard_map/ppermute | solution.py:254
  86.1 1.8 %pad_maximum_fusion.1.populations_ref = f32[19,10,18,128]{3,2,1,0:T(8,128)} fusion(f32[19,10,1,128]{3,2,1,0:T(1,128)S(1)} %get-tuple-element.155, f32[19,1,16,128]{3,2,1,0:T(8,128)S(1)} %slice.741, f32[19,8,16,128]{3,2,1,0:T(8,128)S(1)} %copy-done.1, f32[19,1,16,128]{3,2,1,0:T(8,128)S(1)} %slice.740, f32[19,10,1,128]{3,2,1,0:T(1,128)S(1)} %get-tuple-element.154), kind=kLoop, calls=%fused_computation.1 | loop fusion | flops 1751040 | bytes 3502080 | tf_op jit(solution)/shard_map/concatenate | solution.py:264
  88.4 5.2 %shard_map.97 = (f32[19,8,16,128]{3,2,1,0:T(8,128)}, f32[3,8,16,128]{3,2,1,0:T(8,128)}, f32[8,16,128]{2,1,0:T(8,128)}) custom-call(f32[8]{0:T(128)} %fusion.91.strength_ref, f32[19,10,18,128]{3,2,1,0:T(8,128)} %pad_maximum_fusion.1.populations_ref, f32[8,10,18,128]{3,2,1,0:T(8,128)} %stack.61.discs_ref, f32[10,18,128]{2,1,0:T(8,128)} %pad_maximum_fusion.7.solid_ref), custom_call_target="tpu_custom_call" | custom-call | flops 6912000 | bytes 5253120 | tf_op jit(solution)/shard_map/pallas_call | solution.py:170
  93.6 1.1 reduce_sum.29
  94.6 1.0 fusion.96
  95.7 2.1 %collective-permute-start.14 = (f32[21,1,16,128]{3,2,1,0:T(8,128)S(1)}, f32[21,1,16,128]{3,2,1,0:T(8,128)S(1)}, u32[]{:S(2)}, u32[]{:S(2)}) collective-permute-start(f32[21,1,16,128]{3,2,1,0:T(8,128)S(1)} %get-tuple-element.178), channel_id=1, source_target_pairs={{0,2},{2,4},{4,6},{6,8},{8,10},{10,12},{12,14},{14,16},{16,18},{18... | collective-permute-start | bytes 516104 | tf_op jit(solution)/shard_map/ppermute | solution.py:259
  97.8 3.6 %collective-permute-start.15 = (f32[21,1,16,128]{3,2,1,0:T(8,128)S(1)}, f32[21,1,16,128]{3,2,1,0:T(8,128)S(1)}, u32[]{:S(2)}, u32[]{:S(2)}) collective-permute-start(f32[21,1,16,128]{3,2,1,0:T(8,128)S(1)} %get-tuple-element.179), channel_id=1, source_target_pairs={{2,0},{4,2},{6,4},{8,6},{10,8},{12,10},{14,12},{16,14},{18,16},{20... | collective-permute-start | bytes 516104 | tf_op jit(solution)/shard_map/ppermute | solution.py:260
  101.4 2.0 %collective-permute-start.16 = (f32[8]{0:T(128)S(1)}, f32[8]{0:T(128)S(1)}, u32[]{:S(2)}, u32[]{:S(2)}) collective-permute-start(f32[8]{0:T(128)S(1)} %reduce_sum.29), channel_id=1, source_target_pairs={{0,4},{2,6},{4,8},{6,10},{8,12},{10,14},{12,16},{14,18},{16,20},{1... | collective-permute-start | bytes 104 | tf_op jit(solution)/shard_map/ppermute | solution.py:263
  103.4 2.4 %collective-permute-done.14 = f32[21,1,16,128]{3,2,1,0:T(8,128)S(1)} collective-permute-done((f32[21,1,16,128]{3,2,1,0:T(8,128)S(1)}, f32[21,1,16,128]{3,2,1,0:T(8,128)S(1)}, u32[]{:S(2)}, u32[]{:S(2)}) %collective-permute-start.14) | collective-permute-done | bytes 172064 | tf_op jit(solution)/shard_map/ppermute | solution.py:259
  106.3 1.3 %collective-permute-done.16 = f32[8]{0:T(128)S(1)} collective-permute-done((f32[8]{0:T(128)S(1)}, f32[8]{0:T(128)S(1)}, u32[]{:S(2)}, u32[]{:S(2)}) %collective-permute-start.16) | collective-permute-done | bytes 64 | tf_op jit(solution)/shard_map/ppermute | solution.py:263
  107.9 1.4 %collective-permute-done.18 = f32[42,10,1,128]{3,2,1,0:T(1,128)S(1)} collective-permute-done((f32[42,10,1,128]{3,2,1,0:T(1,128)S(1)}, f32[42,10,1,128]{3,2,1,0:T(1,128)S(1)}, u32[]{:S(2)}, u32[]{:S(2)}) %collective-permute-start.18) | collective-permute-done | bytes 215072 | tf_op jit(solution)/shard_map/ppermute | solution.py:254
  109.3 1.8 %pad_maximum_fusion.2.populations_ref = f32[19,10,18,128]{3,2,1,0:T(8,128)} fusion(f32[19,10,1,128]{3,2,1,0:T(1,128)S(1)} %get-tuple-element.151, f32[19,1,16,128]{3,2,1,0:T(8,128)S(1)} %slice.756, f32[19,8,16,128]{3,2,1,0:T(8,128)S(1)} %copy-done.2, f32[19,1,16,128]{3,2,1,0:T(8,128)S(1)} %slice.755, f32[19,10,1,128]{3,2,1,0:T(1,128)S(1)} %get-tuple-element.150), kind=kLoop, calls=%fused_computation.2 | loop fusion | flops 1751040 | bytes 3502080 | tf_op jit(solution)/shard_map/concatenate | solution.py:264
  111.6 4.9 %shard_map.98 = f32[19,8,16,128]{3,2,1,0:T(8,128)} custom-call(f32[8]{0:T(128)} %fusion.92.strength_ref, f32[19,10,18,128]{3,2,1,0:T(8,128)} %pad_maximum_fusion.2.populations_ref, f32[8,10,18,128]{3,2,1,0:T(8,128)} %stack.61.discs_ref, f32[10,18,128]{2,1,0:T(8,128)} %pad_maximum_fusion.7.solid_ref), custom_call_target="tpu_custom_call" | custom-call | flops 6912000 | bytes 5253120 | tf_op jit(solution)/shard_map/pallas_call | solution.py:170
  116.5 0.7 fusion.12
  (153 shorter events, 16.3 us)
Async XLA Ops:
  0.6 37.0 %copy-start = (f32[19,8,16,128]{3,2,1,0:T(8,128)S(1)}, f32[19,8,16,128]{3,2,1,0:T(8,128)}, u32[]{:S(2)}) copy-start(f32[19,8,16,128]{3,2,1,0:T(8,128)} %populations_ref.1) | copy-start | bytes 3735556
  0.6 37.0 %copy-start.3 = (f32[8,16,128]{2,1,0:T(8,128)S(1)}, f32[8,16,128]{2,1,0:T(8,128)}, u32[]{:S(2)}) copy-start(f32[8,16,128]{2,1,0:T(8,128)} %param.34) | copy-start | bytes 196612
  9.3 37.4 %copy-start.9 = (s32[16,3]{0,1:T(4,128)S(1)}, s32[16,3]{0,1:T(4,128)}, u32[]{:S(2)}) copy-start(s32[16,3]{0,1:T(4,128)} %param.38) | copy-start | bytes 580
  20.9 26.6 %copy-start.10 = (f32[16]{0:T(128)S(1)}, f32[16]{0:T(128)}, u32[]{:S(2)}) copy-start(f32[16]{0:T(128)} %param.39) | copy-start | bytes 196
  25.9 33.6 %collective-permute-start.3 = (f32[8]{0:T(128)S(1)}, f32[8]{0:T(128)S(1)}, u32[]{:S(2)}, u32[]{:S(2)}) collective-permute-start(f32[8]{0:T(128)S(1)} %reduce_sum.27), channel_id=1, source_target_pairs={{0,28},{2,30},{4,0},{6,2},{8,4},{10,6},{12,8},{14,10},{16,12},{18,... | collective-permute-start | bytes 104 | tf_op jit(solution)/shard_map/ppermute | solution.py:263
  31.9 27.6 %collective-permute-start.2 = (f32[8]{0:T(128)S(1)}, f32[8]{0:T(128)S(1)}, u32[]{:S(2)}, u32[]{:S(2)}) collective-permute-start(f32[8]{0:T(128)S(1)} %reduce_sum.27), channel_id=1, source_target_pairs={{0,4},{2,6},{4,8},{6,10},{8,12},{10,14},{12,16},{14,18},{16,20},{1... | collective-permute-start | bytes 104 | tf_op jit(solution)/shard_map/ppermute | solution.py:263
  32.0 16.6 %collective-permute-start.5 = (f32[1,16,128]{2,1,0:T(8,128)S(1)}, f32[1,16,128]{2,1,0:T(8,128)S(1)}, u32[]{:S(2)}, u32[]{:S(2)}) collective-permute-start(f32[1,16,128]{2,1,0:T(8,128)S(1)} %get-tuple-element.174), channel_id=1, source_target_pairs={{0,2},{2,4},{4,6},{6,8},{8,10},{10,12},{12,14},{14,16},{16,18},{18... | collective-permute-start | bytes 24584 | tf_op jit(solution)/shard_map/ppermute | solution.py:49
  33.4 15.1 %collective-permute-start.6 = (f32[1,16,128]{2,1,0:T(8,128)S(1)}, f32[1,16,128]{2,1,0:T(8,128)S(1)}, u32[]{:S(2)}, u32[]{:S(2)}) collective-permute-start(f32[1,16,128]{2,1,0:T(8,128)S(1)} %get-tuple-element.175), channel_id=1, source_target_pairs={{2,0},{4,2},{6,4},{8,6},{10,8},{12,10},{14,12},{16,14},{18,16},{20... | collective-permute-start | bytes 24584 | tf_op jit(solution)/shard_map/ppermute | solution.py:51
  37.7 18.5 %collective-permute-start = (f32[21,1,16,128]{3,2,1,0:T(8,128)S(1)}, f32[21,1,16,128]{3,2,1,0:T(8,128)S(1)}, u32[]{:S(2)}, u32[]{:S(2)}) collective-permute-start(f32[21,1,16,128]{3,2,1,0:T(8,128)S(1)} %get-tuple-element.209), channel_id=1, source_target_pairs={{0,2},{2,4},{4,6},{6,8},{8,10},{10,12},{12,14},{14,16},{16,18},{18... | collective-permute-start | bytes 516104 | tf_op jit(solution)/shard_map/ppermute | solution.py:259
  48.6 1.2 %collective-permute-start.7 = (f32[10,1,128]{2,1,0:T(1,128)S(1)}, f32[10,1,128]{2,1,0:T(1,128)S(1)}, u32[]{:S(2)}, u32[]{:S(2)}) collective-permute-start(f32[10,1,128]{2,1,0:T(1,128)S(1)} %get-tuple-element.160), channel_id=1, source_target_pairs={{0,1},{1,0},{2,3},{3,2},{4,5},{5,4},{6,7},{7,6},{8,9},{9,8},{10,11... | collective-permute-start | bytes 15368 | tf_op jit(solution)/shard_map/ppermute | solution.py:49
  48.7 6.8 %collective-permute-start.8 = (f32[10,1,128]{2,1,0:T(1,128)S(1)}, f32[10,1,128]{2,1,0:T(1,128)S(1)}, u32[]{:S(2)}, u32[]{:S(2)}) collective-permute-start(f32[10,1,128]{2,1,0:T(1,128)S(1)} %get-tuple-element.161), channel_id=1, source_target_pairs={{1,0},{0,1},{3,2},{2,3},{5,4},{4,5},{7,6},{6,7},{9,8},{8,9},{11,10... | collective-permute-start | bytes 15368 | tf_op jit(solution)/shard_map/ppermute | solution.py:51
  49.8 9.6 %collective-permute-start.1 = (f32[21,1,16,128]{3,2,1,0:T(8,128)S(1)}, f32[21,1,16,128]{3,2,1,0:T(8,128)S(1)}, u32[]{:S(2)}, u32[]{:S(2)}) collective-permute-start(f32[21,1,16,128]{3,2,1,0:T(8,128)S(1)} %get-tuple-element.210), channel_id=1, source_target_pairs={{2,0},{4,2},{6,4},{8,6},{10,8},{12,10},{14,12},{16,14},{18,16},{20... | collective-permute-start | bytes 516104 | tf_op jit(solution)/shard_map/ppermute | solution.py:260
  59.4 2.2 %copy-start.4 = (f32[3,8,16,128]{3,2,1,0:T(8,128)S(1)}, f32[3,8,16,128]{3,2,1,0:T(8,128)}, u32[]{:S(2)}) copy-start(f32[3,8,16,128]{3,2,1,0:T(8,128)} %get-tuple-element.133) | copy-start | bytes 589828
  59.7 1.9 %collective-permute-start.4 = (f32[42,10,1,128]{3,2,1,0:T(1,128)S(1)}, f32[42,10,1,128]{3,2,1,0:T(1,128)S(1)}, u32[]{:S(2)}, u32[]{:S(2)}) collective-permute-start(f32[42,10,1,128]{3,2,1,0:T(1,128)S(1)} %constant_dynamic-update-slice_fusion.8), channel_id=1, source_target_pairs={{0,1},{1,0},{2,3},{3,2},{4,5},{5,4},{6,7},{7,6},{8,9},{9,8},{10,11... | collective-permute-start | bytes 645128 | tf_op jit(solution)/shard_map/ppermute | solution.py:254
  61.7 1.8 %copy-start.7 = (f32[8]{0:T(128)S(1)}, f32[8]{0:T(128)}, u32[]{:S(2)}) copy-start(f32[8]{0:T(128)} %param.36) | copy-start | bytes 100
  61.7 1.8 %copy-start.8 = (f32[8]{0:T(128)S(1)}, f32[8]{0:T(128)}, u32[]{:S(2)}) copy-start(f32[8]{0:T(128)} %param.37) | copy-start | bytes 100
  69.2 13.4 %copy-start.1 = (f32[19,8,16,128]{3,2,1,0:T(8,128)S(1)}, f32[19,8,16,128]{3,2,1,0:T(8,128)}, u32[]{:S(2)}) copy-start(f32[19,8,16,128]{3,2,1,0:T(8,128)} %get-tuple-element.132) | copy-start | bytes 3735556
  71.4 14.6 %copy-start.6 = (f32[3,8,16,128]{3,2,1,0:T(8,128)S(1)}, f32[3,8,16,128]{3,2,1,0:T(8,128)}, u32[]{:S(2)}) copy-start(f32[3,8,16,128]{3,2,1,0:T(8,128)} %get-tuple-element.136) | copy-start | bytes 589828
  71.4 11.2 %collective-permute-start.9 = (f32[21,1,16,128]{3,2,1,0:T(8,128)S(1)}, f32[21,1,16,128]{3,2,1,0:T(8,128)S(1)}, u32[]{:S(2)}, u32[]{:S(2)}) collective-permute-start(f32[21,1,16,128]{3,2,1,0:T(8,128)S(1)} %get-tuple-element.180), channel_id=1, source_target_pairs={{0,2},{2,4},{4,6},{6,8},{8,10},{10,12},{12,14},{14,16},{16,18},{18... | collective-permute-start | bytes 516104 | tf_op jit(solution)/shard_map/ppermute | solution.py:259
  71.5 11.1 %collective-permute-start.10 = (f32[21,1,16,128]{3,2,1,0:T(8,128)S(1)}, f32[21,1,16,128]{3,2,1,0:T(8,128)S(1)}, u32[]{:S(2)}, u32[]{:S(2)}) collective-permute-start(f32[21,1,16,128]{3,2,1,0:T(8,128)S(1)} %get-tuple-element.181), channel_id=1, source_target_pairs={{2,0},{4,2},{6,4},{8,6},{10,8},{12,10},{14,12},{16,14},{18,16},{20... | collective-permute-start | bytes 516104 | tf_op jit(solution)/shard_map/ppermute | solution.py:260
  77.6 5.2 %collective-permute-start.12 = (f32[8]{0:T(128)S(1)}, f32[8]{0:T(128)S(1)}, u32[]{:S(2)}, u32[]{:S(2)}) collective-permute-start(f32[8]{0:T(128)S(1)} %reduce_sum.28), channel_id=1, source_target_pairs={{0,28},{2,30},{4,0},{6,2},{8,4},{10,6},{12,8},{14,10},{16,12},{18,... | collective-permute-start | bytes 104 | tf_op jit(solution)/shard_map/ppermute | solution.py:263
  78.1 6.2 %collective-permute-start.11 = (f32[8]{0:T(128)S(1)}, f32[8]{0:T(128)S(1)}, u32[]{:S(2)}, u32[]{:S(2)}) collective-permute-start(f32[8]{0:T(128)S(1)} %reduce_sum.28), channel_id=1, source_target_pairs={{0,4},{2,6},{4,8},{6,10},{8,12},{10,14},{12,16},{14,18},{16,20},{1... | collective-permute-start | bytes 104 | tf_op jit(solution)/shard_map/ppermute | solution.py:263
  84.4 1.5 %collective-permute-start.13 = (f32[42,10,1,128]{3,2,1,0:T(1,128)S(1)}, f32[42,10,1,128]{3,2,1,0:T(1,128)S(1)}, u32[]{:S(2)}, u32[]{:S(2)}) collective-permute-start(f32[42,10,1,128]{3,2,1,0:T(1,128)S(1)} %constant_dynamic-update-slice_fusion.12), channel_id=1, source_target_pairs={{0,1},{1,0},{2,3},{3,2},{4,5},{5,4},{6,7},{7,6},{8,9},{9,8},{10,11... | collective-permute-start | bytes 645128 | tf_op jit(solution)/shard_map/ppermute | solution.py:254
  93.6 12.6 %copy-start.2 = (f32[19,8,16,128]{3,2,1,0:T(8,128)S(1)}, f32[19,8,16,128]{3,2,1,0:T(8,128)}, u32[]{:S(2)}) copy-start(f32[19,8,16,128]{3,2,1,0:T(8,128)} %get-tuple-element.135) | copy-start | bytes 3735556
  95.7 10.1 %collective-permute-start.14 = (f32[21,1,16,128]{3,2,1,0:T(8,128)S(1)}, f32[21,1,16,128]{3,2,1,0:T(8,128)S(1)}, u32[]{:S(2)}, u32[]{:S(2)}) collective-permute-start(f32[21,1,16,128]{3,2,1,0:T(8,128)S(1)} %get-tuple-element.178), channel_id=1, source_target_pairs={{0,2},{2,4},{4,6},{6,8},{8,10},{10,12},{12,14},{14,16},{16,18},{18... | collective-permute-start | bytes 516104 | tf_op jit(solution)/shard_map/ppermute | solution.py:259
  97.8 8.4 %collective-permute-start.15 = (f32[21,1,16,128]{3,2,1,0:T(8,128)S(1)}, f32[21,1,16,128]{3,2,1,0:T(8,128)S(1)}, u32[]{:S(2)}, u32[]{:S(2)}) collective-permute-start(f32[21,1,16,128]{3,2,1,0:T(8,128)S(1)} %get-tuple-element.179), channel_id=1, source_target_pairs={{2,0},{4,2},{6,4},{8,6},{10,8},{12,10},{14,12},{16,14},{18,16},{20... | collective-permute-start | bytes 516104 | tf_op jit(solution)/shard_map/ppermute | solution.py:260
  101.4 4.9 %collective-permute-start.17 = (f32[8]{0:T(128)S(1)}, f32[8]{0:T(128)S(1)}, u32[]{:S(2)}, u32[]{:S(2)}) collective-permute-start(f32[8]{0:T(128)S(1)} %reduce_sum.29), channel_id=1, source_target_pairs={{0,28},{2,30},{4,0},{6,2},{8,4},{10,6},{12,8},{14,10},{16,12},{18,... | collective-permute-start | bytes 104 | tf_op jit(solution)/shard_map/ppermute | solution.py:263
  101.4 6.2 %collective-permute-start.16 = (f32[8]{0:T(128)S(1)}, f32[8]{0:T(128)S(1)}, u32[]{:S(2)}, u32[]{:S(2)}) collective-permute-start(f32[8]{0:T(128)S(1)} %reduce_sum.29), channel_id=1, source_target_pairs={{0,4},{2,6},{4,8},{6,10},{8,12},{10,14},{12,16},{14,18},{16,20},{1... | collective-permute-start | bytes 104 | tf_op jit(solution)/shard_map/ppermute | solution.py:263
  107.8 1.5 %collective-permute-start.18 = (f32[42,10,1,128]{3,2,1,0:T(1,128)S(1)}, f32[42,10,1,128]{3,2,1,0:T(1,128)S(1)}, u32[]{:S(2)}, u32[]{:S(2)}) collective-permute-start(f32[42,10,1,128]{3,2,1,0:T(1,128)S(1)} %constant_dynamic-update-slice_fusion.16), channel_id=1, source_target_pairs={{0,1},{1,0},{2,3},{3,2},{4,5},{5,4},{6,7},{7,6},{8,9},{9,8},{10,11... | collective-permute-start | bytes 645128 | tf_op jit(solution)/shard_map/ppermute | solution.py:254
  111.6 4.9 %copy-start.5 = (f32[3,8,16,128]{3,2,1,0:T(8,128)S(1)}, f32[3,8,16,128]{3,2,1,0:T(8,128)}, u32[]{:S(2)}) copy-start(f32[3,8,16,128]{3,2,1,0:T(8,128)} %get-tuple-element.137) | copy-start | bytes 589828

commit v6 on v5

--- a/solution.py
+++ b/solution.py
@@ -308,32 +308,28 @@
     breadth_total = band_width * lax.axis_size("band")
     solid_flag = solid_mask == 1
     solid_rim = extended_2(solid_flag.astype(jnp.float32), (("len", 0), ("band", 1)), 1)
-    coord_x = offset_len - 1 + jnp.arange(slab_len + 2, dtype=jnp.int32)[:, None, None]
-    coord_y = jnp.mod(
-        offset_band - 1 + jnp.arange(band_width + 2, dtype=jnp.int32)[None, :, None], breadth_total
-    )
-    coord_z = jnp.arange(height, dtype=jnp.int32)[None, None, :]
+    coord_x = offset_len - 1 + jnp.arange(slab_len + 2, dtype=jnp.int32)
+    coord_y = jnp.mod(offset_band - 1 + jnp.arange(band_width + 2, dtype=jnp.int32), breadth_total)
+    coord_z = jnp.arange(height, dtype=jnp.int32)
+    along_in = jnp.mod(coord_x[None, :] - fan_hubs[:, 0:1], length_total) < FAN_LEN
+    offset_y = coord_y[None, :] - fan_hubs[:, 1:2]
+    offset_z = coord_z[None, :] - fan_hubs[:, 2:3]
+    across_in = (
+        offset_y[:, :, None] * offset_y[:, :, None] + offset_z[:, None, :] * offset_z[:, None, :]
+        <= RAD * RAD
+    )
     air_rim = solid_rim == 0.0
-    discs = jnp.stack(
-        [
-            (disc_nodes & air_rim).astype(jnp.float32)
-            for disc_nodes in fan_discs(fan_hubs, coord_x, coord_y, coord_z, length_total)
-        ]
-    )
+    discs = (along_in[:, :, None, None] & across_in[:, None] & air_rim[None]).astype(jnp.float32)
     released = source_release(
         sources, source_rate, offset_len, offset_band, slab_len, band_width, height
     )
     len_reach = max(-(-FAN_LEN // slab_len), (slab_len + FAN_LEN - 1) // slab_len)
     band_reach = max(-(-(2 * RAD + 1) // band_width), (band_width + 2 * RAD) // band_width)
-    inner_x = offset_len + jnp.arange(slab_len, dtype=jnp.int32)[:, None, None]
-    inner_y = offset_band + jnp.arange(band_width, dtype=jnp.int32)[None, :, None]
-    air = jnp.logical_not(solid_flag)
-    inner_discs = jnp.stack(
-        [
-            (disc_nodes & air).astype(jnp.float32)
-            for disc_nodes in fan_discs(fan_hubs, inner_x, inner_y, coord_z, length_total)
-        ]
-    )
+    inner_discs = (
+        along_in[:, 1:-1, None, None]
+        & across_in[:, None, 1:-1]
+        & jnp.logical_not(solid_flag)[None]
+    ).astype(jnp.float32)
     velocity, flow = first_moments(populations, inner_discs)
     partials = jnp.sum(flow, axis=(1, 2))
     for repeat in range(ITERS):

time: 118 us -> 89.2 us (0.76)
  other arithmetic: 43.3 us -> 15.9 us
  local copies, waits for them, and re-layouts: 6.19 us -> 3.51 us
  waiting for transfers between devices: 14.5 us -> 16.4 us
    mul x17 -> x2, other arithmetic: 15.1 us -> 0.14 us  [the longest x1 0.07 us: body(): offset_z[:, None, :] * offset_z[:, None, :]]
    lt x9 -> x1, other arithmetic: 10.2 us -> 0.08 us  [body(): jnp.mod(coord_x[None, :] - fan_hubs[:, 0:1], length_total) < FAN_LEN]
    slice x2, local copies, waits for them, and re-layouts: 3.57 us -> 0.09 us  [the longest x1 0.08 us: body(): along_in[:, 1:-1, None, None] & across_in[:, None, 1:-1]]
    another operation x4 -> x0, other arithmetic: 2.08 us -> none  [the longest x2 1.15 us: body(): jnp.stack([(disc_nodes & air_rim).astype(jnp.float32) for disc_nodes in f...]
    convert_element_type x0 -> x2, other arithmetic: none -> 2.06 us  [the longest x1 1.13 us: body(): (along_in[:, :, None, None] & across_in[:, None] & air_rim[None]).astype(...]
    ppermute x2, waiting for transfers between devices: 0.02 us -> 1.54 us  [extended_2(): lax.ppermute(tail, axis, [(i, (i + 1) % count) for i in range(count)])]
    unnamed x26 -> x12, other arithmetic: 1.85 us -> 0.52 us
  transfers between devices with their start and end apart: 19 -> 19, of which waited for: 8 -> 11; matrix products, arithmetic and copies ran while one was open for 12% -> 3% of each run, Pallas kernels for 0% -> 0%
where the time goes in v6:
time: 89.2 us; the launch traced here: 88.9 us
  starting transfers between devices  34.1 us (38%)
  Pallas kernels  17.6 us (20%)
  waiting for transfers between devices  16.4 us (18%)
  other arithmetic  15.9 us (18%)
  local copies, waits for them, and re-layouts  3.51 us (4%)
  between operations  1.14 us (1%)
    ppermute x3, starting transfers between devices, rim_round(): from_right = lax.ppermute(head, axis, backward)  15.3 us
    pallas_call x3, Pallas kernels, lattice_step(): pl.pallas_call(functools.partial(step_kernel, with_moments), out_shape=tu...  15.2 us
    ppermute x6, starting transfers between devices, rim_round(): lax.ppermute(flow, axis, [(i, (i + offset) % count) for i in range(count)])  10.1 us
    concatenate x3, other arithmetic, rim_round(): jnp.concatenate([from_left[:19], populations, from_right[:19]], axis=dim)  5.44 us
    ppermute x3, waiting for transfers between devices, rim_round(): from_left = lax.ppermute(tail, axis, forward)  5.01 us
    ppermute x2, starting transfers between devices, extended_2(): lax.ppermute(head, axis, [((i + 1) % count, i) for i in range(count)])  4.66 us
    ppermute x3, waiting for transfers between devices, rim_round(): from_right = lax.ppermute(head, axis, backward)  3.58 us
    ppermute x6, waiting for transfers between devices, rim_round(): lax.ppermute(flow, axis, [(i, (i + offset) % count) for i in range(count)])  3.2 us
  transfers between devices with their start and end apart: 19, of which 11 were waited for; matrix products, arithmetic and copies ran while one was open for 3% of the time, Pallas kernels for 0%

profile of v6, /device:TPU:0, one launch (start us, length us, event | category | flops | bytes accessed | tf_op | source)
XLA Modules:
  0.0 88.9 jit_solution(8427609239773202051)
XLA Ops:
  0.7 0.8 slice_bitcast_fusion.30
  1.8 0.1 add_compare_fusion
  1.9 0.9 fusion.64
  2.8 0.9 %and_convert_fusion.1.discs_ref = f32[8,8,16,128]{3,2,1,0:T(8,128)} fusion(pred[8,16,128]{2,1,0:T(8,128)(4,1)S(1)} %not.3, pred[8,16,128]{2,1,0:T(8,128)(4,1)S(1)} %slice.624, pred[8,8]{1,0:T(8,128)(4,1)S(1)} %slice.528), kind=kLoop, calls=%fused_computation.4 | loop fusion | flops 393216 | bytes 557120 | tf_op jit(solution)/shard_map/convert_element_type | solution.py:332
  3.8 2.4 %shard_map.95 = (f32[3,8,16,128]{3,2,1,0:T(8,128)}, f32[8,16,128]{2,1,0:T(8,128)}) custom-call(f32[19,8,16,128]{3,2,1,0:T(8,128)} %populations_ref.1, f32[8,8,16,128]{3,2,1,0:T(8,128)} %and_convert_fusion.1.discs_ref), custom_call_target="tpu_custom_call" | custom-call | flops 983040 | bytes 1245184 | tf_op jit(solution)/shard_map/pallas_call | solution.py:144
  6.2 1.0 %reduce_sum.27 = f32[8]{0:T(128)S(1)} reduce(f32[8,16,128]{2,1,0:T(8,128)} %get-tuple-element.130, f32[]{:T(128)} %constant.272.clone.1), dimensions={1,2}, to_apply=%region_0.1 | reduce | flops 16376 | bytes 65572 | tf_op jit(solution)/shard_map/reduce_sum | solution.py:334
  7.1 6.0 %collective-permute-start.3 = (f32[8]{0:T(128)S(1)}, f32[8]{0:T(128)S(1)}, u32[]{:S(2)}, u32[]{:S(2)}) collective-permute-start(f32[8]{0:T(128)S(1)} %reduce_sum.27), channel_id=1, source_target_pairs={{0,28},{2,30},{4,0},{6,2},{8,4},{10,6},{12,8},{14,10},{16,12},{18,... | collective-permute-start | bytes 104 | tf_op jit(solution)/shard_map/ppermute | solution.py:263
  13.2 1.5 %collective-permute-start.5 = (f32[1,16,128]{2,1,0:T(8,128)S(1)}, f32[1,16,128]{2,1,0:T(8,128)S(1)}, u32[]{:S(2)}, u32[]{:S(2)}) collective-permute-start(f32[1,16,128]{2,1,0:T(8,128)S(1)} %get-tuple-element.170), channel_id=1, source_target_pairs={{0,2},{2,4},{4,6},{6,8},{8,10},{10,12},{12,14},{14,16},{16,18},{18... | collective-permute-start | bytes 24584 | tf_op jit(solution)/shard_map/ppermute | solution.py:49
  14.7 4.2 %collective-permute-start.6 = (f32[1,16,128]{2,1,0:T(8,128)S(1)}, f32[1,16,128]{2,1,0:T(8,128)S(1)}, u32[]{:S(2)}, u32[]{:S(2)}) collective-permute-start(f32[1,16,128]{2,1,0:T(8,128)S(1)} %get-tuple-element.171), channel_id=1, source_target_pairs={{2,0},{4,2},{6,4},{8,6},{10,8},{12,10},{14,12},{16,14},{18,16},{20... | collective-permute-start | bytes 24584 | tf_op jit(solution)/shard_map/ppermute | solution.py:51
  19.2 0.1 broadcast_multiply_fusion
  19.3 0.2 fusion.2
  19.5 1.0 %collective-permute-done.5 = f32[1,16,128]{2,1,0:T(8,128)S(1)} collective-permute-done((f32[1,16,128]{2,1,0:T(8,128)S(1)}, f32[1,16,128]{2,1,0:T(8,128)S(1)}, u32[]{:S(2)}, u32[]{:S(2)}) %collective-permute-start.5) | collective-permute-done | bytes 8224 | tf_op jit(solution)/shard_map/ppermute | solution.py:49
  20.6 0.5 collective-permute-start.8
  21.1 0.6 collective-permute-done.7
  21.7 5.6 %collective-permute-start.1 = (f32[21,1,16,128]{3,2,1,0:T(8,128)S(1)}, f32[21,1,16,128]{3,2,1,0:T(8,128)S(1)}, u32[]{:S(2)}, u32[]{:S(2)}) collective-permute-start(f32[21,1,16,128]{3,2,1,0:T(8,128)S(1)} %get-tuple-element.185), channel_id=1, source_target_pairs={{2,0},{4,2},{6,4},{8,6},{10,8},{12,10},{14,12},{16,14},{18,16},{20... | collective-permute-start | bytes 516104 | tf_op jit(solution)/shard_map/ppermute | solution.py:260
  27.4 0.7 pad_maximum_fusion.7.solid_ref
  28.1 3.2 %collective-permute-done.1 = f32[21,1,16,128]{3,2,1,0:T(8,128)S(1)} collective-permute-done((f32[21,1,16,128]{3,2,1,0:T(8,128)S(1)}, f32[21,1,16,128]{3,2,1,0:T(8,128)S(1)}, u32[]{:S(2)}, u32[]{:S(2)}) %collective-permute-start.1) | collective-permute-done | bytes 172064 | tf_op jit(solution)/shard_map/ppermute | solution.py:260
  31.7 1.1 %and_convert_fusion.discs_ref = f32[8,10,18,128]{3,2,1,0:T(8,128)} fusion(pred[10,18,128]{2,1,0:T(8,128)(4,1)S(1)} %broadcast_compare_fusion, pred[8,18,128]{2,1,0:T(8,128)(4,1)S(1)} %add_compare_fusion, pred[8,10]{1,0:T(8,128)(4,1)S(1)} %fusion.31), kind=kLoop, calls=%fused_computation.3 | loop fusion | flops 552960 | bytes 778832 | tf_op jit(solution)/shard_map/convert_element_type | solution.py:322
  32.8 0.3 collective-permute-done.4
  33.1 0.1 fusion.24
  33.3 1.8 %pad_maximum_fusion.populations_ref = f32[19,10,18,128]{3,2,1,0:T(8,128)} fusion(f32[19,10,1,128]{3,2,1,0:T(1,128)S(1)} %get-tuple-element.157, f32[19,1,16,128]{3,2,1,0:T(8,128)S(1)} %slice.628, f32[19,8,16,128]{3,2,1,0:T(8,128)S(1)} %copy-done, f32[19,1,16,128]{3,2,1,0:T(8,128)S(1)} %slice.627, f32[19,10,1,128]{3,2,1,0:T(1,128)S(1)} %get-tuple-element.156), kind=kLoop, calls=%fused_computation | loop fusion | flops 1751040 | bytes 3502080 | tf_op jit(solution)/shard_map/concatenate | solution.py:264
  35.1 0.5 fusion.60.strength_ref
  35.6 5.2 %shard_map.96 = (f32[19,8,16,128]{3,2,1,0:T(8,128)}, f32[3,8,16,128]{3,2,1,0:T(8,128)}, f32[8,16,128]{2,1,0:T(8,128)}) custom-call(f32[8]{0:T(128)} %fusion.60.strength_ref, f32[19,10,18,128]{3,2,1,0:T(8,128)} %pad_maximum_fusion.populations_ref, f32[8,10,18,128]{3,2,1,0:T(8,128)} %and_convert_fusion.discs_ref, f32[10,18,128]{2,1,0:T(8,128)} %pad_maximum_fusion.7.solid_ref), custom_call_target="tpu_custom_call" | custom-call | flops 6912000 | bytes 5253120 | tf_op jit(solution)/shard_map/pallas_call | solution.py:170
  40.8 1.1 %reduce_sum.28 = f32[8]{0:T(128)S(1)} reduce(f32[8,16,128]{2,1,0:T(8,128)} %get-tuple-element.131, f32[]{:T(128)} %constant.272.clone.1), dimensions={1,2}, to_apply=%region_1.2 | reduce | flops 16376 | bytes 65572 | tf_op jit(solution)/shard_map/reduce_sum | solution.py:360
  41.9 1.0 %fusion.66 = (f32[19,1,16,128]{3,2,1,0:T(8,128)S(1)}, f32[19,1,16,128]{3,2,1,0:T(8,128)S(1)}) fusion(f32[19,8,16,128]{3,2,1,0:T(8,128)} %get-tuple-element.132), kind=kLoop, calls=%fused_computation.198 | loop fusion | bytes 622592 | tf_op jit(solution)/shard_map/slice | solution.py:244
  43.0 6.1 %collective-permute-start.10 = (f32[21,1,16,128]{3,2,1,0:T(8,128)S(1)}, f32[21,1,16,128]{3,2,1,0:T(8,128)S(1)}, u32[]{:S(2)}, u32[]{:S(2)}) collective-permute-start(f32[21,1,16,128]{3,2,1,0:T(8,128)S(1)} %get-tuple-element.177), channel_id=1, source_target_pairs={{2,0},{4,2},{6,4},{8,6},{10,8},{12,10},{14,12},{16,14},{18,16},{20... | collective-permute-start | bytes 516104 | tf_op jit(solution)/shard_map/ppermute | solution.py:260
  49.2 0.5 collective-permute-start.12
  49.7 1.5 %collective-permute-start.11 = (f32[8]{0:T(128)S(1)}, f32[8]{0:T(128)S(1)}, u32[]{:S(2)}, u32[]{:S(2)}) collective-permute-start(f32[8]{0:T(128)S(1)} %reduce_sum.28), channel_id=1, source_target_pairs={{0,4},{2,6},{4,8},{6,10},{8,12},{10,14},{12,16},{14,18},{16,20},{1... | collective-permute-start | bytes 104 | tf_op jit(solution)/shard_map/ppermute | solution.py:263
  51.2 2.6 %collective-permute-done.9 = f32[21,1,16,128]{3,2,1,0:T(8,128)S(1)} collective-permute-done((f32[21,1,16,128]{3,2,1,0:T(8,128)S(1)}, f32[21,1,16,128]{3,2,1,0:T(8,128)S(1)}, u32[]{:S(2)}, u32[]{:S(2)}) %collective-permute-start.9) | collective-permute-done | bytes 172064 | tf_op jit(solution)/shard_map/ppermute | solution.py:259
  54.0 1.9 %collective-permute-done.11 = f32[8]{0:T(128)S(1)} collective-permute-done((f32[8]{0:T(128)S(1)}, f32[8]{0:T(128)S(1)}, u32[]{:S(2)}, u32[]{:S(2)}) %collective-permute-start.11) | collective-permute-done | bytes 64 | tf_op jit(solution)/shard_map/ppermute | solution.py:263
  56.2 1.4 %collective-permute-done.13 = f32[42,10,1,128]{3,2,1,0:T(1,128)S(1)} collective-permute-done((f32[42,10,1,128]{3,2,1,0:T(1,128)S(1)}, f32[42,10,1,128]{3,2,1,0:T(1,128)S(1)}, u32[]{:S(2)}, u32[]{:S(2)}) %collective-permute-start.13) | collective-permute-done | bytes 215072 | tf_op jit(solution)/shard_map/ppermute | solution.py:254
  57.5 0.1 fusion.18
  57.7 1.8 %pad_maximum_fusion.1.populations_ref = f32[19,10,18,128]{3,2,1,0:T(8,128)} fusion(f32[19,10,1,128]{3,2,1,0:T(1,128)S(1)} %get-tuple-element.153, f32[19,1,16,128]{3,2,1,0:T(8,128)S(1)} %slice.643, f32[19,8,16,128]{3,2,1,0:T(8,128)S(1)} %copy-done.1, f32[19,1,16,128]{3,2,1,0:T(8,128)S(1)} %slice.642, f32[19,10,1,128]{3,2,1,0:T(1,128)S(1)} %get-tuple-element.152), kind=kLoop, calls=%fused_computation.1 | loop fusion | flops 1751040 | bytes 3502080 | tf_op jit(solution)/shard_map/concatenate | solution.py:264
  59.5 0.5 fusion.61.strength_ref
  60.0 5.2 %shard_map.97 = (f32[19,8,16,128]{3,2,1,0:T(8,128)}, f32[3,8,16,128]{3,2,1,0:T(8,128)}, f32[8,16,128]{2,1,0:T(8,128)}) custom-call(f32[8]{0:T(128)} %fusion.61.strength_ref, f32[19,10,18,128]{3,2,1,0:T(8,128)} %pad_maximum_fusion.1.populations_ref, f32[8,10,18,128]{3,2,1,0:T(8,128)} %and_convert_fusion.discs_ref, f32[10,18,128]{2,1,0:T(8,128)} %pad_maximum_fusion.7.solid_ref), custom_call_target="tpu_custom_call" | custom-call | flops 6912000 | bytes 5253120 | tf_op jit(solution)/shard_map/pallas_call | solution.py:170
  65.2 1.1 %reduce_sum.29 = f32[8]{0:T(128)S(1)} reduce(f32[8,16,128]{2,1,0:T(8,128)} %get-tuple-element.134, f32[]{:T(128)} %constant.272.clone.1), dimensions={1,2}, to_apply=%region_2.3 | reduce | flops 16376 | bytes 65572 | tf_op jit(solution)/shard_map/reduce_sum | solution.py:360
  66.3 1.0 %fusion.65 = (f32[19,1,16,128]{3,2,1,0:T(8,128)S(1)}, f32[19,1,16,128]{3,2,1,0:T(8,128)S(1)}) fusion(f32[19,8,16,128]{3,2,1,0:T(8,128)} %get-tuple-element.135), kind=kLoop, calls=%fused_computation.197 | loop fusion | bytes 622592 | tf_op jit(solution)/shard_map/slice | solution.py:244
  67.3 2.1 %collective-permute-start.14 = (f32[21,1,16,128]{3,2,1,0:T(8,128)S(1)}, f32[21,1,16,128]{3,2,1,0:T(8,128)S(1)}, u32[]{:S(2)}, u32[]{:S(2)}) collective-permute-start(f32[21,1,16,128]{3,2,1,0:T(8,128)S(1)} %get-tuple-element.174), channel_id=1, source_target_pairs={{0,2},{2,4},{4,6},{6,8},{8,10},{10,12},{12,14},{14,16},{16,18},{18... | collective-permute-start | bytes 516104 | tf_op jit(solution)/shard_map/ppermute | solution.py:259
  69.4 3.6 %collective-permute-start.15 = (f32[21,1,16,128]{3,2,1,0:T(8,128)S(1)}, f32[21,1,16,128]{3,2,1,0:T(8,128)S(1)}, u32[]{:S(2)}, u32[]{:S(2)}) collective-permute-start(f32[21,1,16,128]{3,2,1,0:T(8,128)S(1)} %get-tuple-element.175), channel_id=1, source_target_pairs={{2,0},{4,2},{6,4},{8,6},{10,8},{12,10},{14,12},{16,14},{18,16},{20... | collective-permute-start | bytes 516104 | tf_op jit(solution)/shard_map/ppermute | solution.py:260
  73.0 2.0 %collective-permute-start.16 = (f32[8]{0:T(128)S(1)}, f32[8]{0:T(128)S(1)}, u32[]{:S(2)}, u32[]{:S(2)}) collective-permute-start(f32[8]{0:T(128)S(1)} %reduce_sum.29), channel_id=1, source_target_pairs={{0,4},{2,6},{4,8},{6,10},{8,12},{10,14},{12,16},{14,18},{16,20},{1... | collective-permute-start | bytes 104 | tf_op jit(solution)/shard_map/ppermute | solution.py:263
  75.0 2.4 %collective-permute-done.14 = f32[21,1,16,128]{3,2,1,0:T(8,128)S(1)} collective-permute-done((f32[21,1,16,128]{3,2,1,0:T(8,128)S(1)}, f32[21,1,16,128]{3,2,1,0:T(8,128)S(1)}, u32[]{:S(2)}, u32[]{:S(2)}) %collective-permute-start.14) | collective-permute-done | bytes 172064 | tf_op jit(solution)/shard_map/ppermute | solution.py:259
  77.4 0.3 collective-permute-done.15
  77.9 1.3 %collective-permute-done.16 = f32[8]{0:T(128)S(1)} collective-permute-done((f32[8]{0:T(128)S(1)}, f32[8]{0:T(128)S(1)}, u32[]{:S(2)}, u32[]{:S(2)}) %collective-permute-start.16) | collective-permute-done | bytes 64 | tf_op jit(solution)/shard_map/ppermute | solution.py:263
  79.5 1.4 %collective-permute-done.18 = f32[42,10,1,128]{3,2,1,0:T(1,128)S(1)} collective-permute-done((f32[42,10,1,128]{3,2,1,0:T(1,128)S(1)}, f32[42,10,1,128]{3,2,1,0:T(1,128)S(1)}, u32[]{:S(2)}, u32[]{:S(2)}) %collective-permute-start.18) | collective-permute-done | bytes 215072 | tf_op jit(solution)/shard_map/ppermute | solution.py:254
  80.9 1.8 %pad_maximum_fusion.2.populations_ref = f32[19,10,18,128]{3,2,1,0:T(8,128)} fusion(f32[19,10,1,128]{3,2,1,0:T(1,128)S(1)} %get-tuple-element.149, f32[19,1,16,128]{3,2,1,0:T(8,128)S(1)} %slice.658, f32[19,8,16,128]{3,2,1,0:T(8,128)S(1)} %copy-done.2, f32[19,1,16,128]{3,2,1,0:T(8,128)S(1)} %slice.657, f32[19,10,1,128]{3,2,1,0:T(1,128)S(1)} %get-tuple-element.148), kind=kLoop, calls=%fused_computation.2 | loop fusion | flops 1751040 | bytes 3502080 | tf_op jit(solution)/shard_map/concatenate | solution.py:264
  82.7 0.5 fusion.62.strength_ref
  83.2 4.9 %shard_map.98 = f32[19,8,16,128]{3,2,1,0:T(8,128)} custom-call(f32[8]{0:T(128)} %fusion.62.strength_ref, f32[19,10,18,128]{3,2,1,0:T(8,128)} %pad_maximum_fusion.2.populations_ref, f32[8,10,18,128]{3,2,1,0:T(8,128)} %and_convert_fusion.discs_ref, f32[10,18,128]{2,1,0:T(8,128)} %pad_maximum_fusion.7.solid_ref), custom_call_target="tpu_custom_call" | custom-call | flops 6912000 | bytes 5253120 | tf_op jit(solution)/shard_map/pallas_call | solution.py:170
  88.1 0.7 fusion.12
  (103 shorter events, 2.2 us)
Async XLA Ops:
  0.6 18.2 %copy-start = (f32[19,8,16,128]{3,2,1,0:T(8,128)S(1)}, f32[19,8,16,128]{3,2,1,0:T(8,128)}, u32[]{:S(2)}) copy-start(f32[19,8,16,128]{3,2,1,0:T(8,128)} %populations_ref.1) | copy-start | bytes 3735556
  0.6 18.2 %copy-start.3 = (f32[8,16,128]{2,1,0:T(8,128)S(1)}, f32[8,16,128]{2,1,0:T(8,128)}, u32[]{:S(2)}) copy-start(f32[8,16,128]{2,1,0:T(8,128)} %param.34) | copy-start | bytes 196612
  0.7 18.3 %copy-start.9 = (s32[16,3]{0,1:T(4,128)S(1)}, s32[16,3]{0,1:T(4,128)}, u32[]{:S(2)}) copy-start(s32[16,3]{0,1:T(4,128)} %param.38) | copy-start | bytes 580
  0.7 18.6 %copy-start.10 = (f32[16]{0:T(128)S(1)}, f32[16]{0:T(128)}, u32[]{:S(2)}) copy-start(f32[16]{0:T(128)} %param.39) | copy-start | bytes 196
  7.1 24.3 %collective-permute-start.3 = (f32[8]{0:T(128)S(1)}, f32[8]{0:T(128)S(1)}, u32[]{:S(2)}, u32[]{:S(2)}) collective-permute-start(f32[8]{0:T(128)S(1)} %reduce_sum.27), channel_id=1, source_target_pairs={{0,28},{2,30},{4,0},{6,2},{8,4},{10,6},{12,8},{14,10},{16,12},{18,... | collective-permute-start | bytes 104 | tf_op jit(solution)/shard_map/ppermute | solution.py:263
  13.2 18.3 %collective-permute-start.2 = (f32[8]{0:T(128)S(1)}, f32[8]{0:T(128)S(1)}, u32[]{:S(2)}, u32[]{:S(2)}) collective-permute-start(f32[8]{0:T(128)S(1)} %reduce_sum.27), channel_id=1, source_target_pairs={{0,4},{2,6},{4,8},{6,10},{8,12},{10,14},{12,16},{14,18},{16,20},{1... | collective-permute-start | bytes 104 | tf_op jit(solution)/shard_map/ppermute | solution.py:263
  13.2 7.3 %collective-permute-start.5 = (f32[1,16,128]{2,1,0:T(8,128)S(1)}, f32[1,16,128]{2,1,0:T(8,128)S(1)}, u32[]{:S(2)}, u32[]{:S(2)}) collective-permute-start(f32[1,16,128]{2,1,0:T(8,128)S(1)} %get-tuple-element.170), channel_id=1, source_target_pairs={{0,2},{2,4},{4,6},{6,8},{8,10},{10,12},{12,14},{14,16},{16,18},{18... | collective-permute-start | bytes 24584 | tf_op jit(solution)/shard_map/ppermute | solution.py:49
  14.7 5.8 %collective-permute-start.6 = (f32[1,16,128]{2,1,0:T(8,128)S(1)}, f32[1,16,128]{2,1,0:T(8,128)S(1)}, u32[]{:S(2)}, u32[]{:S(2)}) collective-permute-start(f32[1,16,128]{2,1,0:T(8,128)S(1)} %get-tuple-element.171), channel_id=1, source_target_pairs={{2,0},{4,2},{6,4},{8,6},{10,8},{12,10},{14,12},{16,14},{18,16},{20... | collective-permute-start | bytes 24584 | tf_op jit(solution)/shard_map/ppermute | solution.py:51
  18.9 9.1 %collective-permute-start = (f32[21,1,16,128]{3,2,1,0:T(8,128)S(1)}, f32[21,1,16,128]{3,2,1,0:T(8,128)S(1)}, u32[]{:S(2)}, u32[]{:S(2)}) collective-permute-start(f32[21,1,16,128]{3,2,1,0:T(8,128)S(1)} %get-tuple-element.184), channel_id=1, source_target_pairs={{0,2},{2,4},{4,6},{6,8},{8,10},{10,12},{12,14},{14,16},{16,18},{18... | collective-permute-start | bytes 516104 | tf_op jit(solution)/shard_map/ppermute | solution.py:259
  20.5 1.2 %collective-permute-start.7 = (f32[10,1,128]{2,1,0:T(1,128)S(1)}, f32[10,1,128]{2,1,0:T(1,128)S(1)}, u32[]{:S(2)}, u32[]{:S(2)}) collective-permute-start(f32[10,1,128]{2,1,0:T(1,128)S(1)} %get-tuple-element.158), channel_id=1, source_target_pairs={{0,1},{1,0},{2,3},{3,2},{4,5},{5,4},{6,7},{7,6},{8,9},{9,8},{10,11... | collective-permute-start | bytes 15368 | tf_op jit(solution)/shard_map/ppermute | solution.py:49
  20.6 6.8 %collective-permute-start.8 = (f32[10,1,128]{2,1,0:T(1,128)S(1)}, f32[10,1,128]{2,1,0:T(1,128)S(1)}, u32[]{:S(2)}, u32[]{:S(2)}) collective-permute-start(f32[10,1,128]{2,1,0:T(1,128)S(1)} %get-tuple-element.159), channel_id=1, source_target_pairs={{1,0},{0,1},{3,2},{2,3},{5,4},{4,5},{7,6},{6,7},{9,8},{8,9},{11,10... | collective-permute-start | bytes 15368 | tf_op jit(solution)/shard_map/ppermute | solution.py:51
  21.7 9.6 %collective-permute-start.1 = (f32[21,1,16,128]{3,2,1,0:T(8,128)S(1)}, f32[21,1,16,128]{3,2,1,0:T(8,128)S(1)}, u32[]{:S(2)}, u32[]{:S(2)}) collective-permute-start(f32[21,1,16,128]{3,2,1,0:T(8,128)S(1)} %get-tuple-element.185), channel_id=1, source_target_pairs={{2,0},{4,2},{6,4},{8,6},{10,8},{12,10},{14,12},{16,14},{18,16},{20... | collective-permute-start | bytes 516104 | tf_op jit(solution)/shard_map/ppermute | solution.py:260
  31.3 1.8 %copy-start.4 = (f32[3,8,16,128]{3,2,1,0:T(8,128)S(1)}, f32[3,8,16,128]{3,2,1,0:T(8,128)}, u32[]{:S(2)}) copy-start(f32[3,8,16,128]{3,2,1,0:T(8,128)} %get-tuple-element.133) | copy-start | bytes 589828
  31.6 1.5 %collective-permute-start.4 = (f32[42,10,1,128]{3,2,1,0:T(1,128)S(1)}, f32[42,10,1,128]{3,2,1,0:T(1,128)S(1)}, u32[]{:S(2)}, u32[]{:S(2)}) collective-permute-start(f32[42,10,1,128]{3,2,1,0:T(1,128)S(1)} %constant_dynamic-update-slice_fusion), channel_id=1, source_target_pairs={{0,1},{1,0},{2,3},{3,2},{4,5},{5,4},{6,7},{7,6},{8,9},{9,8},{10,11... | collective-permute-start | bytes 645128 | tf_op jit(solution)/shard_map/ppermute | solution.py:254
  33.2 1.9 %copy-start.7 = (f32[8]{0:T(128)S(1)}, f32[8]{0:T(128)}, u32[]{:S(2)}) copy-start(f32[8]{0:T(128)} %param.36) | copy-start | bytes 100
  33.3 1.9 %copy-start.8 = (f32[8]{0:T(128)S(1)}, f32[8]{0:T(128)}, u32[]{:S(2)}) copy-start(f32[8]{0:T(128)} %param.37) | copy-start | bytes 100
  40.8 13.1 %copy-start.1 = (f32[19,8,16,128]{3,2,1,0:T(8,128)S(1)}, f32[19,8,16,128]{3,2,1,0:T(8,128)}, u32[]{:S(2)}) copy-start(f32[19,8,16,128]{3,2,1,0:T(8,128)} %get-tuple-element.132) | copy-start | bytes 3735556
  42.9 14.6 %copy-start.6 = (f32[3,8,16,128]{3,2,1,0:T(8,128)S(1)}, f32[3,8,16,128]{3,2,1,0:T(8,128)}, u32[]{:S(2)}) copy-start(f32[3,8,16,128]{3,2,1,0:T(8,128)} %get-tuple-element.136) | copy-start | bytes 589828
  43.0 10.9 %collective-permute-start.9 = (f32[21,1,16,128]{3,2,1,0:T(8,128)S(1)}, f32[21,1,16,128]{3,2,1,0:T(8,128)S(1)}, u32[]{:S(2)}, u32[]{:S(2)}) collective-permute-start(f32[21,1,16,128]{3,2,1,0:T(8,128)S(1)} %get-tuple-element.176), channel_id=1, source_target_pairs={{0,2},{2,4},{4,6},{6,8},{8,10},{10,12},{12,14},{14,16},{16,18},{18... | collective-permute-start | bytes 516104 | tf_op jit(solution)/shard_map/ppermute | solution.py:259
  43.0 10.8 %collective-permute-start.10 = (f32[21,1,16,128]{3,2,1,0:T(8,128)S(1)}, f32[21,1,16,128]{3,2,1,0:T(8,128)S(1)}, u32[]{:S(2)}, u32[]{:S(2)}) collective-permute-start(f32[21,1,16,128]{3,2,1,0:T(8,128)S(1)} %get-tuple-element.177), channel_id=1, source_target_pairs={{2,0},{4,2},{6,4},{8,6},{10,8},{12,10},{14,12},{16,14},{18,16},{20... | collective-permute-start | bytes 516104 | tf_op jit(solution)/shard_map/ppermute | solution.py:260
  49.2 4.8 %collective-permute-start.12 = (f32[8]{0:T(128)S(1)}, f32[8]{0:T(128)S(1)}, u32[]{:S(2)}, u32[]{:S(2)}) collective-permute-start(f32[8]{0:T(128)S(1)} %reduce_sum.28), channel_id=1, source_target_pairs={{0,28},{2,30},{4,0},{6,2},{8,4},{10,6},{12,8},{14,10},{16,12},{18,... | collective-permute-start | bytes 104 | tf_op jit(solution)/shard_map/ppermute | solution.py:263
  49.7 6.2 %collective-permute-start.11 = (f32[8]{0:T(128)S(1)}, f32[8]{0:T(128)S(1)}, u32[]{:S(2)}, u32[]{:S(2)}) collective-permute-start(f32[8]{0:T(128)S(1)} %reduce_sum.28), channel_id=1, source_target_pairs={{0,4},{2,6},{4,8},{6,10},{8,12},{10,14},{12,16},{14,18},{16,20},{1... | collective-permute-start | bytes 104 | tf_op jit(solution)/shard_map/ppermute | solution.py:263
  56.0 1.5 %collective-permute-start.13 = (f32[42,10,1,128]{3,2,1,0:T(1,128)S(1)}, f32[42,10,1,128]{3,2,1,0:T(1,128)S(1)}, u32[]{:S(2)}, u32[]{:S(2)}) collective-permute-start(f32[42,10,1,128]{3,2,1,0:T(1,128)S(1)} %constant_dynamic-update-slice_fusion.4), channel_id=1, source_target_pairs={{0,1},{1,0},{2,3},{3,2},{4,5},{5,4},{6,7},{7,6},{8,9},{9,8},{10,11... | collective-permute-start | bytes 645128 | tf_op jit(solution)/shard_map/ppermute | solution.py:254
  65.2 12.6 %copy-start.2 = (f32[19,8,16,128]{3,2,1,0:T(8,128)S(1)}, f32[19,8,16,128]{3,2,1,0:T(8,128)}, u32[]{:S(2)}) copy-start(f32[19,8,16,128]{3,2,1,0:T(8,128)} %get-tuple-element.135) | copy-start | bytes 3735556
  67.3 10.1 %collective-permute-start.14 = (f32[21,1,16,128]{3,2,1,0:T(8,128)S(1)}, f32[21,1,16,128]{3,2,1,0:T(8,128)S(1)}, u32[]{:S(2)}, u32[]{:S(2)}) collective-permute-start(f32[21,1,16,128]{3,2,1,0:T(8,128)S(1)} %get-tuple-element.174), channel_id=1, source_target_pairs={{0,2},{2,4},{4,6},{6,8},{8,10},{10,12},{12,14},{14,16},{16,18},{18... | collective-permute-start | bytes 516104 | tf_op jit(solution)/shard_map/ppermute | solution.py:259
  69.4 8.4 %collective-permute-start.15 = (f32[21,1,16,128]{3,2,1,0:T(8,128)S(1)}, f32[21,1,16,128]{3,2,1,0:T(8,128)S(1)}, u32[]{:S(2)}, u32[]{:S(2)}) collective-permute-start(f32[21,1,16,128]{3,2,1,0:T(8,128)S(1)} %get-tuple-element.175), channel_id=1, source_target_pairs={{2,0},{4,2},{6,4},{8,6},{10,8},{12,10},{14,12},{16,14},{18,16},{20... | collective-permute-start | bytes 516104 | tf_op jit(solution)/shard_map/ppermute | solution.py:260
  73.0 4.9 %collective-permute-start.17 = (f32[8]{0:T(128)S(1)}, f32[8]{0:T(128)S(1)}, u32[]{:S(2)}, u32[]{:S(2)}) collective-permute-start(f32[8]{0:T(128)S(1)} %reduce_sum.29), channel_id=1, source_target_pairs={{0,28},{2,30},{4,0},{6,2},{8,4},{10,6},{12,8},{14,10},{16,12},{18,... | collective-permute-start | bytes 104 | tf_op jit(solution)/shard_map/ppermute | solution.py:263
  73.0 6.2 %collective-permute-start.16 = (f32[8]{0:T(128)S(1)}, f32[8]{0:T(128)S(1)}, u32[]{:S(2)}, u32[]{:S(2)}) collective-permute-start(f32[8]{0:T(128)S(1)} %reduce_sum.29), channel_id=1, source_target_pairs={{0,4},{2,6},{4,8},{6,10},{8,12},{10,14},{12,16},{14,18},{16,20},{1... | collective-permute-start | bytes 104 | tf_op jit(solution)/shard_map/ppermute | solution.py:263
  79.4 1.5 %collective-permute-start.18 = (f32[42,10,1,128]{3,2,1,0:T(1,128)S(1)}, f32[42,10,1,128]{3,2,1,0:T(1,128)S(1)}, u32[]{:S(2)}, u32[]{:S(2)}) collective-permute-start(f32[42,10,1,128]{3,2,1,0:T(1,128)S(1)} %constant_dynamic-update-slice_fusion.8), channel_id=1, source_target_pairs={{0,1},{1,0},{2,3},{3,2},{4,5},{5,4},{6,7},{7,6},{8,9},{9,8},{10,11... | collective-permute-start | bytes 645128 | tf_op jit(solution)/shard_map/ppermute | solution.py:254
  83.2 4.9 %copy-start.5 = (f32[3,8,16,128]{3,2,1,0:T(8,128)S(1)}, f32[3,8,16,128]{3,2,1,0:T(8,128)}, u32[]{:S(2)}) copy-start(f32[3,8,16,128]{3,2,1,0:T(8,128)} %get-tuple-element.137) | copy-start | bytes 589828

commit v7 on v6

--- a/solution.py
+++ b/solution.py
@@ -236,18 +236,18 @@
     return jnp.concatenate([field[..., 1:], zero_layer], axis=-1)
 
 
-def rim_round(populations, smoke, flow, axis, dim, reach):
+def rim_round(fields, flow, axis, dim, reach):
     count = lax.axis_size(axis)
     fans = flow.shape[0]
+    channels = [field.shape[0] for field in fields]
 
     def piece(start):
-        cells = lax.slice_in_dim(populations, start, start + 1, axis=dim)
-        fumes = lax.slice_in_dim(smoke, start, start + 1, axis=dim - 1)[None]
-        carrier = jnp.zeros(cells.shape[1:], jnp.float32).at[0, 0, :fans].set(flow)[None]
-        return jnp.concatenate([cells, fumes, carrier], axis=0)
+        cells = [lax.slice_in_dim(field, start, start + 1, axis=dim) for field in fields]
+        carrier = jnp.zeros(cells[0].shape[1:], jnp.float32).at[0, 0, :fans].set(flow)[None]
+        return jnp.concatenate(cells + [carrier], axis=0)
 
     head = piece(0)
-    tail = piece(populations.shape[dim] - 1)
+    tail = piece(fields[0].shape[dim] - 1)
     forward = [(i, (i + 1) % count) for i in range(count)]
     backward = [((i + 1) % count, i) for i in range(count)]
     if count == 2:
@@ -261,9 +261,17 @@
         total = flow + from_left[-1, 0, 0, :fans] + from_right[-1, 0, 0, :fans]
     for offset in sorted(set(step % count for step in range(-reach, reach + 1)) - {0, 1, count - 1}):
         total = total + lax.ppermute(flow, axis, [(i, (i + offset) % count) for i in range(count)])
-    populations = jnp.concatenate([from_left[:19], populations, from_right[:19]], axis=dim)
-    smoke = jnp.concatenate([from_left[19], smoke, from_right[19]], axis=dim - 1)
-    return (populations, smoke, total)
+    extended = []
+    first = 0
+    for field, channel in zip(fields, channels):
+        extended.append(
+            jnp.concatenate(
+                [from_left[first : first + channel], field, from_right[first : first + channel]],
+                axis=dim,
+            )
+        )
+        first = first + channel
+    return (extended, total)
 
 
 def window_sum(values, axis, width):
@@ -307,7 +315,6 @@
     length_total = slab_len * lax.axis_size("len")
     breadth_total = band_width * lax.axis_size("band")
     solid_flag = solid_mask == 1
-    solid_rim = extended_2(solid_flag.astype(jnp.float32), (("len", 0), ("band", 1)), 1)
     coord_x = offset_len - 1 + jnp.arange(slab_len + 2, dtype=jnp.int32)
     coord_y = jnp.mod(offset_band - 1 + jnp.arange(band_width + 2, dtype=jnp.int32), breadth_total)
     coord_z = jnp.arange(height, dtype=jnp.int32)
@@ -318,8 +325,6 @@
         offset_y[:, :, None] * offset_y[:, :, None] + offset_z[:, None, :] * offset_z[:, None, :]
         <= RAD * RAD
     )
-    air_rim = solid_rim == 0.0
-    discs = (along_in[:, :, None, None] & across_in[:, None] & air_rim[None]).astype(jnp.float32)
     released = source_release(
         sources, source_rate, offset_len, offset_band, slab_len, band_width, height
     )
@@ -333,8 +338,19 @@
     velocity, flow = first_moments(populations, inner_discs)
     partials = jnp.sum(flow, axis=(1, 2))
     for repeat in range(ITERS):
-        extended, rimmed, totals = rim_round(populations, smoke_field, partials, "len", 1, len_reach)
-        extended, rimmed, totals = rim_round(extended, rimmed, totals, "band", 2, band_reach)
+        fields = [populations, smoke_field[None]]
+        if repeat == 0:
+            fields.append(solid_flag.astype(jnp.float32)[None])
+        fields, totals = rim_round(fields, partials, "len", 1, len_reach)
+        fields, totals = rim_round(fields, totals, "band", 2, band_reach)
+        extended = fields[0]
+        rimmed = fields[1][0]
+        if repeat == 0:
+            solid_rim = fields[2][0]
+            air_rim = solid_rim == 0.0
+            discs = (along_in[:, :, None, None] & across_in[:, None] & air_rim[None]).astype(
+                jnp.float32
+            )
         strength = fan_gain * (jet_speed - totals / float(disc_count()))
         last = repeat == ITERS - 1
         stepped = lattice_step(strength, extended, discs, solid_rim, not last)

time: 89.2 us -> 83.4 us (0.935)
  starting transfers between devices: 34.1 us -> 27.4 us
    ppermute x4 -> x0, starting transfers between devices: 6.22 us -> none  [the longest x2 4.66 us: extended_2(): lax.ppermute(head, axis, [((i + 1) % count, i) for i in range(count)])]
    ppermute x3, waiting for transfers between devices: 5.01 us -> 8.39 us  [rim_round(): from_left = lax.ppermute(tail, axis, forward)]
    ppermute x3, waiting for transfers between devices: 3.58 us -> 0.38 us  [rim_round(): from_right = lax.ppermute(head, axis, backward)]
    ppermute x3, starting transfers between devices: 15.3 us -> 13 us  [rim_round(): from_right = lax.ppermute(head, axis, backward)]
    ppermute x3, starting transfers between devices: 2.19 us -> 4.12 us  [rim_round(): from_left = lax.ppermute(tail, axis, forward)]
    ppermute x4 -> x0, waiting for transfers between devices: 1.54 us -> none  [the longest x2 1.54 us: extended_2(): lax.ppermute(tail, axis, [(i, (i + 1) % count) for i in range(count)])]
    ppermute x3, waiting for transfers between devices: 3.08 us -> 4.14 us  [rim_round(): both = lax.ppermute(jnp.concatenate([tail, head], axis=0), axis, forward)]
    ppermute x6, waiting for transfers between devices: 3.2 us -> 4.22 us  [rim_round(): lax.ppermute(flow, axis, [(i, (i + offset) % count) for i in range(count)])]
  transfers between devices with their start and end apart: 19 -> 15, of which waited for: 11 -> 9; matrix products, arithmetic and copies ran while one was open for 3% -> 1% of each run, Pallas kernels for 0% -> 0%
where the time goes in v7:
time: 83.4 us; the launch traced here: 83 us
  starting transfers between devices  27.4 us (33%)
  Pallas kernels  17.6 us (21%)
  waiting for transfers between devices  17.1 us (21%)
  other arithmetic  16 us (19%)
  local copies, waits for them, and re-layouts  3.54 us (4%)
  between operations  1.12 us (1%)
    pallas_call x3, Pallas kernels, lattice_step(): pl.pallas_call(functools.partial(step_kernel, with_moments), out_shape=tu...  15.2 us
    ppermute x3, starting transfers between devices, rim_round(): from_right = lax.ppermute(head, axis, backward)  13 us
    ppermute x6, starting transfers between devices, rim_round(): lax.ppermute(flow, axis, [(i, (i + offset) % count) for i in range(count)])  10.1 us
    ppermute x3, waiting for transfers between devices, rim_round(): from_left = lax.ppermute(tail, axis, forward)  8.39 us
    concatenate x4, other arithmetic, rim_round(): jnp.concatenate([from_left[first:first + channel], field, from_right[firs...  5.38 us
    ppermute x6, waiting for transfers between devices, rim_round(): lax.ppermute(flow, axis, [(i, (i + offset) % count) for i in range(count)])  4.22 us
    ppermute x3, waiting for transfers between devices, rim_round(): both = lax.ppermute(jnp.concatenate([tail, head], axis=0), axis, forward)  4.14 us
    ppermute x3, starting transfers between devices, rim_round(): from_left = lax.ppermute(tail, axis, forward)  4.12 us
  transfers between devices with their start and end apart: 15, of which 9 were waited for; matrix products, arithmetic and copies ran while one was open for 1% of the time, Pallas kernels for 0%

profile of v7, /device:TPU:0, one launch (start us, length us, event | category | flops | bytes accessed | tf_op | source)
XLA Modules:
  0.0 83.0 jit_solution(12480509343429272199)
XLA Ops:
  0.7 0.8 slice_bitcast_fusion.12
  1.8 0.1 add_compare_fusion
  1.9 0.9 %convert_bitcast_fusion = (f32[1,8,16,128]{3,2,1,0:T(8,128)S(1)}, pred[8,16,128]{2,1,0:T(8,128)(4,1)S(1)}) fusion(s32[8,16,128]{2,1,0:T(8,128)} %param.33), kind=kLoop, calls=%fused_computation.63 | loop fusion | flops 32768 | bytes 147456 | tf_op jit(solution)/shard_map/broadcast_in_dim | solution.py:343
  2.8 0.9 %and_convert_fusion.1.discs_ref = f32[8,8,16,128]{3,2,1,0:T(8,128)} fusion(pred[8,16,128]{2,1,0:T(8,128)(4,1)S(1)} %not.3, pred[8,16,128]{2,1,0:T(8,128)(4,1)S(1)} %slice.630, pred[8,8]{1,0:T(8,128)(4,1)S(1)} %slice.530), kind=kLoop, calls=%fused_computation.4 | loop fusion | flops 393216 | bytes 557120 | tf_op jit(solution)/shard_map/convert_element_type | solution.py:337
  3.8 2.4 %shard_map.95 = (f32[3,8,16,128]{3,2,1,0:T(8,128)}, f32[8,16,128]{2,1,0:T(8,128)}) custom-call(f32[19,8,16,128]{3,2,1,0:T(8,128)} %populations_ref.1, f32[8,8,16,128]{3,2,1,0:T(8,128)} %and_convert_fusion.1.discs_ref), custom_call_target="tpu_custom_call" | custom-call | flops 983040 | bytes 1245184 | tf_op jit(solution)/shard_map/pallas_call | solution.py:144
  6.2 1.0 %reduce_sum.27 = f32[8]{0:T(128)S(1)} reduce(f32[8,16,128]{2,1,0:T(8,128)} %get-tuple-element.130, f32[]{:T(128)} %constant.272.clone.1), dimensions={1,2}, to_apply=%region_0.1 | reduce | flops 16376 | bytes 65572 | tf_op jit(solution)/shard_map/reduce_sum | solution.py:339
  7.1 6.0 %collective-permute-start.3 = (f32[8]{0:T(128)S(1)}, f32[8]{0:T(128)S(1)}, u32[]{:S(2)}, u32[]{:S(2)}) collective-permute-start(f32[8]{0:T(128)S(1)} %reduce_sum.27), channel_id=1, source_target_pairs={{0,28},{2,30},{4,0},{6,2},{8,4},{10,6},{12,8},{14,10},{16,12},{18,... | collective-permute-start | bytes 104 | tf_op jit(solution)/shard_map/ppermute | solution.py:263
  13.3 1.5 %collective-permute-start = (f32[22,1,16,128]{3,2,1,0:T(8,128)S(1)}, f32[22,1,16,128]{3,2,1,0:T(8,128)S(1)}, u32[]{:S(2)}, u32[]{:S(2)}) collective-permute-start(f32[22,1,16,128]{3,2,1,0:T(8,128)S(1)} %get-tuple-element.192), channel_id=1, source_target_pairs={{0,2},{2,4},{4,6},{6,8},{8,10},{10,12},{12,14},{14,16},{16,18},{18... | collective-permute-start | bytes 540680 | tf_op jit(solution)/shard_map/ppermute | solution.py:259
  14.8 4.2 %collective-permute-start.1 = (f32[22,1,16,128]{3,2,1,0:T(8,128)S(1)}, f32[22,1,16,128]{3,2,1,0:T(8,128)S(1)}, u32[]{:S(2)}, u32[]{:S(2)}) collective-permute-start(f32[22,1,16,128]{3,2,1,0:T(8,128)S(1)} %get-tuple-element.193), channel_id=1, source_target_pairs={{2,0},{4,2},{6,4},{8,6},{10,8},{12,10},{14,12},{16,14},{18,16},{20... | collective-permute-start | bytes 540680 | tf_op jit(solution)/shard_map/ppermute | solution.py:260
  19.2 0.1 broadcast_multiply_fusion
  19.3 0.2 fusion.2
  19.5 3.5 %collective-permute-done = f32[22,1,16,128]{3,2,1,0:T(8,128)S(1)} collective-permute-done((f32[22,1,16,128]{3,2,1,0:T(8,128)S(1)}, f32[22,1,16,128]{3,2,1,0:T(8,128)S(1)}, u32[]{:S(2)}, u32[]{:S(2)}) %collective-permute-start) | collective-permute-done | bytes 180256 | tf_op jit(solution)/shard_map/ppermute | solution.py:259
  23.1 0.1 maximum_dynamic-update-slice_fusion.2
  23.6 1.4 %collective-permute-done.4 = f32[44,10,1,128]{3,2,1,0:T(1,128)S(1)} collective-permute-done((f32[44,10,1,128]{3,2,1,0:T(1,128)S(1)}, f32[44,10,1,128]{3,2,1,0:T(1,128)S(1)}, u32[]{:S(2)}, u32[]{:S(2)}) %collective-permute-start.4) | collective-permute-done | bytes 225312 | tf_op jit(solution)/shard_map/ppermute | solution.py:254
  25.0 0.1 fusion.24
  25.2 1.1 %and_convert_fusion.discs_ref = f32[8,10,18,128]{3,2,1,0:T(8,128)} fusion(pred[10,18,128]{2,1,0:T(8,128)(4,1)S(1)} %maximum_compare_fusion, pred[8,18,128]{2,1,0:T(8,128)(4,1)S(1)} %add_compare_fusion, pred[8,10]{1,0:T(8,128)(4,1)S(1)} %fusion.28), kind=kLoop, calls=%fused_computation.3 | loop fusion | flops 552960 | bytes 778832 | tf_op jit(solution)/shard_map/convert_element_type | solution.py:351
  26.3 0.7 maximum_bitcast_fusion.solid_ref
  27.0 1.8 %pad_maximum_fusion.populations_ref = f32[19,10,18,128]{3,2,1,0:T(8,128)} fusion(f32[19,10,1,128]{3,2,1,0:T(1,128)S(1)} %get-tuple-element.153, f32[19,1,16,128]{3,2,1,0:T(8,128)S(1)} %slice.638, f32[19,8,16,128]{3,2,1,0:T(8,128)S(1)} %copy-done, f32[19,1,16,128]{3,2,1,0:T(8,128)S(1)} %slice.637, f32[19,10,1,128]{3,2,1,0:T(1,128)S(1)} %get-tuple-element.152), kind=kLoop, calls=%fused_computation | loop fusion | flops 1751040 | bytes 3502080 | tf_op jit(solution)/shard_map/concatenate | solution.py:268
  28.8 0.5 fusion.57.strength_ref
  29.4 5.2 %shard_map.96 = (f32[19,8,16,128]{3,2,1,0:T(8,128)}, f32[3,8,16,128]{3,2,1,0:T(8,128)}, f32[8,16,128]{2,1,0:T(8,128)}) custom-call(f32[8]{0:T(128)} %fusion.57.strength_ref, f32[19,10,18,128]{3,2,1,0:T(8,128)} %pad_maximum_fusion.populations_ref, f32[8,10,18,128]{3,2,1,0:T(8,128)} %and_convert_fusion.discs_ref, f32[10,18,128]{2,1,0:T(8,128)} %maximum_bitcast_fusion.solid_ref), custom_call_target="tpu_custom_call" | custom-call | flops 6912000 | bytes 5253120 | tf_op jit(solution)/shard_map/pallas_call | solution.py:170
  34.5 1.1 %reduce_sum.28 = f32[8]{0:T(128)S(1)} reduce(f32[8,16,128]{2,1,0:T(8,128)} %get-tuple-element.131, f32[]{:T(128)} %constant.272.clone.1), dimensions={1,2}, to_apply=%region_1.2 | reduce | flops 16376 | bytes 65572 | tf_op jit(solution)/shard_map/reduce_sum | solution.py:376
  35.6 1.0 %fusion.63 = (f32[19,1,16,128]{3,2,1,0:T(8,128)S(1)}, f32[19,1,16,128]{3,2,1,0:T(8,128)S(1)}) fusion(f32[19,8,16,128]{3,2,1,0:T(8,128)} %get-tuple-element.132), kind=kLoop, calls=%fused_computation.156 | loop fusion | bytes 622592 | tf_op jit(solution)/shard_map/slice | solution.py:245
  36.7 1.7 %collective-permute-start.5 = (f32[21,1,16,128]{3,2,1,0:T(8,128)S(1)}, f32[21,1,16,128]{3,2,1,0:T(8,128)S(1)}, u32[]{:S(2)}, u32[]{:S(2)}) collective-permute-start(f32[21,1,16,128]{3,2,1,0:T(8,128)S(1)} %get-tuple-element.184), channel_id=1, source_target_pairs={{0,2},{2,4},{4,6},{6,8},{8,10},{10,12},{12,14},{14,16},{16,18},{18... | collective-permute-start | bytes 516104 | tf_op jit(solution)/shard_map/ppermute | solution.py:259
  38.4 4.0 %collective-permute-start.6 = (f32[21,1,16,128]{3,2,1,0:T(8,128)S(1)}, f32[21,1,16,128]{3,2,1,0:T(8,128)S(1)}, u32[]{:S(2)}, u32[]{:S(2)}) collective-permute-start(f32[21,1,16,128]{3,2,1,0:T(8,128)S(1)} %get-tuple-element.185), channel_id=1, source_target_pairs={{2,0},{4,2},{6,4},{8,6},{10,8},{12,10},{14,12},{16,14},{18,16},{20... | collective-permute-start | bytes 516104 | tf_op jit(solution)/shard_map/ppermute | solution.py:260
  42.4 1.4 %collective-permute-start.8 = (f32[8]{0:T(128)S(1)}, f32[8]{0:T(128)S(1)}, u32[]{:S(2)}, u32[]{:S(2)}) collective-permute-start(f32[8]{0:T(128)S(1)} %reduce_sum.28), channel_id=1, source_target_pairs={{0,28},{2,30},{4,0},{6,2},{8,4},{10,6},{12,8},{14,10},{16,12},{18,... | collective-permute-start | bytes 104 | tf_op jit(solution)/shard_map/ppermute | solution.py:263
  43.7 0.6 collective-permute-start.7
  44.4 2.5 %collective-permute-done.5 = f32[21,1,16,128]{3,2,1,0:T(8,128)S(1)} collective-permute-done((f32[21,1,16,128]{3,2,1,0:T(8,128)S(1)}, f32[21,1,16,128]{3,2,1,0:T(8,128)S(1)}, u32[]{:S(2)}, u32[]{:S(2)}) %collective-permute-start.5) | collective-permute-done | bytes 172064 | tf_op jit(solution)/shard_map/ppermute | solution.py:259
  46.9 0.4 collective-permute-done.6
  47.3 0.1 maximum_dynamic-update-slice_fusion.1
  47.4 2.6 %collective-permute-done.7 = f32[8]{0:T(128)S(1)} collective-permute-done((f32[8]{0:T(128)S(1)}, f32[8]{0:T(128)S(1)}, u32[]{:S(2)}, u32[]{:S(2)}) %collective-permute-start.7) | collective-permute-done | bytes 64 | tf_op jit(solution)/shard_map/ppermute | solution.py:263
  50.3 1.4 %collective-permute-done.9 = f32[42,10,1,128]{3,2,1,0:T(1,128)S(1)} collective-permute-done((f32[42,10,1,128]{3,2,1,0:T(1,128)S(1)}, f32[42,10,1,128]{3,2,1,0:T(1,128)S(1)}, u32[]{:S(2)}, u32[]{:S(2)}) %collective-permute-start.9) | collective-permute-done | bytes 215072 | tf_op jit(solution)/shard_map/ppermute | solution.py:254
  51.7 0.1 fusion.18
  51.8 1.8 %pad_maximum_fusion.1.populations_ref = f32[19,10,18,128]{3,2,1,0:T(8,128)} fusion(f32[19,10,1,128]{3,2,1,0:T(1,128)S(1)} %get-tuple-element.161, f32[19,1,16,128]{3,2,1,0:T(8,128)S(1)} %slice.661, f32[19,8,16,128]{3,2,1,0:T(8,128)S(1)} %copy-done.1, f32[19,1,16,128]{3,2,1,0:T(8,128)S(1)} %slice.660, f32[19,10,1,128]{3,2,1,0:T(1,128)S(1)} %get-tuple-element.160), kind=kLoop, calls=%fused_computation.1 | loop fusion | flops 1751040 | bytes 3502080 | tf_op jit(solution)/shard_map/concatenate | solution.py:268
  53.6 0.5 fusion.58.strength_ref
  54.1 5.2 %shard_map.97 = (f32[19,8,16,128]{3,2,1,0:T(8,128)}, f32[3,8,16,128]{3,2,1,0:T(8,128)}, f32[8,16,128]{2,1,0:T(8,128)}) custom-call(f32[8]{0:T(128)} %fusion.58.strength_ref, f32[19,10,18,128]{3,2,1,0:T(8,128)} %pad_maximum_fusion.1.populations_ref, f32[8,10,18,128]{3,2,1,0:T(8,128)} %and_convert_fusion.discs_ref, f32[10,18,128]{2,1,0:T(8,128)} %maximum_bitcast_fusion.solid_ref), custom_call_target="tpu_custom_call" | custom-call | flops 6912000 | bytes 5253120 | tf_op jit(solution)/shard_map/pallas_call | solution.py:170
  59.3 1.1 %reduce_sum.29 = f32[8]{0:T(128)S(1)} reduce(f32[8,16,128]{2,1,0:T(8,128)} %get-tuple-element.134, f32[]{:T(128)} %constant.272.clone.1), dimensions={1,2}, to_apply=%region_2.3 | reduce | flops 16376 | bytes 65572 | tf_op jit(solution)/shard_map/reduce_sum | solution.py:376
  60.4 1.0 %fusion.62 = (f32[19,1,16,128]{3,2,1,0:T(8,128)S(1)}, f32[19,1,16,128]{3,2,1,0:T(8,128)S(1)}) fusion(f32[19,8,16,128]{3,2,1,0:T(8,128)} %get-tuple-element.135), kind=kLoop, calls=%fused_computation.155 | loop fusion | bytes 622592 | tf_op jit(solution)/shard_map/slice | solution.py:245
  61.5 0.9 %collective-permute-start.10 = (f32[21,1,16,128]{3,2,1,0:T(8,128)S(1)}, f32[21,1,16,128]{3,2,1,0:T(8,128)S(1)}, u32[]{:S(2)}, u32[]{:S(2)}) collective-permute-start(f32[21,1,16,128]{3,2,1,0:T(8,128)S(1)} %get-tuple-element.182), channel_id=1, source_target_pairs={{0,2},{2,4},{4,6},{6,8},{8,10},{10,12},{12,14},{14,16},{16,18},{18... | collective-permute-start | bytes 516104 | tf_op jit(solution)/shard_map/ppermute | solution.py:259
  62.4 4.8 %collective-permute-start.11 = (f32[21,1,16,128]{3,2,1,0:T(8,128)S(1)}, f32[21,1,16,128]{3,2,1,0:T(8,128)S(1)}, u32[]{:S(2)}, u32[]{:S(2)}) collective-permute-start(f32[21,1,16,128]{3,2,1,0:T(8,128)S(1)} %get-tuple-element.183), channel_id=1, source_target_pairs={{2,0},{4,2},{6,4},{8,6},{10,8},{12,10},{14,12},{16,14},{18,16},{20... | collective-permute-start | bytes 516104 | tf_op jit(solution)/shard_map/ppermute | solution.py:260
  67.1 2.0 %collective-permute-start.12 = (f32[8]{0:T(128)S(1)}, f32[8]{0:T(128)S(1)}, u32[]{:S(2)}, u32[]{:S(2)}) collective-permute-start(f32[8]{0:T(128)S(1)} %reduce_sum.29), channel_id=1, source_target_pairs={{0,4},{2,6},{4,8},{6,10},{8,12},{10,14},{12,16},{14,18},{16,20},{1... | collective-permute-start | bytes 104 | tf_op jit(solution)/shard_map/ppermute | solution.py:263
  69.2 2.4 %collective-permute-done.10 = f32[21,1,16,128]{3,2,1,0:T(8,128)S(1)} collective-permute-done((f32[21,1,16,128]{3,2,1,0:T(8,128)S(1)}, f32[21,1,16,128]{3,2,1,0:T(8,128)S(1)}, u32[]{:S(2)}, u32[]{:S(2)}) %collective-permute-start.10) | collective-permute-done | bytes 172064 | tf_op jit(solution)/shard_map/ppermute | solution.py:259
  71.6 0.1 maximum_dynamic-update-slice_fusion
  71.7 1.6 %collective-permute-done.12 = f32[8]{0:T(128)S(1)} collective-permute-done((f32[8]{0:T(128)S(1)}, f32[8]{0:T(128)S(1)}, u32[]{:S(2)}, u32[]{:S(2)}) %collective-permute-start.12) | collective-permute-done | bytes 64 | tf_op jit(solution)/shard_map/ppermute | solution.py:263
  73.6 1.4 %collective-permute-done.14 = f32[42,10,1,128]{3,2,1,0:T(1,128)S(1)} collective-permute-done((f32[42,10,1,128]{3,2,1,0:T(1,128)S(1)}, f32[42,10,1,128]{3,2,1,0:T(1,128)S(1)}, u32[]{:S(2)}, u32[]{:S(2)}) %collective-permute-start.14) | collective-permute-done | bytes 215072 | tf_op jit(solution)/shard_map/ppermute | solution.py:254
  75.1 1.8 %pad_maximum_fusion.2.populations_ref = f32[19,10,18,128]{3,2,1,0:T(8,128)} fusion(f32[19,10,1,128]{3,2,1,0:T(1,128)S(1)} %get-tuple-element.157, f32[19,1,16,128]{3,2,1,0:T(8,128)S(1)} %slice.680, f32[19,8,16,128]{3,2,1,0:T(8,128)S(1)} %copy-done.2, f32[19,1,16,128]{3,2,1,0:T(8,128)S(1)} %slice.679, f32[19,10,1,128]{3,2,1,0:T(1,128)S(1)} %get-tuple-element.156), kind=kLoop, calls=%fused_computation.2 | loop fusion | flops 1751040 | bytes 3502080 | tf_op jit(solution)/shard_map/concatenate | solution.py:268
  76.9 0.5 fusion.59.strength_ref
  77.4 4.9 %shard_map.98 = f32[19,8,16,128]{3,2,1,0:T(8,128)} custom-call(f32[8]{0:T(128)} %fusion.59.strength_ref, f32[19,10,18,128]{3,2,1,0:T(8,128)} %pad_maximum_fusion.2.populations_ref, f32[8,10,18,128]{3,2,1,0:T(8,128)} %and_convert_fusion.discs_ref, f32[10,18,128]{2,1,0:T(8,128)} %maximum_bitcast_fusion.solid_ref), custom_call_target="tpu_custom_call" | custom-call | flops 6912000 | bytes 5253120 | tf_op jit(solution)/shard_map/pallas_call | solution.py:170
  82.3 0.7 fusion.12
  (99 shorter events, 1.9 us)
Async XLA Ops:
  0.6 12.5 %copy-start = (f32[19,8,16,128]{3,2,1,0:T(8,128)S(1)}, f32[19,8,16,128]{3,2,1,0:T(8,128)}, u32[]{:S(2)}) copy-start(f32[19,8,16,128]{3,2,1,0:T(8,128)} %populations_ref.1) | copy-start | bytes 3735556
  0.6 12.6 %copy-start.3 = (f32[8,16,128]{2,1,0:T(8,128)S(1)}, f32[8,16,128]{2,1,0:T(8,128)}, u32[]{:S(2)}) copy-start(f32[8,16,128]{2,1,0:T(8,128)} %param.34) | copy-start | bytes 196612
  0.7 18.4 %copy-start.9 = (s32[16,3]{0,1:T(4,128)S(1)}, s32[16,3]{0,1:T(4,128)}, u32[]{:S(2)}) copy-start(s32[16,3]{0,1:T(4,128)} %param.38) | copy-start | bytes 580
  0.7 18.6 %copy-start.10 = (f32[16]{0:T(128)S(1)}, f32[16]{0:T(128)}, u32[]{:S(2)}) copy-start(f32[16]{0:T(128)} %param.39) | copy-start | bytes 196
  7.1 16.1 %collective-permute-start.3 = (f32[8]{0:T(128)S(1)}, f32[8]{0:T(128)S(1)}, u32[]{:S(2)}, u32[]{:S(2)}) collective-permute-start(f32[8]{0:T(128)S(1)} %reduce_sum.27), channel_id=1, source_target_pairs={{0,28},{2,30},{4,0},{6,2},{8,4},{10,6},{12,8},{14,10},{16,12},{18,... | collective-permute-start | bytes 104 | tf_op jit(solution)/shard_map/ppermute | solution.py:263
  13.2 10.1 %collective-permute-start.2 = (f32[8]{0:T(128)S(1)}, f32[8]{0:T(128)S(1)}, u32[]{:S(2)}, u32[]{:S(2)}) collective-permute-start(f32[8]{0:T(128)S(1)} %reduce_sum.27), channel_id=1, source_target_pairs={{0,4},{2,6},{4,8},{6,10},{8,12},{10,14},{12,16},{14,18},{16,20},{1... | collective-permute-start | bytes 104 | tf_op jit(solution)/shard_map/ppermute | solution.py:263
  13.3 9.8 %collective-permute-start = (f32[22,1,16,128]{3,2,1,0:T(8,128)S(1)}, f32[22,1,16,128]{3,2,1,0:T(8,128)S(1)}, u32[]{:S(2)}, u32[]{:S(2)}) collective-permute-start(f32[22,1,16,128]{3,2,1,0:T(8,128)S(1)} %get-tuple-element.192), channel_id=1, source_target_pairs={{0,2},{2,4},{4,6},{6,8},{8,10},{10,12},{12,14},{14,16},{16,18},{18... | collective-permute-start | bytes 540680 | tf_op jit(solution)/shard_map/ppermute | solution.py:259
  14.8 8.3 %collective-permute-start.1 = (f32[22,1,16,128]{3,2,1,0:T(8,128)S(1)}, f32[22,1,16,128]{3,2,1,0:T(8,128)S(1)}, u32[]{:S(2)}, u32[]{:S(2)}) collective-permute-start(f32[22,1,16,128]{3,2,1,0:T(8,128)S(1)} %get-tuple-element.193), channel_id=1, source_target_pairs={{2,0},{4,2},{6,4},{8,6},{10,8},{12,10},{14,12},{16,14},{18,16},{20... | collective-permute-start | bytes 540680 | tf_op jit(solution)/shard_map/ppermute | solution.py:260
  23.1 1.9 %copy-start.4 = (f32[3,8,16,128]{3,2,1,0:T(8,128)S(1)}, f32[3,8,16,128]{3,2,1,0:T(8,128)}, u32[]{:S(2)}) copy-start(f32[3,8,16,128]{3,2,1,0:T(8,128)} %get-tuple-element.133) | copy-start | bytes 589828
  23.4 1.5 %collective-permute-start.4 = (f32[44,10,1,128]{3,2,1,0:T(1,128)S(1)}, f32[44,10,1,128]{3,2,1,0:T(1,128)S(1)}, u32[]{:S(2)}, u32[]{:S(2)}) collective-permute-start(f32[44,10,1,128]{3,2,1,0:T(1,128)S(1)} %constant_dynamic-update-slice_fusion), channel_id=1, source_target_pairs={{0,1},{1,0},{2,3},{3,2},{4,5},{5,4},{6,7},{7,6},{8,9},{9,8},{10,11... | collective-permute-start | bytes 675848 | tf_op jit(solution)/shard_map/ppermute | solution.py:254
  26.3 2.5 %copy-start.7 = (f32[8]{0:T(128)S(1)}, f32[8]{0:T(128)}, u32[]{:S(2)}) copy-start(f32[8]{0:T(128)} %param.36) | copy-start | bytes 100
  26.3 2.5 %copy-start.8 = (f32[8]{0:T(128)S(1)}, f32[8]{0:T(128)}, u32[]{:S(2)}) copy-start(f32[8]{0:T(128)} %param.37) | copy-start | bytes 100
  34.5 12.7 %copy-start.1 = (f32[19,8,16,128]{3,2,1,0:T(8,128)S(1)}, f32[19,8,16,128]{3,2,1,0:T(8,128)}, u32[]{:S(2)}) copy-start(f32[19,8,16,128]{3,2,1,0:T(8,128)} %get-tuple-element.132) | copy-start | bytes 3735556
  36.7 15.0 %copy-start.6 = (f32[3,8,16,128]{3,2,1,0:T(8,128)S(1)}, f32[3,8,16,128]{3,2,1,0:T(8,128)}, u32[]{:S(2)}) copy-start(f32[3,8,16,128]{3,2,1,0:T(8,128)} %get-tuple-element.136) | copy-start | bytes 589828
  36.7 10.2 %collective-permute-start.5 = (f32[21,1,16,128]{3,2,1,0:T(8,128)S(1)}, f32[21,1,16,128]{3,2,1,0:T(8,128)S(1)}, u32[]{:S(2)}, u32[]{:S(2)}) collective-permute-start(f32[21,1,16,128]{3,2,1,0:T(8,128)S(1)} %get-tuple-element.184), channel_id=1, source_target_pairs={{0,2},{2,4},{4,6},{6,8},{8,10},{10,12},{12,14},{14,16},{16,18},{18... | collective-permute-start | bytes 516104 | tf_op jit(solution)/shard_map/ppermute | solution.py:259
  38.4 8.9 %collective-permute-start.6 = (f32[21,1,16,128]{3,2,1,0:T(8,128)S(1)}, f32[21,1,16,128]{3,2,1,0:T(8,128)S(1)}, u32[]{:S(2)}, u32[]{:S(2)}) collective-permute-start(f32[21,1,16,128]{3,2,1,0:T(8,128)S(1)} %get-tuple-element.185), channel_id=1, source_target_pairs={{2,0},{4,2},{6,4},{8,6},{10,8},{12,10},{14,12},{16,14},{18,16},{20... | collective-permute-start | bytes 516104 | tf_op jit(solution)/shard_map/ppermute | solution.py:260
  42.4 5.1 %collective-permute-start.8 = (f32[8]{0:T(128)S(1)}, f32[8]{0:T(128)S(1)}, u32[]{:S(2)}, u32[]{:S(2)}) collective-permute-start(f32[8]{0:T(128)S(1)} %reduce_sum.28), channel_id=1, source_target_pairs={{0,28},{2,30},{4,0},{6,2},{8,4},{10,6},{12,8},{14,10},{16,12},{18,... | collective-permute-start | bytes 104 | tf_op jit(solution)/shard_map/ppermute | solution.py:263
  43.7 6.2 %collective-permute-start.7 = (f32[8]{0:T(128)S(1)}, f32[8]{0:T(128)S(1)}, u32[]{:S(2)}, u32[]{:S(2)}) collective-permute-start(f32[8]{0:T(128)S(1)} %reduce_sum.28), channel_id=1, source_target_pairs={{0,4},{2,6},{4,8},{6,10},{8,12},{10,14},{12,16},{14,18},{16,20},{1... | collective-permute-start | bytes 104 | tf_op jit(solution)/shard_map/ppermute | solution.py:263
  50.1 1.5 %collective-permute-start.9 = (f32[42,10,1,128]{3,2,1,0:T(1,128)S(1)}, f32[42,10,1,128]{3,2,1,0:T(1,128)S(1)}, u32[]{:S(2)}, u32[]{:S(2)}) collective-permute-start(f32[42,10,1,128]{3,2,1,0:T(1,128)S(1)} %constant_dynamic-update-slice_fusion.6), channel_id=1, source_target_pairs={{0,1},{1,0},{2,3},{3,2},{4,5},{5,4},{6,7},{7,6},{8,9},{9,8},{10,11... | collective-permute-start | bytes 645128 | tf_op jit(solution)/shard_map/ppermute | solution.py:254
  59.3 12.3 %copy-start.2 = (f32[19,8,16,128]{3,2,1,0:T(8,128)S(1)}, f32[19,8,16,128]{3,2,1,0:T(8,128)}, u32[]{:S(2)}) copy-start(f32[19,8,16,128]{3,2,1,0:T(8,128)} %get-tuple-element.135) | copy-start | bytes 3735556
  61.5 10.1 %collective-permute-start.10 = (f32[21,1,16,128]{3,2,1,0:T(8,128)S(1)}, f32[21,1,16,128]{3,2,1,0:T(8,128)S(1)}, u32[]{:S(2)}, u32[]{:S(2)}) collective-permute-start(f32[21,1,16,128]{3,2,1,0:T(8,128)S(1)} %get-tuple-element.182), channel_id=1, source_target_pairs={{0,2},{2,4},{4,6},{6,8},{8,10},{10,12},{12,14},{14,16},{16,18},{18... | collective-permute-start | bytes 516104 | tf_op jit(solution)/shard_map/ppermute | solution.py:259
  62.4 9.2 %collective-permute-start.11 = (f32[21,1,16,128]{3,2,1,0:T(8,128)S(1)}, f32[21,1,16,128]{3,2,1,0:T(8,128)S(1)}, u32[]{:S(2)}, u32[]{:S(2)}) collective-permute-start(f32[21,1,16,128]{3,2,1,0:T(8,128)S(1)} %get-tuple-element.183), channel_id=1, source_target_pairs={{2,0},{4,2},{6,4},{8,6},{10,8},{12,10},{14,12},{16,14},{18,16},{20... | collective-permute-start | bytes 516104 | tf_op jit(solution)/shard_map/ppermute | solution.py:260
  67.1 4.6 %collective-permute-start.13 = (f32[8]{0:T(128)S(1)}, f32[8]{0:T(128)S(1)}, u32[]{:S(2)}, u32[]{:S(2)}) collective-permute-start(f32[8]{0:T(128)S(1)} %reduce_sum.29), channel_id=1, source_target_pairs={{0,28},{2,30},{4,0},{6,2},{8,4},{10,6},{12,8},{14,10},{16,12},{18,... | collective-permute-start | bytes 104 | tf_op jit(solution)/shard_map/ppermute | solution.py:263
  67.1 6.2 %collective-permute-start.12 = (f32[8]{0:T(128)S(1)}, f32[8]{0:T(128)S(1)}, u32[]{:S(2)}, u32[]{:S(2)}) collective-permute-start(f32[8]{0:T(128)S(1)} %reduce_sum.29), channel_id=1, source_target_pairs={{0,4},{2,6},{4,8},{6,10},{8,12},{10,14},{12,16},{14,18},{16,20},{1... | collective-permute-start | bytes 104 | tf_op jit(solution)/shard_map/ppermute | solution.py:263
  73.5 1.5 %collective-permute-start.14 = (f32[42,10,1,128]{3,2,1,0:T(1,128)S(1)}, f32[42,10,1,128]{3,2,1,0:T(1,128)S(1)}, u32[]{:S(2)}, u32[]{:S(2)}) collective-permute-start(f32[42,10,1,128]{3,2,1,0:T(1,128)S(1)} %constant_dynamic-update-slice_fusion.10), channel_id=1, source_target_pairs={{0,1},{1,0},{2,3},{3,2},{4,5},{5,4},{6,7},{7,6},{8,9},{9,8},{10,11... | collective-permute-start | bytes 645128 | tf_op jit(solution)/shard_map/ppermute | solution.py:254
  77.4 4.9 %copy-start.5 = (f32[3,8,16,128]{3,2,1,0:T(8,128)S(1)}, f32[3,8,16,128]{3,2,1,0:T(8,128)}, u32[]{:S(2)}) copy-start(f32[3,8,16,128]{3,2,1,0:T(8,128)} %get-tuple-element.137) | copy-start | bytes 589828

commit v8 on v7

--- a/solution.py
+++ b/solution.py
@@ -75,11 +75,21 @@
     return (density, velocity)
 
 
-def step_kernel(with_moments, strength_ref, populations_ref, discs_ref, solid_ref, *rest):
+def step_kernel(
+    with_moments,
+    strength_ref,
+    populations_ref,
+    discs_ref,
+    solid_ref,
+    smoke_ref,
+    motion_ref,
+    released_ref,
+    *rest,
+):
     if with_moments:
-        out_ref, velocity_ref, flow_ref, posts_ref = rest
+        out_ref, smoke_out_ref, velocity_ref, flow_ref, posts_ref, sums_ref = rest
     else:
-        out_ref, posts_ref = rest
+        out_ref, smoke_out_ref, posts_ref = rest
     fans = discs_ref.shape[0]
     slab_len, band_width, height = out_ref.shape[1:]
 
@@ -104,6 +114,28 @@
         return carry
 
     lax.fori_loop(0, populations_ref.shape[1], collide_plane, 0)
+    lane_plane = lax.broadcasted_iota(jnp.int32, (band_width, height), 1)
+
+    def smoke_plane(index, carry):
+        center = smoke_ref[index + 1, 1 : 1 + band_width, :]
+        ahead_x = smoke_ref[index + 2, 1 : 1 + band_width, :]
+        behind_x = smoke_ref[index, 1 : 1 + band_width, :]
+        ahead_y = smoke_ref[index + 1, 2 : 2 + band_width, :]
+        behind_y = smoke_ref[index + 1, 0:band_width, :]
+        ahead_z = jnp.where(lane_plane == height - 1, 0.0, pltpu.roll(center, height - 1, 1))
+        behind_z = jnp.where(lane_plane == 0, 0.0, pltpu.roll(center, 1, 1))
+        laplace = ahead_x + behind_x + ahead_y + behind_y + ahead_z + behind_z - 6.0 * center
+        advect = 0.5 * (
+            motion_ref[0, index] * (ahead_x - behind_x)
+            + motion_ref[1, index] * (ahead_y - behind_y)
+            + motion_ref[2, index] * (ahead_z - behind_z)
+        )
+        solid_flag = solid_ref[index + 1, 1 : 1 + band_width, :] != 0.0
+        fresh = jnp.where(solid_flag, 0.0, center + DIFFUSIVITY * laplace - advect)
+        smoke_out_ref[index] = fresh + released_ref[index]
+        return carry
+
+    lax.fori_loop(0, slab_len, smoke_plane, 0)
     lane = lax.broadcasted_iota(jnp.int32, (slab_len, band_width, height), 2)
     for which in range(19):
         shift_x, shift_y, shift_z = VELOCITIES[which]
@@ -115,68 +147,75 @@
         elif shift_z == -1:
             piece = jnp.where(lane == height - 1, 0.0, pltpu.roll(piece, height - 1, 2))
         out_ref[which] = piece
-    if not with_moments:
-        return
-    moments_into(out_ref, discs_ref, 1, velocity_ref, flow_ref)
-
-
-def moments_into(populations_ref, discs_ref, rim, velocity_ref, flow_ref):
+    if with_moments:
+        moments_into(out_ref, discs_ref, 1, velocity_ref, flow_ref, sums_ref)
+
+
+def moments_into(populations_ref, discs_ref, rim, velocity_ref, flow_ref, sums_ref):
     fans = discs_ref.shape[0]
     band_width = populations_ref.shape[2]
-    flow_ref[...] = jnp.zeros(flow_ref.shape, jnp.float32)
+    sums_ref[...] = jnp.zeros(sums_ref.shape, jnp.float32)
 
     def moment_plane(index, carry):
         density, velocity = plane_moments([populations_ref[which, index] for which in range(19)])
         for dimension in range(3):
             velocity_ref[dimension, index] = velocity[dimension]
         for fan_number in range(fans):
-            flow_ref[fan_number] += (
+            sums_ref[fan_number] += (
                 discs_ref[fan_number, index + rim, rim : rim + band_width, :] * velocity[0]
             )
         return carry
 
     lax.fori_loop(0, populations_ref.shape[1], moment_plane, 0)
+    for fan_number in range(fans):
+        flow_ref[fan_number : fan_number + 1, :] = jnp.sum(sums_ref[fan_number], axis=0, keepdims=True)
 
 
 def first_moments(populations, discs):
     fans, slab_len, band_width, height = discs.shape
     vmem = pl.BlockSpec(memory_space=pltpu.VMEM)
     return pl.pallas_call(
-        lambda populations_ref, discs_ref, velocity_ref, flow_ref: moments_into(
-            populations_ref, discs_ref, 0, velocity_ref, flow_ref
+        lambda populations_ref, discs_ref, velocity_ref, flow_ref, sums_ref: moments_into(
+            populations_ref, discs_ref, 0, velocity_ref, flow_ref, sums_ref
         ),
         out_shape=(
             jax.ShapeDtypeStruct((3, slab_len, band_width, height), jnp.float32),
-            jax.ShapeDtypeStruct((fans, band_width, height), jnp.float32),
+            jax.ShapeDtypeStruct((fans, height), jnp.float32),
         ),
         in_specs=[vmem, vmem],
         out_specs=(vmem, vmem),
+        scratch_shapes=[pltpu.VMEM((fans, band_width, height), jnp.float32)],
         cost_estimate=pl.CostEstimate(
             flops=60 * discs[0].size, transcendentals=0, bytes_accessed=4 * populations.size
         ),
     )(populations, discs)
 
 
-def lattice_step(strength, extended, discs, solid_rim, with_moments):
+def lattice_step(strength, extended, discs, solid_rim, smoke_rim, velocity, released, with_moments):
     slab_len = extended.shape[1] - 2
     band_width = extended.shape[2] - 2
     height = extended.shape[3]
     fans = discs.shape[0]
-    out_shape = [jax.ShapeDtypeStruct((19, slab_len, band_width, height), jnp.float32)]
+    out_shape = [
+        jax.ShapeDtypeStruct((19, slab_len, band_width, height), jnp.float32),
+        jax.ShapeDtypeStruct((slab_len, band_width, height), jnp.float32),
+    ]
+    scratch = [pltpu.VMEM(extended.shape, jnp.float32)]
     if with_moments:
         out_shape.append(jax.ShapeDtypeStruct((3, slab_len, band_width, height), jnp.float32))
-        out_shape.append(jax.ShapeDtypeStruct((fans, band_width, height), jnp.float32))
+        out_shape.append(jax.ShapeDtypeStruct((fans, height), jnp.float32))
+        scratch.append(pltpu.VMEM((fans, band_width, height), jnp.float32))
     vmem = pl.BlockSpec(memory_space=pltpu.VMEM)
     return pl.pallas_call(
         functools.partial(step_kernel, with_moments),
         out_shape=tuple(out_shape),
-        in_specs=[pl.BlockSpec(memory_space=pltpu.SMEM), vmem, vmem, vmem],
+        in_specs=[pl.BlockSpec(memory_space=pltpu.SMEM)] + [vmem] * 6,
         out_specs=tuple([vmem] * len(out_shape)),
-        scratch_shapes=[pltpu.VMEM(extended.shape, jnp.float32)],
+        scratch_shapes=scratch,
         cost_estimate=pl.CostEstimate(
             flops=300 * solid_rim.size, transcendentals=0, bytes_accessed=12 * extended.size
         ),
-    )(strength, extended, discs, solid_rim)
+    )(strength, extended, discs, solid_rim, smoke_rim, velocity, released)
 
 
 def disc_count():
@@ -336,7 +375,7 @@
         & jnp.logical_not(solid_flag)[None]
     ).astype(jnp.float32)
     velocity, flow = first_moments(populations, inner_discs)
-    partials = jnp.sum(flow, axis=(1, 2))
+    partials = jnp.sum(flow, axis=1)
     for repeat in range(ITERS):
         fields = [populations, smoke_field[None]]
         if repeat == 0:
@@ -353,27 +392,14 @@
             )
         strength = fan_gain * (jet_speed - totals / float(disc_count()))
         last = repeat == ITERS - 1
-        stepped = lattice_step(strength, extended, discs, solid_rim, not last)
-        ahead_x = rimmed[2:, 1:-1]
-        behind_x = rimmed[:-2, 1:-1]
-        ahead_y = rimmed[1:-1, 2:]
-        behind_y = rimmed[1:-1, :-2]
-        smoke_field = advance(
-            smoke_field,
-            ahead_x,
-            behind_x,
-            ahead_y,
-            behind_y,
-            shift_height(smoke_field, -1),
-            shift_height(smoke_field, 1),
-            velocity,
-            solid_flag,
-        )
-        smoke_field = smoke_field + released
+        stepped = lattice_step(
+            strength, extended, discs, solid_rim, rimmed, velocity, released, not last
+        )
         populations = stepped[0]
+        smoke_field = stepped[1]
         if not last:
-            velocity = stepped[1]
-            partials = jnp.sum(stepped[2], axis=(1, 2))
+            velocity = stepped[2]
+            partials = jnp.sum(stepped[3], axis=1)
     return (populations, smoke_field)
 
 

time: 83.4 us -> 87.5 us (1.049)
  Pallas kernels: 17.6 us -> 19.6 us
  local copies, waits for them, and re-layouts: 3.54 us -> 5.35 us
    pallas_call x3, Pallas kernels: 15.2 us -> 17.2 us  [lattice_step(): pl.pallas_call(functools.partial(step_kernel, with_moments), out_shape=tu...]
    squeeze x3, other arithmetic: 0.07 us -> 2.02 us  [body(): rimmed = fields[1][0]]
    slice x6, local copies, waits for them, and re-layouts: 2.06 us -> 3.49 us  [piece(): lax.slice_in_dim(field, start, start + 1, axis=dim)]
    add x3 -> x0, other arithmetic: 0.96 us -> none  [body(): smoke_field = smoke_field + released]
  transfers between devices with their start and end apart: 15 -> 15, of which waited for: 9 -> 9; matrix products, arithmetic and copies ran while one was open for 1% -> 2% of each run, Pallas kernels for 0% -> 0%
where the time goes in v8:
time: 87.5 us; the launch traced here: 87 us
  starting transfers between devices  27.4 us (31%)
  Pallas kernels  19.6 us (22%)
  waiting for transfers between devices  16.7 us (19%)
  other arithmetic  16.6 us (19%)
  local copies, waits for them, and re-layouts  5.35 us (6%)
  between operations  1.07 us (1%)
    pallas_call x3, Pallas kernels, lattice_step(): pl.pallas_call(functools.partial(step_kernel, with_moments), out_shape=tu...  17.2 us
    ppermute x3, starting transfers between devices, rim_round(): from_right = lax.ppermute(head, axis, backward)  13 us
    ppermute x6, starting transfers between devices, rim_round(): lax.ppermute(flow, axis, [(i, (i + offset) % count) for i in range(count)])  10.1 us
    ppermute x3, waiting for transfers between devices, rim_round(): from_left = lax.ppermute(tail, axis, forward)  8.62 us
    concatenate x4, other arithmetic, rim_round(): jnp.concatenate([from_left[first:first + channel], field, from_right[firs...  5.4 us
    ppermute x6, waiting for transfers between devices, rim_round(): lax.ppermute(flow, axis, [(i, (i + offset) % count) for i in range(count)])  4.2 us
    ppermute x3, starting transfers between devices, rim_round(): from_left = lax.ppermute(tail, axis, forward)  4.12 us
    ppermute x3, waiting for transfers between devices, rim_round(): both = lax.ppermute(jnp.concatenate([tail, head], axis=0), axis, forward)  3.51 us
  transfers between devices with their start and end apart: 15, of which 9 were waited for; matrix products, arithmetic and copies ran while one was open for 2% of the time, Pallas kernels for 0%

profile of v8, /device:TPU:0, one launch (start us, length us, event | category | flops | bytes accessed | tf_op | source)
XLA Modules:
  0.0 87.0 jit_solution(13596267630424489445)
XLA Ops:
  0.7 0.8 slice_bitcast_fusion.12
  1.8 0.1 add_compare_fusion
  1.9 0.9 convert_bitcast_fusion
  2.8 0.9 %and_convert_fusion.1.discs_ref = f32[8,8,16,128]{3,2,1,0:T(8,128)} fusion(pred[8,16,128]{2,1,0:T(8,128)(4,1)S(1)} %not.3, pred[8,16,128]{2,1,0:T(8,128)(4,1)S(1)} %slice.522, pred[8,8]{1,0:T(8,128)(4,1)S(1)} %slice.449), kind=kLoop, calls=%fused_computation.4 | loop fusion | flops 393216 | bytes 557120 | tf_op jit(solution)/shard_map/convert_element_type | solution.py:376
  3.8 2.4 %shard_map.95 = (f32[3,8,16,128]{3,2,1,0:T(8,128)}, f32[8,128]{1,0:T(8,128)}) custom-call(f32[19,8,16,128]{3,2,1,0:T(8,128)} %populations_ref.1, f32[8,8,16,128]{3,2,1,0:T(8,128)} %and_convert_fusion.1.discs_ref), custom_call_target="tpu_custom_call" | custom-call | flops 983040 | bytes 1245184 | tf_op jit(solution)/shard_map/pallas_call | solution.py:177
  6.1 0.8 reduce_sum.27
  6.9 6.0 %collective-permute-start.3 = (f32[8]{0:T(128)S(1)}, f32[8]{0:T(128)S(1)}, u32[]{:S(2)}, u32[]{:S(2)}) collective-permute-start(f32[8]{0:T(128)S(1)} %reduce_sum.27), channel_id=1, source_target_pairs={{0,28},{2,30},{4,0},{6,2},{8,4},{10,6},{12,8},{14,10},{16,12},{18,... | collective-permute-start | bytes 104 | tf_op jit(solution)/shard_map/ppermute | solution.py:302
  13.1 1.5 %collective-permute-start = (f32[22,1,16,128]{3,2,1,0:T(8,128)S(1)}, f32[22,1,16,128]{3,2,1,0:T(8,128)S(1)}, u32[]{:S(2)}, u32[]{:S(2)}) collective-permute-start(f32[22,1,16,128]{3,2,1,0:T(8,128)S(1)} %get-tuple-element.190), channel_id=1, source_target_pairs={{0,2},{2,4},{4,6},{6,8},{8,10},{10,12},{12,14},{14,16},{16,18},{18... | collective-permute-start | bytes 540680 | tf_op jit(solution)/shard_map/ppermute | solution.py:298
  14.6 4.2 %collective-permute-start.1 = (f32[22,1,16,128]{3,2,1,0:T(8,128)S(1)}, f32[22,1,16,128]{3,2,1,0:T(8,128)S(1)}, u32[]{:S(2)}, u32[]{:S(2)}) collective-permute-start(f32[22,1,16,128]{3,2,1,0:T(8,128)S(1)} %get-tuple-element.191), channel_id=1, source_target_pairs={{2,0},{4,2},{6,4},{8,6},{10,8},{12,10},{14,12},{16,14},{18,16},{20... | collective-permute-start | bytes 540680 | tf_op jit(solution)/shard_map/ppermute | solution.py:299
  19.0 0.1 broadcast_multiply_fusion
  19.1 3.8 %collective-permute-done = f32[22,1,16,128]{3,2,1,0:T(8,128)S(1)} collective-permute-done((f32[22,1,16,128]{3,2,1,0:T(8,128)S(1)}, f32[22,1,16,128]{3,2,1,0:T(8,128)S(1)}, u32[]{:S(2)}, u32[]{:S(2)}) %collective-permute-start) | collective-permute-done | bytes 180256 | tf_op jit(solution)/shard_map/ppermute | solution.py:298
  23.3 0.2 fusion.2
  23.6 0.6 copy.14.released_ref
  24.2 0.6 collective-permute-done.4
  24.9 1.1 %and_convert_fusion.discs_ref = f32[8,10,18,128]{3,2,1,0:T(8,128)} fusion(pred[10,18,128]{2,1,0:T(8,128)(4,1)S(1)} %maximum_compare_fusion, pred[8,18,128]{2,1,0:T(8,128)(4,1)S(1)} %add_compare_fusion, pred[8,10]{1,0:T(8,128)(4,1)S(1)} %fusion.10), kind=kLoop, calls=%fused_computation.3 | loop fusion | flops 552960 | bytes 778832 | tf_op jit(solution)/shard_map/convert_element_type | solution.py:390
  26.0 0.7 maximum_bitcast_fusion.solid_ref
  26.7 0.7 maximum_bitcast_fusion.1.smoke_ref
  27.4 1.8 %pad_maximum_fusion.populations_ref = f32[19,10,18,128]{3,2,1,0:T(8,128)} fusion(f32[19,10,1,128]{3,2,1,0:T(1,128)S(1)} %get-tuple-element.157, f32[19,1,16,128]{3,2,1,0:T(8,128)S(1)} %slice.530, f32[19,8,16,128]{3,2,1,0:T(8,128)S(1)} %copy-done, f32[19,1,16,128]{3,2,1,0:T(8,128)S(1)} %slice.529, f32[19,10,1,128]{3,2,1,0:T(1,128)S(1)} %get-tuple-element.156), kind=kLoop, calls=%fused_computation | loop fusion | flops 1751040 | bytes 3502080 | tf_op jit(solution)/shard_map/concatenate | solution.py:307
  29.2 0.6 fusion.39.strength_ref
  29.7 5.8 %shard_map.96 = (f32[19,8,16,128]{3,2,1,0:T(8,128)}, f32[8,16,128]{2,1,0:T(8,128)}, f32[3,8,16,128]{3,2,1,0:T(8,128)}, f32[8,128]{1,0:T(8,128)}) custom-call(f32[8]{0:T(128)} %fusion.39.strength_ref, f32[19,10,18,128]{3,2,1,0:T(8,128)} %pad_maximum_fusion.populations_ref, f32[8,10,18,128]{3,2,1,0:T(8,128)} %and_convert_fusion.discs_ref, ...), custom_call_target="tpu_custom_call" | custom-call | flops 6912000 | bytes 5253120 | tf_op jit(solution)/shard_map/pallas_call | solution.py:209
  35.6 0.9 %reduce_sum.28 = f32[8]{0:T(128)S(1)} reduce(f32[8,128]{1,0:T(8,128)} %get-tuple-element.134, f32[]{:T(128)} %constant.268.clone.1), dimensions={1}, to_apply=%region_1.2 | reduce | flops 1016 | bytes 4132 | tf_op jit(solution)/shard_map/reduce_sum | solution.py:402
  36.5 0.7 fusion.56
  37.2 1.0 %fusion.45 = (f32[19,1,16,128]{3,2,1,0:T(8,128)S(1)}, f32[19,1,16,128]{3,2,1,0:T(8,128)S(1)}) fusion(f32[19,8,16,128]{3,2,1,0:T(8,128)} %get-tuple-element.135), kind=kLoop, calls=%fused_computation.129 | loop fusion | bytes 622592 | tf_op jit(solution)/shard_map/slice | solution.py:284
  38.3 1.7 %collective-permute-start.5 = (f32[21,1,16,128]{3,2,1,0:T(8,128)S(1)}, f32[21,1,16,128]{3,2,1,0:T(8,128)S(1)}, u32[]{:S(2)}, u32[]{:S(2)}) collective-permute-start(f32[21,1,16,128]{3,2,1,0:T(8,128)S(1)} %get-tuple-element.182), channel_id=1, source_target_pairs={{0,2},{2,4},{4,6},{6,8},{8,10},{10,12},{12,14},{14,16},{16,18},{18... | collective-permute-start | bytes 516104 | tf_op jit(solution)/shard_map/ppermute | solution.py:298
  39.9 4.0 %collective-permute-start.6 = (f32[21,1,16,128]{3,2,1,0:T(8,128)S(1)}, f32[21,1,16,128]{3,2,1,0:T(8,128)S(1)}, u32[]{:S(2)}, u32[]{:S(2)}) collective-permute-start(f32[21,1,16,128]{3,2,1,0:T(8,128)S(1)} %get-tuple-element.183), channel_id=1, source_target_pairs={{2,0},{4,2},{6,4},{8,6},{10,8},{12,10},{14,12},{16,14},{18,16},{20... | collective-permute-start | bytes 516104 | tf_op jit(solution)/shard_map/ppermute | solution.py:299
  43.9 1.4 %collective-permute-start.8 = (f32[8]{0:T(128)S(1)}, f32[8]{0:T(128)S(1)}, u32[]{:S(2)}, u32[]{:S(2)}) collective-permute-start(f32[8]{0:T(128)S(1)} %reduce_sum.28), channel_id=1, source_target_pairs={{0,28},{2,30},{4,0},{6,2},{8,4},{10,6},{12,8},{14,10},{16,12},{18,... | collective-permute-start | bytes 104 | tf_op jit(solution)/shard_map/ppermute | solution.py:302
  45.3 0.6 collective-permute-start.7
  46.0 2.5 %collective-permute-done.5 = f32[21,1,16,128]{3,2,1,0:T(8,128)S(1)} collective-permute-done((f32[21,1,16,128]{3,2,1,0:T(8,128)S(1)}, f32[21,1,16,128]{3,2,1,0:T(8,128)S(1)}, u32[]{:S(2)}, u32[]{:S(2)}) %collective-permute-start.5) | collective-permute-done | bytes 172064 | tf_op jit(solution)/shard_map/ppermute | solution.py:298
  48.5 0.4 collective-permute-done.6
  49.0 2.6 %collective-permute-done.7 = f32[8]{0:T(128)S(1)} collective-permute-done((f32[8]{0:T(128)S(1)}, f32[8]{0:T(128)S(1)}, u32[]{:S(2)}, u32[]{:S(2)}) %collective-permute-start.7) | collective-permute-done | bytes 64 | tf_op jit(solution)/shard_map/ppermute | solution.py:302
  51.8 1.5 %collective-permute-done.9 = f32[42,10,1,128]{3,2,1,0:T(1,128)S(1)} collective-permute-done((f32[42,10,1,128]{3,2,1,0:T(1,128)S(1)}, f32[42,10,1,128]{3,2,1,0:T(1,128)S(1)}, u32[]{:S(2)}, u32[]{:S(2)}) %collective-permute-start.9) | collective-permute-done | bytes 215072 | tf_op jit(solution)/shard_map/ppermute | solution.py:293
  53.2 0.7 maximum_bitcast_fusion.2.smoke_ref
  53.9 1.8 %pad_maximum_fusion.1.populations_ref = f32[19,10,18,128]{3,2,1,0:T(8,128)} fusion(f32[19,10,1,128]{3,2,1,0:T(1,128)S(1)} %get-tuple-element.165, f32[19,1,16,128]{3,2,1,0:T(8,128)S(1)} %slice.549, f32[19,8,16,128]{3,2,1,0:T(8,128)S(1)} %copy-done.2, f32[19,1,16,128]{3,2,1,0:T(8,128)S(1)} %slice.548, f32[19,10,1,128]{3,2,1,0:T(1,128)S(1)} %get-tuple-element.164), kind=kLoop, calls=%fused_computation.1 | loop fusion | flops 1751040 | bytes 3502080 | tf_op jit(solution)/shard_map/concatenate | solution.py:307
  55.7 0.6 fusion.40.strength_ref
  56.3 5.9 %shard_map.97 = (f32[19,8,16,128]{3,2,1,0:T(8,128)}, f32[8,16,128]{2,1,0:T(8,128)}, f32[3,8,16,128]{3,2,1,0:T(8,128)}, f32[8,128]{1,0:T(8,128)}) custom-call(f32[8]{0:T(128)} %fusion.40.strength_ref, f32[19,10,18,128]{3,2,1,0:T(8,128)} %pad_maximum_fusion.1.populations_ref, f32[8,10,18,128]{3,2,1,0:T(8,128)} %and_convert_fusion.discs_ref, ...), custom_call_target="tpu_custom_call" | custom-call | flops 6912000 | bytes 5253120 | tf_op jit(solution)/shard_map/pallas_call | solution.py:209
  62.2 0.9 %reduce_sum.29 = f32[8]{0:T(128)S(1)} reduce(f32[8,128]{1,0:T(8,128)} %get-tuple-element.138, f32[]{:T(128)} %constant.268.clone.1), dimensions={1}, to_apply=%region_2.3 | reduce | flops 1016 | bytes 4132 | tf_op jit(solution)/shard_map/reduce_sum | solution.py:402
  63.1 0.7 fusion.55
  63.8 1.0 %fusion.44 = (f32[19,1,16,128]{3,2,1,0:T(8,128)S(1)}, f32[19,1,16,128]{3,2,1,0:T(8,128)S(1)}) fusion(f32[19,8,16,128]{3,2,1,0:T(8,128)} %get-tuple-element.139), kind=kLoop, calls=%fused_computation.128 | loop fusion | bytes 622592 | tf_op jit(solution)/shard_map/slice | solution.py:284
  64.9 0.9 %collective-permute-start.10 = (f32[21,1,16,128]{3,2,1,0:T(8,128)S(1)}, f32[21,1,16,128]{3,2,1,0:T(8,128)S(1)}, u32[]{:S(2)}, u32[]{:S(2)}) collective-permute-start(f32[21,1,16,128]{3,2,1,0:T(8,128)S(1)} %get-tuple-element.180), channel_id=1, source_target_pairs={{0,2},{2,4},{4,6},{6,8},{8,10},{10,12},{12,14},{14,16},{16,18},{18... | collective-permute-start | bytes 516104 | tf_op jit(solution)/shard_map/ppermute | solution.py:298
  65.8 4.8 %collective-permute-start.11 = (f32[21,1,16,128]{3,2,1,0:T(8,128)S(1)}, f32[21,1,16,128]{3,2,1,0:T(8,128)S(1)}, u32[]{:S(2)}, u32[]{:S(2)}) collective-permute-start(f32[21,1,16,128]{3,2,1,0:T(8,128)S(1)} %get-tuple-element.181), channel_id=1, source_target_pairs={{2,0},{4,2},{6,4},{8,6},{10,8},{12,10},{14,12},{16,14},{18,16},{20... | collective-permute-start | bytes 516104 | tf_op jit(solution)/shard_map/ppermute | solution.py:299
  70.5 2.0 %collective-permute-start.12 = (f32[8]{0:T(128)S(1)}, f32[8]{0:T(128)S(1)}, u32[]{:S(2)}, u32[]{:S(2)}) collective-permute-start(f32[8]{0:T(128)S(1)} %reduce_sum.29), channel_id=1, source_target_pairs={{0,4},{2,6},{4,8},{6,10},{8,12},{10,14},{12,16},{14,18},{16,20},{1... | collective-permute-start | bytes 104 | tf_op jit(solution)/shard_map/ppermute | solution.py:302
  72.6 2.4 %collective-permute-done.10 = f32[21,1,16,128]{3,2,1,0:T(8,128)S(1)} collective-permute-done((f32[21,1,16,128]{3,2,1,0:T(8,128)S(1)}, f32[21,1,16,128]{3,2,1,0:T(8,128)S(1)}, u32[]{:S(2)}, u32[]{:S(2)}) %collective-permute-start.10) | collective-permute-done | bytes 172064 | tf_op jit(solution)/shard_map/ppermute | solution.py:298
  75.1 1.6 %collective-permute-done.12 = f32[8]{0:T(128)S(1)} collective-permute-done((f32[8]{0:T(128)S(1)}, f32[8]{0:T(128)S(1)}, u32[]{:S(2)}, u32[]{:S(2)}) %collective-permute-start.12) | collective-permute-done | bytes 64 | tf_op jit(solution)/shard_map/ppermute | solution.py:302
  77.0 1.5 %collective-permute-done.14 = f32[42,10,1,128]{3,2,1,0:T(1,128)S(1)} collective-permute-done((f32[42,10,1,128]{3,2,1,0:T(1,128)S(1)}, f32[42,10,1,128]{3,2,1,0:T(1,128)S(1)}, u32[]{:S(2)}, u32[]{:S(2)}) %collective-permute-start.14) | collective-permute-done | bytes 215072 | tf_op jit(solution)/shard_map/ppermute | solution.py:293
  78.4 0.7 maximum_bitcast_fusion.3.smoke_ref
  79.1 1.8 %pad_maximum_fusion.2.populations_ref = f32[19,10,18,128]{3,2,1,0:T(8,128)} fusion(f32[19,10,1,128]{3,2,1,0:T(1,128)S(1)} %get-tuple-element.161, f32[19,1,16,128]{3,2,1,0:T(8,128)S(1)} %slice.562, f32[19,8,16,128]{3,2,1,0:T(8,128)S(1)} %copy-done.1, f32[19,1,16,128]{3,2,1,0:T(8,128)S(1)} %slice.561, f32[19,10,1,128]{3,2,1,0:T(1,128)S(1)} %get-tuple-element.160), kind=kLoop, calls=%fused_computation.2 | loop fusion | flops 1751040 | bytes 3502080 | tf_op jit(solution)/shard_map/concatenate | solution.py:307
  80.9 0.5 fusion.41.strength_ref
  81.5 5.5 %shard_map.98 = (f32[19,8,16,128]{3,2,1,0:T(8,128)}, f32[8,16,128]{2,1,0:T(8,128)}) custom-call(f32[8]{0:T(128)} %fusion.41.strength_ref, f32[19,10,18,128]{3,2,1,0:T(8,128)} %pad_maximum_fusion.2.populations_ref, f32[8,10,18,128]{3,2,1,0:T(8,128)} %and_convert_fusion.discs_ref, f32[10,18,128]{2,1,0:T(8,128)} %maximum_bitcast_fusion.solid_ref, ...), custom_call_target="tpu_custom_call" | custom-call | flops 6912000 | bytes 5253120 | tf_op jit(solution)/shard_map/pallas_call | solution.py:209
  (92 shorter events, 1.8 us)
Async XLA Ops:
  0.6 12.4 %copy-start = (f32[19,8,16,128]{3,2,1,0:T(8,128)S(1)}, f32[19,8,16,128]{3,2,1,0:T(8,128)}, u32[]{:S(2)}) copy-start(f32[19,8,16,128]{3,2,1,0:T(8,128)} %populations_ref.1) | copy-start | bytes 3735556
  0.6 12.4 %copy-start.5 = (f32[8,16,128]{2,1,0:T(8,128)S(1)}, f32[8,16,128]{2,1,0:T(8,128)}, u32[]{:S(2)}) copy-start(f32[8,16,128]{2,1,0:T(8,128)} %param.34) | copy-start | bytes 196612
  0.7 18.2 %copy-start.8 = (s32[16,3]{0,1:T(4,128)S(1)}, s32[16,3]{0,1:T(4,128)}, u32[]{:S(2)}) copy-start(s32[16,3]{0,1:T(4,128)} %param.38) | copy-start | bytes 580
  6.9 16.2 %collective-permute-start.3 = (f32[8]{0:T(128)S(1)}, f32[8]{0:T(128)S(1)}, u32[]{:S(2)}, u32[]{:S(2)}) collective-permute-start(f32[8]{0:T(128)S(1)} %reduce_sum.27), channel_id=1, source_target_pairs={{0,28},{2,30},{4,0},{6,2},{8,4},{10,6},{12,8},{14,10},{16,12},{18,... | collective-permute-start | bytes 104 | tf_op jit(solution)/shard_map/ppermute | solution.py:302
  13.0 10.1 %collective-permute-start.2 = (f32[8]{0:T(128)S(1)}, f32[8]{0:T(128)S(1)}, u32[]{:S(2)}, u32[]{:S(2)}) collective-permute-start(f32[8]{0:T(128)S(1)} %reduce_sum.27), channel_id=1, source_target_pairs={{0,4},{2,6},{4,8},{6,10},{8,12},{10,14},{12,16},{14,18},{16,20},{1... | collective-permute-start | bytes 104 | tf_op jit(solution)/shard_map/ppermute | solution.py:302
  13.1 10.3 %copy-start.9 = (f32[16]{0:T(128)S(1)}, f32[16]{0:T(128)}, u32[]{:S(2)}) copy-start(f32[16]{0:T(128)} %param.39) | copy-start | bytes 196
  13.1 9.8 %collective-permute-start = (f32[22,1,16,128]{3,2,1,0:T(8,128)S(1)}, f32[22,1,16,128]{3,2,1,0:T(8,128)S(1)}, u32[]{:S(2)}, u32[]{:S(2)}) collective-permute-start(f32[22,1,16,128]{3,2,1,0:T(8,128)S(1)} %get-tuple-element.190), channel_id=1, source_target_pairs={{0,2},{2,4},{4,6},{6,8},{8,10},{10,12},{12,14},{14,16},{16,18},{18... | collective-permute-start | bytes 540680 | tf_op jit(solution)/shard_map/ppermute | solution.py:298
  14.6 8.3 %collective-permute-start.1 = (f32[22,1,16,128]{3,2,1,0:T(8,128)S(1)}, f32[22,1,16,128]{3,2,1,0:T(8,128)S(1)}, u32[]{:S(2)}, u32[]{:S(2)}) collective-permute-start(f32[22,1,16,128]{3,2,1,0:T(8,128)S(1)} %get-tuple-element.191), channel_id=1, source_target_pairs={{2,0},{4,2},{6,4},{8,6},{10,8},{12,10},{14,12},{16,14},{18,16},{20... | collective-permute-start | bytes 540680 | tf_op jit(solution)/shard_map/ppermute | solution.py:299
  23.3 1.5 %collective-permute-start.4 = (f32[44,10,1,128]{3,2,1,0:T(1,128)S(1)}, f32[44,10,1,128]{3,2,1,0:T(1,128)S(1)}, u32[]{:S(2)}, u32[]{:S(2)}) collective-permute-start(f32[44,10,1,128]{3,2,1,0:T(1,128)S(1)} %constant_dynamic-update-slice_fusion), channel_id=1, source_target_pairs={{0,1},{1,0},{2,3},{3,2},{4,5},{5,4},{6,7},{7,6},{8,9},{9,8},{10,11... | collective-permute-start | bytes 675848 | tf_op jit(solution)/shard_map/ppermute | solution.py:293
  26.7 2.5 %copy-start.6 = (f32[8]{0:T(128)S(1)}, f32[8]{0:T(128)}, u32[]{:S(2)}) copy-start(f32[8]{0:T(128)} %param.36) | copy-start | bytes 100
  26.7 2.5 %copy-start.7 = (f32[8]{0:T(128)S(1)}, f32[8]{0:T(128)}, u32[]{:S(2)}) copy-start(f32[8]{0:T(128)} %param.37) | copy-start | bytes 100
  35.6 13.3 %copy-start.2 = (f32[19,8,16,128]{3,2,1,0:T(8,128)S(1)}, f32[19,8,16,128]{3,2,1,0:T(8,128)}, u32[]{:S(2)}) copy-start(f32[19,8,16,128]{3,2,1,0:T(8,128)} %get-tuple-element.135) | copy-start | bytes 3735556
  35.6 13.4 %copy-start.4 = (f32[8,16,128]{2,1,0:T(8,128)S(1)}, f32[8,16,128]{2,1,0:T(8,128)}, u32[]{:S(2)}) copy-start(f32[8,16,128]{2,1,0:T(8,128)} %get-tuple-element.136) | copy-start | bytes 196612
  38.3 10.2 %collective-permute-start.5 = (f32[21,1,16,128]{3,2,1,0:T(8,128)S(1)}, f32[21,1,16,128]{3,2,1,0:T(8,128)S(1)}, u32[]{:S(2)}, u32[]{:S(2)}) collective-permute-start(f32[21,1,16,128]{3,2,1,0:T(8,128)S(1)} %get-tuple-element.182), channel_id=1, source_target_pairs={{0,2},{2,4},{4,6},{6,8},{8,10},{10,12},{12,14},{14,16},{16,18},{18... | collective-permute-start | bytes 516104 | tf_op jit(solution)/shard_map/ppermute | solution.py:298
  39.9 8.9 %collective-permute-start.6 = (f32[21,1,16,128]{3,2,1,0:T(8,128)S(1)}, f32[21,1,16,128]{3,2,1,0:T(8,128)S(1)}, u32[]{:S(2)}, u32[]{:S(2)}) collective-permute-start(f32[21,1,16,128]{3,2,1,0:T(8,128)S(1)} %get-tuple-element.183), channel_id=1, source_target_pairs={{2,0},{4,2},{6,4},{8,6},{10,8},{12,10},{14,12},{16,14},{18,16},{20... | collective-permute-start | bytes 516104 | tf_op jit(solution)/shard_map/ppermute | solution.py:299
  43.9 5.1 %collective-permute-start.8 = (f32[8]{0:T(128)S(1)}, f32[8]{0:T(128)S(1)}, u32[]{:S(2)}, u32[]{:S(2)}) collective-permute-start(f32[8]{0:T(128)S(1)} %reduce_sum.28), channel_id=1, source_target_pairs={{0,28},{2,30},{4,0},{6,2},{8,4},{10,6},{12,8},{14,10},{16,12},{18,... | collective-permute-start | bytes 104 | tf_op jit(solution)/shard_map/ppermute | solution.py:302
  45.3 6.2 %collective-permute-start.7 = (f32[8]{0:T(128)S(1)}, f32[8]{0:T(128)S(1)}, u32[]{:S(2)}, u32[]{:S(2)}) collective-permute-start(f32[8]{0:T(128)S(1)} %reduce_sum.28), channel_id=1, source_target_pairs={{0,4},{2,6},{4,8},{6,10},{8,12},{10,14},{12,16},{14,18},{16,20},{1... | collective-permute-start | bytes 104 | tf_op jit(solution)/shard_map/ppermute | solution.py:302
  51.7 1.5 %collective-permute-start.9 = (f32[42,10,1,128]{3,2,1,0:T(1,128)S(1)}, f32[42,10,1,128]{3,2,1,0:T(1,128)S(1)}, u32[]{:S(2)}, u32[]{:S(2)}) collective-permute-start(f32[42,10,1,128]{3,2,1,0:T(1,128)S(1)} %constant_dynamic-update-slice_fusion.6), channel_id=1, source_target_pairs={{0,1},{1,0},{2,3},{3,2},{4,5},{5,4},{6,7},{7,6},{8,9},{9,8},{10,11... | collective-permute-start | bytes 645128 | tf_op jit(solution)/shard_map/ppermute | solution.py:293
  62.2 12.8 %copy-start.1 = (f32[19,8,16,128]{3,2,1,0:T(8,128)S(1)}, f32[19,8,16,128]{3,2,1,0:T(8,128)}, u32[]{:S(2)}) copy-start(f32[19,8,16,128]{3,2,1,0:T(8,128)} %get-tuple-element.139) | copy-start | bytes 3735556
  62.2 12.9 %copy-start.3 = (f32[8,16,128]{2,1,0:T(8,128)S(1)}, f32[8,16,128]{2,1,0:T(8,128)}, u32[]{:S(2)}) copy-start(f32[8,16,128]{2,1,0:T(8,128)} %get-tuple-element.140) | copy-start | bytes 196612
  64.9 10.1 %collective-permute-start.10 = (f32[21,1,16,128]{3,2,1,0:T(8,128)S(1)}, f32[21,1,16,128]{3,2,1,0:T(8,128)S(1)}, u32[]{:S(2)}, u32[]{:S(2)}) collective-permute-start(f32[21,1,16,128]{3,2,1,0:T(8,128)S(1)} %get-tuple-element.180), channel_id=1, source_target_pairs={{0,2},{2,4},{4,6},{6,8},{8,10},{10,12},{12,14},{14,16},{16,18},{18... | collective-permute-start | bytes 516104 | tf_op jit(solution)/shard_map/ppermute | solution.py:298
  65.8 9.2 %collective-permute-start.11 = (f32[21,1,16,128]{3,2,1,0:T(8,128)S(1)}, f32[21,1,16,128]{3,2,1,0:T(8,128)S(1)}, u32[]{:S(2)}, u32[]{:S(2)}) collective-permute-start(f32[21,1,16,128]{3,2,1,0:T(8,128)S(1)} %get-tuple-element.181), channel_id=1, source_target_pairs={{2,0},{4,2},{6,4},{8,6},{10,8},{12,10},{14,12},{16,14},{18,16},{20... | collective-permute-start | bytes 516104 | tf_op jit(solution)/shard_map/ppermute | solution.py:299
  70.5 4.6 %collective-permute-start.13 = (f32[8]{0:T(128)S(1)}, f32[8]{0:T(128)S(1)}, u32[]{:S(2)}, u32[]{:S(2)}) collective-permute-start(f32[8]{0:T(128)S(1)} %reduce_sum.29), channel_id=1, source_target_pairs={{0,28},{2,30},{4,0},{6,2},{8,4},{10,6},{12,8},{14,10},{16,12},{18,... | collective-permute-start | bytes 104 | tf_op jit(solution)/shard_map/ppermute | solution.py:302
  70.5 6.2 %collective-permute-start.12 = (f32[8]{0:T(128)S(1)}, f32[8]{0:T(128)S(1)}, u32[]{:S(2)}, u32[]{:S(2)}) collective-permute-start(f32[8]{0:T(128)S(1)} %reduce_sum.29), channel_id=1, source_target_pairs={{0,4},{2,6},{4,8},{6,10},{8,12},{10,14},{12,16},{14,18},{16,20},{1... | collective-permute-start | bytes 104 | tf_op jit(solution)/shard_map/ppermute | solution.py:302
  76.9 1.5 %collective-permute-start.14 = (f32[42,10,1,128]{3,2,1,0:T(1,128)S(1)}, f32[42,10,1,128]{3,2,1,0:T(1,128)S(1)}, u32[]{:S(2)}, u32[]{:S(2)}) collective-permute-start(f32[42,10,1,128]{3,2,1,0:T(1,128)S(1)} %constant_dynamic-update-slice_fusion.10), channel_id=1, source_target_pairs={{0,1},{1,0},{2,3},{3,2},{4,5},{5,4},{6,7},{7,6},{8,9},{9,8},{10,11... | collective-permute-start | bytes 645128 | tf_op jit(solution)/shard_map/ppermute | solution.py:293

commit v9 on v7

--- a/solution.py
+++ b/solution.py
@@ -77,7 +77,7 @@
 
 def step_kernel(with_moments, strength_ref, populations_ref, discs_ref, solid_ref, *rest):
     if with_moments:
-        out_ref, velocity_ref, flow_ref, posts_ref = rest
+        out_ref, velocity_ref, flow_ref, posts_ref, sums_ref = rest
     else:
         out_ref, posts_ref = rest
     fans = discs_ref.shape[0]
@@ -117,40 +117,43 @@
         out_ref[which] = piece
     if not with_moments:
         return
-    moments_into(out_ref, discs_ref, 1, velocity_ref, flow_ref)
-
-
-def moments_into(populations_ref, discs_ref, rim, velocity_ref, flow_ref):
+    moments_into(out_ref, discs_ref, 1, velocity_ref, flow_ref, sums_ref)
+
+
+def moments_into(populations_ref, discs_ref, rim, velocity_ref, flow_ref, sums_ref):
     fans = discs_ref.shape[0]
     band_width = populations_ref.shape[2]
-    flow_ref[...] = jnp.zeros(flow_ref.shape, jnp.float32)
+    sums_ref[...] = jnp.zeros(sums_ref.shape, jnp.float32)
 
     def moment_plane(index, carry):
         density, velocity = plane_moments([populations_ref[which, index] for which in range(19)])
         for dimension in range(3):
             velocity_ref[dimension, index] = velocity[dimension]
         for fan_number in range(fans):
-            flow_ref[fan_number] += (
+            sums_ref[fan_number] += (
                 discs_ref[fan_number, index + rim, rim : rim + band_width, :] * velocity[0]
             )
         return carry
 
     lax.fori_loop(0, populations_ref.shape[1], moment_plane, 0)
+    for fan_number in range(fans):
+        flow_ref[fan_number : fan_number + 1, :] = jnp.sum(sums_ref[fan_number], axis=0, keepdims=True)
 
 
 def first_moments(populations, discs):
     fans, slab_len, band_width, height = discs.shape
     vmem = pl.BlockSpec(memory_space=pltpu.VMEM)
     return pl.pallas_call(
-        lambda populations_ref, discs_ref, velocity_ref, flow_ref: moments_into(
-            populations_ref, discs_ref, 0, velocity_ref, flow_ref
+        lambda populations_ref, discs_ref, velocity_ref, flow_ref, sums_ref: moments_into(
+            populations_ref, discs_ref, 0, velocity_ref, flow_ref, sums_ref
         ),
         out_shape=(
             jax.ShapeDtypeStruct((3, slab_len, band_width, height), jnp.float32),
-            jax.ShapeDtypeStruct((fans, band_width, height), jnp.float32),
+            jax.ShapeDtypeStruct((fans, height), jnp.float32),
         ),
         in_specs=[vmem, vmem],
         out_specs=(vmem, vmem),
+        scratch_shapes=[pltpu.VMEM((fans, band_width, height), jnp.float32)],
         cost_estimate=pl.CostEstimate(
             flops=60 * discs[0].size, transcendentals=0, bytes_accessed=4 * populations.size
         ),
@@ -165,14 +168,17 @@
     out_shape = [jax.ShapeDtypeStruct((19, slab_len, band_width, height), jnp.float32)]
     if with_moments:
         out_shape.append(jax.ShapeDtypeStruct((3, slab_len, band_width, height), jnp.float32))
-        out_shape.append(jax.ShapeDtypeStruct((fans, band_width, height), jnp.float32))
+        out_shape.append(jax.ShapeDtypeStruct((fans, height), jnp.float32))
+    scratch = [pltpu.VMEM(extended.shape, jnp.float32)]
+    if with_moments:
+        scratch.append(pltpu.VMEM((fans, band_width, height), jnp.float32))
     vmem = pl.BlockSpec(memory_space=pltpu.VMEM)
     return pl.pallas_call(
         functools.partial(step_kernel, with_moments),
         out_shape=tuple(out_shape),
         in_specs=[pl.BlockSpec(memory_space=pltpu.SMEM), vmem, vmem, vmem],
         out_specs=tuple([vmem] * len(out_shape)),
-        scratch_shapes=[pltpu.VMEM(extended.shape, jnp.float32)],
+        scratch_shapes=scratch,
         cost_estimate=pl.CostEstimate(
             flops=300 * solid_rim.size, transcendentals=0, bytes_accessed=12 * extended.size
         ),
@@ -243,8 +249,16 @@
 
     def piece(start):
         cells = [lax.slice_in_dim(field, start, start + 1, axis=dim) for field in fields]
-        carrier = jnp.zeros(cells[0].shape[1:], jnp.float32).at[0, 0, :fans].set(flow)[None]
+        carrier = jnp.zeros(cells[0].shape[1:], jnp.float32)
+        carrier = lax.dynamic_update_slice_in_dim(
+            carrier, jnp.expand_dims(flow, dim - 1), 0, axis=2 - dim
+        )[None]
         return jnp.concatenate(cells + [carrier], axis=0)
+
+    def pick(received):
+        return jnp.squeeze(
+            lax.slice_in_dim(received[-1], 0, fans, axis=2 - dim), axis=dim - 1
+        )
 
     head = piece(0)
     tail = piece(fields[0].shape[dim] - 1)
@@ -254,11 +268,11 @@
         both = lax.ppermute(jnp.concatenate([tail, head], axis=0), axis, forward)
         from_left = both[: tail.shape[0]]
         from_right = both[tail.shape[0] :]
-        total = flow + from_left[-1, 0, 0, :fans]
+        total = flow + pick(from_left)
     else:
         from_left = lax.ppermute(tail, axis, forward)
         from_right = lax.ppermute(head, axis, backward)
-        total = flow + from_left[-1, 0, 0, :fans] + from_right[-1, 0, 0, :fans]
+        total = flow + pick(from_left) + pick(from_right)
     for offset in sorted(set(step % count for step in range(-reach, reach + 1)) - {0, 1, count - 1}):
         total = total + lax.ppermute(flow, axis, [(i, (i + offset) % count) for i in range(count)])
     extended = []
@@ -336,7 +350,7 @@
         & jnp.logical_not(solid_flag)[None]
     ).astype(jnp.float32)
     velocity, flow = first_moments(populations, inner_discs)
-    partials = jnp.sum(flow, axis=(1, 2))
+    partials = flow
     for repeat in range(ITERS):
         fields = [populations, smoke_field[None]]
         if repeat == 0:
@@ -351,7 +365,7 @@
             discs = (along_in[:, :, None, None] & across_in[:, None] & air_rim[None]).astype(
                 jnp.float32
             )
-        strength = fan_gain * (jet_speed - totals / float(disc_count()))
+        strength = fan_gain * (jet_speed - jnp.sum(totals, axis=1) / float(disc_count()))
         last = repeat == ITERS - 1
         stepped = lattice_step(strength, extended, discs, solid_rim, not last)
         ahead_x = rimmed[2:, 1:-1]
@@ -373,7 +387,7 @@
         populations = stepped[0]
         if not last:
             velocity = stepped[1]
-            partials = jnp.sum(stepped[2], axis=(1, 2))
+            partials = stepped[2]
     return (populations, smoke_field)
 
 

time: 83.4 us -> 87.8 us (1.053)
  starting transfers between devices: 27.4 us -> 33.3 us
  waiting for transfers between devices: 17.1 us -> 14.2 us
  local copies, waits for them, and re-layouts: 3.54 us -> 5.84 us
    ppermute x6, starting transfers between devices: 10.1 us -> 16.8 us  [rim_round(): lax.ppermute(flow, axis, [(i, (i + offset) % count) for i in range(count)])]
    ppermute x3, waiting for transfers between devices: 0.38 us -> 6.46 us  [rim_round(): from_right = lax.ppermute(head, axis, backward)]
    ppermute x3, waiting for transfers between devices: 8.39 us -> 3.54 us  [rim_round(): from_left = lax.ppermute(tail, axis, forward)]
    ppermute x6, waiting for transfers between devices: 4.22 us -> 0.02 us  [rim_round(): lax.ppermute(flow, axis, [(i, (i + offset) % count) for i in range(count)])]
    reduce_sum x3, other arithmetic: 3.14 us -> 0.35 us  [body(): jnp.sum(totals, axis=1) / float(disc_count())]
    broadcast_in_dim x2 -> x6, local copies, waits for them, and re-layouts: 0.01 us -> 2.31 us  [piece(): lax.dynamic_update_slice_in_dim(carrier, jnp.expand_dims(flow, dim - 1),...]
    add x3, other arithmetic: 0.02 us -> 2.09 us  [rim_round(): total + lax.ppermute(flow, axis, [(i, (i + offset) % count) for i in rang...]
  transfers between devices with their start and end apart: 15 -> 15, of which waited for: 9 -> 6; matrix products, arithmetic and copies ran while one was open for 1% -> 2% of each run, Pallas kernels for 0% -> 0%
where the time goes in v9:
time: 87.8 us; the launch traced here: 87.4 us
  starting transfers between devices  33.3 us (38%)
  Pallas kernels  17.5 us (20%)
  other arithmetic  15.3 us (17%)
  waiting for transfers between devices  14.2 us (16%)
  local copies, waits for them, and re-layouts  5.84 us (7%)
  between operations  1.08 us (1%)
    ppermute x6, starting transfers between devices, rim_round(): lax.ppermute(flow, axis, [(i, (i + offset) % count) for i in range(count)])  16.8 us
    pallas_call x3, Pallas kernels, lattice_step(): pl.pallas_call(functools.partial(step_kernel, with_moments), out_shape=tu...  15.2 us
    ppermute x3, starting transfers between devices, rim_round(): from_right = lax.ppermute(head, axis, backward)  12.9 us
    ppermute x3, waiting for transfers between devices, rim_round(): from_right = lax.ppermute(head, axis, backward)  6.46 us
    concatenate x4, other arithmetic, rim_round(): jnp.concatenate([from_left[first:first + channel], field, from_right[firs...  5.42 us
    ppermute x3, waiting for transfers between devices, rim_round(): both = lax.ppermute(jnp.concatenate([tail, head], axis=0), axis, forward)  4.14 us
    ppermute x3, waiting for transfers between devices, rim_round(): from_left = lax.ppermute(tail, axis, forward)  3.54 us
    ppermute x3, starting transfers between devices, rim_round(): from_left = lax.ppermute(tail, axis, forward)  3.29 us
  transfers between devices with their start and end apart: 15, of which 6 were waited for; matrix products, arithmetic and copies ran while one was open for 2% of the time, Pallas kernels for 0%

profile of v9, /device:TPU:0, one launch (start us, length us, event | category | flops | bytes accessed | tf_op | source)
XLA Modules:
  0.0 87.4 jit_solution(18086523826350577336)
XLA Ops:
  0.7 0.8 slice_bitcast_fusion.15
  1.8 0.1 add_compare_fusion
  1.9 0.9 convert_bitcast_fusion
  2.8 0.9 %and_convert_fusion.1.discs_ref = f32[8,8,16,128]{3,2,1,0:T(8,128)} fusion(pred[8,16,128]{2,1,0:T(8,128)(4,1)S(1)} %not.3, pred[8,16,128]{2,1,0:T(8,128)(4,1)S(1)} %slice.459, pred[8,8]{1,0:T(8,128)(4,1)S(1)} %slice.353), kind=kLoop, calls=%fused_computation.4 | loop fusion | flops 393216 | bytes 557120 | tf_op jit(solution)/shard_map/convert_element_type | solution.py:351
  3.8 2.4 %shard_map.95 = (f32[3,8,16,128]{3,2,1,0:T(8,128)}, f32[8,128]{1,0:T(8,128)}) custom-call(f32[19,8,16,128]{3,2,1,0:T(8,128)} %populations_ref.1, f32[8,8,16,128]{3,2,1,0:T(8,128)} %and_convert_fusion.1.discs_ref), custom_call_target="tpu_custom_call" | custom-call | flops 983040 | bytes 1245184 | tf_op jit(solution)/shard_map/pallas_call | solution.py:146
  6.1 6.0 %collective-permute-start.3 = (f32[8,128]{1,0:T(8,128)}, f32[8,128]{1,0:T(8,128)S(1)}, u32[]{:S(2)}, u32[]{:S(2)}) collective-permute-start(f32[8,128]{1,0:T(8,128)} %get-tuple-element.10), channel_id=1, source_target_pairs={{0,28},{2,30},{4,0},{6,2},{8,4},{10,6},{12,8},{14,10},{16,12},{18,... | collective-permute-start | bytes 12296 | tf_op jit(solution)/shard_map/ppermute | solution.py:277
  12.2 0.7 pad_bitcast_fusion.5
  12.9 1.5 %collective-permute-start = (f32[22,1,16,128]{3,2,1,0:T(8,128)S(1)}, f32[22,1,16,128]{3,2,1,0:T(8,128)S(1)}, u32[]{:S(2)}, u32[]{:S(2)}) collective-permute-start(f32[22,1,16,128]{3,2,1,0:T(8,128)S(1)} %get-tuple-element.76), channel_id=1, source_target_pairs={{0,2},{2,4},{4,6},{6,8},{8,10},{10,12},{12,14},{14,16},{16,18},{18... | collective-permute-start | bytes 540680 | tf_op jit(solution)/shard_map/ppermute | solution.py:273
  14.5 4.2 %collective-permute-start.1 = (f32[22,1,16,128]{3,2,1,0:T(8,128)S(1)}, f32[22,1,16,128]{3,2,1,0:T(8,128)S(1)}, u32[]{:S(2)}, u32[]{:S(2)}) collective-permute-start(f32[22,1,16,128]{3,2,1,0:T(8,128)S(1)} %get-tuple-element.77), channel_id=1, source_target_pairs={{2,0},{4,2},{6,4},{8,6},{10,8},{12,10},{14,12},{16,14},{18,16},{20... | collective-permute-start | bytes 540680 | tf_op jit(solution)/shard_map/ppermute | solution.py:274
  18.8 0.1 broadcast_multiply_fusion
  18.9 0.2 fusion
  19.2 3.5 %collective-permute-done = f32[22,1,16,128]{3,2,1,0:T(8,128)S(1)} collective-permute-done((f32[22,1,16,128]{3,2,1,0:T(8,128)S(1)}, f32[22,1,16,128]{3,2,1,0:T(8,128)S(1)}, u32[]{:S(2)}, u32[]{:S(2)}) %collective-permute-start) | collective-permute-done | bytes 180256 | tf_op jit(solution)/shard_map/ppermute | solution.py:273
  22.7 0.7 fusion.38
  23.9 1.4 %collective-permute-done.4 = f32[44,10,1,128]{3,2,1,0:T(1,128)S(1)} collective-permute-done((f32[44,10,1,128]{3,2,1,0:T(1,128)S(1)}, f32[44,10,1,128]{3,2,1,0:T(1,128)S(1)}, u32[]{:S(2)}, u32[]{:S(2)}) %collective-permute-start.4) | collective-permute-done | bytes 225312 | tf_op jit(solution)/shard_map/ppermute | solution.py:268
  25.3 0.1 add_reduce_fusion.2
  25.5 0.1 fusion.22
  25.7 1.1 %and_convert_fusion.discs_ref = f32[8,10,18,128]{3,2,1,0:T(8,128)} fusion(pred[10,18,128]{2,1,0:T(8,128)(4,1)S(1)} %maximum_compare_fusion, pred[8,18,128]{2,1,0:T(8,128)(4,1)S(1)} %add_compare_fusion, pred[8,10]{1,0:T(8,128)(4,1)S(1)} %fusion.26), kind=kLoop, calls=%fused_computation.3 | loop fusion | flops 552960 | bytes 778832 | tf_op jit(solution)/shard_map/convert_element_type | solution.py:365
  26.8 0.7 maximum_bitcast_fusion.solid_ref
  27.5 1.8 %pad_maximum_fusion.populations_ref = f32[19,10,18,128]{3,2,1,0:T(8,128)} fusion(f32[19,10,1,128]{3,2,1,0:T(1,128)S(1)} %get-tuple-element.33, f32[19,1,16,128]{3,2,1,0:T(8,128)S(1)} %slice.469, f32[19,8,16,128]{3,2,1,0:T(8,128)S(1)} %copy-done, f32[19,1,16,128]{3,2,1,0:T(8,128)S(1)} %slice.468, f32[19,10,1,128]{3,2,1,0:T(1,128)S(1)} %get-tuple-element.32), kind=kLoop, calls=%fused_computation | loop fusion | flops 1751040 | bytes 3502080 | tf_op jit(solution)/shard_map/concatenate | solution.py:282
  29.3 0.5 subtract_multiply_fusion.4.strength_ref
  29.8 5.1 %shard_map.96 = (f32[19,8,16,128]{3,2,1,0:T(8,128)}, f32[3,8,16,128]{3,2,1,0:T(8,128)}, f32[8,128]{1,0:T(8,128)}) custom-call(f32[8]{0:T(128)} %subtract_multiply_fusion.4.strength_ref, f32[19,10,18,128]{3,2,1,0:T(8,128)} %pad_maximum_fusion.populations_ref, f32[8,10,18,128]{3,2,1,0:T(8,128)} %and_convert_fusion.discs_ref, ...), custom_call_target="tpu_custom_call" | custom-call | flops 6912000 | bytes 5253120 | tf_op jit(solution)/shard_map/pallas_call | solution.py:176
  35.0 0.8 pad_bitcast_fusion.3
  35.7 1.0 %fusion.49 = (f32[19,1,16,128]{3,2,1,0:T(8,128)S(1)}, f32[19,1,16,128]{3,2,1,0:T(8,128)S(1)}) fusion(f32[19,8,16,128]{3,2,1,0:T(8,128)} %get-tuple-element.12), kind=kLoop, calls=%fused_computation.155 | loop fusion | bytes 622592 | tf_op jit(solution)/shard_map/slice | solution.py:251
  36.8 1.7 %collective-permute-start.5 = (f32[21,1,16,128]{3,2,1,0:T(8,128)S(1)}, f32[21,1,16,128]{3,2,1,0:T(8,128)S(1)}, u32[]{:S(2)}, u32[]{:S(2)}) collective-permute-start(f32[21,1,16,128]{3,2,1,0:T(8,128)S(1)} %get-tuple-element.74), channel_id=1, source_target_pairs={{0,2},{2,4},{4,6},{6,8},{8,10},{10,12},{12,14},{14,16},{16,18},{18... | collective-permute-start | bytes 516104 | tf_op jit(solution)/shard_map/ppermute | solution.py:273
  38.5 4.2 %collective-permute-start.8 = (f32[8,128]{1,0:T(8,128)}, f32[8,128]{1,0:T(8,128)S(1)}, u32[]{:S(2)}, u32[]{:S(2)}) collective-permute-start(f32[8,128]{1,0:T(8,128)} %get-tuple-element.11), channel_id=1, source_target_pairs={{0,28},{2,30},{4,0},{6,2},{8,4},{10,6},{12,8},{14,10},{16,12},{18,... | collective-permute-start | bytes 12296 | tf_op jit(solution)/shard_map/ppermute | solution.py:277
  42.7 4.5 %collective-permute-start.6 = (f32[21,1,16,128]{3,2,1,0:T(8,128)S(1)}, f32[21,1,16,128]{3,2,1,0:T(8,128)S(1)}, u32[]{:S(2)}, u32[]{:S(2)}) collective-permute-start(f32[21,1,16,128]{3,2,1,0:T(8,128)S(1)} %get-tuple-element.75), channel_id=1, source_target_pairs={{2,0},{4,2},{6,4},{8,6},{10,8},{12,10},{14,12},{16,14},{18,16},{20... | collective-permute-start | bytes 516104 | tf_op jit(solution)/shard_map/ppermute | solution.py:274
  47.2 3.1 %collective-permute-done.6 = f32[21,1,16,128]{3,2,1,0:T(8,128)S(1)} collective-permute-done((f32[21,1,16,128]{3,2,1,0:T(8,128)S(1)}, f32[21,1,16,128]{3,2,1,0:T(8,128)S(1)}, u32[]{:S(2)}, u32[]{:S(2)}) %collective-permute-start.6) | collective-permute-done | bytes 172064 | tf_op jit(solution)/shard_map/ppermute | solution.py:274
  50.3 0.7 fusion.34
  51.1 0.1 maximum_dynamic-update-slice_fusion.1
  51.4 1.4 %collective-permute-done.9 = f32[42,10,1,128]{3,2,1,0:T(1,128)S(1)} collective-permute-done((f32[42,10,1,128]{3,2,1,0:T(1,128)S(1)}, f32[42,10,1,128]{3,2,1,0:T(1,128)S(1)}, u32[]{:S(2)}, u32[]{:S(2)}) %collective-permute-start.9) | collective-permute-done | bytes 215072 | tf_op jit(solution)/shard_map/ppermute | solution.py:268
  52.8 0.1 add_reduce_fusion.1
  52.9 0.5 subtract_multiply_fusion.3.strength_ref
  53.5 0.1 fusion.16
  53.7 1.8 %pad_maximum_fusion.1.populations_ref = f32[19,10,18,128]{3,2,1,0:T(8,128)} fusion(f32[19,10,1,128]{3,2,1,0:T(1,128)S(1)} %get-tuple-element.41, f32[19,1,16,128]{3,2,1,0:T(8,128)S(1)} %slice.494, f32[19,8,16,128]{3,2,1,0:T(8,128)S(1)} %copy-done.1, f32[19,1,16,128]{3,2,1,0:T(8,128)S(1)} %slice.493, f32[19,10,1,128]{3,2,1,0:T(1,128)S(1)} %get-tuple-element.40), kind=kLoop, calls=%fused_computation.1 | loop fusion | flops 1751040 | bytes 3502080 | tf_op jit(solution)/shard_map/concatenate | solution.py:282
  55.5 5.1 %shard_map.97 = (f32[19,8,16,128]{3,2,1,0:T(8,128)}, f32[3,8,16,128]{3,2,1,0:T(8,128)}, f32[8,128]{1,0:T(8,128)}) custom-call(f32[8]{0:T(128)} %subtract_multiply_fusion.3.strength_ref, f32[19,10,18,128]{3,2,1,0:T(8,128)} %pad_maximum_fusion.1.populations_ref, f32[8,10,18,128]{3,2,1,0:T(8,128)} %and_convert_fusion.discs_ref, ...), custom_call_target="tpu_custom_call" | custom-call | flops 6912000 | bytes 5253120 | tf_op jit(solution)/shard_map/pallas_call | solution.py:176
  60.6 0.8 pad_bitcast_fusion.1
  61.4 1.0 %fusion.48 = (f32[19,1,16,128]{3,2,1,0:T(8,128)S(1)}, f32[19,1,16,128]{3,2,1,0:T(8,128)S(1)}) fusion(f32[19,8,16,128]{3,2,1,0:T(8,128)} %get-tuple-element.15), kind=kLoop, calls=%fused_computation.154 | loop fusion | bytes 622592 | tf_op jit(solution)/shard_map/slice | solution.py:251
  62.5 6.6 %collective-permute-start.13 = (f32[8,128]{1,0:T(8,128)}, f32[8,128]{1,0:T(8,128)S(1)}, u32[]{:S(2)}, u32[]{:S(2)}) collective-permute-start(f32[8,128]{1,0:T(8,128)} %get-tuple-element.14), channel_id=1, source_target_pairs={{0,28},{2,30},{4,0},{6,2},{8,4},{10,6},{12,8},{14,10},{16,12},{18,... | collective-permute-start | bytes 12296 | tf_op jit(solution)/shard_map/ppermute | solution.py:277
  69.2 4.2 %collective-permute-start.11 = (f32[21,1,16,128]{3,2,1,0:T(8,128)S(1)}, f32[21,1,16,128]{3,2,1,0:T(8,128)S(1)}, u32[]{:S(2)}, u32[]{:S(2)}) collective-permute-start(f32[21,1,16,128]{3,2,1,0:T(8,128)S(1)} %get-tuple-element.73), channel_id=1, source_target_pairs={{2,0},{4,2},{6,4},{8,6},{10,8},{12,10},{14,12},{16,14},{18,16},{20... | collective-permute-start | bytes 516104 | tf_op jit(solution)/shard_map/ppermute | solution.py:274
  73.4 3.4 %collective-permute-done.11 = f32[21,1,16,128]{3,2,1,0:T(8,128)S(1)} collective-permute-done((f32[21,1,16,128]{3,2,1,0:T(8,128)S(1)}, f32[21,1,16,128]{3,2,1,0:T(8,128)S(1)}, u32[]{:S(2)}, u32[]{:S(2)}) %collective-permute-start.11) | collective-permute-done | bytes 172064 | tf_op jit(solution)/shard_map/ppermute | solution.py:274
  76.8 0.7 fusion.30
  77.5 0.1 maximum_dynamic-update-slice_fusion
  77.9 1.4 %collective-permute-done.14 = f32[42,10,1,128]{3,2,1,0:T(1,128)S(1)} collective-permute-done((f32[42,10,1,128]{3,2,1,0:T(1,128)S(1)}, f32[42,10,1,128]{3,2,1,0:T(1,128)S(1)}, u32[]{:S(2)}, u32[]{:S(2)}) %collective-permute-start.14) | collective-permute-done | bytes 215072 | tf_op jit(solution)/shard_map/ppermute | solution.py:268
  79.3 0.1 add_reduce_fusion
  79.4 0.5 subtract_multiply_fusion.2.strength_ref
  80.0 1.8 %pad_maximum_fusion.2.populations_ref = f32[19,10,18,128]{3,2,1,0:T(8,128)} fusion(f32[19,10,1,128]{3,2,1,0:T(1,128)S(1)} %get-tuple-element.37, f32[19,1,16,128]{3,2,1,0:T(8,128)S(1)} %slice.515, f32[19,8,16,128]{3,2,1,0:T(8,128)S(1)} %copy-done.2, f32[19,1,16,128]{3,2,1,0:T(8,128)S(1)} %slice.514, f32[19,10,1,128]{3,2,1,0:T(1,128)S(1)} %get-tuple-element.36), kind=kLoop, calls=%fused_computation.2 | loop fusion | flops 1751040 | bytes 3502080 | tf_op jit(solution)/shard_map/concatenate | solution.py:282
  81.8 4.9 %shard_map.98 = f32[19,8,16,128]{3,2,1,0:T(8,128)} custom-call(f32[8]{0:T(128)} %subtract_multiply_fusion.2.strength_ref, f32[19,10,18,128]{3,2,1,0:T(8,128)} %pad_maximum_fusion.2.populations_ref, f32[8,10,18,128]{3,2,1,0:T(8,128)} %and_convert_fusion.discs_ref, f32[10,18,128]{2,1,0:T(8,128)} %maximum_bitcast_fusion.solid_ref), custom_call_target="tpu_custom_call" | custom-call | flops 6912000 | bytes 5253120 | tf_op jit(solution)/shard_map/pallas_call | solution.py:176
  86.7 0.7 fusion.10
  (106 shorter events, 2.0 us)
Async XLA Ops:
  0.6 11.5 %copy-start = (f32[19,8,16,128]{3,2,1,0:T(8,128)S(1)}, f32[19,8,16,128]{3,2,1,0:T(8,128)}, u32[]{:S(2)}) copy-start(f32[19,8,16,128]{3,2,1,0:T(8,128)} %populations_ref.1) | copy-start | bytes 3735556
  0.6 12.3 %copy-start.3 = (f32[8,16,128]{2,1,0:T(8,128)S(1)}, f32[8,16,128]{2,1,0:T(8,128)}, u32[]{:S(2)}) copy-start(f32[8,16,128]{2,1,0:T(8,128)} %param.10) | copy-start | bytes 196612
  0.7 18.0 %copy-start.9 = (s32[16,3]{0,1:T(4,128)S(1)}, s32[16,3]{0,1:T(4,128)}, u32[]{:S(2)}) copy-start(s32[16,3]{0,1:T(4,128)} %param.14) | copy-start | bytes 580
  0.7 18.3 %copy-start.10 = (f32[16]{0:T(128)S(1)}, f32[16]{0:T(128)}, u32[]{:S(2)}) copy-start(f32[16]{0:T(128)} %param.15) | copy-start | bytes 196
  6.1 16.6 %collective-permute-start.3 = (f32[8,128]{1,0:T(8,128)}, f32[8,128]{1,0:T(8,128)S(1)}, u32[]{:S(2)}, u32[]{:S(2)}) collective-permute-start(f32[8,128]{1,0:T(8,128)} %get-tuple-element.10), channel_id=1, source_target_pairs={{0,28},{2,30},{4,0},{6,2},{8,4},{10,6},{12,8},{14,10},{16,12},{18,... | collective-permute-start | bytes 12296 | tf_op jit(solution)/shard_map/ppermute | solution.py:277
  12.1 10.6 %collective-permute-start.2 = (f32[8,128]{1,0:T(8,128)}, f32[8,128]{1,0:T(8,128)S(1)}, u32[]{:S(2)}, u32[]{:S(2)}) collective-permute-start(f32[8,128]{1,0:T(8,128)} %get-tuple-element.10), channel_id=1, source_target_pairs={{0,4},{2,6},{4,8},{6,10},{8,12},{10,14},{12,16},{14,18},{16,20},{1... | collective-permute-start | bytes 12296 | tf_op jit(solution)/shard_map/ppermute | solution.py:277
  12.9 9.8 %collective-permute-start = (f32[22,1,16,128]{3,2,1,0:T(8,128)S(1)}, f32[22,1,16,128]{3,2,1,0:T(8,128)S(1)}, u32[]{:S(2)}, u32[]{:S(2)}) collective-permute-start(f32[22,1,16,128]{3,2,1,0:T(8,128)S(1)} %get-tuple-element.76), channel_id=1, source_target_pairs={{0,2},{2,4},{4,6},{6,8},{8,10},{10,12},{12,14},{14,16},{16,18},{18... | collective-permute-start | bytes 540680 | tf_op jit(solution)/shard_map/ppermute | solution.py:273
  14.5 8.2 %collective-permute-start.1 = (f32[22,1,16,128]{3,2,1,0:T(8,128)S(1)}, f32[22,1,16,128]{3,2,1,0:T(8,128)S(1)}, u32[]{:S(2)}, u32[]{:S(2)}) collective-permute-start(f32[22,1,16,128]{3,2,1,0:T(8,128)S(1)} %get-tuple-element.77), channel_id=1, source_target_pairs={{2,0},{4,2},{6,4},{8,6},{10,8},{12,10},{14,12},{16,14},{18,16},{20... | collective-permute-start | bytes 540680 | tf_op jit(solution)/shard_map/ppermute | solution.py:274
  23.5 2.0 %copy-start.4 = (f32[3,8,16,128]{3,2,1,0:T(8,128)S(1)}, f32[3,8,16,128]{3,2,1,0:T(8,128)}, u32[]{:S(2)}) copy-start(f32[3,8,16,128]{3,2,1,0:T(8,128)} %get-tuple-element.13) | copy-start | bytes 589828
  23.8 1.5 %collective-permute-start.4 = (f32[44,10,1,128]{3,2,1,0:T(1,128)S(1)}, f32[44,10,1,128]{3,2,1,0:T(1,128)S(1)}, u32[]{:S(2)}, u32[]{:S(2)}) collective-permute-start(f32[44,10,1,128]{3,2,1,0:T(1,128)S(1)} %constant_dynamic-update-slice_fusion), channel_id=1, source_target_pairs={{0,1},{1,0},{2,3},{3,2},{4,5},{5,4},{6,7},{7,6},{8,9},{9,8},{10,11... | collective-permute-start | bytes 675848 | tf_op jit(solution)/shard_map/ppermute | solution.py:268
  26.8 2.5 %copy-start.7 = (f32[8]{0:T(128)S(1)}, f32[8]{0:T(128)}, u32[]{:S(2)}) copy-start(f32[8]{0:T(128)} %param.12) | copy-start | bytes 100
  26.8 2.5 %copy-start.8 = (f32[8]{0:T(128)S(1)}, f32[8]{0:T(128)}, u32[]{:S(2)}) copy-start(f32[8]{0:T(128)} %param.13) | copy-start | bytes 100
  35.0 16.1 %copy-start.1 = (f32[19,8,16,128]{3,2,1,0:T(8,128)S(1)}, f32[19,8,16,128]{3,2,1,0:T(8,128)}, u32[]{:S(2)}) copy-start(f32[19,8,16,128]{3,2,1,0:T(8,128)} %get-tuple-element.12) | copy-start | bytes 3735556
  36.8 10.4 %collective-permute-start.5 = (f32[21,1,16,128]{3,2,1,0:T(8,128)S(1)}, f32[21,1,16,128]{3,2,1,0:T(8,128)S(1)}, u32[]{:S(2)}, u32[]{:S(2)}) collective-permute-start(f32[21,1,16,128]{3,2,1,0:T(8,128)S(1)} %get-tuple-element.74), channel_id=1, source_target_pairs={{0,2},{2,4},{4,6},{6,8},{8,10},{10,12},{12,14},{14,16},{16,18},{18... | collective-permute-start | bytes 516104 | tf_op jit(solution)/shard_map/ppermute | solution.py:273
  38.5 11.8 %collective-permute-start.8 = (f32[8,128]{1,0:T(8,128)}, f32[8,128]{1,0:T(8,128)S(1)}, u32[]{:S(2)}, u32[]{:S(2)}) collective-permute-start(f32[8,128]{1,0:T(8,128)} %get-tuple-element.11), channel_id=1, source_target_pairs={{0,28},{2,30},{4,0},{6,2},{8,4},{10,6},{12,8},{14,10},{16,12},{18,... | collective-permute-start | bytes 12296 | tf_op jit(solution)/shard_map/ppermute | solution.py:277
  42.7 7.6 %collective-permute-start.7 = (f32[8,128]{1,0:T(8,128)}, f32[8,128]{1,0:T(8,128)S(1)}, u32[]{:S(2)}, u32[]{:S(2)}) collective-permute-start(f32[8,128]{1,0:T(8,128)} %get-tuple-element.11), channel_id=1, source_target_pairs={{0,4},{2,6},{4,8},{6,10},{8,12},{10,14},{12,16},{14,18},{16,20},{1... | collective-permute-start | bytes 12296 | tf_op jit(solution)/shard_map/ppermute | solution.py:277
  42.7 7.6 %collective-permute-start.6 = (f32[21,1,16,128]{3,2,1,0:T(8,128)S(1)}, f32[21,1,16,128]{3,2,1,0:T(8,128)S(1)}, u32[]{:S(2)}, u32[]{:S(2)}) collective-permute-start(f32[21,1,16,128]{3,2,1,0:T(8,128)S(1)} %get-tuple-element.75), channel_id=1, source_target_pairs={{2,0},{4,2},{6,4},{8,6},{10,8},{12,10},{14,12},{16,14},{18,16},{20... | collective-permute-start | bytes 516104 | tf_op jit(solution)/shard_map/ppermute | solution.py:274
  51.0 2.5 %copy-start.6 = (f32[3,8,16,128]{3,2,1,0:T(8,128)S(1)}, f32[3,8,16,128]{3,2,1,0:T(8,128)}, u32[]{:S(2)}) copy-start(f32[3,8,16,128]{3,2,1,0:T(8,128)} %get-tuple-element.16) | copy-start | bytes 589828
  51.3 1.5 %collective-permute-start.9 = (f32[42,10,1,128]{3,2,1,0:T(1,128)S(1)}, f32[42,10,1,128]{3,2,1,0:T(1,128)S(1)}, u32[]{:S(2)}, u32[]{:S(2)}) collective-permute-start(f32[42,10,1,128]{3,2,1,0:T(1,128)S(1)} %constant_dynamic-update-slice_fusion.6), channel_id=1, source_target_pairs={{0,1},{1,0},{2,3},{3,2},{4,5},{5,4},{6,7},{7,6},{8,9},{9,8},{10,11... | collective-permute-start | bytes 645128 | tf_op jit(solution)/shard_map/ppermute | solution.py:268
  60.6 16.9 %copy-start.2 = (f32[19,8,16,128]{3,2,1,0:T(8,128)S(1)}, f32[19,8,16,128]{3,2,1,0:T(8,128)}, u32[]{:S(2)}) copy-start(f32[19,8,16,128]{3,2,1,0:T(8,128)} %get-tuple-element.15) | copy-start | bytes 3735556
  62.5 10.9 %collective-permute-start.10 = (f32[21,1,16,128]{3,2,1,0:T(8,128)S(1)}, f32[21,1,16,128]{3,2,1,0:T(8,128)S(1)}, u32[]{:S(2)}, u32[]{:S(2)}) collective-permute-start(f32[21,1,16,128]{3,2,1,0:T(8,128)S(1)} %get-tuple-element.72), channel_id=1, source_target_pairs={{0,2},{2,4},{4,6},{6,8},{8,10},{10,12},{12,14},{14,16},{16,18},{18... | collective-permute-start | bytes 516104 | tf_op jit(solution)/shard_map/ppermute | solution.py:273
  62.5 14.2 %collective-permute-start.13 = (f32[8,128]{1,0:T(8,128)}, f32[8,128]{1,0:T(8,128)S(1)}, u32[]{:S(2)}, u32[]{:S(2)}) collective-permute-start(f32[8,128]{1,0:T(8,128)} %get-tuple-element.14), channel_id=1, source_target_pairs={{0,28},{2,30},{4,0},{6,2},{8,4},{10,6},{12,8},{14,10},{16,12},{18,... | collective-permute-start | bytes 12296 | tf_op jit(solution)/shard_map/ppermute | solution.py:277
  69.2 7.6 %collective-permute-start.12 = (f32[8,128]{1,0:T(8,128)}, f32[8,128]{1,0:T(8,128)S(1)}, u32[]{:S(2)}, u32[]{:S(2)}) collective-permute-start(f32[8,128]{1,0:T(8,128)} %get-tuple-element.14), channel_id=1, source_target_pairs={{0,4},{2,6},{4,8},{6,10},{8,12},{10,14},{12,16},{14,18},{16,20},{1... | collective-permute-start | bytes 12296 | tf_op jit(solution)/shard_map/ppermute | solution.py:277
  69.2 7.6 %collective-permute-start.11 = (f32[21,1,16,128]{3,2,1,0:T(8,128)S(1)}, f32[21,1,16,128]{3,2,1,0:T(8,128)S(1)}, u32[]{:S(2)}, u32[]{:S(2)}) collective-permute-start(f32[21,1,16,128]{3,2,1,0:T(8,128)S(1)} %get-tuple-element.73), channel_id=1, source_target_pairs={{2,0},{4,2},{6,4},{8,6},{10,8},{12,10},{14,12},{16,14},{18,16},{20... | collective-permute-start | bytes 516104 | tf_op jit(solution)/shard_map/ppermute | solution.py:274
  77.7 1.5 %collective-permute-start.14 = (f32[42,10,1,128]{3,2,1,0:T(1,128)S(1)}, f32[42,10,1,128]{3,2,1,0:T(1,128)S(1)}, u32[]{:S(2)}, u32[]{:S(2)}) collective-permute-start(f32[42,10,1,128]{3,2,1,0:T(1,128)S(1)} %constant_dynamic-update-slice_fusion.10), channel_id=1, source_target_pairs={{0,1},{1,0},{2,3},{3,2},{4,5},{5,4},{6,7},{7,6},{8,9},{9,8},{10,11... | collective-permute-start | bytes 645128 | tf_op jit(solution)/shard_map/ppermute | solution.py:268
  81.8 4.9 %copy-start.5 = (f32[3,8,16,128]{3,2,1,0:T(8,128)S(1)}, f32[3,8,16,128]{3,2,1,0:T(8,128)}, u32[]{:S(2)}) copy-start(f32[3,8,16,128]{3,2,1,0:T(8,128)} %get-tuple-element.17) | copy-start | bytes 589828

commit v10 on v7

--- a/solution.py
+++ b/solution.py
@@ -105,11 +105,17 @@
 
     lax.fori_loop(0, populations_ref.shape[1], collide_plane, 0)
     lane = lax.broadcasted_iota(jnp.int32, (slab_len, band_width, height), 2)
+    row = lax.broadcasted_iota(jnp.int32, (slab_len, band_width, height), 1)
     for which in range(19):
         shift_x, shift_y, shift_z = VELOCITIES[which]
-        piece = posts_ref[
-            which, 1 - shift_x : 1 - shift_x + slab_len, 1 - shift_y : 1 - shift_y + band_width, :
-        ]
+        planes = slice(1 - shift_x, 1 - shift_x + slab_len)
+        piece = posts_ref[which, planes, 0:band_width, :]
+        if shift_y == 1:
+            rim_row = posts_ref[which, planes, band_width : band_width + 1, :]
+            piece = jnp.where(row == 0, rim_row, pltpu.roll(piece, 1, 1))
+        elif shift_y == -1:
+            rim_row = posts_ref[which, planes, band_width + 1 : band_width + 2, :]
+            piece = jnp.where(row == band_width - 1, rim_row, pltpu.roll(piece, band_width - 1, 1))
         if shift_z == 1:
             piece = jnp.where(lane == 0, 0.0, pltpu.roll(piece, 1, 2))
         elif shift_z == -1:
@@ -131,7 +137,7 @@
             velocity_ref[dimension, index] = velocity[dimension]
         for fan_number in range(fans):
             flow_ref[fan_number] += (
-                discs_ref[fan_number, index + rim, rim : rim + band_width, :] * velocity[0]
+                discs_ref[fan_number, index + rim, 0:band_width, :] * velocity[0]
             )
         return carry
 
@@ -264,12 +270,12 @@
     extended = []
     first = 0
     for field, channel in zip(fields, channels):
-        extended.append(
-            jnp.concatenate(
-                [from_left[first : first + channel], field, from_right[first : first + channel]],
-                axis=dim,
-            )
-        )
+        left = from_left[first : first + channel]
+        right = from_right[first : first + channel]
+        if dim == 1:
+            extended.append(jnp.concatenate([left, field, right], axis=dim))
+        else:
+            extended.append(jnp.concatenate([field, left, right], axis=dim))
         first = first + channel
     return (extended, total)
 
@@ -316,7 +322,13 @@
     breadth_total = band_width * lax.axis_size("band")
     solid_flag = solid_mask == 1
     coord_x = offset_len - 1 + jnp.arange(slab_len + 2, dtype=jnp.int32)
-    coord_y = jnp.mod(offset_band - 1 + jnp.arange(band_width + 2, dtype=jnp.int32), breadth_total)
+    coord_y = jnp.mod(
+        offset_band
+        + jnp.concatenate(
+            [jnp.arange(band_width, dtype=jnp.int32), jnp.array([-1, band_width], jnp.int32)]
+        ),
+        breadth_total,
+    )
     coord_z = jnp.arange(height, dtype=jnp.int32)
     along_in = jnp.mod(coord_x[None, :] - fan_hubs[:, 0:1], length_total) < FAN_LEN
     offset_y = coord_y[None, :] - fan_hubs[:, 1:2]
@@ -332,7 +344,7 @@
     band_reach = max(-(-(2 * RAD + 1) // band_width), (band_width + 2 * RAD) // band_width)
     inner_discs = (
         along_in[:, 1:-1, None, None]
-        & across_in[:, None, 1:-1]
+        & across_in[:, None, 0:band_width]
         & jnp.logical_not(solid_flag)[None]
     ).astype(jnp.float32)
     velocity, flow = first_moments(populations, inner_discs)
@@ -354,10 +366,14 @@
         strength = fan_gain * (jet_speed - totals / float(disc_count()))
         last = repeat == ITERS - 1
         stepped = lattice_step(strength, extended, discs, solid_rim, not last)
-        ahead_x = rimmed[2:, 1:-1]
-        behind_x = rimmed[:-2, 1:-1]
-        ahead_y = rimmed[1:-1, 2:]
-        behind_y = rimmed[1:-1, :-2]
+        ahead_x = rimmed[2:, 0:band_width]
+        behind_x = rimmed[:-2, 0:band_width]
+        ahead_y = jnp.concatenate(
+            [rimmed[1:-1, 1:band_width], rimmed[1:-1, band_width + 1 : band_width + 2]], axis=1
+        )
+        behind_y = jnp.concatenate(
+            [rimmed[1:-1, band_width : band_width + 1], rimmed[1:-1, 0 : band_width - 1]], axis=1
+        )
         smoke_field = advance(
             smoke_field,
             ahead_x,

time: 83.4 us -> 83.8 us (level)
  no operation moved by 1% of the time
where the time goes in v10:
time: 83.8 us; the launch traced here: 83.4 us
  starting transfers between devices  27.4 us (33%)
  Pallas kernels  17.6 us (21%)
  waiting for transfers between devices  17.1 us (20%)
  other arithmetic  16.3 us (19%)
  local copies, waits for them, and re-layouts  3.59 us (4%)
  between operations  1.17 us (1%)
    pallas_call x3, Pallas kernels, lattice_step(): pl.pallas_call(functools.partial(step_kernel, with_moments), out_shape=tu...  15.2 us
    ppermute x3, starting transfers between devices, rim_round(): from_right = lax.ppermute(head, axis, backward)  13 us
    ppermute x6, starting transfers between devices, rim_round(): lax.ppermute(flow, axis, [(i, (i + offset) % count) for i in range(count)])  10.1 us
    ppermute x3, waiting for transfers between devices, rim_round(): from_left = lax.ppermute(tail, axis, forward)  8.39 us
    concatenate x4, other arithmetic, rim_round(): extended.append(jnp.concatenate([field, left, right], axis=dim))  5.05 us
    ppermute x6, waiting for transfers between devices, rim_round(): lax.ppermute(flow, axis, [(i, (i + offset) % count) for i in range(count)])  4.22 us
    ppermute x3, waiting for transfers between devices, rim_round(): both = lax.ppermute(jnp.concatenate([tail, head], axis=0), axis, forward)  4.14 us
    ppermute x3, starting transfers between devices, rim_round(): from_left = lax.ppermute(tail, axis, forward)  4.12 us
  transfers between devices with their start and end apart: 15, of which 9 were waited for; matrix products, arithmetic and copies ran while one was open for 1% of the time, Pallas kernels for 0%

profile of v10, /device:TPU:0, one launch (start us, length us, event | category | flops | bytes accessed | tf_op | source)
XLA Modules:
  0.0 83.4 jit_solution(512935090186531583)
XLA Ops:
  0.7 0.8 slice_bitcast_fusion.12
  1.7 0.7 and_select_fusion
  2.5 0.1 add_compare_fusion
  2.6 0.9 %convert_bitcast_fusion = (f32[1,8,16,128]{3,2,1,0:T(8,128)S(1)}, pred[8,16,128]{2,1,0:T(8,128)(4,1)S(1)}) fusion(s32[8,16,128]{2,1,0:T(8,128)} %param.34), kind=kLoop, calls=%fused_computation.69 | loop fusion | flops 32768 | bytes 147456 | tf_op jit(solution)/shard_map/broadcast_in_dim | solution.py:355
  3.5 0.9 %and_convert_fusion.1.discs_ref = f32[8,8,16,128]{3,2,1,0:T(8,128)} fusion(pred[8,16,128]{2,1,0:T(8,128)(4,1)S(1)} %not.3, pred[8,16,128]{2,1,0:T(8,128)(4,1)S(1)} %slice.654, pred[8,8]{1,0:T(8,128)(4,1)S(1)} %slice.548), kind=kLoop, calls=%fused_computation.4 | loop fusion | flops 393216 | bytes 557120 | tf_op jit(solution)/shard_map/convert_element_type | solution.py:349
  4.4 2.4 %shard_map.104 = (f32[3,8,16,128]{3,2,1,0:T(8,128)}, f32[8,16,128]{2,1,0:T(8,128)}) custom-call(f32[19,8,16,128]{3,2,1,0:T(8,128)} %populations_ref.1, f32[8,8,16,128]{3,2,1,0:T(8,128)} %and_convert_fusion.1.discs_ref), custom_call_target="tpu_custom_call" | custom-call | flops 983040 | bytes 1245184 | tf_op jit(solution)/shard_map/pallas_call | solution.py:150
  6.8 1.0 %reduce_sum.27 = f32[8]{0:T(128)S(1)} reduce(f32[8,16,128]{2,1,0:T(8,128)} %get-tuple-element.130, f32[]{:T(128)} %constant.273.clone.1), dimensions={1,2}, to_apply=%region_0.1 | reduce | flops 16376 | bytes 65572 | tf_op jit(solution)/shard_map/reduce_sum | solution.py:351
  7.8 6.0 %collective-permute-start.3 = (f32[8]{0:T(128)S(1)}, f32[8]{0:T(128)S(1)}, u32[]{:S(2)}, u32[]{:S(2)}) collective-permute-start(f32[8]{0:T(128)S(1)} %reduce_sum.27), channel_id=1, source_target_pairs={{0,28},{2,30},{4,0},{6,2},{8,4},{10,6},{12,8},{14,10},{16,12},{18,... | collective-permute-start | bytes 104 | tf_op jit(solution)/shard_map/ppermute | solution.py:269
  13.9 1.5 %collective-permute-start = (f32[22,1,16,128]{3,2,1,0:T(8,128)S(1)}, f32[22,1,16,128]{3,2,1,0:T(8,128)S(1)}, u32[]{:S(2)}, u32[]{:S(2)}) collective-permute-start(f32[22,1,16,128]{3,2,1,0:T(8,128)S(1)} %get-tuple-element.204), channel_id=1, source_target_pairs={{0,2},{2,4},{4,6},{6,8},{8,10},{10,12},{12,14},{14,16},{16,18},{18... | collective-permute-start | bytes 540680 | tf_op jit(solution)/shard_map/ppermute | solution.py:265
  15.5 4.2 %collective-permute-start.1 = (f32[22,1,16,128]{3,2,1,0:T(8,128)S(1)}, f32[22,1,16,128]{3,2,1,0:T(8,128)S(1)}, u32[]{:S(2)}, u32[]{:S(2)}) collective-permute-start(f32[22,1,16,128]{3,2,1,0:T(8,128)S(1)} %get-tuple-element.205), channel_id=1, source_target_pairs={{2,0},{4,2},{6,4},{8,6},{10,8},{12,10},{14,12},{16,14},{18,16},{20... | collective-permute-start | bytes 540680 | tf_op jit(solution)/shard_map/ppermute | solution.py:266
  19.8 0.1 broadcast_multiply_fusion
  19.9 0.2 fusion.2
  20.2 3.5 %collective-permute-done = f32[22,1,16,128]{3,2,1,0:T(8,128)S(1)} collective-permute-done((f32[22,1,16,128]{3,2,1,0:T(8,128)S(1)}, f32[22,1,16,128]{3,2,1,0:T(8,128)S(1)}, u32[]{:S(2)}, u32[]{:S(2)}) %collective-permute-start) | collective-permute-done | bytes 180256 | tf_op jit(solution)/shard_map/ppermute | solution.py:265
  23.8 0.1 maximum_dynamic-update-slice_fusion.2
  24.2 1.4 %collective-permute-done.4 = f32[44,10,1,128]{3,2,1,0:T(1,128)S(1)} collective-permute-done((f32[44,10,1,128]{3,2,1,0:T(1,128)S(1)}, f32[44,10,1,128]{3,2,1,0:T(1,128)S(1)}, u32[]{:S(2)}, u32[]{:S(2)}) %collective-permute-start.4) | collective-permute-done | bytes 225312 | tf_op jit(solution)/shard_map/ppermute | solution.py:260
  25.7 0.1 fusion.24
  25.9 1.1 %and_convert_fusion.discs_ref = f32[8,10,18,128]{3,2,1,0:T(8,128)} fusion(pred[10,18,128]{2,1,0:T(8,128)(4,1)S(1)} %maximum_compare_fusion, pred[8,18,128]{2,1,0:T(8,128)(4,1)S(1)} %add_compare_fusion, pred[8,10]{1,0:T(8,128)(4,1)S(1)} %fusion.28), kind=kLoop, calls=%fused_computation.3 | loop fusion | flops 552960 | bytes 778832 | tf_op jit(solution)/shard_map/convert_element_type | solution.py:363
  27.0 0.6 maximum_bitcast_fusion.solid_ref
  27.7 1.7 %pad_maximum_fusion.populations_ref = f32[19,10,18,128]{3,2,1,0:T(8,128)} fusion(f32[19,10,1,128]{3,2,1,0:T(1,128)S(1)} %get-tuple-element.153, f32[19,10,1,128]{3,2,1,0:T(1,128)S(1)} %get-tuple-element.152, f32[19,1,16,128]{3,2,1,0:T(8,128)S(1)} %slice.662, f32[19,8,16,128]{3,2,1,0:T(8,128)S(1)} %copy-done, f32[19,1,16,128]{3,2,1,0:T(8,128)S(1)} %slice.661), kind=kLoop, calls=%fused_computation | loop fusion | flops 1751040 | bytes 3502080 | tf_op jit(solution)/shard_map/concatenate | solution.py:278
  29.4 0.6 fusion.57.strength_ref
  29.9 5.2 %shard_map.105 = (f32[19,8,16,128]{3,2,1,0:T(8,128)}, f32[3,8,16,128]{3,2,1,0:T(8,128)}, f32[8,16,128]{2,1,0:T(8,128)}) custom-call(f32[8]{0:T(128)} %fusion.57.strength_ref, f32[19,10,18,128]{3,2,1,0:T(8,128)} %pad_maximum_fusion.populations_ref, f32[8,10,18,128]{3,2,1,0:T(8,128)} %and_convert_fusion.discs_ref, f32[10,18,128]{2,1,0:T(8,128)} %maximum_bitcast_fusion.solid_ref), custom_call_target="tpu_custom_call" | custom-call | flops 6912000 | bytes 5253120 | tf_op jit(solution)/shard_map/pallas_call | solution.py:176
  35.1 1.1 %reduce_sum.28 = f32[8]{0:T(128)S(1)} reduce(f32[8,16,128]{2,1,0:T(8,128)} %get-tuple-element.131, f32[]{:T(128)} %constant.273.clone.1), dimensions={1,2}, to_apply=%region_1.2 | reduce | flops 16376 | bytes 65572 | tf_op jit(solution)/shard_map/reduce_sum | solution.py:392
  36.2 1.0 %fusion.63 = (f32[19,1,16,128]{3,2,1,0:T(8,128)S(1)}, f32[19,1,16,128]{3,2,1,0:T(8,128)S(1)}) fusion(f32[19,8,16,128]{3,2,1,0:T(8,128)} %get-tuple-element.132), kind=kLoop, calls=%fused_computation.162 | loop fusion | bytes 622592 | tf_op jit(solution)/shard_map/slice | solution.py:251
  37.3 1.7 %collective-permute-start.5 = (f32[21,1,16,128]{3,2,1,0:T(8,128)S(1)}, f32[21,1,16,128]{3,2,1,0:T(8,128)S(1)}, u32[]{:S(2)}, u32[]{:S(2)}) collective-permute-start(f32[21,1,16,128]{3,2,1,0:T(8,128)S(1)} %get-tuple-element.196), channel_id=1, source_target_pairs={{0,2},{2,4},{4,6},{6,8},{8,10},{10,12},{12,14},{14,16},{16,18},{18... | collective-permute-start | bytes 516104 | tf_op jit(solution)/shard_map/ppermute | solution.py:265
  38.9 4.0 %collective-permute-start.6 = (f32[21,1,16,128]{3,2,1,0:T(8,128)S(1)}, f32[21,1,16,128]{3,2,1,0:T(8,128)S(1)}, u32[]{:S(2)}, u32[]{:S(2)}) collective-permute-start(f32[21,1,16,128]{3,2,1,0:T(8,128)S(1)} %get-tuple-element.197), channel_id=1, source_target_pairs={{2,0},{4,2},{6,4},{8,6},{10,8},{12,10},{14,12},{16,14},{18,16},{20... | collective-permute-start | bytes 516104 | tf_op jit(solution)/shard_map/ppermute | solution.py:266
  42.9 1.4 %collective-permute-start.8 = (f32[8]{0:T(128)S(1)}, f32[8]{0:T(128)S(1)}, u32[]{:S(2)}, u32[]{:S(2)}) collective-permute-start(f32[8]{0:T(128)S(1)} %reduce_sum.28), channel_id=1, source_target_pairs={{0,28},{2,30},{4,0},{6,2},{8,4},{10,6},{12,8},{14,10},{16,12},{18,... | collective-permute-start | bytes 104 | tf_op jit(solution)/shard_map/ppermute | solution.py:269
  44.3 0.6 collective-permute-start.7
  45.0 2.5 %collective-permute-done.5 = f32[21,1,16,128]{3,2,1,0:T(8,128)S(1)} collective-permute-done((f32[21,1,16,128]{3,2,1,0:T(8,128)S(1)}, f32[21,1,16,128]{3,2,1,0:T(8,128)S(1)}, u32[]{:S(2)}, u32[]{:S(2)}) %collective-permute-start.5) | collective-permute-done | bytes 172064 | tf_op jit(solution)/shard_map/ppermute | solution.py:265
  47.5 0.4 collective-permute-done.6
  47.9 0.1 maximum_dynamic-update-slice_fusion.1
  48.0 2.6 %collective-permute-done.7 = f32[8]{0:T(128)S(1)} collective-permute-done((f32[8]{0:T(128)S(1)}, f32[8]{0:T(128)S(1)}, u32[]{:S(2)}, u32[]{:S(2)}) %collective-permute-start.7) | collective-permute-done | bytes 64 | tf_op jit(solution)/shard_map/ppermute | solution.py:269
  50.8 1.4 %collective-permute-done.9 = f32[42,10,1,128]{3,2,1,0:T(1,128)S(1)} collective-permute-done((f32[42,10,1,128]{3,2,1,0:T(1,128)S(1)}, f32[42,10,1,128]{3,2,1,0:T(1,128)S(1)}, u32[]{:S(2)}, u32[]{:S(2)}) %collective-permute-start.9) | collective-permute-done | bytes 215072 | tf_op jit(solution)/shard_map/ppermute | solution.py:260
  52.3 0.1 fusion.18
  52.4 1.7 %pad_maximum_fusion.1.populations_ref = f32[19,10,18,128]{3,2,1,0:T(8,128)} fusion(f32[19,10,1,128]{3,2,1,0:T(1,128)S(1)} %get-tuple-element.161, f32[19,10,1,128]{3,2,1,0:T(1,128)S(1)} %get-tuple-element.160, f32[19,1,16,128]{3,2,1,0:T(8,128)S(1)} %slice.687, f32[19,8,16,128]{3,2,1,0:T(8,128)S(1)} %copy-done.1, f32[19,1,16,128]{3,2,1,0:T(8,128)S(1)} %slice.686), kind=kLoop, calls=%fused_computation.1 | loop fusion | flops 1751040 | bytes 3502080 | tf_op jit(solution)/shard_map/concatenate | solution.py:278
  54.1 0.5 fusion.58.strength_ref
  54.7 5.2 %shard_map.106 = (f32[19,8,16,128]{3,2,1,0:T(8,128)}, f32[3,8,16,128]{3,2,1,0:T(8,128)}, f32[8,16,128]{2,1,0:T(8,128)}) custom-call(f32[8]{0:T(128)} %fusion.58.strength_ref, f32[19,10,18,128]{3,2,1,0:T(8,128)} %pad_maximum_fusion.1.populations_ref, f32[8,10,18,128]{3,2,1,0:T(8,128)} %and_convert_fusion.discs_ref, f32[10,18,128]{2,1,0:T(8,128)} %maximum_bitcast_fusion.solid_ref), custom_call_target="tpu_custom_call" | custom-call | flops 6912000 | bytes 5253120 | tf_op jit(solution)/shard_map/pallas_call | solution.py:176
  59.8 1.1 %reduce_sum.29 = f32[8]{0:T(128)S(1)} reduce(f32[8,16,128]{2,1,0:T(8,128)} %get-tuple-element.134, f32[]{:T(128)} %constant.273.clone.1), dimensions={1,2}, to_apply=%region_2.3 | reduce | flops 16376 | bytes 65572 | tf_op jit(solution)/shard_map/reduce_sum | solution.py:392
  60.9 1.0 %fusion.62 = (f32[19,1,16,128]{3,2,1,0:T(8,128)S(1)}, f32[19,1,16,128]{3,2,1,0:T(8,128)S(1)}) fusion(f32[19,8,16,128]{3,2,1,0:T(8,128)} %get-tuple-element.135), kind=kLoop, calls=%fused_computation.161 | loop fusion | bytes 622592 | tf_op jit(solution)/shard_map/slice | solution.py:251
  62.0 0.9 %collective-permute-start.10 = (f32[21,1,16,128]{3,2,1,0:T(8,128)S(1)}, f32[21,1,16,128]{3,2,1,0:T(8,128)S(1)}, u32[]{:S(2)}, u32[]{:S(2)}) collective-permute-start(f32[21,1,16,128]{3,2,1,0:T(8,128)S(1)} %get-tuple-element.194), channel_id=1, source_target_pairs={{0,2},{2,4},{4,6},{6,8},{8,10},{10,12},{12,14},{14,16},{16,18},{18... | collective-permute-start | bytes 516104 | tf_op jit(solution)/shard_map/ppermute | solution.py:265
  62.9 4.8 %collective-permute-start.11 = (f32[21,1,16,128]{3,2,1,0:T(8,128)S(1)}, f32[21,1,16,128]{3,2,1,0:T(8,128)S(1)}, u32[]{:S(2)}, u32[]{:S(2)}) collective-permute-start(f32[21,1,16,128]{3,2,1,0:T(8,128)S(1)} %get-tuple-element.195), channel_id=1, source_target_pairs={{2,0},{4,2},{6,4},{8,6},{10,8},{12,10},{14,12},{16,14},{18,16},{20... | collective-permute-start | bytes 516104 | tf_op jit(solution)/shard_map/ppermute | solution.py:266
  67.7 2.0 %collective-permute-start.12 = (f32[8]{0:T(128)S(1)}, f32[8]{0:T(128)S(1)}, u32[]{:S(2)}, u32[]{:S(2)}) collective-permute-start(f32[8]{0:T(128)S(1)} %reduce_sum.29), channel_id=1, source_target_pairs={{0,4},{2,6},{4,8},{6,10},{8,12},{10,14},{12,16},{14,18},{16,20},{1... | collective-permute-start | bytes 104 | tf_op jit(solution)/shard_map/ppermute | solution.py:269
  69.7 2.4 %collective-permute-done.10 = f32[21,1,16,128]{3,2,1,0:T(8,128)S(1)} collective-permute-done((f32[21,1,16,128]{3,2,1,0:T(8,128)S(1)}, f32[21,1,16,128]{3,2,1,0:T(8,128)S(1)}, u32[]{:S(2)}, u32[]{:S(2)}) %collective-permute-start.10) | collective-permute-done | bytes 172064 | tf_op jit(solution)/shard_map/ppermute | solution.py:265
  72.3 1.6 %collective-permute-done.12 = f32[8]{0:T(128)S(1)} collective-permute-done((f32[8]{0:T(128)S(1)}, f32[8]{0:T(128)S(1)}, u32[]{:S(2)}, u32[]{:S(2)}) %collective-permute-start.12) | collective-permute-done | bytes 64 | tf_op jit(solution)/shard_map/ppermute | solution.py:269
  74.2 1.4 %collective-permute-done.14 = f32[42,10,1,128]{3,2,1,0:T(1,128)S(1)} collective-permute-done((f32[42,10,1,128]{3,2,1,0:T(1,128)S(1)}, f32[42,10,1,128]{3,2,1,0:T(1,128)S(1)}, u32[]{:S(2)}, u32[]{:S(2)}) %collective-permute-start.14) | collective-permute-done | bytes 215072 | tf_op jit(solution)/shard_map/ppermute | solution.py:260
  75.6 1.7 %pad_maximum_fusion.2.populations_ref = f32[19,10,18,128]{3,2,1,0:T(8,128)} fusion(f32[19,10,1,128]{3,2,1,0:T(1,128)S(1)} %get-tuple-element.157, f32[19,10,1,128]{3,2,1,0:T(1,128)S(1)} %get-tuple-element.156, f32[19,1,16,128]{3,2,1,0:T(8,128)S(1)} %slice.708, f32[19,8,16,128]{3,2,1,0:T(8,128)S(1)} %copy-done.2, f32[19,1,16,128]{3,2,1,0:T(8,128)S(1)} %slice.707), kind=kLoop, calls=%fused_computation.2 | loop fusion | flops 1751040 | bytes 3502080 | tf_op jit(solution)/shard_map/concatenate | solution.py:278
  77.3 0.5 fusion.59.strength_ref
  77.8 4.9 %shard_map.107 = f32[19,8,16,128]{3,2,1,0:T(8,128)} custom-call(f32[8]{0:T(128)} %fusion.59.strength_ref, f32[19,10,18,128]{3,2,1,0:T(8,128)} %pad_maximum_fusion.2.populations_ref, f32[8,10,18,128]{3,2,1,0:T(8,128)} %and_convert_fusion.discs_ref, f32[10,18,128]{2,1,0:T(8,128)} %maximum_bitcast_fusion.solid_ref), custom_call_target="tpu_custom_call" | custom-call | flops 6912000 | bytes 5253120 | tf_op jit(solution)/shard_map/pallas_call | solution.py:176
  82.7 0.7 fusion.12
  (105 shorter events, 1.9 us)
Async XLA Ops:
  0.6 13.2 %copy-start = (f32[19,8,16,128]{3,2,1,0:T(8,128)S(1)}, f32[19,8,16,128]{3,2,1,0:T(8,128)}, u32[]{:S(2)}) copy-start(f32[19,8,16,128]{3,2,1,0:T(8,128)} %populations_ref.1) | copy-start | bytes 3735556
  0.6 13.2 %copy-start.3 = (f32[8,16,128]{2,1,0:T(8,128)S(1)}, f32[8,16,128]{2,1,0:T(8,128)}, u32[]{:S(2)}) copy-start(f32[8,16,128]{2,1,0:T(8,128)} %param.35) | copy-start | bytes 196612
  0.7 19.0 %copy-start.9 = (s32[16,3]{0,1:T(4,128)S(1)}, s32[16,3]{0,1:T(4,128)}, u32[]{:S(2)}) copy-start(s32[16,3]{0,1:T(4,128)} %param.39) | copy-start | bytes 580
  0.7 19.3 %copy-start.10 = (f32[16]{0:T(128)S(1)}, f32[16]{0:T(128)}, u32[]{:S(2)}) copy-start(f32[16]{0:T(128)} %param.40) | copy-start | bytes 196
  7.8 16.1 %collective-permute-start.3 = (f32[8]{0:T(128)S(1)}, f32[8]{0:T(128)S(1)}, u32[]{:S(2)}, u32[]{:S(2)}) collective-permute-start(f32[8]{0:T(128)S(1)} %reduce_sum.27), channel_id=1, source_target_pairs={{0,28},{2,30},{4,0},{6,2},{8,4},{10,6},{12,8},{14,10},{16,12},{18,... | collective-permute-start | bytes 104 | tf_op jit(solution)/shard_map/ppermute | solution.py:269
  13.8 10.1 %collective-permute-start.2 = (f32[8]{0:T(128)S(1)}, f32[8]{0:T(128)S(1)}, u32[]{:S(2)}, u32[]{:S(2)}) collective-permute-start(f32[8]{0:T(128)S(1)} %reduce_sum.27), channel_id=1, source_target_pairs={{0,4},{2,6},{4,8},{6,10},{8,12},{10,14},{12,16},{14,18},{16,20},{1... | collective-permute-start | bytes 104 | tf_op jit(solution)/shard_map/ppermute | solution.py:269
  13.9 9.8 %collective-permute-start = (f32[22,1,16,128]{3,2,1,0:T(8,128)S(1)}, f32[22,1,16,128]{3,2,1,0:T(8,128)S(1)}, u32[]{:S(2)}, u32[]{:S(2)}) collective-permute-start(f32[22,1,16,128]{3,2,1,0:T(8,128)S(1)} %get-tuple-element.204), channel_id=1, source_target_pairs={{0,2},{2,4},{4,6},{6,8},{8,10},{10,12},{12,14},{14,16},{16,18},{18... | collective-permute-start | bytes 540680 | tf_op jit(solution)/shard_map/ppermute | solution.py:265
  15.5 8.3 %collective-permute-start.1 = (f32[22,1,16,128]{3,2,1,0:T(8,128)S(1)}, f32[22,1,16,128]{3,2,1,0:T(8,128)S(1)}, u32[]{:S(2)}, u32[]{:S(2)}) collective-permute-start(f32[22,1,16,128]{3,2,1,0:T(8,128)S(1)} %get-tuple-element.205), channel_id=1, source_target_pairs={{2,0},{4,2},{6,4},{8,6},{10,8},{12,10},{14,12},{16,14},{18,16},{20... | collective-permute-start | bytes 540680 | tf_op jit(solution)/shard_map/ppermute | solution.py:266
  23.8 2.0 %copy-start.4 = (f32[3,8,16,128]{3,2,1,0:T(8,128)S(1)}, f32[3,8,16,128]{3,2,1,0:T(8,128)}, u32[]{:S(2)}) copy-start(f32[3,8,16,128]{3,2,1,0:T(8,128)} %get-tuple-element.133) | copy-start | bytes 589828
  24.1 1.5 %collective-permute-start.4 = (f32[44,10,1,128]{3,2,1,0:T(1,128)S(1)}, f32[44,10,1,128]{3,2,1,0:T(1,128)S(1)}, u32[]{:S(2)}, u32[]{:S(2)}) collective-permute-start(f32[44,10,1,128]{3,2,1,0:T(1,128)S(1)} %constant_dynamic-update-slice_fusion), channel_id=1, source_target_pairs={{0,1},{1,0},{2,3},{3,2},{4,5},{5,4},{6,7},{7,6},{8,9},{9,8},{10,11... | collective-permute-start | bytes 675848 | tf_op jit(solution)/shard_map/ppermute | solution.py:260
  27.0 2.4 %copy-start.7 = (f32[8]{0:T(128)S(1)}, f32[8]{0:T(128)}, u32[]{:S(2)}) copy-start(f32[8]{0:T(128)} %param.37) | copy-start | bytes 100
  27.0 2.4 %copy-start.8 = (f32[8]{0:T(128)S(1)}, f32[8]{0:T(128)}, u32[]{:S(2)}) copy-start(f32[8]{0:T(128)} %param.38) | copy-start | bytes 100
  35.1 12.7 %copy-start.1 = (f32[19,8,16,128]{3,2,1,0:T(8,128)S(1)}, f32[19,8,16,128]{3,2,1,0:T(8,128)}, u32[]{:S(2)}) copy-start(f32[19,8,16,128]{3,2,1,0:T(8,128)} %get-tuple-element.132) | copy-start | bytes 3735556
  37.3 10.2 %collective-permute-start.5 = (f32[21,1,16,128]{3,2,1,0:T(8,128)S(1)}, f32[21,1,16,128]{3,2,1,0:T(8,128)S(1)}, u32[]{:S(2)}, u32[]{:S(2)}) collective-permute-start(f32[21,1,16,128]{3,2,1,0:T(8,128)S(1)} %get-tuple-element.196), channel_id=1, source_target_pairs={{0,2},{2,4},{4,6},{6,8},{8,10},{10,12},{12,14},{14,16},{16,18},{18... | collective-permute-start | bytes 516104 | tf_op jit(solution)/shard_map/ppermute | solution.py:265
  38.9 8.9 %collective-permute-start.6 = (f32[21,1,16,128]{3,2,1,0:T(8,128)S(1)}, f32[21,1,16,128]{3,2,1,0:T(8,128)S(1)}, u32[]{:S(2)}, u32[]{:S(2)}) collective-permute-start(f32[21,1,16,128]{3,2,1,0:T(8,128)S(1)} %get-tuple-element.197), channel_id=1, source_target_pairs={{2,0},{4,2},{6,4},{8,6},{10,8},{12,10},{14,12},{16,14},{18,16},{20... | collective-permute-start | bytes 516104 | tf_op jit(solution)/shard_map/ppermute | solution.py:266
  42.9 5.1 %collective-permute-start.8 = (f32[8]{0:T(128)S(1)}, f32[8]{0:T(128)S(1)}, u32[]{:S(2)}, u32[]{:S(2)}) collective-permute-start(f32[8]{0:T(128)S(1)} %reduce_sum.28), channel_id=1, source_target_pairs={{0,28},{2,30},{4,0},{6,2},{8,4},{10,6},{12,8},{14,10},{16,12},{18,... | collective-permute-start | bytes 104 | tf_op jit(solution)/shard_map/ppermute | solution.py:269
  44.3 6.2 %collective-permute-start.7 = (f32[8]{0:T(128)S(1)}, f32[8]{0:T(128)S(1)}, u32[]{:S(2)}, u32[]{:S(2)}) collective-permute-start(f32[8]{0:T(128)S(1)} %reduce_sum.28), channel_id=1, source_target_pairs={{0,4},{2,6},{4,8},{6,10},{8,12},{10,14},{12,16},{14,18},{16,20},{1... | collective-permute-start | bytes 104 | tf_op jit(solution)/shard_map/ppermute | solution.py:269
  47.5 4.8 %copy-start.6 = (f32[3,8,16,128]{3,2,1,0:T(8,128)S(1)}, f32[3,8,16,128]{3,2,1,0:T(8,128)}, u32[]{:S(2)}) copy-start(f32[3,8,16,128]{3,2,1,0:T(8,128)} %get-tuple-element.136) | copy-start | bytes 589828
  50.7 1.5 %collective-permute-start.9 = (f32[42,10,1,128]{3,2,1,0:T(1,128)S(1)}, f32[42,10,1,128]{3,2,1,0:T(1,128)S(1)}, u32[]{:S(2)}, u32[]{:S(2)}) collective-permute-start(f32[42,10,1,128]{3,2,1,0:T(1,128)S(1)} %constant_dynamic-update-slice_fusion.6), channel_id=1, source_target_pairs={{0,1},{1,0},{2,3},{3,2},{4,5},{5,4},{6,7},{7,6},{8,9},{9,8},{10,11... | collective-permute-start | bytes 645128 | tf_op jit(solution)/shard_map/ppermute | solution.py:260
  59.8 12.3 %copy-start.2 = (f32[19,8,16,128]{3,2,1,0:T(8,128)S(1)}, f32[19,8,16,128]{3,2,1,0:T(8,128)}, u32[]{:S(2)}) copy-start(f32[19,8,16,128]{3,2,1,0:T(8,128)} %get-tuple-element.135) | copy-start | bytes 3735556
  62.0 10.1 %collective-permute-start.10 = (f32[21,1,16,128]{3,2,1,0:T(8,128)S(1)}, f32[21,1,16,128]{3,2,1,0:T(8,128)S(1)}, u32[]{:S(2)}, u32[]{:S(2)}) collective-permute-start(f32[21,1,16,128]{3,2,1,0:T(8,128)S(1)} %get-tuple-element.194), channel_id=1, source_target_pairs={{0,2},{2,4},{4,6},{6,8},{8,10},{10,12},{12,14},{14,16},{16,18},{18... | collective-permute-start | bytes 516104 | tf_op jit(solution)/shard_map/ppermute | solution.py:265
  62.9 9.2 %collective-permute-start.11 = (f32[21,1,16,128]{3,2,1,0:T(8,128)S(1)}, f32[21,1,16,128]{3,2,1,0:T(8,128)S(1)}, u32[]{:S(2)}, u32[]{:S(2)}) collective-permute-start(f32[21,1,16,128]{3,2,1,0:T(8,128)S(1)} %get-tuple-element.195), channel_id=1, source_target_pairs={{2,0},{4,2},{6,4},{8,6},{10,8},{12,10},{14,12},{16,14},{18,16},{20... | collective-permute-start | bytes 516104 | tf_op jit(solution)/shard_map/ppermute | solution.py:266
  67.7 4.6 %collective-permute-start.13 = (f32[8]{0:T(128)S(1)}, f32[8]{0:T(128)S(1)}, u32[]{:S(2)}, u32[]{:S(2)}) collective-permute-start(f32[8]{0:T(128)S(1)} %reduce_sum.29), channel_id=1, source_target_pairs={{0,28},{2,30},{4,0},{6,2},{8,4},{10,6},{12,8},{14,10},{16,12},{18,... | collective-permute-start | bytes 104 | tf_op jit(solution)/shard_map/ppermute | solution.py:269
  67.7 6.2 %collective-permute-start.12 = (f32[8]{0:T(128)S(1)}, f32[8]{0:T(128)S(1)}, u32[]{:S(2)}, u32[]{:S(2)}) collective-permute-start(f32[8]{0:T(128)S(1)} %reduce_sum.29), channel_id=1, source_target_pairs={{0,4},{2,6},{4,8},{6,10},{8,12},{10,14},{12,16},{14,18},{16,20},{1... | collective-permute-start | bytes 104 | tf_op jit(solution)/shard_map/ppermute | solution.py:269
  74.0 1.5 %collective-permute-start.14 = (f32[42,10,1,128]{3,2,1,0:T(1,128)S(1)}, f32[42,10,1,128]{3,2,1,0:T(1,128)S(1)}, u32[]{:S(2)}, u32[]{:S(2)}) collective-permute-start(f32[42,10,1,128]{3,2,1,0:T(1,128)S(1)} %constant_dynamic-update-slice_fusion.10), channel_id=1, source_target_pairs={{0,1},{1,0},{2,3},{3,2},{4,5},{5,4},{6,7},{7,6},{8,9},{9,8},{10,11... | collective-permute-start | bytes 645128 | tf_op jit(solution)/shard_map/ppermute | solution.py:260
  77.8 4.9 %copy-start.5 = (f32[3,8,16,128]{3,2,1,0:T(8,128)S(1)}, f32[3,8,16,128]{3,2,1,0:T(8,128)}, u32[]{:S(2)}) copy-start(f32[3,8,16,128]{3,2,1,0:T(8,128)} %get-tuple-element.137) | copy-start | bytes 589828

commit v11 on v10

--- a/solution.py
+++ b/solution.py
@@ -83,7 +83,7 @@
     fans = discs_ref.shape[0]
     slab_len, band_width, height = out_ref.shape[1:]
 
-    def collide_plane(index, carry):
+    def collide_at(index, chosen):
         populations = [populations_ref[which, index] for which in range(19)]
         density, velocity = plane_moments(populations)
         force_field = strength_ref[0] * discs_ref[0, index]
@@ -91,7 +91,7 @@
             force_field = force_field + strength_ref[fan_number] * discs_ref[fan_number, index]
         solid_flag = solid_ref[index] != 0.0
         speed_sq = velocity[0] * velocity[0] + velocity[1] * velocity[1] + velocity[2] * velocity[2]
-        for which in range(19):
+        for which in chosen:
             shift_x, shift_y, shift_z = VELOCITIES[which]
             along = shift_x * velocity[0] + shift_y * velocity[1] + shift_z * velocity[2]
             balance = (
@@ -101,29 +101,52 @@
             if shift_x != 0:
                 relaxed = relaxed + 3.0 * WEIGHTS[which] * shift_x * force_field
             posts_ref[which, index] = jnp.where(solid_flag, populations[OPPOSITE[which]], relaxed)
+
+    every = tuple(range(19))
+    collide_at(0, tuple(which for which in every if VELOCITIES[which][0] == 1))
+
+    def collide_plane(index, carry):
+        collide_at(index, every)
         return carry
 
-    lax.fori_loop(0, populations_ref.shape[1], collide_plane, 0)
-    lane = lax.broadcasted_iota(jnp.int32, (slab_len, band_width, height), 2)
-    row = lax.broadcasted_iota(jnp.int32, (slab_len, band_width, height), 1)
-    for which in range(19):
-        shift_x, shift_y, shift_z = VELOCITIES[which]
-        planes = slice(1 - shift_x, 1 - shift_x + slab_len)
-        piece = posts_ref[which, planes, 0:band_width, :]
-        if shift_y == 1:
-            rim_row = posts_ref[which, planes, band_width : band_width + 1, :]
-            piece = jnp.where(row == 0, rim_row, pltpu.roll(piece, 1, 1))
-        elif shift_y == -1:
-            rim_row = posts_ref[which, planes, band_width + 1 : band_width + 2, :]
-            piece = jnp.where(row == band_width - 1, rim_row, pltpu.roll(piece, band_width - 1, 1))
-        if shift_z == 1:
-            piece = jnp.where(lane == 0, 0.0, pltpu.roll(piece, 1, 2))
-        elif shift_z == -1:
-            piece = jnp.where(lane == height - 1, 0.0, pltpu.roll(piece, height - 1, 2))
-        out_ref[which] = piece
-    if not with_moments:
-        return
-    moments_into(out_ref, discs_ref, 1, velocity_ref, flow_ref)
+    lax.fori_loop(1, slab_len + 1, collide_plane, 0)
+    collide_at(slab_len + 1, tuple(which for which in every if VELOCITIES[which][0] == -1))
+    row = lax.broadcasted_iota(jnp.int32, (band_width, height), 0)
+    lane = lax.broadcasted_iota(jnp.int32, (band_width, height), 1)
+    if with_moments:
+        flow_ref[...] = jnp.zeros(flow_ref.shape, jnp.float32)
+
+    def stream_plane(index, carry):
+        pieces = []
+        for which in range(19):
+            shift_x, shift_y, shift_z = VELOCITIES[which]
+            plane = index + 1 - shift_x
+            piece = posts_ref[which, plane, 0:band_width, :]
+            if shift_y == 1:
+                rim_row = posts_ref[which, plane, band_width : band_width + 1, :]
+                piece = jnp.where(row == 0, rim_row, pltpu.roll(piece, 1, 0))
+            elif shift_y == -1:
+                rim_row = posts_ref[which, plane, band_width + 1 : band_width + 2, :]
+                piece = jnp.where(
+                    row == band_width - 1, rim_row, pltpu.roll(piece, band_width - 1, 0)
+                )
+            if shift_z == 1:
+                piece = jnp.where(lane == 0, 0.0, pltpu.roll(piece, 1, 1))
+            elif shift_z == -1:
+                piece = jnp.where(lane == height - 1, 0.0, pltpu.roll(piece, height - 1, 1))
+            out_ref[which, index] = piece
+            pieces.append(piece)
+        if with_moments:
+            density, velocity = plane_moments(pieces)
+            for dimension in range(3):
+                velocity_ref[dimension, index] = velocity[dimension]
+            for fan_number in range(fans):
+                flow_ref[fan_number] += (
+                    discs_ref[fan_number, index + 1, 0:band_width, :] * velocity[0]
+                )
+        return carry
+
+    lax.fori_loop(0, slab_len, stream_plane, 0)
 
 
 def moments_into(populations_ref, discs_ref, rim, velocity_ref, flow_ref):

time: 83.8 us -> 84.4 us (level)
  no operation moved by 1% of the time
where the time goes in v11:
time: 84.4 us; the launch traced here: 84 us
  starting transfers between devices  27.4 us (32%)
  Pallas kernels  18.2 us (22%)
  waiting for transfers between devices  17.1 us (20%)
  other arithmetic  16.3 us (19%)
  local copies, waits for them, and re-layouts  3.59 us (4%)
  between operations  1.17 us (1%)
    pallas_call x3, Pallas kernels, lattice_step(): pl.pallas_call(functools.partial(step_kernel, with_moments), out_shape=tu...  15.8 us
    ppermute x3, starting transfers between devices, rim_round(): from_right = lax.ppermute(head, axis, backward)  13 us
    ppermute x6, starting transfers between devices, rim_round(): lax.ppermute(flow, axis, [(i, (i + offset) % count) for i in range(count)])  10.1 us
    ppermute x3, waiting for transfers between devices, rim_round(): from_left = lax.ppermute(tail, axis, forward)  8.39 us
    concatenate x4, other arithmetic, rim_round(): extended.append(jnp.concatenate([field, left, right], axis=dim))  5.05 us
    ppermute x6, waiting for transfers between devices, rim_round(): lax.ppermute(flow, axis, [(i, (i + offset) % count) for i in range(count)])  4.22 us
    ppermute x3, waiting for transfers between devices, rim_round(): both = lax.ppermute(jnp.concatenate([tail, head], axis=0), axis, forward)  4.14 us
    ppermute x3, starting transfers between devices, rim_round(): from_left = lax.ppermute(tail, axis, forward)  4.12 us
  transfers between devices with their start and end apart: 15, of which 9 were waited for; matrix products, arithmetic and copies ran while one was open for 1% of the time, Pallas kernels for 0%

profile of v11, /device:TPU:0, one launch (start us, length us, event | category | flops | bytes accessed | tf_op | source)
XLA Modules:
  0.0 84.0 jit_solution(7213061914678785926)
XLA Ops:
  0.7 0.8 slice_bitcast_fusion.12
  1.7 0.7 and_select_fusion
  2.5 0.1 add_compare_fusion
  2.6 0.9 %convert_bitcast_fusion = (f32[1,8,16,128]{3,2,1,0:T(8,128)S(1)}, pred[8,16,128]{2,1,0:T(8,128)(4,1)S(1)}) fusion(s32[8,16,128]{2,1,0:T(8,128)} %param.34), kind=kLoop, calls=%fused_computation.69 | loop fusion | flops 32768 | bytes 147456 | tf_op jit(solution)/shard_map/broadcast_in_dim | solution.py:378
  3.5 0.9 %and_convert_fusion.1.discs_ref = f32[8,8,16,128]{3,2,1,0:T(8,128)} fusion(pred[8,16,128]{2,1,0:T(8,128)(4,1)S(1)} %not.3, pred[8,16,128]{2,1,0:T(8,128)(4,1)S(1)} %slice.654, pred[8,8]{1,0:T(8,128)(4,1)S(1)} %slice.548), kind=kLoop, calls=%fused_computation.4 | loop fusion | flops 393216 | bytes 557120 | tf_op jit(solution)/shard_map/convert_element_type | solution.py:372
  4.4 2.4 %shard_map.104 = (f32[3,8,16,128]{3,2,1,0:T(8,128)}, f32[8,16,128]{2,1,0:T(8,128)}) custom-call(f32[19,8,16,128]{3,2,1,0:T(8,128)} %populations_ref.1, f32[8,8,16,128]{3,2,1,0:T(8,128)} %and_convert_fusion.1.discs_ref), custom_call_target="tpu_custom_call" | custom-call | flops 983040 | bytes 1245184 | tf_op jit(solution)/shard_map/pallas_call | solution.py:173
  6.8 1.0 %reduce_sum.27 = f32[8]{0:T(128)S(1)} reduce(f32[8,16,128]{2,1,0:T(8,128)} %get-tuple-element.130, f32[]{:T(128)} %constant.273.clone.1), dimensions={1,2}, to_apply=%region_0.1 | reduce | flops 16376 | bytes 65572 | tf_op jit(solution)/shard_map/reduce_sum | solution.py:374
  7.8 6.0 %collective-permute-start.3 = (f32[8]{0:T(128)S(1)}, f32[8]{0:T(128)S(1)}, u32[]{:S(2)}, u32[]{:S(2)}) collective-permute-start(f32[8]{0:T(128)S(1)} %reduce_sum.27), channel_id=1, source_target_pairs={{0,28},{2,30},{4,0},{6,2},{8,4},{10,6},{12,8},{14,10},{16,12},{18,... | collective-permute-start | bytes 104 | tf_op jit(solution)/shard_map/ppermute | solution.py:292
  13.9 1.5 %collective-permute-start = (f32[22,1,16,128]{3,2,1,0:T(8,128)S(1)}, f32[22,1,16,128]{3,2,1,0:T(8,128)S(1)}, u32[]{:S(2)}, u32[]{:S(2)}) collective-permute-start(f32[22,1,16,128]{3,2,1,0:T(8,128)S(1)} %get-tuple-element.204), channel_id=1, source_target_pairs={{0,2},{2,4},{4,6},{6,8},{8,10},{10,12},{12,14},{14,16},{16,18},{18... | collective-permute-start | bytes 540680 | tf_op jit(solution)/shard_map/ppermute | solution.py:288
  15.5 4.2 %collective-permute-start.1 = (f32[22,1,16,128]{3,2,1,0:T(8,128)S(1)}, f32[22,1,16,128]{3,2,1,0:T(8,128)S(1)}, u32[]{:S(2)}, u32[]{:S(2)}) collective-permute-start(f32[22,1,16,128]{3,2,1,0:T(8,128)S(1)} %get-tuple-element.205), channel_id=1, source_target_pairs={{2,0},{4,2},{6,4},{8,6},{10,8},{12,10},{14,12},{16,14},{18,16},{20... | collective-permute-start | bytes 540680 | tf_op jit(solution)/shard_map/ppermute | solution.py:289
  19.8 0.1 broadcast_multiply_fusion
  19.9 0.2 fusion.2
  20.2 3.5 %collective-permute-done = f32[22,1,16,128]{3,2,1,0:T(8,128)S(1)} collective-permute-done((f32[22,1,16,128]{3,2,1,0:T(8,128)S(1)}, f32[22,1,16,128]{3,2,1,0:T(8,128)S(1)}, u32[]{:S(2)}, u32[]{:S(2)}) %collective-permute-start) | collective-permute-done | bytes 180256 | tf_op jit(solution)/shard_map/ppermute | solution.py:288
  23.8 0.1 maximum_dynamic-update-slice_fusion.2
  24.2 1.4 %collective-permute-done.4 = f32[44,10,1,128]{3,2,1,0:T(1,128)S(1)} collective-permute-done((f32[44,10,1,128]{3,2,1,0:T(1,128)S(1)}, f32[44,10,1,128]{3,2,1,0:T(1,128)S(1)}, u32[]{:S(2)}, u32[]{:S(2)}) %collective-permute-start.4) | collective-permute-done | bytes 225312 | tf_op jit(solution)/shard_map/ppermute | solution.py:283
  25.7 0.1 fusion.24
  25.9 1.1 %and_convert_fusion.discs_ref = f32[8,10,18,128]{3,2,1,0:T(8,128)} fusion(pred[10,18,128]{2,1,0:T(8,128)(4,1)S(1)} %maximum_compare_fusion, pred[8,18,128]{2,1,0:T(8,128)(4,1)S(1)} %add_compare_fusion, pred[8,10]{1,0:T(8,128)(4,1)S(1)} %fusion.28), kind=kLoop, calls=%fused_computation.3 | loop fusion | flops 552960 | bytes 778832 | tf_op jit(solution)/shard_map/convert_element_type | solution.py:386
  27.0 0.6 maximum_bitcast_fusion.solid_ref
  27.7 1.7 %pad_maximum_fusion.populations_ref = f32[19,10,18,128]{3,2,1,0:T(8,128)} fusion(f32[19,10,1,128]{3,2,1,0:T(1,128)S(1)} %get-tuple-element.153, f32[19,10,1,128]{3,2,1,0:T(1,128)S(1)} %get-tuple-element.152, f32[19,1,16,128]{3,2,1,0:T(8,128)S(1)} %slice.662, f32[19,8,16,128]{3,2,1,0:T(8,128)S(1)} %copy-done, f32[19,1,16,128]{3,2,1,0:T(8,128)S(1)} %slice.661), kind=kLoop, calls=%fused_computation | loop fusion | flops 1751040 | bytes 3502080 | tf_op jit(solution)/shard_map/concatenate | solution.py:301
  29.4 0.6 fusion.57.strength_ref
  29.9 5.3 %shard_map.105 = (f32[19,8,16,128]{3,2,1,0:T(8,128)}, f32[3,8,16,128]{3,2,1,0:T(8,128)}, f32[8,16,128]{2,1,0:T(8,128)}) custom-call(f32[8]{0:T(128)} %fusion.57.strength_ref, f32[19,10,18,128]{3,2,1,0:T(8,128)} %pad_maximum_fusion.populations_ref, f32[8,10,18,128]{3,2,1,0:T(8,128)} %and_convert_fusion.discs_ref, f32[10,18,128]{2,1,0:T(8,128)} %maximum_bitcast_fusion.solid_ref), custom_call_target="tpu_custom_call" | custom-call | flops 6912000 | bytes 5253120 | tf_op jit(solution)/shard_map/pallas_call | solution.py:199
  35.3 1.1 %reduce_sum.28 = f32[8]{0:T(128)S(1)} reduce(f32[8,16,128]{2,1,0:T(8,128)} %get-tuple-element.131, f32[]{:T(128)} %constant.273.clone.1), dimensions={1,2}, to_apply=%region_1.2 | reduce | flops 16376 | bytes 65572 | tf_op jit(solution)/shard_map/reduce_sum | solution.py:415
  36.4 1.0 %fusion.63 = (f32[19,1,16,128]{3,2,1,0:T(8,128)S(1)}, f32[19,1,16,128]{3,2,1,0:T(8,128)S(1)}) fusion(f32[19,8,16,128]{3,2,1,0:T(8,128)} %get-tuple-element.132), kind=kLoop, calls=%fused_computation.162 | loop fusion | bytes 622592 | tf_op jit(solution)/shard_map/slice | solution.py:274
  37.4 1.7 %collective-permute-start.5 = (f32[21,1,16,128]{3,2,1,0:T(8,128)S(1)}, f32[21,1,16,128]{3,2,1,0:T(8,128)S(1)}, u32[]{:S(2)}, u32[]{:S(2)}) collective-permute-start(f32[21,1,16,128]{3,2,1,0:T(8,128)S(1)} %get-tuple-element.196), channel_id=1, source_target_pairs={{0,2},{2,4},{4,6},{6,8},{8,10},{10,12},{12,14},{14,16},{16,18},{18... | collective-permute-start | bytes 516104 | tf_op jit(solution)/shard_map/ppermute | solution.py:288
  39.1 4.0 %collective-permute-start.6 = (f32[21,1,16,128]{3,2,1,0:T(8,128)S(1)}, f32[21,1,16,128]{3,2,1,0:T(8,128)S(1)}, u32[]{:S(2)}, u32[]{:S(2)}) collective-permute-start(f32[21,1,16,128]{3,2,1,0:T(8,128)S(1)} %get-tuple-element.197), channel_id=1, source_target_pairs={{2,0},{4,2},{6,4},{8,6},{10,8},{12,10},{14,12},{16,14},{18,16},{20... | collective-permute-start | bytes 516104 | tf_op jit(solution)/shard_map/ppermute | solution.py:289
  43.1 1.4 %collective-permute-start.8 = (f32[8]{0:T(128)S(1)}, f32[8]{0:T(128)S(1)}, u32[]{:S(2)}, u32[]{:S(2)}) collective-permute-start(f32[8]{0:T(128)S(1)} %reduce_sum.28), channel_id=1, source_target_pairs={{0,28},{2,30},{4,0},{6,2},{8,4},{10,6},{12,8},{14,10},{16,12},{18,... | collective-permute-start | bytes 104 | tf_op jit(solution)/shard_map/ppermute | solution.py:292
  44.5 0.6 collective-permute-start.7
  45.1 2.5 %collective-permute-done.5 = f32[21,1,16,128]{3,2,1,0:T(8,128)S(1)} collective-permute-done((f32[21,1,16,128]{3,2,1,0:T(8,128)S(1)}, f32[21,1,16,128]{3,2,1,0:T(8,128)S(1)}, u32[]{:S(2)}, u32[]{:S(2)}) %collective-permute-start.5) | collective-permute-done | bytes 172064 | tf_op jit(solution)/shard_map/ppermute | solution.py:288
  47.6 0.4 collective-permute-done.6
  48.0 0.1 maximum_dynamic-update-slice_fusion.1
  48.1 2.6 %collective-permute-done.7 = f32[8]{0:T(128)S(1)} collective-permute-done((f32[8]{0:T(128)S(1)}, f32[8]{0:T(128)S(1)}, u32[]{:S(2)}, u32[]{:S(2)}) %collective-permute-start.7) | collective-permute-done | bytes 64 | tf_op jit(solution)/shard_map/ppermute | solution.py:292
  51.0 1.4 %collective-permute-done.9 = f32[42,10,1,128]{3,2,1,0:T(1,128)S(1)} collective-permute-done((f32[42,10,1,128]{3,2,1,0:T(1,128)S(1)}, f32[42,10,1,128]{3,2,1,0:T(1,128)S(1)}, u32[]{:S(2)}, u32[]{:S(2)}) %collective-permute-start.9) | collective-permute-done | bytes 215072 | tf_op jit(solution)/shard_map/ppermute | solution.py:283
  52.4 0.1 fusion.18
  52.6 1.7 %pad_maximum_fusion.1.populations_ref = f32[19,10,18,128]{3,2,1,0:T(8,128)} fusion(f32[19,10,1,128]{3,2,1,0:T(1,128)S(1)} %get-tuple-element.161, f32[19,10,1,128]{3,2,1,0:T(1,128)S(1)} %get-tuple-element.160, f32[19,1,16,128]{3,2,1,0:T(8,128)S(1)} %slice.687, f32[19,8,16,128]{3,2,1,0:T(8,128)S(1)} %copy-done.1, f32[19,1,16,128]{3,2,1,0:T(8,128)S(1)} %slice.686), kind=kLoop, calls=%fused_computation.1 | loop fusion | flops 1751040 | bytes 3502080 | tf_op jit(solution)/shard_map/concatenate | solution.py:301
  54.3 0.5 fusion.58.strength_ref
  54.8 5.3 %shard_map.106 = (f32[19,8,16,128]{3,2,1,0:T(8,128)}, f32[3,8,16,128]{3,2,1,0:T(8,128)}, f32[8,16,128]{2,1,0:T(8,128)}) custom-call(f32[8]{0:T(128)} %fusion.58.strength_ref, f32[19,10,18,128]{3,2,1,0:T(8,128)} %pad_maximum_fusion.1.populations_ref, f32[8,10,18,128]{3,2,1,0:T(8,128)} %and_convert_fusion.discs_ref, f32[10,18,128]{2,1,0:T(8,128)} %maximum_bitcast_fusion.solid_ref), custom_call_target="tpu_custom_call" | custom-call | flops 6912000 | bytes 5253120 | tf_op jit(solution)/shard_map/pallas_call | solution.py:199
  60.1 1.1 %reduce_sum.29 = f32[8]{0:T(128)S(1)} reduce(f32[8,16,128]{2,1,0:T(8,128)} %get-tuple-element.134, f32[]{:T(128)} %constant.273.clone.1), dimensions={1,2}, to_apply=%region_2.3 | reduce | flops 16376 | bytes 65572 | tf_op jit(solution)/shard_map/reduce_sum | solution.py:415
  61.2 1.0 %fusion.62 = (f32[19,1,16,128]{3,2,1,0:T(8,128)S(1)}, f32[19,1,16,128]{3,2,1,0:T(8,128)S(1)}) fusion(f32[19,8,16,128]{3,2,1,0:T(8,128)} %get-tuple-element.135), kind=kLoop, calls=%fused_computation.161 | loop fusion | bytes 622592 | tf_op jit(solution)/shard_map/slice | solution.py:274
  62.3 0.9 %collective-permute-start.10 = (f32[21,1,16,128]{3,2,1,0:T(8,128)S(1)}, f32[21,1,16,128]{3,2,1,0:T(8,128)S(1)}, u32[]{:S(2)}, u32[]{:S(2)}) collective-permute-start(f32[21,1,16,128]{3,2,1,0:T(8,128)S(1)} %get-tuple-element.194), channel_id=1, source_target_pairs={{0,2},{2,4},{4,6},{6,8},{8,10},{10,12},{12,14},{14,16},{16,18},{18... | collective-permute-start | bytes 516104 | tf_op jit(solution)/shard_map/ppermute | solution.py:288
  63.2 4.8 %collective-permute-start.11 = (f32[21,1,16,128]{3,2,1,0:T(8,128)S(1)}, f32[21,1,16,128]{3,2,1,0:T(8,128)S(1)}, u32[]{:S(2)}, u32[]{:S(2)}) collective-permute-start(f32[21,1,16,128]{3,2,1,0:T(8,128)S(1)} %get-tuple-element.195), channel_id=1, source_target_pairs={{2,0},{4,2},{6,4},{8,6},{10,8},{12,10},{14,12},{16,14},{18,16},{20... | collective-permute-start | bytes 516104 | tf_op jit(solution)/shard_map/ppermute | solution.py:289
  68.0 2.0 %collective-permute-start.12 = (f32[8]{0:T(128)S(1)}, f32[8]{0:T(128)S(1)}, u32[]{:S(2)}, u32[]{:S(2)}) collective-permute-start(f32[8]{0:T(128)S(1)} %reduce_sum.29), channel_id=1, source_target_pairs={{0,4},{2,6},{4,8},{6,10},{8,12},{10,14},{12,16},{14,18},{16,20},{1... | collective-permute-start | bytes 104 | tf_op jit(solution)/shard_map/ppermute | solution.py:292
  70.0 2.4 %collective-permute-done.10 = f32[21,1,16,128]{3,2,1,0:T(8,128)S(1)} collective-permute-done((f32[21,1,16,128]{3,2,1,0:T(8,128)S(1)}, f32[21,1,16,128]{3,2,1,0:T(8,128)S(1)}, u32[]{:S(2)}, u32[]{:S(2)}) %collective-permute-start.10) | collective-permute-done | bytes 172064 | tf_op jit(solution)/shard_map/ppermute | solution.py:288
  72.6 1.6 %collective-permute-done.12 = f32[8]{0:T(128)S(1)} collective-permute-done((f32[8]{0:T(128)S(1)}, f32[8]{0:T(128)S(1)}, u32[]{:S(2)}, u32[]{:S(2)}) %collective-permute-start.12) | collective-permute-done | bytes 64 | tf_op jit(solution)/shard_map/ppermute | solution.py:292
  74.5 1.4 %collective-permute-done.14 = f32[42,10,1,128]{3,2,1,0:T(1,128)S(1)} collective-permute-done((f32[42,10,1,128]{3,2,1,0:T(1,128)S(1)}, f32[42,10,1,128]{3,2,1,0:T(1,128)S(1)}, u32[]{:S(2)}, u32[]{:S(2)}) %collective-permute-start.14) | collective-permute-done | bytes 215072 | tf_op jit(solution)/shard_map/ppermute | solution.py:283
  75.9 1.7 %pad_maximum_fusion.2.populations_ref = f32[19,10,18,128]{3,2,1,0:T(8,128)} fusion(f32[19,10,1,128]{3,2,1,0:T(1,128)S(1)} %get-tuple-element.157, f32[19,10,1,128]{3,2,1,0:T(1,128)S(1)} %get-tuple-element.156, f32[19,1,16,128]{3,2,1,0:T(8,128)S(1)} %slice.708, f32[19,8,16,128]{3,2,1,0:T(8,128)S(1)} %copy-done.2, f32[19,1,16,128]{3,2,1,0:T(8,128)S(1)} %slice.707), kind=kLoop, calls=%fused_computation.2 | loop fusion | flops 1751040 | bytes 3502080 | tf_op jit(solution)/shard_map/concatenate | solution.py:301
  77.6 0.5 fusion.59.strength_ref
  78.1 5.2 %shard_map.107 = f32[19,8,16,128]{3,2,1,0:T(8,128)} custom-call(f32[8]{0:T(128)} %fusion.59.strength_ref, f32[19,10,18,128]{3,2,1,0:T(8,128)} %pad_maximum_fusion.2.populations_ref, f32[8,10,18,128]{3,2,1,0:T(8,128)} %and_convert_fusion.discs_ref, f32[10,18,128]{2,1,0:T(8,128)} %maximum_bitcast_fusion.solid_ref), custom_call_target="tpu_custom_call" | custom-call | flops 6912000 | bytes 5253120 | tf_op jit(solution)/shard_map/pallas_call | solution.py:199
  83.3 0.7 fusion.12
  (105 shorter events, 1.9 us)
Async XLA Ops:
  0.6 13.2 %copy-start = (f32[19,8,16,128]{3,2,1,0:T(8,128)S(1)}, f32[19,8,16,128]{3,2,1,0:T(8,128)}, u32[]{:S(2)}) copy-start(f32[19,8,16,128]{3,2,1,0:T(8,128)} %populations_ref.1) | copy-start | bytes 3735556
  0.6 13.2 %copy-start.3 = (f32[8,16,128]{2,1,0:T(8,128)S(1)}, f32[8,16,128]{2,1,0:T(8,128)}, u32[]{:S(2)}) copy-start(f32[8,16,128]{2,1,0:T(8,128)} %param.35) | copy-start | bytes 196612
  0.7 19.0 %copy-start.9 = (s32[16,3]{0,1:T(4,128)S(1)}, s32[16,3]{0,1:T(4,128)}, u32[]{:S(2)}) copy-start(s32[16,3]{0,1:T(4,128)} %param.39) | copy-start | bytes 580
  0.7 19.3 %copy-start.10 = (f32[16]{0:T(128)S(1)}, f32[16]{0:T(128)}, u32[]{:S(2)}) copy-start(f32[16]{0:T(128)} %param.40) | copy-start | bytes 196
  7.8 16.1 %collective-permute-start.3 = (f32[8]{0:T(128)S(1)}, f32[8]{0:T(128)S(1)}, u32[]{:S(2)}, u32[]{:S(2)}) collective-permute-start(f32[8]{0:T(128)S(1)} %reduce_sum.27), channel_id=1, source_target_pairs={{0,28},{2,30},{4,0},{6,2},{8,4},{10,6},{12,8},{14,10},{16,12},{18,... | collective-permute-start | bytes 104 | tf_op jit(solution)/shard_map/ppermute | solution.py:292
  13.8 10.1 %collective-permute-start.2 = (f32[8]{0:T(128)S(1)}, f32[8]{0:T(128)S(1)}, u32[]{:S(2)}, u32[]{:S(2)}) collective-permute-start(f32[8]{0:T(128)S(1)} %reduce_sum.27), channel_id=1, source_target_pairs={{0,4},{2,6},{4,8},{6,10},{8,12},{10,14},{12,16},{14,18},{16,20},{1... | collective-permute-start | bytes 104 | tf_op jit(solution)/shard_map/ppermute | solution.py:292
  13.9 9.8 %collective-permute-start = (f32[22,1,16,128]{3,2,1,0:T(8,128)S(1)}, f32[22,1,16,128]{3,2,1,0:T(8,128)S(1)}, u32[]{:S(2)}, u32[]{:S(2)}) collective-permute-start(f32[22,1,16,128]{3,2,1,0:T(8,128)S(1)} %get-tuple-element.204), channel_id=1, source_target_pairs={{0,2},{2,4},{4,6},{6,8},{8,10},{10,12},{12,14},{14,16},{16,18},{18... | collective-permute-start | bytes 540680 | tf_op jit(solution)/shard_map/ppermute | solution.py:288
  15.5 8.3 %collective-permute-start.1 = (f32[22,1,16,128]{3,2,1,0:T(8,128)S(1)}, f32[22,1,16,128]{3,2,1,0:T(8,128)S(1)}, u32[]{:S(2)}, u32[]{:S(2)}) collective-permute-start(f32[22,1,16,128]{3,2,1,0:T(8,128)S(1)} %get-tuple-element.205), channel_id=1, source_target_pairs={{2,0},{4,2},{6,4},{8,6},{10,8},{12,10},{14,12},{16,14},{18,16},{20... | collective-permute-start | bytes 540680 | tf_op jit(solution)/shard_map/ppermute | solution.py:289
  23.8 2.0 %copy-start.4 = (f32[3,8,16,128]{3,2,1,0:T(8,128)S(1)}, f32[3,8,16,128]{3,2,1,0:T(8,128)}, u32[]{:S(2)}) copy-start(f32[3,8,16,128]{3,2,1,0:T(8,128)} %get-tuple-element.133) | copy-start | bytes 589828
  24.1 1.5 %collective-permute-start.4 = (f32[44,10,1,128]{3,2,1,0:T(1,128)S(1)}, f32[44,10,1,128]{3,2,1,0:T(1,128)S(1)}, u32[]{:S(2)}, u32[]{:S(2)}) collective-permute-start(f32[44,10,1,128]{3,2,1,0:T(1,128)S(1)} %constant_dynamic-update-slice_fusion), channel_id=1, source_target_pairs={{0,1},{1,0},{2,3},{3,2},{4,5},{5,4},{6,7},{7,6},{8,9},{9,8},{10,11... | collective-permute-start | bytes 675848 | tf_op jit(solution)/shard_map/ppermute | solution.py:283
  27.0 2.4 %copy-start.7 = (f32[8]{0:T(128)S(1)}, f32[8]{0:T(128)}, u32[]{:S(2)}) copy-start(f32[8]{0:T(128)} %param.37) | copy-start | bytes 100
  27.0 2.4 %copy-start.8 = (f32[8]{0:T(128)S(1)}, f32[8]{0:T(128)}, u32[]{:S(2)}) copy-start(f32[8]{0:T(128)} %param.38) | copy-start | bytes 100
  35.3 12.7 %copy-start.1 = (f32[19,8,16,128]{3,2,1,0:T(8,128)S(1)}, f32[19,8,16,128]{3,2,1,0:T(8,128)}, u32[]{:S(2)}) copy-start(f32[19,8,16,128]{3,2,1,0:T(8,128)} %get-tuple-element.132) | copy-start | bytes 3735556
  37.4 10.2 %collective-permute-start.5 = (f32[21,1,16,128]{3,2,1,0:T(8,128)S(1)}, f32[21,1,16,128]{3,2,1,0:T(8,128)S(1)}, u32[]{:S(2)}, u32[]{:S(2)}) collective-permute-start(f32[21,1,16,128]{3,2,1,0:T(8,128)S(1)} %get-tuple-element.196), channel_id=1, source_target_pairs={{0,2},{2,4},{4,6},{6,8},{8,10},{10,12},{12,14},{14,16},{16,18},{18... | collective-permute-start | bytes 516104 | tf_op jit(solution)/shard_map/ppermute | solution.py:288
  39.1 8.9 %collective-permute-start.6 = (f32[21,1,16,128]{3,2,1,0:T(8,128)S(1)}, f32[21,1,16,128]{3,2,1,0:T(8,128)S(1)}, u32[]{:S(2)}, u32[]{:S(2)}) collective-permute-start(f32[21,1,16,128]{3,2,1,0:T(8,128)S(1)} %get-tuple-element.197), channel_id=1, source_target_pairs={{2,0},{4,2},{6,4},{8,6},{10,8},{12,10},{14,12},{16,14},{18,16},{20... | collective-permute-start | bytes 516104 | tf_op jit(solution)/shard_map/ppermute | solution.py:289
  43.1 5.1 %collective-permute-start.8 = (f32[8]{0:T(128)S(1)}, f32[8]{0:T(128)S(1)}, u32[]{:S(2)}, u32[]{:S(2)}) collective-permute-start(f32[8]{0:T(128)S(1)} %reduce_sum.28), channel_id=1, source_target_pairs={{0,28},{2,30},{4,0},{6,2},{8,4},{10,6},{12,8},{14,10},{16,12},{18,... | collective-permute-start | bytes 104 | tf_op jit(solution)/shard_map/ppermute | solution.py:292
  44.5 6.2 %collective-permute-start.7 = (f32[8]{0:T(128)S(1)}, f32[8]{0:T(128)S(1)}, u32[]{:S(2)}, u32[]{:S(2)}) collective-permute-start(f32[8]{0:T(128)S(1)} %reduce_sum.28), channel_id=1, source_target_pairs={{0,4},{2,6},{4,8},{6,10},{8,12},{10,14},{12,16},{14,18},{16,20},{1... | collective-permute-start | bytes 104 | tf_op jit(solution)/shard_map/ppermute | solution.py:292
  47.6 4.8 %copy-start.6 = (f32[3,8,16,128]{3,2,1,0:T(8,128)S(1)}, f32[3,8,16,128]{3,2,1,0:T(8,128)}, u32[]{:S(2)}) copy-start(f32[3,8,16,128]{3,2,1,0:T(8,128)} %get-tuple-element.136) | copy-start | bytes 589828
  50.8 1.5 %collective-permute-start.9 = (f32[42,10,1,128]{3,2,1,0:T(1,128)S(1)}, f32[42,10,1,128]{3,2,1,0:T(1,128)S(1)}, u32[]{:S(2)}, u32[]{:S(2)}) collective-permute-start(f32[42,10,1,128]{3,2,1,0:T(1,128)S(1)} %constant_dynamic-update-slice_fusion.6), channel_id=1, source_target_pairs={{0,1},{1,0},{2,3},{3,2},{4,5},{5,4},{6,7},{7,6},{8,9},{9,8},{10,11... | collective-permute-start | bytes 645128 | tf_op jit(solution)/shard_map/ppermute | solution.py:283
  60.1 12.3 %copy-start.2 = (f32[19,8,16,128]{3,2,1,0:T(8,128)S(1)}, f32[19,8,16,128]{3,2,1,0:T(8,128)}, u32[]{:S(2)}) copy-start(f32[19,8,16,128]{3,2,1,0:T(8,128)} %get-tuple-element.135) | copy-start | bytes 3735556
  62.3 10.1 %collective-permute-start.10 = (f32[21,1,16,128]{3,2,1,0:T(8,128)S(1)}, f32[21,1,16,128]{3,2,1,0:T(8,128)S(1)}, u32[]{:S(2)}, u32[]{:S(2)}) collective-permute-start(f32[21,1,16,128]{3,2,1,0:T(8,128)S(1)} %get-tuple-element.194), channel_id=1, source_target_pairs={{0,2},{2,4},{4,6},{6,8},{8,10},{10,12},{12,14},{14,16},{16,18},{18... | collective-permute-start | bytes 516104 | tf_op jit(solution)/shard_map/ppermute | solution.py:288
  63.2 9.2 %collective-permute-start.11 = (f32[21,1,16,128]{3,2,1,0:T(8,128)S(1)}, f32[21,1,16,128]{3,2,1,0:T(8,128)S(1)}, u32[]{:S(2)}, u32[]{:S(2)}) collective-permute-start(f32[21,1,16,128]{3,2,1,0:T(8,128)S(1)} %get-tuple-element.195), channel_id=1, source_target_pairs={{2,0},{4,2},{6,4},{8,6},{10,8},{12,10},{14,12},{16,14},{18,16},{20... | collective-permute-start | bytes 516104 | tf_op jit(solution)/shard_map/ppermute | solution.py:289
  68.0 4.6 %collective-permute-start.13 = (f32[8]{0:T(128)S(1)}, f32[8]{0:T(128)S(1)}, u32[]{:S(2)}, u32[]{:S(2)}) collective-permute-start(f32[8]{0:T(128)S(1)} %reduce_sum.29), channel_id=1, source_target_pairs={{0,28},{2,30},{4,0},{6,2},{8,4},{10,6},{12,8},{14,10},{16,12},{18,... | collective-permute-start | bytes 104 | tf_op jit(solution)/shard_map/ppermute | solution.py:292
  68.0 6.2 %collective-permute-start.12 = (f32[8]{0:T(128)S(1)}, f32[8]{0:T(128)S(1)}, u32[]{:S(2)}, u32[]{:S(2)}) collective-permute-start(f32[8]{0:T(128)S(1)} %reduce_sum.29), channel_id=1, source_target_pairs={{0,4},{2,6},{4,8},{6,10},{8,12},{10,14},{12,16},{14,18},{16,20},{1... | collective-permute-start | bytes 104 | tf_op jit(solution)/shard_map/ppermute | solution.py:292
  74.3 1.5 %collective-permute-start.14 = (f32[42,10,1,128]{3,2,1,0:T(1,128)S(1)}, f32[42,10,1,128]{3,2,1,0:T(1,128)S(1)}, u32[]{:S(2)}, u32[]{:S(2)}) collective-permute-start(f32[42,10,1,128]{3,2,1,0:T(1,128)S(1)} %constant_dynamic-update-slice_fusion.10), channel_id=1, source_target_pairs={{0,1},{1,0},{2,3},{3,2},{4,5},{5,4},{6,7},{7,6},{8,9},{9,8},{10,11... | collective-permute-start | bytes 645128 | tf_op jit(solution)/shard_map/ppermute | solution.py:283
  78.1 5.2 %copy-start.5 = (f32[3,8,16,128]{3,2,1,0:T(8,128)S(1)}, f32[3,8,16,128]{3,2,1,0:T(8,128)}, u32[]{:S(2)}) copy-start(f32[3,8,16,128]{3,2,1,0:T(8,128)} %get-tuple-element.137) | copy-start | bytes 589828

commit v12 on v10

--- a/solution.py
+++ b/solution.py
@@ -75,7 +75,9 @@
     return (density, velocity)
 
 
-def step_kernel(with_moments, strength_ref, populations_ref, discs_ref, solid_ref, *rest):
+def step_kernel(
+    with_moments, strength_ref, inner_ref, low_ref, high_ref, rows_ref, discs_ref, solid_ref, *rest
+):
     if with_moments:
         out_ref, velocity_ref, flow_ref, posts_ref = rest
     else:
@@ -83,13 +85,12 @@
     fans = discs_ref.shape[0]
     slab_len, band_width, height = out_ref.shape[1:]
 
-    def collide_plane(index, carry):
-        populations = [populations_ref[which, index] for which in range(19)]
+    def collide_into(populations, index, rows):
         density, velocity = plane_moments(populations)
-        force_field = strength_ref[0] * discs_ref[0, index]
+        force_field = strength_ref[0] * discs_ref[0, index, rows]
         for fan_number in range(1, fans):
-            force_field = force_field + strength_ref[fan_number] * discs_ref[fan_number, index]
-        solid_flag = solid_ref[index] != 0.0
+            force_field = force_field + strength_ref[fan_number] * discs_ref[fan_number, index, rows]
+        solid_flag = solid_ref[index, rows] != 0.0
         speed_sq = velocity[0] * velocity[0] + velocity[1] * velocity[1] + velocity[2] * velocity[2]
         for which in range(19):
             shift_x, shift_y, shift_z = VELOCITIES[which]
@@ -100,10 +101,26 @@
             relaxed = populations[which] - RELAX_RATE * (populations[which] - balance)
             if shift_x != 0:
                 relaxed = relaxed + 3.0 * WEIGHTS[which] * shift_x * force_field
-            posts_ref[which, index] = jnp.where(solid_flag, populations[OPPOSITE[which]], relaxed)
+            posts_ref[which, index, rows] = jnp.where(
+                solid_flag, populations[OPPOSITE[which]], relaxed
+            )
+
+    inner = slice(0, band_width)
+    rim = slice(band_width, band_width + 2)
+    collide_into([low_ref[which, 0] for which in range(19)], 0, inner)
+    collide_into([high_ref[which, 0] for which in range(19)], slab_len + 1, inner)
+
+    def collide_plane(index, carry):
+        collide_into([inner_ref[which, index - 1] for which in range(19)], index, inner)
         return carry
 
-    lax.fori_loop(0, populations_ref.shape[1], collide_plane, 0)
+    lax.fori_loop(1, slab_len + 1, collide_plane, 0)
+
+    def collide_rim(index, carry):
+        collide_into([rows_ref[which, index] for which in range(19)], index, rim)
+        return carry
+
+    lax.fori_loop(0, slab_len + 2, collide_rim, 0)
     lane = lax.broadcasted_iota(jnp.int32, (slab_len, band_width, height), 2)
     row = lax.broadcasted_iota(jnp.int32, (slab_len, band_width, height), 1)
     for which in range(19):
@@ -163,10 +180,10 @@
     )(populations, discs)
 
 
-def lattice_step(strength, extended, discs, solid_rim, with_moments):
-    slab_len = extended.shape[1] - 2
-    band_width = extended.shape[2] - 2
-    height = extended.shape[3]
+def lattice_step(strength, inner, low, high, rows, discs, solid_rim, with_moments):
+    slab_len = inner.shape[1]
+    band_width = inner.shape[2]
+    height = inner.shape[3]
     fans = discs.shape[0]
     out_shape = [jax.ShapeDtypeStruct((19, slab_len, band_width, height), jnp.float32)]
     if with_moments:
@@ -176,13 +193,15 @@
     return pl.pallas_call(
         functools.partial(step_kernel, with_moments),
         out_shape=tuple(out_shape),
-        in_specs=[pl.BlockSpec(memory_space=pltpu.SMEM), vmem, vmem, vmem],
+        in_specs=[pl.BlockSpec(memory_space=pltpu.SMEM)] + [vmem] * 6,
         out_specs=tuple([vmem] * len(out_shape)),
-        scratch_shapes=[pltpu.VMEM(extended.shape, jnp.float32)],
+        scratch_shapes=[
+            pltpu.VMEM((19, slab_len + 2, band_width + 2, height), jnp.float32)
+        ],
         cost_estimate=pl.CostEstimate(
-            flops=300 * solid_rim.size, transcendentals=0, bytes_accessed=12 * extended.size
+            flops=300 * solid_rim.size, transcendentals=0, bytes_accessed=12 * inner.size
         ),
-    )(strength, extended, discs, solid_rim)
+    )(strength, inner, low, high, rows, discs, solid_rim)
 
 
 def disc_count():
@@ -267,9 +286,9 @@
         total = flow + from_left[-1, 0, 0, :fans] + from_right[-1, 0, 0, :fans]
     for offset in sorted(set(step % count for step in range(-reach, reach + 1)) - {0, 1, count - 1}):
         total = total + lax.ppermute(flow, axis, [(i, (i + offset) % count) for i in range(count)])
-    extended = []
-    first = 0
-    for field, channel in zip(fields, channels):
+    extended = [(from_left[0 : channels[0]], from_right[0 : channels[0]])]
+    first = channels[0]
+    for field, channel in zip(fields[1:], channels[1:]):
         left = from_left[first : first + channel]
         right = from_right[first : first + channel]
         if dim == 1:
@@ -354,8 +373,10 @@
         if repeat == 0:
             fields.append(solid_flag.astype(jnp.float32)[None])
         fields, totals = rim_round(fields, partials, "len", 1, len_reach)
+        low, high = fields[0]
+        fields[0] = jnp.concatenate([low, populations, high], axis=1)
         fields, totals = rim_round(fields, totals, "band", 2, band_reach)
-        extended = fields[0]
+        rows = jnp.concatenate(fields[0], axis=2)
         rimmed = fields[1][0]
         if repeat == 0:
             solid_rim = fields[2][0]
@@ -365,7 +386,7 @@
             )
         strength = fan_gain * (jet_speed - totals / float(disc_count()))
         last = repeat == ITERS - 1
-        stepped = lattice_step(strength, extended, discs, solid_rim, not last)
+        stepped = lattice_step(strength, populations, low, high, rows, discs, solid_rim, not last)
         ahead_x = rimmed[2:, 0:band_width]
         behind_x = rimmed[:-2, 0:band_width]
         ahead_y = jnp.concatenate(

time: 83.8 us -> 80.7 us (0.963)
  waiting for transfers between devices: 17.1 us -> 10.4 us
  starting transfers between devices: 27.4 us -> 32.8 us
  other arithmetic: 16.3 us -> 13.8 us
    ppermute x6, starting transfers between devices: 10.1 us -> 15.6 us  [rim_round(): lax.ppermute(flow, axis, [(i, (i + offset) % count) for i in range(count)])]
    concatenate x4 -> x1, other arithmetic: 5.05 us -> 0.01 us  [rim_round(): extended.append(jnp.concatenate([field, left, right], axis=dim))]
    ppermute x3, waiting for transfers between devices: 8.39 us -> 3.6 us  [rim_round(): from_left = lax.ppermute(tail, axis, forward)]
    concatenate x0 -> x3, other arithmetic: none -> 2.6 us  [body(): rows = jnp.concatenate(fields[0], axis=2)]
    ppermute x6, waiting for transfers between devices: 4.22 us -> 2.61 us  [rim_round(): lax.ppermute(flow, axis, [(i, (i + offset) % count) for i in range(count)])]
  transfers between devices with their start and end apart: 15 -> 15, of which waited for: 9 -> 6; matrix products, arithmetic and copies ran while one was open for 1% -> 1% of each run, Pallas kernels for 0% -> 0%
where the time goes in v12:
time: 80.7 us; the launch traced here: 80.3 us
  starting transfers between devices  32.8 us (41%)
  Pallas kernels  17.7 us (22%)
  other arithmetic  13.8 us (17%)
  waiting for transfers between devices  10.4 us (13%)
  local copies, waits for them, and re-layouts  4.16 us (5%)
  between operations  1.26 us (2%)
    ppermute x6, starting transfers between devices, rim_round(): lax.ppermute(flow, axis, [(i, (i + offset) % count) for i in range(count)])  15.6 us
    pallas_call x3, Pallas kernels, lattice_step(): pl.pallas_call(functools.partial(step_kernel, with_moments), out_shape=tu...  15.2 us
    ppermute x3, starting transfers between devices, rim_round(): from_right = lax.ppermute(head, axis, backward)  13.1 us
    ppermute x3, waiting for transfers between devices, rim_round(): both = lax.ppermute(jnp.concatenate([tail, head], axis=0), axis, forward)  4.14 us
    ppermute x3, starting transfers between devices, rim_round(): from_left = lax.ppermute(tail, axis, forward)  3.91 us
    ppermute x3, waiting for transfers between devices, rim_round(): from_left = lax.ppermute(tail, axis, forward)  3.6 us
    ppermute x6, waiting for transfers between devices, rim_round(): lax.ppermute(flow, axis, [(i, (i + offset) % count) for i in range(count)])  2.61 us
    concatenate x3, other arithmetic, body(): rows = jnp.concatenate(fields[0], axis=2)  2.6 us
  transfers between devices with their start and end apart: 15, of which 6 were waited for; matrix products, arithmetic and copies ran while one was open for 1% of the time, Pallas kernels for 0%

profile of v12, /device:TPU:0, one launch (start us, length us, event | category | flops | bytes accessed | tf_op | source)
XLA Modules:
  0.0 80.3 jit_solution(18437625565664819795)
XLA Ops:
  0.6 0.8 slice_bitcast_fusion.12
  1.5 0.7 and_select_fusion
  2.2 0.1 add_compare_fusion
  2.4 0.1 fusion.28
  2.5 0.9 %convert_bitcast_fusion = (f32[1,8,16,128]{3,2,1,0:T(8,128)S(1)}, pred[8,16,128]{2,1,0:T(8,128)(4,1)S(1)}) fusion(s32[8,16,128]{2,1,0:T(8,128)} %param.34), kind=kLoop, calls=%fused_computation.69 | loop fusion | flops 32768 | bytes 147456 | tf_op jit(solution)/shard_map/broadcast_in_dim | solution.py:374
  3.4 0.9 %and_convert_fusion.1.discs_ref = f32[8,8,16,128]{3,2,1,0:T(8,128)} fusion(pred[8,16,128]{2,1,0:T(8,128)(4,1)S(1)} %not.3, pred[8,16,128]{2,1,0:T(8,128)(4,1)S(1)} %slice.654, pred[8,8]{1,0:T(8,128)(4,1)S(1)} %slice.548), kind=kLoop, calls=%fused_computation.1 | loop fusion | flops 393216 | bytes 557120 | tf_op jit(solution)/shard_map/convert_element_type | solution.py:368
  4.4 2.4 %shard_map.104 = (f32[3,8,16,128]{3,2,1,0:T(8,128)}, f32[8,16,128]{2,1,0:T(8,128)}) custom-call(f32[19,8,16,128]{3,2,1,0:T(8,128)} %inner_ref.1, f32[8,8,16,128]{3,2,1,0:T(8,128)} %and_convert_fusion.1.discs_ref), custom_call_target="tpu_custom_call" | custom-call | flops 983040 | bytes 1245184 | tf_op jit(solution)/shard_map/pallas_call | solution.py:167
  6.8 1.0 %reduce_sum.27 = f32[8]{0:T(128)S(1)} reduce(f32[8,16,128]{2,1,0:T(8,128)} %get-tuple-element.130, f32[]{:T(128)} %constant.273.clone.1), dimensions={1,2}, to_apply=%region_0.1 | reduce | flops 16376 | bytes 65572 | tf_op jit(solution)/shard_map/reduce_sum | solution.py:370
  7.8 3.0 %collective-permute-start.2 = (f32[8]{0:T(128)S(1)}, f32[8]{0:T(128)S(1)}, u32[]{:S(2)}, u32[]{:S(2)}) collective-permute-start(f32[8]{0:T(128)S(1)} %reduce_sum.27), channel_id=1, source_target_pairs={{0,4},{2,6},{4,8},{6,10},{8,12},{10,14},{12,16},{14,18},{16,20},{1... | collective-permute-start | bytes 104 | tf_op jit(solution)/shard_map/ppermute | solution.py:288
  10.8 3.1 %collective-permute-start.3 = (f32[8]{0:T(128)S(1)}, f32[8]{0:T(128)S(1)}, u32[]{:S(2)}, u32[]{:S(2)}) collective-permute-start(f32[8]{0:T(128)S(1)} %reduce_sum.27), channel_id=1, source_target_pairs={{0,28},{2,30},{4,0},{6,2},{8,4},{10,6},{12,8},{14,10},{16,12},{18,... | collective-permute-start | bytes 104 | tf_op jit(solution)/shard_map/ppermute | solution.py:288
  14.0 1.6 %collective-permute-start = (f32[22,1,16,128]{3,2,1,0:T(8,128)S(1)}, f32[22,1,16,128]{3,2,1,0:T(8,128)S(1)}, u32[]{:S(2)}, u32[]{:S(2)}) collective-permute-start(f32[22,1,16,128]{3,2,1,0:T(8,128)S(1)} %get-tuple-element.204), channel_id=1, source_target_pairs={{0,2},{2,4},{4,6},{6,8},{8,10},{10,12},{12,14},{14,16},{16,18},{18... | collective-permute-start | bytes 540680 | tf_op jit(solution)/shard_map/ppermute | solution.py:284
  15.6 4.0 %collective-permute-start.1 = (f32[22,1,16,128]{3,2,1,0:T(8,128)S(1)}, f32[22,1,16,128]{3,2,1,0:T(8,128)S(1)}, u32[]{:S(2)}, u32[]{:S(2)}) collective-permute-start(f32[22,1,16,128]{3,2,1,0:T(8,128)S(1)} %get-tuple-element.205), channel_id=1, source_target_pairs={{2,0},{4,2},{6,4},{8,6},{10,8},{12,10},{14,12},{16,14},{18,16},{20... | collective-permute-start | bytes 540680 | tf_op jit(solution)/shard_map/ppermute | solution.py:285
  19.8 0.1 broadcast_multiply_fusion
  19.9 0.2 fusion.2
  20.2 3.6 %collective-permute-done = f32[22,1,16,128]{3,2,1,0:T(8,128)S(1)} collective-permute-done((f32[22,1,16,128]{3,2,1,0:T(8,128)S(1)}, f32[22,1,16,128]{3,2,1,0:T(8,128)S(1)}, u32[]{:S(2)}, u32[]{:S(2)}) %collective-permute-start) | collective-permute-done | bytes 180256 | tf_op jit(solution)/shard_map/ppermute | solution.py:284
  23.8 0.1 maximum_dynamic-update-slice_fusion.2
  24.1 0.3 copy-done.6
  24.7 1.4 %collective-permute-done.4 = f32[44,10,1,128]{3,2,1,0:T(1,128)S(1)} collective-permute-done((f32[44,10,1,128]{3,2,1,0:T(1,128)S(1)}, f32[44,10,1,128]{3,2,1,0:T(1,128)S(1)}, u32[]{:S(2)}, u32[]{:S(2)}) %collective-permute-start.4) | collective-permute-done | bytes 225312 | tf_op jit(solution)/shard_map/ppermute | solution.py:279
  26.2 0.1 fusion.24
  26.3 1.1 %and_convert_fusion.discs_ref = f32[8,10,18,128]{3,2,1,0:T(8,128)} fusion(pred[10,18,128]{2,1,0:T(8,128)(4,1)S(1)} %maximum_compare_fusion, pred[8,18,128]{2,1,0:T(8,128)(4,1)S(1)} %add_compare_fusion, pred[8,10]{1,0:T(8,128)(4,1)S(1)} %fusion.28), kind=kLoop, calls=%fused_computation | loop fusion | flops 552960 | bytes 778832 | tf_op jit(solution)/shard_map/convert_element_type | solution.py:384
  27.5 0.7 maximum_bitcast_fusion.solid_ref
  28.2 0.9 %pad_maximum_fusion.4.rows_ref = f32[19,10,2,128]{3,2,1,0:T(2,128)} fusion(f32[19,10,1,128]{3,2,1,0:T(1,128)S(1)} %get-tuple-element.153, f32[19,10,1,128]{3,2,1,0:T(1,128)S(1)} %get-tuple-element.152), kind=kLoop, calls=%fused_computation.6 | loop fusion | flops 48640 | bytes 389120 | tf_op jit(solution)/shard_map/concatenate | solution.py:379
  29.0 0.6 fusion.57.strength_ref
  29.6 5.2 %shard_map.105 = (f32[19,8,16,128]{3,2,1,0:T(8,128)}, f32[3,8,16,128]{3,2,1,0:T(8,128)}, f32[8,16,128]{2,1,0:T(8,128)}) custom-call(f32[8]{0:T(128)} %fusion.57.strength_ref, f32[19,8,16,128]{3,2,1,0:T(8,128)} %inner_ref.1, f32[19,1,16,128]{3,2,1,0:T(8,128)} %copy-done.6, f32[19,1,16,128]{3,2,1,0:T(8,128)} %copy-done.7, ...), custom_call_target="tpu_custom_call" | custom-call | flops 6912000 | bytes 3735552 | tf_op jit(solution)/shard_map/pallas_call | solution.py:193
  34.8 1.1 %fusion.63 = (f32[19,1,16,128]{3,2,1,0:T(8,128)S(1)}, f32[19,1,16,128]{3,2,1,0:T(8,128)S(1)}) fusion(f32[19,8,16,128]{3,2,1,0:T(8,128)} %get-tuple-element.132.inner_ref), kind=kLoop, calls=%fused_computation.162 | loop fusion | bytes 622592 | tf_op jit(solution)/shard_map/slice | solution.py:270
  35.9 1.0 %reduce_sum.28 = f32[8]{0:T(128)S(1)} reduce(f32[8,16,128]{2,1,0:T(8,128)} %get-tuple-element.131, f32[]{:T(128)} %constant.273.clone.1), dimensions={1,2}, to_apply=%region_1.2 | reduce | flops 16376 | bytes 65572 | tf_op jit(solution)/shard_map/reduce_sum | solution.py:413
  37.0 1.7 %collective-permute-start.5 = (f32[21,1,16,128]{3,2,1,0:T(8,128)S(1)}, f32[21,1,16,128]{3,2,1,0:T(8,128)S(1)}, u32[]{:S(2)}, u32[]{:S(2)}) collective-permute-start(f32[21,1,16,128]{3,2,1,0:T(8,128)S(1)} %get-tuple-element.196), channel_id=1, source_target_pairs={{0,2},{2,4},{4,6},{6,8},{8,10},{10,12},{12,14},{14,16},{16,18},{18... | collective-permute-start | bytes 516104 | tf_op jit(solution)/shard_map/ppermute | solution.py:284
  38.7 4.0 %collective-permute-start.6 = (f32[21,1,16,128]{3,2,1,0:T(8,128)S(1)}, f32[21,1,16,128]{3,2,1,0:T(8,128)S(1)}, u32[]{:S(2)}, u32[]{:S(2)}) collective-permute-start(f32[21,1,16,128]{3,2,1,0:T(8,128)S(1)} %get-tuple-element.197), channel_id=1, source_target_pairs={{2,0},{4,2},{6,4},{8,6},{10,8},{12,10},{14,12},{16,14},{18,16},{20... | collective-permute-start | bytes 516104 | tf_op jit(solution)/shard_map/ppermute | solution.py:285
  42.6 4.7 %collective-permute-start.8 = (f32[8]{0:T(128)S(1)}, f32[8]{0:T(128)S(1)}, u32[]{:S(2)}, u32[]{:S(2)}) collective-permute-start(f32[8]{0:T(128)S(1)} %reduce_sum.28), channel_id=1, source_target_pairs={{0,28},{2,30},{4,0},{6,2},{8,4},{10,6},{12,8},{14,10},{16,12},{18,... | collective-permute-start | bytes 104 | tf_op jit(solution)/shard_map/ppermute | solution.py:288
  47.4 0.1 maximum_dynamic-update-slice_fusion.1
  47.6 1.3 %collective-permute-done.7 = f32[8]{0:T(128)S(1)} collective-permute-done((f32[8]{0:T(128)S(1)}, f32[8]{0:T(128)S(1)}, u32[]{:S(2)}, u32[]{:S(2)}) %collective-permute-start.7) | collective-permute-done | bytes 64 | tf_op jit(solution)/shard_map/ppermute | solution.py:288
  49.2 1.4 %collective-permute-done.9 = f32[42,10,1,128]{3,2,1,0:T(1,128)S(1)} collective-permute-done((f32[42,10,1,128]{3,2,1,0:T(1,128)S(1)}, f32[42,10,1,128]{3,2,1,0:T(1,128)S(1)}, u32[]{:S(2)}, u32[]{:S(2)}) %collective-permute-start.9) | collective-permute-done | bytes 215072 | tf_op jit(solution)/shard_map/ppermute | solution.py:279
  50.6 0.1 fusion.18
  50.8 0.9 %pad_maximum_fusion.5.rows_ref = f32[19,10,2,128]{3,2,1,0:T(2,128)} fusion(f32[19,10,1,128]{3,2,1,0:T(1,128)S(1)} %get-tuple-element.161, f32[19,10,1,128]{3,2,1,0:T(1,128)S(1)} %get-tuple-element.160), kind=kLoop, calls=%fused_computation.7 | loop fusion | flops 48640 | bytes 389120 | tf_op jit(solution)/shard_map/concatenate | solution.py:379
  51.7 0.6 fusion.58.strength_ref
  52.2 5.2 %shard_map.106 = (f32[19,8,16,128]{3,2,1,0:T(8,128)}, f32[3,8,16,128]{3,2,1,0:T(8,128)}, f32[8,16,128]{2,1,0:T(8,128)}) custom-call(f32[8]{0:T(128)} %fusion.58.strength_ref, f32[19,8,16,128]{3,2,1,0:T(8,128)} %get-tuple-element.132.inner_ref, f32[19,1,16,128]{3,2,1,0:T(8,128)} %copy-done.8, f32[19,1,16,128]{3,2,1,0:T(8,128)} %copy-done.9, ...), custom_call_target="tpu_custom_call" | custom-call | flops 6912000 | bytes 3735552 | tf_op jit(solution)/shard_map/pallas_call | solution.py:193
  57.4 1.1 %fusion.62 = (f32[19,1,16,128]{3,2,1,0:T(8,128)S(1)}, f32[19,1,16,128]{3,2,1,0:T(8,128)S(1)}) fusion(f32[19,8,16,128]{3,2,1,0:T(8,128)} %get-tuple-element.135.inner_ref), kind=kLoop, calls=%fused_computation.161 | loop fusion | bytes 622592 | tf_op jit(solution)/shard_map/slice | solution.py:270
  58.5 1.0 %reduce_sum.29 = f32[8]{0:T(128)S(1)} reduce(f32[8,16,128]{2,1,0:T(8,128)} %get-tuple-element.134, f32[]{:T(128)} %constant.273.clone.1), dimensions={1,2}, to_apply=%region_2.3 | reduce | flops 16376 | bytes 65572 | tf_op jit(solution)/shard_map/reduce_sum | solution.py:413
  59.6 0.6 collective-permute-start.10
  60.1 5.1 %collective-permute-start.11 = (f32[21,1,16,128]{3,2,1,0:T(8,128)S(1)}, f32[21,1,16,128]{3,2,1,0:T(8,128)S(1)}, u32[]{:S(2)}, u32[]{:S(2)}) collective-permute-start(f32[21,1,16,128]{3,2,1,0:T(8,128)S(1)} %get-tuple-element.195), channel_id=1, source_target_pairs={{2,0},{4,2},{6,4},{8,6},{10,8},{12,10},{14,12},{16,14},{18,16},{20... | collective-permute-start | bytes 516104 | tf_op jit(solution)/shard_map/ppermute | solution.py:285
  65.2 4.7 %collective-permute-start.13 = (f32[8]{0:T(128)S(1)}, f32[8]{0:T(128)S(1)}, u32[]{:S(2)}, u32[]{:S(2)}) collective-permute-start(f32[8]{0:T(128)S(1)} %reduce_sum.29), channel_id=1, source_target_pairs={{0,28},{2,30},{4,0},{6,2},{8,4},{10,6},{12,8},{14,10},{16,12},{18,... | collective-permute-start | bytes 104 | tf_op jit(solution)/shard_map/ppermute | solution.py:288
  70.0 0.1 maximum_dynamic-update-slice_fusion
  70.2 1.3 %collective-permute-done.12 = f32[8]{0:T(128)S(1)} collective-permute-done((f32[8]{0:T(128)S(1)}, f32[8]{0:T(128)S(1)}, u32[]{:S(2)}, u32[]{:S(2)}) %collective-permute-start.12) | collective-permute-done | bytes 64 | tf_op jit(solution)/shard_map/ppermute | solution.py:288
  71.8 1.4 %collective-permute-done.14 = f32[42,10,1,128]{3,2,1,0:T(1,128)S(1)} collective-permute-done((f32[42,10,1,128]{3,2,1,0:T(1,128)S(1)}, f32[42,10,1,128]{3,2,1,0:T(1,128)S(1)}, u32[]{:S(2)}, u32[]{:S(2)}) %collective-permute-start.14) | collective-permute-done | bytes 215072 | tf_op jit(solution)/shard_map/ppermute | solution.py:279
  73.2 0.9 %pad_maximum_fusion.6.rows_ref = f32[19,10,2,128]{3,2,1,0:T(2,128)} fusion(f32[19,10,1,128]{3,2,1,0:T(1,128)S(1)} %get-tuple-element.157, f32[19,10,1,128]{3,2,1,0:T(1,128)S(1)} %get-tuple-element.156), kind=kLoop, calls=%fused_computation.8 | loop fusion | flops 48640 | bytes 389120 | tf_op jit(solution)/shard_map/concatenate | solution.py:379
  74.1 0.5 fusion.59.strength_ref
  74.6 4.9 %shard_map.107 = f32[19,8,16,128]{3,2,1,0:T(8,128)} custom-call(f32[8]{0:T(128)} %fusion.59.strength_ref, f32[19,8,16,128]{3,2,1,0:T(8,128)} %get-tuple-element.135.inner_ref, f32[19,1,16,128]{3,2,1,0:T(8,128)} %copy-done.4, f32[19,1,16,128]{3,2,1,0:T(8,128)} %copy-done.5, f32[19,10,2,128]{3,2,1,0:T(2,128)} %pad_maximum_fusion.6.rows_ref, ...), custom_call_target="tpu_custom_call" | custom-call | flops 6912000 | bytes 3735552 | tf_op jit(solution)/shard_map/pallas_call | solution.py:193
  79.5 0.7 fusion.12
  (117 shorter events, 1.9 us)
Async XLA Ops:
  3.4 10.5 %copy-start = (f32[19,8,16,128]{3,2,1,0:T(8,128)S(1)}, f32[19,8,16,128]{3,2,1,0:T(8,128)}, u32[]{:S(2)}) copy-start(f32[19,8,16,128]{3,2,1,0:T(8,128)} %inner_ref.1) | copy-start | bytes 3735556
  4.4 9.6 %copy-start.3 = (f32[8,16,128]{2,1,0:T(8,128)S(1)}, f32[8,16,128]{2,1,0:T(8,128)}, u32[]{:S(2)}) copy-start(f32[8,16,128]{2,1,0:T(8,128)} %param.35) | copy-start | bytes 196612
  4.4 15.3 %copy-start.15 = (s32[16,3]{0,1:T(4,128)S(1)}, s32[16,3]{0,1:T(4,128)}, u32[]{:S(2)}) copy-start(s32[16,3]{0,1:T(4,128)} %param.39) | copy-start | bytes 580
  6.8 13.1 %copy-start.16 = (f32[16]{0:T(128)S(1)}, f32[16]{0:T(128)}, u32[]{:S(2)}) copy-start(f32[16]{0:T(128)} %param.40) | copy-start | bytes 196
  7.8 16.2 %collective-permute-start.2 = (f32[8]{0:T(128)S(1)}, f32[8]{0:T(128)S(1)}, u32[]{:S(2)}, u32[]{:S(2)}) collective-permute-start(f32[8]{0:T(128)S(1)} %reduce_sum.27), channel_id=1, source_target_pairs={{0,4},{2,6},{4,8},{6,10},{8,12},{10,14},{12,16},{14,18},{16,20},{1... | collective-permute-start | bytes 104 | tf_op jit(solution)/shard_map/ppermute | solution.py:288
  10.8 13.2 %collective-permute-start.3 = (f32[8]{0:T(128)S(1)}, f32[8]{0:T(128)S(1)}, u32[]{:S(2)}, u32[]{:S(2)}) collective-permute-start(f32[8]{0:T(128)S(1)} %reduce_sum.27), channel_id=1, source_target_pairs={{0,28},{2,30},{4,0},{6,2},{8,4},{10,6},{12,8},{14,10},{16,12},{18,... | collective-permute-start | bytes 104 | tf_op jit(solution)/shard_map/ppermute | solution.py:288
  14.0 9.8 %collective-permute-start = (f32[22,1,16,128]{3,2,1,0:T(8,128)S(1)}, f32[22,1,16,128]{3,2,1,0:T(8,128)S(1)}, u32[]{:S(2)}, u32[]{:S(2)}) collective-permute-start(f32[22,1,16,128]{3,2,1,0:T(8,128)S(1)} %get-tuple-element.204), channel_id=1, source_target_pairs={{0,2},{2,4},{4,6},{6,8},{8,10},{10,12},{12,14},{14,16},{16,18},{18... | collective-permute-start | bytes 540680 | tf_op jit(solution)/shard_map/ppermute | solution.py:284
  15.6 8.1 %collective-permute-start.1 = (f32[22,1,16,128]{3,2,1,0:T(8,128)S(1)}, f32[22,1,16,128]{3,2,1,0:T(8,128)S(1)}, u32[]{:S(2)}, u32[]{:S(2)}) collective-permute-start(f32[22,1,16,128]{3,2,1,0:T(8,128)S(1)} %get-tuple-element.205), channel_id=1, source_target_pairs={{2,0},{4,2},{6,4},{8,6},{10,8},{12,10},{14,12},{16,14},{18,16},{20... | collective-permute-start | bytes 540680 | tf_op jit(solution)/shard_map/ppermute | solution.py:285
  23.8 0.7 copy-start.6
  23.8 0.7 copy-start.7
  24.0 2.1 %copy-start.10 = (f32[3,8,16,128]{3,2,1,0:T(8,128)S(1)}, f32[3,8,16,128]{3,2,1,0:T(8,128)}, u32[]{:S(2)}) copy-start(f32[3,8,16,128]{3,2,1,0:T(8,128)} %get-tuple-element.133) | copy-start | bytes 589828
  24.5 1.5 %collective-permute-start.4 = (f32[44,10,1,128]{3,2,1,0:T(1,128)S(1)}, f32[44,10,1,128]{3,2,1,0:T(1,128)S(1)}, u32[]{:S(2)}, u32[]{:S(2)}) collective-permute-start(f32[44,10,1,128]{3,2,1,0:T(1,128)S(1)} %constant_dynamic-update-slice_fusion), channel_id=1, source_target_pairs={{0,1},{1,0},{2,3},{3,2},{4,5},{5,4},{6,7},{7,6},{8,9},{9,8},{10,11... | collective-permute-start | bytes 675848 | tf_op jit(solution)/shard_map/ppermute | solution.py:279
  26.3 2.8 %copy-start.13 = (f32[8]{0:T(128)S(1)}, f32[8]{0:T(128)}, u32[]{:S(2)}) copy-start(f32[8]{0:T(128)} %param.37) | copy-start | bytes 100
  26.3 2.8 %copy-start.14 = (f32[8]{0:T(128)S(1)}, f32[8]{0:T(128)}, u32[]{:S(2)}) copy-start(f32[8]{0:T(128)} %param.38) | copy-start | bytes 100
  34.8 12.6 %copy-start.2 = (f32[19,8,16,128]{3,2,1,0:T(8,128)S(1)}, f32[19,8,16,128]{3,2,1,0:T(8,128)}, u32[]{:S(2)}) copy-start(f32[19,8,16,128]{3,2,1,0:T(8,128)} %get-tuple-element.132.inner_ref) | copy-start | bytes 3735556
  37.0 10.4 %collective-permute-start.5 = (f32[21,1,16,128]{3,2,1,0:T(8,128)S(1)}, f32[21,1,16,128]{3,2,1,0:T(8,128)S(1)}, u32[]{:S(2)}, u32[]{:S(2)}) collective-permute-start(f32[21,1,16,128]{3,2,1,0:T(8,128)S(1)} %get-tuple-element.196), channel_id=1, source_target_pairs={{0,2},{2,4},{4,6},{6,8},{8,10},{10,12},{12,14},{14,16},{16,18},{18... | collective-permute-start | bytes 516104 | tf_op jit(solution)/shard_map/ppermute | solution.py:284
  38.7 8.7 %collective-permute-start.6 = (f32[21,1,16,128]{3,2,1,0:T(8,128)S(1)}, f32[21,1,16,128]{3,2,1,0:T(8,128)S(1)}, u32[]{:S(2)}, u32[]{:S(2)}) collective-permute-start(f32[21,1,16,128]{3,2,1,0:T(8,128)S(1)} %get-tuple-element.197), channel_id=1, source_target_pairs={{2,0},{4,2},{6,4},{8,6},{10,8},{12,10},{14,12},{16,14},{18,16},{20... | collective-permute-start | bytes 516104 | tf_op jit(solution)/shard_map/ppermute | solution.py:285
  42.6 6.2 %collective-permute-start.7 = (f32[8]{0:T(128)S(1)}, f32[8]{0:T(128)S(1)}, u32[]{:S(2)}, u32[]{:S(2)}) collective-permute-start(f32[8]{0:T(128)S(1)} %reduce_sum.28), channel_id=1, source_target_pairs={{0,4},{2,6},{4,8},{6,10},{8,12},{10,14},{12,16},{14,18},{16,20},{1... | collective-permute-start | bytes 104 | tf_op jit(solution)/shard_map/ppermute | solution.py:288
  42.6 6.2 %collective-permute-start.8 = (f32[8]{0:T(128)S(1)}, f32[8]{0:T(128)S(1)}, u32[]{:S(2)}, u32[]{:S(2)}) collective-permute-start(f32[8]{0:T(128)S(1)} %reduce_sum.28), channel_id=1, source_target_pairs={{0,28},{2,30},{4,0},{6,2},{8,4},{10,6},{12,8},{14,10},{16,12},{18,... | collective-permute-start | bytes 104 | tf_op jit(solution)/shard_map/ppermute | solution.py:288
  47.4 1.6 %copy-start.8 = (f32[19,1,16,128]{3,2,1,0:T(8,128)}, f32[19,1,16,128]{3,2,1,0:T(8,128)S(1)}, u32[]{:S(2)}) copy-start(f32[19,1,16,128]{3,2,1,0:T(8,128)S(1)} %slice.686.low_ref) | copy-start | bytes 466948
  47.4 1.6 %copy-start.9 = (f32[19,1,16,128]{3,2,1,0:T(8,128)}, f32[19,1,16,128]{3,2,1,0:T(8,128)S(1)}, u32[]{:S(2)}) copy-start(f32[19,1,16,128]{3,2,1,0:T(8,128)S(1)} %slice.687.high_ref) | copy-start | bytes 466948
  48.9 1.7 %copy-start.12 = (f32[3,8,16,128]{3,2,1,0:T(8,128)S(1)}, f32[3,8,16,128]{3,2,1,0:T(8,128)}, u32[]{:S(2)}) copy-start(f32[3,8,16,128]{3,2,1,0:T(8,128)} %get-tuple-element.136) | copy-start | bytes 589828
  49.0 1.5 %collective-permute-start.9 = (f32[42,10,1,128]{3,2,1,0:T(1,128)S(1)}, f32[42,10,1,128]{3,2,1,0:T(1,128)S(1)}, u32[]{:S(2)}, u32[]{:S(2)}) collective-permute-start(f32[42,10,1,128]{3,2,1,0:T(1,128)S(1)} %constant_dynamic-update-slice_fusion.6), channel_id=1, source_target_pairs={{0,1},{1,0},{2,3},{3,2},{4,5},{5,4},{6,7},{7,6},{8,9},{9,8},{10,11... | collective-permute-start | bytes 645128 | tf_op jit(solution)/shard_map/ppermute | solution.py:279
  57.4 12.6 %copy-start.1 = (f32[19,8,16,128]{3,2,1,0:T(8,128)S(1)}, f32[19,8,16,128]{3,2,1,0:T(8,128)}, u32[]{:S(2)}) copy-start(f32[19,8,16,128]{3,2,1,0:T(8,128)} %get-tuple-element.135.inner_ref) | copy-start | bytes 3735556
  59.6 10.4 %collective-permute-start.10 = (f32[21,1,16,128]{3,2,1,0:T(8,128)S(1)}, f32[21,1,16,128]{3,2,1,0:T(8,128)S(1)}, u32[]{:S(2)}, u32[]{:S(2)}) collective-permute-start(f32[21,1,16,128]{3,2,1,0:T(8,128)S(1)} %get-tuple-element.194), channel_id=1, source_target_pairs={{0,2},{2,4},{4,6},{6,8},{8,10},{10,12},{12,14},{14,16},{16,18},{18... | collective-permute-start | bytes 516104 | tf_op jit(solution)/shard_map/ppermute | solution.py:284
  60.1 9.9 %collective-permute-start.11 = (f32[21,1,16,128]{3,2,1,0:T(8,128)S(1)}, f32[21,1,16,128]{3,2,1,0:T(8,128)S(1)}, u32[]{:S(2)}, u32[]{:S(2)}) collective-permute-start(f32[21,1,16,128]{3,2,1,0:T(8,128)S(1)} %get-tuple-element.195), channel_id=1, source_target_pairs={{2,0},{4,2},{6,4},{8,6},{10,8},{12,10},{14,12},{16,14},{18,16},{20... | collective-permute-start | bytes 516104 | tf_op jit(solution)/shard_map/ppermute | solution.py:285
  65.2 6.2 %collective-permute-start.12 = (f32[8]{0:T(128)S(1)}, f32[8]{0:T(128)S(1)}, u32[]{:S(2)}, u32[]{:S(2)}) collective-permute-start(f32[8]{0:T(128)S(1)} %reduce_sum.29), channel_id=1, source_target_pairs={{0,4},{2,6},{4,8},{6,10},{8,12},{10,14},{12,16},{14,18},{16,20},{1... | collective-permute-start | bytes 104 | tf_op jit(solution)/shard_map/ppermute | solution.py:288
  65.2 6.2 %collective-permute-start.13 = (f32[8]{0:T(128)S(1)}, f32[8]{0:T(128)S(1)}, u32[]{:S(2)}, u32[]{:S(2)}) collective-permute-start(f32[8]{0:T(128)S(1)} %reduce_sum.29), channel_id=1, source_target_pairs={{0,28},{2,30},{4,0},{6,2},{8,4},{10,6},{12,8},{14,10},{16,12},{18,... | collective-permute-start | bytes 104 | tf_op jit(solution)/shard_map/ppermute | solution.py:288
  70.0 1.6 %copy-start.4 = (f32[19,1,16,128]{3,2,1,0:T(8,128)}, f32[19,1,16,128]{3,2,1,0:T(8,128)S(1)}, u32[]{:S(2)}) copy-start(f32[19,1,16,128]{3,2,1,0:T(8,128)S(1)} %slice.707.low_ref) | copy-start | bytes 466948
  70.0 1.6 %copy-start.5 = (f32[19,1,16,128]{3,2,1,0:T(8,128)}, f32[19,1,16,128]{3,2,1,0:T(8,128)S(1)}, u32[]{:S(2)}) copy-start(f32[19,1,16,128]{3,2,1,0:T(8,128)S(1)} %slice.708.high_ref) | copy-start | bytes 466948
  71.6 1.5 %collective-permute-start.14 = (f32[42,10,1,128]{3,2,1,0:T(1,128)S(1)}, f32[42,10,1,128]{3,2,1,0:T(1,128)S(1)}, u32[]{:S(2)}, u32[]{:S(2)}) collective-permute-start(f32[42,10,1,128]{3,2,1,0:T(1,128)S(1)} %constant_dynamic-update-slice_fusion.10), channel_id=1, source_target_pairs={{0,1},{1,0},{2,3},{3,2},{4,5},{5,4},{6,7},{7,6},{8,9},{9,8},{10,11... | collective-permute-start | bytes 645128 | tf_op jit(solution)/shard_map/ppermute | solution.py:279
  74.6 4.9 %copy-start.11 = (f32[3,8,16,128]{3,2,1,0:T(8,128)S(1)}, f32[3,8,16,128]{3,2,1,0:T(8,128)}, u32[]{:S(2)}) copy-start(f32[3,8,16,128]{3,2,1,0:T(8,128)} %get-tuple-element.137) | copy-start | bytes 589828

commit v13 on v12

--- a/solution.py
+++ b/solution.py
@@ -275,10 +275,11 @@
     tail = piece(fields[0].shape[dim] - 1)
     forward = [(i, (i + 1) % count) for i in range(count)]
     backward = [((i + 1) % count, i) for i in range(count)]
+    both = None
     if count == 2:
-        both = lax.ppermute(jnp.concatenate([tail, head], axis=0), axis, forward)
-        from_left = both[: tail.shape[0]]
-        from_right = both[tail.shape[0] :]
+        both = lax.ppermute(jnp.concatenate([tail, head], axis=dim), axis, forward)
+        from_left = lax.slice_in_dim(both, 0, 1, axis=dim)
+        from_right = lax.slice_in_dim(both, 1, 2, axis=dim)
         total = flow + from_left[-1, 0, 0, :fans]
     else:
         from_left = lax.ppermute(tail, axis, forward)
@@ -286,7 +287,8 @@
         total = flow + from_left[-1, 0, 0, :fans] + from_right[-1, 0, 0, :fans]
     for offset in sorted(set(step % count for step in range(-reach, reach + 1)) - {0, 1, count - 1}):
         total = total + lax.ppermute(flow, axis, [(i, (i + offset) % count) for i in range(count)])
-    extended = [(from_left[0 : channels[0]], from_right[0 : channels[0]])]
+    pair = None if both is None else both[0 : channels[0]]
+    extended = [(from_left[0 : channels[0]], from_right[0 : channels[0]], pair)]
     first = channels[0]
     for field, channel in zip(fields[1:], channels[1:]):
         left = from_left[first : first + channel]
@@ -373,10 +375,13 @@
         if repeat == 0:
             fields.append(solid_flag.astype(jnp.float32)[None])
         fields, totals = rim_round(fields, partials, "len", 1, len_reach)
-        low, high = fields[0]
+        low, high, _ = fields[0]
         fields[0] = jnp.concatenate([low, populations, high], axis=1)
         fields, totals = rim_round(fields, totals, "band", 2, band_reach)
-        rows = jnp.concatenate(fields[0], axis=2)
+        if fields[0][2] is None:
+            rows = jnp.concatenate(fields[0][:2], axis=2)
+        else:
+            rows = fields[0][2]
         rimmed = fields[1][0]
         if repeat == 0:
             solid_rim = fields[2][0]

time: 80.7 us -> 80 us (level)
  other arithmetic: 13.8 us -> 11.1 us
  local copies, waits for them, and re-layouts: 4.16 us -> 5.75 us
    concatenate x3, other arithmetic: 2.6 us -> 0.48 us  [rim_round(): both = lax.ppermute(jnp.concatenate([tail, head], axis=dim), axis, forward)]
    slice x9, local copies, waits for them, and re-layouts: 0.15 us -> 2.17 us  [the longest x3 2.1 us: rim_round(): pair = None if both is None else both[0:channels[0]]]
    slice x6 -> x7, local copies, waits for them, and re-layouts: 2.26 us -> 2.27 us  [piece(): lax.slice_in_dim(field, start, start + 1, axis=dim)]
where the time goes in v13:
time: 80 us; the launch traced here: 79.5 us
  starting transfers between devices  32.8 us (41%)
  Pallas kernels  17.7 us (22%)
  other arithmetic  11.1 us (14%)
  waiting for transfers between devices  10.8 us (14%)
  local copies, waits for them, and re-layouts  5.75 us (7%)
  between operations  1.23 us (2%)
    ppermute x6, starting transfers between devices, rim_round(): lax.ppermute(flow, axis, [(i, (i + offset) % count) for i in range(count)])  15.6 us
    pallas_call x3, Pallas kernels, lattice_step(): pl.pallas_call(functools.partial(step_kernel, with_moments), out_shape=tu...  15.3 us
    ppermute x3, starting transfers between devices, rim_round(): from_right = lax.ppermute(head, axis, backward)  13.6 us
    ppermute x3, waiting for transfers between devices, rim_round(): both = lax.ppermute(jnp.concatenate([tail, head], axis=dim), axis, forward)  4.14 us
    ppermute x3, waiting for transfers between devices, rim_round(): from_left = lax.ppermute(tail, axis, forward)  3.58 us
    ppermute x3, starting transfers between devices, rim_round(): from_left = lax.ppermute(tail, axis, forward)  3.4 us
    ppermute x6, waiting for transfers between devices, rim_round(): lax.ppermute(flow, axis, [(i, (i + offset) % count) for i in range(count)])  3.04 us
    pallas_call x1, Pallas kernels, first_moments(): pl.pallas_call(lambda populations_ref, discs_ref, velocity_ref, flow_ref:...  2.42 us
  transfers between devices with their start and end apart: 15, of which 6 were waited for; matrix products, arithmetic and copies ran while one was open for 1% of the time, Pallas kernels for 0%

profile of v13, /device:TPU:0, one launch (start us, length us, event | category | flops | bytes accessed | tf_op | source)
XLA Modules:
  0.0 79.5 jit_solution(12606909255774973250)
XLA Ops:
  0.6 0.8 %slice_bitcast_fusion.12 = (s32[8]{0:T(128)S(1)}, s32[8]{0:T(128)S(1)}, s32[8]{0:T(128)S(1)}) fusion(s32[8,3]{0,1:T(4,128)} %param.36), kind=kLoop, calls=%fused_computation.160 | loop fusion | bytes 192 | tf_op jit(solution)/shard_map/sub | solution.py:354
  1.5 0.7 and_select_fusion
  2.2 0.1 add_compare_fusion
  2.4 0.1 fusion.42
  2.5 0.9 %convert_bitcast_fusion = (f32[1,8,16,128]{3,2,1,0:T(8,128)S(1)}, pred[8,16,128]{2,1,0:T(8,128)(4,1)S(1)}) fusion(s32[8,16,128]{2,1,0:T(8,128)} %param.34), kind=kLoop, calls=%fused_computation.95 | loop fusion | flops 32768 | bytes 147456 | tf_op jit(solution)/shard_map/broadcast_in_dim | solution.py:376
  3.4 0.9 %and_convert_fusion.1.discs_ref = f32[8,8,16,128]{3,2,1,0:T(8,128)} fusion(pred[8,16,128]{2,1,0:T(8,128)(4,1)S(1)} %not.3, pred[8,16,128]{2,1,0:T(8,128)(4,1)S(1)} %slice.628, pred[8,8]{1,0:T(8,128)(4,1)S(1)} %slice.529), kind=kLoop, calls=%fused_computation.1 | loop fusion | flops 393216 | bytes 557120 | tf_op jit(solution)/shard_map/convert_element_type | solution.py:370
  4.4 2.4 %shard_map.104 = (f32[3,8,16,128]{3,2,1,0:T(8,128)}, f32[8,16,128]{2,1,0:T(8,128)}) custom-call(f32[19,8,16,128]{3,2,1,0:T(8,128)} %inner_ref.1, f32[8,8,16,128]{3,2,1,0:T(8,128)} %and_convert_fusion.1.discs_ref), custom_call_target="tpu_custom_call" | custom-call | flops 983040 | bytes 1245184 | tf_op jit(solution)/shard_map/pallas_call | solution.py:167
  6.8 1.0 %reduce_sum.27 = f32[8]{0:T(128)S(1)} reduce(f32[8,16,128]{2,1,0:T(8,128)} %get-tuple-element.130, f32[]{:T(128)} %constant.273.clone.1), dimensions={1,2}, to_apply=%region_0.1 | reduce | flops 16376 | bytes 65572 | tf_op jit(solution)/shard_map/reduce_sum | solution.py:372
  7.8 3.0 %collective-permute-start.2 = (f32[8]{0:T(128)S(1)}, f32[8]{0:T(128)S(1)}, u32[]{:S(2)}, u32[]{:S(2)}) collective-permute-start(f32[8]{0:T(128)S(1)} %reduce_sum.27), channel_id=1, source_target_pairs={{0,4},{2,6},{4,8},{6,10},{8,12},{10,14},{12,16},{14,18},{16,20},{1... | collective-permute-start | bytes 104 | tf_op jit(solution)/shard_map/ppermute | solution.py:289
  10.8 3.1 %collective-permute-start.3 = (f32[8]{0:T(128)S(1)}, f32[8]{0:T(128)S(1)}, u32[]{:S(2)}, u32[]{:S(2)}) collective-permute-start(f32[8]{0:T(128)S(1)} %reduce_sum.27), channel_id=1, source_target_pairs={{0,28},{2,30},{4,0},{6,2},{8,4},{10,6},{12,8},{14,10},{16,12},{18,... | collective-permute-start | bytes 104 | tf_op jit(solution)/shard_map/ppermute | solution.py:289
  14.0 1.6 %collective-permute-start = (f32[22,1,16,128]{3,2,1,0:T(8,128)S(1)}, f32[22,1,16,128]{3,2,1,0:T(8,128)S(1)}, u32[]{:S(2)}, u32[]{:S(2)}) collective-permute-start(f32[22,1,16,128]{3,2,1,0:T(8,128)S(1)} %get-tuple-element.193), channel_id=1, source_target_pairs={{0,2},{2,4},{4,6},{6,8},{8,10},{10,12},{12,14},{14,16},{16,18},{18... | collective-permute-start | bytes 540680 | tf_op jit(solution)/shard_map/ppermute | solution.py:285
  15.6 4.0 %collective-permute-start.1 = (f32[22,1,16,128]{3,2,1,0:T(8,128)S(1)}, f32[22,1,16,128]{3,2,1,0:T(8,128)S(1)}, u32[]{:S(2)}, u32[]{:S(2)}) collective-permute-start(f32[22,1,16,128]{3,2,1,0:T(8,128)S(1)} %get-tuple-element.194), channel_id=1, source_target_pairs={{2,0},{4,2},{6,4},{8,6},{10,8},{12,10},{14,12},{16,14},{18,16},{20... | collective-permute-start | bytes 540680 | tf_op jit(solution)/shard_map/ppermute | solution.py:286
  19.8 0.1 broadcast_multiply_fusion
  19.9 0.2 fusion.19
  20.2 3.6 %collective-permute-done = f32[22,1,16,128]{3,2,1,0:T(8,128)S(1)} collective-permute-done((f32[22,1,16,128]{3,2,1,0:T(8,128)S(1)}, f32[22,1,16,128]{3,2,1,0:T(8,128)S(1)}, u32[]{:S(2)}, u32[]{:S(2)}) %collective-permute-start) | collective-permute-done | bytes 180256 | tf_op jit(solution)/shard_map/ppermute | solution.py:285
  23.9 0.2 fusion.3
  24.2 0.1 fusion.93
  24.2 1.4 %collective-permute-done.4 = f32[22,10,2,128]{3,2,1,0:T(2,128)S(1)} collective-permute-done((f32[22,10,2,128]{3,2,1,0:T(2,128)S(1)}, f32[22,10,2,128]{3,2,1,0:T(2,128)S(1)}, u32[]{:S(2)}, u32[]{:S(2)}) %collective-permute-start.4) | collective-permute-done | bytes 225312 | tf_op jit(solution)/shard_map/ppermute | solution.py:280
  25.7 0.1 fusion.38
  25.9 0.6 maximum_bitcast_fusion.solid_ref
  26.5 1.1 %and_convert_fusion.discs_ref = f32[8,10,18,128]{3,2,1,0:T(8,128)} fusion(pred[10,18,128]{2,1,0:T(8,128)(4,1)S(1)} %maximum_compare_fusion, pred[8,18,128]{2,1,0:T(8,128)(4,1)S(1)} %add_compare_fusion, pred[8,10]{1,0:T(8,128)(4,1)S(1)} %fusion.42), kind=kLoop, calls=%fused_computation | loop fusion | flops 552960 | bytes 778832 | tf_op jit(solution)/shard_map/convert_element_type | solution.py:389
  27.7 0.7 slice.644.rows_ref
  28.4 0.6 fusion.71.strength_ref
  29.0 5.2 %shard_map.105 = (f32[19,8,16,128]{3,2,1,0:T(8,128)}, f32[3,8,16,128]{3,2,1,0:T(8,128)}, f32[8,16,128]{2,1,0:T(8,128)}) custom-call(f32[8]{0:T(128)} %fusion.71.strength_ref, f32[19,8,16,128]{3,2,1,0:T(8,128)} %inner_ref.1, f32[19,1,16,128]{3,2,1,0:T(8,128)} %copy-done.6, f32[19,1,16,128]{3,2,1,0:T(8,128)} %copy-done.7, f32[19,10,2,128]{3,2,1,0:T(2,128)} %slice.644.rows_ref, ...), custom_call_target="tpu_custom_call" | custom-call | flops 6912000 | bytes 3735552 | tf_op jit(solution)/shard_map/pallas_call | solution.py:193
  34.1 1.1 %fusion.77 = (f32[19,1,16,128]{3,2,1,0:T(8,128)S(1)}, f32[19,1,16,128]{3,2,1,0:T(8,128)S(1)}) fusion(f32[19,8,16,128]{3,2,1,0:T(8,128)} %get-tuple-element.132.inner_ref), kind=kLoop, calls=%fused_computation.169 | loop fusion | bytes 622592 | tf_op jit(solution)/shard_map/slice | solution.py:270
  35.3 1.0 %reduce_sum.28 = f32[8]{0:T(128)S(1)} reduce(f32[8,16,128]{2,1,0:T(8,128)} %get-tuple-element.131, f32[]{:T(128)} %constant.273.clone.1), dimensions={1,2}, to_apply=%region_1.2 | reduce | flops 16376 | bytes 65572 | tf_op jit(solution)/shard_map/reduce_sum | solution.py:418
  36.3 1.7 %collective-permute-start.5 = (f32[21,1,16,128]{3,2,1,0:T(8,128)S(1)}, f32[21,1,16,128]{3,2,1,0:T(8,128)S(1)}, u32[]{:S(2)}, u32[]{:S(2)}) collective-permute-start(f32[21,1,16,128]{3,2,1,0:T(8,128)S(1)} %get-tuple-element.185), channel_id=1, source_target_pairs={{0,2},{2,4},{4,6},{6,8},{8,10},{10,12},{12,14},{14,16},{16,18},{18... | collective-permute-start | bytes 516104 | tf_op jit(solution)/shard_map/ppermute | solution.py:285
  38.0 4.0 %collective-permute-start.6 = (f32[21,1,16,128]{3,2,1,0:T(8,128)S(1)}, f32[21,1,16,128]{3,2,1,0:T(8,128)S(1)}, u32[]{:S(2)}, u32[]{:S(2)}) collective-permute-start(f32[21,1,16,128]{3,2,1,0:T(8,128)S(1)} %get-tuple-element.186), channel_id=1, source_target_pairs={{2,0},{4,2},{6,4},{8,6},{10,8},{12,10},{14,12},{16,14},{18,16},{20... | collective-permute-start | bytes 516104 | tf_op jit(solution)/shard_map/ppermute | solution.py:286
  42.0 4.7 %collective-permute-start.8 = (f32[8]{0:T(128)S(1)}, f32[8]{0:T(128)S(1)}, u32[]{:S(2)}, u32[]{:S(2)}) collective-permute-start(f32[8]{0:T(128)S(1)} %reduce_sum.28), channel_id=1, source_target_pairs={{0,28},{2,30},{4,0},{6,2},{8,4},{10,6},{12,8},{14,10},{16,12},{18,... | collective-permute-start | bytes 104 | tf_op jit(solution)/shard_map/ppermute | solution.py:289
  46.7 1.5 %collective-permute-done.7 = f32[8]{0:T(128)S(1)} collective-permute-done((f32[8]{0:T(128)S(1)}, f32[8]{0:T(128)S(1)}, u32[]{:S(2)}, u32[]{:S(2)}) %collective-permute-start.7) | collective-permute-done | bytes 64 | tf_op jit(solution)/shard_map/ppermute | solution.py:289
  48.3 0.2 fusion.14
  48.6 0.1 fusion.91
  48.7 1.4 %collective-permute-done.9 = f32[21,10,2,128]{3,2,1,0:T(2,128)S(1)} collective-permute-done((f32[21,10,2,128]{3,2,1,0:T(2,128)S(1)}, f32[21,10,2,128]{3,2,1,0:T(2,128)S(1)}, u32[]{:S(2)}, u32[]{:S(2)}) %collective-permute-start.9) | collective-permute-done | bytes 215072 | tf_op jit(solution)/shard_map/ppermute | solution.py:280
  50.1 0.1 fusion.32
  50.3 0.7 slice.662.rows_ref
  51.0 0.5 fusion.72.strength_ref
  51.5 5.2 %shard_map.106 = (f32[19,8,16,128]{3,2,1,0:T(8,128)}, f32[3,8,16,128]{3,2,1,0:T(8,128)}, f32[8,16,128]{2,1,0:T(8,128)}) custom-call(f32[8]{0:T(128)} %fusion.72.strength_ref, f32[19,8,16,128]{3,2,1,0:T(8,128)} %get-tuple-element.132.inner_ref, f32[19,1,16,128]{3,2,1,0:T(8,128)} %copy-done.8, f32[19,1,16,128]{3,2,1,0:T(8,128)} %copy-done.9, ...), custom_call_target="tpu_custom_call" | custom-call | flops 6912000 | bytes 3735552 | tf_op jit(solution)/shard_map/pallas_call | solution.py:193
  56.7 1.1 %fusion.76 = (f32[19,1,16,128]{3,2,1,0:T(8,128)S(1)}, f32[19,1,16,128]{3,2,1,0:T(8,128)S(1)}) fusion(f32[19,8,16,128]{3,2,1,0:T(8,128)} %get-tuple-element.135.inner_ref), kind=kLoop, calls=%fused_computation.168 | loop fusion | bytes 622592 | tf_op jit(solution)/shard_map/slice | solution.py:270
  57.8 1.0 %reduce_sum.29 = f32[8]{0:T(128)S(1)} reduce(f32[8,16,128]{2,1,0:T(8,128)} %get-tuple-element.134, f32[]{:T(128)} %constant.273.clone.1), dimensions={1,2}, to_apply=%region_2.3 | reduce | flops 16376 | bytes 65572 | tf_op jit(solution)/shard_map/reduce_sum | solution.py:418
  58.9 5.6 %collective-permute-start.11 = (f32[21,1,16,128]{3,2,1,0:T(8,128)S(1)}, f32[21,1,16,128]{3,2,1,0:T(8,128)S(1)}, u32[]{:S(2)}, u32[]{:S(2)}) collective-permute-start(f32[21,1,16,128]{3,2,1,0:T(8,128)S(1)} %get-tuple-element.184), channel_id=1, source_target_pairs={{2,0},{4,2},{6,4},{8,6},{10,8},{12,10},{14,12},{16,14},{18,16},{20... | collective-permute-start | bytes 516104 | tf_op jit(solution)/shard_map/ppermute | solution.py:286
  64.5 4.7 %collective-permute-start.13 = (f32[8]{0:T(128)S(1)}, f32[8]{0:T(128)S(1)}, u32[]{:S(2)}, u32[]{:S(2)}) collective-permute-start(f32[8]{0:T(128)S(1)} %reduce_sum.29), channel_id=1, source_target_pairs={{0,28},{2,30},{4,0},{6,2},{8,4},{10,6},{12,8},{14,10},{16,12},{18,... | collective-permute-start | bytes 104 | tf_op jit(solution)/shard_map/ppermute | solution.py:289
  69.3 1.5 %collective-permute-done.12 = f32[8]{0:T(128)S(1)} collective-permute-done((f32[8]{0:T(128)S(1)}, f32[8]{0:T(128)S(1)}, u32[]{:S(2)}, u32[]{:S(2)}) %collective-permute-start.12) | collective-permute-done | bytes 64 | tf_op jit(solution)/shard_map/ppermute | solution.py:289
  70.9 0.2 fusion.9
  71.2 1.4 %collective-permute-done.14 = f32[21,10,2,128]{3,2,1,0:T(2,128)S(1)} collective-permute-done((f32[21,10,2,128]{3,2,1,0:T(2,128)S(1)}, f32[21,10,2,128]{3,2,1,0:T(2,128)S(1)}, u32[]{:S(2)}, u32[]{:S(2)}) %collective-permute-start.14) | collective-permute-done | bytes 215072 | tf_op jit(solution)/shard_map/ppermute | solution.py:280
  72.7 0.7 slice.681.rows_ref
  73.4 0.5 fusion.73.strength_ref
  73.9 4.9 %shard_map.107 = f32[19,8,16,128]{3,2,1,0:T(8,128)} custom-call(f32[8]{0:T(128)} %fusion.73.strength_ref, f32[19,8,16,128]{3,2,1,0:T(8,128)} %get-tuple-element.135.inner_ref, f32[19,1,16,128]{3,2,1,0:T(8,128)} %copy-done.4, f32[19,1,16,128]{3,2,1,0:T(8,128)} %copy-done.5, f32[19,10,2,128]{3,2,1,0:T(2,128)} %slice.681.rows_ref, ...), custom_call_target="tpu_custom_call" | custom-call | flops 6912000 | bytes 3735552 | tf_op jit(solution)/shard_map/pallas_call | solution.py:193
  78.8 0.7 fusion.26
  (101 shorter events, 1.3 us)
Async XLA Ops:
  3.4 10.5 %copy-start = (f32[19,8,16,128]{3,2,1,0:T(8,128)S(1)}, f32[19,8,16,128]{3,2,1,0:T(8,128)}, u32[]{:S(2)}) copy-start(f32[19,8,16,128]{3,2,1,0:T(8,128)} %inner_ref.1) | copy-start | bytes 3735556
  4.4 9.6 %copy-start.3 = (f32[8,16,128]{2,1,0:T(8,128)S(1)}, f32[8,16,128]{2,1,0:T(8,128)}, u32[]{:S(2)}) copy-start(f32[8,16,128]{2,1,0:T(8,128)} %param.35) | copy-start | bytes 196612
  4.4 15.3 %copy-start.15 = (s32[16,3]{0,1:T(4,128)S(1)}, s32[16,3]{0,1:T(4,128)}, u32[]{:S(2)}) copy-start(s32[16,3]{0,1:T(4,128)} %param.39) | copy-start | bytes 580
  6.8 13.1 %copy-start.16 = (f32[16]{0:T(128)S(1)}, f32[16]{0:T(128)}, u32[]{:S(2)}) copy-start(f32[16]{0:T(128)} %param.40) | copy-start | bytes 196
  7.8 12.4 %collective-permute-start.2 = (f32[8]{0:T(128)S(1)}, f32[8]{0:T(128)S(1)}, u32[]{:S(2)}, u32[]{:S(2)}) collective-permute-start(f32[8]{0:T(128)S(1)} %reduce_sum.27), channel_id=1, source_target_pairs={{0,4},{2,6},{4,8},{6,10},{8,12},{10,14},{12,16},{14,18},{16,20},{1... | collective-permute-start | bytes 104 | tf_op jit(solution)/shard_map/ppermute | solution.py:289
  10.8 9.4 %collective-permute-start.3 = (f32[8]{0:T(128)S(1)}, f32[8]{0:T(128)S(1)}, u32[]{:S(2)}, u32[]{:S(2)}) collective-permute-start(f32[8]{0:T(128)S(1)} %reduce_sum.27), channel_id=1, source_target_pairs={{0,28},{2,30},{4,0},{6,2},{8,4},{10,6},{12,8},{14,10},{16,12},{18,... | collective-permute-start | bytes 104 | tf_op jit(solution)/shard_map/ppermute | solution.py:289
  14.0 9.8 %collective-permute-start = (f32[22,1,16,128]{3,2,1,0:T(8,128)S(1)}, f32[22,1,16,128]{3,2,1,0:T(8,128)S(1)}, u32[]{:S(2)}, u32[]{:S(2)}) collective-permute-start(f32[22,1,16,128]{3,2,1,0:T(8,128)S(1)} %get-tuple-element.193), channel_id=1, source_target_pairs={{0,2},{2,4},{4,6},{6,8},{8,10},{10,12},{12,14},{14,16},{16,18},{18... | collective-permute-start | bytes 540680 | tf_op jit(solution)/shard_map/ppermute | solution.py:285
  15.6 8.1 %collective-permute-start.1 = (f32[22,1,16,128]{3,2,1,0:T(8,128)S(1)}, f32[22,1,16,128]{3,2,1,0:T(8,128)S(1)}, u32[]{:S(2)}, u32[]{:S(2)}) collective-permute-start(f32[22,1,16,128]{3,2,1,0:T(8,128)S(1)} %get-tuple-element.194), channel_id=1, source_target_pairs={{2,0},{4,2},{6,4},{8,6},{10,8},{12,10},{14,12},{16,14},{18,16},{20... | collective-permute-start | bytes 540680 | tf_op jit(solution)/shard_map/ppermute | solution.py:286
  23.9 1.8 %copy-start.6 = (f32[19,1,16,128]{3,2,1,0:T(8,128)}, f32[19,1,16,128]{3,2,1,0:T(8,128)S(1)}, u32[]{:S(2)}) copy-start(f32[19,1,16,128]{3,2,1,0:T(8,128)S(1)} %slice.635.low_ref) | copy-start | bytes 466948
  23.9 1.8 %copy-start.7 = (f32[19,1,16,128]{3,2,1,0:T(8,128)}, f32[19,1,16,128]{3,2,1,0:T(8,128)S(1)}, u32[]{:S(2)}) copy-start(f32[19,1,16,128]{3,2,1,0:T(8,128)S(1)} %slice.636.high_ref) | copy-start | bytes 466948
  23.9 1.8 %copy-start.10 = (f32[3,8,16,128]{3,2,1,0:T(8,128)S(1)}, f32[3,8,16,128]{3,2,1,0:T(8,128)}, u32[]{:S(2)}) copy-start(f32[3,8,16,128]{3,2,1,0:T(8,128)} %get-tuple-element.133) | copy-start | bytes 589828
  24.1 1.5 %collective-permute-start.4 = (f32[22,10,2,128]{3,2,1,0:T(2,128)S(1)}, f32[22,10,2,128]{3,2,1,0:T(2,128)S(1)}, u32[]{:S(2)}, u32[]{:S(2)}) collective-permute-start(f32[22,10,2,128]{3,2,1,0:T(2,128)S(1)} %fusion.3), channel_id=1, source_target_pairs={{0,1},{1,0},{2,3},{3,2},{4,5},{5,4},{6,7},{7,6},{8,9},{9,8},{10,11... | collective-permute-start | bytes 675848 | tf_op jit(solution)/shard_map/ppermute | solution.py:280
  25.7 2.7 %copy-start.13 = (f32[8]{0:T(128)S(1)}, f32[8]{0:T(128)}, u32[]{:S(2)}) copy-start(f32[8]{0:T(128)} %param.37) | copy-start | bytes 100
  25.7 2.7 %copy-start.14 = (f32[8]{0:T(128)S(1)}, f32[8]{0:T(128)}, u32[]{:S(2)}) copy-start(f32[8]{0:T(128)} %param.38) | copy-start | bytes 100
  34.1 14.2 %copy-start.1 = (f32[19,8,16,128]{3,2,1,0:T(8,128)S(1)}, f32[19,8,16,128]{3,2,1,0:T(8,128)}, u32[]{:S(2)}) copy-start(f32[19,8,16,128]{3,2,1,0:T(8,128)} %get-tuple-element.132.inner_ref) | copy-start | bytes 3735556
  36.3 11.9 %collective-permute-start.5 = (f32[21,1,16,128]{3,2,1,0:T(8,128)S(1)}, f32[21,1,16,128]{3,2,1,0:T(8,128)S(1)}, u32[]{:S(2)}, u32[]{:S(2)}) collective-permute-start(f32[21,1,16,128]{3,2,1,0:T(8,128)S(1)} %get-tuple-element.185), channel_id=1, source_target_pairs={{0,2},{2,4},{4,6},{6,8},{8,10},{10,12},{12,14},{14,16},{16,18},{18... | collective-permute-start | bytes 516104 | tf_op jit(solution)/shard_map/ppermute | solution.py:285
  38.0 10.2 %collective-permute-start.6 = (f32[21,1,16,128]{3,2,1,0:T(8,128)S(1)}, f32[21,1,16,128]{3,2,1,0:T(8,128)S(1)}, u32[]{:S(2)}, u32[]{:S(2)}) collective-permute-start(f32[21,1,16,128]{3,2,1,0:T(8,128)S(1)} %get-tuple-element.186), channel_id=1, source_target_pairs={{2,0},{4,2},{6,4},{8,6},{10,8},{12,10},{14,12},{16,14},{18,16},{20... | collective-permute-start | bytes 516104 | tf_op jit(solution)/shard_map/ppermute | solution.py:286
  42.0 6.2 %collective-permute-start.7 = (f32[8]{0:T(128)S(1)}, f32[8]{0:T(128)S(1)}, u32[]{:S(2)}, u32[]{:S(2)}) collective-permute-start(f32[8]{0:T(128)S(1)} %reduce_sum.28), channel_id=1, source_target_pairs={{0,4},{2,6},{4,8},{6,10},{8,12},{10,14},{12,16},{14,18},{16,20},{1... | collective-permute-start | bytes 104 | tf_op jit(solution)/shard_map/ppermute | solution.py:289
  42.0 6.2 %collective-permute-start.8 = (f32[8]{0:T(128)S(1)}, f32[8]{0:T(128)S(1)}, u32[]{:S(2)}, u32[]{:S(2)}) collective-permute-start(f32[8]{0:T(128)S(1)} %reduce_sum.28), channel_id=1, source_target_pairs={{0,28},{2,30},{4,0},{6,2},{8,4},{10,6},{12,8},{14,10},{16,12},{18,... | collective-permute-start | bytes 104 | tf_op jit(solution)/shard_map/ppermute | solution.py:289
  48.3 1.8 %copy-start.8 = (f32[19,1,16,128]{3,2,1,0:T(8,128)}, f32[19,1,16,128]{3,2,1,0:T(8,128)S(1)}, u32[]{:S(2)}) copy-start(f32[19,1,16,128]{3,2,1,0:T(8,128)S(1)} %slice.657.low_ref) | copy-start | bytes 466948
  48.3 1.8 %copy-start.9 = (f32[19,1,16,128]{3,2,1,0:T(8,128)}, f32[19,1,16,128]{3,2,1,0:T(8,128)S(1)}, u32[]{:S(2)}) copy-start(f32[19,1,16,128]{3,2,1,0:T(8,128)S(1)} %slice.658.high_ref) | copy-start | bytes 466948
  48.3 1.8 %copy-start.12 = (f32[3,8,16,128]{3,2,1,0:T(8,128)S(1)}, f32[3,8,16,128]{3,2,1,0:T(8,128)}, u32[]{:S(2)}) copy-start(f32[3,8,16,128]{3,2,1,0:T(8,128)} %get-tuple-element.136) | copy-start | bytes 589828
  48.5 1.5 %collective-permute-start.9 = (f32[21,10,2,128]{3,2,1,0:T(2,128)S(1)}, f32[21,10,2,128]{3,2,1,0:T(2,128)S(1)}, u32[]{:S(2)}, u32[]{:S(2)}) collective-permute-start(f32[21,10,2,128]{3,2,1,0:T(2,128)S(1)} %fusion.14), channel_id=1, source_target_pairs={{0,1},{1,0},{2,3},{3,2},{4,5},{5,4},{6,7},{7,6},{8,9},{9,8},{10,11... | collective-permute-start | bytes 645128 | tf_op jit(solution)/shard_map/ppermute | solution.py:280
  56.7 14.2 %copy-start.2 = (f32[19,8,16,128]{3,2,1,0:T(8,128)S(1)}, f32[19,8,16,128]{3,2,1,0:T(8,128)}, u32[]{:S(2)}) copy-start(f32[19,8,16,128]{3,2,1,0:T(8,128)} %get-tuple-element.135.inner_ref) | copy-start | bytes 3735556
  58.9 11.9 %collective-permute-start.10 = (f32[21,1,16,128]{3,2,1,0:T(8,128)S(1)}, f32[21,1,16,128]{3,2,1,0:T(8,128)S(1)}, u32[]{:S(2)}, u32[]{:S(2)}) collective-permute-start(f32[21,1,16,128]{3,2,1,0:T(8,128)S(1)} %get-tuple-element.183), channel_id=1, source_target_pairs={{0,2},{2,4},{4,6},{6,8},{8,10},{10,12},{12,14},{14,16},{16,18},{18... | collective-permute-start | bytes 516104 | tf_op jit(solution)/shard_map/ppermute | solution.py:285
  58.9 11.9 %collective-permute-start.11 = (f32[21,1,16,128]{3,2,1,0:T(8,128)S(1)}, f32[21,1,16,128]{3,2,1,0:T(8,128)S(1)}, u32[]{:S(2)}, u32[]{:S(2)}) collective-permute-start(f32[21,1,16,128]{3,2,1,0:T(8,128)S(1)} %get-tuple-element.184), channel_id=1, source_target_pairs={{2,0},{4,2},{6,4},{8,6},{10,8},{12,10},{14,12},{16,14},{18,16},{20... | collective-permute-start | bytes 516104 | tf_op jit(solution)/shard_map/ppermute | solution.py:286
  64.5 6.2 %collective-permute-start.12 = (f32[8]{0:T(128)S(1)}, f32[8]{0:T(128)S(1)}, u32[]{:S(2)}, u32[]{:S(2)}) collective-permute-start(f32[8]{0:T(128)S(1)} %reduce_sum.29), channel_id=1, source_target_pairs={{0,4},{2,6},{4,8},{6,10},{8,12},{10,14},{12,16},{14,18},{16,20},{1... | collective-permute-start | bytes 104 | tf_op jit(solution)/shard_map/ppermute | solution.py:289
  64.5 6.2 %collective-permute-start.13 = (f32[8]{0:T(128)S(1)}, f32[8]{0:T(128)S(1)}, u32[]{:S(2)}, u32[]{:S(2)}) collective-permute-start(f32[8]{0:T(128)S(1)} %reduce_sum.29), channel_id=1, source_target_pairs={{0,28},{2,30},{4,0},{6,2},{8,4},{10,6},{12,8},{14,10},{16,12},{18,... | collective-permute-start | bytes 104 | tf_op jit(solution)/shard_map/ppermute | solution.py:289
  70.8 1.8 %copy-start.4 = (f32[19,1,16,128]{3,2,1,0:T(8,128)}, f32[19,1,16,128]{3,2,1,0:T(8,128)S(1)}, u32[]{:S(2)}) copy-start(f32[19,1,16,128]{3,2,1,0:T(8,128)S(1)} %slice.676.low_ref) | copy-start | bytes 466948
  70.9 1.8 %copy-start.5 = (f32[19,1,16,128]{3,2,1,0:T(8,128)}, f32[19,1,16,128]{3,2,1,0:T(8,128)S(1)}, u32[]{:S(2)}) copy-start(f32[19,1,16,128]{3,2,1,0:T(8,128)S(1)} %slice.677.high_ref) | copy-start | bytes 466948
  71.1 1.5 %collective-permute-start.14 = (f32[21,10,2,128]{3,2,1,0:T(2,128)S(1)}, f32[21,10,2,128]{3,2,1,0:T(2,128)S(1)}, u32[]{:S(2)}, u32[]{:S(2)}) collective-permute-start(f32[21,10,2,128]{3,2,1,0:T(2,128)S(1)} %fusion.9), channel_id=1, source_target_pairs={{0,1},{1,0},{2,3},{3,2},{4,5},{5,4},{6,7},{7,6},{8,9},{9,8},{10,11... | collective-permute-start | bytes 645128 | tf_op jit(solution)/shard_map/ppermute | solution.py:280
  73.9 4.9 %copy-start.11 = (f32[3,8,16,128]{3,2,1,0:T(8,128)S(1)}, f32[3,8,16,128]{3,2,1,0:T(8,128)}, u32[]{:S(2)}) copy-start(f32[3,8,16,128]{3,2,1,0:T(8,128)} %get-tuple-element.137) | copy-start | bytes 589828

commit v14 on v13

--- a/solution.py
+++ b/solution.py
@@ -287,8 +287,7 @@
         total = flow + from_left[-1, 0, 0, :fans] + from_right[-1, 0, 0, :fans]
     for offset in sorted(set(step % count for step in range(-reach, reach + 1)) - {0, 1, count - 1}):
         total = total + lax.ppermute(flow, axis, [(i, (i + offset) % count) for i in range(count)])
-    pair = None if both is None else both[0 : channels[0]]
-    extended = [(from_left[0 : channels[0]], from_right[0 : channels[0]], pair)]
+    extended = [(from_left, from_right, both)]
     first = channels[0]
     for field, channel in zip(fields[1:], channels[1:]):
         left = from_left[first : first + channel]
@@ -376,10 +375,10 @@
             fields.append(solid_flag.astype(jnp.float32)[None])
         fields, totals = rim_round(fields, partials, "len", 1, len_reach)
         low, high, _ = fields[0]
-        fields[0] = jnp.concatenate([low, populations, high], axis=1)
+        fields[0] = jnp.concatenate([low[:19], populations, high[:19]], axis=1)
         fields, totals = rim_round(fields, totals, "band", 2, band_reach)
         if fields[0][2] is None:
-            rows = jnp.concatenate(fields[0][:2], axis=2)
+            rows = jnp.concatenate([fields[0][0][:19], fields[0][1][:19]], axis=2)
         else:
             rows = fields[0][2]
         rimmed = fields[1][0]

time: 80 us -> 79 us (0.988)
  local copies, waits for them, and re-layouts: 5.75 us -> 4.94 us
    slice x9 -> x6, local copies, waits for them, and re-layouts: 2.17 us -> 0.07 us  [body(): fields[0] = jnp.concatenate([low[:19], populations, high[:19]], axis=1)]
    unnamed x34 -> x40, local copies, waits for them, and re-layouts: 0.07 us -> 1.37 us
where the time goes in v14:
time: 79 us; the launch traced here: 78.5 us
  starting transfers between devices  32.6 us (41%)
  Pallas kernels  17.7 us (22%)
  other arithmetic  11.1 us (14%)
  waiting for transfers between devices  10.8 us (14%)
  local copies, waits for them, and re-layouts  4.94 us (6%)
  between operations  1.17 us (1%)
    ppermute x6, starting transfers between devices, rim_round(): lax.ppermute(flow, axis, [(i, (i + offset) % count) for i in range(count)])  15.6 us
    pallas_call x3, Pallas kernels, lattice_step(): pl.pallas_call(functools.partial(step_kernel, with_moments), out_shape=tu...  15.3 us
    ppermute x3, starting transfers between devices, rim_round(): from_right = lax.ppermute(head, axis, backward)  13.6 us
    ppermute x3, waiting for transfers between devices, rim_round(): both = lax.ppermute(jnp.concatenate([tail, head], axis=dim), axis, forward)  4.17 us
    ppermute x3, waiting for transfers between devices, rim_round(): from_left = lax.ppermute(tail, axis, forward)  3.58 us
    ppermute x3, starting transfers between devices, rim_round(): from_left = lax.ppermute(tail, axis, forward)  3.4 us
    ppermute x6, waiting for transfers between devices, rim_round(): lax.ppermute(flow, axis, [(i, (i + offset) % count) for i in range(count)])  3.04 us
    pallas_call x1, Pallas kernels, first_moments(): pl.pallas_call(lambda populations_ref, discs_ref, velocity_ref, flow_ref:...  2.42 us
  transfers between devices with their start and end apart: 15, of which 6 were waited for; matrix products, arithmetic and copies ran while one was open for 1% of the time, Pallas kernels for 0%

profile of v14, /device:TPU:0, one launch (start us, length us, event | category | flops | bytes accessed | tf_op | source)
XLA Modules:
  0.0 78.5 jit_solution(11364077524776129388)
XLA Ops:
  0.6 0.8 %slice_bitcast_fusion.12 = (s32[8]{0:T(128)S(1)}, s32[8]{0:T(128)S(1)}, s32[8]{0:T(128)S(1)}) fusion(s32[8,3]{0,1:T(4,128)} %param.36), kind=kLoop, calls=%fused_computation.160 | loop fusion | bytes 192 | tf_op jit(solution)/shard_map/sub | solution.py:353
  1.5 0.7 and_select_fusion
  2.2 0.1 add_compare_fusion
  2.4 0.1 fusion.42
  2.5 0.9 %convert_bitcast_fusion = (f32[1,8,16,128]{3,2,1,0:T(8,128)S(1)}, pred[8,16,128]{2,1,0:T(8,128)(4,1)S(1)}) fusion(s32[8,16,128]{2,1,0:T(8,128)} %param.34), kind=kLoop, calls=%fused_computation.95 | loop fusion | flops 32768 | bytes 147456 | tf_op jit(solution)/shard_map/broadcast_in_dim | solution.py:375
  3.4 0.9 %and_convert_fusion.1.discs_ref = f32[8,8,16,128]{3,2,1,0:T(8,128)} fusion(pred[8,16,128]{2,1,0:T(8,128)(4,1)S(1)} %not.3, pred[8,16,128]{2,1,0:T(8,128)(4,1)S(1)} %slice.616, pred[8,8]{1,0:T(8,128)(4,1)S(1)} %slice.520), kind=kLoop, calls=%fused_computation.1 | loop fusion | flops 393216 | bytes 557120 | tf_op jit(solution)/shard_map/convert_element_type | solution.py:369
  4.4 2.4 %shard_map.104 = (f32[3,8,16,128]{3,2,1,0:T(8,128)}, f32[8,16,128]{2,1,0:T(8,128)}) custom-call(f32[19,8,16,128]{3,2,1,0:T(8,128)} %inner_ref.1, f32[8,8,16,128]{3,2,1,0:T(8,128)} %and_convert_fusion.1.discs_ref), custom_call_target="tpu_custom_call" | custom-call | flops 983040 | bytes 1245184 | tf_op jit(solution)/shard_map/pallas_call | solution.py:167
  6.8 1.0 %reduce_sum.27 = f32[8]{0:T(128)S(1)} reduce(f32[8,16,128]{2,1,0:T(8,128)} %get-tuple-element.130, f32[]{:T(128)} %constant.273.clone.1), dimensions={1,2}, to_apply=%region_0.1 | reduce | flops 16376 | bytes 65572 | tf_op jit(solution)/shard_map/reduce_sum | solution.py:371
  7.8 3.0 %collective-permute-start.2 = (f32[8]{0:T(128)S(1)}, f32[8]{0:T(128)S(1)}, u32[]{:S(2)}, u32[]{:S(2)}) collective-permute-start(f32[8]{0:T(128)S(1)} %reduce_sum.27), channel_id=1, source_target_pairs={{0,4},{2,6},{4,8},{6,10},{8,12},{10,14},{12,16},{14,18},{16,20},{1... | collective-permute-start | bytes 104 | tf_op jit(solution)/shard_map/ppermute | solution.py:289
  10.8 3.1 %collective-permute-start.3 = (f32[8]{0:T(128)S(1)}, f32[8]{0:T(128)S(1)}, u32[]{:S(2)}, u32[]{:S(2)}) collective-permute-start(f32[8]{0:T(128)S(1)} %reduce_sum.27), channel_id=1, source_target_pairs={{0,28},{2,30},{4,0},{6,2},{8,4},{10,6},{12,8},{14,10},{16,12},{18,... | collective-permute-start | bytes 104 | tf_op jit(solution)/shard_map/ppermute | solution.py:289
  14.0 1.6 %collective-permute-start = (f32[22,1,16,128]{3,2,1,0:T(8,128)S(1)}, f32[22,1,16,128]{3,2,1,0:T(8,128)S(1)}, u32[]{:S(2)}, u32[]{:S(2)}) collective-permute-start(f32[22,1,16,128]{3,2,1,0:T(8,128)S(1)} %get-tuple-element.193), channel_id=1, source_target_pairs={{0,2},{2,4},{4,6},{6,8},{8,10},{10,12},{12,14},{14,16},{16,18},{18... | collective-permute-start | bytes 540680 | tf_op jit(solution)/shard_map/ppermute | solution.py:285
  15.6 4.0 %collective-permute-start.1 = (f32[22,1,16,128]{3,2,1,0:T(8,128)S(1)}, f32[22,1,16,128]{3,2,1,0:T(8,128)S(1)}, u32[]{:S(2)}, u32[]{:S(2)}) collective-permute-start(f32[22,1,16,128]{3,2,1,0:T(8,128)S(1)} %get-tuple-element.194), channel_id=1, source_target_pairs={{2,0},{4,2},{6,4},{8,6},{10,8},{12,10},{14,12},{16,14},{18,16},{20... | collective-permute-start | bytes 540680 | tf_op jit(solution)/shard_map/ppermute | solution.py:286
  19.8 0.1 broadcast_multiply_fusion
  19.9 0.2 fusion.19
  20.2 3.6 %collective-permute-done.low_ref = f32[22,1,16,128]{3,2,1,0:T(8,128)S(1)} collective-permute-done((f32[22,1,16,128]{3,2,1,0:T(8,128)S(1)}, f32[22,1,16,128]{3,2,1,0:T(8,128)S(1)}, u32[]{:S(2)}, u32[]{:S(2)}) %collective-permute-start) | collective-permute-done | bytes 180256 | tf_op jit(solution)/shard_map/ppermute | solution.py:285
  23.9 0.2 fusion.3
  24.1 0.4 copy-done.4
  24.5 0.1 fusion.93
  24.6 1.4 %collective-permute-done.4.rows_ref = f32[22,10,2,128]{3,2,1,0:T(2,128)S(1)} collective-permute-done((f32[22,10,2,128]{3,2,1,0:T(2,128)S(1)}, f32[22,10,2,128]{3,2,1,0:T(2,128)S(1)}, u32[]{:S(2)}, u32[]{:S(2)}) %collective-permute-start.4) | collective-permute-done | bytes 225312 | tf_op jit(solution)/shard_map/ppermute | solution.py:280
  26.1 0.1 fusion.38
  26.2 0.6 maximum_bitcast_fusion.solid_ref
  26.9 1.1 %and_convert_fusion.discs_ref = f32[8,10,18,128]{3,2,1,0:T(8,128)} fusion(pred[10,18,128]{2,1,0:T(8,128)(4,1)S(1)} %maximum_compare_fusion, pred[8,18,128]{2,1,0:T(8,128)(4,1)S(1)} %add_compare_fusion, pred[8,10]{1,0:T(8,128)(4,1)S(1)} %fusion.42), kind=kLoop, calls=%fused_computation | loop fusion | flops 552960 | bytes 778832 | tf_op jit(solution)/shard_map/convert_element_type | solution.py:388
  28.0 0.5 fusion.71.strength_ref
  28.6 5.2 %shard_map.105 = (f32[19,8,16,128]{3,2,1,0:T(8,128)}, f32[3,8,16,128]{3,2,1,0:T(8,128)}, f32[8,16,128]{2,1,0:T(8,128)}) custom-call(f32[8]{0:T(128)} %fusion.71.strength_ref, f32[19,8,16,128]{3,2,1,0:T(8,128)} %inner_ref.1, f32[22,1,16,128]{3,2,1,0:T(8,128)} %copy-done.4, f32[22,1,16,128]{3,2,1,0:T(8,128)} %copy-done.5, f32[22,10,2,128]{3,2,1,0:T(2,128)} %copy-done.10, ...), custom_call_target="tpu_custom_call" | custom-call | flops 6912000 | bytes 3735552 | tf_op jit(solution)/shard_map/pallas_call | solution.py:193
  33.8 1.1 %fusion.77 = (f32[19,1,16,128]{3,2,1,0:T(8,128)S(1)}, f32[19,1,16,128]{3,2,1,0:T(8,128)S(1)}) fusion(f32[19,8,16,128]{3,2,1,0:T(8,128)} %get-tuple-element.132.inner_ref), kind=kLoop, calls=%fused_computation.169 | loop fusion | bytes 622592 | tf_op jit(solution)/shard_map/slice | solution.py:270
  34.9 1.0 %reduce_sum.28 = f32[8]{0:T(128)S(1)} reduce(f32[8,16,128]{2,1,0:T(8,128)} %get-tuple-element.131, f32[]{:T(128)} %constant.273.clone.1), dimensions={1,2}, to_apply=%region_1.2 | reduce | flops 16376 | bytes 65572 | tf_op jit(solution)/shard_map/reduce_sum | solution.py:417
  35.9 1.7 %collective-permute-start.5 = (f32[21,1,16,128]{3,2,1,0:T(8,128)S(1)}, f32[21,1,16,128]{3,2,1,0:T(8,128)S(1)}, u32[]{:S(2)}, u32[]{:S(2)}) collective-permute-start(f32[21,1,16,128]{3,2,1,0:T(8,128)S(1)} %get-tuple-element.185), channel_id=1, source_target_pairs={{0,2},{2,4},{4,6},{6,8},{8,10},{10,12},{12,14},{14,16},{16,18},{18... | collective-permute-start | bytes 516104 | tf_op jit(solution)/shard_map/ppermute | solution.py:285
  37.6 4.0 %collective-permute-start.6 = (f32[21,1,16,128]{3,2,1,0:T(8,128)S(1)}, f32[21,1,16,128]{3,2,1,0:T(8,128)S(1)}, u32[]{:S(2)}, u32[]{:S(2)}) collective-permute-start(f32[21,1,16,128]{3,2,1,0:T(8,128)S(1)} %get-tuple-element.186), channel_id=1, source_target_pairs={{2,0},{4,2},{6,4},{8,6},{10,8},{12,10},{14,12},{16,14},{18,16},{20... | collective-permute-start | bytes 516104 | tf_op jit(solution)/shard_map/ppermute | solution.py:286
  41.6 4.7 %collective-permute-start.8 = (f32[8]{0:T(128)S(1)}, f32[8]{0:T(128)S(1)}, u32[]{:S(2)}, u32[]{:S(2)}) collective-permute-start(f32[8]{0:T(128)S(1)} %reduce_sum.28), channel_id=1, source_target_pairs={{0,28},{2,30},{4,0},{6,2},{8,4},{10,6},{12,8},{14,10},{16,12},{18,... | collective-permute-start | bytes 104 | tf_op jit(solution)/shard_map/ppermute | solution.py:289
  46.3 1.5 %collective-permute-done.7 = f32[8]{0:T(128)S(1)} collective-permute-done((f32[8]{0:T(128)S(1)}, f32[8]{0:T(128)S(1)}, u32[]{:S(2)}, u32[]{:S(2)}) %collective-permute-start.7) | collective-permute-done | bytes 64 | tf_op jit(solution)/shard_map/ppermute | solution.py:289
  48.0 0.2 fusion.14
  48.1 0.4 copy-done.8
  48.6 0.1 fusion.91
  48.6 1.4 %collective-permute-done.9.rows_ref = f32[21,10,2,128]{3,2,1,0:T(2,128)S(1)} collective-permute-done((f32[21,10,2,128]{3,2,1,0:T(2,128)S(1)}, f32[21,10,2,128]{3,2,1,0:T(2,128)S(1)}, u32[]{:S(2)}, u32[]{:S(2)}) %collective-permute-start.9) | collective-permute-done | bytes 215072 | tf_op jit(solution)/shard_map/ppermute | solution.py:280
  50.1 0.1 fusion.32
  50.2 0.6 fusion.72.strength_ref
  50.8 5.2 %shard_map.106 = (f32[19,8,16,128]{3,2,1,0:T(8,128)}, f32[3,8,16,128]{3,2,1,0:T(8,128)}, f32[8,16,128]{2,1,0:T(8,128)}) custom-call(f32[8]{0:T(128)} %fusion.72.strength_ref, f32[19,8,16,128]{3,2,1,0:T(8,128)} %get-tuple-element.132.inner_ref, f32[21,1,16,128]{3,2,1,0:T(8,128)} %copy-done.8, f32[21,1,16,128]{3,2,1,0:T(8,128)} %copy-done.9, ...), custom_call_target="tpu_custom_call" | custom-call | flops 6912000 | bytes 3735552 | tf_op jit(solution)/shard_map/pallas_call | solution.py:193
  56.0 1.1 %fusion.76 = (f32[19,1,16,128]{3,2,1,0:T(8,128)S(1)}, f32[19,1,16,128]{3,2,1,0:T(8,128)S(1)}) fusion(f32[19,8,16,128]{3,2,1,0:T(8,128)} %get-tuple-element.135.inner_ref), kind=kLoop, calls=%fused_computation.168 | loop fusion | bytes 622592 | tf_op jit(solution)/shard_map/slice | solution.py:270
  57.2 1.0 %reduce_sum.29 = f32[8]{0:T(128)S(1)} reduce(f32[8,16,128]{2,1,0:T(8,128)} %get-tuple-element.134, f32[]{:T(128)} %constant.273.clone.1), dimensions={1,2}, to_apply=%region_2.3 | reduce | flops 16376 | bytes 65572 | tf_op jit(solution)/shard_map/reduce_sum | solution.py:417
  58.3 5.6 %collective-permute-start.11 = (f32[21,1,16,128]{3,2,1,0:T(8,128)S(1)}, f32[21,1,16,128]{3,2,1,0:T(8,128)S(1)}, u32[]{:S(2)}, u32[]{:S(2)}) collective-permute-start(f32[21,1,16,128]{3,2,1,0:T(8,128)S(1)} %get-tuple-element.184), channel_id=1, source_target_pairs={{2,0},{4,2},{6,4},{8,6},{10,8},{12,10},{14,12},{16,14},{18,16},{20... | collective-permute-start | bytes 516104 | tf_op jit(solution)/shard_map/ppermute | solution.py:286
  63.9 4.7 %collective-permute-start.13 = (f32[8]{0:T(128)S(1)}, f32[8]{0:T(128)S(1)}, u32[]{:S(2)}, u32[]{:S(2)}) collective-permute-start(f32[8]{0:T(128)S(1)} %reduce_sum.29), channel_id=1, source_target_pairs={{0,28},{2,30},{4,0},{6,2},{8,4},{10,6},{12,8},{14,10},{16,12},{18,... | collective-permute-start | bytes 104 | tf_op jit(solution)/shard_map/ppermute | solution.py:289
  68.6 1.5 %collective-permute-done.12 = f32[8]{0:T(128)S(1)} collective-permute-done((f32[8]{0:T(128)S(1)}, f32[8]{0:T(128)S(1)}, u32[]{:S(2)}, u32[]{:S(2)}) %collective-permute-start.12) | collective-permute-done | bytes 64 | tf_op jit(solution)/shard_map/ppermute | solution.py:289
  70.2 0.2 fusion.9
  70.4 0.4 copy-done.6
  70.9 1.4 %collective-permute-done.14.rows_ref = f32[21,10,2,128]{3,2,1,0:T(2,128)S(1)} collective-permute-done((f32[21,10,2,128]{3,2,1,0:T(2,128)S(1)}, f32[21,10,2,128]{3,2,1,0:T(2,128)S(1)}, u32[]{:S(2)}, u32[]{:S(2)}) %collective-permute-start.14) | collective-permute-done | bytes 215072 | tf_op jit(solution)/shard_map/ppermute | solution.py:280
  72.4 0.7 fusion.26
  73.1 0.5 fusion.73.strength_ref
  73.6 4.9 %shard_map.107 = f32[19,8,16,128]{3,2,1,0:T(8,128)} custom-call(f32[8]{0:T(128)} %fusion.73.strength_ref, f32[19,8,16,128]{3,2,1,0:T(8,128)} %get-tuple-element.135.inner_ref, f32[21,1,16,128]{3,2,1,0:T(8,128)} %copy-done.6, f32[21,1,16,128]{3,2,1,0:T(8,128)} %copy-done.7, f32[21,10,2,128]{3,2,1,0:T(2,128)} %copy-done.12, ...), custom_call_target="tpu_custom_call" | custom-call | flops 6912000 | bytes 3735552 | tf_op jit(solution)/shard_map/pallas_call | solution.py:193
  (104 shorter events, 1.3 us)
Async XLA Ops:
  3.4 10.5 %copy-start = (f32[19,8,16,128]{3,2,1,0:T(8,128)S(1)}, f32[19,8,16,128]{3,2,1,0:T(8,128)}, u32[]{:S(2)}) copy-start(f32[19,8,16,128]{3,2,1,0:T(8,128)} %inner_ref.1) | copy-start | bytes 3735556
  4.4 9.6 %copy-start.3 = (f32[8,16,128]{2,1,0:T(8,128)S(1)}, f32[8,16,128]{2,1,0:T(8,128)}, u32[]{:S(2)}) copy-start(f32[8,16,128]{2,1,0:T(8,128)} %param.35) | copy-start | bytes 196612
  4.4 15.3 %copy-start.18 = (s32[16,3]{0,1:T(4,128)S(1)}, s32[16,3]{0,1:T(4,128)}, u32[]{:S(2)}) copy-start(s32[16,3]{0,1:T(4,128)} %param.39) | copy-start | bytes 580
  6.8 13.1 %copy-start.19 = (f32[16]{0:T(128)S(1)}, f32[16]{0:T(128)}, u32[]{:S(2)}) copy-start(f32[16]{0:T(128)} %param.40) | copy-start | bytes 196
  7.8 12.4 %collective-permute-start.2 = (f32[8]{0:T(128)S(1)}, f32[8]{0:T(128)S(1)}, u32[]{:S(2)}, u32[]{:S(2)}) collective-permute-start(f32[8]{0:T(128)S(1)} %reduce_sum.27), channel_id=1, source_target_pairs={{0,4},{2,6},{4,8},{6,10},{8,12},{10,14},{12,16},{14,18},{16,20},{1... | collective-permute-start | bytes 104 | tf_op jit(solution)/shard_map/ppermute | solution.py:289
  10.8 9.4 %collective-permute-start.3 = (f32[8]{0:T(128)S(1)}, f32[8]{0:T(128)S(1)}, u32[]{:S(2)}, u32[]{:S(2)}) collective-permute-start(f32[8]{0:T(128)S(1)} %reduce_sum.27), channel_id=1, source_target_pairs={{0,28},{2,30},{4,0},{6,2},{8,4},{10,6},{12,8},{14,10},{16,12},{18,... | collective-permute-start | bytes 104 | tf_op jit(solution)/shard_map/ppermute | solution.py:289
  14.0 9.8 %collective-permute-start = (f32[22,1,16,128]{3,2,1,0:T(8,128)S(1)}, f32[22,1,16,128]{3,2,1,0:T(8,128)S(1)}, u32[]{:S(2)}, u32[]{:S(2)}) collective-permute-start(f32[22,1,16,128]{3,2,1,0:T(8,128)S(1)} %get-tuple-element.193), channel_id=1, source_target_pairs={{0,2},{2,4},{4,6},{6,8},{8,10},{10,12},{12,14},{14,16},{16,18},{18... | collective-permute-start | bytes 540680 | tf_op jit(solution)/shard_map/ppermute | solution.py:285
  15.6 8.1 %collective-permute-start.1 = (f32[22,1,16,128]{3,2,1,0:T(8,128)S(1)}, f32[22,1,16,128]{3,2,1,0:T(8,128)S(1)}, u32[]{:S(2)}, u32[]{:S(2)}) collective-permute-start(f32[22,1,16,128]{3,2,1,0:T(8,128)S(1)} %get-tuple-element.194), channel_id=1, source_target_pairs={{2,0},{4,2},{6,4},{8,6},{10,8},{12,10},{14,12},{16,14},{18,16},{20... | collective-permute-start | bytes 540680 | tf_op jit(solution)/shard_map/ppermute | solution.py:286
  23.7 0.7 copy-start.4
  23.7 0.7 copy-start.5
  23.9 2.2 %copy-start.13 = (f32[3,8,16,128]{3,2,1,0:T(8,128)S(1)}, f32[3,8,16,128]{3,2,1,0:T(8,128)}, u32[]{:S(2)}) copy-start(f32[3,8,16,128]{3,2,1,0:T(8,128)} %get-tuple-element.133) | copy-start | bytes 589828
  24.5 1.5 %collective-permute-start.4 = (f32[22,10,2,128]{3,2,1,0:T(2,128)S(1)}, f32[22,10,2,128]{3,2,1,0:T(2,128)S(1)}, u32[]{:S(2)}, u32[]{:S(2)}) collective-permute-start(f32[22,10,2,128]{3,2,1,0:T(2,128)S(1)} %fusion.3), channel_id=1, source_target_pairs={{0,1},{1,0},{2,3},{3,2},{4,5},{5,4},{6,7},{7,6},{8,9},{9,8},{10,11... | collective-permute-start | bytes 675848 | tf_op jit(solution)/shard_map/ppermute | solution.py:280
  26.0 2.0 %copy-start.10 = (f32[22,10,2,128]{3,2,1,0:T(2,128)}, f32[22,10,2,128]{3,2,1,0:T(2,128)S(1)}, u32[]{:S(2)}) copy-start(f32[22,10,2,128]{3,2,1,0:T(2,128)S(1)} %collective-permute-done.4.rows_ref) | copy-start | bytes 675844
  26.0 2.0 %copy-start.16 = (f32[8]{0:T(128)S(1)}, f32[8]{0:T(128)}, u32[]{:S(2)}) copy-start(f32[8]{0:T(128)} %param.37) | copy-start | bytes 100
  26.0 2.0 %copy-start.17 = (f32[8]{0:T(128)S(1)}, f32[8]{0:T(128)}, u32[]{:S(2)}) copy-start(f32[8]{0:T(128)} %param.38) | copy-start | bytes 100
  33.8 14.2 %copy-start.1 = (f32[19,8,16,128]{3,2,1,0:T(8,128)S(1)}, f32[19,8,16,128]{3,2,1,0:T(8,128)}, u32[]{:S(2)}) copy-start(f32[19,8,16,128]{3,2,1,0:T(8,128)} %get-tuple-element.132.inner_ref) | copy-start | bytes 3735556
  35.9 11.9 %collective-permute-start.5 = (f32[21,1,16,128]{3,2,1,0:T(8,128)S(1)}, f32[21,1,16,128]{3,2,1,0:T(8,128)S(1)}, u32[]{:S(2)}, u32[]{:S(2)}) collective-permute-start(f32[21,1,16,128]{3,2,1,0:T(8,128)S(1)} %get-tuple-element.185), channel_id=1, source_target_pairs={{0,2},{2,4},{4,6},{6,8},{8,10},{10,12},{12,14},{14,16},{16,18},{18... | collective-permute-start | bytes 516104 | tf_op jit(solution)/shard_map/ppermute | solution.py:285
  37.6 10.2 %collective-permute-start.6 = (f32[21,1,16,128]{3,2,1,0:T(8,128)S(1)}, f32[21,1,16,128]{3,2,1,0:T(8,128)S(1)}, u32[]{:S(2)}, u32[]{:S(2)}) collective-permute-start(f32[21,1,16,128]{3,2,1,0:T(8,128)S(1)} %get-tuple-element.186), channel_id=1, source_target_pairs={{2,0},{4,2},{6,4},{8,6},{10,8},{12,10},{14,12},{16,14},{18,16},{20... | collective-permute-start | bytes 516104 | tf_op jit(solution)/shard_map/ppermute | solution.py:286
  41.6 6.2 %collective-permute-start.7 = (f32[8]{0:T(128)S(1)}, f32[8]{0:T(128)S(1)}, u32[]{:S(2)}, u32[]{:S(2)}) collective-permute-start(f32[8]{0:T(128)S(1)} %reduce_sum.28), channel_id=1, source_target_pairs={{0,4},{2,6},{4,8},{6,10},{8,12},{10,14},{12,16},{14,18},{16,20},{1... | collective-permute-start | bytes 104 | tf_op jit(solution)/shard_map/ppermute | solution.py:289
  41.6 6.2 %collective-permute-start.8 = (f32[8]{0:T(128)S(1)}, f32[8]{0:T(128)S(1)}, u32[]{:S(2)}, u32[]{:S(2)}) collective-permute-start(f32[8]{0:T(128)S(1)} %reduce_sum.28), channel_id=1, source_target_pairs={{0,28},{2,30},{4,0},{6,2},{8,4},{10,6},{12,8},{14,10},{16,12},{18,... | collective-permute-start | bytes 104 | tf_op jit(solution)/shard_map/ppermute | solution.py:289
  47.8 0.7 copy-start.8
  47.9 0.7 copy-start.9
  48.0 2.1 %copy-start.15 = (f32[3,8,16,128]{3,2,1,0:T(8,128)S(1)}, f32[3,8,16,128]{3,2,1,0:T(8,128)}, u32[]{:S(2)}) copy-start(f32[3,8,16,128]{3,2,1,0:T(8,128)} %get-tuple-element.136) | copy-start | bytes 589828
  48.6 1.5 %collective-permute-start.9 = (f32[21,10,2,128]{3,2,1,0:T(2,128)S(1)}, f32[21,10,2,128]{3,2,1,0:T(2,128)S(1)}, u32[]{:S(2)}, u32[]{:S(2)}) collective-permute-start(f32[21,10,2,128]{3,2,1,0:T(2,128)S(1)} %fusion.14), channel_id=1, source_target_pairs={{0,1},{1,0},{2,3},{3,2},{4,5},{5,4},{6,7},{7,6},{8,9},{9,8},{10,11... | collective-permute-start | bytes 645128 | tf_op jit(solution)/shard_map/ppermute | solution.py:280
  50.0 0.8 copy-start.11
  56.0 14.2 %copy-start.2 = (f32[19,8,16,128]{3,2,1,0:T(8,128)S(1)}, f32[19,8,16,128]{3,2,1,0:T(8,128)}, u32[]{:S(2)}) copy-start(f32[19,8,16,128]{3,2,1,0:T(8,128)} %get-tuple-element.135.inner_ref) | copy-start | bytes 3735556
  58.2 11.9 %collective-permute-start.10 = (f32[21,1,16,128]{3,2,1,0:T(8,128)S(1)}, f32[21,1,16,128]{3,2,1,0:T(8,128)S(1)}, u32[]{:S(2)}, u32[]{:S(2)}) collective-permute-start(f32[21,1,16,128]{3,2,1,0:T(8,128)S(1)} %get-tuple-element.183), channel_id=1, source_target_pairs={{0,2},{2,4},{4,6},{6,8},{8,10},{10,12},{12,14},{14,16},{16,18},{18... | collective-permute-start | bytes 516104 | tf_op jit(solution)/shard_map/ppermute | solution.py:285
  58.3 11.9 %collective-permute-start.11 = (f32[21,1,16,128]{3,2,1,0:T(8,128)S(1)}, f32[21,1,16,128]{3,2,1,0:T(8,128)S(1)}, u32[]{:S(2)}, u32[]{:S(2)}) collective-permute-start(f32[21,1,16,128]{3,2,1,0:T(8,128)S(1)} %get-tuple-element.184), channel_id=1, source_target_pairs={{2,0},{4,2},{6,4},{8,6},{10,8},{12,10},{14,12},{16,14},{18,16},{20... | collective-permute-start | bytes 516104 | tf_op jit(solution)/shard_map/ppermute | solution.py:286
  63.9 6.2 %collective-permute-start.12 = (f32[8]{0:T(128)S(1)}, f32[8]{0:T(128)S(1)}, u32[]{:S(2)}, u32[]{:S(2)}) collective-permute-start(f32[8]{0:T(128)S(1)} %reduce_sum.29), channel_id=1, source_target_pairs={{0,4},{2,6},{4,8},{6,10},{8,12},{10,14},{12,16},{14,18},{16,20},{1... | collective-permute-start | bytes 104 | tf_op jit(solution)/shard_map/ppermute | solution.py:289
  63.9 6.2 %collective-permute-start.13 = (f32[8]{0:T(128)S(1)}, f32[8]{0:T(128)S(1)}, u32[]{:S(2)}, u32[]{:S(2)}) collective-permute-start(f32[8]{0:T(128)S(1)} %reduce_sum.29), channel_id=1, source_target_pairs={{0,28},{2,30},{4,0},{6,2},{8,4},{10,6},{12,8},{14,10},{16,12},{18,... | collective-permute-start | bytes 104 | tf_op jit(solution)/shard_map/ppermute | solution.py:289
  70.1 0.7 copy-start.6
  70.1 0.7 copy-start.7
  70.2 2.1 %copy-start.14 = (f32[3,8,16,128]{3,2,1,0:T(8,128)S(1)}, f32[3,8,16,128]{3,2,1,0:T(8,128)}, u32[]{:S(2)}) copy-start(f32[3,8,16,128]{3,2,1,0:T(8,128)} %get-tuple-element.137) | copy-start | bytes 589828
  70.8 1.5 %collective-permute-start.14 = (f32[21,10,2,128]{3,2,1,0:T(2,128)S(1)}, f32[21,10,2,128]{3,2,1,0:T(2,128)S(1)}, u32[]{:S(2)}, u32[]{:S(2)}) collective-permute-start(f32[21,10,2,128]{3,2,1,0:T(2,128)S(1)} %fusion.9), channel_id=1, source_target_pairs={{0,1},{1,0},{2,3},{3,2},{4,5},{5,4},{6,7},{7,6},{8,9},{9,8},{10,11... | collective-permute-start | bytes 645128 | tf_op jit(solution)/shard_map/ppermute | solution.py:280
  72.3 1.3 %copy-start.12 = (f32[21,10,2,128]{3,2,1,0:T(2,128)}, f32[21,10,2,128]{3,2,1,0:T(2,128)S(1)}, u32[]{:S(2)}) copy-start(f32[21,10,2,128]{3,2,1,0:T(2,128)S(1)} %collective-permute-done.14.rows_ref) | copy-start | bytes 645124

commit v15 on v14

--- a/solution.py
+++ b/solution.py
@@ -79,7 +79,7 @@
     with_moments, strength_ref, inner_ref, low_ref, high_ref, rows_ref, discs_ref, solid_ref, *rest
 ):
     if with_moments:
-        out_ref, velocity_ref, flow_ref, posts_ref = rest
+        out_ref, velocity_ref, flow_ref, posts_ref, sums_ref = rest
     else:
         out_ref, posts_ref = rest
     fans = discs_ref.shape[0]
@@ -140,40 +140,45 @@
         out_ref[which] = piece
     if not with_moments:
         return
-    moments_into(out_ref, discs_ref, 1, velocity_ref, flow_ref)
-
-
-def moments_into(populations_ref, discs_ref, rim, velocity_ref, flow_ref):
+    moments_into(out_ref, discs_ref, 1, velocity_ref, flow_ref, sums_ref)
+
+
+def moments_into(populations_ref, discs_ref, rim, velocity_ref, flow_ref, sums_ref):
     fans = discs_ref.shape[0]
     band_width = populations_ref.shape[2]
-    flow_ref[...] = jnp.zeros(flow_ref.shape, jnp.float32)
+    sums_ref[...] = jnp.zeros(sums_ref.shape, jnp.float32)
 
     def moment_plane(index, carry):
         density, velocity = plane_moments([populations_ref[which, index] for which in range(19)])
         for dimension in range(3):
             velocity_ref[dimension, index] = velocity[dimension]
         for fan_number in range(fans):
-            flow_ref[fan_number] += (
+            sums_ref[fan_number] += (
                 discs_ref[fan_number, index + rim, 0:band_width, :] * velocity[0]
             )
         return carry
 
     lax.fori_loop(0, populations_ref.shape[1], moment_plane, 0)
+    for fan_number in range(fans):
+        flow_ref[fan_number : fan_number + 1, :] = jnp.broadcast_to(
+            jnp.sum(sums_ref[fan_number], axis=(0, 1), keepdims=True), (1, flow_ref.shape[1])
+        )
 
 
 def first_moments(populations, discs):
     fans, slab_len, band_width, height = discs.shape
     vmem = pl.BlockSpec(memory_space=pltpu.VMEM)
     return pl.pallas_call(
-        lambda populations_ref, discs_ref, velocity_ref, flow_ref: moments_into(
-            populations_ref, discs_ref, 0, velocity_ref, flow_ref
+        lambda populations_ref, discs_ref, velocity_ref, flow_ref, sums_ref: moments_into(
+            populations_ref, discs_ref, 0, velocity_ref, flow_ref, sums_ref
         ),
         out_shape=(
             jax.ShapeDtypeStruct((3, slab_len, band_width, height), jnp.float32),
-            jax.ShapeDtypeStruct((fans, band_width, height), jnp.float32),
+            jax.ShapeDtypeStruct((fans, height), jnp.float32),
         ),
         in_specs=[vmem, vmem],
         out_specs=(vmem, vmem),
+        scratch_shapes=[pltpu.VMEM((fans, band_width, height), jnp.float32)],
         cost_estimate=pl.CostEstimate(
             flops=60 * discs[0].size, transcendentals=0, bytes_accessed=4 * populations.size
         ),
@@ -188,16 +193,17 @@
     out_shape = [jax.ShapeDtypeStruct((19, slab_len, band_width, height), jnp.float32)]
     if with_moments:
         out_shape.append(jax.ShapeDtypeStruct((3, slab_len, band_width, height), jnp.float32))
-        out_shape.append(jax.ShapeDtypeStruct((fans, band_width, height), jnp.float32))
+        out_shape.append(jax.ShapeDtypeStruct((fans, height), jnp.float32))
+    scratch = [pltpu.VMEM((19, slab_len + 2, band_width + 2, height), jnp.float32)]
+    if with_moments:
+        scratch.append(pltpu.VMEM((fans, band_width, height), jnp.float32))
     vmem = pl.BlockSpec(memory_space=pltpu.VMEM)
     return pl.pallas_call(
         functools.partial(step_kernel, with_moments),
         out_shape=tuple(out_shape),
         in_specs=[pl.BlockSpec(memory_space=pltpu.SMEM)] + [vmem] * 6,
         out_specs=tuple([vmem] * len(out_shape)),
-        scratch_shapes=[
-            pltpu.VMEM((19, slab_len + 2, band_width + 2, height), jnp.float32)
-        ],
+        scratch_shapes=scratch,
         cost_estimate=pl.CostEstimate(
             flops=300 * solid_rim.size, transcendentals=0, bytes_accessed=12 * inner.size
         ),
@@ -368,7 +374,7 @@
         & jnp.logical_not(solid_flag)[None]
     ).astype(jnp.float32)
     velocity, flow = first_moments(populations, inner_discs)
-    partials = jnp.sum(flow, axis=(1, 2))
+    partials = flow[:, 0]
     for repeat in range(ITERS):
         fields = [populations, smoke_field[None]]
         if repeat == 0:
@@ -414,7 +420,7 @@
         populations = stepped[0]
         if not last:
             velocity = stepped[1]
-            partials = jnp.sum(stepped[2], axis=(1, 2))
+            partials = stepped[2][:, 0]
     return (populations, smoke_field)
 
 

time: 79 us -> 78.5 us (level)
  other arithmetic: 11.1 us -> 8.25 us
  local copies, waits for them, and re-layouts: 4.94 us -> 7.31 us
    reduce_sum x3 -> x0, other arithmetic: 2.95 us -> none  [the longest x2 1.96 us: body(): partials = jnp.sum(stepped[2], axis=(1, 2))]
    slice x0 -> x3, local copies, waits for them, and re-layouts: none -> 2.41 us  [the longest x2 1.61 us: body(): partials = stepped[2][:, 0]]
where the time goes in v15:
time: 78.5 us; the launch traced here: 78.1 us
  starting transfers between devices  32.6 us (42%)
  Pallas kernels  17.8 us (23%)
  waiting for transfers between devices  10.8 us (14%)
  other arithmetic  8.25 us (11%)
  local copies, waits for them, and re-layouts  7.31 us (9%)
  between operations  1.17 us (1%)
    ppermute x6, starting transfers between devices, rim_round(): lax.ppermute(flow, axis, [(i, (i + offset) % count) for i in range(count)])  15.6 us
    pallas_call x3, Pallas kernels, lattice_step(): pl.pallas_call(functools.partial(step_kernel, with_moments), out_shape=tu...  15.3 us
    ppermute x3, starting transfers between devices, rim_round(): from_right = lax.ppermute(head, axis, backward)  13.6 us
    ppermute x3, waiting for transfers between devices, rim_round(): both = lax.ppermute(jnp.concatenate([tail, head], axis=dim), axis, forward)  4.17 us
    ppermute x3, waiting for transfers between devices, rim_round(): from_left = lax.ppermute(tail, axis, forward)  3.6 us
    ppermute x3, starting transfers between devices, rim_round(): from_left = lax.ppermute(tail, axis, forward)  3.4 us
    ppermute x6, waiting for transfers between devices, rim_round(): lax.ppermute(flow, axis, [(i, (i + offset) % count) for i in range(count)])  3.04 us
    pallas_call x1, Pallas kernels, first_moments(): pl.pallas_call(lambda populations_ref, discs_ref, velocity_ref, flow_ref,...  2.45 us
  transfers between devices with their start and end apart: 15, of which 6 were waited for; matrix products, arithmetic and copies ran while one was open for 1% of the time, Pallas kernels for 0%

profile of v15, /device:TPU:0, one launch (start us, length us, event | category | flops | bytes accessed | tf_op | source)
XLA Modules:
  0.0 78.1 jit_solution(3695815246599484503)
XLA Ops:
  0.6 0.8 %slice_bitcast_fusion.12 = (s32[8]{0:T(128)S(1)}, s32[8]{0:T(128)S(1)}, s32[8]{0:T(128)S(1)}) fusion(s32[8,3]{0,1:T(4,128)} %param.36), kind=kLoop, calls=%fused_computation.163 | loop fusion | bytes 192 | tf_op jit(solution)/shard_map/sub | solution.py:359
  1.5 0.7 and_select_fusion
  2.2 0.1 add_compare_fusion
  2.4 0.1 fusion.42
  2.5 1.0 %convert_bitcast_fusion = (f32[1,8,16,128]{3,2,1,0:T(8,128)S(1)}, pred[8,16,128]{2,1,0:T(8,128)(4,1)S(1)}) fusion(s32[8,16,128]{2,1,0:T(8,128)} %param.34), kind=kLoop, calls=%fused_computation.95 | loop fusion | flops 32768 | bytes 147456 | tf_op jit(solution)/shard_map/broadcast_in_dim | solution.py:381
  3.5 0.9 %and_convert_fusion.1.discs_ref = f32[8,8,16,128]{3,2,1,0:T(8,128)} fusion(pred[8,16,128]{2,1,0:T(8,128)(4,1)S(1)} %not.3, pred[8,16,128]{2,1,0:T(8,128)(4,1)S(1)} %slice.628, pred[8,8]{1,0:T(8,128)(4,1)S(1)} %slice.529), kind=kLoop, calls=%fused_computation.1 | loop fusion | flops 393216 | bytes 557120 | tf_op jit(solution)/shard_map/convert_element_type | solution.py:375
  4.5 2.5 %shard_map.104 = (f32[3,8,16,128]{3,2,1,0:T(8,128)}, f32[8,128]{1,0:T(8,128)}) custom-call(f32[19,8,16,128]{3,2,1,0:T(8,128)} %inner_ref.1, f32[8,8,16,128]{3,2,1,0:T(8,128)} %and_convert_fusion.1.discs_ref), custom_call_target="tpu_custom_call" | custom-call | flops 983040 | bytes 1245184 | tf_op jit(solution)/shard_map/pallas_call | solution.py:171
  6.9 0.8 %slice_reduce_fusion.2 = f32[8]{0:T(128)S(1)} fusion(f32[8,128]{1,0:T(8,128)} %get-tuple-element.130), kind=kLoop, calls=%fused_computation.118 | loop fusion | bytes 64 | tf_op jit(solution)/shard_map/slice | solution.py:377
  7.7 3.0 %collective-permute-start.2 = (f32[8]{0:T(128)S(1)}, f32[8]{0:T(128)S(1)}, u32[]{:S(2)}, u32[]{:S(2)}) collective-permute-start(f32[8]{0:T(128)S(1)} %slice_reduce_fusion.2), channel_id=1, source_target_pairs={{0,4},{2,6},{4,8},{6,10},{8,12},{10,14},{12,16},{14,18},{16,20},{1... | collective-permute-start | bytes 104 | tf_op jit(solution)/shard_map/ppermute | solution.py:295
  10.7 3.1 %collective-permute-start.3 = (f32[8]{0:T(128)S(1)}, f32[8]{0:T(128)S(1)}, u32[]{:S(2)}, u32[]{:S(2)}) collective-permute-start(f32[8]{0:T(128)S(1)} %slice_reduce_fusion.2), channel_id=1, source_target_pairs={{0,28},{2,30},{4,0},{6,2},{8,4},{10,6},{12,8},{14,10},{16,12},{18,... | collective-permute-start | bytes 104 | tf_op jit(solution)/shard_map/ppermute | solution.py:295
  13.9 1.6 %collective-permute-start = (f32[22,1,16,128]{3,2,1,0:T(8,128)S(1)}, f32[22,1,16,128]{3,2,1,0:T(8,128)S(1)}, u32[]{:S(2)}, u32[]{:S(2)}) collective-permute-start(f32[22,1,16,128]{3,2,1,0:T(8,128)S(1)} %get-tuple-element.193), channel_id=1, source_target_pairs={{0,2},{2,4},{4,6},{6,8},{8,10},{10,12},{12,14},{14,16},{16,18},{18... | collective-permute-start | bytes 540680 | tf_op jit(solution)/shard_map/ppermute | solution.py:291
  15.6 4.0 %collective-permute-start.1 = (f32[22,1,16,128]{3,2,1,0:T(8,128)S(1)}, f32[22,1,16,128]{3,2,1,0:T(8,128)S(1)}, u32[]{:S(2)}, u32[]{:S(2)}) collective-permute-start(f32[22,1,16,128]{3,2,1,0:T(8,128)S(1)} %get-tuple-element.194), channel_id=1, source_target_pairs={{2,0},{4,2},{6,4},{8,6},{10,8},{12,10},{14,12},{16,14},{18,16},{20... | collective-permute-start | bytes 540680 | tf_op jit(solution)/shard_map/ppermute | solution.py:292
  19.7 0.1 broadcast_multiply_fusion
  19.9 0.2 fusion.19
  20.1 3.6 %collective-permute-done.low_ref = f32[22,1,16,128]{3,2,1,0:T(8,128)S(1)} collective-permute-done((f32[22,1,16,128]{3,2,1,0:T(8,128)S(1)}, f32[22,1,16,128]{3,2,1,0:T(8,128)S(1)}, u32[]{:S(2)}, u32[]{:S(2)}) %collective-permute-start) | collective-permute-done | bytes 180256 | tf_op jit(solution)/shard_map/ppermute | solution.py:291
  23.8 0.2 fusion.3
  24.0 0.3 copy-done.4
  24.4 0.1 fusion.93
  24.5 1.4 %collective-permute-done.4.rows_ref = f32[22,10,2,128]{3,2,1,0:T(2,128)S(1)} collective-permute-done((f32[22,10,2,128]{3,2,1,0:T(2,128)S(1)}, f32[22,10,2,128]{3,2,1,0:T(2,128)S(1)}, u32[]{:S(2)}, u32[]{:S(2)}) %collective-permute-start.4) | collective-permute-done | bytes 225312 | tf_op jit(solution)/shard_map/ppermute | solution.py:286
  26.0 0.1 fusion.38
  26.1 0.6 maximum_bitcast_fusion.solid_ref
  26.8 1.1 %and_convert_fusion.discs_ref = f32[8,10,18,128]{3,2,1,0:T(8,128)} fusion(pred[10,18,128]{2,1,0:T(8,128)(4,1)S(1)} %maximum_compare_fusion, pred[8,18,128]{2,1,0:T(8,128)(4,1)S(1)} %add_compare_fusion, pred[8,10]{1,0:T(8,128)(4,1)S(1)} %fusion.42), kind=kLoop, calls=%fused_computation | loop fusion | flops 552960 | bytes 778832 | tf_op jit(solution)/shard_map/convert_element_type | solution.py:394
  28.0 0.5 fusion.71.strength_ref
  28.5 5.2 %shard_map.105 = (f32[19,8,16,128]{3,2,1,0:T(8,128)}, f32[3,8,16,128]{3,2,1,0:T(8,128)}, f32[8,128]{1,0:T(8,128)}) custom-call(f32[8]{0:T(128)} %fusion.71.strength_ref, f32[19,8,16,128]{3,2,1,0:T(8,128)} %inner_ref.1, f32[22,1,16,128]{3,2,1,0:T(8,128)} %copy-done.4, f32[22,1,16,128]{3,2,1,0:T(8,128)} %copy-done.5, f32[22,10,2,128]{3,2,1,0:T(2,128)} %copy-done.10, ...), custom_call_target="tpu_custom_call" | custom-call | flops 6912000 | bytes 3735552 | tf_op jit(solution)/shard_map/pallas_call | solution.py:201
  33.7 1.1 %fusion.77 = (f32[19,1,16,128]{3,2,1,0:T(8,128)S(1)}, f32[19,1,16,128]{3,2,1,0:T(8,128)S(1)}) fusion(f32[19,8,16,128]{3,2,1,0:T(8,128)} %get-tuple-element.132.inner_ref), kind=kLoop, calls=%fused_computation.172 | loop fusion | bytes 622592 | tf_op jit(solution)/shard_map/slice | solution.py:276
  34.8 0.8 %slice_reduce_fusion.1 = f32[8]{0:T(128)S(1)} fusion(f32[8,128]{1,0:T(8,128)} %get-tuple-element.131), kind=kLoop, calls=%fused_computation.117 | loop fusion | bytes 64 | tf_op jit(solution)/shard_map/slice | solution.py:423
  35.7 1.7 %collective-permute-start.5 = (f32[21,1,16,128]{3,2,1,0:T(8,128)S(1)}, f32[21,1,16,128]{3,2,1,0:T(8,128)S(1)}, u32[]{:S(2)}, u32[]{:S(2)}) collective-permute-start(f32[21,1,16,128]{3,2,1,0:T(8,128)S(1)} %get-tuple-element.185), channel_id=1, source_target_pairs={{0,2},{2,4},{4,6},{6,8},{8,10},{10,12},{12,14},{14,16},{16,18},{18... | collective-permute-start | bytes 516104 | tf_op jit(solution)/shard_map/ppermute | solution.py:291
  37.4 4.0 %collective-permute-start.6 = (f32[21,1,16,128]{3,2,1,0:T(8,128)S(1)}, f32[21,1,16,128]{3,2,1,0:T(8,128)S(1)}, u32[]{:S(2)}, u32[]{:S(2)}) collective-permute-start(f32[21,1,16,128]{3,2,1,0:T(8,128)S(1)} %get-tuple-element.186), channel_id=1, source_target_pairs={{2,0},{4,2},{6,4},{8,6},{10,8},{12,10},{14,12},{16,14},{18,16},{20... | collective-permute-start | bytes 516104 | tf_op jit(solution)/shard_map/ppermute | solution.py:292
  41.3 4.7 %collective-permute-start.8 = (f32[8]{0:T(128)S(1)}, f32[8]{0:T(128)S(1)}, u32[]{:S(2)}, u32[]{:S(2)}) collective-permute-start(f32[8]{0:T(128)S(1)} %slice_reduce_fusion.1), channel_id=1, source_target_pairs={{0,28},{2,30},{4,0},{6,2},{8,4},{10,6},{12,8},{14,10},{16,12},{18,... | collective-permute-start | bytes 104 | tf_op jit(solution)/shard_map/ppermute | solution.py:295
  46.1 1.5 %collective-permute-done.7 = f32[8]{0:T(128)S(1)} collective-permute-done((f32[8]{0:T(128)S(1)}, f32[8]{0:T(128)S(1)}, u32[]{:S(2)}, u32[]{:S(2)}) %collective-permute-start.7) | collective-permute-done | bytes 64 | tf_op jit(solution)/shard_map/ppermute | solution.py:295
  47.7 0.2 fusion.14
  47.9 0.4 copy-done.8
  48.3 0.1 fusion.91
  48.4 1.4 %collective-permute-done.9.rows_ref = f32[21,10,2,128]{3,2,1,0:T(2,128)S(1)} collective-permute-done((f32[21,10,2,128]{3,2,1,0:T(2,128)S(1)}, f32[21,10,2,128]{3,2,1,0:T(2,128)S(1)}, u32[]{:S(2)}, u32[]{:S(2)}) %collective-permute-start.9) | collective-permute-done | bytes 215072 | tf_op jit(solution)/shard_map/ppermute | solution.py:286
  49.8 0.1 fusion.32
  50.0 0.6 fusion.72.strength_ref
  50.6 5.2 %shard_map.106 = (f32[19,8,16,128]{3,2,1,0:T(8,128)}, f32[3,8,16,128]{3,2,1,0:T(8,128)}, f32[8,128]{1,0:T(8,128)}) custom-call(f32[8]{0:T(128)} %fusion.72.strength_ref, f32[19,8,16,128]{3,2,1,0:T(8,128)} %get-tuple-element.132.inner_ref, f32[21,1,16,128]{3,2,1,0:T(8,128)} %copy-done.8, f32[21,1,16,128]{3,2,1,0:T(8,128)} %copy-done.9, ...), custom_call_target="tpu_custom_call" | custom-call | flops 6912000 | bytes 3735552 | tf_op jit(solution)/shard_map/pallas_call | solution.py:201
  55.8 1.1 %fusion.76 = (f32[19,1,16,128]{3,2,1,0:T(8,128)S(1)}, f32[19,1,16,128]{3,2,1,0:T(8,128)S(1)}) fusion(f32[19,8,16,128]{3,2,1,0:T(8,128)} %get-tuple-element.135.inner_ref), kind=kLoop, calls=%fused_computation.171 | loop fusion | bytes 622592 | tf_op jit(solution)/shard_map/slice | solution.py:276
  56.9 0.8 %slice_reduce_fusion = f32[8]{0:T(128)S(1)} fusion(f32[8,128]{1,0:T(8,128)} %get-tuple-element.134), kind=kLoop, calls=%fused_computation.114 | loop fusion | bytes 64 | tf_op jit(solution)/shard_map/slice | solution.py:423
  57.8 5.6 %collective-permute-start.11 = (f32[21,1,16,128]{3,2,1,0:T(8,128)S(1)}, f32[21,1,16,128]{3,2,1,0:T(8,128)S(1)}, u32[]{:S(2)}, u32[]{:S(2)}) collective-permute-start(f32[21,1,16,128]{3,2,1,0:T(8,128)S(1)} %get-tuple-element.184), channel_id=1, source_target_pairs={{2,0},{4,2},{6,4},{8,6},{10,8},{12,10},{14,12},{16,14},{18,16},{20... | collective-permute-start | bytes 516104 | tf_op jit(solution)/shard_map/ppermute | solution.py:292
  63.4 4.7 %collective-permute-start.13 = (f32[8]{0:T(128)S(1)}, f32[8]{0:T(128)S(1)}, u32[]{:S(2)}, u32[]{:S(2)}) collective-permute-start(f32[8]{0:T(128)S(1)} %slice_reduce_fusion), channel_id=1, source_target_pairs={{0,28},{2,30},{4,0},{6,2},{8,4},{10,6},{12,8},{14,10},{16,12},{18,... | collective-permute-start | bytes 104 | tf_op jit(solution)/shard_map/ppermute | solution.py:295
  68.2 1.5 %collective-permute-done.12 = f32[8]{0:T(128)S(1)} collective-permute-done((f32[8]{0:T(128)S(1)}, f32[8]{0:T(128)S(1)}, u32[]{:S(2)}, u32[]{:S(2)}) %collective-permute-start.12) | collective-permute-done | bytes 64 | tf_op jit(solution)/shard_map/ppermute | solution.py:295
  69.8 0.2 fusion.9
  70.0 0.4 copy-done.6
  70.5 1.4 %collective-permute-done.14.rows_ref = f32[21,10,2,128]{3,2,1,0:T(2,128)S(1)} collective-permute-done((f32[21,10,2,128]{3,2,1,0:T(2,128)S(1)}, f32[21,10,2,128]{3,2,1,0:T(2,128)S(1)}, u32[]{:S(2)}, u32[]{:S(2)}) %collective-permute-start.14) | collective-permute-done | bytes 215072 | tf_op jit(solution)/shard_map/ppermute | solution.py:286
  72.0 0.7 fusion.26
  72.7 0.5 fusion.73.strength_ref
  73.2 4.9 %shard_map.107 = f32[19,8,16,128]{3,2,1,0:T(8,128)} custom-call(f32[8]{0:T(128)} %fusion.73.strength_ref, f32[19,8,16,128]{3,2,1,0:T(8,128)} %get-tuple-element.135.inner_ref, f32[21,1,16,128]{3,2,1,0:T(8,128)} %copy-done.6, f32[21,1,16,128]{3,2,1,0:T(8,128)} %copy-done.7, f32[21,10,2,128]{3,2,1,0:T(2,128)} %copy-done.12, ...), custom_call_target="tpu_custom_call" | custom-call | flops 6912000 | bytes 3735552 | tf_op jit(solution)/shard_map/pallas_call | solution.py:201
  (104 shorter events, 1.3 us)
Async XLA Ops:
  2.5 11.3 %copy-start = (f32[19,8,16,128]{3,2,1,0:T(8,128)S(1)}, f32[19,8,16,128]{3,2,1,0:T(8,128)}, u32[]{:S(2)}) copy-start(f32[19,8,16,128]{3,2,1,0:T(8,128)} %inner_ref.1) | copy-start | bytes 3735556
  4.5 9.4 %copy-start.3 = (f32[8,16,128]{2,1,0:T(8,128)S(1)}, f32[8,16,128]{2,1,0:T(8,128)}, u32[]{:S(2)}) copy-start(f32[8,16,128]{2,1,0:T(8,128)} %param.35) | copy-start | bytes 196612
  4.5 15.1 %copy-start.18 = (s32[16,3]{0,1:T(4,128)S(1)}, s32[16,3]{0,1:T(4,128)}, u32[]{:S(2)}) copy-start(s32[16,3]{0,1:T(4,128)} %param.39) | copy-start | bytes 580
  4.5 15.4 %copy-start.19 = (f32[16]{0:T(128)S(1)}, f32[16]{0:T(128)}, u32[]{:S(2)}) copy-start(f32[16]{0:T(128)} %param.40) | copy-start | bytes 196
  7.7 16.0 %collective-permute-start.2 = (f32[8]{0:T(128)S(1)}, f32[8]{0:T(128)S(1)}, u32[]{:S(2)}, u32[]{:S(2)}) collective-permute-start(f32[8]{0:T(128)S(1)} %slice_reduce_fusion.2), channel_id=1, source_target_pairs={{0,4},{2,6},{4,8},{6,10},{8,12},{10,14},{12,16},{14,18},{16,20},{1... | collective-permute-start | bytes 104 | tf_op jit(solution)/shard_map/ppermute | solution.py:295
  10.7 13.0 %collective-permute-start.3 = (f32[8]{0:T(128)S(1)}, f32[8]{0:T(128)S(1)}, u32[]{:S(2)}, u32[]{:S(2)}) collective-permute-start(f32[8]{0:T(128)S(1)} %slice_reduce_fusion.2), channel_id=1, source_target_pairs={{0,28},{2,30},{4,0},{6,2},{8,4},{10,6},{12,8},{14,10},{16,12},{18,... | collective-permute-start | bytes 104 | tf_op jit(solution)/shard_map/ppermute | solution.py:295
  13.9 9.8 %collective-permute-start = (f32[22,1,16,128]{3,2,1,0:T(8,128)S(1)}, f32[22,1,16,128]{3,2,1,0:T(8,128)S(1)}, u32[]{:S(2)}, u32[]{:S(2)}) collective-permute-start(f32[22,1,16,128]{3,2,1,0:T(8,128)S(1)} %get-tuple-element.193), channel_id=1, source_target_pairs={{0,2},{2,4},{4,6},{6,8},{8,10},{10,12},{12,14},{14,16},{16,18},{18... | collective-permute-start | bytes 540680 | tf_op jit(solution)/shard_map/ppermute | solution.py:291
  15.6 8.1 %collective-permute-start.1 = (f32[22,1,16,128]{3,2,1,0:T(8,128)S(1)}, f32[22,1,16,128]{3,2,1,0:T(8,128)S(1)}, u32[]{:S(2)}, u32[]{:S(2)}) collective-permute-start(f32[22,1,16,128]{3,2,1,0:T(8,128)S(1)} %get-tuple-element.194), channel_id=1, source_target_pairs={{2,0},{4,2},{6,4},{8,6},{10,8},{12,10},{14,12},{16,14},{18,16},{20... | collective-permute-start | bytes 540680 | tf_op jit(solution)/shard_map/ppermute | solution.py:292
  23.7 0.7 copy-start.4
  23.7 0.7 copy-start.5
  23.8 2.2 %copy-start.13 = (f32[3,8,16,128]{3,2,1,0:T(8,128)S(1)}, f32[3,8,16,128]{3,2,1,0:T(8,128)}, u32[]{:S(2)}) copy-start(f32[3,8,16,128]{3,2,1,0:T(8,128)} %get-tuple-element.133) | copy-start | bytes 589828
  24.4 1.5 %collective-permute-start.4 = (f32[22,10,2,128]{3,2,1,0:T(2,128)S(1)}, f32[22,10,2,128]{3,2,1,0:T(2,128)S(1)}, u32[]{:S(2)}, u32[]{:S(2)}) collective-permute-start(f32[22,10,2,128]{3,2,1,0:T(2,128)S(1)} %fusion.3), channel_id=1, source_target_pairs={{0,1},{1,0},{2,3},{3,2},{4,5},{5,4},{6,7},{7,6},{8,9},{9,8},{10,11... | collective-permute-start | bytes 675848 | tf_op jit(solution)/shard_map/ppermute | solution.py:286
  25.9 2.0 %copy-start.10 = (f32[22,10,2,128]{3,2,1,0:T(2,128)}, f32[22,10,2,128]{3,2,1,0:T(2,128)S(1)}, u32[]{:S(2)}) copy-start(f32[22,10,2,128]{3,2,1,0:T(2,128)S(1)} %collective-permute-done.4.rows_ref) | copy-start | bytes 675844
  25.9 2.0 %copy-start.16 = (f32[8]{0:T(128)S(1)}, f32[8]{0:T(128)}, u32[]{:S(2)}) copy-start(f32[8]{0:T(128)} %param.37) | copy-start | bytes 100
  26.0 2.0 %copy-start.17 = (f32[8]{0:T(128)S(1)}, f32[8]{0:T(128)}, u32[]{:S(2)}) copy-start(f32[8]{0:T(128)} %param.38) | copy-start | bytes 100
  33.7 14.0 %copy-start.1 = (f32[19,8,16,128]{3,2,1,0:T(8,128)S(1)}, f32[19,8,16,128]{3,2,1,0:T(8,128)}, u32[]{:S(2)}) copy-start(f32[19,8,16,128]{3,2,1,0:T(8,128)} %get-tuple-element.132.inner_ref) | copy-start | bytes 3735556
  35.7 11.9 %collective-permute-start.5 = (f32[21,1,16,128]{3,2,1,0:T(8,128)S(1)}, f32[21,1,16,128]{3,2,1,0:T(8,128)S(1)}, u32[]{:S(2)}, u32[]{:S(2)}) collective-permute-start(f32[21,1,16,128]{3,2,1,0:T(8,128)S(1)} %get-tuple-element.185), channel_id=1, source_target_pairs={{0,2},{2,4},{4,6},{6,8},{8,10},{10,12},{12,14},{14,16},{16,18},{18... | collective-permute-start | bytes 516104 | tf_op jit(solution)/shard_map/ppermute | solution.py:291
  37.4 10.2 %collective-permute-start.6 = (f32[21,1,16,128]{3,2,1,0:T(8,128)S(1)}, f32[21,1,16,128]{3,2,1,0:T(8,128)S(1)}, u32[]{:S(2)}, u32[]{:S(2)}) collective-permute-start(f32[21,1,16,128]{3,2,1,0:T(8,128)S(1)} %get-tuple-element.186), channel_id=1, source_target_pairs={{2,0},{4,2},{6,4},{8,6},{10,8},{12,10},{14,12},{16,14},{18,16},{20... | collective-permute-start | bytes 516104 | tf_op jit(solution)/shard_map/ppermute | solution.py:292
  41.3 6.2 %collective-permute-start.7 = (f32[8]{0:T(128)S(1)}, f32[8]{0:T(128)S(1)}, u32[]{:S(2)}, u32[]{:S(2)}) collective-permute-start(f32[8]{0:T(128)S(1)} %slice_reduce_fusion.1), channel_id=1, source_target_pairs={{0,4},{2,6},{4,8},{6,10},{8,12},{10,14},{12,16},{14,18},{16,20},{1... | collective-permute-start | bytes 104 | tf_op jit(solution)/shard_map/ppermute | solution.py:295
  41.3 6.2 %collective-permute-start.8 = (f32[8]{0:T(128)S(1)}, f32[8]{0:T(128)S(1)}, u32[]{:S(2)}, u32[]{:S(2)}) collective-permute-start(f32[8]{0:T(128)S(1)} %slice_reduce_fusion.1), channel_id=1, source_target_pairs={{0,28},{2,30},{4,0},{6,2},{8,4},{10,6},{12,8},{14,10},{16,12},{18,... | collective-permute-start | bytes 104 | tf_op jit(solution)/shard_map/ppermute | solution.py:295
  47.6 0.7 copy-start.8
  47.6 0.7 copy-start.9
  47.7 2.1 %copy-start.15 = (f32[3,8,16,128]{3,2,1,0:T(8,128)S(1)}, f32[3,8,16,128]{3,2,1,0:T(8,128)}, u32[]{:S(2)}) copy-start(f32[3,8,16,128]{3,2,1,0:T(8,128)} %get-tuple-element.136) | copy-start | bytes 589828
  48.3 1.5 %collective-permute-start.9 = (f32[21,10,2,128]{3,2,1,0:T(2,128)S(1)}, f32[21,10,2,128]{3,2,1,0:T(2,128)S(1)}, u32[]{:S(2)}, u32[]{:S(2)}) collective-permute-start(f32[21,10,2,128]{3,2,1,0:T(2,128)S(1)} %fusion.14), channel_id=1, source_target_pairs={{0,1},{1,0},{2,3},{3,2},{4,5},{5,4},{6,7},{7,6},{8,9},{9,8},{10,11... | collective-permute-start | bytes 645128 | tf_op jit(solution)/shard_map/ppermute | solution.py:286
  49.8 0.8 copy-start.11
  55.8 14.0 %copy-start.2 = (f32[19,8,16,128]{3,2,1,0:T(8,128)S(1)}, f32[19,8,16,128]{3,2,1,0:T(8,128)}, u32[]{:S(2)}) copy-start(f32[19,8,16,128]{3,2,1,0:T(8,128)} %get-tuple-element.135.inner_ref) | copy-start | bytes 3735556
  57.8 11.9 %collective-permute-start.10 = (f32[21,1,16,128]{3,2,1,0:T(8,128)S(1)}, f32[21,1,16,128]{3,2,1,0:T(8,128)S(1)}, u32[]{:S(2)}, u32[]{:S(2)}) collective-permute-start(f32[21,1,16,128]{3,2,1,0:T(8,128)S(1)} %get-tuple-element.183), channel_id=1, source_target_pairs={{0,2},{2,4},{4,6},{6,8},{8,10},{10,12},{12,14},{14,16},{16,18},{18... | collective-permute-start | bytes 516104 | tf_op jit(solution)/shard_map/ppermute | solution.py:291
  57.8 11.9 %collective-permute-start.11 = (f32[21,1,16,128]{3,2,1,0:T(8,128)S(1)}, f32[21,1,16,128]{3,2,1,0:T(8,128)S(1)}, u32[]{:S(2)}, u32[]{:S(2)}) collective-permute-start(f32[21,1,16,128]{3,2,1,0:T(8,128)S(1)} %get-tuple-element.184), channel_id=1, source_target_pairs={{2,0},{4,2},{6,4},{8,6},{10,8},{12,10},{14,12},{16,14},{18,16},{20... | collective-permute-start | bytes 516104 | tf_op jit(solution)/shard_map/ppermute | solution.py:292
  63.4 6.2 %collective-permute-start.12 = (f32[8]{0:T(128)S(1)}, f32[8]{0:T(128)S(1)}, u32[]{:S(2)}, u32[]{:S(2)}) collective-permute-start(f32[8]{0:T(128)S(1)} %slice_reduce_fusion), channel_id=1, source_target_pairs={{0,4},{2,6},{4,8},{6,10},{8,12},{10,14},{12,16},{14,18},{16,20},{1... | collective-permute-start | bytes 104 | tf_op jit(solution)/shard_map/ppermute | solution.py:295
  63.4 6.2 %collective-permute-start.13 = (f32[8]{0:T(128)S(1)}, f32[8]{0:T(128)S(1)}, u32[]{:S(2)}, u32[]{:S(2)}) collective-permute-start(f32[8]{0:T(128)S(1)} %slice_reduce_fusion), channel_id=1, source_target_pairs={{0,28},{2,30},{4,0},{6,2},{8,4},{10,6},{12,8},{14,10},{16,12},{18,... | collective-permute-start | bytes 104 | tf_op jit(solution)/shard_map/ppermute | solution.py:295
  69.7 0.7 copy-start.6
  69.7 0.7 copy-start.7
  69.8 2.1 %copy-start.14 = (f32[3,8,16,128]{3,2,1,0:T(8,128)S(1)}, f32[3,8,16,128]{3,2,1,0:T(8,128)}, u32[]{:S(2)}) copy-start(f32[3,8,16,128]{3,2,1,0:T(8,128)} %get-tuple-element.137) | copy-start | bytes 589828
  70.4 1.5 %collective-permute-start.14 = (f32[21,10,2,128]{3,2,1,0:T(2,128)S(1)}, f32[21,10,2,128]{3,2,1,0:T(2,128)S(1)}, u32[]{:S(2)}, u32[]{:S(2)}) collective-permute-start(f32[21,10,2,128]{3,2,1,0:T(2,128)S(1)} %fusion.9), channel_id=1, source_target_pairs={{0,1},{1,0},{2,3},{3,2},{4,5},{5,4},{6,7},{7,6},{8,9},{9,8},{10,11... | collective-permute-start | bytes 645128 | tf_op jit(solution)/shard_map/ppermute | solution.py:286
  71.9 1.3 %copy-start.12 = (f32[21,10,2,128]{3,2,1,0:T(2,128)}, f32[21,10,2,128]{3,2,1,0:T(2,128)S(1)}, u32[]{:S(2)}) copy-start(f32[21,10,2,128]{3,2,1,0:T(2,128)S(1)} %collective-permute-done.14.rows_ref) | copy-start | bytes 645124

commit v16 on v15

--- a/solution.py
+++ b/solution.py
@@ -79,7 +79,7 @@
     with_moments, strength_ref, inner_ref, low_ref, high_ref, rows_ref, discs_ref, solid_ref, *rest
 ):
     if with_moments:
-        out_ref, velocity_ref, flow_ref, posts_ref, sums_ref = rest
+        out_ref, velocity_ref, flow_ref, head_ref, tail_ref, posts_ref, sums_ref = rest
     else:
         out_ref, posts_ref = rest
     fans = discs_ref.shape[0]
@@ -138,6 +138,9 @@
         elif shift_z == -1:
             piece = jnp.where(lane == height - 1, 0.0, pltpu.roll(piece, height - 1, 2))
         out_ref[which] = piece
+        if with_moments:
+            head_ref[which] = piece[0:1]
+            tail_ref[which] = piece[slab_len - 1 : slab_len]
     if not with_moments:
         return
     moments_into(out_ref, discs_ref, 1, velocity_ref, flow_ref, sums_ref)
@@ -194,6 +197,8 @@
     if with_moments:
         out_shape.append(jax.ShapeDtypeStruct((3, slab_len, band_width, height), jnp.float32))
         out_shape.append(jax.ShapeDtypeStruct((fans, height), jnp.float32))
+        out_shape.append(jax.ShapeDtypeStruct((19, 1, band_width, height), jnp.float32))
+        out_shape.append(jax.ShapeDtypeStruct((19, 1, band_width, height), jnp.float32))
     scratch = [pltpu.VMEM((19, slab_len + 2, band_width + 2, height), jnp.float32)]
     if with_moments:
         scratch.append(pltpu.VMEM((fans, band_width, height), jnp.float32))
@@ -267,13 +272,15 @@
     return jnp.concatenate([field[..., 1:], zero_layer], axis=-1)
 
 
-def rim_round(fields, flow, axis, dim, reach):
+def rim_round(fields, flow, axis, dim, reach, edges=None):
     count = lax.axis_size(axis)
     fans = flow.shape[0]
     channels = [field.shape[0] for field in fields]
 
     def piece(start):
         cells = [lax.slice_in_dim(field, start, start + 1, axis=dim) for field in fields]
+        if edges is not None:
+            cells[0] = edges[0] if start == 0 else edges[1]
         carrier = jnp.zeros(cells[0].shape[1:], jnp.float32).at[0, 0, :fans].set(flow)[None]
         return jnp.concatenate(cells + [carrier], axis=0)
 
@@ -375,11 +382,12 @@
     ).astype(jnp.float32)
     velocity, flow = first_moments(populations, inner_discs)
     partials = flow[:, 0]
+    edges = None
     for repeat in range(ITERS):
         fields = [populations, smoke_field[None]]
         if repeat == 0:
             fields.append(solid_flag.astype(jnp.float32)[None])
-        fields, totals = rim_round(fields, partials, "len", 1, len_reach)
+        fields, totals = rim_round(fields, partials, "len", 1, len_reach, edges)
         low, high, _ = fields[0]
         fields[0] = jnp.concatenate([low[:19], populations, high[:19]], axis=1)
         fields, totals = rim_round(fields, totals, "band", 2, band_reach)
@@ -421,6 +429,7 @@
         if not last:
             velocity = stepped[1]
             partials = stepped[2][:, 0]
+            edges = (stepped[3], stepped[4])
     return (populations, smoke_field)
 
 

time: 78.5 us -> 78.7 us (level)
  local copies, waits for them, and re-layouts: 7.31 us -> 5.3 us
  other arithmetic: 8.25 us -> 10.2 us
    slice x7 -> x5, local copies, waits for them, and re-layouts: 2.27 us -> 0.04 us  [piece(): lax.slice_in_dim(field, start, start + 1, axis=dim)]
    concatenate x3, other arithmetic: 0.12 us -> 2.06 us  [piece(): return jnp.concatenate(cells + [carrier], axis=0)]
where the time goes in v16:
time: 78.7 us; the launch traced here: 78.3 us
  starting transfers between devices  32.6 us (41%)
  Pallas kernels  18 us (23%)
  waiting for transfers between devices  10.8 us (14%)
  other arithmetic  10.2 us (13%)
  local copies, waits for them, and re-layouts  5.3 us (7%)
  between operations  1.17 us (1%)
    ppermute x6, starting transfers between devices, rim_round(): lax.ppermute(flow, axis, [(i, (i + offset) % count) for i in range(count)])  15.6 us
    pallas_call x3, Pallas kernels, lattice_step(): pl.pallas_call(functools.partial(step_kernel, with_moments), out_shape=tu...  15.5 us
    ppermute x3, starting transfers between devices, rim_round(): from_right = lax.ppermute(head, axis, backward)  13.6 us
    ppermute x3, waiting for transfers between devices, rim_round(): both = lax.ppermute(jnp.concatenate([tail, head], axis=dim), axis, forward)  4.17 us
    ppermute x3, waiting for transfers between devices, rim_round(): from_left = lax.ppermute(tail, axis, forward)  3.6 us
    ppermute x3, starting transfers between devices, rim_round(): from_left = lax.ppermute(tail, axis, forward)  3.41 us
    ppermute x6, waiting for transfers between devices, rim_round(): lax.ppermute(flow, axis, [(i, (i + offset) % count) for i in range(count)])  3.04 us
    pallas_call x1, Pallas kernels, first_moments(): pl.pallas_call(lambda populations_ref, discs_ref, velocity_ref, flow_ref,...  2.45 us
  transfers between devices with their start and end apart: 15, of which 6 were waited for; matrix products, arithmetic and copies ran while one was open for 1% of the time, Pallas kernels for 0%

profile of v16, /device:TPU:0, one launch (start us, length us, event | category | flops | bytes accessed | tf_op | source)
XLA Modules:
  0.0 78.3 jit_solution(9072397610886581793)
XLA Ops:
  0.6 0.8 %slice_bitcast_fusion.12 = (s32[8]{0:T(128)S(1)}, s32[8]{0:T(128)S(1)}, s32[8]{0:T(128)S(1)}) fusion(s32[8,3]{0,1:T(4,128)} %param.36), kind=kLoop, calls=%fused_computation.163 | loop fusion | bytes 192 | tf_op jit(solution)/shard_map/sub | solution.py:366
  1.5 0.7 and_select_fusion
  2.2 0.1 add_compare_fusion
  2.4 0.1 fusion.42
  2.5 1.0 %convert_bitcast_fusion = (f32[1,8,16,128]{3,2,1,0:T(8,128)S(1)}, pred[8,16,128]{2,1,0:T(8,128)(4,1)S(1)}) fusion(s32[8,16,128]{2,1,0:T(8,128)} %param.34), kind=kLoop, calls=%fused_computation.95 | loop fusion | flops 32768 | bytes 147456 | tf_op jit(solution)/shard_map/broadcast_in_dim | solution.py:389
  3.5 0.9 %and_convert_fusion.1.discs_ref = f32[8,8,16,128]{3,2,1,0:T(8,128)} fusion(pred[8,16,128]{2,1,0:T(8,128)(4,1)S(1)} %not.3, pred[8,16,128]{2,1,0:T(8,128)(4,1)S(1)} %slice.612, pred[8,8]{1,0:T(8,128)(4,1)S(1)} %slice.517), kind=kLoop, calls=%fused_computation.1 | loop fusion | flops 393216 | bytes 557120 | tf_op jit(solution)/shard_map/convert_element_type | solution.py:382
  4.5 2.5 %shard_map.104 = (f32[3,8,16,128]{3,2,1,0:T(8,128)}, f32[8,128]{1,0:T(8,128)}) custom-call(f32[19,8,16,128]{3,2,1,0:T(8,128)} %inner_ref.1, f32[8,8,16,128]{3,2,1,0:T(8,128)} %and_convert_fusion.1.discs_ref), custom_call_target="tpu_custom_call" | custom-call | flops 983040 | bytes 1245184 | tf_op jit(solution)/shard_map/pallas_call | solution.py:174
  6.9 0.8 %slice_reduce_fusion.2 = f32[8]{0:T(128)S(1)} fusion(f32[8,128]{1,0:T(8,128)} %get-tuple-element.134), kind=kLoop, calls=%fused_computation.118 | loop fusion | bytes 64 | tf_op jit(solution)/shard_map/slice | solution.py:384
  7.7 3.0 %collective-permute-start.2 = (f32[8]{0:T(128)S(1)}, f32[8]{0:T(128)S(1)}, u32[]{:S(2)}, u32[]{:S(2)}) collective-permute-start(f32[8]{0:T(128)S(1)} %slice_reduce_fusion.2), channel_id=1, source_target_pairs={{0,4},{2,6},{4,8},{6,10},{8,12},{10,14},{12,16},{14,18},{16,20},{1... | collective-permute-start | bytes 104 | tf_op jit(solution)/shard_map/ppermute | solution.py:302
  10.7 3.1 %collective-permute-start.3 = (f32[8]{0:T(128)S(1)}, f32[8]{0:T(128)S(1)}, u32[]{:S(2)}, u32[]{:S(2)}) collective-permute-start(f32[8]{0:T(128)S(1)} %slice_reduce_fusion.2), channel_id=1, source_target_pairs={{0,28},{2,30},{4,0},{6,2},{8,4},{10,6},{12,8},{14,10},{16,12},{18,... | collective-permute-start | bytes 104 | tf_op jit(solution)/shard_map/ppermute | solution.py:302
  13.9 1.6 %collective-permute-start = (f32[22,1,16,128]{3,2,1,0:T(8,128)S(1)}, f32[22,1,16,128]{3,2,1,0:T(8,128)S(1)}, u32[]{:S(2)}, u32[]{:S(2)}) collective-permute-start(f32[22,1,16,128]{3,2,1,0:T(8,128)S(1)} %get-tuple-element.197), channel_id=1, source_target_pairs={{0,2},{2,4},{4,6},{6,8},{8,10},{10,12},{12,14},{14,16},{16,18},{18... | collective-permute-start | bytes 540680 | tf_op jit(solution)/shard_map/ppermute | solution.py:298
  15.6 4.0 %collective-permute-start.1 = (f32[22,1,16,128]{3,2,1,0:T(8,128)S(1)}, f32[22,1,16,128]{3,2,1,0:T(8,128)S(1)}, u32[]{:S(2)}, u32[]{:S(2)}) collective-permute-start(f32[22,1,16,128]{3,2,1,0:T(8,128)S(1)} %get-tuple-element.198), channel_id=1, source_target_pairs={{2,0},{4,2},{6,4},{8,6},{10,8},{12,10},{14,12},{16,14},{18,16},{20... | collective-permute-start | bytes 540680 | tf_op jit(solution)/shard_map/ppermute | solution.py:299
  19.7 0.1 broadcast_multiply_fusion
  19.9 0.2 fusion.19
  20.1 3.6 %collective-permute-done.low_ref = f32[22,1,16,128]{3,2,1,0:T(8,128)S(1)} collective-permute-done((f32[22,1,16,128]{3,2,1,0:T(8,128)S(1)}, f32[22,1,16,128]{3,2,1,0:T(8,128)S(1)}, u32[]{:S(2)}, u32[]{:S(2)}) %collective-permute-start) | collective-permute-done | bytes 180256 | tf_op jit(solution)/shard_map/ppermute | solution.py:298
  23.8 0.2 fusion.3
  24.0 0.3 copy-done.4
  24.4 0.1 fusion.91
  24.5 1.4 %collective-permute-done.4.rows_ref = f32[22,10,2,128]{3,2,1,0:T(2,128)S(1)} collective-permute-done((f32[22,10,2,128]{3,2,1,0:T(2,128)S(1)}, f32[22,10,2,128]{3,2,1,0:T(2,128)S(1)}, u32[]{:S(2)}, u32[]{:S(2)}) %collective-permute-start.4) | collective-permute-done | bytes 225312 | tf_op jit(solution)/shard_map/ppermute | solution.py:293
  26.0 0.1 fusion.38
  26.1 0.7 maximum_bitcast_fusion.solid_ref
  26.8 1.1 %and_convert_fusion.discs_ref = f32[8,10,18,128]{3,2,1,0:T(8,128)} fusion(pred[10,18,128]{2,1,0:T(8,128)(4,1)S(1)} %maximum_compare_fusion, pred[8,18,128]{2,1,0:T(8,128)(4,1)S(1)} %add_compare_fusion, pred[8,10]{1,0:T(8,128)(4,1)S(1)} %fusion.42), kind=kLoop, calls=%fused_computation | loop fusion | flops 552960 | bytes 778832 | tf_op jit(solution)/shard_map/convert_element_type | solution.py:402
  28.0 0.6 fusion.71.strength_ref
  28.5 5.3 %shard_map.105 = (f32[19,8,16,128]{3,2,1,0:T(8,128)}, f32[3,8,16,128]{3,2,1,0:T(8,128)}, f32[8,128]{1,0:T(8,128)}, f32[19,1,16,128]{3,2,1,0:T(8,128)}, f32[19,1,16,128]{3,2,1,0:T(8,128)}) custom-call(f32[8]{0:T(128)} %fusion.71.strength_ref, f32[19,8,16,128]{3,2,1,0:T(8,128)} %inner_ref.1, f32[22,1,16,128]{3,2,1,0:T(8,128)} %copy-done.4, ...), custom_call_target="tpu_custom_call" | custom-call | flops 6912000 | bytes 3735552 | tf_op jit(solution)/shard_map/pallas_call | solution.py:206
  33.8 0.9 %slice_reduce_fusion.1 = f32[8]{0:T(128)S(1)} fusion(f32[8,128]{1,0:T(8,128)} %get-tuple-element.135), kind=kLoop, calls=%fused_computation.117 | loop fusion | bytes 64 | tf_op jit(solution)/shard_map/slice | solution.py:431
  34.7 1.0 %pad_maximum_fusion.1 = (f32[21,1,16,128]{3,2,1,0:T(8,128)S(1)}, f32[21,1,16,128]{3,2,1,0:T(8,128)S(1)}) fusion(f32[1,1,16,128]{3,2,1,0:T(8,128)S(1)} %pad_bitcast_fusion.1, f32[1,1,16,128]{3,2,1,0:T(8,128)S(1)} %get-tuple-element.179, f32[19,1,16,128]{3,2,1,0:T(8,128)} %get-tuple-element.136, f32[1,1,16,128]{3,2,1,0:T(8,128)S(1)} %get-tuple-element.180, ...), kind=kLoop, calls=%fused_computation.3 | loop fusion | flops 172032 | bytes 679936 | tf_op jit(solution)/shard_map/concatenate | solution.py:285
  35.7 1.7 %collective-permute-start.5 = (f32[21,1,16,128]{3,2,1,0:T(8,128)S(1)}, f32[21,1,16,128]{3,2,1,0:T(8,128)S(1)}, u32[]{:S(2)}, u32[]{:S(2)}) collective-permute-start(f32[21,1,16,128]{3,2,1,0:T(8,128)S(1)} %get-tuple-element.189), channel_id=1, source_target_pairs={{0,2},{2,4},{4,6},{6,8},{8,10},{10,12},{12,14},{14,16},{16,18},{18... | collective-permute-start | bytes 516104 | tf_op jit(solution)/shard_map/ppermute | solution.py:298
  37.4 4.0 %collective-permute-start.6 = (f32[21,1,16,128]{3,2,1,0:T(8,128)S(1)}, f32[21,1,16,128]{3,2,1,0:T(8,128)S(1)}, u32[]{:S(2)}, u32[]{:S(2)}) collective-permute-start(f32[21,1,16,128]{3,2,1,0:T(8,128)S(1)} %get-tuple-element.190), channel_id=1, source_target_pairs={{2,0},{4,2},{6,4},{8,6},{10,8},{12,10},{14,12},{16,14},{18,16},{20... | collective-permute-start | bytes 516104 | tf_op jit(solution)/shard_map/ppermute | solution.py:299
  41.4 4.7 %collective-permute-start.8 = (f32[8]{0:T(128)S(1)}, f32[8]{0:T(128)S(1)}, u32[]{:S(2)}, u32[]{:S(2)}) collective-permute-start(f32[8]{0:T(128)S(1)} %slice_reduce_fusion.1), channel_id=1, source_target_pairs={{0,28},{2,30},{4,0},{6,2},{8,4},{10,6},{12,8},{14,10},{16,12},{18,... | collective-permute-start | bytes 104 | tf_op jit(solution)/shard_map/ppermute | solution.py:302
  46.1 1.5 %collective-permute-done.7 = f32[8]{0:T(128)S(1)} collective-permute-done((f32[8]{0:T(128)S(1)}, f32[8]{0:T(128)S(1)}, u32[]{:S(2)}, u32[]{:S(2)}) %collective-permute-start.7) | collective-permute-done | bytes 64 | tf_op jit(solution)/shard_map/ppermute | solution.py:302
  47.8 0.2 fusion.14
  48.0 0.4 copy-done.8
  48.4 0.1 fusion.89
  48.5 1.4 %collective-permute-done.9.rows_ref = f32[21,10,2,128]{3,2,1,0:T(2,128)S(1)} collective-permute-done((f32[21,10,2,128]{3,2,1,0:T(2,128)S(1)}, f32[21,10,2,128]{3,2,1,0:T(2,128)S(1)}, u32[]{:S(2)}, u32[]{:S(2)}) %collective-permute-start.9) | collective-permute-done | bytes 215072 | tf_op jit(solution)/shard_map/ppermute | solution.py:293
  49.9 0.1 fusion.32
  50.1 0.5 fusion.72.strength_ref
  50.6 5.4 %shard_map.106 = (f32[19,8,16,128]{3,2,1,0:T(8,128)}, f32[3,8,16,128]{3,2,1,0:T(8,128)}, f32[8,128]{1,0:T(8,128)}, f32[19,1,16,128]{3,2,1,0:T(8,128)}, f32[19,1,16,128]{3,2,1,0:T(8,128)}) custom-call(f32[8]{0:T(128)} %fusion.72.strength_ref, f32[19,8,16,128]{3,2,1,0:T(8,128)} %get-tuple-element.139.inner_ref, f32[21,1,16,128]{3,2,1,0:T(8,128)} %copy-done.8, ...), custom_call_target="tpu_custom_call" | custom-call | flops 6912000 | bytes 3735552 | tf_op jit(solution)/shard_map/pallas_call | solution.py:206
  55.9 0.9 %slice_reduce_fusion = f32[8]{0:T(128)S(1)} fusion(f32[8,128]{1,0:T(8,128)} %get-tuple-element.140), kind=kLoop, calls=%fused_computation.114 | loop fusion | bytes 64 | tf_op jit(solution)/shard_map/slice | solution.py:431
  56.9 1.0 %pad_maximum_fusion.3 = (f32[21,1,16,128]{3,2,1,0:T(8,128)S(1)}, f32[21,1,16,128]{3,2,1,0:T(8,128)S(1)}) fusion(f32[1,1,16,128]{3,2,1,0:T(8,128)S(1)} %pad_bitcast_fusion, f32[1,1,16,128]{3,2,1,0:T(8,128)S(1)} %get-tuple-element.175, f32[19,1,16,128]{3,2,1,0:T(8,128)} %get-tuple-element.141, f32[1,1,16,128]{3,2,1,0:T(8,128)S(1)} %get-tuple-element.176, ...), kind=kLoop, calls=%fused_computation.5 | loop fusion | flops 172032 | bytes 679936 | tf_op jit(solution)/shard_map/concatenate | solution.py:285
  57.9 5.6 %collective-permute-start.11 = (f32[21,1,16,128]{3,2,1,0:T(8,128)S(1)}, f32[21,1,16,128]{3,2,1,0:T(8,128)S(1)}, u32[]{:S(2)}, u32[]{:S(2)}) collective-permute-start(f32[21,1,16,128]{3,2,1,0:T(8,128)S(1)} %get-tuple-element.188), channel_id=1, source_target_pairs={{2,0},{4,2},{6,4},{8,6},{10,8},{12,10},{14,12},{16,14},{18,16},{20... | collective-permute-start | bytes 516104 | tf_op jit(solution)/shard_map/ppermute | solution.py:299
  63.5 4.7 %collective-permute-start.13 = (f32[8]{0:T(128)S(1)}, f32[8]{0:T(128)S(1)}, u32[]{:S(2)}, u32[]{:S(2)}) collective-permute-start(f32[8]{0:T(128)S(1)} %slice_reduce_fusion), channel_id=1, source_target_pairs={{0,28},{2,30},{4,0},{6,2},{8,4},{10,6},{12,8},{14,10},{16,12},{18,... | collective-permute-start | bytes 104 | tf_op jit(solution)/shard_map/ppermute | solution.py:302
  68.3 1.5 %collective-permute-done.12 = f32[8]{0:T(128)S(1)} collective-permute-done((f32[8]{0:T(128)S(1)}, f32[8]{0:T(128)S(1)}, u32[]{:S(2)}, u32[]{:S(2)}) %collective-permute-start.12) | collective-permute-done | bytes 64 | tf_op jit(solution)/shard_map/ppermute | solution.py:302
  69.9 0.2 fusion.9
  70.1 0.4 copy-done.6
  70.6 1.4 %collective-permute-done.14.rows_ref = f32[21,10,2,128]{3,2,1,0:T(2,128)S(1)} collective-permute-done((f32[21,10,2,128]{3,2,1,0:T(2,128)S(1)}, f32[21,10,2,128]{3,2,1,0:T(2,128)S(1)}, u32[]{:S(2)}, u32[]{:S(2)}) %collective-permute-start.14) | collective-permute-done | bytes 215072 | tf_op jit(solution)/shard_map/ppermute | solution.py:293
  72.1 0.7 fusion.26
  72.8 0.6 fusion.73.strength_ref
  73.4 4.9 %shard_map.107 = f32[19,8,16,128]{3,2,1,0:T(8,128)} custom-call(f32[8]{0:T(128)} %fusion.73.strength_ref, f32[19,8,16,128]{3,2,1,0:T(8,128)} %get-tuple-element.144.inner_ref, f32[21,1,16,128]{3,2,1,0:T(8,128)} %copy-done.6, f32[21,1,16,128]{3,2,1,0:T(8,128)} %copy-done.7, f32[21,10,2,128]{3,2,1,0:T(2,128)} %copy-done.12, ...), custom_call_target="tpu_custom_call" | custom-call | flops 6912000 | bytes 3735552 | tf_op jit(solution)/shard_map/pallas_call | solution.py:206
  (102 shorter events, 1.2 us)
Async XLA Ops:
  2.5 11.3 %copy-start = (f32[19,8,16,128]{3,2,1,0:T(8,128)S(1)}, f32[19,8,16,128]{3,2,1,0:T(8,128)}, u32[]{:S(2)}) copy-start(f32[19,8,16,128]{3,2,1,0:T(8,128)} %inner_ref.1) | copy-start | bytes 3735556
  4.5 9.4 %copy-start.3 = (f32[8,16,128]{2,1,0:T(8,128)S(1)}, f32[8,16,128]{2,1,0:T(8,128)}, u32[]{:S(2)}) copy-start(f32[8,16,128]{2,1,0:T(8,128)} %param.35) | copy-start | bytes 196612
  4.5 15.1 %copy-start.18 = (s32[16,3]{0,1:T(4,128)S(1)}, s32[16,3]{0,1:T(4,128)}, u32[]{:S(2)}) copy-start(s32[16,3]{0,1:T(4,128)} %param.39) | copy-start | bytes 580
  4.5 15.4 %copy-start.19 = (f32[16]{0:T(128)S(1)}, f32[16]{0:T(128)}, u32[]{:S(2)}) copy-start(f32[16]{0:T(128)} %param.40) | copy-start | bytes 196
  7.7 16.0 %collective-permute-start.2 = (f32[8]{0:T(128)S(1)}, f32[8]{0:T(128)S(1)}, u32[]{:S(2)}, u32[]{:S(2)}) collective-permute-start(f32[8]{0:T(128)S(1)} %slice_reduce_fusion.2), channel_id=1, source_target_pairs={{0,4},{2,6},{4,8},{6,10},{8,12},{10,14},{12,16},{14,18},{16,20},{1... | collective-permute-start | bytes 104 | tf_op jit(solution)/shard_map/ppermute | solution.py:302
  10.7 13.0 %collective-permute-start.3 = (f32[8]{0:T(128)S(1)}, f32[8]{0:T(128)S(1)}, u32[]{:S(2)}, u32[]{:S(2)}) collective-permute-start(f32[8]{0:T(128)S(1)} %slice_reduce_fusion.2), channel_id=1, source_target_pairs={{0,28},{2,30},{4,0},{6,2},{8,4},{10,6},{12,8},{14,10},{16,12},{18,... | collective-permute-start | bytes 104 | tf_op jit(solution)/shard_map/ppermute | solution.py:302
  13.9 9.8 %collective-permute-start = (f32[22,1,16,128]{3,2,1,0:T(8,128)S(1)}, f32[22,1,16,128]{3,2,1,0:T(8,128)S(1)}, u32[]{:S(2)}, u32[]{:S(2)}) collective-permute-start(f32[22,1,16,128]{3,2,1,0:T(8,128)S(1)} %get-tuple-element.197), channel_id=1, source_target_pairs={{0,2},{2,4},{4,6},{6,8},{8,10},{10,12},{12,14},{14,16},{16,18},{18... | collective-permute-start | bytes 540680 | tf_op jit(solution)/shard_map/ppermute | solution.py:298
  15.6 8.1 %collective-permute-start.1 = (f32[22,1,16,128]{3,2,1,0:T(8,128)S(1)}, f32[22,1,16,128]{3,2,1,0:T(8,128)S(1)}, u32[]{:S(2)}, u32[]{:S(2)}) collective-permute-start(f32[22,1,16,128]{3,2,1,0:T(8,128)S(1)} %get-tuple-element.198), channel_id=1, source_target_pairs={{2,0},{4,2},{6,4},{8,6},{10,8},{12,10},{14,12},{16,14},{18,16},{20... | collective-permute-start | bytes 540680 | tf_op jit(solution)/shard_map/ppermute | solution.py:299
  23.7 0.7 copy-start.4
  23.7 0.7 copy-start.5
  23.8 2.2 %copy-start.13 = (f32[3,8,16,128]{3,2,1,0:T(8,128)S(1)}, f32[3,8,16,128]{3,2,1,0:T(8,128)}, u32[]{:S(2)}) copy-start(f32[3,8,16,128]{3,2,1,0:T(8,128)} %get-tuple-element.137) | copy-start | bytes 589828
  24.4 1.5 %collective-permute-start.4 = (f32[22,10,2,128]{3,2,1,0:T(2,128)S(1)}, f32[22,10,2,128]{3,2,1,0:T(2,128)S(1)}, u32[]{:S(2)}, u32[]{:S(2)}) collective-permute-start(f32[22,10,2,128]{3,2,1,0:T(2,128)S(1)} %fusion.3), channel_id=1, source_target_pairs={{0,1},{1,0},{2,3},{3,2},{4,5},{5,4},{6,7},{7,6},{8,9},{9,8},{10,11... | collective-permute-start | bytes 675848 | tf_op jit(solution)/shard_map/ppermute | solution.py:293
  25.9 2.1 %copy-start.10 = (f32[22,10,2,128]{3,2,1,0:T(2,128)}, f32[22,10,2,128]{3,2,1,0:T(2,128)S(1)}, u32[]{:S(2)}) copy-start(f32[22,10,2,128]{3,2,1,0:T(2,128)S(1)} %collective-permute-done.4.rows_ref) | copy-start | bytes 675844
  25.9 2.0 %copy-start.16 = (f32[8]{0:T(128)S(1)}, f32[8]{0:T(128)}, u32[]{:S(2)}) copy-start(f32[8]{0:T(128)} %param.37) | copy-start | bytes 100
  26.0 2.0 %copy-start.17 = (f32[8]{0:T(128)S(1)}, f32[8]{0:T(128)}, u32[]{:S(2)}) copy-start(f32[8]{0:T(128)} %param.38) | copy-start | bytes 100
  33.8 14.0 %copy-start.1 = (f32[19,8,16,128]{3,2,1,0:T(8,128)S(1)}, f32[19,8,16,128]{3,2,1,0:T(8,128)}, u32[]{:S(2)}) copy-start(f32[19,8,16,128]{3,2,1,0:T(8,128)} %get-tuple-element.139.inner_ref) | copy-start | bytes 3735556
  35.7 11.9 %collective-permute-start.5 = (f32[21,1,16,128]{3,2,1,0:T(8,128)S(1)}, f32[21,1,16,128]{3,2,1,0:T(8,128)S(1)}, u32[]{:S(2)}, u32[]{:S(2)}) collective-permute-start(f32[21,1,16,128]{3,2,1,0:T(8,128)S(1)} %get-tuple-element.189), channel_id=1, source_target_pairs={{0,2},{2,4},{4,6},{6,8},{8,10},{10,12},{12,14},{14,16},{16,18},{18... | collective-permute-start | bytes 516104 | tf_op jit(solution)/shard_map/ppermute | solution.py:298
  37.4 10.2 %collective-permute-start.6 = (f32[21,1,16,128]{3,2,1,0:T(8,128)S(1)}, f32[21,1,16,128]{3,2,1,0:T(8,128)S(1)}, u32[]{:S(2)}, u32[]{:S(2)}) collective-permute-start(f32[21,1,16,128]{3,2,1,0:T(8,128)S(1)} %get-tuple-element.190), channel_id=1, source_target_pairs={{2,0},{4,2},{6,4},{8,6},{10,8},{12,10},{14,12},{16,14},{18,16},{20... | collective-permute-start | bytes 516104 | tf_op jit(solution)/shard_map/ppermute | solution.py:299
  41.4 6.2 %collective-permute-start.7 = (f32[8]{0:T(128)S(1)}, f32[8]{0:T(128)S(1)}, u32[]{:S(2)}, u32[]{:S(2)}) collective-permute-start(f32[8]{0:T(128)S(1)} %slice_reduce_fusion.1), channel_id=1, source_target_pairs={{0,4},{2,6},{4,8},{6,10},{8,12},{10,14},{12,16},{14,18},{16,20},{1... | collective-permute-start | bytes 104 | tf_op jit(solution)/shard_map/ppermute | solution.py:302
  41.4 6.2 %collective-permute-start.8 = (f32[8]{0:T(128)S(1)}, f32[8]{0:T(128)S(1)}, u32[]{:S(2)}, u32[]{:S(2)}) collective-permute-start(f32[8]{0:T(128)S(1)} %slice_reduce_fusion.1), channel_id=1, source_target_pairs={{0,28},{2,30},{4,0},{6,2},{8,4},{10,6},{12,8},{14,10},{16,12},{18,... | collective-permute-start | bytes 104 | tf_op jit(solution)/shard_map/ppermute | solution.py:302
  47.7 0.7 copy-start.8
  47.7 0.7 copy-start.9
  47.8 2.1 %copy-start.15 = (f32[3,8,16,128]{3,2,1,0:T(8,128)S(1)}, f32[3,8,16,128]{3,2,1,0:T(8,128)}, u32[]{:S(2)}) copy-start(f32[3,8,16,128]{3,2,1,0:T(8,128)} %get-tuple-element.142) | copy-start | bytes 589828
  48.4 1.5 %collective-permute-start.9 = (f32[21,10,2,128]{3,2,1,0:T(2,128)S(1)}, f32[21,10,2,128]{3,2,1,0:T(2,128)S(1)}, u32[]{:S(2)}, u32[]{:S(2)}) collective-permute-start(f32[21,10,2,128]{3,2,1,0:T(2,128)S(1)} %fusion.14), channel_id=1, source_target_pairs={{0,1},{1,0},{2,3},{3,2},{4,5},{5,4},{6,7},{7,6},{8,9},{9,8},{10,11... | collective-permute-start | bytes 645128 | tf_op jit(solution)/shard_map/ppermute | solution.py:293
  49.9 0.7 copy-start.11
  55.9 14.0 %copy-start.2 = (f32[19,8,16,128]{3,2,1,0:T(8,128)S(1)}, f32[19,8,16,128]{3,2,1,0:T(8,128)}, u32[]{:S(2)}) copy-start(f32[19,8,16,128]{3,2,1,0:T(8,128)} %get-tuple-element.144.inner_ref) | copy-start | bytes 3735556
  57.9 11.9 %collective-permute-start.10 = (f32[21,1,16,128]{3,2,1,0:T(8,128)S(1)}, f32[21,1,16,128]{3,2,1,0:T(8,128)S(1)}, u32[]{:S(2)}, u32[]{:S(2)}) collective-permute-start(f32[21,1,16,128]{3,2,1,0:T(8,128)S(1)} %get-tuple-element.187), channel_id=1, source_target_pairs={{0,2},{2,4},{4,6},{6,8},{8,10},{10,12},{12,14},{14,16},{16,18},{18... | collective-permute-start | bytes 516104 | tf_op jit(solution)/shard_map/ppermute | solution.py:298
  57.9 11.9 %collective-permute-start.11 = (f32[21,1,16,128]{3,2,1,0:T(8,128)S(1)}, f32[21,1,16,128]{3,2,1,0:T(8,128)S(1)}, u32[]{:S(2)}, u32[]{:S(2)}) collective-permute-start(f32[21,1,16,128]{3,2,1,0:T(8,128)S(1)} %get-tuple-element.188), channel_id=1, source_target_pairs={{2,0},{4,2},{6,4},{8,6},{10,8},{12,10},{14,12},{16,14},{18,16},{20... | collective-permute-start | bytes 516104 | tf_op jit(solution)/shard_map/ppermute | solution.py:299
  63.5 6.2 %collective-permute-start.12 = (f32[8]{0:T(128)S(1)}, f32[8]{0:T(128)S(1)}, u32[]{:S(2)}, u32[]{:S(2)}) collective-permute-start(f32[8]{0:T(128)S(1)} %slice_reduce_fusion), channel_id=1, source_target_pairs={{0,4},{2,6},{4,8},{6,10},{8,12},{10,14},{12,16},{14,18},{16,20},{1... | collective-permute-start | bytes 104 | tf_op jit(solution)/shard_map/ppermute | solution.py:302
  63.5 6.2 %collective-permute-start.13 = (f32[8]{0:T(128)S(1)}, f32[8]{0:T(128)S(1)}, u32[]{:S(2)}, u32[]{:S(2)}) collective-permute-start(f32[8]{0:T(128)S(1)} %slice_reduce_fusion), channel_id=1, source_target_pairs={{0,28},{2,30},{4,0},{6,2},{8,4},{10,6},{12,8},{14,10},{16,12},{18,... | collective-permute-start | bytes 104 | tf_op jit(solution)/shard_map/ppermute | solution.py:302
  69.8 0.7 copy-start.6
  69.8 0.7 copy-start.7
  69.9 2.1 %copy-start.14 = (f32[3,8,16,128]{3,2,1,0:T(8,128)S(1)}, f32[3,8,16,128]{3,2,1,0:T(8,128)}, u32[]{:S(2)}) copy-start(f32[3,8,16,128]{3,2,1,0:T(8,128)} %get-tuple-element.145) | copy-start | bytes 589828
  70.5 1.5 %collective-permute-start.14 = (f32[21,10,2,128]{3,2,1,0:T(2,128)S(1)}, f32[21,10,2,128]{3,2,1,0:T(2,128)S(1)}, u32[]{:S(2)}, u32[]{:S(2)}) collective-permute-start(f32[21,10,2,128]{3,2,1,0:T(2,128)S(1)} %fusion.9), channel_id=1, source_target_pairs={{0,1},{1,0},{2,3},{3,2},{4,5},{5,4},{6,7},{7,6},{8,9},{9,8},{10,11... | collective-permute-start | bytes 645128 | tf_op jit(solution)/shard_map/ppermute | solution.py:293
  72.0 1.4 %copy-start.12 = (f32[21,10,2,128]{3,2,1,0:T(2,128)}, f32[21,10,2,128]{3,2,1,0:T(2,128)S(1)}, u32[]{:S(2)}) copy-start(f32[21,10,2,128]{3,2,1,0:T(2,128)S(1)} %collective-permute-done.14.rows_ref) | copy-start | bytes 645124

commit v17 on v15

--- a/solution.py
+++ b/solution.py
@@ -159,10 +159,16 @@
         return carry
 
     lax.fori_loop(0, populations_ref.shape[1], moment_plane, 0)
+    lane = lax.broadcasted_iota(jnp.int32, (1, flow_ref.shape[1]), 1)
+    head_row = jnp.zeros((1, flow_ref.shape[1]), jnp.float32)
     for fan_number in range(fans):
-        flow_ref[fan_number : fan_number + 1, :] = jnp.broadcast_to(
-            jnp.sum(sums_ref[fan_number], axis=(0, 1), keepdims=True), (1, flow_ref.shape[1])
-        )
+        head_row = jnp.where(
+            lane == fan_number,
+            jnp.sum(sums_ref[fan_number], axis=(0, 1), keepdims=True),
+            head_row,
+        )
+    flow_ref[...] = jnp.zeros(flow_ref.shape, jnp.float32)
+    flow_ref[0:1, :] = head_row
 
 
 def first_moments(populations, discs):
@@ -174,7 +180,7 @@
         ),
         out_shape=(
             jax.ShapeDtypeStruct((3, slab_len, band_width, height), jnp.float32),
-            jax.ShapeDtypeStruct((fans, height), jnp.float32),
+            jax.ShapeDtypeStruct((band_width, height), jnp.float32),
         ),
         in_specs=[vmem, vmem],
         out_specs=(vmem, vmem),
@@ -193,7 +199,7 @@
     out_shape = [jax.ShapeDtypeStruct((19, slab_len, band_width, height), jnp.float32)]
     if with_moments:
         out_shape.append(jax.ShapeDtypeStruct((3, slab_len, band_width, height), jnp.float32))
-        out_shape.append(jax.ShapeDtypeStruct((fans, height), jnp.float32))
+        out_shape.append(jax.ShapeDtypeStruct((band_width, height), jnp.float32))
     scratch = [pltpu.VMEM((19, slab_len + 2, band_width + 2, height), jnp.float32)]
     if with_moments:
         scratch.append(pltpu.VMEM((fans, band_width, height), jnp.float32))
@@ -274,8 +280,16 @@
 
     def piece(start):
         cells = [lax.slice_in_dim(field, start, start + 1, axis=dim) for field in fields]
-        carrier = jnp.zeros(cells[0].shape[1:], jnp.float32).at[0, 0, :fans].set(flow)[None]
+        if flow.ndim == 2:
+            carrier = flow[None, None]
+        else:
+            carrier = jnp.zeros(cells[0].shape[1:], jnp.float32).at[0, 0, :fans].set(flow)[None]
         return jnp.concatenate(cells + [carrier], axis=0)
+
+    def pick(received):
+        if flow.ndim == 2:
+            return received[-1, 0]
+        return received[-1, 0, 0, :fans]
 
     head = piece(0)
     tail = piece(fields[0].shape[dim] - 1)
@@ -286,11 +300,11 @@
         both = lax.ppermute(jnp.concatenate([tail, head], axis=dim), axis, forward)
         from_left = lax.slice_in_dim(both, 0, 1, axis=dim)
         from_right = lax.slice_in_dim(both, 1, 2, axis=dim)
-        total = flow + from_left[-1, 0, 0, :fans]
+        total = flow + pick(from_left)
     else:
         from_left = lax.ppermute(tail, axis, forward)
         from_right = lax.ppermute(head, axis, backward)
-        total = flow + from_left[-1, 0, 0, :fans] + from_right[-1, 0, 0, :fans]
+        total = flow + pick(from_left) + pick(from_right)
     for offset in sorted(set(step % count for step in range(-reach, reach + 1)) - {0, 1, count - 1}):
         total = total + lax.ppermute(flow, axis, [(i, (i + offset) % count) for i in range(count)])
     extended = [(from_left, from_right, both)]
@@ -374,12 +388,13 @@
         & jnp.logical_not(solid_flag)[None]
     ).astype(jnp.float32)
     velocity, flow = first_moments(populations, inner_discs)
-    partials = flow[:, 0]
+    partials = flow
     for repeat in range(ITERS):
         fields = [populations, smoke_field[None]]
         if repeat == 0:
             fields.append(solid_flag.astype(jnp.float32)[None])
         fields, totals = rim_round(fields, partials, "len", 1, len_reach)
+        totals = totals[0, : fan_hubs.shape[0]]
         low, high, _ = fields[0]
         fields[0] = jnp.concatenate([low[:19], populations, high[:19]], axis=1)
         fields, totals = rim_round(fields, totals, "band", 2, band_reach)
@@ -420,7 +435,7 @@
         populations = stepped[0]
         if not last:
             velocity = stepped[1]
-            partials = stepped[2][:, 0]
+            partials = stepped[2]
     return (populations, smoke_field)
 
 

time: 78.5 us -> 84.6 us (1.078)
  waiting for transfers between devices: 10.8 us -> 20 us
  starting transfers between devices: 32.6 us -> 29.4 us
  local copies, waits for them, and re-layouts: 7.31 us -> 4.43 us
  other arithmetic: 8.25 us -> 11 us
    ppermute x3, waiting for transfers between devices: 3.6 us -> 15.3 us  [rim_round(): from_left = lax.ppermute(tail, axis, forward)]
    ppermute x6, waiting for transfers between devices: 3.04 us -> 0.02 us  [rim_round(): lax.ppermute(flow, axis, [(i, (i + offset) % count) for i in range(count)])]
    slice x3 -> x0, local copies, waits for them, and re-layouts: 2.41 us -> none  [the longest x2 1.61 us: body(): partials = stepped[2][:, 0]]
    concatenate x3, other arithmetic: 0.12 us -> 2.24 us  [piece(): return jnp.concatenate(cells + [carrier], axis=0)]
    ppermute x3, starting transfers between devices: 3.4 us -> 1.76 us  [rim_round(): from_left = lax.ppermute(tail, axis, forward)]
    ppermute x3, starting transfers between devices: 13.6 us -> 12.1 us  [rim_round(): from_right = lax.ppermute(head, axis, backward)]
  transfers between devices with their start and end apart: 15 -> 15, of which waited for: 6 -> 7; matrix products, arithmetic and copies ran while one was open for 1% -> 2% of each run, Pallas kernels for 0% -> 0%
where the time goes in v17:
time: 84.6 us; the launch traced here: 84.1 us
  starting transfers between devices  29.4 us (35%)
  waiting for transfers between devices  20 us (24%)
  Pallas kernels  17.8 us (21%)
  other arithmetic  11 us (13%)
  local copies, waits for them, and re-layouts  4.43 us (5%)
  between operations  1.16 us (1%)
    ppermute x6, starting transfers between devices, rim_round(): lax.ppermute(flow, axis, [(i, (i + offset) % count) for i in range(count)])  15.5 us
    pallas_call x3, Pallas kernels, lattice_step(): pl.pallas_call(functools.partial(step_kernel, with_moments), out_shape=tu...  15.3 us
    ppermute x3, waiting for transfers between devices, rim_round(): from_left = lax.ppermute(tail, axis, forward)  15.3 us
    ppermute x3, starting transfers between devices, rim_round(): from_right = lax.ppermute(head, axis, backward)  12.1 us
    ppermute x3, waiting for transfers between devices, rim_round(): both = lax.ppermute(jnp.concatenate([tail, head], axis=dim), axis, forward)  4.16 us
    pallas_call x1, Pallas kernels, first_moments(): pl.pallas_call(lambda populations_ref, discs_ref, velocity_ref, flow_ref,...  2.46 us
    slice x7, local copies, waits for them, and re-layouts, piece(): lax.slice_in_dim(field, start, start + 1, axis=dim)  2.27 us
    concatenate x3, other arithmetic, piece(): return jnp.concatenate(cells + [carrier], axis=0)  2.24 us
  transfers between devices with their start and end apart: 15, of which 7 were waited for; matrix products, arithmetic and copies ran while one was open for 2% of the time, Pallas kernels for 0%

profile of v17, /device:TPU:0, one launch (start us, length us, event | category | flops | bytes accessed | tf_op | source)
XLA Modules:
  0.0 84.1 jit_solution(1679241782675546333)
XLA Ops:
  0.6 0.8 slice_bitcast_fusion.12
  1.5 0.7 and_select_fusion
  2.2 0.1 add_compare_fusion
  2.4 0.1 fusion.40
  2.5 1.0 %convert_bitcast_fusion = (f32[1,8,16,128]{3,2,1,0:T(8,128)S(1)}, pred[8,16,128]{2,1,0:T(8,128)(4,1)S(1)}) fusion(s32[8,16,128]{2,1,0:T(8,128)} %param.22), kind=kLoop, calls=%fused_computation.93 | loop fusion | flops 32768 | bytes 147456 | tf_op jit(solution)/shard_map/broadcast_in_dim | solution.py:395
  3.5 0.9 %and_convert_fusion.1.discs_ref = f32[8,8,16,128]{3,2,1,0:T(8,128)} fusion(pred[8,16,128]{2,1,0:T(8,128)(4,1)S(1)} %not.3, pred[8,16,128]{2,1,0:T(8,128)(4,1)S(1)} %slice.526, pred[8,8]{1,0:T(8,128)(4,1)S(1)} %slice.427), kind=kLoop, calls=%fused_computation.1 | loop fusion | flops 393216 | bytes 557120 | tf_op jit(solution)/shard_map/convert_element_type | solution.py:389
  4.5 2.5 %shard_map.104 = (f32[3,8,16,128]{3,2,1,0:T(8,128)}, f32[16,128]{1,0:T(8,128)}) custom-call(f32[19,8,16,128]{3,2,1,0:T(8,128)} %inner_ref.1, f32[8,8,16,128]{3,2,1,0:T(8,128)} %and_convert_fusion.1.discs_ref), custom_call_target="tpu_custom_call" | custom-call | flops 983040 | bytes 1245184 | tf_op jit(solution)/shard_map/pallas_call | solution.py:177
  6.9 3.0 %collective-permute-start.2 = (f32[16,128]{1,0:T(8,128)}, f32[16,128]{1,0:T(8,128)S(1)}, u32[]{:S(2)}, u32[]{:S(2)}) collective-permute-start(f32[16,128]{1,0:T(8,128)} %get-tuple-element.70), channel_id=1, source_target_pairs={{0,4},{2,6},{4,8},{6,10},{8,12},{10,14},{12,16},{14,18},{16,20},{1... | collective-permute-start | bytes 24584 | tf_op jit(solution)/shard_map/ppermute | solution.py:309
  9.9 3.0 %collective-permute-start.3 = (f32[16,128]{1,0:T(8,128)}, f32[16,128]{1,0:T(8,128)S(1)}, u32[]{:S(2)}, u32[]{:S(2)}) collective-permute-start(f32[16,128]{1,0:T(8,128)} %get-tuple-element.70), channel_id=1, source_target_pairs={{0,28},{2,30},{4,0},{6,2},{8,4},{10,6},{12,8},{14,10},{16,12},{18,... | collective-permute-start | bytes 24584 | tf_op jit(solution)/shard_map/ppermute | solution.py:309
  13.0 0.8 pad_maximum_fusion.1
  13.7 1.7 %collective-permute-start = (f32[22,1,16,128]{3,2,1,0:T(8,128)S(1)}, f32[22,1,16,128]{3,2,1,0:T(8,128)S(1)}, u32[]{:S(2)}, u32[]{:S(2)}) collective-permute-start(f32[22,1,16,128]{3,2,1,0:T(8,128)S(1)} %get-tuple-element.137), channel_id=1, source_target_pairs={{0,2},{2,4},{4,6},{6,8},{8,10},{10,12},{12,14},{14,16},{16,18},{18... | collective-permute-start | bytes 540680 | tf_op jit(solution)/shard_map/ppermute | solution.py:305
  15.4 4.0 %collective-permute-start.1 = (f32[22,1,16,128]{3,2,1,0:T(8,128)S(1)}, f32[22,1,16,128]{3,2,1,0:T(8,128)S(1)}, u32[]{:S(2)}, u32[]{:S(2)}) collective-permute-start(f32[22,1,16,128]{3,2,1,0:T(8,128)S(1)} %get-tuple-element.138), channel_id=1, source_target_pairs={{2,0},{4,2},{6,4},{8,6},{10,8},{12,10},{14,12},{16,14},{18,16},{20... | collective-permute-start | bytes 540680 | tf_op jit(solution)/shard_map/ppermute | solution.py:306
  19.6 0.1 broadcast_multiply_fusion
  19.7 0.2 fusion.17
  19.9 3.6 %collective-permute-done.low_ref = f32[22,1,16,128]{3,2,1,0:T(8,128)S(1)} collective-permute-done((f32[22,1,16,128]{3,2,1,0:T(8,128)S(1)}, f32[22,1,16,128]{3,2,1,0:T(8,128)S(1)}, u32[]{:S(2)}, u32[]{:S(2)}) %collective-permute-start) | collective-permute-done | bytes 180256 | tf_op jit(solution)/shard_map/ppermute | solution.py:305
  23.6 0.7 slice_add_fusion.8
  24.4 0.2 fusion.3
  24.7 0.1 fusion.79
  24.7 1.4 %collective-permute-done.4.rows_ref = f32[22,10,2,128]{3,2,1,0:T(2,128)S(1)} collective-permute-done((f32[22,10,2,128]{3,2,1,0:T(2,128)S(1)}, f32[22,10,2,128]{3,2,1,0:T(2,128)S(1)}, u32[]{:S(2)}, u32[]{:S(2)}) %collective-permute-start.4) | collective-permute-done | bytes 225312 | tf_op jit(solution)/shard_map/ppermute | solution.py:300
  26.2 0.1 fusion.36
  26.4 0.7 maximum_bitcast_fusion.solid_ref
  27.1 1.1 %and_convert_fusion.discs_ref = f32[8,10,18,128]{3,2,1,0:T(8,128)} fusion(pred[10,18,128]{2,1,0:T(8,128)(4,1)S(1)} %maximum_compare_fusion, pred[8,18,128]{2,1,0:T(8,128)(4,1)S(1)} %add_compare_fusion, pred[8,10]{1,0:T(8,128)(4,1)S(1)} %fusion.40), kind=kLoop, calls=%fused_computation | loop fusion | flops 552960 | bytes 778832 | tf_op jit(solution)/shard_map/convert_element_type | solution.py:409
  28.2 0.5 fusion.57.strength_ref
  28.7 5.2 %shard_map.105 = (f32[19,8,16,128]{3,2,1,0:T(8,128)}, f32[3,8,16,128]{3,2,1,0:T(8,128)}, f32[16,128]{1,0:T(8,128)}) custom-call(f32[8]{0:T(128)} %fusion.57.strength_ref, f32[19,8,16,128]{3,2,1,0:T(8,128)} %inner_ref.1, f32[22,1,16,128]{3,2,1,0:T(8,128)} %copy-done.4, f32[22,1,16,128]{3,2,1,0:T(8,128)} %copy-done.5, f32[22,10,2,128]{3,2,1,0:T(2,128)} %copy-done.10, ...), custom_call_target="tpu_custom_call" | custom-call | flops 6912000 | bytes 3735552 | tf_op jit(solution)/shard_map/pallas_call | solution.py:207
  33.9 1.1 %fusion.63 = (f32[19,1,16,128]{3,2,1,0:T(8,128)S(1)}, f32[19,1,16,128]{3,2,1,0:T(8,128)S(1)}) fusion(f32[19,8,16,128]{3,2,1,0:T(8,128)} %get-tuple-element.72.inner_ref), kind=kLoop, calls=%fused_computation.164 | loop fusion | bytes 622592 | tf_op jit(solution)/shard_map/slice | solution.py:282
  35.0 0.7 pad_maximum_fusion.3
  35.8 5.2 %collective-permute-start.6 = (f32[21,1,16,128]{3,2,1,0:T(8,128)S(1)}, f32[21,1,16,128]{3,2,1,0:T(8,128)S(1)}, u32[]{:S(2)}, u32[]{:S(2)}) collective-permute-start(f32[21,1,16,128]{3,2,1,0:T(8,128)S(1)} %get-tuple-element.136), channel_id=1, source_target_pairs={{2,0},{4,2},{6,4},{8,6},{10,8},{12,10},{14,12},{16,14},{18,16},{20... | collective-permute-start | bytes 516104 | tf_op jit(solution)/shard_map/ppermute | solution.py:306
  41.0 4.7 %collective-permute-start.8 = (f32[16,128]{1,0:T(8,128)S(1)}, f32[16,128]{1,0:T(8,128)S(1)}, u32[]{:S(2)}, u32[]{:S(2)}) collective-permute-start(f32[16,128]{1,0:T(8,128)S(1)} %copy-done.17), channel_id=1, source_target_pairs={{0,28},{2,30},{4,0},{6,2},{8,4},{10,6},{12,8},{14,10},{16,12},{18,... | collective-permute-start | bytes 24584 | tf_op jit(solution)/shard_map/ppermute | solution.py:309
  45.8 9.1 %collective-permute-done.5.low_ref = f32[21,1,16,128]{3,2,1,0:T(8,128)S(1)} collective-permute-done((f32[21,1,16,128]{3,2,1,0:T(8,128)S(1)}, f32[21,1,16,128]{3,2,1,0:T(8,128)S(1)}, u32[]{:S(2)}, u32[]{:S(2)}) %collective-permute-start.5) | collective-permute-done | bytes 172064 | tf_op jit(solution)/shard_map/ppermute | solution.py:305
  55.0 0.2 fusion.14
  55.2 0.4 copy-done.9
  55.6 0.1 fusion.77
  55.7 1.4 %collective-permute-done.9.rows_ref = f32[21,10,2,128]{3,2,1,0:T(2,128)S(1)} collective-permute-done((f32[21,10,2,128]{3,2,1,0:T(2,128)S(1)}, f32[21,10,2,128]{3,2,1,0:T(2,128)S(1)}, u32[]{:S(2)}, u32[]{:S(2)}) %collective-permute-start.9) | collective-permute-done | bytes 215072 | tf_op jit(solution)/shard_map/ppermute | solution.py:300
  57.1 0.1 fusion.30
  57.2 0.5 fusion.58.strength_ref
  57.8 5.2 %shard_map.106 = (f32[19,8,16,128]{3,2,1,0:T(8,128)}, f32[3,8,16,128]{3,2,1,0:T(8,128)}, f32[16,128]{1,0:T(8,128)}) custom-call(f32[8]{0:T(128)} %fusion.58.strength_ref, f32[19,8,16,128]{3,2,1,0:T(8,128)} %get-tuple-element.72.inner_ref, f32[21,1,16,128]{3,2,1,0:T(8,128)} %copy-done.9, f32[21,1,16,128]{3,2,1,0:T(8,128)} %copy-done.8, ...), custom_call_target="tpu_custom_call" | custom-call | flops 6912000 | bytes 3735552 | tf_op jit(solution)/shard_map/pallas_call | solution.py:207
  63.0 1.1 %fusion.62 = (f32[19,1,16,128]{3,2,1,0:T(8,128)S(1)}, f32[19,1,16,128]{3,2,1,0:T(8,128)S(1)}) fusion(f32[19,8,16,128]{3,2,1,0:T(8,128)} %get-tuple-element.75.inner_ref), kind=kLoop, calls=%fused_computation.163 | loop fusion | bytes 622592 | tf_op jit(solution)/shard_map/slice | solution.py:282
  64.2 0.7 pad_maximum_fusion.5
  65.0 4.7 %collective-permute-start.13 = (f32[16,128]{1,0:T(8,128)S(1)}, f32[16,128]{1,0:T(8,128)S(1)}, u32[]{:S(2)}, u32[]{:S(2)}) collective-permute-start(f32[16,128]{1,0:T(8,128)S(1)} %copy-done.16), channel_id=1, source_target_pairs={{0,28},{2,30},{4,0},{6,2},{8,4},{10,6},{12,8},{14,10},{16,12},{18,... | collective-permute-start | bytes 24584 | tf_op jit(solution)/shard_map/ppermute | solution.py:309
  69.7 2.9 %collective-permute-start.11 = (f32[21,1,16,128]{3,2,1,0:T(8,128)S(1)}, f32[21,1,16,128]{3,2,1,0:T(8,128)S(1)}, u32[]{:S(2)}, u32[]{:S(2)}) collective-permute-start(f32[21,1,16,128]{3,2,1,0:T(8,128)S(1)} %get-tuple-element.134), channel_id=1, source_target_pairs={{2,0},{4,2},{6,4},{8,6},{10,8},{12,10},{14,12},{16,14},{18,16},{20... | collective-permute-start | bytes 516104 | tf_op jit(solution)/shard_map/ppermute | solution.py:306
  72.6 2.5 %collective-permute-done.10.low_ref = f32[21,1,16,128]{3,2,1,0:T(8,128)S(1)} collective-permute-done((f32[21,1,16,128]{3,2,1,0:T(8,128)S(1)}, f32[21,1,16,128]{3,2,1,0:T(8,128)S(1)}, u32[]{:S(2)}, u32[]{:S(2)}) %collective-permute-start.10) | collective-permute-done | bytes 172064 | tf_op jit(solution)/shard_map/ppermute | solution.py:305
  75.2 0.5 collective-permute-done.11.high_ref
  75.8 0.2 fusion.9
  76.0 0.4 copy-done.7
  76.5 1.4 %collective-permute-done.14.rows_ref = f32[21,10,2,128]{3,2,1,0:T(2,128)S(1)} collective-permute-done((f32[21,10,2,128]{3,2,1,0:T(2,128)S(1)}, f32[21,10,2,128]{3,2,1,0:T(2,128)S(1)}, u32[]{:S(2)}, u32[]{:S(2)}) %collective-permute-start.14) | collective-permute-done | bytes 215072 | tf_op jit(solution)/shard_map/ppermute | solution.py:300
  77.9 0.7 fusion.24
  78.7 0.5 fusion.59.strength_ref
  79.2 4.9 %shard_map.107 = f32[19,8,16,128]{3,2,1,0:T(8,128)} custom-call(f32[8]{0:T(128)} %fusion.59.strength_ref, f32[19,8,16,128]{3,2,1,0:T(8,128)} %get-tuple-element.75.inner_ref, f32[21,1,16,128]{3,2,1,0:T(8,128)} %copy-done.6, f32[21,1,16,128]{3,2,1,0:T(8,128)} %copy-done.7, f32[21,10,2,128]{3,2,1,0:T(2,128)} %copy-done.12, ...), custom_call_target="tpu_custom_call" | custom-call | flops 6912000 | bytes 3735552 | tf_op jit(solution)/shard_map/pallas_call | solution.py:207
  (103 shorter events, 1.1 us)
Async XLA Ops:
  2.5 10.4 %copy-start = (f32[19,8,16,128]{3,2,1,0:T(8,128)S(1)}, f32[19,8,16,128]{3,2,1,0:T(8,128)}, u32[]{:S(2)}) copy-start(f32[19,8,16,128]{3,2,1,0:T(8,128)} %inner_ref.1) | copy-start | bytes 3735556
  4.5 8.5 %copy-start.3 = (f32[8,16,128]{2,1,0:T(8,128)S(1)}, f32[8,16,128]{2,1,0:T(8,128)}, u32[]{:S(2)}) copy-start(f32[8,16,128]{2,1,0:T(8,128)} %param.23) | copy-start | bytes 196612
  4.5 15.0 %copy-start.20 = (s32[16,3]{0,1:T(4,128)S(1)}, s32[16,3]{0,1:T(4,128)}, u32[]{:S(2)}) copy-start(s32[16,3]{0,1:T(4,128)} %param.27) | copy-start | bytes 580
  4.5 15.2 %copy-start.21 = (f32[16]{0:T(128)S(1)}, f32[16]{0:T(128)}, u32[]{:S(2)}) copy-start(f32[16]{0:T(128)} %param.28) | copy-start | bytes 196
  6.9 16.7 %collective-permute-start.2 = (f32[16,128]{1,0:T(8,128)}, f32[16,128]{1,0:T(8,128)S(1)}, u32[]{:S(2)}, u32[]{:S(2)}) collective-permute-start(f32[16,128]{1,0:T(8,128)} %get-tuple-element.70), channel_id=1, source_target_pairs={{0,4},{2,6},{4,8},{6,10},{8,12},{10,14},{12,16},{14,18},{16,20},{1... | collective-permute-start | bytes 24584 | tf_op jit(solution)/shard_map/ppermute | solution.py:309
  9.9 13.7 %collective-permute-start.3 = (f32[16,128]{1,0:T(8,128)}, f32[16,128]{1,0:T(8,128)S(1)}, u32[]{:S(2)}, u32[]{:S(2)}) collective-permute-start(f32[16,128]{1,0:T(8,128)} %get-tuple-element.70), channel_id=1, source_target_pairs={{0,28},{2,30},{4,0},{6,2},{8,4},{10,6},{12,8},{14,10},{16,12},{18,... | collective-permute-start | bytes 24584 | tf_op jit(solution)/shard_map/ppermute | solution.py:309
  13.7 9.8 %collective-permute-start = (f32[22,1,16,128]{3,2,1,0:T(8,128)S(1)}, f32[22,1,16,128]{3,2,1,0:T(8,128)S(1)}, u32[]{:S(2)}, u32[]{:S(2)}) collective-permute-start(f32[22,1,16,128]{3,2,1,0:T(8,128)S(1)} %get-tuple-element.137), channel_id=1, source_target_pairs={{0,2},{2,4},{4,6},{6,8},{8,10},{10,12},{12,14},{14,16},{16,18},{18... | collective-permute-start | bytes 540680 | tf_op jit(solution)/shard_map/ppermute | solution.py:305
  15.4 8.1 %collective-permute-start.1 = (f32[22,1,16,128]{3,2,1,0:T(8,128)S(1)}, f32[22,1,16,128]{3,2,1,0:T(8,128)S(1)}, u32[]{:S(2)}, u32[]{:S(2)}) collective-permute-start(f32[22,1,16,128]{3,2,1,0:T(8,128)S(1)} %get-tuple-element.138), channel_id=1, source_target_pairs={{2,0},{4,2},{6,4},{8,6},{10,8},{12,10},{14,12},{16,14},{18,16},{20... | collective-permute-start | bytes 540680 | tf_op jit(solution)/shard_map/ppermute | solution.py:306
  23.5 1.1 %copy-start.4 = (f32[22,1,16,128]{3,2,1,0:T(8,128)}, f32[22,1,16,128]{3,2,1,0:T(8,128)S(1)}, u32[]{:S(2)}) copy-start(f32[22,1,16,128]{3,2,1,0:T(8,128)S(1)} %collective-permute-done.low_ref) | copy-start | bytes 540676
  23.5 1.1 %copy-start.5 = (f32[22,1,16,128]{3,2,1,0:T(8,128)}, f32[22,1,16,128]{3,2,1,0:T(8,128)S(1)}, u32[]{:S(2)}) copy-start(f32[22,1,16,128]{3,2,1,0:T(8,128)S(1)} %collective-permute-done.1.high_ref) | copy-start | bytes 540676
  24.4 1.8 %copy-start.13 = (f32[3,8,16,128]{3,2,1,0:T(8,128)S(1)}, f32[3,8,16,128]{3,2,1,0:T(8,128)}, u32[]{:S(2)}) copy-start(f32[3,8,16,128]{3,2,1,0:T(8,128)} %get-tuple-element.73) | copy-start | bytes 589828
  24.6 1.5 %collective-permute-start.4 = (f32[22,10,2,128]{3,2,1,0:T(2,128)S(1)}, f32[22,10,2,128]{3,2,1,0:T(2,128)S(1)}, u32[]{:S(2)}, u32[]{:S(2)}) collective-permute-start(f32[22,10,2,128]{3,2,1,0:T(2,128)S(1)} %fusion.3), channel_id=1, source_target_pairs={{0,1},{1,0},{2,3},{3,2},{4,5},{5,4},{6,7},{7,6},{8,9},{9,8},{10,11... | collective-permute-start | bytes 675848 | tf_op jit(solution)/shard_map/ppermute | solution.py:300
  26.1 2.0 %copy-start.10 = (f32[22,10,2,128]{3,2,1,0:T(2,128)}, f32[22,10,2,128]{3,2,1,0:T(2,128)S(1)}, u32[]{:S(2)}) copy-start(f32[22,10,2,128]{3,2,1,0:T(2,128)S(1)} %collective-permute-done.4.rows_ref) | copy-start | bytes 675844
  26.2 2.0 %copy-start.18 = (f32[8]{0:T(128)S(1)}, f32[8]{0:T(128)}, u32[]{:S(2)}) copy-start(f32[8]{0:T(128)} %param.25) | copy-start | bytes 100
  26.2 2.0 %copy-start.19 = (f32[8]{0:T(128)S(1)}, f32[8]{0:T(128)}, u32[]{:S(2)}) copy-start(f32[8]{0:T(128)} %param.26) | copy-start | bytes 100
  33.9 7.1 %copy-start.17 = (f32[16,128]{1,0:T(8,128)S(1)}, f32[16,128]{1,0:T(8,128)}, u32[]{:S(2)}) copy-start(f32[16,128]{1,0:T(8,128)} %get-tuple-element.71) | copy-start | bytes 24580
  33.9 21.1 %copy-start.1 = (f32[19,8,16,128]{3,2,1,0:T(8,128)S(1)}, f32[19,8,16,128]{3,2,1,0:T(8,128)}, u32[]{:S(2)}) copy-start(f32[19,8,16,128]{3,2,1,0:T(8,128)} %get-tuple-element.72.inner_ref) | copy-start | bytes 3735556
  35.8 10.0 %collective-permute-start.6 = (f32[21,1,16,128]{3,2,1,0:T(8,128)S(1)}, f32[21,1,16,128]{3,2,1,0:T(8,128)S(1)}, u32[]{:S(2)}, u32[]{:S(2)}) collective-permute-start(f32[21,1,16,128]{3,2,1,0:T(8,128)S(1)} %get-tuple-element.136), channel_id=1, source_target_pairs={{2,0},{4,2},{6,4},{8,6},{10,8},{12,10},{14,12},{16,14},{18,16},{20... | collective-permute-start | bytes 516104 | tf_op jit(solution)/shard_map/ppermute | solution.py:306
  41.0 13.9 %collective-permute-start.7 = (f32[16,128]{1,0:T(8,128)S(1)}, f32[16,128]{1,0:T(8,128)S(1)}, u32[]{:S(2)}, u32[]{:S(2)}) collective-permute-start(f32[16,128]{1,0:T(8,128)S(1)} %copy-done.17), channel_id=1, source_target_pairs={{0,4},{2,6},{4,8},{6,10},{8,12},{10,14},{12,16},{14,18},{16,20},{1... | collective-permute-start | bytes 24584 | tf_op jit(solution)/shard_map/ppermute | solution.py:309
  41.0 13.9 %collective-permute-start.8 = (f32[16,128]{1,0:T(8,128)S(1)}, f32[16,128]{1,0:T(8,128)S(1)}, u32[]{:S(2)}, u32[]{:S(2)}) collective-permute-start(f32[16,128]{1,0:T(8,128)S(1)} %copy-done.17), channel_id=1, source_target_pairs={{0,28},{2,30},{4,0},{6,2},{8,4},{10,6},{12,8},{14,10},{16,12},{18,... | collective-permute-start | bytes 24584 | tf_op jit(solution)/shard_map/ppermute | solution.py:309
  45.7 9.2 %collective-permute-start.5 = (f32[21,1,16,128]{3,2,1,0:T(8,128)S(1)}, f32[21,1,16,128]{3,2,1,0:T(8,128)S(1)}, u32[]{:S(2)}, u32[]{:S(2)}) collective-permute-start(f32[21,1,16,128]{3,2,1,0:T(8,128)S(1)} %get-tuple-element.135), channel_id=1, source_target_pairs={{0,2},{2,4},{4,6},{6,8},{8,10},{10,12},{12,14},{14,16},{16,18},{18... | collective-permute-start | bytes 516104 | tf_op jit(solution)/shard_map/ppermute | solution.py:305
  45.7 9.4 %copy-start.8 = (f32[21,1,16,128]{3,2,1,0:T(8,128)}, f32[21,1,16,128]{3,2,1,0:T(8,128)S(1)}, u32[]{:S(2)}) copy-start(f32[21,1,16,128]{3,2,1,0:T(8,128)S(1)} %collective-permute-done.6.high_ref) | copy-start | bytes 516100
  54.9 0.7 copy-start.9
  55.0 2.1 %copy-start.15 = (f32[3,8,16,128]{3,2,1,0:T(8,128)S(1)}, f32[3,8,16,128]{3,2,1,0:T(8,128)}, u32[]{:S(2)}) copy-start(f32[3,8,16,128]{3,2,1,0:T(8,128)} %get-tuple-element.76) | copy-start | bytes 589828
  55.6 1.5 %collective-permute-start.9 = (f32[21,10,2,128]{3,2,1,0:T(2,128)S(1)}, f32[21,10,2,128]{3,2,1,0:T(2,128)S(1)}, u32[]{:S(2)}, u32[]{:S(2)}) collective-permute-start(f32[21,10,2,128]{3,2,1,0:T(2,128)S(1)} %fusion.14), channel_id=1, source_target_pairs={{0,1},{1,0},{2,3},{3,2},{4,5},{5,4},{6,7},{7,6},{8,9},{9,8},{10,11... | collective-permute-start | bytes 645128 | tf_op jit(solution)/shard_map/ppermute | solution.py:300
  57.0 0.7 copy-start.11
  63.0 1.9 %copy-start.16 = (f32[16,128]{1,0:T(8,128)S(1)}, f32[16,128]{1,0:T(8,128)}, u32[]{:S(2)}) copy-start(f32[16,128]{1,0:T(8,128)} %get-tuple-element.74) | copy-start | bytes 24580
  63.0 12.7 %copy-start.2 = (f32[19,8,16,128]{3,2,1,0:T(8,128)S(1)}, f32[19,8,16,128]{3,2,1,0:T(8,128)}, u32[]{:S(2)}) copy-start(f32[19,8,16,128]{3,2,1,0:T(8,128)} %get-tuple-element.75.inner_ref) | copy-start | bytes 3735556
  64.9 10.2 %collective-permute-start.10 = (f32[21,1,16,128]{3,2,1,0:T(8,128)S(1)}, f32[21,1,16,128]{3,2,1,0:T(8,128)S(1)}, u32[]{:S(2)}, u32[]{:S(2)}) collective-permute-start(f32[21,1,16,128]{3,2,1,0:T(8,128)S(1)} %get-tuple-element.133), channel_id=1, source_target_pairs={{0,2},{2,4},{4,6},{6,8},{8,10},{10,12},{12,14},{14,16},{16,18},{18... | collective-permute-start | bytes 516104 | tf_op jit(solution)/shard_map/ppermute | solution.py:305
  65.0 10.7 %collective-permute-start.12 = (f32[16,128]{1,0:T(8,128)S(1)}, f32[16,128]{1,0:T(8,128)S(1)}, u32[]{:S(2)}, u32[]{:S(2)}) collective-permute-start(f32[16,128]{1,0:T(8,128)S(1)} %copy-done.16), channel_id=1, source_target_pairs={{0,4},{2,6},{4,8},{6,10},{8,12},{10,14},{12,16},{14,18},{16,20},{1... | collective-permute-start | bytes 24584 | tf_op jit(solution)/shard_map/ppermute | solution.py:309
  65.0 10.7 %collective-permute-start.13 = (f32[16,128]{1,0:T(8,128)S(1)}, f32[16,128]{1,0:T(8,128)S(1)}, u32[]{:S(2)}, u32[]{:S(2)}) collective-permute-start(f32[16,128]{1,0:T(8,128)S(1)} %copy-done.16), channel_id=1, source_target_pairs={{0,28},{2,30},{4,0},{6,2},{8,4},{10,6},{12,8},{14,10},{16,12},{18,... | collective-permute-start | bytes 24584 | tf_op jit(solution)/shard_map/ppermute | solution.py:309
  69.7 5.9 %collective-permute-start.11 = (f32[21,1,16,128]{3,2,1,0:T(8,128)S(1)}, f32[21,1,16,128]{3,2,1,0:T(8,128)S(1)}, u32[]{:S(2)}, u32[]{:S(2)}) collective-permute-start(f32[21,1,16,128]{3,2,1,0:T(8,128)S(1)} %get-tuple-element.134), channel_id=1, source_target_pairs={{2,0},{4,2},{6,4},{8,6},{10,8},{12,10},{14,12},{16,14},{18,16},{20... | collective-permute-start | bytes 516104 | tf_op jit(solution)/shard_map/ppermute | solution.py:306
  75.1 0.8 copy-start.6
  75.7 0.7 copy-start.7
  75.8 2.1 %copy-start.14 = (f32[3,8,16,128]{3,2,1,0:T(8,128)S(1)}, f32[3,8,16,128]{3,2,1,0:T(8,128)}, u32[]{:S(2)}) copy-start(f32[3,8,16,128]{3,2,1,0:T(8,128)} %get-tuple-element.77) | copy-start | bytes 589828
  76.4 1.5 %collective-permute-start.14 = (f32[21,10,2,128]{3,2,1,0:T(2,128)S(1)}, f32[21,10,2,128]{3,2,1,0:T(2,128)S(1)}, u32[]{:S(2)}, u32[]{:S(2)}) collective-permute-start(f32[21,10,2,128]{3,2,1,0:T(2,128)S(1)} %fusion.9), channel_id=1, source_target_pairs={{0,1},{1,0},{2,3},{3,2},{4,5},{5,4},{6,7},{7,6},{8,9},{9,8},{10,11... | collective-permute-start | bytes 645128 | tf_op jit(solution)/shard_map/ppermute | solution.py:300
  77.8 1.3 %copy-start.12 = (f32[21,10,2,128]{3,2,1,0:T(2,128)}, f32[21,10,2,128]{3,2,1,0:T(2,128)S(1)}, u32[]{:S(2)}) copy-start(f32[21,10,2,128]{3,2,1,0:T(2,128)S(1)} %collective-permute-done.14.rows_ref) | copy-start | bytes 645124

commit v18 on v15

--- a/solution.py
+++ b/solution.py
@@ -140,10 +140,10 @@
         out_ref[which] = piece
     if not with_moments:
         return
-    moments_into(out_ref, discs_ref, 1, velocity_ref, flow_ref, sums_ref)
-
-
-def moments_into(populations_ref, discs_ref, rim, velocity_ref, flow_ref, sums_ref):
+    moments_into(out_ref, discs_ref, solid_ref, 1, velocity_ref, flow_ref, sums_ref)
+
+
+def moments_into(populations_ref, discs_ref, solid_ref, rim, velocity_ref, flow_ref, sums_ref):
     fans = discs_ref.shape[0]
     band_width = populations_ref.shape[2]
     sums_ref[...] = jnp.zeros(sums_ref.shape, jnp.float32)
@@ -152,9 +152,10 @@
         density, velocity = plane_moments([populations_ref[which, index] for which in range(19)])
         for dimension in range(3):
             velocity_ref[dimension, index] = velocity[dimension]
+        solid_flag = solid_ref[index + rim, 0:band_width, :] != 0.0
         for fan_number in range(fans):
-            sums_ref[fan_number] += (
-                discs_ref[fan_number, index + rim, 0:band_width, :] * velocity[0]
+            sums_ref[fan_number] += jnp.where(
+                solid_flag, 0.0, discs_ref[fan_number, index + rim, 0:band_width, :] * velocity[0]
             )
         return carry
 
@@ -165,24 +166,24 @@
         )
 
 
-def first_moments(populations, discs):
+def first_moments(populations, discs, solid):
     fans, slab_len, band_width, height = discs.shape
     vmem = pl.BlockSpec(memory_space=pltpu.VMEM)
     return pl.pallas_call(
-        lambda populations_ref, discs_ref, velocity_ref, flow_ref, sums_ref: moments_into(
-            populations_ref, discs_ref, 0, velocity_ref, flow_ref, sums_ref
+        lambda populations_ref, discs_ref, solid_ref, velocity_ref, flow_ref, sums_ref: moments_into(
+            populations_ref, discs_ref, solid_ref, 0, velocity_ref, flow_ref, sums_ref
         ),
         out_shape=(
             jax.ShapeDtypeStruct((3, slab_len, band_width, height), jnp.float32),
             jax.ShapeDtypeStruct((fans, height), jnp.float32),
         ),
-        in_specs=[vmem, vmem],
+        in_specs=[vmem, vmem, vmem],
         out_specs=(vmem, vmem),
         scratch_shapes=[pltpu.VMEM((fans, band_width, height), jnp.float32)],
         cost_estimate=pl.CostEstimate(
             flops=60 * discs[0].size, transcendentals=0, bytes_accessed=4 * populations.size
         ),
-    )(populations, discs)
+    )(populations, discs, solid)
 
 
 def lattice_step(strength, inner, low, high, rows, discs, solid_rim, with_moments):
@@ -368,17 +369,14 @@
     )
     len_reach = max(-(-FAN_LEN // slab_len), (slab_len + FAN_LEN - 1) // slab_len)
     band_reach = max(-(-(2 * RAD + 1) // band_width), (band_width + 2 * RAD) // band_width)
-    inner_discs = (
-        along_in[:, 1:-1, None, None]
-        & across_in[:, None, 0:band_width]
-        & jnp.logical_not(solid_flag)[None]
-    ).astype(jnp.float32)
-    velocity, flow = first_moments(populations, inner_discs)
+    discs = (along_in[:, :, None, None] & across_in[:, None]).astype(jnp.float32)
+    solid_planes = solid_flag.astype(jnp.float32)
+    velocity, flow = first_moments(populations, discs[:, 1:-1, 0:band_width], solid_planes)
     partials = flow[:, 0]
     for repeat in range(ITERS):
         fields = [populations, smoke_field[None]]
         if repeat == 0:
-            fields.append(solid_flag.astype(jnp.float32)[None])
+            fields.append(solid_planes[None])
         fields, totals = rim_round(fields, partials, "len", 1, len_reach)
         low, high, _ = fields[0]
         fields[0] = jnp.concatenate([low[:19], populations, high[:19]], axis=1)
@@ -390,10 +388,6 @@
         rimmed = fields[1][0]
         if repeat == 0:
             solid_rim = fields[2][0]
-            air_rim = solid_rim == 0.0
-            discs = (along_in[:, :, None, None] & across_in[:, None] & air_rim[None]).astype(
-                jnp.float32
-            )
         strength = fan_gain * (jet_speed - totals / float(disc_count()))
         last = repeat == ITERS - 1
         stepped = lattice_step(strength, populations, low, high, rows, discs, solid_rim, not last)

time: 78.5 us -> 77.1 us (0.982)
  other arithmetic: 8.25 us -> 5.99 us
  local copies, waits for them, and re-layouts: 7.31 us -> 8.18 us
    slice x2, local copies, waits for them, and re-layouts: 0.08 us -> 1.69 us  [the longest x1 0.89 us: body(): discs[:, 1:-1, 0:band_width]]
    convert_element_type x2, other arithmetic: 2.06 us -> 0.79 us  [the longest x1 0.64 us: body(): solid_planes = solid_flag.astype(jnp.float32)]
    broadcast_in_dim x1, other arithmetic: 0.95 us -> 0.01 us  [body(): fields.append(solid_planes[None])]
    sub x1 -> x0, local copies, waits for them, and re-layouts: 0.8 us -> none  [body(): coord_x[None, :] - fan_hubs[:, 0:1]]
    slice x7 -> x6, local copies, waits for them, and re-layouts: 2.27 us -> 2.26 us  [piece(): lax.slice_in_dim(field, start, start + 1, axis=dim)]
where the time goes in v18:
time: 77.1 us; the launch traced here: 76.7 us
  starting transfers between devices  32.6 us (42%)
  Pallas kernels  17.8 us (23%)
  waiting for transfers between devices  10.8 us (14%)
  local copies, waits for them, and re-layouts  8.18 us (11%)
  other arithmetic  5.99 us (8%)
  between operations  1.11 us (1%)
    ppermute x6, starting transfers between devices, rim_round(): lax.ppermute(flow, axis, [(i, (i + offset) % count) for i in range(count)])  15.6 us
    pallas_call x3, Pallas kernels, lattice_step(): pl.pallas_call(functools.partial(step_kernel, with_moments), out_shape=tu...  15.3 us
    ppermute x3, starting transfers between devices, rim_round(): from_right = lax.ppermute(head, axis, backward)  13.6 us
    ppermute x3, waiting for transfers between devices, rim_round(): both = lax.ppermute(jnp.concatenate([tail, head], axis=dim), axis, forward)  4.17 us
    ppermute x3, waiting for transfers between devices, rim_round(): from_left = lax.ppermute(tail, axis, forward)  3.58 us
    ppermute x3, starting transfers between devices, rim_round(): from_left = lax.ppermute(tail, axis, forward)  3.4 us
    ppermute x6, waiting for transfers between devices, rim_round(): lax.ppermute(flow, axis, [(i, (i + offset) % count) for i in range(count)])  3.04 us
    pallas_call x1, Pallas kernels, first_moments(): pl.pallas_call(lambda populations_ref, discs_ref, solid_ref, velocity_ref...  2.49 us
  transfers between devices with their start and end apart: 15, of which 6 were waited for; matrix products, arithmetic and copies ran while one was open for 1% of the time, Pallas kernels for 0%

profile of v18, /device:TPU:0, one launch (start us, length us, event | category | flops | bytes accessed | tf_op | source)
XLA Modules:
  0.0 76.7 jit_solution(15092524510738993815)
XLA Ops:
  0.6 0.8 %slice_bitcast_fusion.12 = (s32[8]{0:T(128)S(1)}, s32[8]{0:T(128)S(1)}, s32[8]{0:T(128)S(1)}) fusion(s32[8,3]{0,1:T(4,128)} %param.36), kind=kLoop, calls=%fused_computation.164 | loop fusion | bytes 192 | tf_op jit(solution)/shard_map/slice | solution.py:360
  1.5 0.7 and_select_fusion
  2.3 0.1 add_compare_fusion
  2.4 0.1 fusion.42
  2.4 0.2 and_convert_fusion.discs_ref
  2.6 0.9 %slice.627.discs_ref = f32[8,8,16,128]{3,2,1,0:T(8,128)} slice(f32[8,10,18,128]{3,2,1,0:T(8,128)S(1)} %and_convert_fusion.discs_ref), slice={[0:8], [1:9], [0:16], [0:128]} | slice | bytes 1048576 | tf_op jit(solution)/shard_map/slice | solution.py:374
  3.5 0.6 convert_element_type.22.solid_ref
  4.2 2.5 %shard_map.104 = (f32[3,8,16,128]{3,2,1,0:T(8,128)}, f32[8,128]{1,0:T(8,128)}) custom-call(f32[19,8,16,128]{3,2,1,0:T(8,128)} %inner_ref.1, f32[8,8,16,128]{3,2,1,0:T(8,128)} %slice.627.discs_ref, f32[8,16,128]{2,1,0:T(8,128)} %convert_element_type.22.solid_ref), custom_call_target="tpu_custom_call" | custom-call | flops 983040 | bytes 1245184 | tf_op jit(solution)/shard_map/pallas_call | solution.py:172
  6.7 0.8 %slice_reduce_fusion.2 = f32[8]{0:T(128)S(1)} fusion(f32[8,128]{1,0:T(8,128)} %get-tuple-element.130), kind=kLoop, calls=%fused_computation.119 | loop fusion | bytes 64 | tf_op jit(solution)/shard_map/slice | solution.py:375
  7.5 3.0 %collective-permute-start.2 = (f32[8]{0:T(128)S(1)}, f32[8]{0:T(128)S(1)}, u32[]{:S(2)}, u32[]{:S(2)}) collective-permute-start(f32[8]{0:T(128)S(1)} %slice_reduce_fusion.2), channel_id=1, source_target_pairs={{0,4},{2,6},{4,8},{6,10},{8,12},{10,14},{12,16},{14,18},{16,20},{1... | collective-permute-start | bytes 104 | tf_op jit(solution)/shard_map/ppermute | solution.py:296
  10.5 3.1 %collective-permute-start.3 = (f32[8]{0:T(128)S(1)}, f32[8]{0:T(128)S(1)}, u32[]{:S(2)}, u32[]{:S(2)}) collective-permute-start(f32[8]{0:T(128)S(1)} %slice_reduce_fusion.2), channel_id=1, source_target_pairs={{0,28},{2,30},{4,0},{6,2},{8,4},{10,6},{12,8},{14,10},{16,12},{18,... | collective-permute-start | bytes 104 | tf_op jit(solution)/shard_map/ppermute | solution.py:296
  13.7 1.6 %collective-permute-start = (f32[22,1,16,128]{3,2,1,0:T(8,128)S(1)}, f32[22,1,16,128]{3,2,1,0:T(8,128)S(1)}, u32[]{:S(2)}, u32[]{:S(2)}) collective-permute-start(f32[22,1,16,128]{3,2,1,0:T(8,128)S(1)} %get-tuple-element.188), channel_id=1, source_target_pairs={{0,2},{2,4},{4,6},{6,8},{8,10},{10,12},{12,14},{14,16},{16,18},{18... | collective-permute-start | bytes 540680 | tf_op jit(solution)/shard_map/ppermute | solution.py:292
  15.3 4.0 %collective-permute-start.1 = (f32[22,1,16,128]{3,2,1,0:T(8,128)S(1)}, f32[22,1,16,128]{3,2,1,0:T(8,128)S(1)}, u32[]{:S(2)}, u32[]{:S(2)}) collective-permute-start(f32[22,1,16,128]{3,2,1,0:T(8,128)S(1)} %get-tuple-element.189), channel_id=1, source_target_pairs={{2,0},{4,2},{6,4},{8,6},{10,8},{12,10},{14,12},{16,14},{18,16},{20... | collective-permute-start | bytes 540680 | tf_op jit(solution)/shard_map/ppermute | solution.py:293
  19.5 0.1 broadcast_multiply_fusion
  19.6 0.2 fusion.19
  19.9 3.6 %collective-permute-done.low_ref = f32[22,1,16,128]{3,2,1,0:T(8,128)S(1)} collective-permute-done((f32[22,1,16,128]{3,2,1,0:T(8,128)S(1)}, f32[22,1,16,128]{3,2,1,0:T(8,128)S(1)}, u32[]{:S(2)}, u32[]{:S(2)}) %collective-permute-start) | collective-permute-done | bytes 180256 | tf_op jit(solution)/shard_map/ppermute | solution.py:292
  23.5 0.2 fusion.2
  23.7 0.4 copy-done.5
  24.2 0.1 fusion.91
  24.3 1.4 %collective-permute-done.4.rows_ref = f32[22,10,2,128]{3,2,1,0:T(2,128)S(1)} collective-permute-done((f32[22,10,2,128]{3,2,1,0:T(2,128)S(1)}, f32[22,10,2,128]{3,2,1,0:T(2,128)S(1)}, u32[]{:S(2)}, u32[]{:S(2)}) %collective-permute-start.4) | collective-permute-done | bytes 225312 | tf_op jit(solution)/shard_map/ppermute | solution.py:287
  25.7 0.1 fusion.38
  25.9 0.6 maximum_bitcast_fusion.solid_ref
  26.5 0.5 fusion.71.strength_ref
  27.1 5.2 %shard_map.105 = (f32[19,8,16,128]{3,2,1,0:T(8,128)}, f32[3,8,16,128]{3,2,1,0:T(8,128)}, f32[8,128]{1,0:T(8,128)}) custom-call(f32[8]{0:T(128)} %fusion.71.strength_ref, f32[19,8,16,128]{3,2,1,0:T(8,128)} %inner_ref.1, f32[22,1,16,128]{3,2,1,0:T(8,128)} %copy-done.5, f32[22,1,16,128]{3,2,1,0:T(8,128)} %copy-done.6, f32[22,10,2,128]{3,2,1,0:T(2,128)} %copy-done.11, ...), custom_call_target="tpu_custom_call" | custom-call | flops 6912000 | bytes 3735552 | tf_op jit(solution)/shard_map/pallas_call | solution.py:202
  32.3 1.1 %fusion.76 = (f32[19,1,16,128]{3,2,1,0:T(8,128)S(1)}, f32[19,1,16,128]{3,2,1,0:T(8,128)S(1)}) fusion(f32[19,8,16,128]{3,2,1,0:T(8,128)} %get-tuple-element.132.inner_ref), kind=kLoop, calls=%fused_computation.171 | loop fusion | bytes 622592 | tf_op jit(solution)/shard_map/slice | solution.py:277
  33.4 0.8 %slice_reduce_fusion.1 = f32[8]{0:T(128)S(1)} fusion(f32[8,128]{1,0:T(8,128)} %get-tuple-element.131), kind=kLoop, calls=%fused_computation.118 | loop fusion | bytes 64 | tf_op jit(solution)/shard_map/slice | solution.py:417
  34.2 1.7 %collective-permute-start.5 = (f32[21,1,16,128]{3,2,1,0:T(8,128)S(1)}, f32[21,1,16,128]{3,2,1,0:T(8,128)S(1)}, u32[]{:S(2)}, u32[]{:S(2)}) collective-permute-start(f32[21,1,16,128]{3,2,1,0:T(8,128)S(1)} %get-tuple-element.180), channel_id=1, source_target_pairs={{0,2},{2,4},{4,6},{6,8},{8,10},{10,12},{12,14},{14,16},{16,18},{18... | collective-permute-start | bytes 516104 | tf_op jit(solution)/shard_map/ppermute | solution.py:292
  35.9 4.0 %collective-permute-start.6 = (f32[21,1,16,128]{3,2,1,0:T(8,128)S(1)}, f32[21,1,16,128]{3,2,1,0:T(8,128)S(1)}, u32[]{:S(2)}, u32[]{:S(2)}) collective-permute-start(f32[21,1,16,128]{3,2,1,0:T(8,128)S(1)} %get-tuple-element.181), channel_id=1, source_target_pairs={{2,0},{4,2},{6,4},{8,6},{10,8},{12,10},{14,12},{16,14},{18,16},{20... | collective-permute-start | bytes 516104 | tf_op jit(solution)/shard_map/ppermute | solution.py:293
  39.9 4.7 %collective-permute-start.8 = (f32[8]{0:T(128)S(1)}, f32[8]{0:T(128)S(1)}, u32[]{:S(2)}, u32[]{:S(2)}) collective-permute-start(f32[8]{0:T(128)S(1)} %slice_reduce_fusion.1), channel_id=1, source_target_pairs={{0,28},{2,30},{4,0},{6,2},{8,4},{10,6},{12,8},{14,10},{16,12},{18,... | collective-permute-start | bytes 104 | tf_op jit(solution)/shard_map/ppermute | solution.py:296
  44.6 1.5 %collective-permute-done.7 = f32[8]{0:T(128)S(1)} collective-permute-done((f32[8]{0:T(128)S(1)}, f32[8]{0:T(128)S(1)}, u32[]{:S(2)}, u32[]{:S(2)}) %collective-permute-start.7) | collective-permute-done | bytes 64 | tf_op jit(solution)/shard_map/ppermute | solution.py:296
  46.3 0.2 fusion.14
  46.5 0.4 copy-done.9
  46.9 0.1 fusion.89
  47.0 1.4 %collective-permute-done.9.rows_ref = f32[21,10,2,128]{3,2,1,0:T(2,128)S(1)} collective-permute-done((f32[21,10,2,128]{3,2,1,0:T(2,128)S(1)}, f32[21,10,2,128]{3,2,1,0:T(2,128)S(1)}, u32[]{:S(2)}, u32[]{:S(2)}) %collective-permute-start.9) | collective-permute-done | bytes 215072 | tf_op jit(solution)/shard_map/ppermute | solution.py:287
  48.4 0.1 fusion.32
  48.6 0.6 fusion.72.strength_ref
  49.1 5.2 %shard_map.106 = (f32[19,8,16,128]{3,2,1,0:T(8,128)}, f32[3,8,16,128]{3,2,1,0:T(8,128)}, f32[8,128]{1,0:T(8,128)}) custom-call(f32[8]{0:T(128)} %fusion.72.strength_ref, f32[19,8,16,128]{3,2,1,0:T(8,128)} %get-tuple-element.132.inner_ref, f32[21,1,16,128]{3,2,1,0:T(8,128)} %copy-done.9, f32[21,1,16,128]{3,2,1,0:T(8,128)} %copy-done.10, ...), custom_call_target="tpu_custom_call" | custom-call | flops 6912000 | bytes 3735552 | tf_op jit(solution)/shard_map/pallas_call | solution.py:202
  54.4 1.1 %fusion.75 = (f32[19,1,16,128]{3,2,1,0:T(8,128)S(1)}, f32[19,1,16,128]{3,2,1,0:T(8,128)S(1)}) fusion(f32[19,8,16,128]{3,2,1,0:T(8,128)} %get-tuple-element.135.inner_ref), kind=kLoop, calls=%fused_computation.170 | loop fusion | bytes 622592 | tf_op jit(solution)/shard_map/slice | solution.py:277
  55.5 0.8 %slice_reduce_fusion = f32[8]{0:T(128)S(1)} fusion(f32[8,128]{1,0:T(8,128)} %get-tuple-element.134), kind=kLoop, calls=%fused_computation.115 | loop fusion | bytes 64 | tf_op jit(solution)/shard_map/slice | solution.py:417
  56.4 5.6 %collective-permute-start.11 = (f32[21,1,16,128]{3,2,1,0:T(8,128)S(1)}, f32[21,1,16,128]{3,2,1,0:T(8,128)S(1)}, u32[]{:S(2)}, u32[]{:S(2)}) collective-permute-start(f32[21,1,16,128]{3,2,1,0:T(8,128)S(1)} %get-tuple-element.179), channel_id=1, source_target_pairs={{2,0},{4,2},{6,4},{8,6},{10,8},{12,10},{14,12},{16,14},{18,16},{20... | collective-permute-start | bytes 516104 | tf_op jit(solution)/shard_map/ppermute | solution.py:293
  62.0 4.7 %collective-permute-start.13 = (f32[8]{0:T(128)S(1)}, f32[8]{0:T(128)S(1)}, u32[]{:S(2)}, u32[]{:S(2)}) collective-permute-start(f32[8]{0:T(128)S(1)} %slice_reduce_fusion), channel_id=1, source_target_pairs={{0,28},{2,30},{4,0},{6,2},{8,4},{10,6},{12,8},{14,10},{16,12},{18,... | collective-permute-start | bytes 104 | tf_op jit(solution)/shard_map/ppermute | solution.py:296
  66.8 1.5 %collective-permute-done.12 = f32[8]{0:T(128)S(1)} collective-permute-done((f32[8]{0:T(128)S(1)}, f32[8]{0:T(128)S(1)}, u32[]{:S(2)}, u32[]{:S(2)}) %collective-permute-start.12) | collective-permute-done | bytes 64 | tf_op jit(solution)/shard_map/ppermute | solution.py:296
  68.4 0.2 fusion.9
  68.6 0.4 copy-done.7
  69.1 1.4 %collective-permute-done.14.rows_ref = f32[21,10,2,128]{3,2,1,0:T(2,128)S(1)} collective-permute-done((f32[21,10,2,128]{3,2,1,0:T(2,128)S(1)}, f32[21,10,2,128]{3,2,1,0:T(2,128)S(1)}, u32[]{:S(2)}, u32[]{:S(2)}) %collective-permute-start.14) | collective-permute-done | bytes 215072 | tf_op jit(solution)/shard_map/ppermute | solution.py:287
  70.5 0.7 fusion.26
  71.3 0.5 fusion.73.strength_ref
  71.8 4.9 %shard_map.107 = f32[19,8,16,128]{3,2,1,0:T(8,128)} custom-call(f32[8]{0:T(128)} %fusion.73.strength_ref, f32[19,8,16,128]{3,2,1,0:T(8,128)} %get-tuple-element.135.inner_ref, f32[21,1,16,128]{3,2,1,0:T(8,128)} %copy-done.7, f32[21,1,16,128]{3,2,1,0:T(8,128)} %copy-done.8, f32[21,10,2,128]{3,2,1,0:T(2,128)} %copy-done.13, f32[8,10,18,128]{3,2,1,0:T(8,128)} %copy-done, ...), custom_call_target="tpu_custom_call" | custom-call | flops 6912000 | bytes 3735552 | tf_op jit(solution)/shard_map/pallas_call | solution.py:202
  (103 shorter events, 1.1 us)
Async XLA Ops:
  0.6 2.9 %copy-start.17 = (s32[8,16,128]{2,1,0:T(8,128)S(1)}, s32[8,16,128]{2,1,0:T(8,128)}, u32[]{:S(2)}) copy-start(s32[8,16,128]{2,1,0:T(8,128)} %param.34) | copy-start | bytes 196612
  2.6 4.1 %copy-start = (f32[8,10,18,128]{3,2,1,0:T(8,128)}, f32[8,10,18,128]{3,2,1,0:T(8,128)S(1)}, u32[]{:S(2)}) copy-start(f32[8,10,18,128]{3,2,1,0:T(8,128)S(1)} %and_convert_fusion.discs_ref) | copy-start | bytes 2211844
  3.5 10.1 %copy-start.1 = (f32[19,8,16,128]{3,2,1,0:T(8,128)S(1)}, f32[19,8,16,128]{3,2,1,0:T(8,128)}, u32[]{:S(2)}) copy-start(f32[19,8,16,128]{3,2,1,0:T(8,128)} %inner_ref.1) | copy-start | bytes 3735556
  4.2 9.4 %copy-start.4 = (f32[8,16,128]{2,1,0:T(8,128)S(1)}, f32[8,16,128]{2,1,0:T(8,128)}, u32[]{:S(2)}) copy-start(f32[8,16,128]{2,1,0:T(8,128)} %param.35) | copy-start | bytes 196612
  4.2 15.2 %copy-start.20 = (s32[16,3]{0,1:T(4,128)S(1)}, s32[16,3]{0,1:T(4,128)}, u32[]{:S(2)}) copy-start(s32[16,3]{0,1:T(4,128)} %param.39) | copy-start | bytes 580
  6.7 12.9 %copy-start.21 = (f32[16]{0:T(128)S(1)}, f32[16]{0:T(128)}, u32[]{:S(2)}) copy-start(f32[16]{0:T(128)} %param.40) | copy-start | bytes 196
  7.5 12.4 %collective-permute-start.2 = (f32[8]{0:T(128)S(1)}, f32[8]{0:T(128)S(1)}, u32[]{:S(2)}, u32[]{:S(2)}) collective-permute-start(f32[8]{0:T(128)S(1)} %slice_reduce_fusion.2), channel_id=1, source_target_pairs={{0,4},{2,6},{4,8},{6,10},{8,12},{10,14},{12,16},{14,18},{16,20},{1... | collective-permute-start | bytes 104 | tf_op jit(solution)/shard_map/ppermute | solution.py:296
  10.5 9.4 %collective-permute-start.3 = (f32[8]{0:T(128)S(1)}, f32[8]{0:T(128)S(1)}, u32[]{:S(2)}, u32[]{:S(2)}) collective-permute-start(f32[8]{0:T(128)S(1)} %slice_reduce_fusion.2), channel_id=1, source_target_pairs={{0,28},{2,30},{4,0},{6,2},{8,4},{10,6},{12,8},{14,10},{16,12},{18,... | collective-permute-start | bytes 104 | tf_op jit(solution)/shard_map/ppermute | solution.py:296
  13.7 9.8 %collective-permute-start = (f32[22,1,16,128]{3,2,1,0:T(8,128)S(1)}, f32[22,1,16,128]{3,2,1,0:T(8,128)S(1)}, u32[]{:S(2)}, u32[]{:S(2)}) collective-permute-start(f32[22,1,16,128]{3,2,1,0:T(8,128)S(1)} %get-tuple-element.188), channel_id=1, source_target_pairs={{0,2},{2,4},{4,6},{6,8},{8,10},{10,12},{12,14},{14,16},{16,18},{18... | collective-permute-start | bytes 540680 | tf_op jit(solution)/shard_map/ppermute | solution.py:292
  15.3 8.1 %collective-permute-start.1 = (f32[22,1,16,128]{3,2,1,0:T(8,128)S(1)}, f32[22,1,16,128]{3,2,1,0:T(8,128)S(1)}, u32[]{:S(2)}, u32[]{:S(2)}) collective-permute-start(f32[22,1,16,128]{3,2,1,0:T(8,128)S(1)} %get-tuple-element.189), channel_id=1, source_target_pairs={{2,0},{4,2},{6,4},{8,6},{10,8},{12,10},{14,12},{16,14},{18,16},{20... | collective-permute-start | bytes 540680 | tf_op jit(solution)/shard_map/ppermute | solution.py:293
  23.4 0.7 copy-start.5
  23.4 0.7 copy-start.6
  23.5 2.2 %copy-start.14 = (f32[3,8,16,128]{3,2,1,0:T(8,128)S(1)}, f32[3,8,16,128]{3,2,1,0:T(8,128)}, u32[]{:S(2)}) copy-start(f32[3,8,16,128]{3,2,1,0:T(8,128)} %get-tuple-element.133) | copy-start | bytes 589828
  24.2 2.3 %copy-start.18 = (f32[8]{0:T(128)S(1)}, f32[8]{0:T(128)}, u32[]{:S(2)}) copy-start(f32[8]{0:T(128)} %param.37) | copy-start | bytes 100
  24.2 2.3 %copy-start.19 = (f32[8]{0:T(128)S(1)}, f32[8]{0:T(128)}, u32[]{:S(2)}) copy-start(f32[8]{0:T(128)} %param.38) | copy-start | bytes 100
  24.2 1.5 %collective-permute-start.4 = (f32[22,10,2,128]{3,2,1,0:T(2,128)S(1)}, f32[22,10,2,128]{3,2,1,0:T(2,128)S(1)}, u32[]{:S(2)}, u32[]{:S(2)}) collective-permute-start(f32[22,10,2,128]{3,2,1,0:T(2,128)S(1)} %fusion.2), channel_id=1, source_target_pairs={{0,1},{1,0},{2,3},{3,2},{4,5},{5,4},{6,7},{7,6},{8,9},{9,8},{10,11... | collective-permute-start | bytes 675848 | tf_op jit(solution)/shard_map/ppermute | solution.py:287
  25.7 1.4 %copy-start.11 = (f32[22,10,2,128]{3,2,1,0:T(2,128)}, f32[22,10,2,128]{3,2,1,0:T(2,128)S(1)}, u32[]{:S(2)}) copy-start(f32[22,10,2,128]{3,2,1,0:T(2,128)S(1)} %collective-permute-done.4.rows_ref) | copy-start | bytes 675844
  32.3 14.0 %copy-start.2 = (f32[19,8,16,128]{3,2,1,0:T(8,128)S(1)}, f32[19,8,16,128]{3,2,1,0:T(8,128)}, u32[]{:S(2)}) copy-start(f32[19,8,16,128]{3,2,1,0:T(8,128)} %get-tuple-element.132.inner_ref) | copy-start | bytes 3735556
  34.2 11.9 %collective-permute-start.5 = (f32[21,1,16,128]{3,2,1,0:T(8,128)S(1)}, f32[21,1,16,128]{3,2,1,0:T(8,128)S(1)}, u32[]{:S(2)}, u32[]{:S(2)}) collective-permute-start(f32[21,1,16,128]{3,2,1,0:T(8,128)S(1)} %get-tuple-element.180), channel_id=1, source_target_pairs={{0,2},{2,4},{4,6},{6,8},{8,10},{10,12},{12,14},{14,16},{16,18},{18... | collective-permute-start | bytes 516104 | tf_op jit(solution)/shard_map/ppermute | solution.py:292
  35.9 10.2 %collective-permute-start.6 = (f32[21,1,16,128]{3,2,1,0:T(8,128)S(1)}, f32[21,1,16,128]{3,2,1,0:T(8,128)S(1)}, u32[]{:S(2)}, u32[]{:S(2)}) collective-permute-start(f32[21,1,16,128]{3,2,1,0:T(8,128)S(1)} %get-tuple-element.181), channel_id=1, source_target_pairs={{2,0},{4,2},{6,4},{8,6},{10,8},{12,10},{14,12},{16,14},{18,16},{20... | collective-permute-start | bytes 516104 | tf_op jit(solution)/shard_map/ppermute | solution.py:293
  39.9 6.2 %collective-permute-start.7 = (f32[8]{0:T(128)S(1)}, f32[8]{0:T(128)S(1)}, u32[]{:S(2)}, u32[]{:S(2)}) collective-permute-start(f32[8]{0:T(128)S(1)} %slice_reduce_fusion.1), channel_id=1, source_target_pairs={{0,4},{2,6},{4,8},{6,10},{8,12},{10,14},{12,16},{14,18},{16,20},{1... | collective-permute-start | bytes 104 | tf_op jit(solution)/shard_map/ppermute | solution.py:296
  39.9 6.2 %collective-permute-start.8 = (f32[8]{0:T(128)S(1)}, f32[8]{0:T(128)S(1)}, u32[]{:S(2)}, u32[]{:S(2)}) collective-permute-start(f32[8]{0:T(128)S(1)} %slice_reduce_fusion.1), channel_id=1, source_target_pairs={{0,28},{2,30},{4,0},{6,2},{8,4},{10,6},{12,8},{14,10},{16,12},{18,... | collective-permute-start | bytes 104 | tf_op jit(solution)/shard_map/ppermute | solution.py:296
  46.2 0.7 copy-start.9
  46.2 0.7 copy-start.10
  46.3 2.1 %copy-start.16 = (f32[3,8,16,128]{3,2,1,0:T(8,128)S(1)}, f32[3,8,16,128]{3,2,1,0:T(8,128)}, u32[]{:S(2)}) copy-start(f32[3,8,16,128]{3,2,1,0:T(8,128)} %get-tuple-element.136) | copy-start | bytes 589828
  46.9 1.5 %collective-permute-start.9 = (f32[21,10,2,128]{3,2,1,0:T(2,128)S(1)}, f32[21,10,2,128]{3,2,1,0:T(2,128)S(1)}, u32[]{:S(2)}, u32[]{:S(2)}) collective-permute-start(f32[21,10,2,128]{3,2,1,0:T(2,128)S(1)} %fusion.14), channel_id=1, source_target_pairs={{0,1},{1,0},{2,3},{3,2},{4,5},{5,4},{6,7},{7,6},{8,9},{9,8},{10,11... | collective-permute-start | bytes 645128 | tf_op jit(solution)/shard_map/ppermute | solution.py:287
  48.4 0.8 %copy-start.12 = (f32[21,10,2,128]{3,2,1,0:T(2,128)}, f32[21,10,2,128]{3,2,1,0:T(2,128)S(1)}, u32[]{:S(2)}) copy-start(f32[21,10,2,128]{3,2,1,0:T(2,128)S(1)} %collective-permute-done.9.rows_ref) | copy-start | bytes 645124
  54.4 14.0 %copy-start.3 = (f32[19,8,16,128]{3,2,1,0:T(8,128)S(1)}, f32[19,8,16,128]{3,2,1,0:T(8,128)}, u32[]{:S(2)}) copy-start(f32[19,8,16,128]{3,2,1,0:T(8,128)} %get-tuple-element.135.inner_ref) | copy-start | bytes 3735556
  56.4 11.9 %collective-permute-start.10 = (f32[21,1,16,128]{3,2,1,0:T(8,128)S(1)}, f32[21,1,16,128]{3,2,1,0:T(8,128)S(1)}, u32[]{:S(2)}, u32[]{:S(2)}) collective-permute-start(f32[21,1,16,128]{3,2,1,0:T(8,128)S(1)} %get-tuple-element.178), channel_id=1, source_target_pairs={{0,2},{2,4},{4,6},{6,8},{8,10},{10,12},{12,14},{14,16},{16,18},{18... | collective-permute-start | bytes 516104 | tf_op jit(solution)/shard_map/ppermute | solution.py:292
  56.4 11.9 %collective-permute-start.11 = (f32[21,1,16,128]{3,2,1,0:T(8,128)S(1)}, f32[21,1,16,128]{3,2,1,0:T(8,128)S(1)}, u32[]{:S(2)}, u32[]{:S(2)}) collective-permute-start(f32[21,1,16,128]{3,2,1,0:T(8,128)S(1)} %get-tuple-element.179), channel_id=1, source_target_pairs={{2,0},{4,2},{6,4},{8,6},{10,8},{12,10},{14,12},{16,14},{18,16},{20... | collective-permute-start | bytes 516104 | tf_op jit(solution)/shard_map/ppermute | solution.py:293
  62.0 6.2 %collective-permute-start.12 = (f32[8]{0:T(128)S(1)}, f32[8]{0:T(128)S(1)}, u32[]{:S(2)}, u32[]{:S(2)}) collective-permute-start(f32[8]{0:T(128)S(1)} %slice_reduce_fusion), channel_id=1, source_target_pairs={{0,4},{2,6},{4,8},{6,10},{8,12},{10,14},{12,16},{14,18},{16,20},{1... | collective-permute-start | bytes 104 | tf_op jit(solution)/shard_map/ppermute | solution.py:296
  62.0 6.2 %collective-permute-start.13 = (f32[8]{0:T(128)S(1)}, f32[8]{0:T(128)S(1)}, u32[]{:S(2)}, u32[]{:S(2)}) collective-permute-start(f32[8]{0:T(128)S(1)} %slice_reduce_fusion), channel_id=1, source_target_pairs={{0,28},{2,30},{4,0},{6,2},{8,4},{10,6},{12,8},{14,10},{16,12},{18,... | collective-permute-start | bytes 104 | tf_op jit(solution)/shard_map/ppermute | solution.py:296
  68.3 0.7 copy-start.7
  68.3 0.7 copy-start.8
  68.4 2.1 %copy-start.15 = (f32[3,8,16,128]{3,2,1,0:T(8,128)S(1)}, f32[3,8,16,128]{3,2,1,0:T(8,128)}, u32[]{:S(2)}) copy-start(f32[3,8,16,128]{3,2,1,0:T(8,128)} %get-tuple-element.137) | copy-start | bytes 589828
  69.0 1.5 %collective-permute-start.14 = (f32[21,10,2,128]{3,2,1,0:T(2,128)S(1)}, f32[21,10,2,128]{3,2,1,0:T(2,128)S(1)}, u32[]{:S(2)}, u32[]{:S(2)}) collective-permute-start(f32[21,10,2,128]{3,2,1,0:T(2,128)S(1)} %fusion.9), channel_id=1, source_target_pairs={{0,1},{1,0},{2,3},{3,2},{4,5},{5,4},{6,7},{7,6},{8,9},{9,8},{10,11... | collective-permute-start | bytes 645128 | tf_op jit(solution)/shard_map/ppermute | solution.py:287
  70.5 1.3 %copy-start.13 = (f32[21,10,2,128]{3,2,1,0:T(2,128)}, f32[21,10,2,128]{3,2,1,0:T(2,128)S(1)}, u32[]{:S(2)}) copy-start(f32[21,10,2,128]{3,2,1,0:T(2,128)S(1)} %collective-permute-done.14.rows_ref) | copy-start | bytes 645124

commit v19 on v18

--- a/solution.py
+++ b/solution.py
@@ -155,7 +155,7 @@
         solid_flag = solid_ref[index + rim, 0:band_width, :] != 0.0
         for fan_number in range(fans):
             sums_ref[fan_number] += jnp.where(
-                solid_flag, 0.0, discs_ref[fan_number, index + rim, 0:band_width, :] * velocity[0]
+                solid_flag, 0.0, discs_ref[fan_number, index + 1, 0:band_width, :] * velocity[0]
             )
         return carry
 
@@ -167,7 +167,8 @@
 
 
 def first_moments(populations, discs, solid):
-    fans, slab_len, band_width, height = discs.shape
+    fans = discs.shape[0]
+    slab_len, band_width, height = populations.shape[1:]
     vmem = pl.BlockSpec(memory_space=pltpu.VMEM)
     return pl.pallas_call(
         lambda populations_ref, discs_ref, solid_ref, velocity_ref, flow_ref, sums_ref: moments_into(
@@ -371,7 +372,7 @@
     band_reach = max(-(-(2 * RAD + 1) // band_width), (band_width + 2 * RAD) // band_width)
     discs = (along_in[:, :, None, None] & across_in[:, None]).astype(jnp.float32)
     solid_planes = solid_flag.astype(jnp.float32)
-    velocity, flow = first_moments(populations, discs[:, 1:-1, 0:band_width], solid_planes)
+    velocity, flow = first_moments(populations, discs, solid_planes)
     partials = flow[:, 0]
     for repeat in range(ITERS):
         fields = [populations, smoke_field[None]]

time: 77.1 us -> 78.3 us (1.016)
  other arithmetic: 5.99 us -> 7.84 us
  local copies, waits for them, and re-layouts: 8.18 us -> 7.32 us
    convert_element_type x1, other arithmetic: 0.16 us -> 1.12 us  [body(): (along_in[:, :, None, None] & across_in[:, None]).astype(jnp.float32)]
    slice x1 -> x0, local copies, waits for them, and re-layouts: 0.89 us -> none  [body(): discs[:, 1:-1, 0:band_width]]
    broadcast_in_dim x1, other arithmetic: 0.01 us -> 0.85 us  [body(): fields.append(solid_planes[None])]
where the time goes in v19:
time: 78.3 us; the launch traced here: 77.9 us
  starting transfers between devices  32.6 us (42%)
  Pallas kernels  18 us (23%)
  waiting for transfers between devices  10.8 us (14%)
  other arithmetic  7.84 us (10%)
  local copies, waits for them, and re-layouts  7.32 us (9%)
  between operations  1.1 us (1%)
    ppermute x6, starting transfers between devices, rim_round(): lax.ppermute(flow, axis, [(i, (i + offset) % count) for i in range(count)])  15.6 us
    pallas_call x3, Pallas kernels, lattice_step(): pl.pallas_call(functools.partial(step_kernel, with_moments), out_shape=tu...  15.3 us
    ppermute x3, starting transfers between devices, rim_round(): from_right = lax.ppermute(head, axis, backward)  13.6 us
    ppermute x3, waiting for transfers between devices, rim_round(): both = lax.ppermute(jnp.concatenate([tail, head], axis=dim), axis, forward)  4.17 us
    ppermute x3, waiting for transfers between devices, rim_round(): from_left = lax.ppermute(tail, axis, forward)  3.58 us
    ppermute x3, starting transfers between devices, rim_round(): from_left = lax.ppermute(tail, axis, forward)  3.4 us
    ppermute x6, waiting for transfers between devices, rim_round(): lax.ppermute(flow, axis, [(i, (i + offset) % count) for i in range(count)])  3.04 us
    pallas_call x1, Pallas kernels, first_moments(): pl.pallas_call(lambda populations_ref, discs_ref, solid_ref, velocity_ref...  2.71 us
  transfers between devices with their start and end apart: 15, of which 6 were waited for; matrix products, arithmetic and copies ran while one was open for 1% of the time, Pallas kernels for 0%

profile of v19, /device:TPU:0, one launch (start us, length us, event | category | flops | bytes accessed | tf_op | source)
XLA Modules:
  0.0 77.9 jit_solution(15394656741630617716)
XLA Ops:
  0.6 0.8 %slice_bitcast_fusion.12 = (s32[8]{0:T(128)S(1)}, s32[8]{0:T(128)S(1)}, s32[8]{0:T(128)S(1)}) fusion(s32[8,3]{0,1:T(4,128)} %param.36), kind=kLoop, calls=%fused_computation.164 | loop fusion | bytes 192 | tf_op jit(solution)/shard_map/slice | solution.py:361
  1.5 0.9 %convert_bitcast_fusion = (f32[1,8,16,128]{3,2,1,0:T(8,128)S(1)}, pred[8,16,128]{2,1,0:T(8,128)(4,1)S(1)}) fusion(s32[8,16,128]{2,1,0:T(8,128)} %param.34), kind=kLoop, calls=%fused_computation.98 | loop fusion | flops 32768 | bytes 147456 | tf_op jit(solution)/shard_map/broadcast_in_dim | solution.py:380
  2.4 0.6 convert_element_type.22.solid_ref
  3.0 0.7 and_select_fusion
  3.7 0.1 add_compare_fusion
  3.8 0.1 fusion.42
  3.9 1.1 %and_convert_fusion.discs_ref = f32[8,10,18,128]{3,2,1,0:T(8,128)} fusion(pred[8,18,128]{2,1,0:T(8,128)(4,1)S(1)} %add_compare_fusion, pred[8,10]{1,0:T(8,128)(4,1)S(1)} %fusion.42), kind=kLoop, calls=%fused_computation | loop fusion | flops 368640 | bytes 755792 | tf_op jit(solution)/shard_map/convert_element_type | solution.py:373
  5.1 2.7 %shard_map.104 = (f32[3,8,16,128]{3,2,1,0:T(8,128)}, f32[8,128]{1,0:T(8,128)}) custom-call(f32[19,8,16,128]{3,2,1,0:T(8,128)} %inner_ref.1, f32[8,10,18,128]{3,2,1,0:T(8,128)} %and_convert_fusion.discs_ref, f32[8,16,128]{2,1,0:T(8,128)} %convert_element_type.22.solid_ref), custom_call_target="tpu_custom_call" | custom-call | flops 1382400 | bytes 1245184 | tf_op jit(solution)/shard_map/pallas_call | solution.py:173
  7.8 0.8 %slice_reduce_fusion.2 = f32[8]{0:T(128)S(1)} fusion(f32[8,128]{1,0:T(8,128)} %get-tuple-element.130), kind=kLoop, calls=%fused_computation.119 | loop fusion | bytes 64 | tf_op jit(solution)/shard_map/slice | solution.py:376
  8.6 3.0 %collective-permute-start.2 = (f32[8]{0:T(128)S(1)}, f32[8]{0:T(128)S(1)}, u32[]{:S(2)}, u32[]{:S(2)}) collective-permute-start(f32[8]{0:T(128)S(1)} %slice_reduce_fusion.2), channel_id=1, source_target_pairs={{0,4},{2,6},{4,8},{6,10},{8,12},{10,14},{12,16},{14,18},{16,20},{1... | collective-permute-start | bytes 104 | tf_op jit(solution)/shard_map/ppermute | solution.py:297
  11.6 3.1 %collective-permute-start.3 = (f32[8]{0:T(128)S(1)}, f32[8]{0:T(128)S(1)}, u32[]{:S(2)}, u32[]{:S(2)}) collective-permute-start(f32[8]{0:T(128)S(1)} %slice_reduce_fusion.2), channel_id=1, source_target_pairs={{0,28},{2,30},{4,0},{6,2},{8,4},{10,6},{12,8},{14,10},{16,12},{18,... | collective-permute-start | bytes 104 | tf_op jit(solution)/shard_map/ppermute | solution.py:297
  14.8 1.6 %collective-permute-start = (f32[22,1,16,128]{3,2,1,0:T(8,128)S(1)}, f32[22,1,16,128]{3,2,1,0:T(8,128)S(1)}, u32[]{:S(2)}, u32[]{:S(2)}) collective-permute-start(f32[22,1,16,128]{3,2,1,0:T(8,128)S(1)} %get-tuple-element.188), channel_id=1, source_target_pairs={{0,2},{2,4},{4,6},{6,8},{8,10},{10,12},{12,14},{14,16},{16,18},{18... | collective-permute-start | bytes 540680 | tf_op jit(solution)/shard_map/ppermute | solution.py:293
  16.4 4.0 %collective-permute-start.1 = (f32[22,1,16,128]{3,2,1,0:T(8,128)S(1)}, f32[22,1,16,128]{3,2,1,0:T(8,128)S(1)}, u32[]{:S(2)}, u32[]{:S(2)}) collective-permute-start(f32[22,1,16,128]{3,2,1,0:T(8,128)S(1)} %get-tuple-element.189), channel_id=1, source_target_pairs={{2,0},{4,2},{6,4},{8,6},{10,8},{12,10},{14,12},{16,14},{18,16},{20... | collective-permute-start | bytes 540680 | tf_op jit(solution)/shard_map/ppermute | solution.py:294
  20.6 0.1 broadcast_multiply_fusion
  20.7 0.2 fusion.19
  21.0 3.6 %collective-permute-done.low_ref = f32[22,1,16,128]{3,2,1,0:T(8,128)S(1)} collective-permute-done((f32[22,1,16,128]{3,2,1,0:T(8,128)S(1)}, f32[22,1,16,128]{3,2,1,0:T(8,128)S(1)}, u32[]{:S(2)}, u32[]{:S(2)}) %collective-permute-start) | collective-permute-done | bytes 180256 | tf_op jit(solution)/shard_map/ppermute | solution.py:293
  24.7 0.2 fusion.2
  24.8 0.4 copy-done.4
  25.3 0.1 fusion.91
  25.4 1.4 %collective-permute-done.4.rows_ref = f32[22,10,2,128]{3,2,1,0:T(2,128)S(1)} collective-permute-done((f32[22,10,2,128]{3,2,1,0:T(2,128)S(1)}, f32[22,10,2,128]{3,2,1,0:T(2,128)S(1)}, u32[]{:S(2)}, u32[]{:S(2)}) %collective-permute-start.4) | collective-permute-done | bytes 225312 | tf_op jit(solution)/shard_map/ppermute | solution.py:288
  26.9 0.1 fusion.38
  27.0 0.7 maximum_bitcast_fusion.solid_ref
  27.7 0.5 fusion.71.strength_ref
  28.2 5.2 %shard_map.105 = (f32[19,8,16,128]{3,2,1,0:T(8,128)}, f32[3,8,16,128]{3,2,1,0:T(8,128)}, f32[8,128]{1,0:T(8,128)}) custom-call(f32[8]{0:T(128)} %fusion.71.strength_ref, f32[19,8,16,128]{3,2,1,0:T(8,128)} %inner_ref.1, f32[22,1,16,128]{3,2,1,0:T(8,128)} %copy-done.4, f32[22,1,16,128]{3,2,1,0:T(8,128)} %copy-done.5, f32[22,10,2,128]{3,2,1,0:T(2,128)} %copy-done.10, ...), custom_call_target="tpu_custom_call" | custom-call | flops 6912000 | bytes 3735552 | tf_op jit(solution)/shard_map/pallas_call | solution.py:203
  33.4 1.1 %fusion.76 = (f32[19,1,16,128]{3,2,1,0:T(8,128)S(1)}, f32[19,1,16,128]{3,2,1,0:T(8,128)S(1)}) fusion(f32[19,8,16,128]{3,2,1,0:T(8,128)} %get-tuple-element.132.inner_ref), kind=kLoop, calls=%fused_computation.171 | loop fusion | bytes 622592 | tf_op jit(solution)/shard_map/slice | solution.py:278
  34.5 0.8 %slice_reduce_fusion.1 = f32[8]{0:T(128)S(1)} fusion(f32[8,128]{1,0:T(8,128)} %get-tuple-element.131), kind=kLoop, calls=%fused_computation.118 | loop fusion | bytes 64 | tf_op jit(solution)/shard_map/slice | solution.py:418
  35.4 1.7 %collective-permute-start.5 = (f32[21,1,16,128]{3,2,1,0:T(8,128)S(1)}, f32[21,1,16,128]{3,2,1,0:T(8,128)S(1)}, u32[]{:S(2)}, u32[]{:S(2)}) collective-permute-start(f32[21,1,16,128]{3,2,1,0:T(8,128)S(1)} %get-tuple-element.180), channel_id=1, source_target_pairs={{0,2},{2,4},{4,6},{6,8},{8,10},{10,12},{12,14},{14,16},{16,18},{18... | collective-permute-start | bytes 516104 | tf_op jit(solution)/shard_map/ppermute | solution.py:293
  37.1 4.0 %collective-permute-start.6 = (f32[21,1,16,128]{3,2,1,0:T(8,128)S(1)}, f32[21,1,16,128]{3,2,1,0:T(8,128)S(1)}, u32[]{:S(2)}, u32[]{:S(2)}) collective-permute-start(f32[21,1,16,128]{3,2,1,0:T(8,128)S(1)} %get-tuple-element.181), channel_id=1, source_target_pairs={{2,0},{4,2},{6,4},{8,6},{10,8},{12,10},{14,12},{16,14},{18,16},{20... | collective-permute-start | bytes 516104 | tf_op jit(solution)/shard_map/ppermute | solution.py:294
  41.0 4.7 %collective-permute-start.8 = (f32[8]{0:T(128)S(1)}, f32[8]{0:T(128)S(1)}, u32[]{:S(2)}, u32[]{:S(2)}) collective-permute-start(f32[8]{0:T(128)S(1)} %slice_reduce_fusion.1), channel_id=1, source_target_pairs={{0,28},{2,30},{4,0},{6,2},{8,4},{10,6},{12,8},{14,10},{16,12},{18,... | collective-permute-start | bytes 104 | tf_op jit(solution)/shard_map/ppermute | solution.py:297
  45.8 1.5 %collective-permute-done.7 = f32[8]{0:T(128)S(1)} collective-permute-done((f32[8]{0:T(128)S(1)}, f32[8]{0:T(128)S(1)}, u32[]{:S(2)}, u32[]{:S(2)}) %collective-permute-start.7) | collective-permute-done | bytes 64 | tf_op jit(solution)/shard_map/ppermute | solution.py:297
  47.4 0.2 fusion.14
  47.6 0.4 copy-done.8
  48.0 0.1 fusion.89
  48.1 1.4 %collective-permute-done.9.rows_ref = f32[21,10,2,128]{3,2,1,0:T(2,128)S(1)} collective-permute-done((f32[21,10,2,128]{3,2,1,0:T(2,128)S(1)}, f32[21,10,2,128]{3,2,1,0:T(2,128)S(1)}, u32[]{:S(2)}, u32[]{:S(2)}) %collective-permute-start.9) | collective-permute-done | bytes 215072 | tf_op jit(solution)/shard_map/ppermute | solution.py:288
  49.6 0.1 fusion.32
  49.7 0.6 fusion.72.strength_ref
  50.3 5.3 %shard_map.106 = (f32[19,8,16,128]{3,2,1,0:T(8,128)}, f32[3,8,16,128]{3,2,1,0:T(8,128)}, f32[8,128]{1,0:T(8,128)}) custom-call(f32[8]{0:T(128)} %fusion.72.strength_ref, f32[19,8,16,128]{3,2,1,0:T(8,128)} %get-tuple-element.132.inner_ref, f32[21,1,16,128]{3,2,1,0:T(8,128)} %copy-done.8, f32[21,1,16,128]{3,2,1,0:T(8,128)} %copy-done.9, ...), custom_call_target="tpu_custom_call" | custom-call | flops 6912000 | bytes 3735552 | tf_op jit(solution)/shard_map/pallas_call | solution.py:203
  55.5 1.1 %fusion.75 = (f32[19,1,16,128]{3,2,1,0:T(8,128)S(1)}, f32[19,1,16,128]{3,2,1,0:T(8,128)S(1)}) fusion(f32[19,8,16,128]{3,2,1,0:T(8,128)} %get-tuple-element.135.inner_ref), kind=kLoop, calls=%fused_computation.170 | loop fusion | bytes 622592 | tf_op jit(solution)/shard_map/slice | solution.py:278
  56.6 0.8 %slice_reduce_fusion = f32[8]{0:T(128)S(1)} fusion(f32[8,128]{1,0:T(8,128)} %get-tuple-element.134), kind=kLoop, calls=%fused_computation.115 | loop fusion | bytes 64 | tf_op jit(solution)/shard_map/slice | solution.py:418
  57.6 5.6 %collective-permute-start.11 = (f32[21,1,16,128]{3,2,1,0:T(8,128)S(1)}, f32[21,1,16,128]{3,2,1,0:T(8,128)S(1)}, u32[]{:S(2)}, u32[]{:S(2)}) collective-permute-start(f32[21,1,16,128]{3,2,1,0:T(8,128)S(1)} %get-tuple-element.179), channel_id=1, source_target_pairs={{2,0},{4,2},{6,4},{8,6},{10,8},{12,10},{14,12},{16,14},{18,16},{20... | collective-permute-start | bytes 516104 | tf_op jit(solution)/shard_map/ppermute | solution.py:294
  63.2 4.7 %collective-permute-start.13 = (f32[8]{0:T(128)S(1)}, f32[8]{0:T(128)S(1)}, u32[]{:S(2)}, u32[]{:S(2)}) collective-permute-start(f32[8]{0:T(128)S(1)} %slice_reduce_fusion), channel_id=1, source_target_pairs={{0,28},{2,30},{4,0},{6,2},{8,4},{10,6},{12,8},{14,10},{16,12},{18,... | collective-permute-start | bytes 104 | tf_op jit(solution)/shard_map/ppermute | solution.py:297
  67.9 1.5 %collective-permute-done.12 = f32[8]{0:T(128)S(1)} collective-permute-done((f32[8]{0:T(128)S(1)}, f32[8]{0:T(128)S(1)}, u32[]{:S(2)}, u32[]{:S(2)}) %collective-permute-start.12) | collective-permute-done | bytes 64 | tf_op jit(solution)/shard_map/ppermute | solution.py:297
  69.6 0.2 fusion.9
  69.7 0.4 copy-done.6
  70.2 1.4 %collective-permute-done.14.rows_ref = f32[21,10,2,128]{3,2,1,0:T(2,128)S(1)} collective-permute-done((f32[21,10,2,128]{3,2,1,0:T(2,128)S(1)}, f32[21,10,2,128]{3,2,1,0:T(2,128)S(1)}, u32[]{:S(2)}, u32[]{:S(2)}) %collective-permute-start.14) | collective-permute-done | bytes 215072 | tf_op jit(solution)/shard_map/ppermute | solution.py:288
  71.7 0.7 fusion.26
  72.4 0.6 fusion.73.strength_ref
  73.0 4.9 %shard_map.107 = f32[19,8,16,128]{3,2,1,0:T(8,128)} custom-call(f32[8]{0:T(128)} %fusion.73.strength_ref, f32[19,8,16,128]{3,2,1,0:T(8,128)} %get-tuple-element.135.inner_ref, f32[21,1,16,128]{3,2,1,0:T(8,128)} %copy-done.6, f32[21,1,16,128]{3,2,1,0:T(8,128)} %copy-done.7, f32[21,10,2,128]{3,2,1,0:T(2,128)} %copy-done.12, ...), custom_call_target="tpu_custom_call" | custom-call | flops 6912000 | bytes 3735552 | tf_op jit(solution)/shard_map/pallas_call | solution.py:203
  (98 shorter events, 1.2 us)
Async XLA Ops:
  5.0 9.7 %copy-start = (f32[19,8,16,128]{3,2,1,0:T(8,128)S(1)}, f32[19,8,16,128]{3,2,1,0:T(8,128)}, u32[]{:S(2)}) copy-start(f32[19,8,16,128]{3,2,1,0:T(8,128)} %inner_ref.1) | copy-start | bytes 3735556
  5.1 9.7 %copy-start.3 = (f32[8,16,128]{2,1,0:T(8,128)S(1)}, f32[8,16,128]{2,1,0:T(8,128)}, u32[]{:S(2)}) copy-start(f32[8,16,128]{2,1,0:T(8,128)} %param.35) | copy-start | bytes 196612
  7.8 12.7 %copy-start.18 = (s32[16,3]{0,1:T(4,128)S(1)}, s32[16,3]{0,1:T(4,128)}, u32[]{:S(2)}) copy-start(s32[16,3]{0,1:T(4,128)} %param.39) | copy-start | bytes 580
  7.8 13.0 %copy-start.19 = (f32[16]{0:T(128)S(1)}, f32[16]{0:T(128)}, u32[]{:S(2)}) copy-start(f32[16]{0:T(128)} %param.40) | copy-start | bytes 196
  8.6 12.4 %collective-permute-start.2 = (f32[8]{0:T(128)S(1)}, f32[8]{0:T(128)S(1)}, u32[]{:S(2)}, u32[]{:S(2)}) collective-permute-start(f32[8]{0:T(128)S(1)} %slice_reduce_fusion.2), channel_id=1, source_target_pairs={{0,4},{2,6},{4,8},{6,10},{8,12},{10,14},{12,16},{14,18},{16,20},{1... | collective-permute-start | bytes 104 | tf_op jit(solution)/shard_map/ppermute | solution.py:297
  11.6 9.4 %collective-permute-start.3 = (f32[8]{0:T(128)S(1)}, f32[8]{0:T(128)S(1)}, u32[]{:S(2)}, u32[]{:S(2)}) collective-permute-start(f32[8]{0:T(128)S(1)} %slice_reduce_fusion.2), channel_id=1, source_target_pairs={{0,28},{2,30},{4,0},{6,2},{8,4},{10,6},{12,8},{14,10},{16,12},{18,... | collective-permute-start | bytes 104 | tf_op jit(solution)/shard_map/ppermute | solution.py:297
  14.8 9.8 %collective-permute-start = (f32[22,1,16,128]{3,2,1,0:T(8,128)S(1)}, f32[22,1,16,128]{3,2,1,0:T(8,128)S(1)}, u32[]{:S(2)}, u32[]{:S(2)}) collective-permute-start(f32[22,1,16,128]{3,2,1,0:T(8,128)S(1)} %get-tuple-element.188), channel_id=1, source_target_pairs={{0,2},{2,4},{4,6},{6,8},{8,10},{10,12},{12,14},{14,16},{16,18},{18... | collective-permute-start | bytes 540680 | tf_op jit(solution)/shard_map/ppermute | solution.py:293
  16.4 8.1 %collective-permute-start.1 = (f32[22,1,16,128]{3,2,1,0:T(8,128)S(1)}, f32[22,1,16,128]{3,2,1,0:T(8,128)S(1)}, u32[]{:S(2)}, u32[]{:S(2)}) collective-permute-start(f32[22,1,16,128]{3,2,1,0:T(8,128)S(1)} %get-tuple-element.189), channel_id=1, source_target_pairs={{2,0},{4,2},{6,4},{8,6},{10,8},{12,10},{14,12},{16,14},{18,16},{20... | collective-permute-start | bytes 540680 | tf_op jit(solution)/shard_map/ppermute | solution.py:294
  24.6 0.7 copy-start.4
  24.6 0.7 copy-start.5
  24.7 2.2 %copy-start.13 = (f32[3,8,16,128]{3,2,1,0:T(8,128)S(1)}, f32[3,8,16,128]{3,2,1,0:T(8,128)}, u32[]{:S(2)}) copy-start(f32[3,8,16,128]{3,2,1,0:T(8,128)} %get-tuple-element.133) | copy-start | bytes 589828
  25.3 2.3 %copy-start.16 = (f32[8]{0:T(128)S(1)}, f32[8]{0:T(128)}, u32[]{:S(2)}) copy-start(f32[8]{0:T(128)} %param.37) | copy-start | bytes 100
  25.3 2.3 %copy-start.17 = (f32[8]{0:T(128)S(1)}, f32[8]{0:T(128)}, u32[]{:S(2)}) copy-start(f32[8]{0:T(128)} %param.38) | copy-start | bytes 100
  25.3 1.5 %collective-permute-start.4 = (f32[22,10,2,128]{3,2,1,0:T(2,128)S(1)}, f32[22,10,2,128]{3,2,1,0:T(2,128)S(1)}, u32[]{:S(2)}, u32[]{:S(2)}) collective-permute-start(f32[22,10,2,128]{3,2,1,0:T(2,128)S(1)} %fusion.2), channel_id=1, source_target_pairs={{0,1},{1,0},{2,3},{3,2},{4,5},{5,4},{6,7},{7,6},{8,9},{9,8},{10,11... | collective-permute-start | bytes 675848 | tf_op jit(solution)/shard_map/ppermute | solution.py:288
  26.8 1.4 %copy-start.10 = (f32[22,10,2,128]{3,2,1,0:T(2,128)}, f32[22,10,2,128]{3,2,1,0:T(2,128)S(1)}, u32[]{:S(2)}) copy-start(f32[22,10,2,128]{3,2,1,0:T(2,128)S(1)} %collective-permute-done.4.rows_ref) | copy-start | bytes 675844
  33.4 14.0 %copy-start.1 = (f32[19,8,16,128]{3,2,1,0:T(8,128)S(1)}, f32[19,8,16,128]{3,2,1,0:T(8,128)}, u32[]{:S(2)}) copy-start(f32[19,8,16,128]{3,2,1,0:T(8,128)} %get-tuple-element.132.inner_ref) | copy-start | bytes 3735556
  35.4 11.9 %collective-permute-start.5 = (f32[21,1,16,128]{3,2,1,0:T(8,128)S(1)}, f32[21,1,16,128]{3,2,1,0:T(8,128)S(1)}, u32[]{:S(2)}, u32[]{:S(2)}) collective-permute-start(f32[21,1,16,128]{3,2,1,0:T(8,128)S(1)} %get-tuple-element.180), channel_id=1, source_target_pairs={{0,2},{2,4},{4,6},{6,8},{8,10},{10,12},{12,14},{14,16},{16,18},{18... | collective-permute-start | bytes 516104 | tf_op jit(solution)/shard_map/ppermute | solution.py:293
  37.1 10.2 %collective-permute-start.6 = (f32[21,1,16,128]{3,2,1,0:T(8,128)S(1)}, f32[21,1,16,128]{3,2,1,0:T(8,128)S(1)}, u32[]{:S(2)}, u32[]{:S(2)}) collective-permute-start(f32[21,1,16,128]{3,2,1,0:T(8,128)S(1)} %get-tuple-element.181), channel_id=1, source_target_pairs={{2,0},{4,2},{6,4},{8,6},{10,8},{12,10},{14,12},{16,14},{18,16},{20... | collective-permute-start | bytes 516104 | tf_op jit(solution)/shard_map/ppermute | solution.py:294
  41.0 6.2 %collective-permute-start.7 = (f32[8]{0:T(128)S(1)}, f32[8]{0:T(128)S(1)}, u32[]{:S(2)}, u32[]{:S(2)}) collective-permute-start(f32[8]{0:T(128)S(1)} %slice_reduce_fusion.1), channel_id=1, source_target_pairs={{0,4},{2,6},{4,8},{6,10},{8,12},{10,14},{12,16},{14,18},{16,20},{1... | collective-permute-start | bytes 104 | tf_op jit(solution)/shard_map/ppermute | solution.py:297
  41.0 6.2 %collective-permute-start.8 = (f32[8]{0:T(128)S(1)}, f32[8]{0:T(128)S(1)}, u32[]{:S(2)}, u32[]{:S(2)}) collective-permute-start(f32[8]{0:T(128)S(1)} %slice_reduce_fusion.1), channel_id=1, source_target_pairs={{0,28},{2,30},{4,0},{6,2},{8,4},{10,6},{12,8},{14,10},{16,12},{18,... | collective-permute-start | bytes 104 | tf_op jit(solution)/shard_map/ppermute | solution.py:297
  47.3 0.7 copy-start.8
  47.3 0.7 copy-start.9
  47.4 2.1 %copy-start.15 = (f32[3,8,16,128]{3,2,1,0:T(8,128)S(1)}, f32[3,8,16,128]{3,2,1,0:T(8,128)}, u32[]{:S(2)}) copy-start(f32[3,8,16,128]{3,2,1,0:T(8,128)} %get-tuple-element.136) | copy-start | bytes 589828
  48.0 1.5 %collective-permute-start.9 = (f32[21,10,2,128]{3,2,1,0:T(2,128)S(1)}, f32[21,10,2,128]{3,2,1,0:T(2,128)S(1)}, u32[]{:S(2)}, u32[]{:S(2)}) collective-permute-start(f32[21,10,2,128]{3,2,1,0:T(2,128)S(1)} %fusion.14), channel_id=1, source_target_pairs={{0,1},{1,0},{2,3},{3,2},{4,5},{5,4},{6,7},{7,6},{8,9},{9,8},{10,11... | collective-permute-start | bytes 645128 | tf_op jit(solution)/shard_map/ppermute | solution.py:288
  49.5 0.8 %copy-start.11 = (f32[21,10,2,128]{3,2,1,0:T(2,128)}, f32[21,10,2,128]{3,2,1,0:T(2,128)S(1)}, u32[]{:S(2)}) copy-start(f32[21,10,2,128]{3,2,1,0:T(2,128)S(1)} %collective-permute-done.9.rows_ref) | copy-start | bytes 645124
  55.5 14.0 %copy-start.2 = (f32[19,8,16,128]{3,2,1,0:T(8,128)S(1)}, f32[19,8,16,128]{3,2,1,0:T(8,128)}, u32[]{:S(2)}) copy-start(f32[19,8,16,128]{3,2,1,0:T(8,128)} %get-tuple-element.135.inner_ref) | copy-start | bytes 3735556
  57.5 11.9 %collective-permute-start.10 = (f32[21,1,16,128]{3,2,1,0:T(8,128)S(1)}, f32[21,1,16,128]{3,2,1,0:T(8,128)S(1)}, u32[]{:S(2)}, u32[]{:S(2)}) collective-permute-start(f32[21,1,16,128]{3,2,1,0:T(8,128)S(1)} %get-tuple-element.178), channel_id=1, source_target_pairs={{0,2},{2,4},{4,6},{6,8},{8,10},{10,12},{12,14},{14,16},{16,18},{18... | collective-permute-start | bytes 516104 | tf_op jit(solution)/shard_map/ppermute | solution.py:293
  57.6 11.9 %collective-permute-start.11 = (f32[21,1,16,128]{3,2,1,0:T(8,128)S(1)}, f32[21,1,16,128]{3,2,1,0:T(8,128)S(1)}, u32[]{:S(2)}, u32[]{:S(2)}) collective-permute-start(f32[21,1,16,128]{3,2,1,0:T(8,128)S(1)} %get-tuple-element.179), channel_id=1, source_target_pairs={{2,0},{4,2},{6,4},{8,6},{10,8},{12,10},{14,12},{16,14},{18,16},{20... | collective-permute-start | bytes 516104 | tf_op jit(solution)/shard_map/ppermute | solution.py:294
  63.2 6.2 %collective-permute-start.12 = (f32[8]{0:T(128)S(1)}, f32[8]{0:T(128)S(1)}, u32[]{:S(2)}, u32[]{:S(2)}) collective-permute-start(f32[8]{0:T(128)S(1)} %slice_reduce_fusion), channel_id=1, source_target_pairs={{0,4},{2,6},{4,8},{6,10},{8,12},{10,14},{12,16},{14,18},{16,20},{1... | collective-permute-start | bytes 104 | tf_op jit(solution)/shard_map/ppermute | solution.py:297
  63.2 6.2 %collective-permute-start.13 = (f32[8]{0:T(128)S(1)}, f32[8]{0:T(128)S(1)}, u32[]{:S(2)}, u32[]{:S(2)}) collective-permute-start(f32[8]{0:T(128)S(1)} %slice_reduce_fusion), channel_id=1, source_target_pairs={{0,28},{2,30},{4,0},{6,2},{8,4},{10,6},{12,8},{14,10},{16,12},{18,... | collective-permute-start | bytes 104 | tf_op jit(solution)/shard_map/ppermute | solution.py:297
  69.4 0.7 copy-start.6
  69.4 0.7 copy-start.7
  69.5 2.1 %copy-start.14 = (f32[3,8,16,128]{3,2,1,0:T(8,128)S(1)}, f32[3,8,16,128]{3,2,1,0:T(8,128)}, u32[]{:S(2)}) copy-start(f32[3,8,16,128]{3,2,1,0:T(8,128)} %get-tuple-element.137) | copy-start | bytes 589828
  70.2 1.5 %collective-permute-start.14 = (f32[21,10,2,128]{3,2,1,0:T(2,128)S(1)}, f32[21,10,2,128]{3,2,1,0:T(2,128)S(1)}, u32[]{:S(2)}, u32[]{:S(2)}) collective-permute-start(f32[21,10,2,128]{3,2,1,0:T(2,128)S(1)} %fusion.9), channel_id=1, source_target_pairs={{0,1},{1,0},{2,3},{3,2},{4,5},{5,4},{6,7},{7,6},{8,9},{9,8},{10,11... | collective-permute-start | bytes 645128 | tf_op jit(solution)/shard_map/ppermute | solution.py:288
  71.6 1.4 %copy-start.12 = (f32[21,10,2,128]{3,2,1,0:T(2,128)}, f32[21,10,2,128]{3,2,1,0:T(2,128)S(1)}, u32[]{:S(2)}) copy-start(f32[21,10,2,128]{3,2,1,0:T(2,128)S(1)} %collective-permute-done.14.rows_ref) | copy-start | bytes 645124

commit v20 on v18

--- a/solution.py
+++ b/solution.py
@@ -161,9 +161,7 @@
 
     lax.fori_loop(0, populations_ref.shape[1], moment_plane, 0)
     for fan_number in range(fans):
-        flow_ref[fan_number : fan_number + 1, :] = jnp.broadcast_to(
-            jnp.sum(sums_ref[fan_number], axis=(0, 1), keepdims=True), (1, flow_ref.shape[1])
-        )
+        flow_ref[fan_number] = jnp.sum(sums_ref[fan_number])
 
 
 def first_moments(populations, discs, solid):
@@ -175,10 +173,10 @@
         ),
         out_shape=(
             jax.ShapeDtypeStruct((3, slab_len, band_width, height), jnp.float32),
-            jax.ShapeDtypeStruct((fans, height), jnp.float32),
+            jax.ShapeDtypeStruct((fans,), jnp.float32),
         ),
         in_specs=[vmem, vmem, vmem],
-        out_specs=(vmem, vmem),
+        out_specs=(vmem, pl.BlockSpec(memory_space=pltpu.SMEM)),
         scratch_shapes=[pltpu.VMEM((fans, band_width, height), jnp.float32)],
         cost_estimate=pl.CostEstimate(
             flops=60 * discs[0].size, transcendentals=0, bytes_accessed=4 * populations.size
@@ -194,7 +192,7 @@
     out_shape = [jax.ShapeDtypeStruct((19, slab_len, band_width, height), jnp.float32)]
     if with_moments:
         out_shape.append(jax.ShapeDtypeStruct((3, slab_len, band_width, height), jnp.float32))
-        out_shape.append(jax.ShapeDtypeStruct((fans, height), jnp.float32))
+        out_shape.append(jax.ShapeDtypeStruct((fans,), jnp.float32))
     scratch = [pltpu.VMEM((19, slab_len + 2, band_width + 2, height), jnp.float32)]
     if with_moments:
         scratch.append(pltpu.VMEM((fans, band_width, height), jnp.float32))
@@ -203,7 +201,10 @@
         functools.partial(step_kernel, with_moments),
         out_shape=tuple(out_shape),
         in_specs=[pl.BlockSpec(memory_space=pltpu.SMEM)] + [vmem] * 6,
-        out_specs=tuple([vmem] * len(out_shape)),
+        out_specs=tuple(
+            [vmem] * (len(out_shape) - 1)
+            + [pl.BlockSpec(memory_space=pltpu.SMEM) if with_moments else vmem]
+        ),
         scratch_shapes=scratch,
         cost_estimate=pl.CostEstimate(
             flops=300 * solid_rim.size, transcendentals=0, bytes_accessed=12 * inner.size
@@ -372,7 +373,7 @@
     discs = (along_in[:, :, None, None] & across_in[:, None]).astype(jnp.float32)
     solid_planes = solid_flag.astype(jnp.float32)
     velocity, flow = first_moments(populations, discs[:, 1:-1, 0:band_width], solid_planes)
-    partials = flow[:, 0]
+    partials = flow
     for repeat in range(ITERS):
         fields = [populations, smoke_field[None]]
         if repeat == 0:
@@ -414,7 +415,7 @@
         populations = stepped[0]
         if not last:
             velocity = stepped[1]
-            partials = stepped[2][:, 0]
+            partials = stepped[2]
     return (populations, smoke_field)
 
 

time: 77.1 us -> 76.6 us (level)
  local copies, waits for them, and re-layouts: 8.18 us -> 7.06 us
    slice x3 -> x0, local copies, waits for them, and re-layouts: 2.4 us -> none  [the longest x2 1.61 us: body(): partials = stepped[2][:, 0]]
    broadcast_in_dim x4, local copies, waits for them, and re-layouts: 0.02 us -> 1.27 us  [piece(): jnp.zeros(cells[0].shape[1:], jnp.float32).at[0, 0, :fans].set(flow)[None]]
  transfers between devices with their start and end apart: 15 -> 15, of which waited for: 6 -> 6; matrix products, arithmetic and copies ran while one was open for 1% -> 2% of each run, Pallas kernels for 0% -> 0%
where the time goes in v20:
time: 76.6 us; the launch traced here: 76.3 us
  starting transfers between devices  32.6 us (43%)
  Pallas kernels  17.8 us (23%)
  waiting for transfers between devices  10.8 us (14%)
  local copies, waits for them, and re-layouts  7.06 us (9%)
  other arithmetic  6.57 us (9%)
  between operations  1.2 us (2%)
    ppermute x6, starting transfers between devices, rim_round(): lax.ppermute(flow, axis, [(i, (i + offset) % count) for i in range(count)])  15.6 us
    pallas_call x3, Pallas kernels, lattice_step(): pl.pallas_call(functools.partial(step_kernel, with_moments), out_shape=tu...  15.4 us
    ppermute x3, starting transfers between devices, rim_round(): from_right = lax.ppermute(head, axis, backward)  13.6 us
    ppermute x3, waiting for transfers between devices, rim_round(): both = lax.ppermute(jnp.concatenate([tail, head], axis=dim), axis, forward)  4.17 us
    ppermute x3, waiting for transfers between devices, rim_round(): from_left = lax.ppermute(tail, axis, forward)  3.58 us
    ppermute x3, starting transfers between devices, rim_round(): from_left = lax.ppermute(tail, axis, forward)  3.39 us
    ppermute x6, waiting for transfers between devices, rim_round(): lax.ppermute(flow, axis, [(i, (i + offset) % count) for i in range(count)])  3.04 us
    pallas_call x1, Pallas kernels, first_moments(): pl.pallas_call(lambda populations_ref, discs_ref, solid_ref, velocity_ref...  2.47 us
  transfers between devices with their start and end apart: 15, of which 6 were waited for; matrix products, arithmetic and copies ran while one was open for 2% of the time, Pallas kernels for 0%

profile of v20, /device:TPU:0, one launch (start us, length us, event | category | flops | bytes accessed | tf_op | source)
XLA Modules:
  0.0 76.3 jit_solution(17299446107408808525)
XLA Ops:
  0.6 0.8 %slice_bitcast_fusion.12 = (s32[8]{0:T(128)S(1)}, s32[8]{0:T(128)S(1)}, s32[8]{0:T(128)S(1)}) fusion(s32[8,3]{0,1:T(4,128)} %param.36), kind=kLoop, calls=%fused_computation.161 | loop fusion | bytes 192 | tf_op jit(solution)/shard_map/slice | solution.py:361
  1.5 0.7 and_select_fusion
  2.3 0.1 add_compare_fusion
  2.4 0.1 fusion.42
  2.4 0.2 and_convert_fusion.discs_ref
  2.6 0.9 %slice.615.discs_ref = f32[8,8,16,128]{3,2,1,0:T(8,128)} slice(f32[8,10,18,128]{3,2,1,0:T(8,128)S(1)} %and_convert_fusion.discs_ref), slice={[0:8], [1:9], [0:16], [0:128]} | slice | bytes 1048576 | tf_op jit(solution)/shard_map/slice | solution.py:375
  3.5 0.6 convert_element_type.22.solid_ref
  4.2 2.5 %shard_map.104 = (f32[3,8,16,128]{3,2,1,0:T(8,128)}, f32[8]{0:T(128)}) custom-call(f32[19,8,16,128]{3,2,1,0:T(8,128)} %inner_ref.1, f32[8,8,16,128]{3,2,1,0:T(8,128)} %slice.615.discs_ref, f32[8,16,128]{2,1,0:T(8,128)} %convert_element_type.22.solid_ref), custom_call_target="tpu_custom_call" | custom-call | flops 983040 | bytes 1245184 | tf_op jit(solution)/shard_map/pallas_call | solution.py:170
  6.7 3.0 %collective-permute-start.2 = (f32[8]{0:T(128)}, f32[8]{0:T(128)S(1)}, u32[]{:S(2)}, u32[]{:S(2)}) collective-permute-start(f32[8]{0:T(128)} %get-tuple-element.130), channel_id=1, source_target_pairs={{0,4},{2,6},{4,8},{6,10},{8,12},{10,14},{12,16},{14,18},{16,20},{1... | collective-permute-start | bytes 104 | tf_op jit(solution)/shard_map/ppermute | solution.py:297
  9.7 3.1 %collective-permute-start.3 = (f32[8]{0:T(128)}, f32[8]{0:T(128)S(1)}, u32[]{:S(2)}, u32[]{:S(2)}) collective-permute-start(f32[8]{0:T(128)} %get-tuple-element.130), channel_id=1, source_target_pairs={{0,28},{2,30},{4,0},{6,2},{8,4},{10,6},{12,8},{14,10},{16,12},{18,... | collective-permute-start | bytes 104 | tf_op jit(solution)/shard_map/ppermute | solution.py:297
  12.9 0.7 fusion.17
  13.6 1.6 %collective-permute-start = (f32[22,1,16,128]{3,2,1,0:T(8,128)S(1)}, f32[22,1,16,128]{3,2,1,0:T(8,128)S(1)}, u32[]{:S(2)}, u32[]{:S(2)}) collective-permute-start(f32[22,1,16,128]{3,2,1,0:T(8,128)S(1)} %get-tuple-element.188), channel_id=1, source_target_pairs={{0,2},{2,4},{4,6},{6,8},{8,10},{10,12},{12,14},{14,16},{16,18},{18... | collective-permute-start | bytes 540680 | tf_op jit(solution)/shard_map/ppermute | solution.py:293
  15.2 4.0 %collective-permute-start.1 = (f32[22,1,16,128]{3,2,1,0:T(8,128)S(1)}, f32[22,1,16,128]{3,2,1,0:T(8,128)S(1)}, u32[]{:S(2)}, u32[]{:S(2)}) collective-permute-start(f32[22,1,16,128]{3,2,1,0:T(8,128)S(1)} %get-tuple-element.189), channel_id=1, source_target_pairs={{2,0},{4,2},{6,4},{8,6},{10,8},{12,10},{14,12},{16,14},{18,16},{20... | collective-permute-start | bytes 540680 | tf_op jit(solution)/shard_map/ppermute | solution.py:294
  19.4 0.1 broadcast_multiply_fusion
  19.5 0.2 fusion.19
  19.8 3.6 %collective-permute-done.low_ref = f32[22,1,16,128]{3,2,1,0:T(8,128)S(1)} collective-permute-done((f32[22,1,16,128]{3,2,1,0:T(8,128)S(1)}, f32[22,1,16,128]{3,2,1,0:T(8,128)S(1)}, u32[]{:S(2)}, u32[]{:S(2)}) %collective-permute-start) | collective-permute-done | bytes 180256 | tf_op jit(solution)/shard_map/ppermute | solution.py:293
  23.5 0.2 fusion.2
  23.6 0.4 copy-done.5
  24.0 0.1 copy-done.6
  24.1 0.1 fusion.91
  24.2 1.4 %collective-permute-done.4.rows_ref = f32[22,10,2,128]{3,2,1,0:T(2,128)S(1)} collective-permute-done((f32[22,10,2,128]{3,2,1,0:T(2,128)S(1)}, f32[22,10,2,128]{3,2,1,0:T(2,128)S(1)}, u32[]{:S(2)}, u32[]{:S(2)}) %collective-permute-start.4) | collective-permute-done | bytes 225312 | tf_op jit(solution)/shard_map/ppermute | solution.py:288
  25.6 0.1 fusion.38
  25.8 0.7 maximum_bitcast_fusion.solid_ref
  26.4 0.5 fusion.71.strength_ref
  27.0 5.2 %shard_map.105 = (f32[19,8,16,128]{3,2,1,0:T(8,128)}, f32[3,8,16,128]{3,2,1,0:T(8,128)}, f32[8]{0:T(128)}) custom-call(f32[8]{0:T(128)} %fusion.71.strength_ref, f32[19,8,16,128]{3,2,1,0:T(8,128)} %inner_ref.1, f32[22,1,16,128]{3,2,1,0:T(8,128)} %copy-done.5, f32[22,1,16,128]{3,2,1,0:T(8,128)} %copy-done.6, f32[22,10,2,128]{3,2,1,0:T(2,128)} %copy-done.11, ...), custom_call_target="tpu_custom_call" | custom-call | flops 6912000 | bytes 3735552 | tf_op jit(solution)/shard_map/pallas_call | solution.py:200
  32.2 1.1 %fusion.76 = (f32[19,1,16,128]{3,2,1,0:T(8,128)S(1)}, f32[19,1,16,128]{3,2,1,0:T(8,128)S(1)}) fusion(f32[19,8,16,128]{3,2,1,0:T(8,128)} %get-tuple-element.132.inner_ref), kind=kLoop, calls=%fused_computation.168 | loop fusion | bytes 622592 | tf_op jit(solution)/shard_map/slice | solution.py:278
  33.3 0.7 pad_bitcast_fusion.1
  34.0 1.7 %collective-permute-start.5 = (f32[21,1,16,128]{3,2,1,0:T(8,128)S(1)}, f32[21,1,16,128]{3,2,1,0:T(8,128)S(1)}, u32[]{:S(2)}, u32[]{:S(2)}) collective-permute-start(f32[21,1,16,128]{3,2,1,0:T(8,128)S(1)} %get-tuple-element.180), channel_id=1, source_target_pairs={{0,2},{2,4},{4,6},{6,8},{8,10},{10,12},{12,14},{14,16},{16,18},{18... | collective-permute-start | bytes 516104 | tf_op jit(solution)/shard_map/ppermute | solution.py:293
  35.7 4.0 %collective-permute-start.6 = (f32[21,1,16,128]{3,2,1,0:T(8,128)S(1)}, f32[21,1,16,128]{3,2,1,0:T(8,128)S(1)}, u32[]{:S(2)}, u32[]{:S(2)}) collective-permute-start(f32[21,1,16,128]{3,2,1,0:T(8,128)S(1)} %get-tuple-element.181), channel_id=1, source_target_pairs={{2,0},{4,2},{6,4},{8,6},{10,8},{12,10},{14,12},{16,14},{18,16},{20... | collective-permute-start | bytes 516104 | tf_op jit(solution)/shard_map/ppermute | solution.py:294
  39.7 4.7 %collective-permute-start.8 = (f32[8]{0:T(128)S(1)}, f32[8]{0:T(128)S(1)}, u32[]{:S(2)}, u32[]{:S(2)}) collective-permute-start(f32[8]{0:T(128)S(1)} %copy-done.22), channel_id=1, source_target_pairs={{0,28},{2,30},{4,0},{6,2},{8,4},{10,6},{12,8},{14,10},{16,12},{18,... | collective-permute-start | bytes 104 | tf_op jit(solution)/shard_map/ppermute | solution.py:297
  44.4 1.5 %collective-permute-done.7 = f32[8]{0:T(128)S(1)} collective-permute-done((f32[8]{0:T(128)S(1)}, f32[8]{0:T(128)S(1)}, u32[]{:S(2)}, u32[]{:S(2)}) %collective-permute-start.7) | collective-permute-done | bytes 64 | tf_op jit(solution)/shard_map/ppermute | solution.py:297
  46.1 0.2 fusion.14
  46.3 0.4 copy-done.9
  46.8 1.4 %collective-permute-done.9.rows_ref = f32[21,10,2,128]{3,2,1,0:T(2,128)S(1)} collective-permute-done((f32[21,10,2,128]{3,2,1,0:T(2,128)S(1)}, f32[21,10,2,128]{3,2,1,0:T(2,128)S(1)}, u32[]{:S(2)}, u32[]{:S(2)}) %collective-permute-start.9) | collective-permute-done | bytes 215072 | tf_op jit(solution)/shard_map/ppermute | solution.py:288
  48.2 0.1 fusion.32
  48.4 0.5 fusion.72.strength_ref
  48.9 5.3 %shard_map.106 = (f32[19,8,16,128]{3,2,1,0:T(8,128)}, f32[3,8,16,128]{3,2,1,0:T(8,128)}, f32[8]{0:T(128)}) custom-call(f32[8]{0:T(128)} %fusion.72.strength_ref, f32[19,8,16,128]{3,2,1,0:T(8,128)} %get-tuple-element.132.inner_ref, f32[21,1,16,128]{3,2,1,0:T(8,128)} %copy-done.9, f32[21,1,16,128]{3,2,1,0:T(8,128)} %copy-done.10, ...), custom_call_target="tpu_custom_call" | custom-call | flops 6912000 | bytes 3735552 | tf_op jit(solution)/shard_map/pallas_call | solution.py:200
  54.2 1.1 %fusion.75 = (f32[19,1,16,128]{3,2,1,0:T(8,128)S(1)}, f32[19,1,16,128]{3,2,1,0:T(8,128)S(1)}) fusion(f32[19,8,16,128]{3,2,1,0:T(8,128)} %get-tuple-element.135.inner_ref), kind=kLoop, calls=%fused_computation.167 | loop fusion | bytes 622592 | tf_op jit(solution)/shard_map/slice | solution.py:278
  55.3 0.6 pad_bitcast_fusion
  56.0 5.6 %collective-permute-start.11 = (f32[21,1,16,128]{3,2,1,0:T(8,128)S(1)}, f32[21,1,16,128]{3,2,1,0:T(8,128)S(1)}, u32[]{:S(2)}, u32[]{:S(2)}) collective-permute-start(f32[21,1,16,128]{3,2,1,0:T(8,128)S(1)} %get-tuple-element.179), channel_id=1, source_target_pairs={{2,0},{4,2},{6,4},{8,6},{10,8},{12,10},{14,12},{16,14},{18,16},{20... | collective-permute-start | bytes 516104 | tf_op jit(solution)/shard_map/ppermute | solution.py:294
  61.6 4.7 %collective-permute-start.13 = (f32[8]{0:T(128)S(1)}, f32[8]{0:T(128)S(1)}, u32[]{:S(2)}, u32[]{:S(2)}) collective-permute-start(f32[8]{0:T(128)S(1)} %copy-done.21), channel_id=1, source_target_pairs={{0,28},{2,30},{4,0},{6,2},{8,4},{10,6},{12,8},{14,10},{16,12},{18,... | collective-permute-start | bytes 104 | tf_op jit(solution)/shard_map/ppermute | solution.py:297
  66.3 1.5 %collective-permute-done.12 = f32[8]{0:T(128)S(1)} collective-permute-done((f32[8]{0:T(128)S(1)}, f32[8]{0:T(128)S(1)}, u32[]{:S(2)}, u32[]{:S(2)}) %collective-permute-start.12) | collective-permute-done | bytes 64 | tf_op jit(solution)/shard_map/ppermute | solution.py:297
  68.0 0.2 fusion.9
  68.2 0.4 copy-done.7
  68.7 1.4 %collective-permute-done.14.rows_ref = f32[21,10,2,128]{3,2,1,0:T(2,128)S(1)} collective-permute-done((f32[21,10,2,128]{3,2,1,0:T(2,128)S(1)}, f32[21,10,2,128]{3,2,1,0:T(2,128)S(1)}, u32[]{:S(2)}, u32[]{:S(2)}) %collective-permute-start.14) | collective-permute-done | bytes 215072 | tf_op jit(solution)/shard_map/ppermute | solution.py:288
  70.2 0.7 fusion.26
  70.9 0.5 fusion.73.strength_ref
  71.4 4.9 %shard_map.107 = f32[19,8,16,128]{3,2,1,0:T(8,128)} custom-call(f32[8]{0:T(128)} %fusion.73.strength_ref, f32[19,8,16,128]{3,2,1,0:T(8,128)} %get-tuple-element.135.inner_ref, f32[21,1,16,128]{3,2,1,0:T(8,128)} %copy-done.7, f32[21,1,16,128]{3,2,1,0:T(8,128)} %copy-done.8, f32[21,10,2,128]{3,2,1,0:T(2,128)} %copy-done.13, f32[8,10,18,128]{3,2,1,0:T(8,128)} %copy-done, ...), custom_call_target="tpu_custom_call" | custom-call | flops 6912000 | bytes 3735552 | tf_op jit(solution)/shard_map/pallas_call | solution.py:200
  (106 shorter events, 1.2 us)
Async XLA Ops:
  0.6 2.9 %copy-start.17 = (s32[8,16,128]{2,1,0:T(8,128)S(1)}, s32[8,16,128]{2,1,0:T(8,128)}, u32[]{:S(2)}) copy-start(s32[8,16,128]{2,1,0:T(8,128)} %param.34) | copy-start | bytes 196612
  2.6 4.1 %copy-start = (f32[8,10,18,128]{3,2,1,0:T(8,128)}, f32[8,10,18,128]{3,2,1,0:T(8,128)S(1)}, u32[]{:S(2)}) copy-start(f32[8,10,18,128]{3,2,1,0:T(8,128)S(1)} %and_convert_fusion.discs_ref) | copy-start | bytes 2211844
  3.5 9.3 %copy-start.1 = (f32[19,8,16,128]{3,2,1,0:T(8,128)S(1)}, f32[19,8,16,128]{3,2,1,0:T(8,128)}, u32[]{:S(2)}) copy-start(f32[19,8,16,128]{3,2,1,0:T(8,128)} %inner_ref.1) | copy-start | bytes 3735556
  4.2 8.7 %copy-start.4 = (f32[8,16,128]{2,1,0:T(8,128)S(1)}, f32[8,16,128]{2,1,0:T(8,128)}, u32[]{:S(2)}) copy-start(f32[8,16,128]{2,1,0:T(8,128)} %param.35) | copy-start | bytes 196612
  4.2 15.1 %copy-start.23 = (s32[16,3]{0,1:T(4,128)S(1)}, s32[16,3]{0,1:T(4,128)}, u32[]{:S(2)}) copy-start(s32[16,3]{0,1:T(4,128)} %param.39) | copy-start | bytes 580
  6.7 12.9 %copy-start.24 = (f32[16]{0:T(128)S(1)}, f32[16]{0:T(128)}, u32[]{:S(2)}) copy-start(f32[16]{0:T(128)} %param.40) | copy-start | bytes 196
  6.7 16.7 %copy-start.20 = (f32[8]{0:T(128)S(1)}, f32[8]{0:T(128)}, u32[]{:S(2)}) copy-start(f32[8]{0:T(128)} %get-tuple-element.130) | copy-start | bytes 100
  6.7 13.1 %collective-permute-start.2 = (f32[8]{0:T(128)}, f32[8]{0:T(128)S(1)}, u32[]{:S(2)}, u32[]{:S(2)}) collective-permute-start(f32[8]{0:T(128)} %get-tuple-element.130), channel_id=1, source_target_pairs={{0,4},{2,6},{4,8},{6,10},{8,12},{10,14},{12,16},{14,18},{16,20},{1... | collective-permute-start | bytes 104 | tf_op jit(solution)/shard_map/ppermute | solution.py:297
  9.7 10.1 %collective-permute-start.3 = (f32[8]{0:T(128)}, f32[8]{0:T(128)S(1)}, u32[]{:S(2)}, u32[]{:S(2)}) collective-permute-start(f32[8]{0:T(128)} %get-tuple-element.130), channel_id=1, source_target_pairs={{0,28},{2,30},{4,0},{6,2},{8,4},{10,6},{12,8},{14,10},{16,12},{18,... | collective-permute-start | bytes 104 | tf_op jit(solution)/shard_map/ppermute | solution.py:297
  13.6 9.8 %collective-permute-start = (f32[22,1,16,128]{3,2,1,0:T(8,128)S(1)}, f32[22,1,16,128]{3,2,1,0:T(8,128)S(1)}, u32[]{:S(2)}, u32[]{:S(2)}) collective-permute-start(f32[22,1,16,128]{3,2,1,0:T(8,128)S(1)} %get-tuple-element.188), channel_id=1, source_target_pairs={{0,2},{2,4},{4,6},{6,8},{8,10},{10,12},{12,14},{14,16},{16,18},{18... | collective-permute-start | bytes 540680 | tf_op jit(solution)/shard_map/ppermute | solution.py:293
  15.2 8.1 %collective-permute-start.1 = (f32[22,1,16,128]{3,2,1,0:T(8,128)S(1)}, f32[22,1,16,128]{3,2,1,0:T(8,128)S(1)}, u32[]{:S(2)}, u32[]{:S(2)}) collective-permute-start(f32[22,1,16,128]{3,2,1,0:T(8,128)S(1)} %get-tuple-element.189), channel_id=1, source_target_pairs={{2,0},{4,2},{6,4},{8,6},{10,8},{12,10},{14,12},{16,14},{18,16},{20... | collective-permute-start | bytes 540680 | tf_op jit(solution)/shard_map/ppermute | solution.py:294
  23.4 0.7 copy-start.5
  23.4 0.7 copy-start.6
  23.5 2.2 %copy-start.14 = (f32[3,8,16,128]{3,2,1,0:T(8,128)S(1)}, f32[3,8,16,128]{3,2,1,0:T(8,128)}, u32[]{:S(2)}) copy-start(f32[3,8,16,128]{3,2,1,0:T(8,128)} %get-tuple-element.133) | copy-start | bytes 589828
  24.1 2.4 %copy-start.18 = (f32[8]{0:T(128)S(1)}, f32[8]{0:T(128)}, u32[]{:S(2)}) copy-start(f32[8]{0:T(128)} %param.37) | copy-start | bytes 100
  24.1 2.4 %copy-start.19 = (f32[8]{0:T(128)S(1)}, f32[8]{0:T(128)}, u32[]{:S(2)}) copy-start(f32[8]{0:T(128)} %param.38) | copy-start | bytes 100
  24.1 1.5 %collective-permute-start.4 = (f32[22,10,2,128]{3,2,1,0:T(2,128)S(1)}, f32[22,10,2,128]{3,2,1,0:T(2,128)S(1)}, u32[]{:S(2)}, u32[]{:S(2)}) collective-permute-start(f32[22,10,2,128]{3,2,1,0:T(2,128)S(1)} %fusion.2), channel_id=1, source_target_pairs={{0,1},{1,0},{2,3},{3,2},{4,5},{5,4},{6,7},{7,6},{8,9},{9,8},{10,11... | collective-permute-start | bytes 675848 | tf_op jit(solution)/shard_map/ppermute | solution.py:288
  25.6 1.4 %copy-start.11 = (f32[22,10,2,128]{3,2,1,0:T(2,128)}, f32[22,10,2,128]{3,2,1,0:T(2,128)S(1)}, u32[]{:S(2)}) copy-start(f32[22,10,2,128]{3,2,1,0:T(2,128)S(1)} %collective-permute-done.4.rows_ref) | copy-start | bytes 675844
  32.2 7.5 %copy-start.22 = (f32[8]{0:T(128)S(1)}, f32[8]{0:T(128)}, u32[]{:S(2)}) copy-start(f32[8]{0:T(128)} %get-tuple-element.131) | copy-start | bytes 100
  32.2 13.9 %copy-start.2 = (f32[19,8,16,128]{3,2,1,0:T(8,128)S(1)}, f32[19,8,16,128]{3,2,1,0:T(8,128)}, u32[]{:S(2)}) copy-start(f32[19,8,16,128]{3,2,1,0:T(8,128)} %get-tuple-element.132.inner_ref) | copy-start | bytes 3735556
  34.0 11.9 %collective-permute-start.5 = (f32[21,1,16,128]{3,2,1,0:T(8,128)S(1)}, f32[21,1,16,128]{3,2,1,0:T(8,128)S(1)}, u32[]{:S(2)}, u32[]{:S(2)}) collective-permute-start(f32[21,1,16,128]{3,2,1,0:T(8,128)S(1)} %get-tuple-element.180), channel_id=1, source_target_pairs={{0,2},{2,4},{4,6},{6,8},{8,10},{10,12},{12,14},{14,16},{16,18},{18... | collective-permute-start | bytes 516104 | tf_op jit(solution)/shard_map/ppermute | solution.py:293
  35.7 10.2 %collective-permute-start.6 = (f32[21,1,16,128]{3,2,1,0:T(8,128)S(1)}, f32[21,1,16,128]{3,2,1,0:T(8,128)S(1)}, u32[]{:S(2)}, u32[]{:S(2)}) collective-permute-start(f32[21,1,16,128]{3,2,1,0:T(8,128)S(1)} %get-tuple-element.181), channel_id=1, source_target_pairs={{2,0},{4,2},{6,4},{8,6},{10,8},{12,10},{14,12},{16,14},{18,16},{20... | collective-permute-start | bytes 516104 | tf_op jit(solution)/shard_map/ppermute | solution.py:294
  39.7 6.2 %collective-permute-start.7 = (f32[8]{0:T(128)S(1)}, f32[8]{0:T(128)S(1)}, u32[]{:S(2)}, u32[]{:S(2)}) collective-permute-start(f32[8]{0:T(128)S(1)} %copy-done.22), channel_id=1, source_target_pairs={{0,4},{2,6},{4,8},{6,10},{8,12},{10,14},{12,16},{14,18},{16,20},{1... | collective-permute-start | bytes 104 | tf_op jit(solution)/shard_map/ppermute | solution.py:297
  39.7 6.2 %collective-permute-start.8 = (f32[8]{0:T(128)S(1)}, f32[8]{0:T(128)S(1)}, u32[]{:S(2)}, u32[]{:S(2)}) collective-permute-start(f32[8]{0:T(128)S(1)} %copy-done.22), channel_id=1, source_target_pairs={{0,28},{2,30},{4,0},{6,2},{8,4},{10,6},{12,8},{14,10},{16,12},{18,... | collective-permute-start | bytes 104 | tf_op jit(solution)/shard_map/ppermute | solution.py:297
  46.0 0.7 copy-start.9
  46.0 0.7 copy-start.10
  46.1 2.2 %copy-start.16 = (f32[3,8,16,128]{3,2,1,0:T(8,128)S(1)}, f32[3,8,16,128]{3,2,1,0:T(8,128)}, u32[]{:S(2)}) copy-start(f32[3,8,16,128]{3,2,1,0:T(8,128)} %get-tuple-element.136) | copy-start | bytes 589828
  46.7 1.5 %collective-permute-start.9 = (f32[21,10,2,128]{3,2,1,0:T(2,128)S(1)}, f32[21,10,2,128]{3,2,1,0:T(2,128)S(1)}, u32[]{:S(2)}, u32[]{:S(2)}) collective-permute-start(f32[21,10,2,128]{3,2,1,0:T(2,128)S(1)} %fusion.14), channel_id=1, source_target_pairs={{0,1},{1,0},{2,3},{3,2},{4,5},{5,4},{6,7},{7,6},{8,9},{9,8},{10,11... | collective-permute-start | bytes 645128 | tf_op jit(solution)/shard_map/ppermute | solution.py:288
  48.2 0.7 copy-start.12
  54.2 7.5 %copy-start.21 = (f32[8]{0:T(128)S(1)}, f32[8]{0:T(128)}, u32[]{:S(2)}) copy-start(f32[8]{0:T(128)} %get-tuple-element.134) | copy-start | bytes 100
  54.2 13.8 %copy-start.3 = (f32[19,8,16,128]{3,2,1,0:T(8,128)S(1)}, f32[19,8,16,128]{3,2,1,0:T(8,128)}, u32[]{:S(2)}) copy-start(f32[19,8,16,128]{3,2,1,0:T(8,128)} %get-tuple-element.135.inner_ref) | copy-start | bytes 3735556
  56.0 11.9 %collective-permute-start.10 = (f32[21,1,16,128]{3,2,1,0:T(8,128)S(1)}, f32[21,1,16,128]{3,2,1,0:T(8,128)S(1)}, u32[]{:S(2)}, u32[]{:S(2)}) collective-permute-start(f32[21,1,16,128]{3,2,1,0:T(8,128)S(1)} %get-tuple-element.178), channel_id=1, source_target_pairs={{0,2},{2,4},{4,6},{6,8},{8,10},{10,12},{12,14},{14,16},{16,18},{18... | collective-permute-start | bytes 516104 | tf_op jit(solution)/shard_map/ppermute | solution.py:293
  56.0 11.9 %collective-permute-start.11 = (f32[21,1,16,128]{3,2,1,0:T(8,128)S(1)}, f32[21,1,16,128]{3,2,1,0:T(8,128)S(1)}, u32[]{:S(2)}, u32[]{:S(2)}) collective-permute-start(f32[21,1,16,128]{3,2,1,0:T(8,128)S(1)} %get-tuple-element.179), channel_id=1, source_target_pairs={{2,0},{4,2},{6,4},{8,6},{10,8},{12,10},{14,12},{16,14},{18,16},{20... | collective-permute-start | bytes 516104 | tf_op jit(solution)/shard_map/ppermute | solution.py:294
  61.6 6.2 %collective-permute-start.12 = (f32[8]{0:T(128)S(1)}, f32[8]{0:T(128)S(1)}, u32[]{:S(2)}, u32[]{:S(2)}) collective-permute-start(f32[8]{0:T(128)S(1)} %copy-done.21), channel_id=1, source_target_pairs={{0,4},{2,6},{4,8},{6,10},{8,12},{10,14},{12,16},{14,18},{16,20},{1... | collective-permute-start | bytes 104 | tf_op jit(solution)/shard_map/ppermute | solution.py:297
  61.6 6.2 %collective-permute-start.13 = (f32[8]{0:T(128)S(1)}, f32[8]{0:T(128)S(1)}, u32[]{:S(2)}, u32[]{:S(2)}) collective-permute-start(f32[8]{0:T(128)S(1)} %copy-done.21), channel_id=1, source_target_pairs={{0,28},{2,30},{4,0},{6,2},{8,4},{10,6},{12,8},{14,10},{16,12},{18,... | collective-permute-start | bytes 104 | tf_op jit(solution)/shard_map/ppermute | solution.py:297
  67.9 0.7 copy-start.7
  67.9 0.7 copy-start.8
  68.0 2.2 %copy-start.15 = (f32[3,8,16,128]{3,2,1,0:T(8,128)S(1)}, f32[3,8,16,128]{3,2,1,0:T(8,128)}, u32[]{:S(2)}) copy-start(f32[3,8,16,128]{3,2,1,0:T(8,128)} %get-tuple-element.137) | copy-start | bytes 589828
  68.6 1.5 %collective-permute-start.14 = (f32[21,10,2,128]{3,2,1,0:T(2,128)S(1)}, f32[21,10,2,128]{3,2,1,0:T(2,128)S(1)}, u32[]{:S(2)}, u32[]{:S(2)}) collective-permute-start(f32[21,10,2,128]{3,2,1,0:T(2,128)S(1)} %fusion.9), channel_id=1, source_target_pairs={{0,1},{1,0},{2,3},{3,2},{4,5},{5,4},{6,7},{7,6},{8,9},{9,8},{10,11... | collective-permute-start | bytes 645128 | tf_op jit(solution)/shard_map/ppermute | solution.py:288
  70.1 1.3 %copy-start.13 = (f32[21,10,2,128]{3,2,1,0:T(2,128)}, f32[21,10,2,128]{3,2,1,0:T(2,128)S(1)}, u32[]{:S(2)}) copy-start(f32[21,10,2,128]{3,2,1,0:T(2,128)S(1)} %collective-permute-done.14.rows_ref) | copy-start | bytes 645124

commit v21 on v20

--- a/solution.py
+++ b/solution.py
@@ -152,7 +152,7 @@
         density, velocity = plane_moments([populations_ref[which, index] for which in range(19)])
         for dimension in range(3):
             velocity_ref[dimension, index] = velocity[dimension]
-        solid_flag = solid_ref[index + rim, 0:band_width, :] != 0.0
+        solid_flag = solid_ref[index + rim, 0:band_width, :] != 0
         for fan_number in range(fans):
             sums_ref[fan_number] += jnp.where(
                 solid_flag, 0.0, discs_ref[fan_number, index + rim, 0:band_width, :] * velocity[0]
@@ -372,7 +372,7 @@
     band_reach = max(-(-(2 * RAD + 1) // band_width), (band_width + 2 * RAD) // band_width)
     discs = (along_in[:, :, None, None] & across_in[:, None]).astype(jnp.float32)
     solid_planes = solid_flag.astype(jnp.float32)
-    velocity, flow = first_moments(populations, discs[:, 1:-1, 0:band_width], solid_planes)
+    velocity, flow = first_moments(populations, discs[:, 1:-1, 0:band_width], solid_mask)
     partials = flow
     for repeat in range(ITERS):
         fields = [populations, smoke_field[None]]

time: 76.6 us -> 76 us (level)
  no operation moved by 1% of the time
where the time goes in v21:
time: 76 us; the launch traced here: 75.6 us
  starting transfers between devices  32.6 us (43%)
  Pallas kernels  17.9 us (24%)
  waiting for transfers between devices  10.8 us (14%)
  local copies, waits for them, and re-layouts  7.01 us (9%)
  other arithmetic  5.91 us (8%)
  between operations  1.2 us (2%)
    ppermute x6, starting transfers between devices, rim_round(): lax.ppermute(flow, axis, [(i, (i + offset) % count) for i in range(count)])  15.6 us
    pallas_call x3, Pallas kernels, lattice_step(): pl.pallas_call(functools.partial(step_kernel, with_moments), out_shape=tu...  15.4 us
    ppermute x3, starting transfers between devices, rim_round(): from_right = lax.ppermute(head, axis, backward)  13.6 us
    ppermute x3, waiting for transfers between devices, rim_round(): both = lax.ppermute(jnp.concatenate([tail, head], axis=dim), axis, forward)  4.17 us
    ppermute x3, waiting for transfers between devices, rim_round(): from_left = lax.ppermute(tail, axis, forward)  3.58 us
    ppermute x3, starting transfers between devices, rim_round(): from_left = lax.ppermute(tail, axis, forward)  3.39 us
    ppermute x6, waiting for transfers between devices, rim_round(): lax.ppermute(flow, axis, [(i, (i + offset) % count) for i in range(count)])  3.04 us
    pallas_call x1, Pallas kernels, first_moments(): pl.pallas_call(lambda populations_ref, discs_ref, solid_ref, velocity_ref...  2.55 us
  transfers between devices with their start and end apart: 15, of which 6 were waited for; matrix products, arithmetic and copies ran while one was open for 2% of the time, Pallas kernels for 0%

profile of v21, /device:TPU:0, one launch (start us, length us, event | category | flops | bytes accessed | tf_op | source)
XLA Modules:
  0.0 75.6 jit_solution(5531176947866087829)
XLA Ops:
  0.6 0.8 %slice_bitcast_fusion.12 = (s32[8]{0:T(128)S(1)}, s32[8]{0:T(128)S(1)}, s32[8]{0:T(128)S(1)}) fusion(s32[8,3]{0,1:T(4,128)} %param.36), kind=kLoop, calls=%fused_computation.161 | loop fusion | bytes 192 | tf_op jit(solution)/shard_map/slice | solution.py:361
  1.5 0.7 and_select_fusion
  2.2 0.1 add_compare_fusion
  2.4 0.1 fusion.42
  2.4 0.2 and_convert_fusion.discs_ref
  2.6 0.8 %slice.615.discs_ref = f32[8,8,16,128]{3,2,1,0:T(8,128)} slice(f32[8,10,18,128]{3,2,1,0:T(8,128)S(1)} %and_convert_fusion.discs_ref), slice={[0:8], [1:9], [0:16], [0:128]} | slice | bytes 1048576 | tf_op jit(solution)/shard_map/slice | solution.py:375
  3.5 2.5 %shard_map.104 = (f32[3,8,16,128]{3,2,1,0:T(8,128)}, f32[8]{0:T(128)}) custom-call(f32[19,8,16,128]{3,2,1,0:T(8,128)} %inner_ref.1, f32[8,8,16,128]{3,2,1,0:T(8,128)} %slice.615.discs_ref, s32[8,16,128]{2,1,0:T(8,128)} %solid_ref.1), custom_call_target="tpu_custom_call" | custom-call | flops 983040 | bytes 1245184 | tf_op jit(solution)/shard_map/pallas_call | solution.py:170
  6.1 3.0 %collective-permute-start.2 = (f32[8]{0:T(128)}, f32[8]{0:T(128)S(1)}, u32[]{:S(2)}, u32[]{:S(2)}) collective-permute-start(f32[8]{0:T(128)} %get-tuple-element.130), channel_id=1, source_target_pairs={{0,4},{2,6},{4,8},{6,10},{8,12},{10,14},{12,16},{14,18},{16,20},{1... | collective-permute-start | bytes 104 | tf_op jit(solution)/shard_map/ppermute | solution.py:297
  9.1 3.1 %collective-permute-start.3 = (f32[8]{0:T(128)}, f32[8]{0:T(128)S(1)}, u32[]{:S(2)}, u32[]{:S(2)}) collective-permute-start(f32[8]{0:T(128)} %get-tuple-element.130), channel_id=1, source_target_pairs={{0,28},{2,30},{4,0},{6,2},{8,4},{10,6},{12,8},{14,10},{16,12},{18,... | collective-permute-start | bytes 104 | tf_op jit(solution)/shard_map/ppermute | solution.py:297
  12.3 0.7 fusion.17
  13.0 1.6 %collective-permute-start = (f32[22,1,16,128]{3,2,1,0:T(8,128)S(1)}, f32[22,1,16,128]{3,2,1,0:T(8,128)S(1)}, u32[]{:S(2)}, u32[]{:S(2)}) collective-permute-start(f32[22,1,16,128]{3,2,1,0:T(8,128)S(1)} %get-tuple-element.188), channel_id=1, source_target_pairs={{0,2},{2,4},{4,6},{6,8},{8,10},{10,12},{12,14},{14,16},{16,18},{18... | collective-permute-start | bytes 540680 | tf_op jit(solution)/shard_map/ppermute | solution.py:293
  14.6 4.0 %collective-permute-start.1 = (f32[22,1,16,128]{3,2,1,0:T(8,128)S(1)}, f32[22,1,16,128]{3,2,1,0:T(8,128)S(1)}, u32[]{:S(2)}, u32[]{:S(2)}) collective-permute-start(f32[22,1,16,128]{3,2,1,0:T(8,128)S(1)} %get-tuple-element.189), channel_id=1, source_target_pairs={{2,0},{4,2},{6,4},{8,6},{10,8},{12,10},{14,12},{16,14},{18,16},{20... | collective-permute-start | bytes 540680 | tf_op jit(solution)/shard_map/ppermute | solution.py:294
  18.8 0.1 broadcast_multiply_fusion
  18.9 0.2 fusion.19
  19.1 3.6 %collective-permute-done.low_ref = f32[22,1,16,128]{3,2,1,0:T(8,128)S(1)} collective-permute-done((f32[22,1,16,128]{3,2,1,0:T(8,128)S(1)}, f32[22,1,16,128]{3,2,1,0:T(8,128)S(1)}, u32[]{:S(2)}, u32[]{:S(2)}) %collective-permute-start) | collective-permute-done | bytes 180256 | tf_op jit(solution)/shard_map/ppermute | solution.py:293
  22.8 0.2 fusion.2
  23.0 0.4 copy-done.5
  23.4 0.1 copy-done.6
  23.5 0.1 fusion.91
  23.5 1.4 %collective-permute-done.4.rows_ref = f32[22,10,2,128]{3,2,1,0:T(2,128)S(1)} collective-permute-done((f32[22,10,2,128]{3,2,1,0:T(2,128)S(1)}, f32[22,10,2,128]{3,2,1,0:T(2,128)S(1)}, u32[]{:S(2)}, u32[]{:S(2)}) %collective-permute-start.4) | collective-permute-done | bytes 225312 | tf_op jit(solution)/shard_map/ppermute | solution.py:288
  25.0 0.1 fusion.38
  25.2 0.7 maximum_bitcast_fusion.solid_ref
  25.8 0.5 fusion.71.strength_ref
  26.3 5.2 %shard_map.105 = (f32[19,8,16,128]{3,2,1,0:T(8,128)}, f32[3,8,16,128]{3,2,1,0:T(8,128)}, f32[8]{0:T(128)}) custom-call(f32[8]{0:T(128)} %fusion.71.strength_ref, f32[19,8,16,128]{3,2,1,0:T(8,128)} %inner_ref.1, f32[22,1,16,128]{3,2,1,0:T(8,128)} %copy-done.5, f32[22,1,16,128]{3,2,1,0:T(8,128)} %copy-done.6, f32[22,10,2,128]{3,2,1,0:T(2,128)} %copy-done.11, ...), custom_call_target="tpu_custom_call" | custom-call | flops 6912000 | bytes 3735552 | tf_op jit(solution)/shard_map/pallas_call | solution.py:200
  31.6 1.1 %fusion.76 = (f32[19,1,16,128]{3,2,1,0:T(8,128)S(1)}, f32[19,1,16,128]{3,2,1,0:T(8,128)S(1)}) fusion(f32[19,8,16,128]{3,2,1,0:T(8,128)} %get-tuple-element.132.inner_ref), kind=kLoop, calls=%fused_computation.168 | loop fusion | bytes 622592 | tf_op jit(solution)/shard_map/slice | solution.py:278
  32.7 0.7 pad_bitcast_fusion.1
  33.4 1.7 %collective-permute-start.5 = (f32[21,1,16,128]{3,2,1,0:T(8,128)S(1)}, f32[21,1,16,128]{3,2,1,0:T(8,128)S(1)}, u32[]{:S(2)}, u32[]{:S(2)}) collective-permute-start(f32[21,1,16,128]{3,2,1,0:T(8,128)S(1)} %get-tuple-element.180), channel_id=1, source_target_pairs={{0,2},{2,4},{4,6},{6,8},{8,10},{10,12},{12,14},{14,16},{16,18},{18... | collective-permute-start | bytes 516104 | tf_op jit(solution)/shard_map/ppermute | solution.py:293
  35.1 4.0 %collective-permute-start.6 = (f32[21,1,16,128]{3,2,1,0:T(8,128)S(1)}, f32[21,1,16,128]{3,2,1,0:T(8,128)S(1)}, u32[]{:S(2)}, u32[]{:S(2)}) collective-permute-start(f32[21,1,16,128]{3,2,1,0:T(8,128)S(1)} %get-tuple-element.181), channel_id=1, source_target_pairs={{2,0},{4,2},{6,4},{8,6},{10,8},{12,10},{14,12},{16,14},{18,16},{20... | collective-permute-start | bytes 516104 | tf_op jit(solution)/shard_map/ppermute | solution.py:294
  39.1 4.7 %collective-permute-start.8 = (f32[8]{0:T(128)S(1)}, f32[8]{0:T(128)S(1)}, u32[]{:S(2)}, u32[]{:S(2)}) collective-permute-start(f32[8]{0:T(128)S(1)} %copy-done.22), channel_id=1, source_target_pairs={{0,28},{2,30},{4,0},{6,2},{8,4},{10,6},{12,8},{14,10},{16,12},{18,... | collective-permute-start | bytes 104 | tf_op jit(solution)/shard_map/ppermute | solution.py:297
  43.8 1.5 %collective-permute-done.7 = f32[8]{0:T(128)S(1)} collective-permute-done((f32[8]{0:T(128)S(1)}, f32[8]{0:T(128)S(1)}, u32[]{:S(2)}, u32[]{:S(2)}) %collective-permute-start.7) | collective-permute-done | bytes 64 | tf_op jit(solution)/shard_map/ppermute | solution.py:297
  45.5 0.2 fusion.14
  45.6 0.4 copy-done.9
  46.2 1.4 %collective-permute-done.9.rows_ref = f32[21,10,2,128]{3,2,1,0:T(2,128)S(1)} collective-permute-done((f32[21,10,2,128]{3,2,1,0:T(2,128)S(1)}, f32[21,10,2,128]{3,2,1,0:T(2,128)S(1)}, u32[]{:S(2)}, u32[]{:S(2)}) %collective-permute-start.9) | collective-permute-done | bytes 215072 | tf_op jit(solution)/shard_map/ppermute | solution.py:288
  47.6 0.1 fusion.32
  47.7 0.5 fusion.72.strength_ref
  48.3 5.3 %shard_map.106 = (f32[19,8,16,128]{3,2,1,0:T(8,128)}, f32[3,8,16,128]{3,2,1,0:T(8,128)}, f32[8]{0:T(128)}) custom-call(f32[8]{0:T(128)} %fusion.72.strength_ref, f32[19,8,16,128]{3,2,1,0:T(8,128)} %get-tuple-element.132.inner_ref, f32[21,1,16,128]{3,2,1,0:T(8,128)} %copy-done.9, f32[21,1,16,128]{3,2,1,0:T(8,128)} %copy-done.10, ...), custom_call_target="tpu_custom_call" | custom-call | flops 6912000 | bytes 3735552 | tf_op jit(solution)/shard_map/pallas_call | solution.py:200
  53.6 1.1 %fusion.75 = (f32[19,1,16,128]{3,2,1,0:T(8,128)S(1)}, f32[19,1,16,128]{3,2,1,0:T(8,128)S(1)}) fusion(f32[19,8,16,128]{3,2,1,0:T(8,128)} %get-tuple-element.135.inner_ref), kind=kLoop, calls=%fused_computation.167 | loop fusion | bytes 622592 | tf_op jit(solution)/shard_map/slice | solution.py:278
  54.7 0.6 pad_bitcast_fusion
  55.4 5.6 %collective-permute-start.11 = (f32[21,1,16,128]{3,2,1,0:T(8,128)S(1)}, f32[21,1,16,128]{3,2,1,0:T(8,128)S(1)}, u32[]{:S(2)}, u32[]{:S(2)}) collective-permute-start(f32[21,1,16,128]{3,2,1,0:T(8,128)S(1)} %get-tuple-element.179), channel_id=1, source_target_pairs={{2,0},{4,2},{6,4},{8,6},{10,8},{12,10},{14,12},{16,14},{18,16},{20... | collective-permute-start | bytes 516104 | tf_op jit(solution)/shard_map/ppermute | solution.py:294
  61.0 4.7 %collective-permute-start.13 = (f32[8]{0:T(128)S(1)}, f32[8]{0:T(128)S(1)}, u32[]{:S(2)}, u32[]{:S(2)}) collective-permute-start(f32[8]{0:T(128)S(1)} %copy-done.21), channel_id=1, source_target_pairs={{0,28},{2,30},{4,0},{6,2},{8,4},{10,6},{12,8},{14,10},{16,12},{18,... | collective-permute-start | bytes 104 | tf_op jit(solution)/shard_map/ppermute | solution.py:297
  65.7 1.5 %collective-permute-done.12 = f32[8]{0:T(128)S(1)} collective-permute-done((f32[8]{0:T(128)S(1)}, f32[8]{0:T(128)S(1)}, u32[]{:S(2)}, u32[]{:S(2)}) %collective-permute-start.12) | collective-permute-done | bytes 64 | tf_op jit(solution)/shard_map/ppermute | solution.py:297
  67.4 0.2 fusion.9
  67.5 0.4 copy-done.7
  68.0 0.1 fusion.87
  68.1 1.4 %collective-permute-done.14.rows_ref = f32[21,10,2,128]{3,2,1,0:T(2,128)S(1)} collective-permute-done((f32[21,10,2,128]{3,2,1,0:T(2,128)S(1)}, f32[21,10,2,128]{3,2,1,0:T(2,128)S(1)}, u32[]{:S(2)}, u32[]{:S(2)}) %collective-permute-start.14) | collective-permute-done | bytes 215072 | tf_op jit(solution)/shard_map/ppermute | solution.py:288
  69.5 0.7 fusion.26
  70.3 0.5 fusion.73.strength_ref
  70.8 4.9 %shard_map.107 = f32[19,8,16,128]{3,2,1,0:T(8,128)} custom-call(f32[8]{0:T(128)} %fusion.73.strength_ref, f32[19,8,16,128]{3,2,1,0:T(8,128)} %get-tuple-element.135.inner_ref, f32[21,1,16,128]{3,2,1,0:T(8,128)} %copy-done.7, f32[21,1,16,128]{3,2,1,0:T(8,128)} %copy-done.8, f32[21,10,2,128]{3,2,1,0:T(2,128)} %copy-done.14, f32[8,10,18,128]{3,2,1,0:T(8,128)} %copy-done, ...), custom_call_target="tpu_custom_call" | custom-call | flops 6912000 | bytes 3735552 | tf_op jit(solution)/shard_map/pallas_call | solution.py:200
  (105 shorter events, 1.1 us)
Async XLA Ops:
  2.6 3.4 %copy-start = (f32[8,10,18,128]{3,2,1,0:T(8,128)}, f32[8,10,18,128]{3,2,1,0:T(8,128)S(1)}, u32[]{:S(2)}) copy-start(f32[8,10,18,128]{3,2,1,0:T(8,128)S(1)} %and_convert_fusion.discs_ref) | copy-start | bytes 2211844
  2.6 9.6 %copy-start.12 = (s32[8,16,128]{2,1,0:T(8,128)S(1)}, s32[8,16,128]{2,1,0:T(8,128)}, u32[]{:S(2)}) copy-start(s32[8,16,128]{2,1,0:T(8,128)} %solid_ref.1) | copy-start | bytes 196612
  3.5 8.7 %copy-start.1 = (f32[19,8,16,128]{3,2,1,0:T(8,128)S(1)}, f32[19,8,16,128]{3,2,1,0:T(8,128)}, u32[]{:S(2)}) copy-start(f32[19,8,16,128]{3,2,1,0:T(8,128)} %inner_ref.1) | copy-start | bytes 3735556
  3.5 8.8 %copy-start.4 = (f32[8,16,128]{2,1,0:T(8,128)S(1)}, f32[8,16,128]{2,1,0:T(8,128)}, u32[]{:S(2)}) copy-start(f32[8,16,128]{2,1,0:T(8,128)} %param.35) | copy-start | bytes 196612
  3.5 15.2 %copy-start.23 = (s32[16,3]{0,1:T(4,128)S(1)}, s32[16,3]{0,1:T(4,128)}, u32[]{:S(2)}) copy-start(s32[16,3]{0,1:T(4,128)} %param.39) | copy-start | bytes 580
  6.0 12.9 %copy-start.24 = (f32[16]{0:T(128)S(1)}, f32[16]{0:T(128)}, u32[]{:S(2)}) copy-start(f32[16]{0:T(128)} %param.40) | copy-start | bytes 196
  6.0 16.7 %copy-start.20 = (f32[8]{0:T(128)S(1)}, f32[8]{0:T(128)}, u32[]{:S(2)}) copy-start(f32[8]{0:T(128)} %get-tuple-element.130) | copy-start | bytes 100
  6.1 13.1 %collective-permute-start.2 = (f32[8]{0:T(128)}, f32[8]{0:T(128)S(1)}, u32[]{:S(2)}, u32[]{:S(2)}) collective-permute-start(f32[8]{0:T(128)} %get-tuple-element.130), channel_id=1, source_target_pairs={{0,4},{2,6},{4,8},{6,10},{8,12},{10,14},{12,16},{14,18},{16,20},{1... | collective-permute-start | bytes 104 | tf_op jit(solution)/shard_map/ppermute | solution.py:297
  9.1 10.1 %collective-permute-start.3 = (f32[8]{0:T(128)}, f32[8]{0:T(128)S(1)}, u32[]{:S(2)}, u32[]{:S(2)}) collective-permute-start(f32[8]{0:T(128)} %get-tuple-element.130), channel_id=1, source_target_pairs={{0,28},{2,30},{4,0},{6,2},{8,4},{10,6},{12,8},{14,10},{16,12},{18,... | collective-permute-start | bytes 104 | tf_op jit(solution)/shard_map/ppermute | solution.py:297
  13.0 9.8 %collective-permute-start = (f32[22,1,16,128]{3,2,1,0:T(8,128)S(1)}, f32[22,1,16,128]{3,2,1,0:T(8,128)S(1)}, u32[]{:S(2)}, u32[]{:S(2)}) collective-permute-start(f32[22,1,16,128]{3,2,1,0:T(8,128)S(1)} %get-tuple-element.188), channel_id=1, source_target_pairs={{0,2},{2,4},{4,6},{6,8},{8,10},{10,12},{12,14},{14,16},{16,18},{18... | collective-permute-start | bytes 540680 | tf_op jit(solution)/shard_map/ppermute | solution.py:293
  14.6 8.1 %collective-permute-start.1 = (f32[22,1,16,128]{3,2,1,0:T(8,128)S(1)}, f32[22,1,16,128]{3,2,1,0:T(8,128)S(1)}, u32[]{:S(2)}, u32[]{:S(2)}) collective-permute-start(f32[22,1,16,128]{3,2,1,0:T(8,128)S(1)} %get-tuple-element.189), channel_id=1, source_target_pairs={{2,0},{4,2},{6,4},{8,6},{10,8},{12,10},{14,12},{16,14},{18,16},{20... | collective-permute-start | bytes 540680 | tf_op jit(solution)/shard_map/ppermute | solution.py:294
  22.7 0.7 copy-start.5
  22.7 0.7 copy-start.6
  22.8 2.2 %copy-start.15 = (f32[3,8,16,128]{3,2,1,0:T(8,128)S(1)}, f32[3,8,16,128]{3,2,1,0:T(8,128)}, u32[]{:S(2)}) copy-start(f32[3,8,16,128]{3,2,1,0:T(8,128)} %get-tuple-element.133) | copy-start | bytes 589828
  23.5 2.4 %copy-start.18 = (f32[8]{0:T(128)S(1)}, f32[8]{0:T(128)}, u32[]{:S(2)}) copy-start(f32[8]{0:T(128)} %param.37) | copy-start | bytes 100
  23.5 2.4 %copy-start.19 = (f32[8]{0:T(128)S(1)}, f32[8]{0:T(128)}, u32[]{:S(2)}) copy-start(f32[8]{0:T(128)} %param.38) | copy-start | bytes 100
  23.5 1.5 %collective-permute-start.4 = (f32[22,10,2,128]{3,2,1,0:T(2,128)S(1)}, f32[22,10,2,128]{3,2,1,0:T(2,128)S(1)}, u32[]{:S(2)}, u32[]{:S(2)}) collective-permute-start(f32[22,10,2,128]{3,2,1,0:T(2,128)S(1)} %fusion.2), channel_id=1, source_target_pairs={{0,1},{1,0},{2,3},{3,2},{4,5},{5,4},{6,7},{7,6},{8,9},{9,8},{10,11... | collective-permute-start | bytes 675848 | tf_op jit(solution)/shard_map/ppermute | solution.py:288
  25.0 1.4 %copy-start.11 = (f32[22,10,2,128]{3,2,1,0:T(2,128)}, f32[22,10,2,128]{3,2,1,0:T(2,128)S(1)}, u32[]{:S(2)}) copy-start(f32[22,10,2,128]{3,2,1,0:T(2,128)S(1)} %collective-permute-done.4.rows_ref) | copy-start | bytes 675844
  31.6 7.5 %copy-start.22 = (f32[8]{0:T(128)S(1)}, f32[8]{0:T(128)}, u32[]{:S(2)}) copy-start(f32[8]{0:T(128)} %get-tuple-element.131) | copy-start | bytes 100
  31.6 13.9 %copy-start.2 = (f32[19,8,16,128]{3,2,1,0:T(8,128)S(1)}, f32[19,8,16,128]{3,2,1,0:T(8,128)}, u32[]{:S(2)}) copy-start(f32[19,8,16,128]{3,2,1,0:T(8,128)} %get-tuple-element.132.inner_ref) | copy-start | bytes 3735556
  33.4 11.9 %collective-permute-start.5 = (f32[21,1,16,128]{3,2,1,0:T(8,128)S(1)}, f32[21,1,16,128]{3,2,1,0:T(8,128)S(1)}, u32[]{:S(2)}, u32[]{:S(2)}) collective-permute-start(f32[21,1,16,128]{3,2,1,0:T(8,128)S(1)} %get-tuple-element.180), channel_id=1, source_target_pairs={{0,2},{2,4},{4,6},{6,8},{8,10},{10,12},{12,14},{14,16},{16,18},{18... | collective-permute-start | bytes 516104 | tf_op jit(solution)/shard_map/ppermute | solution.py:293
  35.1 10.2 %collective-permute-start.6 = (f32[21,1,16,128]{3,2,1,0:T(8,128)S(1)}, f32[21,1,16,128]{3,2,1,0:T(8,128)S(1)}, u32[]{:S(2)}, u32[]{:S(2)}) collective-permute-start(f32[21,1,16,128]{3,2,1,0:T(8,128)S(1)} %get-tuple-element.181), channel_id=1, source_target_pairs={{2,0},{4,2},{6,4},{8,6},{10,8},{12,10},{14,12},{16,14},{18,16},{20... | collective-permute-start | bytes 516104 | tf_op jit(solution)/shard_map/ppermute | solution.py:294
  39.1 6.2 %collective-permute-start.7 = (f32[8]{0:T(128)S(1)}, f32[8]{0:T(128)S(1)}, u32[]{:S(2)}, u32[]{:S(2)}) collective-permute-start(f32[8]{0:T(128)S(1)} %copy-done.22), channel_id=1, source_target_pairs={{0,4},{2,6},{4,8},{6,10},{8,12},{10,14},{12,16},{14,18},{16,20},{1... | collective-permute-start | bytes 104 | tf_op jit(solution)/shard_map/ppermute | solution.py:297
  39.1 6.2 %collective-permute-start.8 = (f32[8]{0:T(128)S(1)}, f32[8]{0:T(128)S(1)}, u32[]{:S(2)}, u32[]{:S(2)}) collective-permute-start(f32[8]{0:T(128)S(1)} %copy-done.22), channel_id=1, source_target_pairs={{0,28},{2,30},{4,0},{6,2},{8,4},{10,6},{12,8},{14,10},{16,12},{18,... | collective-permute-start | bytes 104 | tf_op jit(solution)/shard_map/ppermute | solution.py:297
  45.3 0.7 copy-start.9
  45.3 0.7 copy-start.10
  45.5 2.2 %copy-start.17 = (f32[3,8,16,128]{3,2,1,0:T(8,128)S(1)}, f32[3,8,16,128]{3,2,1,0:T(8,128)}, u32[]{:S(2)}) copy-start(f32[3,8,16,128]{3,2,1,0:T(8,128)} %get-tuple-element.136) | copy-start | bytes 589828
  46.1 1.5 %collective-permute-start.9 = (f32[21,10,2,128]{3,2,1,0:T(2,128)S(1)}, f32[21,10,2,128]{3,2,1,0:T(2,128)S(1)}, u32[]{:S(2)}, u32[]{:S(2)}) collective-permute-start(f32[21,10,2,128]{3,2,1,0:T(2,128)S(1)} %fusion.14), channel_id=1, source_target_pairs={{0,1},{1,0},{2,3},{3,2},{4,5},{5,4},{6,7},{7,6},{8,9},{9,8},{10,11... | collective-permute-start | bytes 645128 | tf_op jit(solution)/shard_map/ppermute | solution.py:288
  47.5 0.7 copy-start.13
  53.5 7.5 %copy-start.21 = (f32[8]{0:T(128)S(1)}, f32[8]{0:T(128)}, u32[]{:S(2)}) copy-start(f32[8]{0:T(128)} %get-tuple-element.134) | copy-start | bytes 100
  53.6 13.8 %copy-start.3 = (f32[19,8,16,128]{3,2,1,0:T(8,128)S(1)}, f32[19,8,16,128]{3,2,1,0:T(8,128)}, u32[]{:S(2)}) copy-start(f32[19,8,16,128]{3,2,1,0:T(8,128)} %get-tuple-element.135.inner_ref) | copy-start | bytes 3735556
  55.3 11.9 %collective-permute-start.10 = (f32[21,1,16,128]{3,2,1,0:T(8,128)S(1)}, f32[21,1,16,128]{3,2,1,0:T(8,128)S(1)}, u32[]{:S(2)}, u32[]{:S(2)}) collective-permute-start(f32[21,1,16,128]{3,2,1,0:T(8,128)S(1)} %get-tuple-element.178), channel_id=1, source_target_pairs={{0,2},{2,4},{4,6},{6,8},{8,10},{10,12},{12,14},{14,16},{16,18},{18... | collective-permute-start | bytes 516104 | tf_op jit(solution)/shard_map/ppermute | solution.py:293
  55.4 11.9 %collective-permute-start.11 = (f32[21,1,16,128]{3,2,1,0:T(8,128)S(1)}, f32[21,1,16,128]{3,2,1,0:T(8,128)S(1)}, u32[]{:S(2)}, u32[]{:S(2)}) collective-permute-start(f32[21,1,16,128]{3,2,1,0:T(8,128)S(1)} %get-tuple-element.179), channel_id=1, source_target_pairs={{2,0},{4,2},{6,4},{8,6},{10,8},{12,10},{14,12},{16,14},{18,16},{20... | collective-permute-start | bytes 516104 | tf_op jit(solution)/shard_map/ppermute | solution.py:294
  61.0 6.2 %collective-permute-start.12 = (f32[8]{0:T(128)S(1)}, f32[8]{0:T(128)S(1)}, u32[]{:S(2)}, u32[]{:S(2)}) collective-permute-start(f32[8]{0:T(128)S(1)} %copy-done.21), channel_id=1, source_target_pairs={{0,4},{2,6},{4,8},{6,10},{8,12},{10,14},{12,16},{14,18},{16,20},{1... | collective-permute-start | bytes 104 | tf_op jit(solution)/shard_map/ppermute | solution.py:297
  61.0 6.2 %collective-permute-start.13 = (f32[8]{0:T(128)S(1)}, f32[8]{0:T(128)S(1)}, u32[]{:S(2)}, u32[]{:S(2)}) collective-permute-start(f32[8]{0:T(128)S(1)} %copy-done.21), channel_id=1, source_target_pairs={{0,28},{2,30},{4,0},{6,2},{8,4},{10,6},{12,8},{14,10},{16,12},{18,... | collective-permute-start | bytes 104 | tf_op jit(solution)/shard_map/ppermute | solution.py:297
  67.2 0.7 copy-start.7
  67.3 0.7 copy-start.8
  67.4 2.2 %copy-start.16 = (f32[3,8,16,128]{3,2,1,0:T(8,128)S(1)}, f32[3,8,16,128]{3,2,1,0:T(8,128)}, u32[]{:S(2)}) copy-start(f32[3,8,16,128]{3,2,1,0:T(8,128)} %get-tuple-element.137) | copy-start | bytes 589828
  68.0 1.5 %collective-permute-start.14 = (f32[21,10,2,128]{3,2,1,0:T(2,128)S(1)}, f32[21,10,2,128]{3,2,1,0:T(2,128)S(1)}, u32[]{:S(2)}, u32[]{:S(2)}) collective-permute-start(f32[21,10,2,128]{3,2,1,0:T(2,128)S(1)} %fusion.9), channel_id=1, source_target_pairs={{0,1},{1,0},{2,3},{3,2},{4,5},{5,4},{6,7},{7,6},{8,9},{9,8},{10,11... | collective-permute-start | bytes 645128 | tf_op jit(solution)/shard_map/ppermute | solution.py:288
  69.5 1.3 %copy-start.14 = (f32[21,10,2,128]{3,2,1,0:T(2,128)}, f32[21,10,2,128]{3,2,1,0:T(2,128)S(1)}, u32[]{:S(2)}) copy-start(f32[21,10,2,128]{3,2,1,0:T(2,128)S(1)} %collective-permute-done.14.rows_ref) | copy-start | bytes 645124

commit v22 on v21

--- a/solution.py
+++ b/solution.py
@@ -372,7 +372,10 @@
     band_reach = max(-(-(2 * RAD + 1) // band_width), (band_width + 2 * RAD) // band_width)
     discs = (along_in[:, :, None, None] & across_in[:, None]).astype(jnp.float32)
     solid_planes = solid_flag.astype(jnp.float32)
-    velocity, flow = first_moments(populations, discs[:, 1:-1, 0:band_width], solid_mask)
+    inner_discs = (along_in[:, 1:-1, None, None] & across_in[:, None, 0:band_width]).astype(
+        jnp.float32
+    )
+    velocity, flow = first_moments(populations, inner_discs, solid_mask)
     partials = flow
     for repeat in range(ITERS):
         fields = [populations, smoke_field[None]]

time: 76 us -> 76 us (level)
  other arithmetic: 5.91 us -> 7.81 us
  waiting for transfers between devices: 10.8 us -> 9.69 us
    slice x2, local copies, waits for them, and re-layouts: 1.64 us -> 0.08 us  [the longest x1 0.08 us: body(): along_in[:, 1:-1, None, None] & across_in[:, None, 0:band_width]]
    ppermute x3, waiting for transfers between devices: 3.58 us -> 2.47 us  [rim_round(): from_left = lax.ppermute(tail, axis, forward)]
    convert_element_type x1, other arithmetic: 0.15 us -> 1.11 us  [body(): (along_in[:, :, None, None] & across_in[:, None]).astype(jnp.float32)]
    convert_element_type x0 -> x1, other arithmetic: none -> 0.93 us  [body(): (along_in[:, 1:-1, None, None] & across_in[:, None, 0:band_width]).astype...]
    sub x0 -> x1, local copies, waits for them, and re-layouts: none -> 0.8 us  [body(): coord_x[None, :] - fan_hubs[:, 0:1]]
  transfers between devices with their start and end apart: 15 -> 15, of which waited for: 6 -> 6; matrix products, arithmetic and copies ran while one was open for 2% -> 3% of each run, Pallas kernels for 0% -> 0%
where the time goes in v22:
time: 76 us; the launch traced here: 75.6 us
  starting transfers between devices  32.6 us (43%)
  Pallas kernels  17.8 us (23%)
  waiting for transfers between devices  9.69 us (13%)
  other arithmetic  7.81 us (10%)
  local copies, waits for them, and re-layouts  6.31 us (8%)
  between operations  1.22 us (2%)
    ppermute x6, starting transfers between devices, rim_round(): lax.ppermute(flow, axis, [(i, (i + offset) % count) for i in range(count)])  15.6 us
    pallas_call x3, Pallas kernels, lattice_step(): pl.pallas_call(functools.partial(step_kernel, with_moments), out_shape=tu...  15.3 us
    ppermute x3, starting transfers between devices, rim_round(): from_right = lax.ppermute(head, axis, backward)  13.6 us
    ppermute x3, waiting for transfers between devices, rim_round(): both = lax.ppermute(jnp.concatenate([tail, head], axis=dim), axis, forward)  4.17 us
    ppermute x3, starting transfers between devices, rim_round(): from_left = lax.ppermute(tail, axis, forward)  3.39 us
    ppermute x6, waiting for transfers between devices, rim_round(): lax.ppermute(flow, axis, [(i, (i + offset) % count) for i in range(count)])  3.04 us
    ppermute x3, waiting for transfers between devices, rim_round(): from_left = lax.ppermute(tail, axis, forward)  2.47 us
    pallas_call x1, Pallas kernels, first_moments(): pl.pallas_call(lambda populations_ref, discs_ref, solid_ref, velocity_ref...  2.46 us
  transfers between devices with their start and end apart: 15, of which 6 were waited for; matrix products, arithmetic and copies ran while one was open for 3% of the time, Pallas kernels for 0%

profile of v22, /device:TPU:0, one launch (start us, length us, event | category | flops | bytes accessed | tf_op | source)
XLA Modules:
  0.0 75.6 jit_solution(17323872538389336731)
XLA Ops:
  0.6 0.8 %slice_bitcast_fusion.12 = (s32[8]{0:T(128)S(1)}, s32[8]{0:T(128)S(1)}, s32[8]{0:T(128)S(1)}) fusion(s32[8,3]{0,1:T(4,128)} %param.36), kind=kLoop, calls=%fused_computation.162 | loop fusion | bytes 192 | tf_op jit(solution)/shard_map/sub | solution.py:361
  1.5 0.7 and_select_fusion
  2.3 0.1 add_compare_fusion
  2.4 0.1 fusion.42
  2.6 0.9 %and_convert_fusion.1.discs_ref = f32[8,8,16,128]{3,2,1,0:T(8,128)} fusion(pred[8,16,128]{2,1,0:T(8,128)(4,1)S(1)} %slice.616, pred[8,8]{1,0:T(8,128)(4,1)S(1)} %slice.520), kind=kLoop, calls=%fused_computation.1 | loop fusion | flops 262144 | bytes 540736 | tf_op jit(solution)/shard_map/convert_element_type | solution.py:375
  3.5 2.5 %shard_map.104 = (f32[3,8,16,128]{3,2,1,0:T(8,128)}, f32[8]{0:T(128)}) custom-call(f32[19,8,16,128]{3,2,1,0:T(8,128)} %inner_ref.1, f32[8,8,16,128]{3,2,1,0:T(8,128)} %and_convert_fusion.1.discs_ref, s32[8,16,128]{2,1,0:T(8,128)} %solid_ref.1), custom_call_target="tpu_custom_call" | custom-call | flops 983040 | bytes 1245184 | tf_op jit(solution)/shard_map/pallas_call | solution.py:170
  6.0 3.0 %collective-permute-start.2 = (f32[8]{0:T(128)}, f32[8]{0:T(128)S(1)}, u32[]{:S(2)}, u32[]{:S(2)}) collective-permute-start(f32[8]{0:T(128)} %get-tuple-element.130), channel_id=1, source_target_pairs={{0,4},{2,6},{4,8},{6,10},{8,12},{10,14},{12,16},{14,18},{16,20},{1... | collective-permute-start | bytes 104 | tf_op jit(solution)/shard_map/ppermute | solution.py:297
  9.0 3.1 %collective-permute-start.3 = (f32[8]{0:T(128)}, f32[8]{0:T(128)S(1)}, u32[]{:S(2)}, u32[]{:S(2)}) collective-permute-start(f32[8]{0:T(128)} %get-tuple-element.130), channel_id=1, source_target_pairs={{0,28},{2,30},{4,0},{6,2},{8,4},{10,6},{12,8},{14,10},{16,12},{18,... | collective-permute-start | bytes 104 | tf_op jit(solution)/shard_map/ppermute | solution.py:297
  12.2 0.7 fusion.17
  12.9 1.6 %collective-permute-start = (f32[22,1,16,128]{3,2,1,0:T(8,128)S(1)}, f32[22,1,16,128]{3,2,1,0:T(8,128)S(1)}, u32[]{:S(2)}, u32[]{:S(2)}) collective-permute-start(f32[22,1,16,128]{3,2,1,0:T(8,128)S(1)} %get-tuple-element.188), channel_id=1, source_target_pairs={{0,2},{2,4},{4,6},{6,8},{8,10},{10,12},{12,14},{14,16},{16,18},{18... | collective-permute-start | bytes 540680 | tf_op jit(solution)/shard_map/ppermute | solution.py:293
  14.6 4.0 %collective-permute-start.1 = (f32[22,1,16,128]{3,2,1,0:T(8,128)S(1)}, f32[22,1,16,128]{3,2,1,0:T(8,128)S(1)}, u32[]{:S(2)}, u32[]{:S(2)}) collective-permute-start(f32[22,1,16,128]{3,2,1,0:T(8,128)S(1)} %get-tuple-element.189), channel_id=1, source_target_pairs={{2,0},{4,2},{6,4},{8,6},{10,8},{12,10},{14,12},{16,14},{18,16},{20... | collective-permute-start | bytes 540680 | tf_op jit(solution)/shard_map/ppermute | solution.py:294
  18.6 1.1 %and_convert_fusion.discs_ref = f32[8,10,18,128]{3,2,1,0:T(8,128)} fusion(pred[8,18,128]{2,1,0:T(8,128)(4,1)S(1)} %add_compare_fusion, pred[8,10]{1,0:T(8,128)(4,1)S(1)} %fusion.42), kind=kLoop, calls=%fused_computation | loop fusion | flops 368640 | bytes 755792 | tf_op jit(solution)/shard_map/convert_element_type | solution.py:373
  19.9 0.1 broadcast_multiply_fusion
  20.0 0.2 fusion.19
  20.2 2.5 %collective-permute-done.low_ref = f32[22,1,16,128]{3,2,1,0:T(8,128)S(1)} collective-permute-done((f32[22,1,16,128]{3,2,1,0:T(8,128)S(1)}, f32[22,1,16,128]{3,2,1,0:T(8,128)S(1)}, u32[]{:S(2)}, u32[]{:S(2)}) %collective-permute-start) | collective-permute-done | bytes 180256 | tf_op jit(solution)/shard_map/ppermute | solution.py:293
  22.8 0.2 fusion.2
  23.0 0.4 copy-done.4
  23.4 0.1 fusion.91
  23.5 1.4 %collective-permute-done.4.rows_ref = f32[22,10,2,128]{3,2,1,0:T(2,128)S(1)} collective-permute-done((f32[22,10,2,128]{3,2,1,0:T(2,128)S(1)}, f32[22,10,2,128]{3,2,1,0:T(2,128)S(1)}, u32[]{:S(2)}, u32[]{:S(2)}) %collective-permute-start.4) | collective-permute-done | bytes 225312 | tf_op jit(solution)/shard_map/ppermute | solution.py:288
  25.0 0.1 fusion.38
  25.1 0.7 maximum_bitcast_fusion.solid_ref
  25.8 0.5 fusion.71.strength_ref
  26.3 5.2 %shard_map.105 = (f32[19,8,16,128]{3,2,1,0:T(8,128)}, f32[3,8,16,128]{3,2,1,0:T(8,128)}, f32[8]{0:T(128)}) custom-call(f32[8]{0:T(128)} %fusion.71.strength_ref, f32[19,8,16,128]{3,2,1,0:T(8,128)} %inner_ref.1, f32[22,1,16,128]{3,2,1,0:T(8,128)} %copy-done.4, f32[22,1,16,128]{3,2,1,0:T(8,128)} %copy-done.5, f32[22,10,2,128]{3,2,1,0:T(2,128)} %copy-done.10, ...), custom_call_target="tpu_custom_call" | custom-call | flops 6912000 | bytes 3735552 | tf_op jit(solution)/shard_map/pallas_call | solution.py:200
  31.5 1.1 %fusion.76 = (f32[19,1,16,128]{3,2,1,0:T(8,128)S(1)}, f32[19,1,16,128]{3,2,1,0:T(8,128)S(1)}) fusion(f32[19,8,16,128]{3,2,1,0:T(8,128)} %get-tuple-element.132.inner_ref), kind=kLoop, calls=%fused_computation.169 | loop fusion | bytes 622592 | tf_op jit(solution)/shard_map/slice | solution.py:278
  32.6 0.7 pad_bitcast_fusion.1
  33.4 1.7 %collective-permute-start.5 = (f32[21,1,16,128]{3,2,1,0:T(8,128)S(1)}, f32[21,1,16,128]{3,2,1,0:T(8,128)S(1)}, u32[]{:S(2)}, u32[]{:S(2)}) collective-permute-start(f32[21,1,16,128]{3,2,1,0:T(8,128)S(1)} %get-tuple-element.180), channel_id=1, source_target_pairs={{0,2},{2,4},{4,6},{6,8},{8,10},{10,12},{12,14},{14,16},{16,18},{18... | collective-permute-start | bytes 516104 | tf_op jit(solution)/shard_map/ppermute | solution.py:293
  35.1 4.0 %collective-permute-start.6 = (f32[21,1,16,128]{3,2,1,0:T(8,128)S(1)}, f32[21,1,16,128]{3,2,1,0:T(8,128)S(1)}, u32[]{:S(2)}, u32[]{:S(2)}) collective-permute-start(f32[21,1,16,128]{3,2,1,0:T(8,128)S(1)} %get-tuple-element.181), channel_id=1, source_target_pairs={{2,0},{4,2},{6,4},{8,6},{10,8},{12,10},{14,12},{16,14},{18,16},{20... | collective-permute-start | bytes 516104 | tf_op jit(solution)/shard_map/ppermute | solution.py:294
  39.0 4.7 %collective-permute-start.8 = (f32[8]{0:T(128)S(1)}, f32[8]{0:T(128)S(1)}, u32[]{:S(2)}, u32[]{:S(2)}) collective-permute-start(f32[8]{0:T(128)S(1)} %copy-done.21), channel_id=1, source_target_pairs={{0,28},{2,30},{4,0},{6,2},{8,4},{10,6},{12,8},{14,10},{16,12},{18,... | collective-permute-start | bytes 104 | tf_op jit(solution)/shard_map/ppermute | solution.py:297
  43.8 1.5 %collective-permute-done.7 = f32[8]{0:T(128)S(1)} collective-permute-done((f32[8]{0:T(128)S(1)}, f32[8]{0:T(128)S(1)}, u32[]{:S(2)}, u32[]{:S(2)}) %collective-permute-start.7) | collective-permute-done | bytes 64 | tf_op jit(solution)/shard_map/ppermute | solution.py:297
  45.4 0.2 fusion.14
  45.6 0.4 copy-done.8
  46.0 0.1 fusion.89
  46.1 1.4 %collective-permute-done.9.rows_ref = f32[21,10,2,128]{3,2,1,0:T(2,128)S(1)} collective-permute-done((f32[21,10,2,128]{3,2,1,0:T(2,128)S(1)}, f32[21,10,2,128]{3,2,1,0:T(2,128)S(1)}, u32[]{:S(2)}, u32[]{:S(2)}) %collective-permute-start.9) | collective-permute-done | bytes 215072 | tf_op jit(solution)/shard_map/ppermute | solution.py:288
  47.5 0.1 fusion.32
  47.7 0.5 fusion.72.strength_ref
  48.2 5.3 %shard_map.106 = (f32[19,8,16,128]{3,2,1,0:T(8,128)}, f32[3,8,16,128]{3,2,1,0:T(8,128)}, f32[8]{0:T(128)}) custom-call(f32[8]{0:T(128)} %fusion.72.strength_ref, f32[19,8,16,128]{3,2,1,0:T(8,128)} %get-tuple-element.132.inner_ref, f32[21,1,16,128]{3,2,1,0:T(8,128)} %copy-done.8, f32[21,1,16,128]{3,2,1,0:T(8,128)} %copy-done.9, ...), custom_call_target="tpu_custom_call" | custom-call | flops 6912000 | bytes 3735552 | tf_op jit(solution)/shard_map/pallas_call | solution.py:200
  53.5 1.1 %fusion.75 = (f32[19,1,16,128]{3,2,1,0:T(8,128)S(1)}, f32[19,1,16,128]{3,2,1,0:T(8,128)S(1)}) fusion(f32[19,8,16,128]{3,2,1,0:T(8,128)} %get-tuple-element.135.inner_ref), kind=kLoop, calls=%fused_computation.168 | loop fusion | bytes 622592 | tf_op jit(solution)/shard_map/slice | solution.py:278
  54.6 0.7 pad_bitcast_fusion
  55.4 5.6 %collective-permute-start.11 = (f32[21,1,16,128]{3,2,1,0:T(8,128)S(1)}, f32[21,1,16,128]{3,2,1,0:T(8,128)S(1)}, u32[]{:S(2)}, u32[]{:S(2)}) collective-permute-start(f32[21,1,16,128]{3,2,1,0:T(8,128)S(1)} %get-tuple-element.179), channel_id=1, source_target_pairs={{2,0},{4,2},{6,4},{8,6},{10,8},{12,10},{14,12},{16,14},{18,16},{20... | collective-permute-start | bytes 516104 | tf_op jit(solution)/shard_map/ppermute | solution.py:294
  61.0 4.7 %collective-permute-start.13 = (f32[8]{0:T(128)S(1)}, f32[8]{0:T(128)S(1)}, u32[]{:S(2)}, u32[]{:S(2)}) collective-permute-start(f32[8]{0:T(128)S(1)} %copy-done.20), channel_id=1, source_target_pairs={{0,28},{2,30},{4,0},{6,2},{8,4},{10,6},{12,8},{14,10},{16,12},{18,... | collective-permute-start | bytes 104 | tf_op jit(solution)/shard_map/ppermute | solution.py:297
  65.7 1.5 %collective-permute-done.12 = f32[8]{0:T(128)S(1)} collective-permute-done((f32[8]{0:T(128)S(1)}, f32[8]{0:T(128)S(1)}, u32[]{:S(2)}, u32[]{:S(2)}) %collective-permute-start.12) | collective-permute-done | bytes 64 | tf_op jit(solution)/shard_map/ppermute | solution.py:297
  67.4 0.2 fusion.9
  67.5 0.4 copy-done.6
  68.0 0.1 fusion.87
  68.1 1.4 %collective-permute-done.14.rows_ref = f32[21,10,2,128]{3,2,1,0:T(2,128)S(1)} collective-permute-done((f32[21,10,2,128]{3,2,1,0:T(2,128)S(1)}, f32[21,10,2,128]{3,2,1,0:T(2,128)S(1)}, u32[]{:S(2)}, u32[]{:S(2)}) %collective-permute-start.14) | collective-permute-done | bytes 215072 | tf_op jit(solution)/shard_map/ppermute | solution.py:288
  69.5 0.7 fusion.26
  70.3 0.5 fusion.73.strength_ref
  70.8 4.9 %shard_map.107 = f32[19,8,16,128]{3,2,1,0:T(8,128)} custom-call(f32[8]{0:T(128)} %fusion.73.strength_ref, f32[19,8,16,128]{3,2,1,0:T(8,128)} %get-tuple-element.135.inner_ref, f32[21,1,16,128]{3,2,1,0:T(8,128)} %copy-done.6, f32[21,1,16,128]{3,2,1,0:T(8,128)} %copy-done.7, f32[21,10,2,128]{3,2,1,0:T(2,128)} %copy-done.13, ...), custom_call_target="tpu_custom_call" | custom-call | flops 6912000 | bytes 3735552 | tf_op jit(solution)/shard_map/pallas_call | solution.py:200
  (105 shorter events, 1.1 us)
Async XLA Ops:
  0.6 11.5 %copy-start.11 = (s32[8,16,128]{2,1,0:T(8,128)S(1)}, s32[8,16,128]{2,1,0:T(8,128)}, u32[]{:S(2)}) copy-start(s32[8,16,128]{2,1,0:T(8,128)} %solid_ref.1) | copy-start | bytes 196612
  2.5 9.6 %copy-start = (f32[19,8,16,128]{3,2,1,0:T(8,128)S(1)}, f32[19,8,16,128]{3,2,1,0:T(8,128)}, u32[]{:S(2)}) copy-start(f32[19,8,16,128]{3,2,1,0:T(8,128)} %inner_ref.1) | copy-start | bytes 3735556
  3.5 8.7 %copy-start.3 = (f32[8,16,128]{2,1,0:T(8,128)S(1)}, f32[8,16,128]{2,1,0:T(8,128)}, u32[]{:S(2)}) copy-start(f32[8,16,128]{2,1,0:T(8,128)} %param.35) | copy-start | bytes 196612
  6.0 14.2 %collective-permute-start.2 = (f32[8]{0:T(128)}, f32[8]{0:T(128)S(1)}, u32[]{:S(2)}, u32[]{:S(2)}) collective-permute-start(f32[8]{0:T(128)} %get-tuple-element.130), channel_id=1, source_target_pairs={{0,4},{2,6},{4,8},{6,10},{8,12},{10,14},{12,16},{14,18},{16,20},{1... | collective-permute-start | bytes 104 | tf_op jit(solution)/shard_map/ppermute | solution.py:297
  9.0 11.2 %collective-permute-start.3 = (f32[8]{0:T(128)}, f32[8]{0:T(128)S(1)}, u32[]{:S(2)}, u32[]{:S(2)}) collective-permute-start(f32[8]{0:T(128)} %get-tuple-element.130), channel_id=1, source_target_pairs={{0,28},{2,30},{4,0},{6,2},{8,4},{10,6},{12,8},{14,10},{16,12},{18,... | collective-permute-start | bytes 104 | tf_op jit(solution)/shard_map/ppermute | solution.py:297
  12.1 7.6 %copy-start.22 = (s32[16,3]{0,1:T(4,128)S(1)}, s32[16,3]{0,1:T(4,128)}, u32[]{:S(2)}) copy-start(s32[16,3]{0,1:T(4,128)} %param.39) | copy-start | bytes 580
  12.1 7.8 %copy-start.23 = (f32[16]{0:T(128)S(1)}, f32[16]{0:T(128)}, u32[]{:S(2)}) copy-start(f32[16]{0:T(128)} %param.40) | copy-start | bytes 196
  12.1 10.6 %copy-start.19 = (f32[8]{0:T(128)S(1)}, f32[8]{0:T(128)}, u32[]{:S(2)}) copy-start(f32[8]{0:T(128)} %get-tuple-element.130) | copy-start | bytes 100
  12.9 9.8 %collective-permute-start = (f32[22,1,16,128]{3,2,1,0:T(8,128)S(1)}, f32[22,1,16,128]{3,2,1,0:T(8,128)S(1)}, u32[]{:S(2)}, u32[]{:S(2)}) collective-permute-start(f32[22,1,16,128]{3,2,1,0:T(8,128)S(1)} %get-tuple-element.188), channel_id=1, source_target_pairs={{0,2},{2,4},{4,6},{6,8},{8,10},{10,12},{12,14},{14,16},{16,18},{18... | collective-permute-start | bytes 540680 | tf_op jit(solution)/shard_map/ppermute | solution.py:293
  14.6 8.1 %collective-permute-start.1 = (f32[22,1,16,128]{3,2,1,0:T(8,128)S(1)}, f32[22,1,16,128]{3,2,1,0:T(8,128)S(1)}, u32[]{:S(2)}, u32[]{:S(2)}) collective-permute-start(f32[22,1,16,128]{3,2,1,0:T(8,128)S(1)} %get-tuple-element.189), channel_id=1, source_target_pairs={{2,0},{4,2},{6,4},{8,6},{10,8},{12,10},{14,12},{16,14},{18,16},{20... | collective-permute-start | bytes 540680 | tf_op jit(solution)/shard_map/ppermute | solution.py:294
  22.7 0.7 copy-start.4
  22.7 0.7 copy-start.5
  22.8 2.2 %copy-start.14 = (f32[3,8,16,128]{3,2,1,0:T(8,128)S(1)}, f32[3,8,16,128]{3,2,1,0:T(8,128)}, u32[]{:S(2)}) copy-start(f32[3,8,16,128]{3,2,1,0:T(8,128)} %get-tuple-element.133) | copy-start | bytes 589828
  23.4 2.3 %copy-start.17 = (f32[8]{0:T(128)S(1)}, f32[8]{0:T(128)}, u32[]{:S(2)}) copy-start(f32[8]{0:T(128)} %param.37) | copy-start | bytes 100
  23.4 2.3 %copy-start.18 = (f32[8]{0:T(128)S(1)}, f32[8]{0:T(128)}, u32[]{:S(2)}) copy-start(f32[8]{0:T(128)} %param.38) | copy-start | bytes 100
  23.4 1.5 %collective-permute-start.4 = (f32[22,10,2,128]{3,2,1,0:T(2,128)S(1)}, f32[22,10,2,128]{3,2,1,0:T(2,128)S(1)}, u32[]{:S(2)}, u32[]{:S(2)}) collective-permute-start(f32[22,10,2,128]{3,2,1,0:T(2,128)S(1)} %fusion.2), channel_id=1, source_target_pairs={{0,1},{1,0},{2,3},{3,2},{4,5},{5,4},{6,7},{7,6},{8,9},{9,8},{10,11... | collective-permute-start | bytes 675848 | tf_op jit(solution)/shard_map/ppermute | solution.py:288
  24.9 1.4 %copy-start.10 = (f32[22,10,2,128]{3,2,1,0:T(2,128)}, f32[22,10,2,128]{3,2,1,0:T(2,128)S(1)}, u32[]{:S(2)}) copy-start(f32[22,10,2,128]{3,2,1,0:T(2,128)S(1)} %collective-permute-done.4.rows_ref) | copy-start | bytes 675844
  31.5 7.5 %copy-start.21 = (f32[8]{0:T(128)S(1)}, f32[8]{0:T(128)}, u32[]{:S(2)}) copy-start(f32[8]{0:T(128)} %get-tuple-element.131) | copy-start | bytes 100
  31.5 13.9 %copy-start.1 = (f32[19,8,16,128]{3,2,1,0:T(8,128)S(1)}, f32[19,8,16,128]{3,2,1,0:T(8,128)}, u32[]{:S(2)}) copy-start(f32[19,8,16,128]{3,2,1,0:T(8,128)} %get-tuple-element.132.inner_ref) | copy-start | bytes 3735556
  33.4 11.9 %collective-permute-start.5 = (f32[21,1,16,128]{3,2,1,0:T(8,128)S(1)}, f32[21,1,16,128]{3,2,1,0:T(8,128)S(1)}, u32[]{:S(2)}, u32[]{:S(2)}) collective-permute-start(f32[21,1,16,128]{3,2,1,0:T(8,128)S(1)} %get-tuple-element.180), channel_id=1, source_target_pairs={{0,2},{2,4},{4,6},{6,8},{8,10},{10,12},{12,14},{14,16},{16,18},{18... | collective-permute-start | bytes 516104 | tf_op jit(solution)/shard_map/ppermute | solution.py:293
  35.1 10.2 %collective-permute-start.6 = (f32[21,1,16,128]{3,2,1,0:T(8,128)S(1)}, f32[21,1,16,128]{3,2,1,0:T(8,128)S(1)}, u32[]{:S(2)}, u32[]{:S(2)}) collective-permute-start(f32[21,1,16,128]{3,2,1,0:T(8,128)S(1)} %get-tuple-element.181), channel_id=1, source_target_pairs={{2,0},{4,2},{6,4},{8,6},{10,8},{12,10},{14,12},{16,14},{18,16},{20... | collective-permute-start | bytes 516104 | tf_op jit(solution)/shard_map/ppermute | solution.py:294
  39.0 6.2 %collective-permute-start.7 = (f32[8]{0:T(128)S(1)}, f32[8]{0:T(128)S(1)}, u32[]{:S(2)}, u32[]{:S(2)}) collective-permute-start(f32[8]{0:T(128)S(1)} %copy-done.21), channel_id=1, source_target_pairs={{0,4},{2,6},{4,8},{6,10},{8,12},{10,14},{12,16},{14,18},{16,20},{1... | collective-permute-start | bytes 104 | tf_op jit(solution)/shard_map/ppermute | solution.py:297
  39.0 6.2 %collective-permute-start.8 = (f32[8]{0:T(128)S(1)}, f32[8]{0:T(128)S(1)}, u32[]{:S(2)}, u32[]{:S(2)}) collective-permute-start(f32[8]{0:T(128)S(1)} %copy-done.21), channel_id=1, source_target_pairs={{0,28},{2,30},{4,0},{6,2},{8,4},{10,6},{12,8},{14,10},{16,12},{18,... | collective-permute-start | bytes 104 | tf_op jit(solution)/shard_map/ppermute | solution.py:297
  45.3 0.7 copy-start.8
  45.3 0.7 copy-start.9
  45.4 2.1 %copy-start.16 = (f32[3,8,16,128]{3,2,1,0:T(8,128)S(1)}, f32[3,8,16,128]{3,2,1,0:T(8,128)}, u32[]{:S(2)}) copy-start(f32[3,8,16,128]{3,2,1,0:T(8,128)} %get-tuple-element.136) | copy-start | bytes 589828
  46.0 1.5 %collective-permute-start.9 = (f32[21,10,2,128]{3,2,1,0:T(2,128)S(1)}, f32[21,10,2,128]{3,2,1,0:T(2,128)S(1)}, u32[]{:S(2)}, u32[]{:S(2)}) collective-permute-start(f32[21,10,2,128]{3,2,1,0:T(2,128)S(1)} %fusion.14), channel_id=1, source_target_pairs={{0,1},{1,0},{2,3},{3,2},{4,5},{5,4},{6,7},{7,6},{8,9},{9,8},{10,11... | collective-permute-start | bytes 645128 | tf_op jit(solution)/shard_map/ppermute | solution.py:288
  47.5 0.7 copy-start.12
  53.5 7.5 %copy-start.20 = (f32[8]{0:T(128)S(1)}, f32[8]{0:T(128)}, u32[]{:S(2)}) copy-start(f32[8]{0:T(128)} %get-tuple-element.134) | copy-start | bytes 100
  53.5 13.9 %copy-start.2 = (f32[19,8,16,128]{3,2,1,0:T(8,128)S(1)}, f32[19,8,16,128]{3,2,1,0:T(8,128)}, u32[]{:S(2)}) copy-start(f32[19,8,16,128]{3,2,1,0:T(8,128)} %get-tuple-element.135.inner_ref) | copy-start | bytes 3735556
  55.3 11.9 %collective-permute-start.10 = (f32[21,1,16,128]{3,2,1,0:T(8,128)S(1)}, f32[21,1,16,128]{3,2,1,0:T(8,128)S(1)}, u32[]{:S(2)}, u32[]{:S(2)}) collective-permute-start(f32[21,1,16,128]{3,2,1,0:T(8,128)S(1)} %get-tuple-element.178), channel_id=1, source_target_pairs={{0,2},{2,4},{4,6},{6,8},{8,10},{10,12},{12,14},{14,16},{16,18},{18... | collective-permute-start | bytes 516104 | tf_op jit(solution)/shard_map/ppermute | solution.py:293
  55.4 11.9 %collective-permute-start.11 = (f32[21,1,16,128]{3,2,1,0:T(8,128)S(1)}, f32[21,1,16,128]{3,2,1,0:T(8,128)S(1)}, u32[]{:S(2)}, u32[]{:S(2)}) collective-permute-start(f32[21,1,16,128]{3,2,1,0:T(8,128)S(1)} %get-tuple-element.179), channel_id=1, source_target_pairs={{2,0},{4,2},{6,4},{8,6},{10,8},{12,10},{14,12},{16,14},{18,16},{20... | collective-permute-start | bytes 516104 | tf_op jit(solution)/shard_map/ppermute | solution.py:294
  61.0 6.2 %collective-permute-start.12 = (f32[8]{0:T(128)S(1)}, f32[8]{0:T(128)S(1)}, u32[]{:S(2)}, u32[]{:S(2)}) collective-permute-start(f32[8]{0:T(128)S(1)} %copy-done.20), channel_id=1, source_target_pairs={{0,4},{2,6},{4,8},{6,10},{8,12},{10,14},{12,16},{14,18},{16,20},{1... | collective-permute-start | bytes 104 | tf_op jit(solution)/shard_map/ppermute | solution.py:297
  61.0 6.2 %collective-permute-start.13 = (f32[8]{0:T(128)S(1)}, f32[8]{0:T(128)S(1)}, u32[]{:S(2)}, u32[]{:S(2)}) collective-permute-start(f32[8]{0:T(128)S(1)} %copy-done.20), channel_id=1, source_target_pairs={{0,28},{2,30},{4,0},{6,2},{8,4},{10,6},{12,8},{14,10},{16,12},{18,... | collective-permute-start | bytes 104 | tf_op jit(solution)/shard_map/ppermute | solution.py:297
  67.2 0.7 copy-start.6
  67.3 0.7 copy-start.7
  67.4 2.1 %copy-start.15 = (f32[3,8,16,128]{3,2,1,0:T(8,128)S(1)}, f32[3,8,16,128]{3,2,1,0:T(8,128)}, u32[]{:S(2)}) copy-start(f32[3,8,16,128]{3,2,1,0:T(8,128)} %get-tuple-element.137) | copy-start | bytes 589828
  68.0 1.5 %collective-permute-start.14 = (f32[21,10,2,128]{3,2,1,0:T(2,128)S(1)}, f32[21,10,2,128]{3,2,1,0:T(2,128)S(1)}, u32[]{:S(2)}, u32[]{:S(2)}) collective-permute-start(f32[21,10,2,128]{3,2,1,0:T(2,128)S(1)} %fusion.9), channel_id=1, source_target_pairs={{0,1},{1,0},{2,3},{3,2},{4,5},{5,4},{6,7},{7,6},{8,9},{9,8},{10,11... | collective-permute-start | bytes 645128 | tf_op jit(solution)/shard_map/ppermute | solution.py:288
  69.4 1.3 %copy-start.13 = (f32[21,10,2,128]{3,2,1,0:T(2,128)}, f32[21,10,2,128]{3,2,1,0:T(2,128)S(1)}, u32[]{:S(2)}) copy-start(f32[21,10,2,128]{3,2,1,0:T(2,128)S(1)} %collective-permute-done.14.rows_ref) | copy-start | bytes 645124
